TPU v7x, 32 devices: a whole 2x2x4 slice. The times are simulated.
32 devices in a mesh: grp: 2 (over x), cand: 8 (over z, y), seq: 2 (over core).
Axes of the slice: x: 2, y: 2, z: 4, core: 2. Of those that a mesh axis runs over, the one named last changes fastest.
Arguments:
- x_prefix: bfloat16 [8192, 2560], P(('grp', 'cand', 'seq')), parts along dimension 0, may hold values from -6 to 6
- b_prefix: bfloat16 [8192, 128], P(('grp', 'cand', 'seq')), parts along dimension 0, may hold values from -0.5 to 0.5
- code_prefix: int32 [8192, 40], P(('grp', 'cand', 'seq')), parts along dimension 0, may hold values from 0 to 500
- x_cand: bfloat16 [32, 512, 2560], P(('grp', 'cand'), None, 'seq'), parts along dimension 0, may hold values from -6 to 6
- b_cand: bfloat16 [32, 512, 128], P(('grp', 'cand')), parts along dimension 0, may hold values from -0.5 to 0.5
- c_cand: bfloat16 [32, 512, 128], P(('grp', 'cand')), parts along dimension 0, may hold values from -0.5 to 0.5
- code_cand: int32 [32, 512, 40], P(('grp', 'cand'), None, 'seq'), parts along dimension 0, may hold values from 0 to 500
- lengths: int32 [32], P(('grp', 'cand')), parts along dimension 0, may hold values from 1 to 2, as said below
- dy_cand: bfloat16 [32, 512, 2560], P(('grp', 'cand'), None, 'seq'), parts along dimension 0, may hold values from -1.5 to 1.5
Outputs:
- dx_prefix: bfloat16 [8192, 2560], P(('grp', 'cand', 'seq')), parts along dimension 0
- db_prefix: float32 [8192, 128], P(('grp', 'cand', 'seq')), parts along dimension 0
- dx_cand: bfloat16 [32, 512, 2560], P(('grp', 'cand'), None, 'seq'), parts along dimension 0
- db_cand: float32 [32, 512, 128], P(('grp', 'cand'), 'seq'), parts along dimension 0
- dc_cand: float32 [32, 512, 128], P(('grp', 'cand'), 'seq'), parts along dimension 0
There are 2 independent parts, one for each index of `grp`. A program takes and returns all parts, laid end to end along the dimension named above; each array names one. Nothing has to cross between parts.
Inputs may be any that keep to these rules, and one draw needn't show every extreme that they name: lengths count blocks of 256 tokens.
All inputs are finite; a program needn't handle non-finite values.
Results may differ from a plain program's by a relative error of at most 0.0015.
The roundings to bfloat16 on the way count: a program that leaves them out, or rounds other values in their place, can miss the bound.
Values may be sent and summed in bfloat16 or wider, within the bound.
No kernel may reach another device: no remote copies, remote signals or barrier semaphores. Data moves between devices by JAX's collectives and lax.ppermute only.
A program may use at most 256 MiB of HBM per device.

v0:
```python
import jax
import jax.numpy as jnp
from jax import lax
from jax.sharding import PartitionSpec as P

BLOCK = 256


def entering(shard, axis, combine, identity, reverse):
    length, mine = (lax.axis_size(axis), lax.axis_index(axis))
    everything = jax.tree.map(lambda part: lax.all_gather(part, axis), shard)
    start = jax.tree.map(
        lambda part, zero: jnp.broadcast_to(jnp.asarray(zero, part.dtype), part.shape),
        shard,
        identity,
    )

    def turn(k, before):
        at = length - 1 - k if reverse else k
        reached = at > mine if reverse else at < mine
        new = combine(before, jax.tree.map(lambda part: part[at], everything))
        return jax.tree.map(lambda a, b: jnp.where(reached, a, b), new, before)

    return lax.fori_loop(0, length, turn, start)


def broadcast(shard, axis, root):
    mine = lax.axis_index(axis) == root
    return lax.psum(jnp.where(mine, shard, jnp.zeros_like(shard)), axis)


def add_pair(earlier, later_part):
    return earlier + later_part


def link_states(earlier, later_part):
    return (
        earlier[0] * jnp.exp(later_part[1])[:, None, None] + later_part[0],
        earlier[1] + later_part[1],
    )


def candidate_terms(candidate, head_size):
    x_one, g_one, b_one, c_one, level_sum = candidate
    cand_len = x_one.shape[0]
    heads_total = level_sum.shape[1]
    position = jnp.arange(cand_len, dtype=jnp.int32)
    causal = position[:, None] >= position[None, :]
    scores = lax.dot_general(
        c_one, b_one, (((1,), (1,)), ((), ())), preferred_element_type=jnp.float32
    )

    def per_head(head_at, carry):
        weight_sum, grad_x = carry
        x_head = lax.dynamic_slice_in_dim(x_one, head_at * head_size, head_size, 1)
        g_head = lax.dynamic_slice_in_dim(g_one, head_at * head_size, head_size, 1)
        level_head = lax.dynamic_slice_in_dim(level_sum, head_at, 1, 1)[:, 0]
        decay_mat = jnp.where(
            causal, jnp.exp(level_head[:, None] - level_head[None, :]), jnp.zeros((), jnp.float32)
        )
        kernel = (scores * decay_mat).astype(jnp.bfloat16)
        dx_piece = lax.dot_general(
            kernel, g_head, (((0,), (0,)), ((), ())), preferred_element_type=jnp.float32
        )
        grad_x = lax.dynamic_update_slice_in_dim(
            grad_x, dx_piece.astype(jnp.bfloat16), head_at * head_size, 1
        )
        inner_prod = lax.dot_general(
            g_head, x_head, (((1,), (1,)), ((), ())), preferred_element_type=jnp.float32
        )
        return (weight_sum + inner_prod * decay_mat, grad_x)

    start = (jnp.zeros((cand_len, cand_len), jnp.float32), jnp.zeros_like(x_one))
    weight_sum, grad_x = lax.fori_loop(0, heads_total, per_head, start)
    db_part = jnp.dot(weight_sum.T, c_one.astype(jnp.float32), precision=lax.Precision.HIGHEST)
    dc_part = jnp.dot(weight_sum, b_one.astype(jnp.float32), precision=lax.Precision.HIGHEST)
    return (grad_x, db_part, dc_part)


def shards(x_prefix, b_prefix, code_prefix, x_cand, b_cand, c_cand, code_cand, lengths, dy_cand):
    pre_len, width = x_prefix.shape
    heads_total = code_prefix.shape[1]
    head_size = width // heads_total
    nstate = b_prefix.shape[1]
    cand_dev, cand_len, half_width = x_cand.shape
    half_heads = code_cand.shape[2]
    seq_at = lax.axis_index("seq")
    log_prefix = jnp.log1p(-code_prefix.astype(jnp.float32) * 1e-06)
    own_total = jnp.sum(log_prefix, axis=0)
    later_total = entering(own_total, ("cand", "seq"), add_pair, jnp.zeros_like(own_total), True)
    after_local = own_total[None, :] - jnp.cumsum(log_prefix, axis=0)
    weight = jnp.exp(after_local + later_total[None, :])
    weighted_b = (weight[:, :, None] * b_prefix[:, None, :].astype(jnp.float32)).astype(
        jnp.bfloat16
    )
    x_heads = x_prefix.reshape(pre_len, heads_total, head_size)
    state_full = jnp.einsum("jhp,jhn->hpn", x_heads, weighted_b, preferred_element_type=jnp.float32)
    own_state = state_full * jnp.exp(-later_total)[:, None, None]
    empty = (jnp.zeros_like(own_state), jnp.zeros_like(own_total))
    before = entering((own_state, own_total), ("cand", "seq"), link_states, empty, False)
    final_state = before[0] * jnp.exp(own_total)[:, None, None] + own_state
    root_last = lax.axis_size(("cand", "seq")) - 1
    whole_init = broadcast(final_state.astype(jnp.bfloat16), ("cand", "seq"), root_last)
    init_half = lax.dynamic_slice_in_dim(whole_init, seq_at * half_heads, half_heads, 0)
    position = jnp.arange(cand_len, dtype=jnp.int32)
    valid_rows = position[None, :] < lengths[:, None] * BLOCK
    g_cand = jnp.where(valid_rows[:, :, None], dy_cand, jnp.zeros_like(dy_cand))
    level_all = jnp.cumsum(jnp.log1p(-code_cand.astype(jnp.float32) * 1e-06), axis=1)

    def run_candidate(candidate):
        return candidate_terms(candidate, head_size)

    dx_cand, db_part, dc_part = lax.map(run_candidate, (x_cand, g_cand, b_cand, c_cand, level_all))
    amplitude = jnp.exp(level_all)
    g_heads = g_cand.reshape(cand_dev, cand_len, half_heads, head_size)
    decayed_g = (g_heads.astype(jnp.float32) * amplitude[:, :, :, None]).astype(jnp.bfloat16)
    dstate = jnp.einsum("cthp,ctn->hpn", decayed_g, c_cand, preferred_element_type=jnp.float32)
    dc_state = jnp.dot(
        decayed_g.reshape(cand_dev * cand_len, half_width),
        init_half.reshape(half_width, nstate),
        preferred_element_type=jnp.float32,
    )
    dc_total = dc_part + dc_state.reshape(cand_dev, cand_len, nstate)
    db_cand, dc_cand = (
        lax.psum_scatter(db_part, "seq", scatter_dimension=1, tiled=True),
        lax.psum_scatter(dc_total, "seq", scatter_dimension=1, tiled=True),
    )
    summed = lax.psum(dstate, "cand")
    grad_state = lax.all_gather(summed.astype(jnp.bfloat16), "seq", axis=0, tiled=True)
    dx_prefix = jnp.einsum(
        "jhn,hpn->jhp", weighted_b, grad_state, preferred_element_type=jnp.float32
    )
    dx_prefix = dx_prefix.astype(jnp.bfloat16).reshape(pre_len, width)
    projected = jnp.einsum("jhp,hpn->jhn", x_heads, grad_state, preferred_element_type=jnp.float32)
    db_prefix = jnp.sum(projected * weight[:, :, None], axis=1)
    return (dx_prefix, db_prefix, dx_cand, db_cand, dc_cand)


def solution(mesh):
    return jax.shard_map(
        shards,
        mesh=mesh,
        in_specs=(
            P(("grp", "cand", "seq"), None),
            P(("grp", "cand", "seq"), None),
            P(("grp", "cand", "seq"), None),
            P(("grp", "cand"), None, "seq"),
            P(("grp", "cand"), None, None),
            P(("grp", "cand"), None, None),
            P(("grp", "cand"), None, "seq"),
            P(("grp", "cand")),
            P(("grp", "cand"), None, "seq"),
        ),
        out_specs=(
            P(("grp", "cand", "seq"), None),
            P(("grp", "cand", "seq"), None),
            P(("grp", "cand"), None, "seq"),
            P(("grp", "cand"), "seq", None),
            P(("grp", "cand"), "seq", None),
        ),
        check_vma=False,
    )
```

profile of v0, /device:TPU:0, one launch (start us, length us, event | category | flops | bytes accessed | tf_op | source)
XLA Modules:
  0.0 392.8 jit_solution(4771028220192774179)
XLA Ops:
  11.1 34.9 %all-reduce = f32[640]{0:T(1024)S(1)} all-reduce(f32[640]{0:T(1024)S(1)} %dynamic-update-slice), channel_id=2, replica_groups=mesh['grp'=2,'cand'=8,'seq'=2] {'cand','seq'}, use_global_device_ids=true, to_apply=%add | all-reduce | flops 640 | bytes 5120
  47.9 1.6 copy.51
  49.6 2.1 fusion.40
  52.9 2.3 reduce-window.14
  55.7 4.6 %copy.43 = bf16[2,512,1280]{1,2,0:T(8,128)(2,1)} copy(bf16[2,512,1280]{2,1,0:T(8,128)(2,1)} %param.25) | data formatting | bytes 5242880 | tf_op args[8]
  60.4 5.0 %fusion.28 = (bf16[2,512,1280]{1,2,0:T(8,128)(2,1)}, bf16[2,512,1280]{1,2,0:T(8,128)(2,1)}) fusion(f32[2,512,20]{1,2,0:T(8,128)S(1)} %copy.46, bf16[2,512,1280]{1,2,0:T(8,128)(2,1)} %copy.43, pred[2,512]{1,0:T(4,128)(4,1)S(1)} %iota_compare_fusion.1), kind=kLoop, calls=%fused_computation.45 | loop fusion | flops 5242880 | bytes 7947264 | tf_op jit(solution)/shard_map/convert_element_type | solution.py:116
  65.4 92.7 %all-gather.4.cloned.1.call-done = f32[640,64,128]{2,1,0:T(8,128)} async-done(((f32[40,64,128]{2,1,0:T(8,128)}), f32[640,64,128]{2,1,0:T(8,128)}) %all-gather.4.cloned.1.call-update) | async-done | bytes 20971536 | tf_op jit(solution)/shard_map/all_gather | solution.py:11
  158.0 26.6 %while.63 = (s32[]{:T(128)}, f32[40,64,128]{2,1,0:T(8,128)S(1)}, s32[]{:T(128)}, f32[16,40]{1,0:T(8,128)S(1)}, f32[16,40,64,128]{3,2,1,0:T(8,128)}, /*index=5*/s32[]{:T(128)}, s32[]{:T(128)}) while((s32[]{:T(128)}, f32[40,64,128]{2,1,0:T(8,128)S(1)}, s32[]{:T(128)}, f32[16,40]{1,0:T(8,128)S(1)}, f32[16,40,64,128]{3,2,1,0:T(8,128)}, ...), condition=%wide.region_15.16_spmd.clone, body=%wide.region_14.15_spmd.clone.sunk | while | flops 1310724 | bytes 3932745 | solution.py:24
  158.1 1.7 fusion.82
  159.8 1.6 fusion.82
  161.5 1.6 fusion.82
  163.1 1.6 fusion.82
  164.8 1.6 fusion.82
  166.5 1.6 fusion.82
  168.1 1.6 fusion.82
  169.8 1.6 fusion.82
  171.4 1.6 fusion.82
  173.1 1.6 fusion.82
  174.8 1.6 fusion.82
  176.4 1.6 fusion.82
  178.1 1.6 fusion.82
  179.7 1.6 fusion.82
  181.4 1.6 fusion.82
  183.1 1.6 fusion.82
  185.9 144.2 %while.61 = (s32[]{:T(128)}, bf16[2,512,1280]{2,1,0:T(8,128)(2,1)}, f32[2,512,128]{2,1,0:T(8,128)}, f32[2,512,128]{2,1,0:T(8,128)}, bf16[2,512,1280]{2,1,0:T(8,1...) while((s32[]{:T(128)}, bf16[2,512,1280]{2,1,0:T(8,128)(2,1)}, ...), condition=%wide.region_12.13_spmd, body=%wide.region_9.12_spmd.sunk | while | flops 942440448 | bytes 26593764 | solution.py:113
  190.0 2.5 dynamic-slice_bitcast_fusion.2
  192.6 59.2 %while.64 = (s32[]{:T(128)}, f32[512,512]{1,0:T(8,128)S(1)}, bf16[512,1280]{0,1:T(8,128)(2,1)S(1)}, bf16[512,1280]{1,0:T(8,128)(2,1)}, bf16[512,1280]{1,0:T(8,12...) while((s32[]{:T(128)}, f32[512,512]{1,0:T(8,128)S(1)}, ...), condition=%wide.region_11.11_spmd.clone, body=%wide.region_10.10_spmd.clone.sunk | while | flops 70025224 | bytes 3619496 | solution.py:74
  192.7 1.6 fusion.86
  195.7 1.6 fusion.86
  198.6 1.6 fusion.86
  201.6 1.6 fusion.86
  204.5 1.6 fusion.86
  207.5 1.6 fusion.86
  210.5 1.6 fusion.86
  213.4 1.6 fusion.86
  216.4 1.6 fusion.86
  219.4 1.6 fusion.86
  222.3 1.6 fusion.86
  225.3 1.6 fusion.86
  228.2 1.6 fusion.86
  231.2 1.6 fusion.86
  234.2 1.6 fusion.86
  237.1 1.6 fusion.86
  240.1 1.6 fusion.86
  243.1 1.6 fusion.86
  246.0 1.6 fusion.86
  249.0 1.6 fusion.86
  251.9 2.7 fusion.80
  262.2 2.5 dynamic-slice_bitcast_fusion.2
  264.8 59.2 %while.64 = (s32[]{:T(128)}, f32[512,512]{1,0:T(8,128)S(1)}, bf16[512,1280]{0,1:T(8,128)(2,1)S(1)}, bf16[512,1280]{1,0:T(8,128)(2,1)}, bf16[512,1280]{1,0:T(8,12...) while((s32[]{:T(128)}, f32[512,512]{1,0:T(8,128)S(1)}, ...), condition=%wide.region_11.11_spmd.clone, body=%wide.region_10.10_spmd.clone.sunk | while | flops 70025224 | bytes 3619496 | solution.py:74
  264.8 1.6 fusion.86
  270.8 1.6 fusion.86
  276.7 1.6 fusion.86
  288.5 1.6 fusion.86
  294.4 1.6 fusion.86
  300.4 1.6 fusion.86
  306.3 1.6 fusion.86
  312.2 1.6 fusion.86
  324.0 2.7 fusion.80
  331.3 3.6 convolution_add_fusion
  334.9 1.8 fusion.41
  336.8 42.5 %all-reduce.5 = bf16[20,64,128]{2,1,0:T(8,128)(2,1)S(1)} all-reduce(f32[20,64,128]{2,1,0:T(8,128)S(1)} %fusion.41), channel_id=1, replica_groups=mesh['grp'=2,'cand'=8,'seq'=2] {'cand'}, use_global_device_ids=true, to_apply=%region_2.3 | all-reduce | flops 163840 | bytes 983040 | tf_op jit(solution)/shard_map/psum | solution.py:128
  379.3 2.3 all_gather.15
  382.1 1.6 copy.56
  (229 shorter events, 98.7 us)
Async XLA Ops:
  8.0 150.0 %all-gather.4.cloned.1.call-start = ((), (), s32[]{:S(2)}) async-start(), calls=%async_computation.5 | async-start | bytes 22282240 | tf_op jit(solution)/shard_map/all_gather | solution.py:11
  47.8 1.8 copy-start.13
  47.8 1.6 copy-start.12
  49.5 2.2 copy-start.2
  49.6 2.1 copy-start.9
  51.7 0.9 copy-start.11
  51.8 278.5 %all-reduce.4.cloned.1.call-start = ((), (), s32[]{:S(2)}) async-start(), calls=%async_computation.3 | async-start | bytes 1310720 | tf_op jit(solution)/shard_map/psum | solution.py:29
  55.7 4.7 %copy-start.7 = (f32[2,512,20]{1,2,0:T(8,128)}, f32[2,512,20]{1,2,0:T(8,128)S(1)}, u32[]{:S(2)}) copy-start(f32[2,512,20]{1,2,0:T(8,128)S(1)} %copy.46) | copy-start | bytes 245764
  55.7 4.6 %copy-start.15 = (s32[2]{0:T(128)S(1)}, s32[2]{0:T(128)}, u32[]{:S(2)}) copy-start(s32[2]{0:T(128)} %param.24) | copy-start | bytes 28
  158.0 26.7 %copy-start.1 = (f32[40,64,128]{2,1,0:T(8,128)S(1)}, f32[40,64,128]{2,1,0:T(8,128)}, u32[]{:S(2)}) copy-start(f32[40,64,128]{2,1,0:T(8,128)} %fusion.40) | copy-start | bytes 3932164
  185.8 199.5 %reduce-scatter.3.cloned.1.call-start = ((), (), s32[]{:S(2)}) async-start(), calls=%async_computation.2 | async-start | bytes 786432 | tf_op jit(solution)/shard_map/reduce_scatter | solution.py:125
  251.9 2.7 copy-start.4
  256.1 0.8 copy-start.5
  324.0 2.7 copy-start.4
  328.2 0.8 copy-start.5
  330.1 1.2 copy-start.6
  330.2 55.2 %reduce-scatter.5.cloned.1.call-start = ((), (), s32[]{:S(2)}) async-start(), calls=%async_computation.4 | async-start | bytes 786432 | tf_op jit(solution)/shard_map/reduce_scatter | solution.py:126
  331.3 3.6 copy-start
  331.3 3.6 copy-start.8
  336.7 44.9 %copy-start.10 = (f32[256,128]{0,1:T(8,128)S(1)}, f32[256,128]{0,1:T(8,128)}, u32[]{:S(2)}) copy-start(f32[256,128]{0,1:T(8,128)} %copy-done.9) | copy-start | bytes 393220
  336.7 44.8 %copy-start.14 = (f32[256,40]{0,1:T(8,128)S(1)}, f32[256,40]{0,1:T(8,128)}, u32[]{:S(2)}) copy-start(f32[256,40]{0,1:T(8,128)} %copy-done.13) | copy-start | bytes 122884
  382.1 1.6 copy-start.3
Sparse Core Ops, SparseCore 0:
  51.9 106.1 all-gather.3
  186.0 91.2 all-reduce.3
Sparse Core Ops, SparseCore 1:
  330.2 7.9 reduce-scatter.2
  341.0 9.0 reduce-scatter.4
where the time goes:
time: 396 us; the launch traced here: 393 us
  matrix products  136 us (34%)
  waiting for transfers between devices  92.8 us (23%)
  blocking collectives  79.7 us (20%)
  other arithmetic  36.7 us (9%)
  local copies, waits for them, and re-layouts  28.1 us (7%)
  between operations  16.5 us (4%)
    all_gather x1, waiting for transfers between devices, entering(): everything = jax.tree.map(lambda part: lax.all_gather(part, axis), shard)  92.7 us
    dot_general x40, matrix products, per_head(): lax.dot_general(g_head, x_head, (((1,), (1,)), ((), ())), preferred_eleme...  63 us
    dot_general x40, matrix products, per_head(): lax.dot_general(kernel, g_head, (((0,), (0,)), ((), ())), preferred_eleme...  53.1 us
    psum x1, blocking collectives, shards(): summed = lax.psum(dstate, 'cand')  42.5 us
    unnamed x1, blocking collectives  34.9 us
    select_n x32, other arithmetic, turn(): return jax.tree.map(lambda a, b: jnp.where(reached, a, b), new, before)  26.3 us
    unnamed x35, local copies, waits for them, and re-layouts  10.9 us
  transfers between devices with their start and end apart: 4, of which 1 were waited for; matrix products, arithmetic and copies ran while one was open for 42% of the time, Pallas kernels for 0%

commit v1 on v0

v1 whole, which is shorter than its diff:
```python
import jax
import jax.numpy as jnp
from jax import lax
from jax.sharding import PartitionSpec as P

BLOCK = 256


def split_bf16(value):
    high = lax.reduce_precision(value, exponent_bits=8, mantissa_bits=7)
    low = (value - high).astype(jnp.bfloat16)
    return high.astype(jnp.bfloat16), low


def shards(x_prefix, b_prefix, code_prefix, x_cand, b_cand, c_cand, code_cand, lengths, dy_cand):
    pre_len, width = x_prefix.shape
    heads_total = code_prefix.shape[1]
    head_size = width // heads_total
    nstate = b_prefix.shape[1]
    cand_dev, cand_len, half_width = x_cand.shape
    half_heads = code_cand.shape[2]
    pre_axes = ("cand", "seq")

    log_prefix = jnp.log1p(-code_prefix.astype(jnp.float32) * 1e-06)
    own_total = jnp.sum(log_prefix, axis=0)
    totals = lax.all_gather(own_total, pre_axes)
    mine = lax.axis_index(pre_axes)
    shard_at = jnp.arange(totals.shape[0], dtype=jnp.int32)
    later_total = jnp.sum(jnp.where((shard_at > mine)[:, None], totals, 0.0), axis=0)
    after_local = own_total[None, :] - jnp.cumsum(log_prefix, axis=0)
    weight = jnp.exp(after_local + later_total[None, :])
    weighted_b = (weight[:, :, None] * b_prefix[:, None, :].astype(jnp.float32)).astype(
        jnp.bfloat16
    )
    x_heads = x_prefix.reshape(pre_len, heads_total, head_size)
    state_full = jnp.einsum("jhp,jhn->hpn", x_heads, weighted_b, preferred_element_type=jnp.float32)
    init_part = lax.psum_scatter(state_full, "seq", scatter_dimension=0, tiled=True)
    init_half = lax.psum(init_part, "cand").astype(jnp.bfloat16)

    position = jnp.arange(cand_len, dtype=jnp.int32)
    valid_rows = position[None, :] < lengths[:, None] * BLOCK
    g_cand = jnp.where(valid_rows[:, :, None], dy_cand, jnp.zeros_like(dy_cand))
    level_all = jnp.cumsum(jnp.log1p(-code_cand.astype(jnp.float32) * 1e-06), axis=1)
    amplitude = jnp.exp(level_all)
    inverse = jnp.exp(-level_all)
    g_heads = g_cand.reshape(cand_dev, cand_len, half_heads, head_size)
    xc_heads = x_cand.reshape(cand_dev, cand_len, half_heads, head_size)
    scaled_g = g_heads.astype(jnp.float32) * amplitude[:, :, :, None]
    decayed_g, g_low = split_bf16(scaled_g)
    x_high, x_low = split_bf16(xc_heads.astype(jnp.float32) * inverse[:, :, :, None])

    dstate = jnp.einsum("cthp,ctn->hpn", decayed_g, c_cand, preferred_element_type=jnp.float32)
    grad_half = lax.psum(dstate, "cand").astype(jnp.bfloat16)
    grad_state = lax.all_gather(grad_half, "seq", axis=0, tiled=True)

    causal = position[:, None] >= position[None, :]
    flat = (cand_dev, cand_len, half_width)

    def pair(left, right):
        return jnp.einsum(
            "ctk,csk->cts", left.reshape(flat), right.reshape(flat),
            preferred_element_type=jnp.float32,
        )

    weight_sum = pair(decayed_g, x_high) + pair(decayed_g, x_low) + pair(g_low, x_high)
    weight_sum = jnp.where(causal[None], weight_sum, 0.0)
    db_part = jnp.einsum(
        "cts,ctn->csn", weight_sum, c_cand.astype(jnp.float32), precision=lax.Precision.HIGHEST
    )
    dc_part = jnp.einsum(
        "cts,csn->ctn", weight_sum, b_cand.astype(jnp.float32), precision=lax.Precision.HIGHEST
    )

    scores = jnp.einsum("ctn,csn->cts", c_cand, b_cand, preferred_element_type=jnp.float32)
    amp_t = jnp.transpose(amplitude, (0, 2, 1))
    inv_t = jnp.transpose(inverse, (0, 2, 1))
    decay_mat = amp_t[:, :, :, None] * inv_t[:, :, None, :]
    kernel = jnp.where(causal[None, None], scores[:, None] * decay_mat, 0.0).astype(jnp.bfloat16)
    dx_cand = jnp.einsum("chts,cthp->cshp", kernel, g_heads, preferred_element_type=jnp.float32)
    dx_cand = dx_cand.astype(jnp.bfloat16).reshape(flat)

    dc_state = jnp.dot(
        decayed_g.reshape(cand_dev * cand_len, half_width),
        init_half.reshape(half_width, nstate),
        preferred_element_type=jnp.float32,
    )
    dc_total = dc_part + dc_state.reshape(cand_dev, cand_len, nstate)
    db_cand = lax.psum_scatter(db_part, "seq", scatter_dimension=1, tiled=True)
    dc_cand = lax.psum_scatter(dc_total, "seq", scatter_dimension=1, tiled=True)

    dx_prefix = jnp.einsum(
        "jhn,hpn->jhp", weighted_b, grad_state, preferred_element_type=jnp.float32
    )
    dx_prefix = dx_prefix.astype(jnp.bfloat16).reshape(pre_len, width)
    projected = jnp.einsum("jhp,hpn->jhn", x_heads, grad_state, preferred_element_type=jnp.float32)
    db_prefix = jnp.sum(projected * weight[:, :, None], axis=1)
    return (dx_prefix, db_prefix, dx_cand, db_cand, dc_cand)


def solution(mesh):
    return jax.shard_map(
        shards,
        mesh=mesh,
        in_specs=(
            P(("grp", "cand", "seq"), None),
            P(("grp", "cand", "seq"), None),
            P(("grp", "cand", "seq"), None),
            P(("grp", "cand"), None, "seq"),
            P(("grp", "cand"), None, None),
            P(("grp", "cand"), None, None),
            P(("grp", "cand"), None, "seq"),
            P(("grp", "cand")),
            P(("grp", "cand"), None, "seq"),
        ),
        out_specs=(
            P(("grp", "cand", "seq"), None),
            P(("grp", "cand", "seq"), None),
            P(("grp", "cand"), None, "seq"),
            P(("grp", "cand"), "seq", None),
            P(("grp", "cand"), "seq", None),
        ),
        check_vma=False,
    )
```

time: 396 us -> 192 us (0.48)
  matrix products: 136 us -> 31.4 us
  waiting for transfers between devices: 92.8 us -> 0.05 us
  blocking collectives: 79.7 us -> 115 us
  other arithmetic: 36.7 us -> 8.66 us
  local copies, waits for them, and re-layouts: 28.1 us -> 21.1 us
    dot_general x86 -> x7, matrix products: 127 us -> 19 us  [the longest x1 7.77 us: shards(): jnp.einsum('chts,cthp->cshp', kernel, g_heads, preferred_element_type=jnp...]
    all_gather x1 -> x0, waiting for transfers between devices: 92.7 us -> none  [entering(): everything = jax.tree.map(lambda part: lax.all_gather(part, axis), shard)]
    psum x1, blocking collectives: 42.5 us -> 78.3 us  [shards(): grad_half = lax.psum(dstate, 'cand').astype(jnp.bfloat16)]
    select_n x33 -> x0, other arithmetic: 27.4 us -> none  [the longest x32 26.3 us: turn(): return jax.tree.map(lambda a, b: jnp.where(reached, a, b), new, before)]
    unnamed x35, local copies, waits for them, and re-layouts: 10.9 us -> 19 us
    dynamic_slice x49 -> x0, local copies, waits for them, and re-layouts: 7.23 us -> none  [the longest x8 5.79 us: shards(): lax.map(run_candidate, (x_cand, g_cand, b_cand, c_cand, level_all))]
    squeeze x2 -> x0, local copies, waits for them, and re-layouts: 4.93 us -> none  [shards(): lax.map(run_candidate, (x_cand, g_cand, b_cand, c_cand, level_all))]
  transfers between devices with their start and end apart: 4 -> 3, of which waited for: 1 -> 0; matrix products, arithmetic and copies ran while one was open for 42% -> 27% of each run, Pallas kernels for 0% -> 0%
where the time goes in v1:
time: 192 us
  blocking collectives  115 us (60%)
  matrix products  31.4 us (16%)
  local copies, waits for them, and re-layouts  21.1 us (11%)
  between operations  14.7 us (8%)
  other arithmetic  8.66 us (5%)
    psum x1, blocking collectives, shards(): grad_half = lax.psum(dstate, 'cand').astype(jnp.bfloat16)  78.3 us
    unnamed x1, blocking collectives  34.9 us
    unnamed x35, local copies, waits for them, and re-layouts  19 us
    dot_general x1, matrix products, shards(): jnp.einsum('chts,cthp->cshp', kernel, g_heads, preferred_element_type=jnp...  7.77 us
    dot_general x3, matrix products, pair(): jnp.einsum('ctk,csk->cts', left.reshape(flat), right.reshape(flat), prefe...  4.97 us
  transfers between devices with their start and end apart: 3, of which 0 were waited for; matrix products, arithmetic and copies ran while one was open for 27% of the time, Pallas kernels for 0%

profile of v1, /device:TPU:0, one launch (start us, length us, event | category | flops | bytes accessed | tf_op | source)
XLA Modules:
  0.0 191.7 jit_solution(8660132420747086920)
XLA Ops:
  7.2 0.0 copy-start
  7.2 0.0 copy-start.10
  7.2 0.0 reduce-scatter.6.cloned.1.call-start
  7.2 0.9 fusion.26
  8.2 1.2 dynamic-slice
  10.1 0.2 dynamic-update-slice
  10.3 34.9 %all-reduce = f32[640]{0:T(1024)S(1)} all-reduce(f32[640]{0:T(1024)S(1)} %dynamic-update-slice), channel_id=2, replica_groups=mesh['grp'=2,'cand'=8,'seq'=2] {'cand','seq'}, use_global_device_ids=true, to_apply=%add | all-reduce | flops 640 | bytes 5120
  45.3 0.1 reshape.137
  45.4 0.6 reduce-window.16
  46.0 0.2 slice_reduce_fusion.1
  46.2 1.6 copy.89
  47.8 0.0 copy-done.10
  47.8 0.0 copy-start.4
  47.8 0.0 copy-start.9
  47.8 0.1 copy.87
  47.9 0.0 copy-start.8
  47.9 0.1 select_reduce_fusion
  48.0 0.1 fusion.24
  48.1 0.0 copy-start.11
  48.1 0.8 copy-done.11
  48.9 2.1 %fusion.19 = f32[40,64,128]{2,1,0:T(8,128)} fusion(bf16[256,40,64]{0,2,1:T(8,128)(2,1)S(1)} %bitcast.88, f32[256,128]{0,1:T(8,128)S(1)} %copy.87, f32[256,40]{0,1:T(8,128)S(1)} %fusion.24), kind=kOutput, calls=%fused_computation.31 | convolution fusion | flops 170393600 | bytes 2793472 | tf_op jit(solution)/shard_map/jhp,jhn->hpn/dot_general | solution.py:36
  51.0 0.0 reduce-scatter.6.cloned.1.call-update
  51.0 0.0 copy-done.4
  51.0 0.0 reduce-scatter.4.cloned.1.call-start
  51.1 0.1 log-plus-one_bitcast_fusion
  51.2 0.0 copy-done.8
  51.2 0.1 reshape.129
  51.4 2.3 %reduce-window.14 = f32[2,20,4,128]{3,1,2,0:T(8,128)S(1)} reduce-window(f32[2,20,4,128]{3,1,2,0:T(8,128)S(1)} %copy.82, f32[]{:T(128)} %constant.11.clone.1), window={size=1x1x1x128 pad=0_0x0_0x0_0x127_0}, to_apply=%region_0.0 | reduce-window | flops 2600960 | bytes 163844 | tf_op jit(solution)/shard_map/reduce-window
  53.7 0.2 slice_reduce_fusion
  53.9 0.1 negate_exponential_fusion
  54.0 0.1 exp.29
  54.2 0.1 exp.34
  54.3 3.1 %copy.81 = bf16[2,512,1280]{1,2,0:T(8,128)(2,1)S(1)} copy(bf16[2,512,1280]{2,1,0:T(8,128)(2,1)} %param.17) | data formatting | bytes 5242880 | tf_op args[8]
  57.3 0.0 copy-start.12
  57.3 4.4 %copy.93 = bf16[2,512,1280]{1,2,0:T(8,128)(2,1)} copy(bf16[2,512,1280]{2,1,0:T(8,128)(2,1)} %param.12) | data formatting | bytes 5242880 | tf_op args[3]
  61.7 0.1 iota_compare_fusion.1
  61.8 3.5 %fusion.6 = (bf16[2,512,1280]{1,2,0:T(8,128)(2,1)S(1)}, bf16[2,512,1280]{1,2,0:T(8,128)(2,1)S(1)}, bf16[2,512,1280]{1,2,0:T(8,128)(2,1)S(1)}, bf16[2,512,1280]{1,2,0:T(8,128)(2,1)S(1)}) fusion(f32[2,512,20]{1,2,0:T(8,128)S(1)} %copy.84, bf16[2,512,1280]{1,2,0:T(8,128)(2,1)S(1)} %copy.81, pred[2,512]{1,0:T(4,128)(4,1)S(1)} %iota_compare_fusion.1, ...), kind=kLoop, calls=%fused_computation.11 | loop fusion | flops 15728640 | bytes 15893504 | tf_op jit(solution)/shard_map/convert_element_type | solution.py:11
  65.3 0.0 copy-start.1
  65.4 0.6 reduce-precision_convert_fusion.1
  66.0 0.8 copy-done.1
  66.8 0.1 iota_compare_fusion
  66.9 1.6 fusion.29
  68.5 1.6 fusion.30
  70.1 1.8 add_select_fusion
  71.9 2.6 %fusion.31 = f32[2,512,128]{2,1,0:T(8,128)} fusion(f32[2,512,512]{2,1,0:T(8,128)S(1)} %add_select_fusion, bf16[2,512,128]{2,1,0:T(8,128)(2,1)S(1)} %copy-done), kind=kOutput, calls=%fused_computation.58 | convolution fusion | flops 805306368 | bytes 2883584 | tf_op jit(solution)/shard_map/cts,ctn->csn/dot_general | solution.py:67
  74.6 0.0 reduce-scatter.4.cloned.1.call-update
  74.6 0.2 reduce-scatter.8.cloned.1.call-start
  74.8 0.0 copy-start.6
  74.8 3.5 %fusion.20 = f32[20,64,128]{2,1,0:T(8,128)} fusion(bf16[2,512,20,64]{1,3,2,0:T(8,128)(2,1)} %bitcast.85, f32[2,512,20]{1,2,0:T(8,128)S(1)} %copy.84, bf16[2,512,128]{2,1,0:T(8,128)(2,1)S(1)} %copy-done), kind=kOutput, calls=%fused_computation.32 | convolution fusion | flops 340787200 | bytes 3620864 | tf_op jit(solution)/shard_map/cthp,ctn->hpn/dot_general | solution.py:52
  78.3 1.7 fusion.28
  80.1 0.6 copy.90
  80.7 0.7 copy.92
  81.4 1.9 fusion.32
  83.3 78.3 %all-reduce.3 = (bf16[20,64,128]{2,1,0:T(8,128)(2,1)}, bf16[20,64,128]{2,1,0:T(8,128)(2,1)S(1)}) all-reduce(f32[20,64,128]{2,1,0:T(8,128)} %fusion.20, f32[20,64,128]{2,1,0:T(8,128)} %reduce-scatter.6.cloned.1.call-done), channel_id=1, replica_groups=mesh['grp'=2,'cand'=8,'seq'=2] {'cand'}, use_global_device_ids=true, to_apply=%region_2.3 | all-reduce | flops 327680 | bytes 1966080 | tf_op jit(solution)/shard_map/psum | solution.py:53
  161.6 3.5 %convolution_add_fusion = f32[2,512,128]{2,1,0:T(8,128)} fusion(f32[2,512,128]{2,1,0:T(8,128)} %fusion.32, bf16[2,512,1280]{1,2,0:T(8,128)(2,1)} %copy-done.3, bf16[1280,128,1]{1,0,2:T(8,128)(2,1)S(1)} %bitcast.93), kind=kOutput, calls=%fused_computation.33 | convolution fusion | flops 335675392 | bytes 3997696 | tf_op jit(solution)/shard_map/dot_general | solution.py:82
  165.1 0.0 reduce-scatter.8.cloned.1.call-update
  165.1 7.8 %fusion.17 = bf16[2,20,64,512]{3,2,1,0:T(8,128)(2,1)} fusion(bf16[2,512,20,64]{1,3,2,0:T(8,128)(2,1)S(1)} %bitcast.86, f32[2,20,512]{2,1,0:T(8,128)} %copy.92, f32[2,20,512]{2,1,0:T(8,128)} %copy.90, f32[2,512,512]{2,1,0:T(8,128)} %fusion.28, pred[512,512]{1,0:T(8,128)(4,1)S(1)} %iota_compare_fusion), kind=kOutput, calls=%fused_computation.29 | convolution fusion | flops 1385431040 | bytes 7766016 | tf_op jit(solution)/shard_map/chts,cthp->cshp/dot_general | solution.py:79
  172.9 4.4 %copy.106 = bf16[2,512,1280]{2,1,0:T(8,128)(2,1)} copy(bf16[2,512,1280]{1,2,0:T(8,128)(2,1)} %bitcast.87) | data formatting | bytes 5242880
  177.3 2.3 %all_gather.7 = bf16[40,64,128]{2,1,0:T(8,128)(2,1)S(1)} all-gather(bf16[20,64,128]{2,1,0:T(8,128)(2,1)S(1)} %copy-done.7), channel_id=1, replica_groups=mesh['grp'=2,'cand'=8,'seq'=2] {'seq'}, dimensions={0}, use_global_device_ids=true | all-gather | bytes 983040 | tf_op jit(solution)/shard_map/all_gather | solution.py:54
  179.6 1.5 fusion.18
  181.1 1.6 copy.104
  182.7 0.0 copy-done.5
  182.7 1.7 fusion.8
  184.4 0.8 copy.105
  (27 shorter events, 0.2 us)
Async XLA Ops:
  7.2 64.7 %copy-start = (bf16[2,512,128]{2,1,0:T(8,128)(2,1)S(1)}, bf16[2,512,128]{2,1,0:T(8,128)(2,1)}, u32[]{:S(2)}) copy-start(bf16[2,512,128]{2,1,0:T(8,128)(2,1)} %param.14) | copy-start | bytes 786436
  7.2 40.6 %copy-start.10 = (bf16[256,128]{1,0:T(8,128)(2,1)S(1)}, bf16[256,128]{1,0:T(8,128)(2,1)}, u32[]{:S(2)}) copy-start(bf16[256,128]{1,0:T(8,128)(2,1)} %param.10) | copy-start | bytes 196612
  7.2 76.1 %reduce-scatter.6.cloned.1.call-start = ((), (), s32[]{:S(2)}) async-start(), calls=%async_computation.4 | async-start | bytes 1966080 | tf_op jit(solution)/shard_map/reduce_scatter | solution.py:37
  47.8 3.2 %copy-start.4 = (bf16[256,2560]{0,1:T(8,128)(2,1)}, bf16[256,2560]{0,1:T(8,128)(2,1)S(1)}, u32[]{:S(2)}) copy-start(bf16[256,2560]{0,1:T(8,128)(2,1)S(1)} %copy.89) | copy-start | bytes 3932164
  47.8 3.3 %copy-start.9 = (s32[2,512,20]{1,0,2:T(2,128)S(1)}, s32[2,512,20]{1,0,2:T(2,128)}, u32[]{:S(2)}) copy-start(s32[2,512,20]{1,0,2:T(2,128)} %param.15) | copy-start | bytes 245764
  47.9 3.3 %copy-start.8 = (f32[256,128]{0,1:T(8,128)}, f32[256,128]{0,1:T(8,128)S(1)}, u32[]{:S(2)}) copy-start(f32[256,128]{0,1:T(8,128)S(1)} %copy.87) | copy-start | bytes 393220
  48.1 0.8 copy-start.11
  51.0 134.1 %reduce-scatter.4.cloned.1.call-start = ((), (), s32[]{:S(2)}) async-start(), calls=%async_computation.3 | async-start | bytes 786432 | tf_op jit(solution)/shard_map/reduce_scatter | solution.py:88
  57.3 4.4 %copy-start.12 = (s32[2]{0:T(128)S(1)}, s32[2]{0:T(128)}, u32[]{:S(2)}) copy-start(s32[2]{0:T(128)} %param.16) | copy-start | bytes 28
  65.3 1.5 copy-start.1
  66.8 1.7 copy-start.3
  74.6 110.6 %reduce-scatter.8.cloned.1.call-start = ((), (), s32[]{:S(2)}) async-start(), calls=%async_computation.5 | async-start | bytes 786432 | tf_op jit(solution)/shard_map/reduce_scatter | solution.py:89
  74.8 3.5 %copy-start.6 = (bf16[2,512,128]{2,1,0:T(8,128)(2,1)S(1)}, bf16[2,512,128]{2,1,0:T(8,128)(2,1)}, u32[]{:S(2)}) copy-start(bf16[2,512,128]{2,1,0:T(8,128)(2,1)} %param.13) | copy-start | bytes 786436
  83.3 81.8 %copy-start.2 = (bf16[2,512,1280]{1,2,0:T(8,128)(2,1)S(1)}, bf16[2,512,1280]{1,2,0:T(8,128)(2,1)}, u32[]{:S(2)}) copy-start(bf16[2,512,1280]{1,2,0:T(8,128)(2,1)} %copy-done.1) | copy-start | bytes 7864324
  172.9 4.4 %copy-start.7 = (bf16[20,64,128]{2,1,0:T(8,128)(2,1)S(1)}, bf16[20,64,128]{2,1,0:T(8,128)(2,1)}, u32[]{:S(2)}) copy-start(bf16[20,64,128]{2,1,0:T(8,128)(2,1)} %get-tuple-element.25) | copy-start | bytes 983044
  179.6 3.1 %copy-start.5 = (bf16[256,2560]{0,1:T(8,128)(2,1)S(1)}, bf16[256,2560]{0,1:T(8,128)(2,1)}, u32[]{:S(2)}) copy-start(bf16[256,2560]{0,1:T(8,128)(2,1)} %copy-done.4) | copy-start | bytes 3932164
Sparse Core Ops, SparseCore 0:
  51.2 6.0 reduce-scatter.5
  74.7 5.2 reduce-scatter.3
  165.2 7.1 reduce-scatter.7

commit v2 on v1

--- a/solution.py
+++ b/solution.py
@@ -23,10 +23,11 @@
 
     log_prefix = jnp.log1p(-code_prefix.astype(jnp.float32) * 1e-06)
     own_total = jnp.sum(log_prefix, axis=0)
-    totals = lax.all_gather(own_total, pre_axes)
+    shard_count = lax.axis_size(pre_axes)
     mine = lax.axis_index(pre_axes)
-    shard_at = jnp.arange(totals.shape[0], dtype=jnp.int32)
-    later_total = jnp.sum(jnp.where((shard_at > mine)[:, None], totals, 0.0), axis=0)
+    shard_at = jnp.arange(shard_count, dtype=jnp.int32)
+    rows = jnp.where((shard_at < mine)[:, None], own_total[None, :], 0.0)
+    later_total = lax.psum_scatter(rows, pre_axes, scatter_dimension=0, tiled=True)[0]
     after_local = own_total[None, :] - jnp.cumsum(log_prefix, axis=0)
     weight = jnp.exp(after_local + later_total[None, :])
     weighted_b = (weight[:, :, None] * b_prefix[:, None, :].astype(jnp.float32)).astype(
@@ -34,8 +35,14 @@
     )
     x_heads = x_prefix.reshape(pre_len, heads_total, head_size)
     state_full = jnp.einsum("jhp,jhn->hpn", x_heads, weighted_b, preferred_element_type=jnp.float32)
-    init_part = lax.psum_scatter(state_full, "seq", scatter_dimension=0, tiled=True)
-    init_half = lax.psum(init_part, "cand").astype(jnp.bfloat16)
+    cand_count = lax.axis_size("cand")
+    seq_count = lax.axis_size("seq")
+    piece = head_size // cand_count
+    state_pieces = state_full.reshape(seq_count, half_heads, cand_count, piece, nstate)
+    state_pieces = jnp.transpose(state_pieces, (2, 0, 1, 3, 4)).reshape(-1, piece, nstate)
+    init_piece = lax.psum_scatter(state_pieces, pre_axes, scatter_dimension=0, tiled=True)
+    init_pieces = lax.all_gather(init_piece.astype(jnp.bfloat16), "cand")
+    init_half = jnp.transpose(init_pieces, (1, 0, 2, 3)).reshape(half_heads, head_size, nstate)
 
     position = jnp.arange(cand_len, dtype=jnp.int32)
     valid_rows = position[None, :] < lengths[:, None] * BLOCK
@@ -50,8 +57,12 @@
     x_high, x_low = split_bf16(xc_heads.astype(jnp.float32) * inverse[:, :, :, None])
 
     dstate = jnp.einsum("cthp,ctn->hpn", decayed_g, c_cand, preferred_element_type=jnp.float32)
-    grad_half = lax.psum(dstate, "cand").astype(jnp.bfloat16)
-    grad_state = lax.all_gather(grad_half, "seq", axis=0, tiled=True)
+    dstate_pieces = dstate.reshape(half_heads, cand_count, piece, nstate)
+    dstate_pieces = jnp.transpose(dstate_pieces, (1, 0, 2, 3)).reshape(-1, piece, nstate)
+    grad_piece = lax.psum_scatter(dstate_pieces, "cand", scatter_dimension=0, tiled=True)
+    grad_pieces = lax.all_gather(grad_piece.astype(jnp.bfloat16), pre_axes)
+    grad_pieces = grad_pieces.reshape(cand_count, seq_count, half_heads, piece, nstate)
+    grad_state = jnp.transpose(grad_pieces, (1, 2, 0, 3, 4)).reshape(heads_total, head_size, nstate)
 
     causal = position[:, None] >= position[None, :]
     flat = (cand_dev, cand_len, half_width)

time: 192 us -> 206 us (1.073)
  waiting for transfers between devices: 0.05 us -> 40.7 us
  blocking collectives: 115 us -> 88.2 us
  other arithmetic: 8.66 us -> 13.8 us
  matrix products: 31.4 us -> 27.7 us
    psum x1 -> x0, blocking collectives: 78.3 us -> none  [shards(): grad_half = lax.psum(dstate, 'cand').astype(jnp.bfloat16)]
    all_gather x1 -> x2, blocking collectives: 2.26 us -> 52.8 us  [the longest x1 31.6 us: shards(): init_pieces = lax.all_gather(init_piece.astype(jnp.bfloat16), 'cand')]
    reduce_scatter x1 -> x2, waiting for transfers between devices: 0.01 us -> 40.6 us  [the longest x1 24.3 us: shards(): lax.psum_scatter(state_pieces, pre_axes, scatter_dimension=0, tiled=True)]
    convert_element_type x1 -> x2, other arithmetic: 3.52 us -> 7.54 us  [split_bf16(): low = (value - high).astype(jnp.bfloat16)]
    dot_general x1, matrix products: 3.51 us -> 0.84 us  [shards(): jnp.einsum('cthp,ctn->hpn', decayed_g, c_cand, preferred_element_type=jnp...]
    unnamed x35 -> x37, local copies, waits for them, and re-layouts: 19 us -> 16.4 us
  transfers between devices with their start and end apart: 3 -> 4, of which waited for: 0 -> 2; matrix products, arithmetic and copies ran while one was open for 27% -> 26% of each run, Pallas kernels for 0% -> 0%
where the time goes in v2:
time: 206 us; the launch traced here: 205 us
  blocking collectives  88.2 us (43%)
  waiting for transfers between devices  40.7 us (20%)
  matrix products  27.7 us (13%)
  local copies, waits for them, and re-layouts  20.2 us (10%)
  between operations  14.2 us (7%)
  other arithmetic  13.8 us (7%)
    unnamed x1, blocking collectives  35.4 us
    all_gather x1, blocking collectives, shards(): init_pieces = lax.all_gather(init_piece.astype(jnp.bfloat16), 'cand')  31.6 us
    reduce_scatter x1, waiting for transfers between devices, shards(): lax.psum_scatter(state_pieces, pre_axes, scatter_dimension=0, tiled=True)  24.3 us
    all_gather x1, blocking collectives, shards(): grad_pieces = lax.all_gather(grad_piece.astype(jnp.bfloat16), pre_axes)  21.2 us
    unnamed x37, local copies, waits for them, and re-layouts  16.4 us
    reduce_scatter x1, waiting for transfers between devices, shards(): lax.psum_scatter(dstate_pieces, 'cand', scatter_dimension=0, tiled=True)  16.3 us
    dot_general x1, matrix products, shards(): jnp.einsum('chts,cthp->cshp', kernel, g_heads, preferred_element_type=jnp...  7.72 us
    convert_element_type x2, other arithmetic, split_bf16(): low = (value - high).astype(jnp.bfloat16)  7.54 us
  transfers between devices with their start and end apart: 4, of which 2 were waited for; matrix products, arithmetic and copies ran while one was open for 26% of the time, Pallas kernels for 0%

profile of v2, /device:TPU:0, one launch (start us, length us, event | category | flops | bytes accessed | tf_op | source)
XLA Modules:
  0.0 205.1 jit_solution(7269176251271718075)
XLA Ops:
  7.2 0.0 copy-start
  7.2 0.0 copy-start.14
  7.2 0.0 reduce-scatter.9.cloned.1.call-start
  7.3 0.9 fusion.29
  8.2 0.1 broadcast_select_fusion.1
  8.3 35.4 %all-reduce = f32[16,40]{1,0:T(8,128)S(1)} all-reduce(f32[16,40]{1,0:T(8,128)S(1)} %broadcast_select_fusion.1), channel_id=5, replica_groups=mesh['grp'=2,'cand'=8,'seq'=2] {'cand','seq'}, use_global_device_ids=true, to_apply=%region_6.7.clone | all-reduce | flops 640 | bytes 5120
  43.7 0.6 reduce-window.16
  44.3 0.2 slice_reduce_fusion.1
  44.5 1.6 copy.70
  46.2 0.1 copy.68
  46.3 0.0 copy-start.9
  46.3 0.8 dynamic-slice
  47.1 0.7 dynamic-slice_bitcast_fusion
  47.7 0.1 fusion.27
  47.9 1.0 fusion.9
  48.9 0.0 copy-start.10
  48.9 0.0 copy-start.5
  48.9 1.2 copy.84
  50.1 0.0 reduce-scatter.9.cloned.1.call-update
  50.1 0.0 reduce-scatter.5.cloned.1.call-start
  50.2 0.1 log-plus-one_bitcast_fusion
  50.3 0.1 reshape.142
  50.5 2.3 %reduce-window.14 = f32[2,20,4,128]{3,1,2,0:T(8,128)S(1)} reduce-window(f32[2,20,4,128]{3,1,2,0:T(8,128)S(1)} %copy.59, f32[]{:T(128)} %constant.11.clone.1), window={size=1x1x1x128 pad=0_0x0_0x0_0x127_0}, to_apply=%region_0.0 | reduce-window | flops 2600960 | bytes 163844 | tf_op jit(solution)/shard_map/reduce-window
  52.8 0.2 slice_reduce_fusion
  53.0 0.1 negate_exponential_fusion
  53.1 0.1 exp.29
  53.2 0.0 copy-start.13
  53.3 2.6 %copy.58 = bf16[2,512,1280]{1,2,0:T(8,128)(2,1)} copy(bf16[2,512,1280]{2,1,0:T(8,128)(2,1)S(1)} %copy-done.5) | data formatting | bytes 5242880 | tf_op args[8]
  55.9 0.1 iota_compare_fusion.1
  56.0 4.5 %fusion.6 = (bf16[2,512,1280]{1,2,0:T(8,128)(2,1)}, bf16[2,512,1280]{1,2,0:T(8,128)(2,1)S(1)}) fusion(f32[2,512,20]{1,2,0:T(8,128)S(1)} %copy.61, bf16[2,512,1280]{1,2,0:T(8,128)(2,1)} %copy.58, pred[2,512]{1,0:T(4,128)(4,1)S(1)} %iota_compare_fusion.1), kind=kLoop, calls=%fused_computation.11 | loop fusion | flops 7864320 | bytes 7947264 | tf_op jit(solution)/shard_map/convert_element_type | solution.py:11
  60.4 0.8 fusion.21
  61.3 0.9 copy.64
  62.2 0.0 reduce-scatter.5.cloned.1.call-update
  62.2 0.2 reduce-scatter.7.cloned.1.call-start
  62.4 0.1 iota_compare_fusion
  62.5 0.1 exp.34
  62.6 4.4 %copy.74 = bf16[2,512,1280]{1,2,0:T(8,128)(2,1)} copy(bf16[2,512,1280]{2,1,0:T(8,128)(2,1)} %param.12) | data formatting | bytes 5242880 | tf_op args[3]
  67.1 3.1 %fusion.7 = (bf16[2,512,1280]{1,2,0:T(8,128)(2,1)S(1)}, bf16[2,512,1280]{1,2,0:T(8,128)(2,1)S(1)}, bf16[2,512,1280]{1,2,0:T(8,128)(2,1)S(1)}) fusion(bf16[2,512,1280]{1,2,0:T(8,128)(2,1)} %copy.74, f32[2,512,20]{1,2,0:T(8,128)S(1)} %copy.75, f32[2,512,20]{1,2,0:T(8,128)S(1)} %copy.61, bf16[2,512,1280]{1,2,0:T(8,128)(2,1)S(1)} %get-tuple-element.21), kind=kLoop, calls=%fused_computation.12 | loop fusion | flops 13107200 | bytes 13271040 | tf_op jit(solution)/shard_map/convert_element_type | solution.py:11
  70.2 1.6 fusion.32
  71.8 0.0 copy-start.4
  71.8 1.6 fusion.33
  73.3 0.2 copy-done.4
  73.5 1.8 add_select_fusion
  75.3 2.6 %fusion.34 = f32[2,512,128]{2,1,0:T(8,128)} fusion(f32[2,512,512]{2,1,0:T(8,128)S(1)} %add_select_fusion, bf16[2,512,128]{2,1,0:T(8,128)(2,1)S(1)} %copy-done), kind=kOutput, calls=%fused_computation.59 | convolution fusion | flops 805306368 | bytes 2883584 | tf_op jit(solution)/shard_map/cts,ctn->csn/dot_general | solution.py:78
  78.0 0.0 reduce-scatter.7.cloned.1.call-update
  78.0 0.0 reduce-scatter.11.cloned.1.call-start
  78.1 1.8 fusion.31
  79.8 1.9 fusion.35
  81.7 24.3 %reduce-scatter.9.cloned.1.call-done = f32[20,8,128]{2,1,0:T(8,128)} async-done(((f32[320,8,128]{2,1,0:T(8,128)}), f32[20,8,128]{2,1,0:T(8,128)}) %reduce-scatter.9.cloned.1.call-update) | async-done | bytes 81936 | tf_op jit(solution)/shard_map/reduce_scatter | solution.py:43
  106.0 0.9 convert_element_type.88
  106.9 31.6 %all-gather.1 = bf16[160,8,128]{2,1,0:T(8,128)(2,1)S(1)} all-gather(bf16[20,8,128]{2,1,0:T(8,128)(2,1)S(1)} %convert_element_type.88), channel_id=3, replica_groups=mesh['grp'=2,'cand'=8,'seq'=2] {'cand'}, dimensions={0}, use_global_device_ids=true | all-gather | bytes 368640 | tf_op jit(solution)/shard_map/all_gather | solution.py:44
  138.5 0.1 copy.85
  138.6 3.7 %convolution_add_fusion = f32[2,512,128]{2,1,0:T(8,128)} fusion(f32[2,512,128]{2,1,0:T(8,128)} %fusion.35, bf16[2,512,1280]{1,2,0:T(8,128)(2,1)} %copy-done.3, bf16[1280,128,1]{1,0,2:T(8,128)(2,1)S(1)} %bitcast.124), kind=kOutput, calls=%fused_computation.33 | convolution fusion | flops 335675392 | bytes 3997696 | tf_op jit(solution)/shard_map/dot_general | solution.py:93
  142.3 0.0 reduce-scatter.11.cloned.1.call-update
  142.3 7.7 %fusion.19 = bf16[2,20,64,512]{3,2,1,0:T(8,128)(2,1)} fusion(bf16[2,512,20,64]{1,3,2,0:T(8,128)(2,1)S(1)} %bitcast.114, f32[2,20,512]{2,1,0:T(8,128)S(1)} %copy.73, f32[2,20,512]{2,1,0:T(8,128)S(1)} %copy.71, f32[2,512,512]{2,1,0:T(8,128)} %fusion.31, pred[512,512]{1,0:T(8,128)(4,1)S(1)} %iota_compare_fusion), kind=kOutput, calls=%fused_computation.30 | convolution fusion | flops 1385431040 | bytes 7766016 | tf_op jit(solution)/shard_map/chts,cthp->cshp/dot_general | solution.py:90
  150.0 4.4 %copy.89 = bf16[2,512,1280]{2,1,0:T(8,128)(2,1)} copy(bf16[2,512,1280]{1,2,0:T(8,128)(2,1)} %bitcast.116) | data formatting | bytes 5242880
  154.4 16.3 %reduce-scatter.5.cloned.1.call-done = f32[20,8,128]{2,1,0:T(8,128)} async-done(((f32[160,8,128]{2,1,0:T(8,128)}), f32[20,8,128]{2,1,0:T(8,128)}) %reduce-scatter.5.cloned.1.call-update) | async-done | bytes 81936 | tf_op jit(solution)/shard_map/reduce_scatter | solution.py:62
  170.7 0.9 convert_element_type.73
  171.6 21.2 %all-gather = bf16[320,8,128]{2,1,0:T(8,128)(2,1)S(1)} all-gather(bf16[20,8,128]{2,1,0:T(8,128)(2,1)S(1)} %convert_element_type.73), channel_id=2, replica_groups=mesh['grp'=2,'cand'=8,'seq'=2] {'cand','seq'}, dimensions={0}, use_global_device_ids=true | all-gather | bytes 696320 | tf_op jit(solution)/shard_map/all_gather | solution.py:63
  192.8 0.2 copy.65
  193.0 1.5 fusion.20
  194.5 1.6 copy.87
  196.1 1.7 fusion.8
  197.8 0.8 copy.88
  (38 shorter events, 0.3 us)
Async XLA Ops:
  7.2 53.3 %copy-start = (bf16[2,512,128]{2,1,0:T(8,128)(2,1)S(1)}, bf16[2,512,128]{2,1,0:T(8,128)(2,1)}, u32[]{:S(2)}) copy-start(bf16[2,512,128]{2,1,0:T(8,128)(2,1)} %param.14) | copy-start | bytes 786436
  7.2 39.1 %copy-start.14 = (u32[32]{0:T(128)S(1)}, u32[32]{0:T(128)}, u32[]{:S(2)}) copy-start(u32[32]{0:T(128)} %constant.33) | copy-start | bytes 388
  7.2 39.0 %copy-start.11 = (bf16[256,128]{1,0:T(8,128)(2,1)S(1)}, bf16[256,128]{1,0:T(8,128)(2,1)}, u32[]{:S(2)}) copy-start(bf16[256,128]{1,0:T(8,128)(2,1)} %param.10) | copy-start | bytes 196612
  7.2 98.8 %reduce-scatter.9.cloned.1.call-start = ((), (), s32[]{:S(2)}) async-start(), calls=%async_computation.6 | async-start | bytes 1392640 | tf_op jit(solution)/shard_map/reduce_scatter | solution.py:43
  46.2 2.7 %copy-start.6 = (bf16[256,2560]{0,1:T(8,128)(2,1)}, bf16[256,2560]{0,1:T(8,128)(2,1)S(1)}, u32[]{:S(2)}) copy-start(bf16[256,2560]{0,1:T(8,128)(2,1)S(1)} %copy.70) | copy-start | bytes 3932164
  46.3 2.6 %copy-start.9 = (f32[256,128]{0,1:T(8,128)}, f32[256,128]{0,1:T(8,128)S(1)}, u32[]{:S(2)}) copy-start(f32[256,128]{0,1:T(8,128)S(1)} %copy.68) | copy-start | bytes 393220
  47.8 2.3 %copy-start.12 = (f32[256,40]{0,1:T(8,128)}, f32[256,40]{0,1:T(8,128)S(1)}, u32[]{:S(2)}) copy-start(f32[256,40]{0,1:T(8,128)S(1)} %fusion.27) | copy-start | bytes 122884
  48.9 1.3 copy-start.10
  48.9 4.3 %copy-start.5 = (bf16[2,512,1280]{2,1,0:T(8,128)(2,1)S(1)}, bf16[2,512,1280]{2,1,0:T(8,128)(2,1)}, u32[]{:S(2)}) copy-start(bf16[2,512,1280]{2,1,0:T(8,128)(2,1)} %param.17) | copy-start | bytes 7864324
  50.1 120.5 %reduce-scatter.5.cloned.1.call-start = ((), (), s32[]{:S(2)}) async-start(), calls=%async_computation.4 | async-start | bytes 737280 | tf_op jit(solution)/shard_map/reduce_scatter | solution.py:62
  53.2 2.6 %copy-start.13 = (s32[2]{0:T(128)S(1)}, s32[2]{0:T(128)}, u32[]{:S(2)}) copy-start(s32[2]{0:T(128)} %param.16) | copy-start | bytes 28
  60.4 6.7 %copy-start.1 = (bf16[2,512,1280]{1,2,0:T(8,128)(2,1)}, bf16[2,512,1280]{1,2,0:T(8,128)(2,1)S(1)}, u32[]{:S(2)}) copy-start(bf16[2,512,1280]{1,2,0:T(8,128)(2,1)S(1)} %get-tuple-element.21) | copy-start | bytes 7864324
  62.2 136.4 %reduce-scatter.7.cloned.1.call-start = ((), (), s32[]{:S(2)}) async-start(), calls=%async_computation.5 | async-start | bytes 786432 | tf_op jit(solution)/shard_map/reduce_scatter | solution.py:99
  70.2 1.6 copy-start.3
  71.8 1.7 copy-start.4
  75.3 2.8 %copy-start.8 = (bf16[2,512,128]{2,1,0:T(8,128)(2,1)S(1)}, bf16[2,512,128]{2,1,0:T(8,128)(2,1)}, u32[]{:S(2)}) copy-start(bf16[2,512,128]{2,1,0:T(8,128)(2,1)} %param.13) | copy-start | bytes 786436
  78.0 120.6 %reduce-scatter.11.cloned.1.call-start = ((), (), s32[]{:S(2)}) async-start(), calls=%async_computation.7 | async-start | bytes 786432 | tf_op jit(solution)/shard_map/reduce_scatter | solution.py:100
  138.5 3.8 %copy-start.2 = (bf16[2,512,1280]{1,2,0:T(8,128)(2,1)S(1)}, bf16[2,512,1280]{1,2,0:T(8,128)(2,1)}, u32[]{:S(2)}) copy-start(bf16[2,512,1280]{1,2,0:T(8,128)(2,1)} %copy-done.1) | copy-start | bytes 7864324
  193.0 3.1 %copy-start.7 = (bf16[256,2560]{0,1:T(8,128)(2,1)S(1)}, bf16[256,2560]{0,1:T(8,128)(2,1)}, u32[]{:S(2)}) copy-start(bf16[256,2560]{0,1:T(8,128)(2,1)} %copy-done.6) | copy-start | bytes 3932164
Sparse Core Ops, SparseCore 0:
  50.3 55.7 reduce-scatter.8
  109.7 60.9 reduce-scatter.4
  173.5 7.0 reduce-scatter.6
  183.4 9.1 reduce-scatter.10

commit v3 on v1

--- a/solution.py
+++ b/solution.py
@@ -23,10 +23,15 @@
 
     log_prefix = jnp.log1p(-code_prefix.astype(jnp.float32) * 1e-06)
     own_total = jnp.sum(log_prefix, axis=0)
-    totals = lax.all_gather(own_total, pre_axes)
+    shard_count = lax.axis_size(pre_axes)
     mine = lax.axis_index(pre_axes)
-    shard_at = jnp.arange(totals.shape[0], dtype=jnp.int32)
-    later_total = jnp.sum(jnp.where((shard_at > mine)[:, None], totals, 0.0), axis=0)
+    shard_at = jnp.arange(shard_count, dtype=jnp.int32)
+    lanes = -(-heads_total // 128) * 128
+    padded = jnp.pad(own_total, (0, lanes - heads_total))
+    rows = jnp.where((shard_at < mine)[:, None], padded[None, :], 0.0)
+    rows = jnp.broadcast_to(rows[:, None, :], (shard_count, 8, lanes))
+    later_total = lax.psum_scatter(rows, pre_axes, scatter_dimension=0, tiled=True)
+    later_total = later_total[0, 0, :heads_total]
     after_local = own_total[None, :] - jnp.cumsum(log_prefix, axis=0)
     weight = jnp.exp(after_local + later_total[None, :])
     weighted_b = (weight[:, :, None] * b_prefix[:, None, :].astype(jnp.float32)).astype(
@@ -34,8 +39,11 @@
     )
     x_heads = x_prefix.reshape(pre_len, heads_total, head_size)
     state_full = jnp.einsum("jhp,jhn->hpn", x_heads, weighted_b, preferred_element_type=jnp.float32)
-    init_part = lax.psum_scatter(state_full, "seq", scatter_dimension=0, tiled=True)
-    init_half = lax.psum(init_part, "cand").astype(jnp.bfloat16)
+    seq_at = lax.axis_index("seq")
+    traced_zero = later_total[0] * 0.0
+    init_full = lax.psum(state_full, pre_axes) + traced_zero
+    init_half = lax.dynamic_slice_in_dim(init_full, seq_at * half_heads, half_heads, 0)
+    init_half = init_half.astype(jnp.bfloat16)
 
     position = jnp.arange(cand_len, dtype=jnp.int32)
     valid_rows = position[None, :] < lengths[:, None] * BLOCK
@@ -50,7 +58,7 @@
     x_high, x_low = split_bf16(xc_heads.astype(jnp.float32) * inverse[:, :, :, None])
 
     dstate = jnp.einsum("cthp,ctn->hpn", decayed_g, c_cand, preferred_element_type=jnp.float32)
-    grad_half = lax.psum(dstate, "cand").astype(jnp.bfloat16)
+    grad_half = (lax.psum(dstate, "cand") + traced_zero).astype(jnp.bfloat16)
     grad_state = lax.all_gather(grad_half, "seq", axis=0, tiled=True)
 
     causal = position[:, None] >= position[None, :]

time: 192 us -> 306 us (1.59)
  waiting for transfers between devices: 0.05 us -> 220 us
  blocking collectives: 115 us -> 2.28 us
  other arithmetic: 8.66 us -> 14 us
    psum x0 -> x2, waiting for transfers between devices: none -> 125 us  [the longest x1 64.6 us: shards(): init_full = lax.psum(state_full, pre_axes) + traced_zero]
    unnamed x3 -> x6, waiting for transfers between devices: 0.05 us -> 82.6 us
    psum x1 -> x0, blocking collectives: 78.3 us -> none  [shards(): grad_half = lax.psum(dstate, 'cand').astype(jnp.bfloat16)]
    unnamed x1 -> x0, blocking collectives: 34.9 us -> none
    reduce_scatter x1, waiting for transfers between devices: 0.01 us -> 11.9 us  [shards(): dc_cand = lax.psum_scatter(dc_total, 'seq', scatter_dimension=1, tiled=True)]
    unnamed x35 -> x38, local copies, waits for them, and re-layouts: 19 us -> 20.8 us
  transfers between devices with their start and end apart: 3 -> 5, of which waited for: 0 -> 5; matrix products, arithmetic and copies ran while one was open for 27% -> 19% of each run, Pallas kernels for 0% -> 0%
where the time goes in v3:
time: 306 us
  waiting for transfers between devices  220 us (72%)
  matrix products  31 us (10%)
  local copies, waits for them, and re-layouts  22.8 us (7%)
  between operations  14.8 us (5%)
  other arithmetic  14 us (5%)
    unnamed x6, waiting for transfers between devices  82.6 us
    psum x1, waiting for transfers between devices, shards(): init_full = lax.psum(state_full, pre_axes) + traced_zero  64.6 us
    psum x1, waiting for transfers between devices, shards(): grad_half = (lax.psum(dstate, 'cand') + traced_zero).astype(jnp.bfloat16)  60.1 us
    unnamed x38, local copies, waits for them, and re-layouts  20.8 us
    reduce_scatter x1, waiting for transfers between devices, shards(): dc_cand = lax.psum_scatter(dc_total, 'seq', scatter_dimension=1, tiled=True)  11.9 us
    dot_general x1, matrix products, shards(): jnp.einsum('chts,cthp->cshp', kernel, g_heads, preferred_element_type=jnp...  7.72 us
  transfers between devices with their start and end apart: 5, of which 5 were waited for; matrix products, arithmetic and copies ran while one was open for 19% of the time, Pallas kernels for 0%

profile of v3, /device:TPU:0, one launch (start us, length us, event | category | flops | bytes accessed | tf_op | source)
XLA Modules:
  0.0 305.6 jit_solution(1528307880977346940)
XLA Ops:
  7.2 0.0 copy-start
  7.2 0.0 copy-start.14
  7.2 0.0 all-reduce.10.cloned.1.call-start
  7.3 0.9 fusion.26
  8.2 0.1 broadcast_select_fusion.1
  8.3 0.6 broadcast_in_dim.84
  8.9 0.0 all-reduce.10.cloned.1.call-update
  9.0 0.0 all-reduce.8.cloned.1.call-start
  9.0 1.0 log-plus-one_bitcast_fusion
  10.0 0.1 reshape.156
  10.1 2.3 reduce-window.14
  12.5 0.2 slice_reduce_fusion
  12.7 0.1 negate_exponential_fusion
  12.8 0.6 reduce-window.16
  13.4 0.2 slice_reduce_fusion.1
  13.6 2.4 copy.63
  16.1 0.1 copy.61
  16.2 0.0 copy-start.10
  16.2 0.6 dynamic-slice
  16.8 82.5 %all-reduce.10.cloned.1.call-done = f32[16,8,128]{2,1,0:T(8,128)} async-done(((f32[16,8,128]{2,1,0:T(8,128)}), f32[16,8,128]{2,1,0:T(8,128)}) %all-reduce.10.cloned.1.call-update) | async-done | bytes 65552
  99.3 1.3 constant_dynamic-slice_fusion
  100.6 0.1 fusion.25
  100.7 0.6 copy-done.12
  101.3 3.5 %fusion.19 = f32[40,64,128]{2,1,0:T(8,128)} fusion(bf16[256,40,64]{0,2,1:T(8,128)(2,1)} %bitcast.91, f32[256,128]{0,1:T(8,128)S(1)} %copy.61, f32[256,40]{0,1:T(8,128)S(1)} %fusion.25), kind=kOutput, calls=%fused_computation.31 | convolution fusion | flops 170393600 | bytes 2793472 | tf_op jit(solution)/shard_map/jhp,jhn->hpn/dot_general | solution.py:41
  104.9 0.0 all-reduce.8.cloned.1.call-update
  104.9 0.0 all-reduce.6.cloned.1.call-start
  105.0 0.1 exp.29
  105.1 0.1 exp.34
  105.2 2.6 copy.55
  107.9 4.4 %copy.67 = bf16[2,512,1280]{1,2,0:T(8,128)(2,1)} copy(bf16[2,512,1280]{2,1,0:T(8,128)(2,1)} %param.12) | data formatting | bytes 5242880 | tf_op args[3]
  112.3 0.1 iota_compare_fusion.1
  112.4 5.7 %fusion.6 = (bf16[2,512,1280]{1,2,0:T(8,128)(2,1)}, bf16[2,512,1280]{1,2,0:T(8,128)(2,1)S(1)}, bf16[2,512,1280]{1,2,0:T(8,128)(2,1)}, bf16[2,512,1280]{1,2,0:T(8,128)(2,1)}) fusion(f32[2,512,20]{1,2,0:T(8,128)S(1)} %copy.58, bf16[2,512,1280]{1,2,0:T(8,128)(2,1)} %copy.55, pred[2,512]{1,0:T(4,128)(4,1)S(1)} %iota_compare_fusion.1, ...), kind=kLoop, calls=%fused_computation.11 | loop fusion | flops 15728640 | bytes 15893504 | tf_op jit(solution)/shard_map/convert_element_type | solution.py:11
  118.0 1.7 fusion.20
  119.8 0.0 all-reduce.6.cloned.1.call-update
  119.8 0.2 reduce-scatter.3.cloned.1.call-start
  120.0 0.5 reduce-precision_convert_fusion.1
  120.6 0.1 iota_compare_fusion
  120.7 1.7 copy-done.5
  122.4 1.6 fusion.30
  124.0 0.2 copy-done.6
  124.2 1.6 fusion.31
  125.8 0.2 copy-done.4
  125.9 1.8 add_select_fusion
  127.7 2.7 fusion.32
  130.4 0.0 reduce-scatter.3.cloned.1.call-update
  130.4 0.3 reduce-scatter.5.cloned.1.call-start
  130.7 1.8 fusion.29
  132.5 1.9 fusion.33
  134.4 0.5 slice.22
  135.6 64.6 %all-reduce.8.cloned.1.call-done = f32[40,64,128]{2,1,0:T(8,128)} async-done(((f32[40,64,128]{2,1,0:T(8,128)}), f32[40,64,128]{2,1,0:T(8,128)}) %all-reduce.8.cloned.1.call-update) | async-done | bytes 1310736 | tf_op jit(solution)/shard_map/psum | solution.py:44
  200.2 1.3 fusion.21
  201.5 3.5 %convolution_add_fusion = f32[2,512,128]{2,1,0:T(8,128)} fusion(f32[2,512,128]{2,1,0:T(8,128)} %fusion.33, bf16[2,512,1280]{1,2,0:T(8,128)(2,1)} %copy-done.3, bf16[1280,128,1]{1,0,2:T(8,128)(2,1)S(1)} %bitcast.94), kind=kOutput, calls=%fused_computation.33 | convolution fusion | flops 335675392 | bytes 3997696 | tf_op jit(solution)/shard_map/dot_general | solution.py:90
  205.0 0.0 reduce-scatter.5.cloned.1.call-update
  205.0 7.7 %fusion.17 = bf16[2,20,64,512]{3,2,1,0:T(8,128)(2,1)} fusion(bf16[2,512,20,64]{1,3,2,0:T(8,128)(2,1)S(1)} %bitcast.89, f32[2,20,512]{2,1,0:T(8,128)S(1)} %copy.66, f32[2,20,512]{2,1,0:T(8,128)S(1)} %copy.64, f32[2,512,512]{2,1,0:T(8,128)} %fusion.29, pred[512,512]{1,0:T(8,128)(4,1)S(1)} %iota_compare_fusion), kind=kOutput, calls=%fused_computation.29 | convolution fusion | flops 1385431040 | bytes 7766016 | tf_op jit(solution)/shard_map/chts,cthp->cshp/dot_general | solution.py:87
  212.8 4.4 %copy.80 = bf16[2,512,1280]{2,1,0:T(8,128)(2,1)} copy(bf16[2,512,1280]{1,2,0:T(8,128)(2,1)} %bitcast.90) | data formatting | bytes 5242880
  217.1 60.1 %all-reduce.6.cloned.1.call-done = f32[20,64,128]{2,1,0:T(8,128)} async-done(((f32[20,64,128]{2,1,0:T(8,128)}), f32[20,64,128]{2,1,0:T(8,128)}) %all-reduce.6.cloned.1.call-update) | async-done | bytes 655376 | tf_op jit(solution)/shard_map/psum | solution.py:61
  277.3 1.2 add_convert_fusion
  278.4 2.3 all_gather.3
  280.7 1.5 fusion.18
  282.3 1.6 copy.78
  283.8 1.7 fusion.8
  285.5 0.8 copy.79
  286.3 0.9 reduce-scatter.3.cloned.1.call-done
  287.2 11.9 %reduce-scatter.5.cloned.1.call-done = f32[2,256,128]{2,1,0:T(8,128)} async-done(((f32[2,512,128]{2,1,0:T(8,128)}), f32[2,256,128]{2,1,0:T(8,128)}) %reduce-scatter.5.cloned.1.call-update) | async-done | bytes 262160 | tf_op jit(solution)/shard_map/reduce_scatter | solution.py:97
  (39 shorter events, 0.3 us)
Async XLA Ops:
  7.2 110.9 %copy-start = (bf16[2,512,128]{2,1,0:T(8,128)(2,1)S(1)}, bf16[2,512,128]{2,1,0:T(8,128)(2,1)}, u32[]{:S(2)}) copy-start(bf16[2,512,128]{2,1,0:T(8,128)(2,1)} %param.14) | copy-start | bytes 786436
  7.2 9.0 %copy-start.14 = (u32[32]{0:T(128)S(1)}, u32[32]{0:T(128)}, u32[]{:S(2)}) copy-start(u32[32]{0:T(128)} %constant.44) | copy-start | bytes 388
  7.2 8.9 %copy-start.11 = (bf16[256,128]{1,0:T(8,128)(2,1)S(1)}, bf16[256,128]{1,0:T(8,128)(2,1)}, u32[]{:S(2)}) copy-start(bf16[256,128]{1,0:T(8,128)(2,1)} %param.10) | copy-start | bytes 196612
  7.2 92.1 %all-reduce.10.cloned.1.call-start = ((), (), s32[]{:S(2)}) async-start(), calls=%async_computation.6 | async-start | bytes 131072
  9.0 191.2 %all-reduce.8.cloned.1.call-start = ((), (), s32[]{:S(2)}) async-start(), calls=%async_computation.4 | async-start | bytes 2621440 | tf_op jit(solution)/shard_map/psum | solution.py:44
  16.1 88.9 %copy-start.13 = (s32[2]{0:T(128)S(1)}, s32[2]{0:T(128)}, u32[]{:S(2)}) copy-start(s32[2]{0:T(128)} %param.16) | copy-start | bytes 28
  16.2 88.8 %copy-start.10 = (f32[256,128]{0,1:T(8,128)}, f32[256,128]{0,1:T(8,128)S(1)}, u32[]{:S(2)}) copy-start(f32[256,128]{0,1:T(8,128)S(1)} %copy.61) | copy-start | bytes 393220
  100.7 0.6 copy-start.12
  101.3 3.9 %copy-start.7 = (bf16[2,512,1280]{2,1,0:T(8,128)(2,1)S(1)}, bf16[2,512,1280]{2,1,0:T(8,128)(2,1)}, u32[]{:S(2)}) copy-start(bf16[2,512,1280]{2,1,0:T(8,128)(2,1)} %param.17) | copy-start | bytes 7864324
  104.9 172.4 %all-reduce.6.cloned.1.call-start = ((), (), s32[]{:S(2)}) async-start(), calls=%async_computation.2 | async-start | bytes 1310720 | tf_op jit(solution)/shard_map/psum | solution.py:61
  118.0 2.0 copy-start.1
  119.8 167.4 %reduce-scatter.3.cloned.1.call-start = ((), (), s32[]{:S(2)}) async-start(), calls=%async_computation.3 | async-start | bytes 786432 | tf_op jit(solution)/shard_map/reduce_scatter | solution.py:96
  120.0 2.4 copy-start.5
  120.6 3.4 %copy-start.3 = (bf16[2,512,1280]{1,2,0:T(8,128)(2,1)}, bf16[2,512,1280]{1,2,0:T(8,128)(2,1)S(1)}, u32[]{:S(2)}) copy-start(bf16[2,512,1280]{1,2,0:T(8,128)(2,1)S(1)} %reduce-precision_convert_fusion.1) | copy-start | bytes 7864324
  122.4 1.8 copy-start.6
  124.2 1.7 copy-start.4
  127.7 3.0 copy-start.9
  130.4 168.7 %reduce-scatter.5.cloned.1.call-start = ((), (), s32[]{:S(2)}) async-start(), calls=%async_computation.5 | async-start | bytes 786432 | tf_op jit(solution)/shard_map/reduce_scatter | solution.py:97
  200.2 4.9 %copy-start.2 = (bf16[2,512,1280]{1,2,0:T(8,128)(2,1)S(1)}, bf16[2,512,1280]{1,2,0:T(8,128)(2,1)}, u32[]{:S(2)}) copy-start(bf16[2,512,1280]{1,2,0:T(8,128)(2,1)} %copy-done.1) | copy-start | bytes 7864324
  280.7 3.1 %copy-start.8 = (bf16[256,2560]{0,1:T(8,128)(2,1)S(1)}, bf16[256,2560]{0,1:T(8,128)(2,1)}, u32[]{:S(2)}) copy-start(bf16[256,2560]{0,1:T(8,128)(2,1)} %copy.63) | copy-start | bytes 3932164
Sparse Core Ops, SparseCore 0:
  12.1 87.1 all-reduce.9
  105.0 95.1 all-reduce.7
  204.0 73.2 all-reduce.5
  280.0 7.2 reduce-scatter.2
  290.0 9.0 reduce-scatter.4

commit v4 on v1

--- a/solution.py
+++ b/solution.py
@@ -12,6 +12,31 @@
     return high.astype(jnp.bfloat16), low
 
 
+def butterfly_sum(value, axis):
+    count = lax.axis_size(axis)
+    step = 1
+    while step < count:
+        partner = [(at, at ^ step) for at in range(count)]
+        value = value + lax.ppermute(value, axis, partner)
+        step *= 2
+    return value
+
+
+def suffix_sum(value, axis):
+    count = lax.axis_size(axis)
+    step = 1
+    while step < count:
+        back = [(at, at - step) for at in range(step, count)]
+        value = value + lax.ppermute(value, axis, back)
+        step *= 2
+    return value
+
+
+def other_core(value):
+    count = lax.axis_size("seq")
+    return lax.ppermute(value, "seq", [(at, (at + 1) % count) for at in range(count)])
+
+
 def shards(x_prefix, b_prefix, code_prefix, x_cand, b_cand, c_cand, code_cand, lengths, dy_cand):
     pre_len, width = x_prefix.shape
     heads_total = code_prefix.shape[1]
@@ -23,10 +48,7 @@
 
     log_prefix = jnp.log1p(-code_prefix.astype(jnp.float32) * 1e-06)
     own_total = jnp.sum(log_prefix, axis=0)
-    totals = lax.all_gather(own_total, pre_axes)
-    mine = lax.axis_index(pre_axes)
-    shard_at = jnp.arange(totals.shape[0], dtype=jnp.int32)
-    later_total = jnp.sum(jnp.where((shard_at > mine)[:, None], totals, 0.0), axis=0)
+    later_total = suffix_sum(own_total, pre_axes) - own_total
     after_local = own_total[None, :] - jnp.cumsum(log_prefix, axis=0)
     weight = jnp.exp(after_local + later_total[None, :])
     weighted_b = (weight[:, :, None] * b_prefix[:, None, :].astype(jnp.float32)).astype(
@@ -34,8 +56,12 @@
     )
     x_heads = x_prefix.reshape(pre_len, heads_total, head_size)
     state_full = jnp.einsum("jhp,jhn->hpn", x_heads, weighted_b, preferred_element_type=jnp.float32)
-    init_part = lax.psum_scatter(state_full, "seq", scatter_dimension=0, tiled=True)
-    init_half = lax.psum(init_part, "cand").astype(jnp.bfloat16)
+    seq_at = lax.axis_index("seq")
+    state_halves = state_full.reshape(2, half_heads, head_size, nstate)
+    mine_first = seq_at == 0
+    own_half = jnp.where(mine_first, state_halves[0], state_halves[1])
+    give_half = jnp.where(mine_first, state_halves[1], state_halves[0])
+    init_half = butterfly_sum(own_half + other_core(give_half), "cand").astype(jnp.bfloat16)
 
     position = jnp.arange(cand_len, dtype=jnp.int32)
     valid_rows = position[None, :] < lengths[:, None] * BLOCK
@@ -50,8 +76,13 @@
     x_high, x_low = split_bf16(xc_heads.astype(jnp.float32) * inverse[:, :, :, None])
 
     dstate = jnp.einsum("cthp,ctn->hpn", decayed_g, c_cand, preferred_element_type=jnp.float32)
-    grad_half = lax.psum(dstate, "cand").astype(jnp.bfloat16)
-    grad_state = lax.all_gather(grad_half, "seq", axis=0, tiled=True)
+    grad_half = butterfly_sum(dstate, "cand").astype(jnp.bfloat16)
+    grad_other = other_core(grad_half)
+    grad_state = jnp.where(
+        mine_first,
+        jnp.concatenate([grad_half, grad_other], axis=0),
+        jnp.concatenate([grad_other, grad_half], axis=0),
+    )
 
     causal = position[:, None] >= position[None, :]
     flat = (cand_dev, cand_len, half_width)
@@ -85,8 +116,14 @@
         preferred_element_type=jnp.float32,
     )
     dc_total = dc_part + dc_state.reshape(cand_dev, cand_len, nstate)
-    db_cand = lax.psum_scatter(db_part, "seq", scatter_dimension=1, tiled=True)
-    dc_cand = lax.psum_scatter(dc_total, "seq", scatter_dimension=1, tiled=True)
+    def token_half_sum(part):
+        halves = part.reshape(cand_dev, 2, cand_len // 2, nstate)
+        own = jnp.where(mine_first, halves[:, 0], halves[:, 1])
+        give = jnp.where(mine_first, halves[:, 1], halves[:, 0])
+        return own + other_core(give)
+
+    db_cand = token_half_sum(db_part)
+    dc_cand = token_half_sum(dc_total)
 
     dx_prefix = jnp.einsum(
         "jhn,hpn->jhp", weighted_b, grad_state, preferred_element_type=jnp.float32

time: 192 us -> 150 us (0.78)
  blocking collectives: 115 us -> 0 us
  waiting for transfers between devices: 0.05 us -> 60.4 us
  starting transfers between devices: 0.3 us -> 19.7 us
  other arithmetic: 8.66 us -> 23.2 us
  between operations: 14.7 us -> 1.09 us
  local copies, waits for them, and re-layouts: 21.1 us -> 15.8 us
    psum x1 -> x0, blocking collectives: 78.3 us -> none  [shards(): grad_half = lax.psum(dstate, 'cand').astype(jnp.bfloat16)]
    ppermute x0 -> x14, waiting for transfers between devices: none -> 60.4 us  [the longest x6 49.8 us: butterfly_sum(): value = value + lax.ppermute(value, axis, partner)]
    unnamed x1 -> x0, blocking collectives: 34.9 us -> none
    ppermute x0 -> x14, starting transfers between devices: none -> 19.7 us  [the longest x6 14.2 us: butterfly_sum(): value = value + lax.ppermute(value, axis, partner)]
    dot_general x3, matrix products: 4.97 us -> 12.5 us  [pair(): jnp.einsum('ctk,csk->cts', left.reshape(flat), right.reshape(flat), prefe...]
    add x0 -> x10, other arithmetic: none -> 6.05 us  [the longest x4 3.31 us: butterfly_sum(): value = value + lax.ppermute(value, axis, partner)]
    unnamed x35 -> x38, local copies, waits for them, and re-layouts: 19 us -> 15 us
    convert_element_type x0 -> x2, other arithmetic: none -> 2.74 us  [the longest x1 1.37 us: shards(): grad_half = butterfly_sum(dstate, 'cand').astype(jnp.bfloat16)]
  transfers between devices with their start and end apart: 3 -> 14, of which waited for: 0 -> 6; matrix products, arithmetic and copies ran while one was open for 27% -> 44% of each run, Pallas kernels for 0% -> 0%
where the time goes in v4:
time: 150 us
  waiting for transfers between devices  60.4 us (40%)
  matrix products  29.7 us (20%)
  other arithmetic  23.2 us (15%)
  starting transfers between devices  19.7 us (13%)
  local copies, waits for them, and re-layouts  15.8 us (11%)
    ppermute x6, waiting for transfers between devices, butterfly_sum(): value = value + lax.ppermute(value, axis, partner)  49.8 us
    unnamed x38, local copies, waits for them, and re-layouts  15 us
    ppermute x6, starting transfers between devices, butterfly_sum(): value = value + lax.ppermute(value, axis, partner)  14.2 us
    dot_general x3, matrix products, pair(): jnp.einsum('ctk,csk->cts', left.reshape(flat), right.reshape(flat), prefe...  12.5 us
    ppermute x4, waiting for transfers between devices, suffix_sum(): value = value + lax.ppermute(value, axis, back)  10.5 us
    dot_general x1, matrix products, shards(): jnp.einsum('chts,cthp->cshp', kernel, g_heads, preferred_element_type=jnp...  6.43 us
    convert_element_type x1, other arithmetic, split_bf16(): low = (value - high).astype(jnp.bfloat16)  5.66 us
    ppermute x4, starting transfers between devices, suffix_sum(): value = value + lax.ppermute(value, axis, back)  5.32 us
  transfers between devices with their start and end apart: 14, of which 6 were waited for; matrix products, arithmetic and copies ran while one was open for 44% of the time, Pallas kernels for 0%

profile of v4, /device:TPU:0, one launch (start us, length us, event | category | flops | bytes accessed | tf_op | source)
XLA Modules:
  0.0 149.9 jit_solution(10900049767278097475)
XLA Ops:
  0.6 0.9 fusion.26
  1.6 1.3 collective-permute-start.4
  2.9 0.7 broadcast_multiply_fusion
  3.6 0.1 iota_compare_fusion.1
  3.6 1.0 log-plus-one_bitcast_fusion
  4.6 0.1 reshape.144
  4.8 2.3 %reduce-window.14 = f32[2,20,4,128]{3,1,2,0:T(8,128)S(1)} reduce-window(f32[2,20,4,128]{3,1,2,0:T(8,128)S(1)} %copy.64, f32[]{:T(128)} %constant.20.clone.1), window={size=1x1x1x128 pad=0_0x0_0x0_0x127_0}, to_apply=%region_0.0 | reduce-window | flops 2600960 | bytes 163844 | tf_op jit(solution)/shard_map/reduce-window
  7.1 0.2 slice_reduce_fusion
  7.3 0.1 negate_exponential_fusion
  7.7 4.6 %copy.75 = bf16[2,512,1280]{1,2,0:T(8,128)(2,1)} copy(bf16[2,512,1280]{2,1,0:T(8,128)(2,1)} %param.12) | data formatting | bytes 5242880 | tf_op args[3]
  12.3 2.6 %copy.63 = bf16[2,512,1280]{1,2,0:T(8,128)(2,1)} copy(bf16[2,512,1280]{2,1,0:T(8,128)(2,1)S(1)} %copy-done.6) | data formatting | bytes 5242880 | tf_op args[8]
  14.9 5.7 %fusion.6 = (bf16[2,512,1280]{1,2,0:T(8,128)(2,1)}, bf16[2,512,1280]{1,2,0:T(8,128)(2,1)S(1)}, bf16[2,512,1280]{1,2,0:T(8,128)(2,1)}, bf16[2,512,1280]{1,2,0:T(8,128)(2,1)}) fusion(f32[2,512,20]{1,2,0:T(8,128)S(1)} %copy.66, bf16[2,512,1280]{1,2,0:T(8,128)(2,1)} %copy.63, pred[2,512]{1,0:T(4,128)(4,1)S(1)} %iota_compare_fusion.1, ...), kind=kLoop, calls=%fused_computation.11 | loop fusion | flops 15728640 | bytes 15893504 | tf_op jit(solution)/shard_map/convert_element_type | solution.py:11
  20.6 1.7 %fusion.20 = f32[20,64,128]{2,1,0:T(8,128)} fusion(bf16[2,512,20,64]{1,3,2,0:T(8,128)(2,1)S(1)} %bitcast.116, f32[2,512,20]{1,2,0:T(8,128)S(1)} %copy.66, bf16[2,512,128]{2,1,0:T(8,128)(2,1)S(1)} %copy-done), kind=kOutput, calls=%fused_computation.32 | convolution fusion | flops 340787200 | bytes 3620864 | tf_op jit(solution)/shard_map/cthp,ctn->hpn/dot_general | solution.py:78
  22.3 3.6 %collective-permute-start = (f32[20,64,128]{2,1,0:T(8,128)}, f32[20,64,128]{2,1,0:T(8,128)}, u32[]{:S(2)}, u32[]{:S(2)}) collective-permute-start(f32[20,64,128]{2,1,0:T(8,128)} %fusion.20), channel_id=1, source_target_pairs={{0,2},{2,0},{4,6},{6,4},{8,10},{10,8},{12,14},{14,12},{1,3},{3,1},... | collective-permute-start | bytes 1966088 | tf_op jit(solution)/shard_map/ppermute | solution.py:20
  25.9 2.0 %reduce-precision_convert_fusion.1 = bf16[2,512,1280]{1,2,0:T(8,128)(2,1)} fusion(bf16[2,512,1280]{1,2,0:T(8,128)(2,1)S(1)} %get-tuple-element.21, f32[2,512,20]{1,2,0:T(8,128)S(1)} %copy.66), kind=kLoop, calls=%fused_computation.10 | loop fusion | flops 5242880 | bytes 5324800 | tf_op jit(solution)/shard_map/convert_element_type | solution.py:12
  27.9 0.6 reduce-window.16
  28.5 5.6 %fusion.32 = f32[2,512,512]{2,1,0:T(8,128)} fusion(bf16[2,512,1280]{1,2,0:T(8,128)(2,1)} %reduce-precision_convert_fusion.1, bf16[2,512,1280]{1,2,0:T(8,128)(2,1)} %get-tuple-element.29), kind=kOutput, calls=%fused_computation.71 | convolution fusion | flops 1342177280 | bytes 7340032 | tf_op jit(solution)/shard_map/ctk,csk->cts/dot_general | solution.py:91
  34.1 2.9 %fusion.31 = f32[2,512,512]{2,1,0:T(8,128)} fusion(bf16[2,512,1280]{1,2,0:T(8,128)(2,1)S(1)} %copy-done.1, bf16[2,512,1280]{1,2,0:T(8,128)(2,1)S(1)} %copy-done.4), kind=kOutput, calls=%fused_computation.70 | convolution fusion | flops 1342177280 | bytes 7340032 | tf_op jit(solution)/shard_map/ctk,csk->cts/dot_general | solution.py:91
  37.0 0.2 slice_reduce_fusion.1
  37.2 1.3 collective-permute-start.5
  38.5 4.1 %collective-permute-done.5 = f32[40]{0:T(128)S(1)} collective-permute-done((f32[40]{0:T(128)S(1)}, f32[40]{0:T(128)S(1)}, u32[]{:S(2)}, u32[]{:S(2)}) %collective-permute-start.5) | collective-permute-done | bytes 192 | tf_op jit(solution)/shard_map/ppermute | solution.py:30
  42.6 1.3 collective-permute-start.6
  43.9 0.1 copy.69
  44.1 4.0 %collective-permute-done.6 = f32[40]{0:T(128)S(1)} collective-permute-done((f32[40]{0:T(128)S(1)}, f32[40]{0:T(128)S(1)}, u32[]{:S(2)}, u32[]{:S(2)}) %collective-permute-start.6) | collective-permute-done | bytes 192 | tf_op jit(solution)/shard_map/ppermute | solution.py:30
  48.1 1.5 collective-permute-start.7
  49.5 2.4 %copy.71 = bf16[256,2560]{0,1:T(8,128)(2,1)} copy(bf16[256,2560]{1,0:T(8,128)(2,1)} %param.9) | data formatting | bytes 2621440 | tf_op args[0]
  52.0 2.4 %collective-permute-done.7 = f32[40]{0:T(128)S(1)} collective-permute-done((f32[40]{0:T(128)S(1)}, f32[40]{0:T(128)S(1)}, u32[]{:S(2)}, u32[]{:S(2)}) %collective-permute-start.7) | collective-permute-done | bytes 192 | tf_op jit(solution)/shard_map/ppermute | solution.py:30
  54.4 0.1 fusion.24
  54.5 2.5 %fusion.19 = f32[40,64,128]{2,1,0:T(8,128)S(1)} fusion(bf16[256,40,64]{0,2,1:T(8,128)(2,1)} %bitcast.123, f32[256,128]{0,1:T(8,128)S(1)} %copy.69, f32[256,40]{0,1:T(8,128)S(1)} %fusion.24), kind=kOutput, calls=%fused_computation.31 | convolution fusion | flops 170393600 | bytes 2793472 | tf_op jit(solution)/shard_map/jhp,jhn->hpn/dot_general | solution.py:58
  57.0 0.1 slice_select_fusion
  57.1 0.1 collective-permute-start.9
  57.2 0.1 iota_compare_fusion
  57.3 0.1 copy-done.5
  57.4 4.0 %add_select_fusion = f32[2,512,512]{2,1,0:T(8,128)S(1)} fusion(f32[2,512,512]{2,1,0:T(8,128)} %fusion.31, f32[2,512,512]{2,1,0:T(8,128)} %fusion.32, bf16[2,512,1280]{1,2,0:T(8,128)(2,1)S(1)} %copy-done.3, bf16[2,512,1280]{1,2,0:T(8,128)(2,1)S(1)} %copy-done.5, pred[512,512]{1,0:T(8,128)(4,1)S(1)} %iota_compare_fusion), kind=kOutput, calls=%fused_computation.28 | convolution fusion | flops 1343750144 | bytes 11796480 | tf_op jit(solution)/shard_map/ctk,csk->cts/dot_general | solution.py:91
  61.4 1.4 add.57
  62.8 1.7 %collective-permute-start.1 = (f32[20,64,128]{2,1,0:T(8,128)S(1)}, f32[20,64,128]{2,1,0:T(8,128)S(1)}, u32[]{:S(2)}, u32[]{:S(2)}) collective-permute-start(f32[20,64,128]{2,1,0:T(8,128)S(1)} %add.57), channel_id=1, source_target_pairs={{0,4},{2,6},{4,0},{6,2},{8,12},{10,14},{12,8},{14,10},{1,5},{3,7},... | collective-permute-start | bytes 1966088 | tf_op jit(solution)/shard_map/ppermute | solution.py:20
  64.5 0.1 select_add_fusion
  64.6 2.3 %collective-permute-start.10 = (f32[20,64,128]{2,1,0:T(8,128)S(1)}, f32[20,64,128]{2,1,0:T(8,128)S(1)}, u32[]{:S(2)}, u32[]{:S(2)}) collective-permute-start(f32[20,64,128]{2,1,0:T(8,128)S(1)} %select_add_fusion), channel_id=1, source_target_pairs={{0,2},{2,0},{4,6},{6,4},{8,10},{10,8},{12,14},{14,12},{1,3},{3,1},... | collective-permute-start | bytes 1966088 | tf_op jit(solution)/shard_map/ppermute | solution.py:20
  66.9 1.9 %fusion.33 = f32[2,512,128]{2,1,0:T(8,128)S(1)} fusion(f32[2,512,512]{2,1,0:T(8,128)S(1)} %add_select_fusion, bf16[2,512,128]{2,1,0:T(8,128)(2,1)S(1)} %copy-done), kind=kOutput, calls=%fused_computation.72 | convolution fusion | flops 805306368 | bytes 2883584 | tf_op jit(solution)/shard_map/cts,ctn->csn/dot_general | solution.py:98
  68.8 0.7 select_bitcast_fusion.1
  69.6 0.4 fusion.30
  70.0 9.8 %collective-permute-done.1 = f32[20,64,128]{2,1,0:T(8,128)S(1)} collective-permute-done((f32[20,64,128]{2,1,0:T(8,128)S(1)}, f32[20,64,128]{2,1,0:T(8,128)S(1)}, u32[]{:S(2)}, u32[]{:S(2)}) %collective-permute-start.1) | collective-permute-done | bytes 655392 | tf_op jit(solution)/shard_map/ppermute | solution.py:20
  79.9 0.9 add.58
  80.8 1.1 collective-permute-start.2
  81.9 0.1 add.70
  82.0 1.7 %collective-permute-start.11 = (f32[20,64,128]{2,1,0:T(8,128)S(1)}, f32[20,64,128]{2,1,0:T(8,128)S(1)}, u32[]{:S(2)}, u32[]{:S(2)}) collective-permute-start(f32[20,64,128]{2,1,0:T(8,128)S(1)} %add.70), channel_id=1, source_target_pairs={{0,4},{2,6},{4,0},{6,2},{8,12},{10,14},{12,8},{14,10},{1,5},{3,7},... | collective-permute-start | bytes 1966088 | tf_op jit(solution)/shard_map/ppermute | solution.py:20
  83.7 6.4 %fusion.17 = bf16[2,20,64,512]{3,2,1,0:T(8,128)(2,1)} fusion(bf16[2,512,20,64]{1,3,2,0:T(8,128)(2,1)S(1)} %bitcast.117, f32[2,20,512]{2,1,0:T(8,128)S(1)} %copy.74, f32[2,20,512]{2,1,0:T(8,128)S(1)} %copy.72, f32[2,512,512]{2,1,0:T(8,128)S(1)} %fusion.30, pred[512,512]{1,0:T(8,128)(4,1)S(1)} %iota_compare_fusion), kind=kOutput, calls=%fused_computation.29 | convolution fusion | flops 1385431040 | bytes 7766016 | tf_op jit(solution)/shard_map/chts,cthp->cshp/dot_general | solution.py:110
  90.1 19.8 %collective-permute-done.11 = f32[20,64,128]{2,1,0:T(8,128)S(1)} collective-permute-done((f32[20,64,128]{2,1,0:T(8,128)S(1)}, f32[20,64,128]{2,1,0:T(8,128)S(1)}, u32[]{:S(2)}, u32[]{:S(2)}) %collective-permute-start.11) | collective-permute-done | bytes 655392 | tf_op jit(solution)/shard_map/ppermute | solution.py:20
  109.9 0.9 add.71
  110.9 3.9 %collective-permute-start.12 = (f32[20,64,128]{2,1,0:T(8,128)}, f32[20,64,128]{2,1,0:T(8,128)}, u32[]{:S(2)}, u32[]{:S(2)}) collective-permute-start(f32[20,64,128]{2,1,0:T(8,128)} %add.71), channel_id=1, source_target_pairs={{0,8},{2,10},{4,12},{6,14},{8,0},{10,2},{12,4},{14,6},{1,9},{3,11}... | collective-permute-start | bytes 1966088 | tf_op jit(solution)/shard_map/ppermute | solution.py:20
  114.7 1.9 %fusion.34 = f32[2,512,128]{2,1,0:T(8,128)} fusion(f32[2,512,512]{2,1,0:T(8,128)S(1)} %add_select_fusion, bf16[2,512,128]{2,1,0:T(8,128)(2,1)S(1)} %copy-done.10), kind=kOutput, calls=%fused_computation.73 | convolution fusion | flops 805306368 | bytes 2883584 | tf_op jit(solution)/shard_map/cts,csn->ctn/dot_general | solution.py:101
  116.6 2.6 %copy.92 = bf16[2,512,1280]{2,1,0:T(8,128)(2,1)} copy(bf16[2,512,1280]{1,2,0:T(8,128)(2,1)S(1)} %bitcast.122) | data formatting | bytes 5242880
  119.2 1.8 %bitcast_add_fusion.1 = f32[2,256,128]{2,1,0:T(8,128)} fusion(f32[2,256,128]{2,1,0:T(8,128)} %collective-permute-done.8, f32[2,2,256,128]{3,2,1,0:T(8,128)S(1)} %bitcast.121, pred[]{:T(512)S(6)} %eq.3), kind=kLoop, calls=%fused_computation.46 | loop fusion | flops 131072 | bytes 1048577 | tf_op jit(solution)/shard_map/add | solution.py:123
  121.0 1.4 add_convert_fusion.1
  122.4 0.1 collective-permute-start.3
  122.5 20.2 %collective-permute-done.12 = f32[20,64,128]{2,1,0:T(8,128)} collective-permute-done((f32[20,64,128]{2,1,0:T(8,128)}, f32[20,64,128]{2,1,0:T(8,128)}, u32[]{:S(2)}, u32[]{:S(2)}) %collective-permute-start.12) | collective-permute-done | bytes 655392 | tf_op jit(solution)/shard_map/ppermute | solution.py:20
  142.7 1.4 add_convert_fusion
  144.1 0.9 convolution_add_fusion
  145.1 0.3 copy-done.9
  145.4 0.9 fusion.8
  146.3 0.8 copy.91
  147.0 0.5 fusion.18
  147.6 1.6 %copy.90 = bf16[256,2560]{1,0:T(8,128)(2,1)} copy(bf16[256,2560]{0,1:T(8,128)(2,1)S(1)} %bitcast.125) | data formatting | bytes 2621440
  149.2 0.7 bitcast_add_fusion
  (59 shorter events, 0.6 us)
Async XLA Ops:
  0.6 19.9 %copy-start = (bf16[2,512,128]{2,1,0:T(8,128)(2,1)S(1)}, bf16[2,512,128]{2,1,0:T(8,128)(2,1)}, u32[]{:S(2)}) copy-start(bf16[2,512,128]{2,1,0:T(8,128)(2,1)} %param.14) | copy-start | bytes 786436
  1.6 35.6 %collective-permute-start.4 = (f32[40]{0:T(128)S(1)}, f32[40]{0:T(128)S(1)}, u32[]{:S(2)}, u32[]{:S(2)}) collective-permute-start(f32[40]{0:T(128)S(1)} %get-tuple-element.26), channel_id=1, source_target_pairs={{1,0},{2,1},{3,2},{4,3},{5,4},{6,5},{7,6},{8,7},{9,8},{10,9},{11,1... | collective-permute-start | bytes 488 | tf_op jit(solution)/shard_map/ppermute | solution.py:30
  7.6 4.7 %copy-start.11 = (f32[2,20,512]{2,0,1:T(2,128)}, f32[2,20,512]{2,0,1:T(2,128)S(1)}, u32[]{:S(2)}) copy-start(f32[2,20,512]{2,0,1:T(2,128)S(1)} %exp.29) | copy-start | bytes 245764
  7.7 4.6 %copy-start.6 = (bf16[2,512,1280]{2,1,0:T(8,128)(2,1)S(1)}, bf16[2,512,1280]{2,1,0:T(8,128)(2,1)}, u32[]{:S(2)}) copy-start(bf16[2,512,1280]{2,1,0:T(8,128)(2,1)} %param.17) | copy-start | bytes 7864324
  22.3 39.1 %collective-permute-start = (f32[20,64,128]{2,1,0:T(8,128)}, f32[20,64,128]{2,1,0:T(8,128)}, u32[]{:S(2)}, u32[]{:S(2)}) collective-permute-start(f32[20,64,128]{2,1,0:T(8,128)} %fusion.20), channel_id=1, source_target_pairs={{0,2},{2,0},{4,6},{6,4},{8,10},{10,8},{12,14},{14,12},{1,3},{3,1},... | collective-permute-start | bytes 1966088 | tf_op jit(solution)/shard_map/ppermute | solution.py:20
  28.5 5.6 %copy-start.1 = (bf16[2,512,1280]{1,2,0:T(8,128)(2,1)S(1)}, bf16[2,512,1280]{1,2,0:T(8,128)(2,1)}, u32[]{:S(2)}) copy-start(bf16[2,512,1280]{1,2,0:T(8,128)(2,1)} %reduce-precision_convert_fusion.1) | copy-start | bytes 7864324
  28.5 5.6 %copy-start.4 = (bf16[2,512,1280]{1,2,0:T(8,128)(2,1)S(1)}, bf16[2,512,1280]{1,2,0:T(8,128)(2,1)}, u32[]{:S(2)}) copy-start(bf16[2,512,1280]{1,2,0:T(8,128)(2,1)} %get-tuple-element.28) | copy-start | bytes 7864324
  34.1 9.8 %copy-start.15 = (bf16[256,128]{1,0:T(8,128)(2,1)S(1)}, bf16[256,128]{1,0:T(8,128)(2,1)}, u32[]{:S(2)}) copy-start(bf16[256,128]{1,0:T(8,128)(2,1)} %param.10) | copy-start | bytes 196612
  37.2 5.4 %collective-permute-start.5 = (f32[40]{0:T(128)S(1)}, f32[40]{0:T(128)S(1)}, u32[]{:S(2)}, u32[]{:S(2)}) collective-permute-start(f32[40]{0:T(128)S(1)} %add.60), channel_id=1, source_target_pairs={{2,0},{3,1},{4,2},{5,3},{6,4},{7,5},{8,6},{9,7},{10,8},{11,9},{12,... | collective-permute-start | bytes 488 | tf_op jit(solution)/shard_map/ppermute | solution.py:30
  42.6 5.4 %collective-permute-start.6 = (f32[40]{0:T(128)S(1)}, f32[40]{0:T(128)S(1)}, u32[]{:S(2)}, u32[]{:S(2)}) collective-permute-start(f32[40]{0:T(128)S(1)} %add.61), channel_id=1, source_target_pairs={{4,0},{5,1},{6,2},{7,3},{8,4},{9,5},{10,6},{11,7},{12,8},{13,9},{1... | collective-permute-start | bytes 488 | tf_op jit(solution)/shard_map/ppermute | solution.py:30
  44.1 13.0 %copy-start.13 = (f32[256,128]{0,1:T(8,128)}, f32[256,128]{0,1:T(8,128)S(1)}, u32[]{:S(2)}) copy-start(f32[256,128]{0,1:T(8,128)S(1)} %copy.69) | copy-start | bytes 393220
  48.1 6.3 %collective-permute-start.7 = (f32[40]{0:T(128)S(1)}, f32[40]{0:T(128)S(1)}, u32[]{:S(2)}, u32[]{:S(2)}) collective-permute-start(f32[40]{0:T(128)S(1)} %add.62), channel_id=1, source_target_pairs={{8,0},{9,1},{10,2},{11,3},{12,4},{13,5},{14,6},{15,7},{24,16},{25,... | collective-permute-start | bytes 488 | tf_op jit(solution)/shard_map/ppermute | solution.py:30
  54.5 2.8 %copy-start.3 = (bf16[2,512,1280]{1,2,0:T(8,128)(2,1)S(1)}, bf16[2,512,1280]{1,2,0:T(8,128)(2,1)}, u32[]{:S(2)}) copy-start(bf16[2,512,1280]{1,2,0:T(8,128)(2,1)} %get-tuple-element.20) | copy-start | bytes 7864324
  54.5 2.9 %copy-start.5 = (bf16[2,512,1280]{1,2,0:T(8,128)(2,1)S(1)}, bf16[2,512,1280]{1,2,0:T(8,128)(2,1)}, u32[]{:S(2)}) copy-start(bf16[2,512,1280]{1,2,0:T(8,128)(2,1)} %get-tuple-element.28) | copy-start | bytes 7864324
  57.1 7.3 %collective-permute-start.9 = (f32[20,64,128]{2,1,0:T(8,128)S(1)}, f32[20,64,128]{2,1,0:T(8,128)S(1)}, u32[]{:S(2)}, u32[]{:S(2)}) collective-permute-start(f32[20,64,128]{2,1,0:T(8,128)S(1)} %slice_select_fusion), channel_id=1, source_target_pairs={{0,1},{1,0},{2,3},{3,2},{4,5},{5,4},{6,7},{7,6},{8,9},{9,8},{10,11... | collective-permute-start | bytes 1966088 | tf_op jit(solution)/shard_map/ppermute | solution.py:37
  62.8 6.8 %copy-start.12 = (f32[2,20,512]{2,0,1:T(2,128)S(1)}, f32[2,20,512]{2,0,1:T(2,128)}, u32[]{:S(2)}) copy-start(f32[2,20,512]{2,0,1:T(2,128)} %copy-done.11) | copy-start | bytes 245764
  62.8 17.1 %collective-permute-start.1 = (f32[20,64,128]{2,1,0:T(8,128)S(1)}, f32[20,64,128]{2,1,0:T(8,128)S(1)}, u32[]{:S(2)}, u32[]{:S(2)}) collective-permute-start(f32[20,64,128]{2,1,0:T(8,128)S(1)} %add.57), channel_id=1, source_target_pairs={{0,4},{2,6},{4,0},{6,2},{8,12},{10,14},{12,8},{14,10},{1,5},{3,7},... | collective-permute-start | bytes 1966088 | tf_op jit(solution)/shard_map/ppermute | solution.py:20
  64.6 5.0 %copy-start.10 = (bf16[2,512,128]{2,1,0:T(8,128)(2,1)S(1)}, bf16[2,512,128]{2,1,0:T(8,128)(2,1)}, u32[]{:S(2)}) copy-start(bf16[2,512,128]{2,1,0:T(8,128)(2,1)} %param.13) | copy-start | bytes 786436
  64.6 17.3 %collective-permute-start.10 = (f32[20,64,128]{2,1,0:T(8,128)S(1)}, f32[20,64,128]{2,1,0:T(8,128)S(1)}, u32[]{:S(2)}, u32[]{:S(2)}) collective-permute-start(f32[20,64,128]{2,1,0:T(8,128)S(1)} %select_add_fusion), channel_id=1, source_target_pairs={{0,2},{2,0},{4,6},{6,4},{8,10},{10,8},{12,14},{14,12},{1,3},{3,1},... | collective-permute-start | bytes 1966088 | tf_op jit(solution)/shard_map/ppermute | solution.py:20
  69.5 49.7 %collective-permute-start.8 = (f32[2,256,128]{2,1,0:T(8,128)}, f32[2,256,128]{2,1,0:T(8,128)}, u32[]{:S(2)}, u32[]{:S(2)}) collective-permute-start(f32[2,256,128]{2,1,0:T(8,128)} %select_bitcast_fusion.1), channel_id=1, source_target_pairs={{0,1},{1,0},{2,3},{3,2},{4,5},{5,4},{6,7},{7,6},{8,9},{9,8},{10,11... | collective-permute-start | bytes 786440 | tf_op jit(solution)/shard_map/ppermute | solution.py:37
  80.8 40.2 %collective-permute-start.2 = (f32[20,64,128]{2,1,0:T(8,128)}, f32[20,64,128]{2,1,0:T(8,128)}, u32[]{:S(2)}, u32[]{:S(2)}) collective-permute-start(f32[20,64,128]{2,1,0:T(8,128)} %add.58), channel_id=1, source_target_pairs={{0,8},{2,10},{4,12},{6,14},{8,0},{10,2},{12,4},{14,6},{1,9},{3,11}... | collective-permute-start | bytes 1966088 | tf_op jit(solution)/shard_map/ppermute | solution.py:20
  82.0 27.9 %collective-permute-start.11 = (f32[20,64,128]{2,1,0:T(8,128)S(1)}, f32[20,64,128]{2,1,0:T(8,128)S(1)}, u32[]{:S(2)}, u32[]{:S(2)}) collective-permute-start(f32[20,64,128]{2,1,0:T(8,128)S(1)} %add.70), channel_id=1, source_target_pairs={{0,4},{2,6},{4,0},{6,2},{8,12},{10,14},{12,8},{14,10},{1,5},{3,7},... | collective-permute-start | bytes 1966088 | tf_op jit(solution)/shard_map/ppermute | solution.py:20
  90.1 26.5 %copy-start.7 = (bf16[2,20,64,512]{3,2,1,0:T(8,128)(2,1)S(1)}, bf16[2,20,64,512]{3,2,1,0:T(8,128)(2,1)}, u32[]{:S(2)}) copy-start(bf16[2,20,64,512]{3,2,1,0:T(8,128)(2,1)} %fusion.17) | copy-start | bytes 7864324
  110.9 31.8 %collective-permute-start.12 = (f32[20,64,128]{2,1,0:T(8,128)}, f32[20,64,128]{2,1,0:T(8,128)}, u32[]{:S(2)}, u32[]{:S(2)}) collective-permute-start(f32[20,64,128]{2,1,0:T(8,128)} %add.71), channel_id=1, source_target_pairs={{0,8},{2,10},{4,12},{6,14},{8,0},{10,2},{12,4},{14,6},{1,9},{3,11}... | collective-permute-start | bytes 1966088 | tf_op jit(solution)/shard_map/ppermute | solution.py:20
  119.2 24.9 %copy-start.2 = (bf16[2,512,1280]{1,2,0:T(8,128)(2,1)S(1)}, bf16[2,512,1280]{1,2,0:T(8,128)(2,1)}, u32[]{:S(2)}) copy-start(bf16[2,512,1280]{1,2,0:T(8,128)(2,1)} %reduce-precision_convert_fusion.1) | copy-start | bytes 7864324
  119.2 24.9 %copy-start.8 = (f32[2,512,128]{2,1,0:T(8,128)S(1)}, f32[2,512,128]{2,1,0:T(8,128)}, u32[]{:S(2)}) copy-start(f32[2,512,128]{2,1,0:T(8,128)} %fusion.34) | copy-start | bytes 1572868
  122.4 22.7 %collective-permute-start.3 = (bf16[20,64,128]{2,1,0:T(8,128)(2,1)S(1)}, bf16[20,64,128]{2,1,0:T(8,128)(2,1)S(1)}, u32[]{:S(2)}, u32[]{:S(2)}) collective-permute-start(bf16[20,64,128]{2,1,0:T(8,128)(2,1)S(1)} %add_convert_fusion.1), channel_id=1, source_target_pairs={{0,1},{1,0},{2,3},{3,2},{4,5},{5,4},{6,7},{7,6},{8,9},{9,8},{10,11... | collective-permute-start | bytes 983048 | tf_op jit(solution)/shard_map/ppermute | solution.py:37
  144.0 1.3 copy-start.9
  145.0 2.0 %copy-start.14 = (f32[256,128]{0,1:T(8,128)S(1)}, f32[256,128]{0,1:T(8,128)}, u32[]{:S(2)}) copy-start(f32[256,128]{0,1:T(8,128)} %copy-done.13) | copy-start | bytes 393220
  145.0 4.2 %collective-permute-start.13 = (f32[2,256,128]{2,1,0:T(8,128)S(1)}, f32[2,256,128]{2,1,0:T(8,128)S(1)}, u32[]{:S(2)}, u32[]{:S(2)}) collective-permute-start(f32[2,256,128]{2,1,0:T(8,128)S(1)} %select_bitcast_fusion), channel_id=1, source_target_pairs={{0,1},{1,0},{2,3},{3,2},{4,5},{5,4},{6,7},{7,6},{8,9},{9,8},{10,11... | collective-permute-start | bytes 786440 | tf_op jit(solution)/shard_map/ppermute | solution.py:37

commit v5 on v4

--- a/solution.py
+++ b/solution.py
@@ -30,6 +30,47 @@
         value = value + lax.ppermute(value, axis, back)
         step *= 2
     return value
+
+
+def halving_scatter(blocks, axis):
+    count = lax.axis_size(axis)
+    me = lax.axis_index(axis)
+    rest = blocks.shape[1:]
+    value = blocks
+    step = count // 2
+    while step >= 1:
+        value = value.reshape((2, -1) + rest)
+        upper = me // step % 2 == 1
+        keep = jnp.where(upper, value[1], value[0])
+        give = jnp.where(upper, value[0], value[1])
+        value = keep + lax.ppermute(give, axis, [(at, at ^ step) for at in range(count)])
+        step //= 2
+    return value[0]
+
+
+def doubling_gather(piece, axis):
+    count = lax.axis_size(axis)
+    me = lax.axis_index(axis)
+    value = piece[None]
+    step = 1
+    while step < count:
+        other = lax.ppermute(value, axis, [(at, at ^ step) for at in range(count)])
+        upper = me // step % 2 == 1
+        value = jnp.where(
+            upper, jnp.concatenate([other, value]), jnp.concatenate([value, other])
+        )
+        step *= 2
+    return value
+
+
+def cand_sum_bf16(state):
+    heads, size, width = state.shape
+    count = lax.axis_size("cand")
+    piece = size // count
+    blocks = jnp.transpose(state.reshape(heads, count, piece, width), (1, 0, 2, 3))
+    summed = halving_scatter(blocks, "cand").astype(jnp.bfloat16)
+    gathered = doubling_gather(summed, "cand")
+    return jnp.transpose(gathered, (1, 0, 2, 3)).reshape(heads, size, width)
 
 
 def other_core(value):
@@ -61,7 +102,7 @@
     mine_first = seq_at == 0
     own_half = jnp.where(mine_first, state_halves[0], state_halves[1])
     give_half = jnp.where(mine_first, state_halves[1], state_halves[0])
-    init_half = butterfly_sum(own_half + other_core(give_half), "cand").astype(jnp.bfloat16)
+    init_half = cand_sum_bf16(own_half + other_core(give_half))
 
     position = jnp.arange(cand_len, dtype=jnp.int32)
     valid_rows = position[None, :] < lengths[:, None] * BLOCK
@@ -76,7 +117,7 @@
     x_high, x_low = split_bf16(xc_heads.astype(jnp.float32) * inverse[:, :, :, None])
 
     dstate = jnp.einsum("cthp,ctn->hpn", decayed_g, c_cand, preferred_element_type=jnp.float32)
-    grad_half = butterfly_sum(dstate, "cand").astype(jnp.bfloat16)
+    grad_half = cand_sum_bf16(dstate)
     grad_other = other_core(grad_half)
     grad_state = jnp.where(
         mine_first,

time: 150 us -> 141 us (0.940)
  waiting for transfers between devices: 60.4 us -> 31.4 us
  local copies, waits for them, and re-layouts: 15.8 us -> 25.1 us
  other arithmetic: 23.2 us -> 30.3 us
  starting transfers between devices: 19.7 us -> 25.8 us
  matrix products: 29.7 us -> 26.3 us
    ppermute x6 -> x12, waiting for transfers between devices: 49.8 us -> 26.3 us  [the longest x6 14.3 us: halving_scatter(): lax.ppermute(give, axis, [(at, at ^ step) for at in range(count)])]
    ppermute x6 -> x12, starting transfers between devices: 14.2 us -> 20.3 us  [the longest x6 13.7 us: halving_scatter(): lax.ppermute(give, axis, [(at, at ^ step) for at in range(count)])]
    ppermute x4, waiting for transfers between devices: 10.5 us -> 5.08 us  [suffix_sum(): value = value + lax.ppermute(value, axis, back)]
    dot_general x3, matrix products: 12.5 us -> 7.58 us  [pair(): jnp.einsum('ctk,csk->cts', left.reshape(flat), right.reshape(flat), prefe...]
    unnamed x38 -> x64, local copies, waits for them, and re-layouts: 15 us -> 18.3 us
    convert_element_type x2, other arithmetic: 2.74 us -> 0.03 us  [cand_sum_bf16(): summed = halving_scatter(blocks, 'cand').astype(jnp.bfloat16)]
    select_n x0 -> x11, other arithmetic: none -> 2.5 us  [the longest x6 2.38 us: halving_scatter(): give = jnp.where(upper, value[0], value[1])]
    exp x4, local copies, waits for them, and re-layouts: 0.12 us -> 1.66 us  [shards(): amplitude = jnp.exp(level_all)]
  transfers between devices with their start and end apart: 14 -> 20, of which waited for: 6 -> 11; matrix products, arithmetic and copies ran while one was open for 44% -> 55% of each run, Pallas kernels for 0% -> 0%
where the time goes in v5:
time: 141 us; the launch traced here: 140 us
  waiting for transfers between devices  31.4 us (22%)
  other arithmetic  30.3 us (21%)
  matrix products  26.3 us (19%)
  starting transfers between devices  25.8 us (18%)
  local copies, waits for them, and re-layouts  25.1 us (18%)
    unnamed x64, local copies, waits for them, and re-layouts  18.3 us
    ppermute x6, waiting for transfers between devices, halving_scatter(): lax.ppermute(give, axis, [(at, at ^ step) for at in range(count)])  14.3 us
    ppermute x6, starting transfers between devices, halving_scatter(): lax.ppermute(give, axis, [(at, at ^ step) for at in range(count)])  13.7 us
    ppermute x6, waiting for transfers between devices, doubling_gather(): other = lax.ppermute(value, axis, [(at, at ^ step) for at in range(count)])  12 us
    dot_general x3, matrix products, pair(): jnp.einsum('ctk,csk->cts', left.reshape(flat), right.reshape(flat), prefe...  7.58 us
    ppermute x6, starting transfers between devices, doubling_gather(): other = lax.ppermute(value, axis, [(at, at ^ step) for at in range(count)])  6.59 us
    dot_general x1, matrix products, shards(): jnp.einsum('chts,cthp->cshp', kernel, g_heads, preferred_element_type=jnp...  6.48 us
    convert_element_type x1, other arithmetic, split_bf16(): low = (value - high).astype(jnp.bfloat16)  5.66 us
  transfers between devices with their start and end apart: 20, of which 11 were waited for; matrix products, arithmetic and copies ran while one was open for 55% of the time, Pallas kernels for 0%

profile of v5, /device:TPU:0, one launch (start us, length us, event | category | flops | bytes accessed | tf_op | source)
XLA Modules:
  0.0 140.2 jit_solution(9239477175462654141)
XLA Ops:
  0.6 1.6 %fusion.31 = (f32[40]{0:T(128)S(1)}, f32[5,2,8,128]{3,2,1,0:T(8,128)}) fusion(s32[256,40]{0,1:T(8,128)} %param.11), kind=kLoop, calls=%fused_computation.80 | loop fusion | flops 40920 | bytes 82080 | tf_op jit(solution)/shard_map/reduce_sum | solution.py:91
  2.2 1.3 collective-permute-start.7
  4.3 1.0 log-plus-one_bitcast_fusion
  5.4 2.3 %reduce-window.14 = f32[2,20,4,128]{3,1,2,0:T(8,128)S(1)} reduce-window(f32[2,20,4,128]{3,1,2,0:T(8,128)S(1)} %copy.63, f32[]{:T(128)} %constant.110.clone.1), window={size=1x1x1x128 pad=0_0x0_0x0_0x127_0}, to_apply=%region_0.0 | reduce-window | flops 2600960 | bytes 163844 | tf_op jit(solution)/shard_map/reduce-window
  8.9 4.6 %copy.76 = bf16[2,512,1280]{1,2,0:T(8,128)(2,1)} copy(bf16[2,512,1280]{2,1,0:T(8,128)(2,1)} %param.12) | data formatting | bytes 5242880 | tf_op args[3]
  13.6 2.6 %copy.62 = bf16[2,512,1280]{1,2,0:T(8,128)(2,1)} copy(bf16[2,512,1280]{2,1,0:T(8,128)(2,1)S(1)} %copy-done.11) | data formatting | bytes 5242880 | tf_op args[8]
  16.2 5.7 %fusion.6 = (bf16[2,512,1280]{1,2,0:T(8,128)(2,1)}, bf16[2,512,1280]{1,2,0:T(8,128)(2,1)S(1)}, bf16[2,512,1280]{1,2,0:T(8,128)(2,1)}, bf16[2,512,1280]{1,2,0:T(8,128)(2,1)}) fusion(f32[2,512,20]{1,2,0:T(8,128)S(1)} %copy.65, bf16[2,512,1280]{1,2,0:T(8,128)(2,1)} %copy.62, pred[2,512]{1,0:T(4,128)(4,1)S(1)} %iota_compare_fusion.1, ...), kind=kLoop, calls=%fused_computation.11 | loop fusion | flops 15728640 | bytes 15893504 | tf_op jit(solution)/shard_map/convert_element_type | solution.py:11
  21.9 1.8 %fusion.22 = f32[8,20,8,128]{3,2,0,1:T(8,128)S(1)} fusion(bf16[2,512,20,64]{1,3,2,0:T(8,128)(2,1)S(1)} %bitcast.140, f32[2,512,20]{1,2,0:T(8,128)} %copy-done.19, bf16[2,512,128]{2,1,0:T(8,128)(2,1)S(1)} %copy-done), kind=kOutput, calls=%fused_computation.33 | convolution fusion | flops 340787200 | bytes 3620864 | tf_op jit(solution)/shard_map/cthp,ctn->hpn/dot_general | solution.py:119
  23.7 0.8 slice_select_fusion.2
  24.5 5.5 %collective-permute-start = (f32[4,20,8,128]{3,2,0,1:T(8,128)}, f32[4,20,8,128]{3,2,0,1:T(8,128)}, u32[]{:S(2)}, u32[]{:S(2)}) collective-permute-start(f32[4,20,8,128]{3,2,0,1:T(8,128)} %slice_select_fusion.2), channel_id=1, source_target_pairs={{0,8},{2,10},{4,12},{6,14},{8,0},{10,2},{12,4},{14,6},{1,9},{3,11}... | collective-permute-start | bytes 983048 | tf_op jit(solution)/shard_map/ppermute | solution.py:46
  30.0 0.8 iota_compare_fusion
  30.8 2.9 %reduce-precision_convert_fusion.1 = bf16[2,512,1280]{1,2,0:T(8,128)(2,1)} fusion(bf16[2,512,1280]{1,2,0:T(8,128)(2,1)S(1)} %get-tuple-element.21, f32[2,512,20]{1,2,0:T(8,128)} %copy-done.19), kind=kLoop, calls=%fused_computation.10 | loop fusion | flops 5242880 | bytes 5324800 | tf_op jit(solution)/shard_map/convert_element_type | solution.py:12
  33.7 4.2 %fusion.37 = f32[2,512,512]{2,1,0:T(8,128)S(1)} fusion(bf16[2,512,1280]{1,2,0:T(8,128)(2,1)} %reduce-precision_convert_fusion.1, bf16[2,512,1280]{1,2,0:T(8,128)(2,1)} %get-tuple-element.29), kind=kOutput, calls=%fused_computation.89 | convolution fusion | flops 1342177280 | bytes 7340032 | tf_op jit(solution)/shard_map/ctk,csk->cts/dot_general | solution.py:132
  38.0 1.6 %fusion.36 = f32[2,512,512]{2,1,0:T(8,128)S(1)} fusion(bf16[2,512,1280]{1,2,0:T(8,128)(2,1)S(1)} %copy-done.3, bf16[2,512,1280]{1,2,0:T(8,128)(2,1)S(1)} %copy-done.6), kind=kOutput, calls=%fused_computation.88 | convolution fusion | flops 1342177280 | bytes 7340032 | tf_op jit(solution)/shard_map/ctk,csk->cts/dot_general | solution.py:132
  39.7 1.8 %add_select_fusion = f32[2,512,512]{2,1,0:T(8,128)S(1)} fusion(f32[2,512,512]{2,1,0:T(8,128)S(1)} %fusion.36, f32[2,512,512]{2,1,0:T(8,128)S(1)} %fusion.37, bf16[2,512,1280]{1,2,0:T(8,128)(2,1)S(1)} %copy-done.5, bf16[2,512,1280]{1,2,0:T(8,128)(2,1)S(1)} %copy-done.6, pred[512,512]{1,0:T(8,128)(4,1)S(1)} %copy-done.12), kind=kOutput, calls=%fused_computation.29 | convolution fusion | flops 1343750144 | bytes 11796480 | tf_op jit(solution)/shard_map/ctk,csk->cts/dot_general | solution.py:132
  41.5 1.9 %fusion.38 = f32[2,512,128]{2,1,0:T(8,128)S(1)} fusion(f32[2,512,512]{2,1,0:T(8,128)S(1)} %add_select_fusion, bf16[2,512,128]{2,1,0:T(8,128)(2,1)S(1)} %copy-done), kind=kOutput, calls=%fused_computation.90 | convolution fusion | flops 805306368 | bytes 2883584 | tf_op jit(solution)/shard_map/cts,ctn->csn/dot_general | solution.py:139
  43.4 0.7 select_bitcast_fusion.1
  44.1 1.8 %fusion.35 = f32[2,512,512]{2,1,0:T(8,128)} fusion(bf16[2,512,128]{2,1,0:T(8,128)(2,1)S(1)} %copy-done, bf16[2,512,128]{2,1,0:T(8,128)(2,1)S(1)} %copy-done.17), kind=kOutput, calls=%fused_computation.87 | convolution fusion | flops 134217728 | bytes 2621440 | tf_op jit(solution)/shard_map/ctn,csn->cts/dot_general | solution.py:146
  46.5 1.9 %reduce-window.16 = f32[40,2,128]{2,0,1:T(8,128)} reduce-window(f32[40,2,128]{2,0,1:T(8,128)} %bitcast.153, f32[]{:T(128)} %constant.110.clone.1), window={size=1x1x128 pad=0_0x0_0x127_0}, to_apply=%region_3.4 | reduce-window | flops 1300480 | bytes 81924 | tf_op jit(solution)/shard_map/reduce-window.2
  48.4 1.3 collective-permute-start.8
  49.7 0.9 slice_reduce_fusion.1
  50.6 1.6 %copy.73 = f32[2,20,512]{2,1,0:T(8,128)} copy(f32[2,20,512]{2,0,1:T(2,128)} %copy-done.21) | data formatting | bytes 163840 | tf_op jit(solution)/shard_map/exp | solution.py:111
  52.2 1.6 %collective-permute-done.8 = f32[40]{0:T(128)S(1)} collective-permute-done((f32[40]{0:T(128)S(1)}, f32[40]{0:T(128)S(1)}, u32[]{:S(2)}, u32[]{:S(2)}) %collective-permute-start.8) | collective-permute-done | bytes 192 | tf_op jit(solution)/shard_map/ppermute | solution.py:30
  53.8 1.3 collective-permute-start.9
  55.1 1.5 %copy.75 = f32[2,20,512]{2,1,0:T(8,128)} copy(f32[2,20,512]{2,0,1:T(2,128)} %copy-done.20) | data formatting | bytes 163840 | tf_op jit(solution)/shard_map/exp | solution.py:112
  56.7 2.5 %collective-permute-done.9 = f32[40]{0:T(128)} collective-permute-done((f32[40]{0:T(128)S(1)}, f32[40]{0:T(128)}, u32[]{:S(2)}, u32[]{:S(2)}) %collective-permute-start.9) | collective-permute-done | bytes 192 | tf_op jit(solution)/shard_map/ppermute | solution.py:30
  59.2 0.7 add.87
  59.9 1.5 %collective-permute-start.10 = (f32[40]{0:T(128)S(1)}, f32[40]{0:T(128)}, u32[]{:S(2)}, u32[]{:S(2)}) collective-permute-start(f32[40]{0:T(128)S(1)} %add.87), channel_id=1, source_target_pairs={{8,0},{9,1},{10,2},{11,3},{12,4},{13,5},{14,6},{15,7},{24,16},{25,... | collective-permute-start | bytes 488 | tf_op jit(solution)/shard_map/ppermute | solution.py:30
  61.4 1.6 %copy.70 = f32[256,128]{0,1:T(8,128)} copy(bf16[256,128]{1,0:T(8,128)(2,1)} %param.10) | data formatting | bytes 196608 | tf_op jit(solution)/shard_map/convert_element_type | solution.py:95
  63.0 2.4 %copy.72 = bf16[256,2560]{0,1:T(8,128)(2,1)} copy(bf16[256,2560]{1,0:T(8,128)(2,1)} %param.9) | data formatting | bytes 2621440 | tf_op args[0]
  65.4 0.9 collective-permute-done.10
  66.9 0.9 fusion.29
  67.8 2.6 %fusion.21 = f32[40,64,128]{2,1,0:T(8,128)S(1)} fusion(bf16[256,40,64]{0,2,1:T(8,128)(2,1)} %bitcast.147, f32[256,128]{0,1:T(8,128)} %copy.70, f32[256,40]{0,1:T(8,128)S(1)} %fusion.29), kind=kOutput, calls=%fused_computation.32 | convolution fusion | flops 170393600 | bytes 2793472 | tf_op jit(solution)/shard_map/jhp,jhn->hpn/dot_general | solution.py:99
  70.4 1.1 copy-done.7
  71.5 0.9 slice_select_fusion
  72.5 6.5 %fusion.19 = bf16[2,20,64,512]{3,2,1,0:T(8,128)(2,1)} fusion(bf16[2,512,20,64]{1,3,2,0:T(8,128)(2,1)S(1)} %bitcast.141, f32[2,20,512]{2,1,0:T(8,128)S(1)} %copy-done.25, f32[2,20,512]{2,1,0:T(8,128)S(1)} %copy-done.24, f32[2,512,512]{2,1,0:T(8,128)S(1)} %copy-done.14, pred[512,512]{1,0:T(8,128)(4,1)S(1)} %copy-done.13), kind=kOutput, calls=%fused_computation.30 | convolution fusion | flops 1385431040 | bytes 7766016 | tf_op jit(solution)/shard_map/chts,cthp->cshp/dot_general | solution.py:151
  79.0 1.2 select_add_fusion.1
  80.1 0.8 slice_select_fusion.4
  80.9 1.6 %collective-permute-start.1 = (f32[2,20,8,128]{3,2,0,1:T(8,128)}, f32[2,20,8,128]{3,2,0,1:T(8,128)}, u32[]{:S(2)}, u32[]{:S(2)}) collective-permute-start(f32[2,20,8,128]{3,2,0,1:T(8,128)} %slice_select_fusion.4), channel_id=1, source_target_pairs={{0,4},{2,6},{4,0},{6,2},{8,12},{10,14},{12,8},{14,10},{1,5},{3,7},... | collective-permute-start | bytes 491528 | tf_op jit(solution)/shard_map/ppermute | solution.py:46
  82.5 1.2 add_bitcast_fusion
  83.7 0.8 slice_select_fusion.1
  84.5 2.9 %collective-permute-start.13 = (f32[4,20,8,128]{3,2,0,1:T(8,128)}, f32[4,20,8,128]{3,2,0,1:T(8,128)}, u32[]{:S(2)}, u32[]{:S(2)}) collective-permute-start(f32[4,20,8,128]{3,2,0,1:T(8,128)} %slice_select_fusion.1), channel_id=1, source_target_pairs={{0,8},{2,10},{4,12},{6,14},{8,0},{10,2},{12,4},{14,6},{1,9},{3,11}... | collective-permute-start | bytes 983048 | tf_op jit(solution)/shard_map/ppermute | solution.py:46
  87.4 1.9 %fusion.39 = f32[2,512,128]{2,1,0:T(8,128)} fusion(f32[2,512,512]{2,1,0:T(8,128)S(1)} %add_select_fusion, bf16[2,512,128]{2,1,0:T(8,128)(2,1)S(1)} %copy-done.18), kind=kOutput, calls=%fused_computation.91 | convolution fusion | flops 805306368 | bytes 2883584 | tf_op jit(solution)/shard_map/cts,csn->ctn/dot_general | solution.py:142
  89.3 4.4 %copy.93 = bf16[2,512,1280]{2,1,0:T(8,128)(2,1)} copy(bf16[2,512,1280]{1,2,0:T(8,128)(2,1)} %bitcast.146) | data formatting | bytes 5242880
  93.7 0.9 select_add_fusion.3
  94.7 8.1 %collective-permute-done.13 = f32[4,20,8,128]{3,2,0,1:T(8,128)} collective-permute-done((f32[4,20,8,128]{3,2,0,1:T(8,128)}, f32[4,20,8,128]{3,2,0,1:T(8,128)}, u32[]{:S(2)}, u32[]{:S(2)}) %collective-permute-start.13) | collective-permute-done | bytes 327712 | tf_op jit(solution)/shard_map/ppermute | solution.py:46
  102.8 1.0 select_add_fusion
  104.0 1.9 %collective-permute-start.2 = (f32[1,20,8,128]{3,2,0,1:T(8,128)S(1)}, f32[1,20,8,128]{3,2,0,1:T(8,128)S(1)}, u32[]{:S(2)}, u32[]{:S(2)}) collective-permute-start(f32[1,20,8,128]{3,2,0,1:T(8,128)S(1)} %slice_select_fusion.6), channel_id=1, source_target_pairs={{0,2},{2,0},{4,6},{6,4},{8,10},{10,8},{12,14},{14,12},{1,3},{3,1},... | collective-permute-start | bytes 245768 | tf_op jit(solution)/shard_map/ppermute | solution.py:46
  105.8 3.9 %collective-permute-done.14 = f32[2,20,8,128]{3,2,0,1:T(8,128)S(1)} collective-permute-done((f32[2,20,8,128]{3,2,0,1:T(8,128)S(1)}, f32[2,20,8,128]{3,2,0,1:T(8,128)S(1)}, u32[]{:S(2)}, u32[]{:S(2)}) %collective-permute-start.14) | collective-permute-done | bytes 163872 | tf_op jit(solution)/shard_map/ppermute | solution.py:46
  109.8 1.9 %collective-permute-start.15 = (f32[1,20,8,128]{3,2,0,1:T(8,128)S(1)}, f32[1,20,8,128]{3,2,0,1:T(8,128)S(1)}, u32[]{:S(2)}, u32[]{:S(2)}) collective-permute-start(f32[1,20,8,128]{3,2,0,1:T(8,128)S(1)} %slice_select_fusion.5), channel_id=1, source_target_pairs={{0,2},{2,0},{4,6},{6,4},{8,10},{10,8},{12,14},{14,12},{1,3},{3,1},... | collective-permute-start | bytes 245768 | tf_op jit(solution)/shard_map/ppermute | solution.py:46
  112.0 2.3 %collective-permute-done.15 = f32[1,20,8,128]{3,2,0,1:T(8,128)S(1)} collective-permute-done((f32[1,20,8,128]{3,2,0,1:T(8,128)S(1)}, f32[1,20,8,128]{3,2,0,1:T(8,128)S(1)}, u32[]{:S(2)}, u32[]{:S(2)}) %collective-permute-start.15) | collective-permute-done | bytes 81952 | tf_op jit(solution)/shard_map/ppermute | solution.py:46
  114.3 1.9 %collective-permute-start.16 = (bf16[1,20,8,128]{3,2,0,1:T(8,128)(2,1)S(1)}, bf16[1,20,8,128]{3,2,0,1:T(8,128)(2,1)S(1)}, u32[]{:S(2)}, u32[]{:S(2)}) collective-permute-start(bf16[1,20,8,128]{3,2,0,1:T(8,128)(2,1)S(1)} %add_convert_fusion), channel_id=1, source_target_pairs={{0,2},{2,0},{4,6},{6,4},{8,10},{10,8},{12,14},{14,12},{1,3},{3,1},... | collective-permute-start | bytes 122888 | tf_op jit(solution)/shard_map/ppermute | solution.py:57
  116.5 1.8 %collective-permute-done.16 = bf16[1,20,8,128]{3,2,0,1:T(8,128)(2,1)S(1)} collective-permute-done((bf16[1,20,8,128]{3,2,0,1:T(8,128)(2,1)S(1)}, bf16[1,20,8,128]{3,2,0,1:T(8,128)(2,1)S(1)}, u32[]{:S(2)}, u32[]{:S(2)}) %collective-permute-start.16) | collective-permute-done | bytes 40992 | tf_op jit(solution)/shard_map/ppermute | solution.py:57
  118.9 2.1 %collective-permute-done.4 = bf16[2,20,8,128]{3,2,0,1:T(8,128)(2,1)S(1)} collective-permute-done((bf16[2,20,8,128]{3,2,0,1:T(8,128)(2,1)S(1)}, bf16[2,20,8,128]{3,2,0,1:T(8,128)(2,1)S(1)}, u32[]{:S(2)}, u32[]{:S(2)}) %collective-permute-start.4) | collective-permute-done | bytes 81952 | tf_op jit(solution)/shard_map/ppermute | solution.py:57
  121.0 1.6 %collective-permute-start.5 = (bf16[4,20,8,128]{3,2,0,1:T(8,128)(2,1)S(1)}, bf16[4,20,8,128]{3,2,0,1:T(8,128)(2,1)S(1)}, u32[]{:S(2)}, u32[]{:S(2)}) collective-permute-start(bf16[4,20,8,128]{3,2,0,1:T(8,128)(2,1)S(1)} %maximum_select_fusion.3), channel_id=1, source_target_pairs={{0,8},{2,10},{4,12},{6,14},{8,0},{10,2},{12,4},{14,6},{1,9},{3,11}... | collective-permute-start | bytes 491528 | tf_op jit(solution)/shard_map/ppermute | solution.py:57
  123.1 1.9 %collective-permute-start.18 = (bf16[4,20,8,128]{3,2,0,1:T(8,128)(2,1)S(1)}, bf16[4,20,8,128]{3,2,0,1:T(8,128)(2,1)S(1)}, u32[]{:S(2)}, u32[]{:S(2)}) collective-permute-start(bf16[4,20,8,128]{3,2,0,1:T(8,128)(2,1)S(1)} %maximum_select_fusion.4), channel_id=1, source_target_pairs={{0,8},{2,10},{4,12},{6,14},{8,0},{10,2},{12,4},{14,6},{1,9},{3,11}... | collective-permute-start | bytes 491528 | tf_op jit(solution)/shard_map/ppermute | solution.py:57
  125.1 1.7 %bitcast_add_fusion.1 = f32[2,256,128]{2,1,0:T(8,128)} fusion(f32[2,256,128]{2,1,0:T(8,128)} %collective-permute-done.11, f32[2,2,256,128]{3,2,1,0:T(8,128)S(1)} %bitcast.145, pred[]{:T(512)S(6)} %eq.34), kind=kLoop, calls=%fused_computation.52 | loop fusion | flops 131072 | bytes 1048577 | tf_op jit(solution)/shard_map/add | solution.py:164
  126.8 6.0 %collective-permute-done.5 = bf16[4,20,8,128]{3,2,0,1:T(8,128)(2,1)S(1)} collective-permute-done((bf16[4,20,8,128]{3,2,0,1:T(8,128)(2,1)S(1)}, bf16[4,20,8,128]{3,2,0,1:T(8,128)(2,1)S(1)}, u32[]{:S(2)}, u32[]{:S(2)}) %collective-permute-start.5) | collective-permute-done | bytes 163872 | tf_op jit(solution)/shard_map/ppermute | solution.py:57
  132.9 1.6 %collective-permute-done.18 = bf16[4,20,8,128]{3,2,0,1:T(8,128)(2,1)S(1)} collective-permute-done((bf16[4,20,8,128]{3,2,0,1:T(8,128)(2,1)S(1)}, bf16[4,20,8,128]{3,2,0,1:T(8,128)(2,1)S(1)}, u32[]{:S(2)}, u32[]{:S(2)}) %collective-permute-start.18) | collective-permute-done | bytes 163872 | tf_op jit(solution)/shard_map/ppermute | solution.py:57
  134.6 0.9 convolution_add_fusion
  135.6 0.9 fusion.8
  136.5 0.8 copy.92
  137.8 1.6 %copy.91 = bf16[256,2560]{1,0:T(8,128)(2,1)} copy(bf16[256,2560]{0,1:T(8,128)(2,1)S(1)} %bitcast.149) | data formatting | bytes 2621440
  139.4 0.7 bitcast_add_fusion
  (109 shorter events, 6.2 us)
Async XLA Ops:
  0.6 21.2 %copy-start = (bf16[2,512,128]{2,1,0:T(8,128)(2,1)S(1)}, bf16[2,512,128]{2,1,0:T(8,128)(2,1)}, u32[]{:S(2)}) copy-start(bf16[2,512,128]{2,1,0:T(8,128)(2,1)} %param.14) | copy-start | bytes 786436
  2.2 46.2 %collective-permute-start.7 = (f32[40]{0:T(128)S(1)}, f32[40]{0:T(128)S(1)}, u32[]{:S(2)}, u32[]{:S(2)}) collective-permute-start(f32[40]{0:T(128)S(1)} %get-tuple-element.26), channel_id=1, source_target_pairs={{1,0},{2,1},{3,2},{4,3},{5,4},{6,5},{7,6},{8,7},{9,8},{10,9},{11,1... | collective-permute-start | bytes 488 | tf_op jit(solution)/shard_map/ppermute | solution.py:30
  8.2 0.6 copy-start.20
  8.3 0.6 copy-start.21
  8.3 7.9 %copy-start.19 = (f32[2,512,20]{1,2,0:T(8,128)}, f32[2,512,20]{1,2,0:T(8,128)S(1)}, u32[]{:S(2)}) copy-start(f32[2,512,20]{1,2,0:T(8,128)S(1)} %copy.65) | copy-start | bytes 245764
  8.9 4.6 %copy-start.11 = (bf16[2,512,1280]{2,1,0:T(8,128)(2,1)S(1)}, bf16[2,512,1280]{2,1,0:T(8,128)(2,1)}, u32[]{:S(2)}) copy-start(bf16[2,512,1280]{2,1,0:T(8,128)(2,1)} %param.17) | copy-start | bytes 7864324
  21.8 8.9 %copy-start.1 = (bf16[2,512,1280]{1,2,0:T(8,128)(2,1)}, bf16[2,512,1280]{1,2,0:T(8,128)(2,1)S(1)}, u32[]{:S(2)}) copy-start(bf16[2,512,1280]{1,2,0:T(8,128)(2,1)S(1)} %get-tuple-element.21) | copy-start | bytes 7864324
  24.5 54.5 %collective-permute-start = (f32[4,20,8,128]{3,2,0,1:T(8,128)}, f32[4,20,8,128]{3,2,0,1:T(8,128)}, u32[]{:S(2)}, u32[]{:S(2)}) collective-permute-start(f32[4,20,8,128]{3,2,0,1:T(8,128)} %slice_select_fusion.2), channel_id=1, source_target_pairs={{0,8},{2,10},{4,12},{6,14},{8,0},{10,2},{12,4},{14,6},{1,9},{3,11}... | collective-permute-start | bytes 983048 | tf_op jit(solution)/shard_map/ppermute | solution.py:46
  33.7 4.3 %copy-start.3 = (bf16[2,512,1280]{1,2,0:T(8,128)(2,1)S(1)}, bf16[2,512,1280]{1,2,0:T(8,128)(2,1)}, u32[]{:S(2)}) copy-start(bf16[2,512,1280]{1,2,0:T(8,128)(2,1)} %reduce-precision_convert_fusion.1) | copy-start | bytes 7864324
  33.7 4.3 %copy-start.6 = (bf16[2,512,1280]{1,2,0:T(8,128)(2,1)S(1)}, bf16[2,512,1280]{1,2,0:T(8,128)(2,1)}, u32[]{:S(2)}) copy-start(bf16[2,512,1280]{1,2,0:T(8,128)(2,1)} %get-tuple-element.28) | copy-start | bytes 7864324
  38.0 1.7 %copy-start.5 = (bf16[2,512,1280]{1,2,0:T(8,128)(2,1)S(1)}, bf16[2,512,1280]{1,2,0:T(8,128)(2,1)}, u32[]{:S(2)}) copy-start(bf16[2,512,1280]{1,2,0:T(8,128)(2,1)} %get-tuple-element.20) | copy-start | bytes 7864324
  38.0 1.7 %copy-start.12 = (pred[512,512]{1,0:T(8,128)(4,1)S(1)}, pred[512,512]{1,0:T(8,128)(4,1)}, u32[]{:S(2)}) copy-start(pred[512,512]{1,0:T(8,128)(4,1)} %iota_compare_fusion) | copy-start | bytes 786436
  41.5 2.6 %copy-start.17 = (bf16[2,512,128]{2,1,0:T(8,128)(2,1)S(1)}, bf16[2,512,128]{2,1,0:T(8,128)(2,1)}, u32[]{:S(2)}) copy-start(bf16[2,512,128]{2,1,0:T(8,128)(2,1)} %param.13) | copy-start | bytes 786436
  41.5 4.4 %copy-start.22 = (f32[5,2,8,128]{3,2,1,0:T(8,128)S(1)}, f32[5,2,8,128]{3,2,1,0:T(8,128)}, u32[]{:S(2)}) copy-start(f32[5,2,8,128]{3,2,1,0:T(8,128)} %get-tuple-element.27) | copy-start | bytes 122884
  44.1 81.0 %collective-permute-start.11 = (f32[2,256,128]{2,1,0:T(8,128)}, f32[2,256,128]{2,1,0:T(8,128)}, u32[]{:S(2)}, u32[]{:S(2)}) collective-permute-start(f32[2,256,128]{2,1,0:T(8,128)} %select_bitcast_fusion.1), channel_id=1, source_target_pairs={{0,1},{1,0},{2,3},{3,2},{4,5},{5,4},{6,7},{7,6},{8,9},{9,8},{10,11... | collective-permute-start | bytes 786440 | tf_op jit(solution)/shard_map/ppermute | solution.py:78
  48.4 5.4 %collective-permute-start.8 = (f32[40]{0:T(128)S(1)}, f32[40]{0:T(128)S(1)}, u32[]{:S(2)}, u32[]{:S(2)}) collective-permute-start(f32[40]{0:T(128)S(1)} %add.85), channel_id=1, source_target_pairs={{2,0},{3,1},{4,2},{5,3},{6,4},{7,5},{8,6},{9,7},{10,8},{11,9},{12,... | collective-permute-start | bytes 488 | tf_op jit(solution)/shard_map/ppermute | solution.py:30
  53.8 2.9 %copy-start.28 = (f32[40]{0:T(128)}, f32[40]{0:T(128)S(1)}, u32[]{:S(2)}) copy-start(f32[40]{0:T(128)S(1)} %add.86) | copy-start | bytes 484
  53.8 5.4 %collective-permute-start.9 = (f32[40]{0:T(128)S(1)}, f32[40]{0:T(128)}, u32[]{:S(2)}, u32[]{:S(2)}) collective-permute-start(f32[40]{0:T(128)S(1)} %add.86), channel_id=1, source_target_pairs={{4,0},{5,1},{6,2},{7,3},{8,4},{9,5},{10,6},{11,7},{12,8},{13,9},{1... | collective-permute-start | bytes 488 | tf_op jit(solution)/shard_map/ppermute | solution.py:30
  59.9 6.4 %collective-permute-start.10 = (f32[40]{0:T(128)S(1)}, f32[40]{0:T(128)}, u32[]{:S(2)}, u32[]{:S(2)}) collective-permute-start(f32[40]{0:T(128)S(1)} %add.87), channel_id=1, source_target_pairs={{8,0},{9,1},{10,2},{11,3},{12,4},{13,5},{14,6},{15,7},{24,16},{25,... | collective-permute-start | bytes 488 | tf_op jit(solution)/shard_map/ppermute | solution.py:30
  67.8 4.6 %copy-start.26 = (f32[256,40]{0,1:T(8,128)}, f32[256,40]{0,1:T(8,128)S(1)}, u32[]{:S(2)}) copy-start(f32[256,40]{0,1:T(8,128)S(1)} %fusion.29) | copy-start | bytes 122884
  67.8 4.6 %copy-start.2 = (bf16[2,512,1280]{1,2,0:T(8,128)(2,1)S(1)}, bf16[2,512,1280]{1,2,0:T(8,128)(2,1)}, u32[]{:S(2)}) copy-start(bf16[2,512,1280]{1,2,0:T(8,128)(2,1)} %copy-done.1) | copy-start | bytes 7864324
  67.8 4.6 %copy-start.13 = (pred[512,512]{1,0:T(8,128)(4,1)S(1)}, pred[512,512]{1,0:T(8,128)(4,1)}, u32[]{:S(2)}) copy-start(pred[512,512]{1,0:T(8,128)(4,1)} %iota_compare_fusion) | copy-start | bytes 786436
  67.8 4.6 %copy-start.14 = (f32[2,512,512]{2,1,0:T(8,128)S(1)}, f32[2,512,512]{2,1,0:T(8,128)}, u32[]{:S(2)}) copy-start(f32[2,512,512]{2,1,0:T(8,128)} %fusion.35) | copy-start | bytes 6291460
  67.8 4.6 %copy-start.24 = (f32[2,20,512]{2,1,0:T(8,128)S(1)}, f32[2,20,512]{2,1,0:T(8,128)}, u32[]{:S(2)}) copy-start(f32[2,20,512]{2,1,0:T(8,128)} %copy.73) | copy-start | bytes 245764
  67.8 4.6 %copy-start.25 = (f32[2,20,512]{2,1,0:T(8,128)S(1)}, f32[2,20,512]{2,1,0:T(8,128)}, u32[]{:S(2)}) copy-start(f32[2,20,512]{2,1,0:T(8,128)} %copy.75) | copy-start | bytes 245764
  70.4 1.1 copy-start.7
  72.4 10.1 %collective-permute-start.12 = (f32[20,64,128]{2,1,0:T(8,128)}, f32[20,64,128]{2,1,0:T(8,128)}, u32[]{:S(2)}, u32[]{:S(2)}) collective-permute-start(f32[20,64,128]{2,1,0:T(8,128)} %slice_select_fusion), channel_id=1, source_target_pairs={{0,1},{1,0},{2,3},{3,2},{4,5},{5,4},{6,7},{7,6},{8,9},{9,8},{10,11... | collective-permute-start | bytes 1966088 | tf_op jit(solution)/shard_map/ppermute | solution.py:78
  78.9 3.5 %copy-start.8 = (f32[40,64,128]{2,1,0:T(8,128)S(1)}, f32[40,64,128]{2,1,0:T(8,128)}, u32[]{:S(2)}) copy-start(f32[40,64,128]{2,1,0:T(8,128)} %copy-done.7) | copy-start | bytes 3932164
  78.9 8.4 %copy-start.18 = (bf16[2,512,128]{2,1,0:T(8,128)(2,1)S(1)}, bf16[2,512,128]{2,1,0:T(8,128)(2,1)}, u32[]{:S(2)}) copy-start(bf16[2,512,128]{2,1,0:T(8,128)(2,1)} %param.13) | copy-start | bytes 786436
  80.1 2.4 %copy-start.9 = (f32[4,20,8,128]{3,2,0,1:T(8,128)}, f32[4,20,8,128]{3,2,0,1:T(8,128)S(1)}, u32[]{:S(2)}) copy-start(f32[4,20,8,128]{3,2,0,1:T(8,128)S(1)} %select_add_fusion.1) | copy-start | bytes 983044
  80.9 12.8 %collective-permute-start.1 = (f32[2,20,8,128]{3,2,0,1:T(8,128)}, f32[2,20,8,128]{3,2,0,1:T(8,128)}, u32[]{:S(2)}, u32[]{:S(2)}) collective-permute-start(f32[2,20,8,128]{3,2,0,1:T(8,128)} %slice_select_fusion.4), channel_id=1, source_target_pairs={{0,4},{2,6},{4,0},{6,2},{8,12},{10,14},{12,8},{14,10},{1,5},{3,7},... | collective-permute-start | bytes 491528 | tf_op jit(solution)/shard_map/ppermute | solution.py:46
  84.5 18.3 %collective-permute-start.13 = (f32[4,20,8,128]{3,2,0,1:T(8,128)}, f32[4,20,8,128]{3,2,0,1:T(8,128)}, u32[]{:S(2)}, u32[]{:S(2)}) collective-permute-start(f32[4,20,8,128]{3,2,0,1:T(8,128)} %slice_select_fusion.1), channel_id=1, source_target_pairs={{0,8},{2,10},{4,12},{6,14},{8,0},{10,2},{12,4},{14,6},{1,9},{3,11}... | collective-permute-start | bytes 983048 | tf_op jit(solution)/shard_map/ppermute | solution.py:46
  89.3 4.4 %copy-start.10 = (f32[4,20,8,128]{3,2,0,1:T(8,128)S(1)}, f32[4,20,8,128]{3,2,0,1:T(8,128)}, u32[]{:S(2)}) copy-start(f32[4,20,8,128]{3,2,0,1:T(8,128)} %copy-done.9) | copy-start | bytes 983044
  103.9 30.7 %copy-start.4 = (bf16[2,512,1280]{1,2,0:T(8,128)(2,1)S(1)}, bf16[2,512,1280]{1,2,0:T(8,128)(2,1)}, u32[]{:S(2)}) copy-start(bf16[2,512,1280]{1,2,0:T(8,128)(2,1)} %reduce-precision_convert_fusion.1) | copy-start | bytes 7864324
  103.9 30.7 %copy-start.15 = (f32[2,512,128]{2,1,0:T(8,128)S(1)}, f32[2,512,128]{2,1,0:T(8,128)}, u32[]{:S(2)}) copy-start(f32[2,512,128]{2,1,0:T(8,128)} %fusion.39) | copy-start | bytes 1572868
  103.9 5.8 %collective-permute-start.14 = (f32[2,20,8,128]{3,2,0,1:T(8,128)S(1)}, f32[2,20,8,128]{3,2,0,1:T(8,128)S(1)}, u32[]{:S(2)}, u32[]{:S(2)}) collective-permute-start(f32[2,20,8,128]{3,2,0,1:T(8,128)S(1)} %slice_select_fusion.3), channel_id=1, source_target_pairs={{0,4},{2,6},{4,0},{6,2},{8,12},{10,14},{12,8},{14,10},{1,5},{3,7},... | collective-permute-start | bytes 491528 | tf_op jit(solution)/shard_map/ppermute | solution.py:46
  104.0 7.6 %collective-permute-start.2 = (f32[1,20,8,128]{3,2,0,1:T(8,128)S(1)}, f32[1,20,8,128]{3,2,0,1:T(8,128)S(1)}, u32[]{:S(2)}, u32[]{:S(2)}) collective-permute-start(f32[1,20,8,128]{3,2,0,1:T(8,128)S(1)} %slice_select_fusion.6), channel_id=1, source_target_pairs={{0,2},{2,0},{4,6},{6,4},{8,10},{10,8},{12,14},{14,12},{1,3},{3,1},... | collective-permute-start | bytes 245768 | tf_op jit(solution)/shard_map/ppermute | solution.py:46
  109.8 4.5 %collective-permute-start.15 = (f32[1,20,8,128]{3,2,0,1:T(8,128)S(1)}, f32[1,20,8,128]{3,2,0,1:T(8,128)S(1)}, u32[]{:S(2)}, u32[]{:S(2)}) collective-permute-start(f32[1,20,8,128]{3,2,0,1:T(8,128)S(1)} %slice_select_fusion.5), channel_id=1, source_target_pairs={{0,2},{2,0},{4,6},{6,4},{8,10},{10,8},{12,14},{14,12},{1,3},{3,1},... | collective-permute-start | bytes 245768 | tf_op jit(solution)/shard_map/ppermute | solution.py:46
  111.7 4.5 %collective-permute-start.3 = (bf16[1,20,8,128]{3,2,0,1:T(8,128)(2,1)S(1)}, bf16[1,20,8,128]{3,2,0,1:T(8,128)(2,1)S(1)}, u32[]{:S(2)}, u32[]{:S(2)}) collective-permute-start(bf16[1,20,8,128]{3,2,0,1:T(8,128)(2,1)S(1)} %add_convert_fusion.1), channel_id=1, source_target_pairs={{0,2},{2,0},{4,6},{6,4},{8,10},{10,8},{12,14},{14,12},{1,3},{3,1},... | collective-permute-start | bytes 122888 | tf_op jit(solution)/shard_map/ppermute | solution.py:57
  114.3 4.1 %collective-permute-start.16 = (bf16[1,20,8,128]{3,2,0,1:T(8,128)(2,1)S(1)}, bf16[1,20,8,128]{3,2,0,1:T(8,128)(2,1)S(1)}, u32[]{:S(2)}, u32[]{:S(2)}) collective-permute-start(bf16[1,20,8,128]{3,2,0,1:T(8,128)(2,1)S(1)} %add_convert_fusion), channel_id=1, source_target_pairs={{0,2},{2,0},{4,6},{6,4},{8,10},{10,8},{12,14},{14,12},{1,3},{3,1},... | collective-permute-start | bytes 122888 | tf_op jit(solution)/shard_map/ppermute | solution.py:57
  116.2 4.8 %collective-permute-start.4 = (bf16[2,20,8,128]{3,2,0,1:T(8,128)(2,1)S(1)}, bf16[2,20,8,128]{3,2,0,1:T(8,128)(2,1)S(1)}, u32[]{:S(2)}, u32[]{:S(2)}) collective-permute-start(bf16[2,20,8,128]{3,2,0,1:T(8,128)(2,1)S(1)} %maximum_select_fusion.7), channel_id=1, source_target_pairs={{0,4},{2,6},{4,0},{6,2},{8,12},{10,14},{12,8},{14,10},{1,5},{3,7},... | collective-permute-start | bytes 245768 | tf_op jit(solution)/shard_map/ppermute | solution.py:57
  118.4 4.7 %collective-permute-start.17 = (bf16[2,20,8,128]{3,2,0,1:T(8,128)(2,1)S(1)}, bf16[2,20,8,128]{3,2,0,1:T(8,128)(2,1)S(1)}, u32[]{:S(2)}, u32[]{:S(2)}) collective-permute-start(bf16[2,20,8,128]{3,2,0,1:T(8,128)(2,1)S(1)} %maximum_select_fusion.8), channel_id=1, source_target_pairs={{0,4},{2,6},{4,0},{6,2},{8,12},{10,14},{12,8},{14,10},{1,5},{3,7},... | collective-permute-start | bytes 245768 | tf_op jit(solution)/shard_map/ppermute | solution.py:57
  121.0 11.7 %collective-permute-start.5 = (bf16[4,20,8,128]{3,2,0,1:T(8,128)(2,1)S(1)}, bf16[4,20,8,128]{3,2,0,1:T(8,128)(2,1)S(1)}, u32[]{:S(2)}, u32[]{:S(2)}) collective-permute-start(bf16[4,20,8,128]{3,2,0,1:T(8,128)(2,1)S(1)} %maximum_select_fusion.3), channel_id=1, source_target_pairs={{0,8},{2,10},{4,12},{6,14},{8,0},{10,2},{12,4},{14,6},{1,9},{3,11}... | collective-permute-start | bytes 491528 | tf_op jit(solution)/shard_map/ppermute | solution.py:57
  123.1 11.4 %collective-permute-start.18 = (bf16[4,20,8,128]{3,2,0,1:T(8,128)(2,1)S(1)}, bf16[4,20,8,128]{3,2,0,1:T(8,128)(2,1)S(1)}, u32[]{:S(2)}, u32[]{:S(2)}) collective-permute-start(bf16[4,20,8,128]{3,2,0,1:T(8,128)(2,1)S(1)} %maximum_select_fusion.4), channel_id=1, source_target_pairs={{0,8},{2,10},{4,12},{6,14},{8,0},{10,2},{12,4},{14,6},{1,9},{3,11}... | collective-permute-start | bytes 491528 | tf_op jit(solution)/shard_map/ppermute | solution.py:57
  132.8 2.8 %copy-start.16 = (bf16[256,2560]{0,1:T(8,128)(2,1)S(1)}, bf16[256,2560]{0,1:T(8,128)(2,1)}, u32[]{:S(2)}) copy-start(bf16[256,2560]{0,1:T(8,128)(2,1)} %copy.72) | copy-start | bytes 3932164
  132.8 2.8 %copy-start.27 = (f32[256,40]{0,1:T(8,128)S(1)}, f32[256,40]{0,1:T(8,128)}, u32[]{:S(2)}) copy-start(f32[256,40]{0,1:T(8,128)} %copy-done.26) | copy-start | bytes 122884
  132.8 2.8 %collective-permute-start.6 = (bf16[20,64,128]{2,1,0:T(8,128)(2,1)S(1)}, bf16[20,64,128]{2,1,0:T(8,128)(2,1)S(1)}, u32[]{:S(2)}, u32[]{:S(2)}) collective-permute-start(bf16[20,64,128]{2,1,0:T(8,128)(2,1)S(1)} %fusion.25), channel_id=1, source_target_pairs={{0,1},{1,0},{2,3},{3,2},{4,5},{5,4},{6,7},{7,6},{8,9},{9,8},{10,11... | collective-permute-start | bytes 983048 | tf_op jit(solution)/shard_map/ppermute | solution.py:78
  135.5 1.8 %copy-start.23 = (f32[256,128]{0,1:T(8,128)S(1)}, f32[256,128]{0,1:T(8,128)}, u32[]{:S(2)}) copy-start(f32[256,128]{0,1:T(8,128)} %copy.70) | copy-start | bytes 393220
  135.5 3.9 %collective-permute-start.19 = (f32[2,256,128]{2,1,0:T(8,128)S(1)}, f32[2,256,128]{2,1,0:T(8,128)S(1)}, u32[]{:S(2)}, u32[]{:S(2)}) collective-permute-start(f32[2,256,128]{2,1,0:T(8,128)S(1)} %select_bitcast_fusion), channel_id=1, source_target_pairs={{0,1},{1,0},{2,3},{3,2},{4,5},{5,4},{6,7},{7,6},{8,9},{9,8},{10,11... | collective-permute-start | bytes 786440 | tf_op jit(solution)/shard_map/ppermute | solution.py:78

commit v6 on v5

--- a/solution.py
+++ b/solution.py
@@ -102,7 +102,7 @@
     mine_first = seq_at == 0
     own_half = jnp.where(mine_first, state_halves[0], state_halves[1])
     give_half = jnp.where(mine_first, state_halves[1], state_halves[0])
-    init_half = cand_sum_bf16(own_half + other_core(give_half))
+    init_local = own_half + other_core(give_half)
 
     position = jnp.arange(cand_len, dtype=jnp.int32)
     valid_rows = position[None, :] < lengths[:, None] * BLOCK
@@ -117,7 +117,8 @@
     x_high, x_low = split_bf16(xc_heads.astype(jnp.float32) * inverse[:, :, :, None])
 
     dstate = jnp.einsum("cthp,ctn->hpn", decayed_g, c_cand, preferred_element_type=jnp.float32)
-    grad_half = cand_sum_bf16(dstate)
+    both = cand_sum_bf16(jnp.concatenate([init_local, dstate], axis=0))
+    init_half, grad_half = both[:half_heads], both[half_heads:]
     grad_other = other_core(grad_half)
     grad_state = jnp.where(
         mine_first,
@@ -158,13 +159,13 @@
     )
     dc_total = dc_part + dc_state.reshape(cand_dev, cand_len, nstate)
     def token_half_sum(part):
-        halves = part.reshape(cand_dev, 2, cand_len // 2, nstate)
+        halves = part.reshape(cand_dev, 2, cand_len // 2, part.shape[2])
         own = jnp.where(mine_first, halves[:, 0], halves[:, 1])
         give = jnp.where(mine_first, halves[:, 1], halves[:, 0])
         return own + other_core(give)
 
-    db_cand = token_half_sum(db_part)
-    dc_cand = token_half_sum(dc_total)
+    db_dc = token_half_sum(jnp.concatenate([db_part, dc_total], axis=2))
+    db_cand, dc_cand = db_dc[:, :, :nstate], db_dc[:, :, nstate:]
 
     dx_prefix = jnp.einsum(
         "jhn,hpn->jhp", weighted_b, grad_state, preferred_element_type=jnp.float32

time: 141 us -> 134 us (0.950)
  waiting for transfers between devices: 31.4 us -> 55 us
  starting transfers between devices: 25.8 us -> 13.6 us
  other arithmetic: 30.3 us -> 19.1 us
  matrix products: 26.3 us -> 20.1 us
    ppermute x6 -> x3, waiting for transfers between devices: 14.3 us -> 33.1 us  [halving_scatter(): lax.ppermute(give, axis, [(at, at ^ step) for at in range(count)])]
    ppermute x6 -> x3, starting transfers between devices: 13.7 us -> 2.3 us  [halving_scatter(): lax.ppermute(give, axis, [(at, at ^ step) for at in range(count)])]
    ppermute x4, waiting for transfers between devices: 5.08 us -> 13.2 us  [suffix_sum(): value = value + lax.ppermute(value, axis, back)]
    ppermute x6 -> x3, waiting for transfers between devices: 12 us -> 8.75 us  [doubling_gather(): other = lax.ppermute(value, axis, [(at, at ^ step) for at in range(count)])]
    convert_element_type x1 -> x0, other arithmetic: 2.93 us -> none  [split_bf16(): return (high.astype(jnp.bfloat16), low)]
    dot_general x3, matrix products: 7.58 us -> 4.9 us  [pair(): jnp.einsum('ctk,csk->cts', left.reshape(flat), right.reshape(flat), prefe...]
    slice x1 -> x4, local copies, waits for them, and re-layouts: 0.18 us -> 1.84 us  [the longest x1 0.82 us: shards(): db_cand, dc_cand = (db_dc[:, :, :nstate], db_dc[:, :, nstate:])]
    dot_general x1, matrix products: 2.55 us -> 1.03 us  [shards(): jnp.einsum('jhp,jhn->hpn', x_heads, weighted_b, preferred_element_type=jn...]
  transfers between devices with their start and end apart: 20 -> 13, of which waited for: 11 -> 8; matrix products, arithmetic and copies ran while one was open for 55% -> 38% of each run, Pallas kernels for 0% -> 0%
where the time goes in v6:
time: 134 us; the launch traced here: 133 us
  waiting for transfers between devices  55 us (41%)
  local copies, waits for them, and re-layouts  24.4 us (18%)
  matrix products  20.1 us (15%)
  other arithmetic  19.1 us (14%)
  starting transfers between devices  13.6 us (10%)
    ppermute x3, waiting for transfers between devices, halving_scatter(): lax.ppermute(give, axis, [(at, at ^ step) for at in range(count)])  33.1 us
    unnamed x50, local copies, waits for them, and re-layouts  19.1 us
    ppermute x4, waiting for transfers between devices, suffix_sum(): value = value + lax.ppermute(value, axis, back)  13.2 us
    ppermute x3, waiting for transfers between devices, doubling_gather(): other = lax.ppermute(value, axis, [(at, at ^ step) for at in range(count)])  8.75 us
    dot_general x1, matrix products, shards(): jnp.einsum('chts,cthp->cshp', kernel, g_heads, preferred_element_type=jnp...  6.46 us
    convert_element_type x2, other arithmetic, split_bf16(): low = (value - high).astype(jnp.bfloat16)  5.81 us
    ppermute x3, starting transfers between devices, doubling_gather(): other = lax.ppermute(value, axis, [(at, at ^ step) for at in range(count)])  5.56 us
    ppermute x4, starting transfers between devices, suffix_sum(): value = value + lax.ppermute(value, axis, back)  5.14 us
  transfers between devices with their start and end apart: 13, of which 8 were waited for; matrix products, arithmetic and copies ran while one was open for 38% of the time, Pallas kernels for 0%

profile of v6, /device:TPU:0, one launch (start us, length us, event | category | flops | bytes accessed | tf_op | source)
XLA Modules:
  0.0 133.4 jit_solution(16366812679647138642)
XLA Ops:
  0.6 0.9 fusion.27
  1.6 1.3 collective-permute-start
  2.9 1.0 log-plus-one_bitcast_fusion
  4.0 0.6 reduce-window.14
  4.6 2.3 %reduce-window.16 = f32[2,20,4,128]{3,1,2,0:T(8,128)S(1)} reduce-window(f32[2,20,4,128]{3,1,2,0:T(8,128)S(1)} %copy.69, f32[]{:T(128)} %constant.84.clone.1), window={size=1x1x1x128 pad=0_0x0_0x0_0x127_0}, to_apply=%region_3.4 | reduce-window | flops 2600960 | bytes 163844 | tf_op jit(solution)/shard_map/reduce-window.2
  6.9 0.2 slice_reduce_fusion
  7.3 0.2 slice_reduce_fusion.1
  7.5 1.3 collective-permute-start.1
  8.8 5.7 %collective-permute-done.1 = f32[40]{0:T(128)S(1)} collective-permute-done((f32[40]{0:T(128)S(1)}, f32[40]{0:T(128)S(1)}, u32[]{:S(2)}, u32[]{:S(2)}) %collective-permute-start.1) | collective-permute-done | bytes 192 | tf_op jit(solution)/shard_map/ppermute | solution.py:30
  14.5 1.3 collective-permute-start.2
  15.8 0.9 copy.65
  16.7 4.1 %collective-permute-done.2 = f32[40]{0:T(128)S(1)} collective-permute-done((f32[40]{0:T(128)S(1)}, f32[40]{0:T(128)S(1)}, u32[]{:S(2)}, u32[]{:S(2)}) %collective-permute-start.2) | collective-permute-done | bytes 192 | tf_op jit(solution)/shard_map/ppermute | solution.py:30
  20.8 1.3 collective-permute-start.3
  22.1 1.6 %copy.66 = bf16[256,2560]{0,1:T(8,128)(2,1)S(1)} copy(bf16[256,2560]{1,0:T(8,128)(2,1)} %param.9) | data formatting | bytes 2621440 | tf_op args[0]
  23.7 3.4 %collective-permute-done.3 = f32[40]{0:T(128)S(1)} collective-permute-done((f32[40]{0:T(128)S(1)}, f32[40]{0:T(128)S(1)}, u32[]{:S(2)}, u32[]{:S(2)}) %collective-permute-start.3) | collective-permute-done | bytes 192 | tf_op jit(solution)/shard_map/ppermute | solution.py:30
  27.2 1.0 fusion.19
  28.3 1.0 copy-done.7
  29.3 0.9 slice_select_fusion.1
  30.5 3.0 %copy.68 = bf16[2,512,1280]{1,2,0:T(8,128)(2,1)S(1)} copy(bf16[2,512,1280]{2,1,0:T(8,128)(2,1)} %param.17) | data formatting | bytes 5242880 | tf_op args[8]
  33.6 2.7 %fusion.6 = (bf16[2,512,1280]{1,2,0:T(8,128)(2,1)}, bf16[2,512,1280]{1,2,0:T(8,128)(2,1)S(1)}) fusion(f32[2,512,20]{1,2,0:T(8,128)S(1)} %copy.71, bf16[2,512,1280]{1,2,0:T(8,128)(2,1)S(1)} %copy.68, pred[2,512]{1,0:T(4,128)(4,1)S(1)} %iota_compare_fusion.1), kind=kLoop, calls=%fused_computation.11 | loop fusion | flops 7864320 | bytes 7947264 | tf_op jit(solution)/shard_map/convert_element_type | solution.py:11
  36.3 0.9 fusion.20
  37.1 0.6 copy-done.1
  37.8 0.8 copy-done.8
  38.5 1.3 select_add_fusion.1
  39.8 0.1 maximum_bitcast_fusion
  39.9 0.1 slice_select_fusion
  40.0 0.2 collective-permute-start.5
  40.2 0.7 copy.73
  41.1 0.4 fusion.34
  41.6 30.7 %collective-permute-done.5 = f32[4,40,8,128]{3,2,0,1:T(8,128)} collective-permute-done((f32[4,40,8,128]{3,2,0,1:T(8,128)S(1)}, f32[4,40,8,128]{3,2,0,1:T(8,128)}, u32[]{:S(2)}, u32[]{:S(2)}) %collective-permute-start.5) | collective-permute-done | bytes 655392 | tf_op jit(solution)/shard_map/ppermute | solution.py:46
  72.2 1.3 select_add_fusion
  73.5 0.8 slice_select_fusion.2
  74.3 6.5 %fusion.17 = bf16[2,20,64,512]{3,2,1,0:T(8,128)(2,1)} fusion(bf16[2,512,20,64]{1,3,2,0:T(8,128)(2,1)S(1)} %bitcast.97, f32[2,20,512]{2,1,0:T(8,128)S(1)} %copy.75, f32[2,20,512]{2,1,0:T(8,128)S(1)} %copy-done.17, f32[2,512,512]{2,1,0:T(8,128)S(1)} %fusion.34, pred[512,512]{1,0:T(8,128)(4,1)S(1)} %iota_compare_fusion), kind=kOutput, calls=%fused_computation.29 | convolution fusion | flops 1385431040 | bytes 7766016 | tf_op jit(solution)/shard_map/chts,cthp->cshp/dot_general | solution.py:152
  80.8 0.7 copy.77
  81.4 4.6 %copy.76 = bf16[2,512,1280]{1,2,0:T(8,128)(2,1)} copy(bf16[2,512,1280]{2,1,0:T(8,128)(2,1)} %param.12) | data formatting | bytes 5242880 | tf_op args[3]
  86.0 3.1 %fusion.7 = (bf16[2,512,1280]{1,2,0:T(8,128)(2,1)S(1)}, bf16[2,512,1280]{1,2,0:T(8,128)(2,1)S(1)}, bf16[2,512,1280]{1,2,0:T(8,128)(2,1)S(1)}) fusion(bf16[2,512,1280]{1,2,0:T(8,128)(2,1)} %copy.76, f32[2,512,20]{1,2,0:T(8,128)} %copy.77, f32[2,512,20]{1,2,0:T(8,128)} %copy-done.15, bf16[2,512,1280]{1,2,0:T(8,128)(2,1)S(1)} %copy-done.3), kind=kLoop, calls=%fused_computation.12 | loop fusion | flops 13107200 | bytes 13271040 | tf_op jit(solution)/shard_map/convert_element_type | solution.py:11
  89.2 1.3 select_add_fusion.2
  90.5 2.1 %collective-permute-start.7 = (f32[1,40,8,128]{3,2,0,1:T(8,128)S(1)}, f32[1,40,8,128]{3,2,0,1:T(8,128)S(1)}, u32[]{:S(2)}, u32[]{:S(2)}) collective-permute-start(f32[1,40,8,128]{3,2,0,1:T(8,128)S(1)} %slice_select_fusion.3), channel_id=1, source_target_pairs={{0,2},{2,0},{4,6},{6,4},{8,10},{10,8},{12,14},{14,12},{1,3},{3,1},... | collective-permute-start | bytes 491528 | tf_op jit(solution)/shard_map/ppermute | solution.py:46
  92.6 1.6 %fusion.36 = f32[2,512,512]{2,1,0:T(8,128)S(1)} fusion(bf16[2,512,1280]{1,2,0:T(8,128)(2,1)S(1)} %get-tuple-element.34, bf16[2,512,1280]{1,2,0:T(8,128)(2,1)S(1)} %get-tuple-element.22), kind=kOutput, calls=%fused_computation.79 | convolution fusion | flops 1342177280 | bytes 7340032 | tf_op jit(solution)/shard_map/ctk,csk->cts/dot_general | solution.py:133
  94.2 2.5 %collective-permute-done.7 = f32[1,40,8,128]{3,2,0,1:T(8,128)S(1)} collective-permute-done((f32[1,40,8,128]{3,2,0,1:T(8,128)S(1)}, f32[1,40,8,128]{3,2,0,1:T(8,128)S(1)}, u32[]{:S(2)}, u32[]{:S(2)}) %collective-permute-start.7) | collective-permute-done | bytes 163872 | tf_op jit(solution)/shard_map/ppermute | solution.py:46
  96.6 1.8 %collective-permute-start.8 = (bf16[1,40,8,128]{3,2,0,1:T(8,128)(2,1)S(1)}, bf16[1,40,8,128]{3,2,0,1:T(8,128)(2,1)S(1)}, u32[]{:S(2)}, u32[]{:S(2)}) collective-permute-start(bf16[1,40,8,128]{3,2,0,1:T(8,128)(2,1)S(1)} %add_convert_fusion), channel_id=1, source_target_pairs={{0,2},{2,0},{4,6},{6,4},{8,10},{10,8},{12,14},{14,12},{1,3},{3,1},... | collective-permute-start | bytes 245768 | tf_op jit(solution)/shard_map/ppermute | solution.py:57
  98.5 1.6 %fusion.35 = f32[2,512,512]{2,1,0:T(8,128)S(1)} fusion(bf16[2,512,1280]{1,2,0:T(8,128)(2,1)S(1)} %get-tuple-element.34, bf16[2,512,1280]{1,2,0:T(8,128)(2,1)S(1)} %get-tuple-element.23), kind=kOutput, calls=%fused_computation.78 | convolution fusion | flops 1342177280 | bytes 7340032 | tf_op jit(solution)/shard_map/ctk,csk->cts/dot_general | solution.py:133
  100.0 1.1 collective-permute-done.8
  101.2 1.8 %collective-permute-start.9 = (bf16[2,40,8,128]{3,2,0,1:T(8,128)(2,1)S(1)}, bf16[2,40,8,128]{3,2,0,1:T(8,128)(2,1)S(1)}, u32[]{:S(2)}, u32[]{:S(2)}) collective-permute-start(bf16[2,40,8,128]{3,2,0,1:T(8,128)(2,1)S(1)} %maximum_select_fusion.3), channel_id=1, source_target_pairs={{0,4},{2,6},{4,0},{6,2},{8,12},{10,14},{12,8},{14,10},{1,5},{3,7},... | collective-permute-start | bytes 491528 | tf_op jit(solution)/shard_map/ppermute | solution.py:57
  103.0 1.8 %add_select_fusion = f32[2,512,512]{2,1,0:T(8,128)S(1)} fusion(f32[2,512,512]{2,1,0:T(8,128)S(1)} %fusion.35, f32[2,512,512]{2,1,0:T(8,128)S(1)} %fusion.36, bf16[2,512,1280]{1,2,0:T(8,128)(2,1)S(1)} %copy-done.6, bf16[2,512,1280]{1,2,0:T(8,128)(2,1)S(1)} %get-tuple-element.23, pred[512,512]{1,0:T(8,128)(4,1)S(1)} %copy-done.10), kind=kOutput, calls=%fused_computation.28 | convolution fusion | flops 1343750144 | bytes 11796480 | tf_op jit(solution)/shard_map/ctk,csk->cts/dot_general | solution.py:133
  104.8 1.8 %collective-permute-done.9 = bf16[2,40,8,128]{3,2,0,1:T(8,128)(2,1)S(1)} collective-permute-done((bf16[2,40,8,128]{3,2,0,1:T(8,128)(2,1)S(1)}, bf16[2,40,8,128]{3,2,0,1:T(8,128)(2,1)S(1)}, u32[]{:S(2)}, u32[]{:S(2)}) %collective-permute-start.9) | collective-permute-done | bytes 163872 | tf_op jit(solution)/shard_map/ppermute | solution.py:57
  106.6 2.0 %collective-permute-start.10 = (bf16[4,40,8,128]{3,2,0,1:T(8,128)(2,1)S(1)}, bf16[4,40,8,128]{3,2,0,1:T(8,128)(2,1)S(1)}, u32[]{:S(2)}, u32[]{:S(2)}) collective-permute-start(bf16[4,40,8,128]{3,2,0,1:T(8,128)(2,1)S(1)} %maximum_select_fusion.2), channel_id=1, source_target_pairs={{0,8},{2,10},{4,12},{6,14},{8,0},{10,2},{12,4},{14,6},{1,9},{3,11}... | collective-permute-start | bytes 983048 | tf_op jit(solution)/shard_map/ppermute | solution.py:57
  108.6 1.3 fusion.38
  109.9 4.4 %copy.92 = bf16[2,512,1280]{2,1,0:T(8,128)(2,1)} copy(bf16[2,512,1280]{1,2,0:T(8,128)(2,1)} %bitcast.98) | data formatting | bytes 5242880
  114.3 0.9 fusion.37
  115.2 5.8 %collective-permute-done.10 = bf16[4,40,8,128]{3,2,0,1:T(8,128)(2,1)S(1)} collective-permute-done((bf16[4,40,8,128]{3,2,0,1:T(8,128)(2,1)S(1)}, bf16[4,40,8,128]{3,2,0,1:T(8,128)(2,1)S(1)}, u32[]{:S(2)}, u32[]{:S(2)}) %collective-permute-start.10) | collective-permute-done | bytes 327712 | tf_op jit(solution)/shard_map/ppermute | solution.py:57
  121.2 0.6 convolution_add_fusion
  121.9 0.7 reshape.168
  122.6 0.8 fusion.31
  123.4 0.3 copy.107
  123.8 0.3 copy.108
  124.1 0.9 select_bitcast_fusion
  125.0 0.5 collective-permute-start.12
  125.5 2.0 %fusion.8 = f32[256,128]{0,1:T(8,128)S(1)} fusion(f32[256,40]{0,1:T(8,128)S(1)} %copy-done.19, bf16[256,40,64]{0,2,1:T(8,128)(2,1)S(1)} %bitcast.100, bf16[20,64,128]{2,1,0:T(8,128)(2,1)} %collective-permute-done.11, bf16[20,64,128]{2,1,0:T(8,128)(2,1)S(1)} %get-tuple-element.27, pred[]{:T(512)S(6)} %eq.22), kind=kOutput, calls=%fused_computation.16 | convolution fusion | flops 171343872 | bytes 2138113 | tf_op jit(solution)/shard_map/jhp,hpn->jhn/dot_general | solution.py:174
  127.5 0.8 copy.91
  128.2 1.6 %fusion.18 = bf16[40,64,256]{2,1,0:T(8,128)(2,1)S(1)} fusion(f32[256,128]{0,1:T(8,128)} %copy-done.16, f32[256,40]{0,1:T(8,128)S(1)} %copy-done.19, bf16[20,64,128]{2,1,0:T(8,128)(2,1)} %collective-permute-done.11, bf16[20,64,128]{2,1,0:T(8,128)(2,1)S(1)} %get-tuple-element.27, pred[]{:T(512)S(6)} %eq.22), kind=kOutput, calls=%fused_computation.30 | convolution fusion | flops 172032000 | bytes 2138113 | tf_op jit(solution)/shard_map/jhn,hpn->jhp/dot_general | solution.py:170
  129.9 1.6 %copy.90 = bf16[256,2560]{1,0:T(8,128)(2,1)} copy(bf16[256,2560]{0,1:T(8,128)(2,1)S(1)} %bitcast.101) | data formatting | bytes 2621440
  131.4 1.1 bitcast_add_fusion
  132.6 0.8 fusion.33
  (76 shorter events, 1.3 us)
Async XLA Ops:
  0.6 35.6 %copy-start = (bf16[2,512,128]{2,1,0:T(8,128)(2,1)S(1)}, bf16[2,512,128]{2,1,0:T(8,128)(2,1)}, u32[]{:S(2)}) copy-start(bf16[2,512,128]{2,1,0:T(8,128)(2,1)} %param.14) | copy-start | bytes 786436
  1.6 5.8 %collective-permute-start = (f32[40]{0:T(128)S(1)}, f32[40]{0:T(128)S(1)}, u32[]{:S(2)}, u32[]{:S(2)}) collective-permute-start(f32[40]{0:T(128)S(1)} %get-tuple-element.32), channel_id=1, source_target_pairs={{1,0},{2,1},{3,2},{4,3},{5,4},{6,5},{7,6},{8,7},{9,8},{10,9},{11,1... | collective-permute-start | bytes 488 | tf_op jit(solution)/shard_map/ppermute | solution.py:30
  7.5 7.0 %collective-permute-start.1 = (f32[40]{0:T(128)S(1)}, f32[40]{0:T(128)S(1)}, u32[]{:S(2)}, u32[]{:S(2)}) collective-permute-start(f32[40]{0:T(128)S(1)} %add.64), channel_id=1, source_target_pairs={{2,0},{3,1},{4,2},{5,3},{6,4},{7,5},{8,6},{9,7},{10,8},{11,9},{12,... | collective-permute-start | bytes 488 | tf_op jit(solution)/shard_map/ppermute | solution.py:30
  14.5 6.3 %collective-permute-start.2 = (f32[40]{0:T(128)S(1)}, f32[40]{0:T(128)S(1)}, u32[]{:S(2)}, u32[]{:S(2)}) collective-permute-start(f32[40]{0:T(128)S(1)} %add.65), channel_id=1, source_target_pairs={{4,0},{5,1},{6,2},{7,3},{8,4},{9,5},{10,6},{11,7},{12,8},{13,9},{1... | collective-permute-start | bytes 488 | tf_op jit(solution)/shard_map/ppermute | solution.py:30
  16.7 11.6 %copy-start.16 = (f32[256,128]{0,1:T(8,128)}, f32[256,128]{0,1:T(8,128)S(1)}, u32[]{:S(2)}) copy-start(f32[256,128]{0,1:T(8,128)S(1)} %copy.65) | copy-start | bytes 393220
  20.8 6.3 %collective-permute-start.3 = (f32[40]{0:T(128)S(1)}, f32[40]{0:T(128)S(1)}, u32[]{:S(2)}, u32[]{:S(2)}) collective-permute-start(f32[40]{0:T(128)S(1)} %add.66), channel_id=1, source_target_pairs={{8,0},{9,1},{10,2},{11,3},{12,4},{13,5},{14,6},{15,7},{24,16},{25,... | collective-permute-start | bytes 488 | tf_op jit(solution)/shard_map/ppermute | solution.py:30
  23.7 6.6 %copy-start.11 = (bf16[256,2560]{0,1:T(8,128)(2,1)}, bf16[256,2560]{0,1:T(8,128)(2,1)S(1)}, u32[]{:S(2)}) copy-start(bf16[256,2560]{0,1:T(8,128)(2,1)S(1)} %copy.66) | copy-start | bytes 3932164
  27.2 3.1 %copy-start.18 = (f32[256,40]{0,1:T(8,128)}, f32[256,40]{0,1:T(8,128)S(1)}, u32[]{:S(2)}) copy-start(f32[256,40]{0,1:T(8,128)S(1)} %fusion.25) | copy-start | bytes 122884
  27.2 3.0 %copy-start.20 = (s32[2]{0:T(128)S(1)}, s32[2]{0:T(128)}, u32[]{:S(2)}) copy-start(s32[2]{0:T(128)} %param.16) | copy-start | bytes 28
  28.3 1.1 copy-start.7
  30.3 7.5 %collective-permute-start.4 = (f32[20,64,128]{2,1,0:T(8,128)}, f32[20,64,128]{2,1,0:T(8,128)}, u32[]{:S(2)}, u32[]{:S(2)}) collective-permute-start(f32[20,64,128]{2,1,0:T(8,128)} %slice_select_fusion.1), channel_id=1, source_target_pairs={{0,1},{1,0},{2,3},{3,2},{4,5},{5,4},{6,7},{7,6},{8,9},{9,8},{10,11... | collective-permute-start | bytes 1966088 | tf_op jit(solution)/shard_map/ppermute | solution.py:78
  30.5 5.8 %copy-start.15 = (f32[2,512,20]{1,2,0:T(8,128)}, f32[2,512,20]{1,2,0:T(8,128)S(1)}, u32[]{:S(2)}) copy-start(f32[2,512,20]{1,2,0:T(8,128)S(1)} %copy.71) | copy-start | bytes 245764
  36.3 1.5 %copy-start.1 = (bf16[2,512,1280]{1,2,0:T(8,128)(2,1)}, bf16[2,512,1280]{1,2,0:T(8,128)(2,1)S(1)}, u32[]{:S(2)}) copy-start(bf16[2,512,1280]{1,2,0:T(8,128)(2,1)S(1)} %get-tuple-element.21) | copy-start | bytes 7864324
  36.3 2.3 %copy-start.8 = (f32[40,64,128]{2,1,0:T(8,128)S(1)}, f32[40,64,128]{2,1,0:T(8,128)}, u32[]{:S(2)}) copy-start(f32[40,64,128]{2,1,0:T(8,128)} %copy-done.7) | copy-start | bytes 3932164
  39.8 1.3 copy-start.13
  40.0 32.2 %collective-permute-start.5 = (f32[4,40,8,128]{3,2,0,1:T(8,128)S(1)}, f32[4,40,8,128]{3,2,0,1:T(8,128)}, u32[]{:S(2)}, u32[]{:S(2)}) collective-permute-start(f32[4,40,8,128]{3,2,0,1:T(8,128)S(1)} %slice_select_fusion), channel_id=1, source_target_pairs={{0,8},{2,10},{4,12},{6,14},{8,0},{10,2},{12,4},{14,6},{1,9},{3,11}... | collective-permute-start | bytes 1966088 | tf_op jit(solution)/shard_map/ppermute | solution.py:46
  41.1 33.2 %copy-start.9 = (pred[512,512]{1,0:T(8,128)(4,1)}, pred[512,512]{1,0:T(8,128)(4,1)S(1)}, u32[]{:S(2)}) copy-start(pred[512,512]{1,0:T(8,128)(4,1)S(1)} %iota_compare_fusion) | copy-start | bytes 786436
  41.1 33.2 %copy-start.2 = (bf16[2,512,1280]{1,2,0:T(8,128)(2,1)S(1)}, bf16[2,512,1280]{1,2,0:T(8,128)(2,1)}, u32[]{:S(2)}) copy-start(bf16[2,512,1280]{1,2,0:T(8,128)(2,1)} %copy-done.1) | copy-start | bytes 7864324
  41.1 33.2 %copy-start.17 = (f32[2,20,512]{2,1,0:T(8,128)S(1)}, f32[2,20,512]{2,1,0:T(8,128)}, u32[]{:S(2)}) copy-start(f32[2,20,512]{2,1,0:T(8,128)} %copy.73) | copy-start | bytes 245764
  74.3 14.9 %collective-permute-start.6 = (f32[2,40,8,128]{3,2,0,1:T(8,128)}, f32[2,40,8,128]{3,2,0,1:T(8,128)}, u32[]{:S(2)}, u32[]{:S(2)}) collective-permute-start(f32[2,40,8,128]{3,2,0,1:T(8,128)} %slice_select_fusion.2), channel_id=1, source_target_pairs={{0,4},{2,6},{4,0},{6,2},{8,12},{10,14},{12,8},{14,10},{1,5},{3,7},... | collective-permute-start | bytes 983048 | tf_op jit(solution)/shard_map/ppermute | solution.py:46
  81.4 4.6 %copy-start.3 = (bf16[2,512,1280]{1,2,0:T(8,128)(2,1)S(1)}, bf16[2,512,1280]{1,2,0:T(8,128)(2,1)}, u32[]{:S(2)}) copy-start(bf16[2,512,1280]{1,2,0:T(8,128)(2,1)} %copy-done.1) | copy-start | bytes 7864324
  89.1 9.3 %copy-start.4 = (bf16[2,512,1280]{1,2,0:T(8,128)(2,1)}, bf16[2,512,1280]{1,2,0:T(8,128)(2,1)S(1)}, u32[]{:S(2)}) copy-start(bf16[2,512,1280]{1,2,0:T(8,128)(2,1)S(1)} %get-tuple-element.34) | copy-start | bytes 7864324
  90.5 6.1 %collective-permute-start.7 = (f32[1,40,8,128]{3,2,0,1:T(8,128)S(1)}, f32[1,40,8,128]{3,2,0,1:T(8,128)S(1)}, u32[]{:S(2)}, u32[]{:S(2)}) collective-permute-start(f32[1,40,8,128]{3,2,0,1:T(8,128)S(1)} %slice_select_fusion.3), channel_id=1, source_target_pairs={{0,2},{2,0},{4,6},{6,4},{8,10},{10,8},{12,14},{14,12},{1,3},{3,1},... | collective-permute-start | bytes 491528 | tf_op jit(solution)/shard_map/ppermute | solution.py:46
  96.6 4.5 %collective-permute-start.8 = (bf16[1,40,8,128]{3,2,0,1:T(8,128)(2,1)S(1)}, bf16[1,40,8,128]{3,2,0,1:T(8,128)(2,1)S(1)}, u32[]{:S(2)}, u32[]{:S(2)}) collective-permute-start(bf16[1,40,8,128]{3,2,0,1:T(8,128)(2,1)S(1)} %add_convert_fusion), channel_id=1, source_target_pairs={{0,2},{2,0},{4,6},{6,4},{8,10},{10,8},{12,14},{14,12},{1,3},{3,1},... | collective-permute-start | bytes 245768 | tf_op jit(solution)/shard_map/ppermute | solution.py:57
  98.5 4.6 %copy-start.6 = (bf16[2,512,1280]{1,2,0:T(8,128)(2,1)S(1)}, bf16[2,512,1280]{1,2,0:T(8,128)(2,1)}, u32[]{:S(2)}) copy-start(bf16[2,512,1280]{1,2,0:T(8,128)(2,1)} %get-tuple-element.20) | copy-start | bytes 7864324
  98.5 4.6 %copy-start.10 = (pred[512,512]{1,0:T(8,128)(4,1)S(1)}, pred[512,512]{1,0:T(8,128)(4,1)}, u32[]{:S(2)}) copy-start(pred[512,512]{1,0:T(8,128)(4,1)} %copy-done.9) | copy-start | bytes 786436
  101.2 5.4 %collective-permute-start.9 = (bf16[2,40,8,128]{3,2,0,1:T(8,128)(2,1)S(1)}, bf16[2,40,8,128]{3,2,0,1:T(8,128)(2,1)S(1)}, u32[]{:S(2)}, u32[]{:S(2)}) collective-permute-start(bf16[2,40,8,128]{3,2,0,1:T(8,128)(2,1)S(1)} %maximum_select_fusion.3), channel_id=1, source_target_pairs={{0,4},{2,6},{4,0},{6,2},{8,12},{10,14},{12,8},{14,10},{1,5},{3,7},... | collective-permute-start | bytes 491528 | tf_op jit(solution)/shard_map/ppermute | solution.py:57
  103.0 5.6 %copy-start.14 = (bf16[2,512,128]{2,1,0:T(8,128)(2,1)S(1)}, bf16[2,512,128]{2,1,0:T(8,128)(2,1)}, u32[]{:S(2)}) copy-start(bf16[2,512,128]{2,1,0:T(8,128)(2,1)} %param.13) | copy-start | bytes 786436
  106.6 14.4 %collective-permute-start.10 = (bf16[4,40,8,128]{3,2,0,1:T(8,128)(2,1)S(1)}, bf16[4,40,8,128]{3,2,0,1:T(8,128)(2,1)S(1)}, u32[]{:S(2)}, u32[]{:S(2)}) collective-permute-start(bf16[4,40,8,128]{3,2,0,1:T(8,128)(2,1)S(1)} %maximum_select_fusion.2), channel_id=1, source_target_pairs={{0,8},{2,10},{4,12},{6,14},{8,0},{10,2},{12,4},{14,6},{1,9},{3,11}... | collective-permute-start | bytes 983048 | tf_op jit(solution)/shard_map/ppermute | solution.py:57
  114.3 6.9 %copy-start.5 = (bf16[2,512,1280]{1,2,0:T(8,128)(2,1)S(1)}, bf16[2,512,1280]{1,2,0:T(8,128)(2,1)}, u32[]{:S(2)}) copy-start(bf16[2,512,1280]{1,2,0:T(8,128)(2,1)} %copy-done.4) | copy-start | bytes 7864324
  121.1 4.3 %collective-permute-start.11 = (bf16[20,64,128]{2,1,0:T(8,128)(2,1)S(1)}, bf16[20,64,128]{2,1,0:T(8,128)(2,1)}, u32[]{:S(2)}, u32[]{:S(2)}) collective-permute-start(bf16[20,64,128]{2,1,0:T(8,128)(2,1)S(1)} %get-tuple-element.27), channel_id=1, source_target_pairs={{0,1},{1,0},{2,3},{3,2},{4,5},{5,4},{6,7},{7,6},{8,9},{9,8},{10,11... | collective-permute-start | bytes 983048 | tf_op jit(solution)/shard_map/ppermute | solution.py:78
  122.6 2.9 %copy-start.19 = (f32[256,40]{0,1:T(8,128)S(1)}, f32[256,40]{0,1:T(8,128)}, u32[]{:S(2)}) copy-start(f32[256,40]{0,1:T(8,128)} %copy-done.18) | copy-start | bytes 122884
  123.8 1.7 %copy-start.12 = (bf16[256,2560]{0,1:T(8,128)(2,1)S(1)}, bf16[256,2560]{0,1:T(8,128)(2,1)}, u32[]{:S(2)}) copy-start(bf16[256,2560]{0,1:T(8,128)(2,1)} %copy-done.11) | copy-start | bytes 3932164
  125.0 6.5 %collective-permute-start.12 = (f32[2,256,256]{2,1,0:T(8,128)}, f32[2,256,256]{2,1,0:T(8,128)}, u32[]{:S(2)}, u32[]{:S(2)}) collective-permute-start(f32[2,256,256]{2,1,0:T(8,128)} %select_bitcast_fusion), channel_id=1, source_target_pairs={{0,1},{1,0},{2,3},{3,2},{4,5},{5,4},{6,7},{7,6},{8,9},{9,8},{10,11... | collective-permute-start | bytes 1572872 | tf_op jit(solution)/shard_map/ppermute | solution.py:78

commit v7 on v6

--- a/solution.py
+++ b/solution.py
@@ -32,35 +32,48 @@
     return value
 
 
+def bit_order(value, count, first_bits):
+    nbits = count.bit_length() - 1
+    rest = value.shape[1:]
+    value = value.reshape((2,) * nbits + rest)
+    axes = [nbits - 1 - bit for bit in first_bits]
+    value = jnp.transpose(value, axes + list(range(nbits, nbits + len(rest))))
+    return value.reshape((count,) + rest)
+
+
 def halving_scatter(blocks, axis):
     count = lax.axis_size(axis)
     me = lax.axis_index(axis)
     rest = blocks.shape[1:]
-    value = blocks
-    step = count // 2
-    while step >= 1:
+    nbits = count.bit_length() - 1
+    value = bit_order(blocks, count, list(range(nbits)))
+    for bit in range(nbits):
+        step = 1 << bit
         value = value.reshape((2, -1) + rest)
         upper = me // step % 2 == 1
         keep = jnp.where(upper, value[1], value[0])
         give = jnp.where(upper, value[0], value[1])
         value = keep + lax.ppermute(give, axis, [(at, at ^ step) for at in range(count)])
-        step //= 2
     return value[0]
 
 
 def doubling_gather(piece, axis):
     count = lax.axis_size(axis)
     me = lax.axis_index(axis)
+    nbits = count.bit_length() - 1
     value = piece[None]
-    step = 1
-    while step < count:
+    for bit in reversed(range(nbits)):
+        step = 1 << bit
         other = lax.ppermute(value, axis, [(at, at ^ step) for at in range(count)])
         upper = me // step % 2 == 1
         value = jnp.where(
             upper, jnp.concatenate([other, value]), jnp.concatenate([value, other])
         )
-        step *= 2
-    return value
+    rest = piece.shape
+    value = value.reshape((2,) * nbits + rest)
+    axes = list(reversed(range(nbits)))
+    value = jnp.transpose(value, axes + list(range(nbits, nbits + len(rest))))
+    return value.reshape((count,) + rest)
 
 
 def cand_sum_bf16(state):

time: 134 us -> 125 us (0.933)
  waiting for transfers between devices: 55 us -> 35.4 us
  local copies, waits for them, and re-layouts: 24.4 us -> 32 us
  matrix products: 20.1 us -> 22.6 us
  other arithmetic: 19.1 us -> 21.4 us
  starting transfers between devices: 13.6 us -> 11.7 us
    ppermute x3, waiting for transfers between devices: 33.1 us -> 15.9 us  [halving_scatter(): lax.ppermute(give, axis, [(at, at ^ step) for at in range(count)])]
    exp x4, local copies, waits for them, and re-layouts: 0.76 us -> 5.56 us  [shards(): inverse = jnp.exp(-level_all)]
    ppermute x3, starting transfers between devices: 5.56 us -> 1.74 us  [doubling_gather(): other = lax.ppermute(value, axis, [(at, at ^ step) for at in range(count)])]
    ppermute x3, starting transfers between devices: 2.3 us -> 4.75 us  [halving_scatter(): lax.ppermute(give, axis, [(at, at ^ step) for at in range(count)])]
    convert_element_type x2, other arithmetic: 5.81 us -> 7.55 us  [split_bf16(): low = (value - high).astype(jnp.bfloat16)]
    ppermute x3, waiting for transfers between devices: 8.75 us -> 7.21 us  [doubling_gather(): other = lax.ppermute(value, axis, [(at, at ^ step) for at in range(count)])]
    dot_general x1, matrix products: 1.03 us -> 2.49 us  [shards(): jnp.einsum('jhp,jhn->hpn', x_heads, weighted_b, preferred_element_type=jn...]
    unnamed x50 -> x44, local copies, waits for them, and re-layouts: 19.1 us -> 19.8 us
  transfers between devices with their start and end apart: 13 -> 13, of which waited for: 8 -> 7; matrix products, arithmetic and copies ran while one was open for 38% -> 49% of each run, Pallas kernels for 0% -> 0%
where the time goes in v7:
time: 125 us; the launch traced here: 124 us
  waiting for transfers between devices  35.4 us (28%)
  local copies, waits for them, and re-layouts  32 us (26%)
  matrix products  22.6 us (18%)
  other arithmetic  21.4 us (17%)
  starting transfers between devices  11.7 us (9%)
  between operations  1.26 us (1%)
    unnamed x44, local copies, waits for them, and re-layouts  19.8 us
    ppermute x3, waiting for transfers between devices, halving_scatter(): lax.ppermute(give, axis, [(at, at ^ step) for at in range(count)])  15.9 us
    ppermute x4, waiting for transfers between devices, suffix_sum(): value = value + lax.ppermute(value, axis, back)  12.3 us
    convert_element_type x2, other arithmetic, split_bf16(): low = (value - high).astype(jnp.bfloat16)  7.55 us
    ppermute x3, waiting for transfers between devices, doubling_gather(): other = lax.ppermute(value, axis, [(at, at ^ step) for at in range(count)])  7.21 us
    dot_general x1, matrix products, shards(): jnp.einsum('chts,cthp->cshp', kernel, g_heads, preferred_element_type=jnp...  6.44 us
    exp x4, local copies, waits for them, and re-layouts, shards(): inverse = jnp.exp(-level_all)  5.56 us
    ppermute x4, starting transfers between devices, suffix_sum(): value = value + lax.ppermute(value, axis, back)  5.14 us
  transfers between devices with their start and end apart: 13, of which 7 were waited for; matrix products, arithmetic and copies ran while one was open for 49% of the time, Pallas kernels for 0%

profile of v7, /device:TPU:0, one launch (start us, length us, event | category | flops | bytes accessed | tf_op | source)
XLA Modules:
  0.0 124.3 jit_solution(16470924657123044465)
XLA Ops:
  0.6 0.9 fusion.26
  1.6 1.3 %collective-permute-start = (f32[40]{0:T(128)S(1)}, f32[40]{0:T(128)S(1)}, u32[]{:S(2)}, u32[]{:S(2)}) collective-permute-start(f32[40]{0:T(128)S(1)} %get-tuple-element.44), channel_id=1, source_target_pairs={{1,0},{2,1},{3,2},{4,3},{5,4},{6,5},{7,6},{8,7},{9,8},{10,9},{11,1... | collective-permute-start | bytes 488 | tf_op jit(solution)/shard_map/ppermute | solution.py:30
  2.9 1.0 log-plus-one_bitcast_fusion
  4.0 0.6 reduce-window.14
  4.6 2.3 %reduce-window.16 = f32[2,20,4,128]{3,1,2,0:T(8,128)S(1)} reduce-window(f32[2,20,4,128]{3,1,2,0:T(8,128)S(1)} %copy.138, f32[]{:T(128)} %constant.84.clone.1), window={size=1x1x1x128 pad=0_0x0_0x0_0x127_0}, to_apply=%region_3.4 | reduce-window | flops 2600960 | bytes 163844 | tf_op jit(solution)/shard_map/reduce-window.2
  6.9 0.2 slice_reduce_fusion
  7.2 0.8 negate_exponential_fusion
  7.9 0.2 slice_reduce_fusion.1
  8.1 1.3 %collective-permute-start.1 = (f32[40]{0:T(128)S(1)}, f32[40]{0:T(128)S(1)}, u32[]{:S(2)}, u32[]{:S(2)}) collective-permute-start(f32[40]{0:T(128)S(1)} %add.64), channel_id=1, source_target_pairs={{2,0},{3,1},{4,2},{5,3},{6,4},{7,5},{8,6},{9,7},{10,8},{11,9},{12,... | collective-permute-start | bytes 488 | tf_op jit(solution)/shard_map/ppermute | solution.py:30
  9.4 5.7 %collective-permute-done.1 = f32[40]{0:T(128)S(1)} collective-permute-done((f32[40]{0:T(128)S(1)}, f32[40]{0:T(128)S(1)}, u32[]{:S(2)}, u32[]{:S(2)}) %collective-permute-start.1) | collective-permute-done | bytes 192 | tf_op jit(solution)/shard_map/ppermute | solution.py:30
  15.1 1.3 %collective-permute-start.2 = (f32[40]{0:T(128)S(1)}, f32[40]{0:T(128)S(1)}, u32[]{:S(2)}, u32[]{:S(2)}) collective-permute-start(f32[40]{0:T(128)S(1)} %add.65), channel_id=1, source_target_pairs={{4,0},{5,1},{6,2},{7,3},{8,4},{9,5},{10,6},{11,7},{12,8},{13,9},{1... | collective-permute-start | bytes 488 | tf_op jit(solution)/shard_map/ppermute | solution.py:30
  16.4 0.9 copy.134
  17.4 4.1 %collective-permute-done.2 = f32[40]{0:T(128)S(1)} collective-permute-done((f32[40]{0:T(128)S(1)}, f32[40]{0:T(128)S(1)}, u32[]{:S(2)}, u32[]{:S(2)}) %collective-permute-start.2) | collective-permute-done | bytes 192 | tf_op jit(solution)/shard_map/ppermute | solution.py:30
  21.4 1.3 %collective-permute-start.3 = (f32[40]{0:T(128)S(1)}, f32[40]{0:T(128)S(1)}, u32[]{:S(2)}, u32[]{:S(2)}) collective-permute-start(f32[40]{0:T(128)S(1)} %add.66), channel_id=1, source_target_pairs={{8,0},{9,1},{10,2},{11,3},{12,4},{13,5},{14,6},{15,7},{24,16},{25,... | collective-permute-start | bytes 488 | tf_op jit(solution)/shard_map/ppermute | solution.py:30
  22.7 2.4 %copy.135 = bf16[256,2560]{0,1:T(8,128)(2,1)} copy(bf16[256,2560]{1,0:T(8,128)(2,1)} %param.9) | data formatting | bytes 2621440 | tf_op args[0]
  25.1 2.6 %collective-permute-done.3 = f32[40]{0:T(128)S(1)} collective-permute-done((f32[40]{0:T(128)S(1)}, f32[40]{0:T(128)S(1)}, u32[]{:S(2)}, u32[]{:S(2)}) %collective-permute-start.3) | collective-permute-done | bytes 192 | tf_op jit(solution)/shard_map/ppermute | solution.py:30
  27.9 2.5 %fusion.19 = f32[40,64,128]{2,1,0:T(8,128)S(1)} fusion(bf16[256,40,64]{0,2,1:T(8,128)(2,1)} %bitcast.113, f32[256,128]{0,1:T(8,128)S(1)} %copy.134, f32[256,40]{0,1:T(8,128)S(1)} %fusion.24), kind=kOutput, calls=%fused_computation.31 | convolution fusion | flops 170393600 | bytes 2793472 | tf_op jit(solution)/shard_map/jhp,jhn->hpn/dot_general | solution.py:112
  30.4 1.1 copy-done.4
  31.5 0.9 slice_select_fusion.2
  32.6 2.6 %copy.137 = bf16[2,512,1280]{1,2,0:T(8,128)(2,1)} copy(bf16[2,512,1280]{2,1,0:T(8,128)(2,1)S(1)} %copy-done.6) | data formatting | bytes 5242880 | tf_op args[8]
  35.3 4.4 %fusion.6 = (bf16[2,512,1280]{1,2,0:T(8,128)(2,1)}, bf16[2,512,1280]{1,2,0:T(8,128)(2,1)S(1)}) fusion(f32[2,512,20]{1,2,0:T(8,128)S(1)} %copy.140, bf16[2,512,1280]{1,2,0:T(8,128)(2,1)} %copy.137, pred[2,512]{1,0:T(4,128)(4,1)S(1)} %iota_compare_fusion.1), kind=kLoop, calls=%fused_computation.11 | loop fusion | flops 7864320 | bytes 7947264 | tf_op jit(solution)/shard_map/convert_element_type | solution.py:11
  39.7 0.9 fusion.20
  40.6 0.4 copy-done.5
  41.0 1.3 %select_add_fusion = f32[20,64,128]{2,1,0:T(8,128)S(1)} fusion(f32[20,64,128]{2,1,0:T(8,128)} %collective-permute-done.4, f32[40,64,128]{2,1,0:T(8,128)S(1)} %copy-done.5, pred[]{:T(512)S(6)} %eq.22), kind=kLoop, calls=%fused_computation.40 | loop fusion | flops 327680 | bytes 2621441 | tf_op jit(solution)/shard_map/add | solution.py:118
  42.6 0.9 copy.143
  43.5 2.0 %collective-permute-start.5 = (f32[4,40,8,128]{3,2,1,0:T(8,128)}, f32[4,40,8,128]{3,2,1,0:T(8,128)}, u32[]{:S(2)}, u32[]{:S(2)}) collective-permute-start(f32[4,40,8,128]{3,2,1,0:T(8,128)} %bitcast.17), channel_id=1, source_target_pairs={{0,2},{2,0},{4,6},{6,4},{8,10},{10,8},{12,14},{14,12},{1,3},{3,1},... | collective-permute-start | bytes 1966088 | tf_op jit(solution)/shard_map/ppermute | solution.py:56
  45.5 1.5 %copy.147 = f32[2,20,512]{2,1,0:T(8,128)} copy(f32[2,20,512]{2,0,1:T(2,128)} %copy-done.12) | data formatting | bytes 163840 | tf_op jit(solution)/shard_map/exp | solution.py:124
  47.0 1.5 %copy.148 = f32[2,20,4,128]{3,2,0,1:T(4,128)} copy(f32[2,20,4,128]{3,1,2,0:T(8,128)} %get-tuple-element.42) | data formatting | bytes 163840 | tf_op jit(solution)/shard_map/exp | solution.py:125
  48.6 1.6 %exp.34 = f32[2,20,512]{2,0,1:T(2,128)} reshape(f32[2,20,4,128]{3,2,0,1:T(4,128)} %copy.148) | data formatting | bytes 163840 | tf_op jit(solution)/shard_map/exp | solution.py:125
  50.2 0.9 copy.149
  51.2 1.5 %fusion.33 = f32[2,512,512]{2,1,0:T(8,128)S(1)} fusion(bf16[2,512,128]{2,1,0:T(8,128)(2,1)S(1)} %copy-done, bf16[2,512,128]{2,1,0:T(8,128)(2,1)} %param.13), kind=kOutput, calls=%fused_computation.77 | convolution fusion | flops 134217728 | bytes 2621440 | tf_op jit(solution)/shard_map/ctn,csn->cts/dot_general | solution.py:160
  52.7 8.5 %collective-permute-done.5 = f32[4,40,8,128]{3,2,1,0:T(8,128)} collective-permute-done((f32[4,40,8,128]{3,2,1,0:T(8,128)}, f32[4,40,8,128]{3,2,1,0:T(8,128)}, u32[]{:S(2)}, u32[]{:S(2)}) %collective-permute-start.5) | collective-permute-done | bytes 655392 | tf_op jit(solution)/shard_map/ppermute | solution.py:56
  61.2 1.1 bitcast_add_fusion
  62.4 0.8 slice_select_fusion.3
  63.1 1.7 %collective-permute-start.6 = (f32[2,40,8,128]{3,2,1,0:T(8,128)}, f32[2,40,8,128]{3,2,1,0:T(8,128)}, u32[]{:S(2)}, u32[]{:S(2)}) collective-permute-start(f32[2,40,8,128]{3,2,1,0:T(8,128)} %slice_select_fusion.3), channel_id=1, source_target_pairs={{0,4},{2,6},{4,0},{6,2},{8,12},{10,14},{12,8},{14,10},{1,5},{3,7},... | collective-permute-start | bytes 983048 | tf_op jit(solution)/shard_map/ppermute | solution.py:56
  64.9 6.4 %fusion.17 = bf16[2,20,64,512]{3,2,1,0:T(8,128)(2,1)} fusion(bf16[2,512,20,64]{1,3,2,0:T(8,128)(2,1)S(1)} %bitcast.108, f32[2,20,512]{2,1,0:T(8,128)S(1)} %copy.149, f32[2,20,512]{2,1,0:T(8,128)S(1)} %copy-done.14, f32[2,512,512]{2,1,0:T(8,128)S(1)} %fusion.33, pred[512,512]{1,0:T(8,128)(4,1)S(1)} %iota_compare_fusion), kind=kOutput, calls=%fused_computation.29 | convolution fusion | flops 1385431040 | bytes 7766016 | tf_op jit(solution)/shard_map/chts,cthp->cshp/dot_general | solution.py:165
  71.3 1.5 %copy.151 = f32[2,512,20]{1,2,0:T(8,128)} copy(f32[2,512,20]{1,0,2:T(2,128)} %bitcast.117) | data formatting | bytes 163840 | tf_op jit(solution)/shard_map/exp | solution.py:125
  72.9 4.4 %copy.150 = bf16[2,512,1280]{1,2,0:T(8,128)(2,1)} copy(bf16[2,512,1280]{2,1,0:T(8,128)(2,1)} %param.12) | data formatting | bytes 5242880 | tf_op args[3]
  77.3 3.1 %fusion.7 = (bf16[2,512,1280]{1,2,0:T(8,128)(2,1)S(1)}, bf16[2,512,1280]{1,2,0:T(8,128)(2,1)S(1)}, bf16[2,512,1280]{1,2,0:T(8,128)(2,1)S(1)}) fusion(bf16[2,512,1280]{1,2,0:T(8,128)(2,1)} %copy.150, f32[2,512,20]{1,2,0:T(8,128)} %copy.151, f32[2,512,20]{1,2,0:T(8,128)} %copy-done.11, bf16[2,512,1280]{1,2,0:T(8,128)(2,1)S(1)} %get-tuple-element.31), kind=kLoop, calls=%fused_computation.12 | loop fusion | flops 13107200 | bytes 13271040 | tf_op jit(solution)/shard_map/convert_element_type | solution.py:11
  80.4 1.3 %select_add_fusion.1 = f32[2,40,8,128]{3,2,1,0:T(8,128)S(1)} fusion(f32[2,40,8,128]{3,2,1,0:T(8,128)} %collective-permute-done.6, f32[4,40,8,128]{3,2,1,0:T(8,128)S(1)} %bitcast_add_fusion, pred[]{:T(512)S(6)} %eq.24), kind=kLoop, calls=%fused_computation.48 | loop fusion | flops 163840 | bytes 1310721 | tf_op jit(solution)/shard_map/add | solution.py:56
  81.8 1.0 collective-permute-start.7
  82.8 1.6 %fusion.35 = f32[2,512,512]{2,1,0:T(8,128)S(1)} fusion(bf16[2,512,1280]{1,2,0:T(8,128)(2,1)S(1)} %get-tuple-element.46, bf16[2,512,1280]{1,2,0:T(8,128)(2,1)S(1)} %get-tuple-element.32), kind=kOutput, calls=%fused_computation.79 | convolution fusion | flops 1342177280 | bytes 7340032 | tf_op jit(solution)/shard_map/ctk,csk->cts/dot_general | solution.py:146
  84.3 7.4 %collective-permute-done.7 = f32[1,40,8,128]{3,2,1,0:T(8,128)S(1)} collective-permute-done((f32[1,40,8,128]{3,2,1,0:T(8,128)S(1)}, f32[1,40,8,128]{3,2,1,0:T(8,128)S(1)}, u32[]{:S(2)}, u32[]{:S(2)}) %collective-permute-start.7) | collective-permute-done | bytes 163872 | tf_op jit(solution)/shard_map/ppermute | solution.py:56
  91.8 1.6 %fusion.34 = f32[2,512,512]{2,1,0:T(8,128)S(1)} fusion(bf16[2,512,1280]{1,2,0:T(8,128)(2,1)S(1)} %get-tuple-element.46, bf16[2,512,1280]{1,2,0:T(8,128)(2,1)S(1)} %get-tuple-element.33), kind=kOutput, calls=%fused_computation.78 | convolution fusion | flops 1342177280 | bytes 7340032 | tf_op jit(solution)/shard_map/ctk,csk->cts/dot_general | solution.py:146
  93.4 3.7 %collective-permute-done.8 = bf16[1,40,8,128]{3,2,1,0:T(8,128)(2,1)S(1)} collective-permute-done((bf16[1,40,8,128]{3,2,1,0:T(8,128)(2,1)S(1)}, bf16[1,40,8,128]{3,2,1,0:T(8,128)(2,1)S(1)}, u32[]{:S(2)}, u32[]{:S(2)}) %collective-permute-start.8) | collective-permute-done | bytes 81952 | tf_op jit(solution)/shard_map/ppermute | solution.py:67
  97.2 1.8 %add_select_fusion = f32[2,512,512]{2,1,0:T(8,128)S(1)} fusion(f32[2,512,512]{2,1,0:T(8,128)S(1)} %fusion.34, f32[2,512,512]{2,1,0:T(8,128)S(1)} %fusion.35, bf16[2,512,1280]{1,2,0:T(8,128)(2,1)S(1)} %copy-done.3, bf16[2,512,1280]{1,2,0:T(8,128)(2,1)S(1)} %get-tuple-element.33, pred[512,512]{1,0:T(8,128)(4,1)S(1)} %copy-done.8), kind=kOutput, calls=%fused_computation.28 | convolution fusion | flops 1343750144 | bytes 11796480 | tf_op jit(solution)/shard_map/ctk,csk->cts/dot_general | solution.py:146
  99.0 3.5 %collective-permute-done.9 = bf16[2,40,8,128]{3,2,1,0:T(8,128)(2,1)S(1)} collective-permute-done((bf16[2,40,8,128]{3,2,1,0:T(8,128)(2,1)S(1)}, bf16[2,40,8,128]{3,2,1,0:T(8,128)(2,1)S(1)}, u32[]{:S(2)}, u32[]{:S(2)}) %collective-permute-start.9) | collective-permute-done | bytes 163872 | tf_op jit(solution)/shard_map/ppermute | solution.py:67
  102.6 1.6 %collective-permute-start.10 = (bf16[4,40,8,128]{3,2,1,0:T(8,128)(2,1)S(1)}, bf16[4,40,8,128]{3,2,1,0:T(8,128)(2,1)S(1)}, u32[]{:S(2)}, u32[]{:S(2)}) collective-permute-start(bf16[4,40,8,128]{3,2,1,0:T(8,128)(2,1)S(1)} %maximum_select_fusion.2), channel_id=1, source_target_pairs={{0,2},{2,0},{4,6},{6,4},{8,10},{10,8},{12,14},{14,12},{1,3},{3,1},... | collective-permute-start | bytes 983048 | tf_op jit(solution)/shard_map/ppermute | solution.py:67
  104.2 1.3 %fusion.37 = f32[2,512,128]{1,2,0:T(8,128)S(1)} fusion(f32[2,512,512]{2,1,0:T(8,128)S(1)} %add_select_fusion, bf16[2,512,128]{2,1,0:T(8,128)(2,1)S(1)} %copy-done.10), kind=kOutput, calls=%fused_computation.81 | convolution fusion | flops 805306368 | bytes 2883584 | tf_op jit(solution)/shard_map/cts,csn->ctn/dot_general | solution.py:156
  105.5 4.4 %copy.167 = bf16[2,512,1280]{2,1,0:T(8,128)(2,1)} copy(bf16[2,512,1280]{1,2,0:T(8,128)(2,1)} %bitcast.110) | data formatting | bytes 5242880
  109.8 0.9 fusion.36
  111.2 1.2 %copy-done.2 = bf16[2,512,1280]{1,2,0:T(8,128)(2,1)S(1)} copy-done((bf16[2,512,1280]{1,2,0:T(8,128)(2,1)S(1)}, bf16[2,512,1280]{1,2,0:T(8,128)(2,1)}, u32[]{:S(2)}) %copy-start.2) | copy-done | bytes 2621464
  112.5 0.6 convolution_add_fusion
  113.1 0.7 reshape.184
  113.8 0.8 fusion.30
  114.7 0.3 copy.182
  115.0 0.3 copy.183
  115.4 0.9 select_bitcast_fusion
  116.3 2.0 %fusion.8 = f32[256,128]{0,1:T(8,128)S(1)} fusion(f32[256,40]{0,1:T(8,128)S(1)} %copy-done.16, bf16[256,40,64]{0,2,1:T(8,128)(2,1)S(1)} %bitcast.114, bf16[20,64,128]{2,1,0:T(8,128)(2,1)} %collective-permute-done.11, bf16[20,64,128]{2,1,0:T(8,128)(2,1)S(1)} %bitcast.120, pred[]{:T(512)S(6)} %eq.22), kind=kOutput, calls=%fused_computation.16 | convolution fusion | flops 171343872 | bytes 2138113 | tf_op jit(solution)/shard_map/jhp,hpn->jhn/dot_general | solution.py:187
  118.3 0.8 copy.166
  119.1 1.6 %fusion.18 = bf16[40,64,256]{2,1,0:T(8,128)(2,1)S(1)} fusion(f32[256,128]{0,1:T(8,128)} %copy-done.13, f32[256,40]{0,1:T(8,128)S(1)} %copy-done.16, bf16[20,64,128]{2,1,0:T(8,128)(2,1)} %collective-permute-done.11, bf16[20,64,128]{2,1,0:T(8,128)(2,1)S(1)} %bitcast.121, pred[]{:T(512)S(6)} %eq.22), kind=kOutput, calls=%fused_computation.30 | convolution fusion | flops 172032000 | bytes 2138113 | tf_op jit(solution)/shard_map/jhn,hpn->jhp/dot_general | solution.py:183
  120.7 1.6 %copy.165 = bf16[256,2560]{1,0:T(8,128)(2,1)} copy(bf16[256,2560]{0,1:T(8,128)(2,1)S(1)} %bitcast.115) | data formatting | bytes 2621440
  122.3 1.1 bitcast_add_fusion.1
  123.5 0.8 fusion.32
  (76 shorter events, 1.8 us)
Async XLA Ops:
  0.6 39.1 %copy-start = (bf16[2,512,128]{2,1,0:T(8,128)(2,1)S(1)}, bf16[2,512,128]{2,1,0:T(8,128)(2,1)}, u32[]{:S(2)}) copy-start(bf16[2,512,128]{2,1,0:T(8,128)(2,1)} %param.14) | copy-start | bytes 786436
  1.6 6.5 %collective-permute-start = (f32[40]{0:T(128)S(1)}, f32[40]{0:T(128)S(1)}, u32[]{:S(2)}, u32[]{:S(2)}) collective-permute-start(f32[40]{0:T(128)S(1)} %get-tuple-element.44), channel_id=1, source_target_pairs={{1,0},{2,1},{3,2},{4,3},{5,4},{6,5},{7,6},{8,7},{9,8},{10,9},{11,1... | collective-permute-start | bytes 488 | tf_op jit(solution)/shard_map/ppermute | solution.py:30
  8.1 7.0 %collective-permute-start.1 = (f32[40]{0:T(128)S(1)}, f32[40]{0:T(128)S(1)}, u32[]{:S(2)}, u32[]{:S(2)}) collective-permute-start(f32[40]{0:T(128)S(1)} %add.64), channel_id=1, source_target_pairs={{2,0},{3,1},{4,2},{5,3},{6,4},{7,5},{8,6},{9,7},{10,8},{11,9},{12,... | collective-permute-start | bytes 488 | tf_op jit(solution)/shard_map/ppermute | solution.py:30
  15.1 6.3 %collective-permute-start.2 = (f32[40]{0:T(128)S(1)}, f32[40]{0:T(128)S(1)}, u32[]{:S(2)}, u32[]{:S(2)}) collective-permute-start(f32[40]{0:T(128)S(1)} %add.65), channel_id=1, source_target_pairs={{4,0},{5,1},{6,2},{7,3},{8,4},{9,5},{10,6},{11,7},{12,8},{13,9},{1... | collective-permute-start | bytes 488 | tf_op jit(solution)/shard_map/ppermute | solution.py:30
  17.4 13.0 %copy-start.13 = (f32[256,128]{0,1:T(8,128)}, f32[256,128]{0,1:T(8,128)S(1)}, u32[]{:S(2)}) copy-start(f32[256,128]{0,1:T(8,128)S(1)} %copy.134) | copy-start | bytes 393220
  21.4 6.3 %collective-permute-start.3 = (f32[40]{0:T(128)S(1)}, f32[40]{0:T(128)S(1)}, u32[]{:S(2)}, u32[]{:S(2)}) collective-permute-start(f32[40]{0:T(128)S(1)} %add.66), channel_id=1, source_target_pairs={{8,0},{9,1},{10,2},{11,3},{12,4},{13,5},{14,6},{15,7},{24,16},{25,... | collective-permute-start | bytes 488 | tf_op jit(solution)/shard_map/ppermute | solution.py:30
  27.9 4.5 %copy-start.15 = (f32[256,40]{0,1:T(8,128)}, f32[256,40]{0,1:T(8,128)S(1)}, u32[]{:S(2)}) copy-start(f32[256,40]{0,1:T(8,128)S(1)} %fusion.24) | copy-start | bytes 122884
  27.9 4.5 %copy-start.17 = (s32[2]{0:T(128)S(1)}, s32[2]{0:T(128)}, u32[]{:S(2)}) copy-start(s32[2]{0:T(128)} %param.16) | copy-start | bytes 28
  27.9 4.7 %copy-start.6 = (bf16[2,512,1280]{2,1,0:T(8,128)(2,1)S(1)}, bf16[2,512,1280]{2,1,0:T(8,128)(2,1)}, u32[]{:S(2)}) copy-start(bf16[2,512,1280]{2,1,0:T(8,128)(2,1)} %param.17) | copy-start | bytes 7864324
  30.4 1.1 copy-start.4
  32.4 8.2 %collective-permute-start.4 = (f32[20,64,128]{2,1,0:T(8,128)}, f32[20,64,128]{2,1,0:T(8,128)}, u32[]{:S(2)}, u32[]{:S(2)}) collective-permute-start(f32[20,64,128]{2,1,0:T(8,128)} %slice_select_fusion.2), channel_id=1, source_target_pairs={{0,1},{1,0},{2,3},{3,2},{4,5},{5,4},{6,7},{7,6},{8,9},{9,8},{10,11... | collective-permute-start | bytes 1966088 | tf_op jit(solution)/shard_map/ppermute | solution.py:91
  32.5 2.7 %copy-start.12 = (f32[2,20,512]{2,0,1:T(2,128)}, f32[2,20,512]{2,0,1:T(2,128)S(1)}, u32[]{:S(2)}) copy-start(f32[2,20,512]{2,0,1:T(2,128)S(1)} %exp.31) | copy-start | bytes 245764
  32.6 7.1 %copy-start.11 = (f32[2,512,20]{1,2,0:T(8,128)}, f32[2,512,20]{1,2,0:T(8,128)S(1)}, u32[]{:S(2)}) copy-start(f32[2,512,20]{1,2,0:T(8,128)S(1)} %copy.140) | copy-start | bytes 245764
  39.7 1.3 %copy-start.5 = (f32[40,64,128]{2,1,0:T(8,128)S(1)}, f32[40,64,128]{2,1,0:T(8,128)}, u32[]{:S(2)}) copy-start(f32[40,64,128]{2,1,0:T(8,128)} %copy-done.4) | copy-start | bytes 3932164
  43.5 17.7 %collective-permute-start.5 = (f32[4,40,8,128]{3,2,1,0:T(8,128)}, f32[4,40,8,128]{3,2,1,0:T(8,128)}, u32[]{:S(2)}, u32[]{:S(2)}) collective-permute-start(f32[4,40,8,128]{3,2,1,0:T(8,128)} %bitcast.17), channel_id=1, source_target_pairs={{0,2},{2,0},{4,6},{6,4},{8,10},{10,8},{12,14},{14,12},{1,3},{3,1},... | collective-permute-start | bytes 1966088 | tf_op jit(solution)/shard_map/ppermute | solution.py:56
  51.2 13.7 %copy-start.7 = (pred[512,512]{1,0:T(8,128)(4,1)}, pred[512,512]{1,0:T(8,128)(4,1)S(1)}, u32[]{:S(2)}) copy-start(pred[512,512]{1,0:T(8,128)(4,1)S(1)} %iota_compare_fusion) | copy-start | bytes 786436
  52.7 12.2 %copy-start.14 = (f32[2,20,512]{2,1,0:T(8,128)S(1)}, f32[2,20,512]{2,1,0:T(8,128)}, u32[]{:S(2)}) copy-start(f32[2,20,512]{2,1,0:T(8,128)} %copy.147) | copy-start | bytes 245764
  63.1 17.3 %collective-permute-start.6 = (f32[2,40,8,128]{3,2,1,0:T(8,128)}, f32[2,40,8,128]{3,2,1,0:T(8,128)}, u32[]{:S(2)}, u32[]{:S(2)}) collective-permute-start(f32[2,40,8,128]{3,2,1,0:T(8,128)} %slice_select_fusion.3), channel_id=1, source_target_pairs={{0,4},{2,6},{4,0},{6,2},{8,12},{10,14},{12,8},{14,10},{1,5},{3,7},... | collective-permute-start | bytes 983048 | tf_op jit(solution)/shard_map/ppermute | solution.py:56
  80.4 11.4 %copy-start.1 = (bf16[2,512,1280]{1,2,0:T(8,128)(2,1)}, bf16[2,512,1280]{1,2,0:T(8,128)(2,1)S(1)}, u32[]{:S(2)}) copy-start(bf16[2,512,1280]{1,2,0:T(8,128)(2,1)S(1)} %get-tuple-element.46) | copy-start | bytes 7864324
  81.8 9.9 %collective-permute-start.7 = (f32[1,40,8,128]{3,2,1,0:T(8,128)S(1)}, f32[1,40,8,128]{3,2,1,0:T(8,128)S(1)}, u32[]{:S(2)}, u32[]{:S(2)}) collective-permute-start(f32[1,40,8,128]{3,2,1,0:T(8,128)S(1)} %slice_select_fusion.4), channel_id=1, source_target_pairs={{0,8},{2,10},{4,12},{6,14},{8,0},{10,2},{12,4},{14,6},{1,9},{3,11}... | collective-permute-start | bytes 491528 | tf_op jit(solution)/shard_map/ppermute | solution.py:56
  91.7 5.4 %collective-permute-start.8 = (bf16[1,40,8,128]{3,2,1,0:T(8,128)(2,1)S(1)}, bf16[1,40,8,128]{3,2,1,0:T(8,128)(2,1)S(1)}, u32[]{:S(2)}, u32[]{:S(2)}) collective-permute-start(bf16[1,40,8,128]{3,2,1,0:T(8,128)(2,1)S(1)} %add_convert_fusion), channel_id=1, source_target_pairs={{0,8},{2,10},{4,12},{6,14},{8,0},{10,2},{12,4},{14,6},{1,9},{3,11}... | collective-permute-start | bytes 245768 | tf_op jit(solution)/shard_map/ppermute | solution.py:67
  91.8 5.4 %copy-start.3 = (bf16[2,512,1280]{1,2,0:T(8,128)(2,1)S(1)}, bf16[2,512,1280]{1,2,0:T(8,128)(2,1)}, u32[]{:S(2)}) copy-start(bf16[2,512,1280]{1,2,0:T(8,128)(2,1)} %get-tuple-element.30) | copy-start | bytes 7864324
  91.8 5.4 %copy-start.8 = (pred[512,512]{1,0:T(8,128)(4,1)S(1)}, pred[512,512]{1,0:T(8,128)(4,1)}, u32[]{:S(2)}) copy-start(pred[512,512]{1,0:T(8,128)(4,1)} %copy-done.7) | copy-start | bytes 786436
  97.1 5.4 %collective-permute-start.9 = (bf16[2,40,8,128]{3,2,1,0:T(8,128)(2,1)S(1)}, bf16[2,40,8,128]{3,2,1,0:T(8,128)(2,1)S(1)}, u32[]{:S(2)}, u32[]{:S(2)}) collective-permute-start(bf16[2,40,8,128]{3,2,1,0:T(8,128)(2,1)S(1)} %maximum_select_fusion.3), channel_id=1, source_target_pairs={{0,4},{2,6},{4,0},{6,2},{8,12},{10,14},{12,8},{14,10},{1,5},{3,7},... | collective-permute-start | bytes 491528 | tf_op jit(solution)/shard_map/ppermute | solution.py:67
  97.2 6.9 %copy-start.10 = (bf16[2,512,128]{2,1,0:T(8,128)(2,1)S(1)}, bf16[2,512,128]{2,1,0:T(8,128)(2,1)}, u32[]{:S(2)}) copy-start(bf16[2,512,128]{2,1,0:T(8,128)(2,1)} %param.13) | copy-start | bytes 786436
  102.6 8.2 %collective-permute-start.10 = (bf16[4,40,8,128]{3,2,1,0:T(8,128)(2,1)S(1)}, bf16[4,40,8,128]{3,2,1,0:T(8,128)(2,1)S(1)}, u32[]{:S(2)}, u32[]{:S(2)}) collective-permute-start(bf16[4,40,8,128]{3,2,1,0:T(8,128)(2,1)S(1)} %maximum_select_fusion.2), channel_id=1, source_target_pairs={{0,2},{2,0},{4,6},{6,4},{8,10},{10,8},{12,14},{14,12},{1,3},{3,1},... | collective-permute-start | bytes 983048 | tf_op jit(solution)/shard_map/ppermute | solution.py:67
  110.7 1.7 %copy-start.2 = (bf16[2,512,1280]{1,2,0:T(8,128)(2,1)S(1)}, bf16[2,512,1280]{1,2,0:T(8,128)(2,1)}, u32[]{:S(2)}) copy-start(bf16[2,512,1280]{1,2,0:T(8,128)(2,1)} %copy-done.1) | copy-start | bytes 7864324
  111.2 5.1 %collective-permute-start.11 = (bf16[20,64,128]{2,1,0:T(8,128)(2,1)S(1)}, bf16[20,64,128]{2,1,0:T(8,128)(2,1)}, u32[]{:S(2)}, u32[]{:S(2)}) collective-permute-start(bf16[20,64,128]{2,1,0:T(8,128)(2,1)S(1)} %bitcast.119), channel_id=1, source_target_pairs={{0,1},{1,0},{2,3},{3,2},{4,5},{5,4},{6,7},{7,6},{8,9},{9,8},{10,11... | collective-permute-start | bytes 983048 | tf_op jit(solution)/shard_map/ppermute | solution.py:91
  113.8 2.4 %copy-start.16 = (f32[256,40]{0,1:T(8,128)S(1)}, f32[256,40]{0,1:T(8,128)}, u32[]{:S(2)}) copy-start(f32[256,40]{0,1:T(8,128)} %copy-done.15) | copy-start | bytes 122884
  115.0 1.3 %copy-start.9 = (bf16[256,2560]{0,1:T(8,128)(2,1)S(1)}, bf16[256,2560]{0,1:T(8,128)(2,1)}, u32[]{:S(2)}) copy-start(bf16[256,2560]{0,1:T(8,128)(2,1)} %copy.135) | copy-start | bytes 3932164
  116.2 6.1 %collective-permute-start.12 = (f32[2,256,256]{2,1,0:T(8,128)}, f32[2,256,256]{2,1,0:T(8,128)}, u32[]{:S(2)}, u32[]{:S(2)}) collective-permute-start(f32[2,256,256]{2,1,0:T(8,128)} %select_bitcast_fusion), channel_id=1, source_target_pairs={{0,1},{1,0},{2,3},{3,2},{4,5},{5,4},{6,7},{7,6},{8,9},{9,8},{10,11... | collective-permute-start | bytes 1572872 | tf_op jit(solution)/shard_map/ppermute | solution.py:91

commit v8 on v7

--- a/solution.py
+++ b/solution.py
@@ -22,14 +22,23 @@
     return value
 
 
-def suffix_sum(value, axis):
+def suffix_sum(value, axis, works):
     count = lax.axis_size(axis)
     step = 1
+    done = []
+    rounds = 0
     while step < count:
         back = [(at, at - step) for at in range(step, count)]
+        if rounds < len(works):
+            fn, args = works[rounds]
+            value, args = lax.optimization_barrier((value, args))
         value = value + lax.ppermute(value, axis, back)
+        if rounds < len(works):
+            value, piece = lax.optimization_barrier((value, fn(*args)))
+            done.append(piece)
         step *= 2
-    return value
+        rounds += 1
+    return value, done
 
 
 def bit_order(value, count, first_bits):
@@ -102,7 +111,27 @@
 
     log_prefix = jnp.log1p(-code_prefix.astype(jnp.float32) * 1e-06)
     own_total = jnp.sum(log_prefix, axis=0)
-    later_total = suffix_sum(own_total, pre_axes) - own_total
+    position = jnp.arange(cand_len, dtype=jnp.int32)
+
+    def level_work(code_cand):
+        level_all = jnp.cumsum(jnp.log1p(-code_cand.astype(jnp.float32) * 1e-06), axis=1)
+        return jnp.exp(level_all), jnp.exp(-level_all)
+
+    def g_work(dy_cand, lengths):
+        valid_rows = position[None, :] < lengths[:, None] * BLOCK
+        g_cand = jnp.where(valid_rows[:, :, None], dy_cand, jnp.zeros_like(dy_cand))
+        return g_cand.reshape(cand_dev, cand_len, half_heads, head_size)
+
+    def scores_work(c_cand, b_cand):
+        return jnp.einsum("ctn,csn->cts", c_cand, b_cand, preferred_element_type=jnp.float32)
+
+    inclusive, (levels, g_heads, scores) = suffix_sum(
+        own_total,
+        pre_axes,
+        [(level_work, (code_cand,)), (g_work, (dy_cand, lengths)), (scores_work, (c_cand, b_cand))],
+    )
+    amplitude, inverse = levels
+    later_total = inclusive - own_total
     after_local = own_total[None, :] - jnp.cumsum(log_prefix, axis=0)
     weight = jnp.exp(after_local + later_total[None, :])
     weighted_b = (weight[:, :, None] * b_prefix[:, None, :].astype(jnp.float32)).astype(
@@ -117,13 +146,6 @@
     give_half = jnp.where(mine_first, state_halves[1], state_halves[0])
     init_local = own_half + other_core(give_half)
 
-    position = jnp.arange(cand_len, dtype=jnp.int32)
-    valid_rows = position[None, :] < lengths[:, None] * BLOCK
-    g_cand = jnp.where(valid_rows[:, :, None], dy_cand, jnp.zeros_like(dy_cand))
-    level_all = jnp.cumsum(jnp.log1p(-code_cand.astype(jnp.float32) * 1e-06), axis=1)
-    amplitude = jnp.exp(level_all)
-    inverse = jnp.exp(-level_all)
-    g_heads = g_cand.reshape(cand_dev, cand_len, half_heads, head_size)
     xc_heads = x_cand.reshape(cand_dev, cand_len, half_heads, head_size)
     scaled_g = g_heads.astype(jnp.float32) * amplitude[:, :, :, None]
     decayed_g, g_low = split_bf16(scaled_g)
@@ -157,7 +179,6 @@
         "cts,csn->ctn", weight_sum, b_cand.astype(jnp.float32), precision=lax.Precision.HIGHEST
     )
 
-    scores = jnp.einsum("ctn,csn->cts", c_cand, b_cand, preferred_element_type=jnp.float32)
     amp_t = jnp.transpose(amplitude, (0, 2, 1))
     inv_t = jnp.transpose(inverse, (0, 2, 1))
     decay_mat = amp_t[:, :, :, None] * inv_t[:, :, None, :]

time: 125 us -> 115 us (0.920)
  local copies, waits for them, and re-layouts: 32 us -> 25.3 us
  other arithmetic: 21.4 us -> 18.1 us
  matrix products: 22.6 us -> 23.9 us
    unnamed x44 -> x41, local copies, waits for them, and re-layouts: 19.8 us -> 13 us
    exp x8 -> x4, local copies, waits for them, and re-layouts: 7.19 us -> 0.8 us  [level_work(): return (jnp.exp(level_all), jnp.exp(-level_all))]
    optimization_barrier x0 -> x3, local copies, waits for them, and re-layouts: none -> 3.92 us  [the longest x1 3 us: suffix_sum(): value, args = lax.optimization_barrier((value, args))]
    convert_element_type x2, other arithmetic: 7.55 us -> 5.47 us  [split_bf16(): low = (value - high).astype(jnp.bfloat16)]
    select_n x3, other arithmetic: 0.15 us -> 2.15 us  [doubling_gather(): jnp.where(upper, jnp.concatenate([other, value]), jnp.concatenate([value,...]
    ppermute x4, waiting for transfers between devices: 12.3 us -> 10.4 us  [suffix_sum(): value = value + lax.ppermute(value, axis, back)]
    transpose x0 -> x2, local copies, waits for them, and re-layouts: none -> 1.81 us  [the longest x1 0.9 us: shards(): inv_t = jnp.transpose(inverse, (0, 2, 1))]
    select_n x0 -> x1, other arithmetic: none -> 1.67 us  [g_work(): g_cand = jnp.where(valid_rows[:, :, None], dy_cand, jnp.zeros_like(dy_cand))]
  transfers between devices with their start and end apart: 13 -> 13, of which waited for: 7 -> 8; matrix products, arithmetic and copies ran while one was open for 49% -> 50% of each run, Pallas kernels for 0% -> 0%
where the time goes in v8:
time: 115 us; the launch traced here: 114 us
  waiting for transfers between devices  34.5 us (30%)
  local copies, waits for them, and re-layouts  25.3 us (22%)
  matrix products  23.9 us (21%)
  other arithmetic  18.1 us (16%)
  starting transfers between devices  11 us (10%)
  between operations  1.27 us (1%)
    ppermute x3, waiting for transfers between devices, halving_scatter(): lax.ppermute(give, axis, [(at, at ^ step) for at in range(count)])  16.6 us
    unnamed x41, local copies, waits for them, and re-layouts  13 us
    ppermute x4, waiting for transfers between devices, suffix_sum(): value = value + lax.ppermute(value, axis, back)  10.4 us
    ppermute x3, waiting for transfers between devices, doubling_gather(): other = lax.ppermute(value, axis, [(at, at ^ step) for at in range(count)])  7.58 us
    dot_general x1, matrix products, shards(): jnp.einsum('chts,cthp->cshp', kernel, g_heads, preferred_element_type=jnp...  7.33 us
    convert_element_type x2, other arithmetic, split_bf16(): low = (value - high).astype(jnp.bfloat16)  5.47 us
    ppermute x4, starting transfers between devices, suffix_sum(): value = value + lax.ppermute(value, axis, back)  5.26 us
    dot_general x3, matrix products, pair(): jnp.einsum('ctk,csk->cts', left.reshape(flat), right.reshape(flat), prefe...  4.94 us
  transfers between devices with their start and end apart: 13, of which 8 were waited for; matrix products, arithmetic and copies ran while one was open for 50% of the time, Pallas kernels for 0%

profile of v8, /device:TPU:0, one launch (start us, length us, event | category | flops | bytes accessed | tf_op | source)
XLA Modules:
  0.0 114.1 jit_solution(2039527086229874437)
XLA Ops:
  0.6 0.9 fusion.23
  1.6 1.3 %collective-permute-start = (f32[40]{0:T(128)S(1)}, f32[40]{0:T(128)S(1)}, u32[]{:S(2)}, u32[]{:S(2)}) collective-permute-start(f32[40]{0:T(128)S(1)} %get-tuple-element.20), channel_id=1, source_target_pairs={{1,0},{2,1},{3,2},{4,3},{5,4},{6,5},{7,6},{8,7},{9,8},{10,9},{11,1... | collective-permute-start | bytes 488 | tf_op jit(solution)/shard_map/ppermute | solution.py:35
  2.9 0.6 reduce-window.14
  3.5 0.2 slice_reduce_fusion.1
  3.7 1.0 log-plus-one_bitcast_fusion
  4.9 2.3 %reduce-window.16 = f32[2,20,4,128]{3,1,2,0:T(8,128)S(1)} reduce-window(f32[2,20,4,128]{3,1,2,0:T(8,128)S(1)} %copy.135, f32[]{:T(128)} %constant.84.clone.1), window={size=1x1x1x128 pad=0_0x0_0x0_0x127_0}, to_apply=%region_3.4 | reduce-window | flops 2600960 | bytes 163844 | tf_op jit(solution)/shard_map/reduce-window.2
  7.2 0.2 slice_reduce_fusion
  7.4 0.1 negate_exponential_fusion
  7.6 0.7 exp.28
  8.4 1.0 copy.139
  9.4 0.7 broadcast_multiply_fusion
  10.1 1.3 %collective-permute-start.1 = (f32[40]{0:T(128)S(1)}, f32[40]{0:T(128)S(1)}, u32[]{:S(2)}, u32[]{:S(2)}) collective-permute-start(f32[40]{0:T(128)S(1)} %add.64), channel_id=1, source_target_pairs={{2,0},{3,1},{4,2},{5,3},{6,4},{7,5},{8,6},{9,7},{10,8},{11,9},{12,... | collective-permute-start | bytes 488 | tf_op jit(solution)/shard_map/ppermute | solution.py:35
  11.4 3.0 %copy.138 = bf16[2,512,1280]{1,2,0:T(8,128)(2,1)S(1)} copy(bf16[2,512,1280]{2,1,0:T(8,128)(2,1)} %param.17) | data formatting | bytes 5242880 | tf_op jit(solution)/shard_map/optimization_barrier | solution.py:34
  14.5 1.7 %broadcast_select_fusion = bf16[2,512,1280]{1,2,0:T(8,128)(2,1)} fusion(bf16[2,512,1280]{1,2,0:T(8,128)(2,1)S(1)} %copy.138, pred[2,512]{1,0:T(4,128)(4,1)S(1)} %iota_compare_fusion.1), kind=kLoop, calls=%fused_computation.24 | loop fusion | flops 1310720 | bytes 5243904 | tf_op jit(solution)/shard_map/jit(_where)/select_n | solution.py:122
  16.1 1.0 collective-permute-done.1
  17.2 1.4 %collective-permute-start.2 = (f32[40]{0:T(128)S(1)}, f32[40]{0:T(128)S(1)}, u32[]{:S(2)}, u32[]{:S(2)}) collective-permute-start(f32[40]{0:T(128)S(1)} %add.65), channel_id=1, source_target_pairs={{4,0},{5,1},{6,2},{7,3},{8,4},{9,5},{10,6},{11,7},{12,8},{13,9},{1... | collective-permute-start | bytes 488 | tf_op jit(solution)/shard_map/ppermute | solution.py:35
  18.6 1.8 %fusion.30 = f32[2,512,512]{2,1,0:T(8,128)} fusion(bf16[2,512,128]{2,1,0:T(8,128)(2,1)S(1)} %copy-done, bf16[2,512,128]{2,1,0:T(8,128)(2,1)S(1)} %copy-done.9), kind=kOutput, calls=%fused_computation.74 | convolution fusion | flops 134217728 | bytes 2621440 | tf_op jit(solution)/shard_map/ctn,csn->cts/dot_general | solution.py:126
  20.4 5.0 %collective-permute-done.2 = f32[40]{0:T(128)S(1)} collective-permute-done((f32[40]{0:T(128)S(1)}, f32[40]{0:T(128)S(1)}, u32[]{:S(2)}, u32[]{:S(2)}) %collective-permute-start.2) | collective-permute-done | bytes 192 | tf_op jit(solution)/shard_map/ppermute | solution.py:35
  25.4 1.3 %collective-permute-start.3 = (f32[40]{0:T(128)S(1)}, f32[40]{0:T(128)S(1)}, u32[]{:S(2)}, u32[]{:S(2)}) collective-permute-start(f32[40]{0:T(128)S(1)} %add.66), channel_id=1, source_target_pairs={{8,0},{9,1},{10,2},{11,3},{12,4},{13,5},{14,6},{15,7},{24,16},{25,... | collective-permute-start | bytes 488 | tf_op jit(solution)/shard_map/ppermute | solution.py:35
  26.7 0.6 copy.140
  27.3 4.4 %collective-permute-done.3 = f32[40]{0:T(128)S(1)} collective-permute-done((f32[40]{0:T(128)S(1)}, f32[40]{0:T(128)S(1)}, u32[]{:S(2)}, u32[]{:S(2)}) %collective-permute-start.3) | collective-permute-done | bytes 192 | tf_op jit(solution)/shard_map/ppermute | solution.py:35
  31.8 1.0 fusion.17
  33.1 0.5 copy-done.2
  33.6 2.8 %fusion.6 = (bf16[2,512,20,64]{1,3,2,0:T(8,128)(2,1)}, bf16[2,512,20,64]{1,3,2,0:T(8,128)(2,1)S(1)}) fusion(bf16[2,512,20,64]{1,3,2,0:T(8,128)(2,1)S(1)} %bitcast.109, f32[2,512,20]{1,2,0:T(8,128)S(1)} %copy.142), kind=kLoop, calls=%fused_computation.11 | loop fusion | flops 7864320 | bytes 7946240 | tf_op jit(solution)/shard_map/convert_element_type | solution.py:11
  36.4 0.8 convolution_bitcast_fusion
  37.2 0.1 select_add_fusion
  37.4 0.1 maximum_bitcast_fusion
  37.7 0.9 copy.145
  38.6 1.5 %collective-permute-start.5 = (f32[4,40,8,128]{3,2,1,0:T(8,128)}, f32[4,40,8,128]{3,2,1,0:T(8,128)}, u32[]{:S(2)}, u32[]{:S(2)}) collective-permute-start(f32[4,40,8,128]{3,2,1,0:T(8,128)} %bitcast.18), channel_id=1, source_target_pairs={{0,2},{2,0},{4,6},{6,4},{8,10},{10,8},{12,14},{14,12},{1,3},{3,1},... | collective-permute-start | bytes 1966088 | tf_op jit(solution)/shard_map/ppermute | solution.py:65
  40.0 4.4 %copy.151 = bf16[2,512,1280]{1,2,0:T(8,128)(2,1)} copy(bf16[2,512,1280]{2,1,0:T(8,128)(2,1)} %param.12) | data formatting | bytes 5242880 | tf_op args[3]
  44.5 0.9 copy.152
  45.4 0.9 copy.150
  46.3 0.9 copy.149
  47.3 2.7 %fusion.7 = (bf16[2,512,1280]{1,2,0:T(8,128)(2,1)S(1)}, bf16[2,512,1280]{1,2,0:T(8,128)(2,1)S(1)}) fusion(bf16[2,512,1280]{1,2,0:T(8,128)(2,1)} %copy.151, f32[2,512,20]{1,2,0:T(8,128)S(1)} %copy.152), kind=kLoop, calls=%fused_computation.12 | loop fusion | flops 7864320 | bytes 7946240 | tf_op jit(solution)/shard_map/convert_element_type | solution.py:11
  49.9 1.6 %fusion.32 = f32[2,512,512]{2,1,0:T(8,128)S(1)} fusion(bf16[2,512,1280]{1,2,0:T(8,128)(2,1)S(1)} %bitcast.106, bf16[2,512,1280]{1,2,0:T(8,128)(2,1)S(1)} %get-tuple-element.62), kind=kOutput, calls=%fused_computation.76 | convolution fusion | flops 1342177280 | bytes 7340032 | tf_op jit(solution)/shard_map/ctk,csk->cts/dot_general | solution.py:168
  51.6 4.0 %collective-permute-done.5 = f32[4,40,8,128]{3,2,1,0:T(8,128)} collective-permute-done((f32[4,40,8,128]{3,2,1,0:T(8,128)}, f32[4,40,8,128]{3,2,1,0:T(8,128)}, u32[]{:S(2)}, u32[]{:S(2)}) %collective-permute-start.5) | collective-permute-done | bytes 655392 | tf_op jit(solution)/shard_map/ppermute | solution.py:65
  55.5 1.1 %bitcast_add_fusion = f32[4,40,8,128]{3,2,1,0:T(8,128)S(1)} fusion(f32[4,40,8,128]{3,2,1,0:T(8,128)} %collective-permute-done.5, f32[1,2,2,40,8,128]{5,4,3,2,1,0:T(8,128)S(1)} %copy.144), kind=kLoop, calls=%fused_computation.36 | loop fusion | flops 163840 | bytes 1966080 | tf_op jit(solution)/shard_map/add | solution.py:65
  56.7 2.1 %collective-permute-start.6 = (f32[2,40,8,128]{3,2,1,0:T(8,128)S(1)}, f32[2,40,8,128]{3,2,1,0:T(8,128)S(1)}, u32[]{:S(2)}, u32[]{:S(2)}) collective-permute-start(f32[2,40,8,128]{3,2,1,0:T(8,128)S(1)} %slice_select_fusion.3), channel_id=1, source_target_pairs={{0,4},{2,6},{4,0},{6,2},{8,12},{10,14},{12,8},{14,10},{1,5},{3,7},... | collective-permute-start | bytes 983048 | tf_op jit(solution)/shard_map/ppermute | solution.py:65
  58.8 1.6 %fusion.31 = f32[2,512,512]{2,1,0:T(8,128)S(1)} fusion(bf16[2,512,1280]{1,2,0:T(8,128)(2,1)S(1)} %bitcast.107, bf16[2,512,1280]{1,2,0:T(8,128)(2,1)S(1)} %get-tuple-element.63), kind=kOutput, calls=%fused_computation.75 | convolution fusion | flops 1342177280 | bytes 7340032 | tf_op jit(solution)/shard_map/ctk,csk->cts/dot_general | solution.py:168
  60.4 5.4 %collective-permute-done.6 = f32[2,40,8,128]{3,2,1,0:T(8,128)S(1)} collective-permute-done((f32[2,40,8,128]{3,2,1,0:T(8,128)S(1)}, f32[2,40,8,128]{3,2,1,0:T(8,128)S(1)}, u32[]{:S(2)}, u32[]{:S(2)}) %collective-permute-start.6) | collective-permute-done | bytes 327712 | tf_op jit(solution)/shard_map/ppermute | solution.py:65
  66.0 1.8 %add_select_fusion = f32[2,512,512]{2,1,0:T(8,128)S(1)} fusion(f32[2,512,512]{2,1,0:T(8,128)S(1)} %fusion.31, f32[2,512,512]{2,1,0:T(8,128)S(1)} %fusion.32, bf16[2,512,1280]{1,2,0:T(8,128)(2,1)S(1)} %bitcast.111, bf16[2,512,1280]{1,2,0:T(8,128)(2,1)S(1)} %get-tuple-element.63, pred[512,512]{1,0:T(8,128)(4,1)S(1)} %iota_compare_fusion), kind=kOutput, calls=%fused_computation.25 | convolution fusion | flops 1343750144 | bytes 11796480 | tf_op jit(solution)/shard_map/ctk,csk->cts/dot_general | solution.py:168
  67.8 7.2 %collective-permute-done.7 = f32[1,40,8,128]{3,2,1,0:T(8,128)S(1)} collective-permute-done((f32[1,40,8,128]{3,2,1,0:T(8,128)S(1)}, f32[1,40,8,128]{3,2,1,0:T(8,128)S(1)}, u32[]{:S(2)}, u32[]{:S(2)}) %collective-permute-start.7) | collective-permute-done | bytes 163872 | tf_op jit(solution)/shard_map/ppermute | solution.py:65
  75.1 1.3 %fusion.34 = f32[2,512,128]{1,2,0:T(8,128)S(1)} fusion(f32[2,512,512]{2,1,0:T(8,128)S(1)} %add_select_fusion, bf16[2,512,128]{2,1,0:T(8,128)(2,1)S(1)} %copy-done.10), kind=kOutput, calls=%fused_computation.78 | convolution fusion | flops 805306368 | bytes 2883584 | tf_op jit(solution)/shard_map/cts,csn->ctn/dot_general | solution.py:178
  76.4 4.0 %collective-permute-done.8 = bf16[1,40,8,128]{3,2,1,0:T(8,128)(2,1)S(1)} collective-permute-done((bf16[1,40,8,128]{3,2,1,0:T(8,128)(2,1)S(1)}, bf16[1,40,8,128]{3,2,1,0:T(8,128)(2,1)S(1)}, u32[]{:S(2)}, u32[]{:S(2)}) %collective-permute-start.8) | collective-permute-done | bytes 81952 | tf_op jit(solution)/shard_map/ppermute | solution.py:76
  80.5 1.7 %fusion.33 = f32[2,512,128]{1,2,0:T(8,128)} fusion(f32[2,512,512]{2,1,0:T(8,128)S(1)} %add_select_fusion, bf16[2,512,128]{2,1,0:T(8,128)(2,1)S(1)} %copy-done), kind=kOutput, calls=%fused_computation.77 | convolution fusion | flops 805306368 | bytes 2883584 | tf_op jit(solution)/shard_map/cts,ctn->csn/dot_general | solution.py:175
  82.2 3.6 %collective-permute-done.9 = bf16[2,40,8,128]{3,2,1,0:T(8,128)(2,1)S(1)} collective-permute-done((bf16[2,40,8,128]{3,2,1,0:T(8,128)(2,1)S(1)}, bf16[2,40,8,128]{3,2,1,0:T(8,128)(2,1)S(1)}, u32[]{:S(2)}, u32[]{:S(2)}) %collective-permute-start.9) | collective-permute-done | bytes 163872 | tf_op jit(solution)/shard_map/ppermute | solution.py:76
  85.8 0.8 maximum_select_fusion.2
  86.6 1.5 %collective-permute-start.10 = (bf16[4,40,8,128]{3,2,1,0:T(8,128)(2,1)}, bf16[4,40,8,128]{3,2,1,0:T(8,128)(2,1)}, u32[]{:S(2)}, u32[]{:S(2)}) collective-permute-start(bf16[4,40,8,128]{3,2,1,0:T(8,128)(2,1)} %maximum_select_fusion.2), channel_id=1, source_target_pairs={{0,2},{2,0},{4,6},{6,4},{8,10},{10,8},{12,14},{14,12},{1,3},{3,1},... | collective-permute-start | bytes 983048 | tf_op jit(solution)/shard_map/ppermute | solution.py:76
  88.0 7.3 %fusion.15 = bf16[2,20,64,512]{3,2,1,0:T(8,128)(2,1)} fusion(bf16[2,512,20,64]{1,3,2,0:T(8,128)(2,1)S(1)} %bitcast.110, f32[2,20,512]{2,1,0:T(8,128)S(1)} %copy.150, f32[2,20,512]{2,1,0:T(8,128)S(1)} %copy.149, f32[2,512,512]{2,1,0:T(8,128)S(1)} %copy-done.5, pred[512,512]{1,0:T(8,128)(4,1)S(1)} %iota_compare_fusion), kind=kOutput, calls=%fused_computation.26 | convolution fusion | flops 1385431040 | bytes 7766016 | tf_op jit(solution)/shard_map/chts,cthp->cshp/dot_general | solution.py:186
  95.4 4.4 %copy.168 = bf16[2,512,1280]{2,1,0:T(8,128)(2,1)} copy(bf16[2,512,1280]{1,2,0:T(8,128)(2,1)} %bitcast.113) | data formatting | bytes 5242880
  99.7 1.4 %maximum_select_fusion = bf16[8,40,8,128]{3,2,1,0:T(8,128)(2,1)S(1)} fusion(bf16[4,40,8,128]{3,2,1,0:T(8,128)(2,1)} %maximum_select_fusion.2, bf16[4,40,8,128]{3,2,1,0:T(8,128)(2,1)} %collective-permute-done.10, pred[]{:T(512)S(6)} %eq.23), kind=kLoop, calls=%fused_computation.34 | loop fusion | flops 983040 | bytes 1310721 | tf_op jit(solution)/shard_map/jit(_where)/select_n | solution.py:78
  101.3 0.8 copy.190
  102.1 0.6 convolution_add_fusion
  102.8 0.7 reshape.183
  103.5 0.8 fusion.27
  104.3 0.3 copy.183
  104.7 0.3 copy.184
  105.0 0.9 select_bitcast_fusion
  105.9 0.5 collective-permute-start.12
  106.4 2.6 %fusion.8 = f32[256,128]{0,1:T(8,128)S(1)} fusion(f32[256,40]{0,1:T(8,128)S(1)} %copy-done.15, bf16[256,40,64]{0,2,1:T(8,128)(2,1)} %bitcast.117, bf16[20,64,128]{2,1,0:T(8,128)(2,1)} %collective-permute-done.11, bf16[20,64,128]{2,1,0:T(8,128)(2,1)} %bitcast.104, pred[]{:T(512)S(6)} %eq.22), kind=kOutput, calls=%fused_computation.15 | convolution fusion | flops 171343872 | bytes 2138113 | tf_op jit(solution)/shard_map/jhp,hpn->jhn/dot_general | solution.py:208
  109.0 0.8 copy.167
  109.8 1.8 %fusion.16 = bf16[40,64,256]{2,1,0:T(8,128)(2,1)S(1)} fusion(f32[256,128]{0,1:T(8,128)S(1)} %copy-done.13, f32[256,40]{0,1:T(8,128)S(1)} %copy-done.15, bf16[20,64,128]{2,1,0:T(8,128)(2,1)} %collective-permute-done.11, bf16[20,64,128]{2,1,0:T(8,128)(2,1)} %bitcast.104, pred[]{:T(512)S(6)} %eq.22), kind=kOutput, calls=%fused_computation.27 | convolution fusion | flops 172032000 | bytes 2138113 | tf_op jit(solution)/shard_map/jhn,hpn->jhp/dot_general | solution.py:204
  111.6 1.6 %copy.166 = bf16[256,2560]{1,0:T(8,128)(2,1)} copy(bf16[256,2560]{0,1:T(8,128)(2,1)S(1)} %bitcast.118) | data formatting | bytes 2621440
  113.3 0.8 fusion.29
  (76 shorter events, 1.8 us)
Async XLA Ops:
  0.6 17.9 %copy-start = (bf16[2,512,128]{2,1,0:T(8,128)(2,1)S(1)}, bf16[2,512,128]{2,1,0:T(8,128)(2,1)}, u32[]{:S(2)}) copy-start(bf16[2,512,128]{2,1,0:T(8,128)(2,1)} %param.14) | copy-start | bytes 786436
  1.6 7.8 %collective-permute-start = (f32[40]{0:T(128)S(1)}, f32[40]{0:T(128)S(1)}, u32[]{:S(2)}, u32[]{:S(2)}) collective-permute-start(f32[40]{0:T(128)S(1)} %get-tuple-element.20), channel_id=1, source_target_pairs={{1,0},{2,1},{3,2},{4,3},{5,4},{6,5},{7,6},{8,7},{9,8},{10,9},{11,1... | collective-permute-start | bytes 488 | tf_op jit(solution)/shard_map/ppermute | solution.py:35
  3.7 10.7 %copy-start.16 = (f32[40,3]{0,1:T(4,128)}, f32[40,3]{0,1:T(4,128)S(1)}, u32[]{:S(2)}) copy-start(f32[40,3]{0,1:T(4,128)S(1)} %reduce-window.15) | copy-start | bytes 1444
  8.3 19.0 %copy-start.11 = (f32[2,20,512]{2,0,1:T(2,128)}, f32[2,20,512]{2,0,1:T(2,128)S(1)}, u32[]{:S(2)}) copy-start(f32[2,20,512]{2,0,1:T(2,128)S(1)} %exp.25) | copy-start | bytes 245764
  9.3 22.5 %copy-start.12 = (f32[256,128]{0,1:T(8,128)}, f32[256,128]{0,1:T(8,128)S(1)}, u32[]{:S(2)}) copy-start(f32[256,128]{0,1:T(8,128)S(1)} %copy.139) | copy-start | bytes 393220
  10.1 7.0 %collective-permute-start.1 = (f32[40]{0:T(128)S(1)}, f32[40]{0:T(128)S(1)}, u32[]{:S(2)}, u32[]{:S(2)}) collective-permute-start(f32[40]{0:T(128)S(1)} %add.64), channel_id=1, source_target_pairs={{2,0},{3,1},{4,2},{5,3},{6,4},{7,5},{8,6},{9,7},{10,8},{11,9},{12,... | collective-permute-start | bytes 488 | tf_op jit(solution)/shard_map/ppermute | solution.py:35
  14.4 4.1 %copy-start.9 = (bf16[2,512,128]{2,1,0:T(8,128)(2,1)S(1)}, bf16[2,512,128]{2,1,0:T(8,128)(2,1)}, u32[]{:S(2)}) copy-start(bf16[2,512,128]{2,1,0:T(8,128)(2,1)} %param.13) | copy-start | bytes 786436
  16.1 10.5 %copy-start.7 = (bf16[256,2560]{1,0:T(8,128)(2,1)S(1)}, bf16[256,2560]{1,0:T(8,128)(2,1)}, u32[]{:S(2)}) copy-start(bf16[256,2560]{1,0:T(8,128)(2,1)} %param.9) | copy-start | bytes 3932164
  17.1 14.6 %slice-start = ((f32[40,3]{0,1:T(4,128)}), f32[40,2]{0,1:T(2,128)S(1)}, s32[]{:S(2)}) async-start(f32[40,3]{0,1:T(4,128)} %copy-done.16), calls=%async_computation | async-start | bytes 2048 | tf_op jit(solution)/shard_map/slice.1
  17.2 8.2 %collective-permute-start.2 = (f32[40]{0:T(128)S(1)}, f32[40]{0:T(128)S(1)}, u32[]{:S(2)}, u32[]{:S(2)}) collective-permute-start(f32[40]{0:T(128)S(1)} %add.65), channel_id=1, source_target_pairs={{4,0},{5,1},{6,2},{7,3},{8,4},{9,5},{10,6},{11,7},{12,8},{13,9},{1... | collective-permute-start | bytes 488 | tf_op jit(solution)/shard_map/ppermute | solution.py:35
  25.4 6.3 %collective-permute-start.3 = (f32[40]{0:T(128)S(1)}, f32[40]{0:T(128)S(1)}, u32[]{:S(2)}, u32[]{:S(2)}) collective-permute-start(f32[40]{0:T(128)S(1)} %add.66), channel_id=1, source_target_pairs={{8,0},{9,1},{10,2},{11,3},{12,4},{13,5},{14,6},{15,7},{24,16},{25,... | collective-permute-start | bytes 488 | tf_op jit(solution)/shard_map/ppermute | solution.py:35
  27.3 5.7 %copy-start.8 = (bf16[256,2560]{0,1:T(8,128)(2,1)}, bf16[256,2560]{0,1:T(8,128)(2,1)S(1)}, u32[]{:S(2)}) copy-start(bf16[256,2560]{0,1:T(8,128)(2,1)S(1)} %copy.140) | copy-start | bytes 3932164
  31.8 1.2 %copy-start.14 = (f32[256,40]{0,1:T(8,128)}, f32[256,40]{0,1:T(8,128)S(1)}, u32[]{:S(2)}) copy-start(f32[256,40]{0,1:T(8,128)S(1)} %fusion.21) | copy-start | bytes 122884
  31.8 1.7 %copy-start.2 = (bf16[2,512,1280]{1,2,0:T(8,128)(2,1)S(1)}, bf16[2,512,1280]{1,2,0:T(8,128)(2,1)}, u32[]{:S(2)}) copy-start(bf16[2,512,1280]{1,2,0:T(8,128)(2,1)} %broadcast_select_fusion) | copy-start | bytes 7864324
  33.0 4.2 %collective-permute-start.4 = (f32[20,64,128]{2,1,0:T(8,128)S(1)}, f32[20,64,128]{2,1,0:T(8,128)S(1)}, u32[]{:S(2)}, u32[]{:S(2)}) collective-permute-start(f32[20,64,128]{2,1,0:T(8,128)S(1)} %slice_select_fusion.2), channel_id=1, source_target_pairs={{0,1},{1,0},{2,3},{3,2},{4,5},{5,4},{6,7},{7,6},{8,9},{9,8},{10,11... | collective-permute-start | bytes 1966088 | tf_op jit(solution)/shard_map/ppermute | solution.py:100
  38.6 16.9 %collective-permute-start.5 = (f32[4,40,8,128]{3,2,1,0:T(8,128)}, f32[4,40,8,128]{3,2,1,0:T(8,128)}, u32[]{:S(2)}, u32[]{:S(2)}) collective-permute-start(f32[4,40,8,128]{3,2,1,0:T(8,128)} %bitcast.18), channel_id=1, source_target_pairs={{0,2},{2,0},{4,6},{6,4},{8,10},{10,8},{12,14},{14,12},{1,3},{3,1},... | collective-permute-start | bytes 1966088 | tf_op jit(solution)/shard_map/ppermute | solution.py:65
  56.7 9.1 %collective-permute-start.6 = (f32[2,40,8,128]{3,2,1,0:T(8,128)S(1)}, f32[2,40,8,128]{3,2,1,0:T(8,128)S(1)}, u32[]{:S(2)}, u32[]{:S(2)}) collective-permute-start(f32[2,40,8,128]{3,2,1,0:T(8,128)S(1)} %slice_select_fusion.3), channel_id=1, source_target_pairs={{0,4},{2,6},{4,0},{6,2},{8,12},{10,14},{12,8},{14,10},{1,5},{3,7},... | collective-permute-start | bytes 983048 | tf_op jit(solution)/shard_map/ppermute | solution.py:65
  58.8 7.2 %copy-start.4 = (bf16[2,512,20,64]{1,3,2,0:T(8,128)(2,1)S(1)}, bf16[2,512,20,64]{1,3,2,0:T(8,128)(2,1)}, u32[]{:S(2)}) copy-start(bf16[2,512,20,64]{1,3,2,0:T(8,128)(2,1)} %get-tuple-element.60) | copy-start | bytes 7864324
  65.9 9.1 %collective-permute-start.7 = (f32[1,40,8,128]{3,2,1,0:T(8,128)S(1)}, f32[1,40,8,128]{3,2,1,0:T(8,128)S(1)}, u32[]{:S(2)}, u32[]{:S(2)}) collective-permute-start(f32[1,40,8,128]{3,2,1,0:T(8,128)S(1)} %slice_select_fusion.4), channel_id=1, source_target_pairs={{0,8},{2,10},{4,12},{6,14},{8,0},{10,2},{12,4},{14,6},{1,9},{3,11}... | collective-permute-start | bytes 491528 | tf_op jit(solution)/shard_map/ppermute | solution.py:65
  66.0 9.1 %copy-start.10 = (bf16[2,512,128]{2,1,0:T(8,128)(2,1)S(1)}, bf16[2,512,128]{2,1,0:T(8,128)(2,1)}, u32[]{:S(2)}) copy-start(bf16[2,512,128]{2,1,0:T(8,128)(2,1)} %param.13) | copy-start | bytes 786436
  75.0 5.4 %collective-permute-start.8 = (bf16[1,40,8,128]{3,2,1,0:T(8,128)(2,1)S(1)}, bf16[1,40,8,128]{3,2,1,0:T(8,128)(2,1)S(1)}, u32[]{:S(2)}, u32[]{:S(2)}) collective-permute-start(bf16[1,40,8,128]{3,2,1,0:T(8,128)(2,1)S(1)} %add_convert_fusion), channel_id=1, source_target_pairs={{0,8},{2,10},{4,12},{6,14},{8,0},{10,2},{12,4},{14,6},{1,9},{3,11}... | collective-permute-start | bytes 245768 | tf_op jit(solution)/shard_map/ppermute | solution.py:76
  75.1 12.9 %copy-start.5 = (f32[2,512,512]{2,1,0:T(8,128)S(1)}, f32[2,512,512]{2,1,0:T(8,128)}, u32[]{:S(2)}) copy-start(f32[2,512,512]{2,1,0:T(8,128)} %fusion.30) | copy-start | bytes 6291460
  76.4 11.6 %copy-start.3 = (bf16[2,512,1280]{1,2,0:T(8,128)(2,1)S(1)}, bf16[2,512,1280]{1,2,0:T(8,128)(2,1)}, u32[]{:S(2)}) copy-start(bf16[2,512,1280]{1,2,0:T(8,128)(2,1)} %broadcast_select_fusion) | copy-start | bytes 7864324
  80.4 5.4 %collective-permute-start.9 = (bf16[2,40,8,128]{3,2,1,0:T(8,128)(2,1)S(1)}, bf16[2,40,8,128]{3,2,1,0:T(8,128)(2,1)S(1)}, u32[]{:S(2)}, u32[]{:S(2)}) collective-permute-start(bf16[2,40,8,128]{3,2,1,0:T(8,128)(2,1)S(1)} %maximum_select_fusion.3), channel_id=1, source_target_pairs={{0,4},{2,6},{4,0},{6,2},{8,12},{10,14},{12,8},{14,10},{1,5},{3,7},... | collective-permute-start | bytes 491528 | tf_op jit(solution)/shard_map/ppermute | solution.py:76
  86.6 13.2 %collective-permute-start.10 = (bf16[4,40,8,128]{3,2,1,0:T(8,128)(2,1)}, bf16[4,40,8,128]{3,2,1,0:T(8,128)(2,1)}, u32[]{:S(2)}, u32[]{:S(2)}) collective-permute-start(bf16[4,40,8,128]{3,2,1,0:T(8,128)(2,1)} %maximum_select_fusion.2), channel_id=1, source_target_pairs={{0,2},{2,0},{4,6},{6,4},{8,10},{10,8},{12,14},{14,12},{1,3},{3,1},... | collective-permute-start | bytes 983048 | tf_op jit(solution)/shard_map/ppermute | solution.py:76
  101.2 1.5 %copy-start.6 = (f32[2,512,128]{1,2,0:T(8,128)S(1)}, f32[2,512,128]{1,2,0:T(8,128)}, u32[]{:S(2)}) copy-start(f32[2,512,128]{1,2,0:T(8,128)} %fusion.33) | copy-start | bytes 1572868
  102.1 4.3 %collective-permute-start.11 = (bf16[20,64,128]{2,1,0:T(8,128)(2,1)}, bf16[20,64,128]{2,1,0:T(8,128)(2,1)}, u32[]{:S(2)}, u32[]{:S(2)}) collective-permute-start(bf16[20,64,128]{2,1,0:T(8,128)(2,1)} %bitcast.104), channel_id=1, source_target_pairs={{0,1},{1,0},{2,3},{3,2},{4,5},{5,4},{6,7},{7,6},{8,9},{9,8},{10,11... | collective-permute-start | bytes 983048 | tf_op jit(solution)/shard_map/ppermute | solution.py:100
  103.5 2.9 %copy-start.15 = (f32[256,40]{0,1:T(8,128)S(1)}, f32[256,40]{0,1:T(8,128)}, u32[]{:S(2)}) copy-start(f32[256,40]{0,1:T(8,128)} %copy-done.14) | copy-start | bytes 122884
  105.9 3.9 %copy-start.13 = (f32[256,128]{0,1:T(8,128)S(1)}, f32[256,128]{0,1:T(8,128)}, u32[]{:S(2)}) copy-start(f32[256,128]{0,1:T(8,128)} %copy-done.12) | copy-start | bytes 393220
  105.9 7.3 %collective-permute-start.12 = (f32[2,256,256]{2,1,0:T(8,128)}, f32[2,256,256]{2,1,0:T(8,128)S(1)}, u32[]{:S(2)}, u32[]{:S(2)}) collective-permute-start(f32[2,256,256]{2,1,0:T(8,128)} %select_bitcast_fusion), channel_id=1, source_target_pairs={{0,1},{1,0},{2,3},{3,2},{4,5},{5,4},{6,7},{7,6},{8,9},{9,8},{10,11... | collective-permute-start | bytes 1572872 | tf_op jit(solution)/shard_map/ppermute | solution.py:100
  111.6 2.5 %copy-start.1 = (bf16[2,512,128]{2,1,0:T(8,128)(2,1)S(1)}, bf16[2,512,128]{2,1,0:T(8,128)(2,1)}, u32[]{:S(2)}) copy-start(bf16[2,512,128]{2,1,0:T(8,128)(2,1)} %param.14) | copy-start | bytes 786436

commit v9 on v8

--- a/solution.py
+++ b/solution.py
@@ -30,8 +30,8 @@
     while step < count:
         back = [(at, at - step) for at in range(step, count)]
         if rounds < len(works):
-            fn, args = works[rounds]
-            value, args = lax.optimization_barrier((value, args))
+            fn, pick = works[rounds]
+            value, args = lax.optimization_barrier((value, pick(done)))
         value = value + lax.ppermute(value, axis, back)
         if rounds < len(works):
             value, piece = lax.optimization_barrier((value, fn(*args)))
@@ -117,20 +117,33 @@
         level_all = jnp.cumsum(jnp.log1p(-code_cand.astype(jnp.float32) * 1e-06), axis=1)
         return jnp.exp(level_all), jnp.exp(-level_all)
 
-    def g_work(dy_cand, lengths):
+    def g_work(dy_cand, lengths, amplitude, c_cand):
         valid_rows = position[None, :] < lengths[:, None] * BLOCK
         g_cand = jnp.where(valid_rows[:, :, None], dy_cand, jnp.zeros_like(dy_cand))
-        return g_cand.reshape(cand_dev, cand_len, half_heads, head_size)
-
-    def scores_work(c_cand, b_cand):
-        return jnp.einsum("ctn,csn->cts", c_cand, b_cand, preferred_element_type=jnp.float32)
-
-    inclusive, (levels, g_heads, scores) = suffix_sum(
+        g_heads = g_cand.reshape(cand_dev, cand_len, half_heads, head_size)
+        scaled_g = g_heads.astype(jnp.float32) * amplitude[:, :, :, None]
+        decayed_g, g_low = split_bf16(scaled_g)
+        dstate = jnp.einsum("cthp,ctn->hpn", decayed_g, c_cand, preferred_element_type=jnp.float32)
+        return g_heads, decayed_g, g_low, dstate
+
+    def x_work(x_cand, inverse, c_cand, b_cand):
+        xc_heads = x_cand.reshape(cand_dev, cand_len, half_heads, head_size)
+        x_high, x_low = split_bf16(xc_heads.astype(jnp.float32) * inverse[:, :, :, None])
+        scores = jnp.einsum("ctn,csn->cts", c_cand, b_cand, preferred_element_type=jnp.float32)
+        return x_high, x_low, scores
+
+    inclusive, (levels, g_parts, x_parts) = suffix_sum(
         own_total,
         pre_axes,
-        [(level_work, (code_cand,)), (g_work, (dy_cand, lengths)), (scores_work, (c_cand, b_cand))],
+        [
+            (level_work, lambda done: (code_cand,)),
+            (g_work, lambda done: (dy_cand, lengths, done[0][0], c_cand)),
+            (x_work, lambda done: (x_cand, done[0][1], c_cand, b_cand)),
+        ],
     )
     amplitude, inverse = levels
+    g_heads, decayed_g, g_low, dstate = g_parts
+    x_high, x_low, scores = x_parts
     later_total = inclusive - own_total
     after_local = own_total[None, :] - jnp.cumsum(log_prefix, axis=0)
     weight = jnp.exp(after_local + later_total[None, :])
@@ -146,14 +159,8 @@
     give_half = jnp.where(mine_first, state_halves[1], state_halves[0])
     init_local = own_half + other_core(give_half)
 
-    xc_heads = x_cand.reshape(cand_dev, cand_len, half_heads, head_size)
-    scaled_g = g_heads.astype(jnp.float32) * amplitude[:, :, :, None]
-    decayed_g, g_low = split_bf16(scaled_g)
-    x_high, x_low = split_bf16(xc_heads.astype(jnp.float32) * inverse[:, :, :, None])
-
-    dstate = jnp.einsum("cthp,ctn->hpn", decayed_g, c_cand, preferred_element_type=jnp.float32)
-    both = cand_sum_bf16(jnp.concatenate([init_local, dstate], axis=0))
-    init_half, grad_half = both[:half_heads], both[half_heads:]
+    grad_half = cand_sum_bf16(dstate)
+    init_half = cand_sum_bf16(init_local)
     grad_other = other_core(grad_half)
     grad_state = jnp.where(
         mine_first,

time: 115 us -> 114 us (level)
  starting transfers between devices: 11 us -> 26 us
  waiting for transfers between devices: 34.5 us -> 20.6 us
  matrix products: 23.9 us -> 21.4 us
    ppermute x4, waiting for transfers between devices: 10.4 us -> 0.01 us  [suffix_sum(): value = value + lax.ppermute(value, axis, back)]
    ppermute x3 -> x6, starting transfers between devices: 3.6 us -> 13.9 us  [halving_scatter(): lax.ppermute(give, axis, [(at, at ^ step) for at in range(count)])]
    ppermute x3 -> x6, starting transfers between devices: 1.59 us -> 6.54 us  [doubling_gather(): other = lax.ppermute(value, axis, [(at, at ^ step) for at in range(count)])]
    optimization_barrier x3 -> x4, local copies, waits for them, and re-layouts: 3.92 us -> 8.09 us  [suffix_sum(): value, args = lax.optimization_barrier((value, pick(done)))]
    unnamed x41 -> x44, local copies, waits for them, and re-layouts: 13 us -> 9.33 us
    ppermute x3 -> x6, waiting for transfers between devices: 16.6 us -> 13.9 us  [halving_scatter(): lax.ppermute(give, axis, [(at, at ^ step) for at in range(count)])]
    select_n x1, other arithmetic: 1.67 us -> 0.18 us  [g_work(): g_cand = jnp.where(valid_rows[:, :, None], dy_cand, jnp.zeros_like(dy_cand))]
    add x3, other arithmetic: 0.01 us -> 1.49 us  [suffix_sum(): value = value + lax.ppermute(value, axis, back)]
  transfers between devices with their start and end apart: 13 -> 19, of which waited for: 8 -> 8; matrix products, arithmetic and copies ran while one was open for 50% -> 54% of each run, Pallas kernels for 0% -> 0%
where the time goes in v9:
time: 114 us; the launch traced here: 113 us
  starting transfers between devices  26 us (23%)
  local copies, waits for them, and re-layouts  25.2 us (22%)
  matrix products  21.4 us (19%)
  waiting for transfers between devices  20.6 us (18%)
  other arithmetic  18.4 us (16%)
  between operations  1.37 us (1%)
    ppermute x6, waiting for transfers between devices, halving_scatter(): lax.ppermute(give, axis, [(at, at ^ step) for at in range(count)])  13.9 us
    ppermute x6, starting transfers between devices, halving_scatter(): lax.ppermute(give, axis, [(at, at ^ step) for at in range(count)])  13.9 us
    unnamed x44, local copies, waits for them, and re-layouts  9.33 us
    optimization_barrier x4, local copies, waits for them, and re-layouts, suffix_sum(): value, args = lax.optimization_barrier((value, pick(done)))  8.09 us
    ppermute x6, waiting for transfers between devices, doubling_gather(): other = lax.ppermute(value, axis, [(at, at ^ step) for at in range(count)])  6.68 us
    ppermute x6, starting transfers between devices, doubling_gather(): other = lax.ppermute(value, axis, [(at, at ^ step) for at in range(count)])  6.54 us
    dot_general x1, matrix products, shards(): jnp.einsum('chts,cthp->cshp', kernel, g_heads, preferred_element_type=jnp...  6.54 us
    convert_element_type x2, other arithmetic, split_bf16(): low = (value - high).astype(jnp.bfloat16)  5.76 us
  transfers between devices with their start and end apart: 19, of which 8 were waited for; matrix products, arithmetic and copies ran while one was open for 54% of the time, Pallas kernels for 0%

profile of v9, /device:TPU:0, one launch (start us, length us, event | category | flops | bytes accessed | tf_op | source)
XLA Modules:
  0.0 113.0 jit_solution(3468982895772900733)
XLA Ops:
  0.7 1.0 fusion.23
  1.7 1.3 %collective-permute-start = (f32[40]{0:T(128)S(1)}, f32[40]{0:T(128)S(1)}, u32[]{:S(2)}, u32[]{:S(2)}) collective-permute-start(f32[40]{0:T(128)S(1)} %get-tuple-element.29), channel_id=1, source_target_pairs={{1,0},{2,1},{3,2},{4,3},{5,4},{6,5},{7,6},{8,7},{9,8},{10,9},{11,1... | collective-permute-start | bytes 488 | tf_op jit(solution)/shard_map/ppermute | solution.py:35
  3.2 0.6 reduce-window.16
  4.0 1.0 log-plus-one_bitcast_fusion
  5.1 2.3 %reduce-window.14 = f32[2,20,4,128]{3,1,2,0:T(8,128)S(1)} reduce-window(f32[2,20,4,128]{3,1,2,0:T(8,128)S(1)} %copy.140, f32[]{:T(128)} %constant.108.clone.1), window={size=1x1x1x128 pad=0_0x0_0x0_0x127_0}, to_apply=%region_1.0 | reduce-window | flops 2600960 | bytes 163844 | tf_op jit(solution)/shard_map/reduce-window
  8.0 1.6 %copy.154 = f32[256,128]{0,1:T(8,128)} copy(bf16[256,128]{1,0:T(8,128)(2,1)} %param.10) | data formatting | bytes 196608 | tf_op jit(solution)/shard_map/convert_element_type | solution.py:150
  9.6 1.4 %copy.156 = bf16[256,2560]{0,1:T(8,128)(2,1)} copy(bf16[256,2560]{1,0:T(8,128)(2,1)S(1)} %copy-done.5) | data formatting | bytes 2621440 | tf_op args[0]
  11.1 1.3 %collective-permute-start.1 = (f32[40]{0:T(128)S(1)}, f32[40]{0:T(128)S(1)}, u32[]{:S(2)}, u32[]{:S(2)}) collective-permute-start(f32[40]{0:T(128)S(1)} %add.79), channel_id=1, source_target_pairs={{2,0},{3,1},{4,2},{5,3},{6,4},{7,5},{8,6},{9,7},{10,8},{11,9},{12,... | collective-permute-start | bytes 488 | tf_op jit(solution)/shard_map/ppermute | solution.py:35
  12.5 3.0 %copy.143 = bf16[2,512,1280]{1,2,0:T(8,128)(2,1)S(1)} copy(bf16[2,512,1280]{2,1,0:T(8,128)(2,1)} %param.17) | data formatting | bytes 5242880 | tf_op jit(solution)/shard_map/optimization_barrier | solution.py:34
  15.7 2.8 %fusion.6 = (bf16[2,512,20,64]{1,3,2,0:T(8,128)(2,1)}, bf16[2,512,20,64]{1,3,2,0:T(8,128)(2,1)S(1)}) fusion(bf16[2,512,20,64]{1,3,2,0:T(8,128)(2,1)S(1)} %bitcast.123, f32[2,512,20]{1,2,0:T(8,128)S(1)} %copy.144), kind=kLoop, calls=%fused_computation.11 | loop fusion | flops 7864320 | bytes 7946240 | tf_op jit(solution)/shard_map/convert_element_type | solution.py:11
  18.4 0.8 convolution_bitcast_fusion
  19.3 0.7 copy.158
  19.9 0.7 copy.157
  20.6 0.6 add.80
  21.3 1.3 %collective-permute-start.9 = (f32[40]{0:T(128)}, f32[40]{0:T(128)}, u32[]{:S(2)}, u32[]{:S(2)}) collective-permute-start(f32[40]{0:T(128)} %add.80), channel_id=1, source_target_pairs={{4,0},{5,1},{6,2},{7,3},{8,4},{9,5},{10,6},{11,7},{12,8},{13,9},{1... | collective-permute-start | bytes 488 | tf_op jit(solution)/shard_map/ppermute | solution.py:35
  22.6 0.7 copy.153
  23.3 0.8 copy.147
  24.0 4.2 %collective-permute-start.2 = (f32[4,20,8,128]{3,2,1,0:T(8,128)}, f32[4,20,8,128]{3,2,1,0:T(8,128)}, u32[]{:S(2)}, u32[]{:S(2)}) collective-permute-start(f32[4,20,8,128]{3,2,1,0:T(8,128)} %bitcast.14), channel_id=1, source_target_pairs={{0,2},{2,0},{4,6},{6,4},{8,10},{10,8},{12,14},{14,12},{1,3},{3,1},... | collective-permute-start | bytes 983048 | tf_op jit(solution)/shard_map/ppermute | solution.py:65
  28.2 4.4 %copy.152 = bf16[2,512,1280]{1,2,0:T(8,128)(2,1)} copy(bf16[2,512,1280]{2,1,0:T(8,128)(2,1)} %param.12) | data formatting | bytes 5242880 | tf_op jit(solution)/shard_map/optimization_barrier | solution.py:34
  32.7 3.0 %fusion.7 = (bf16[2,512,20,64]{1,3,2,0:T(8,128)(2,1)S(1)}, bf16[2,512,20,64]{1,3,2,0:T(8,128)(2,1)S(1)}) fusion(bf16[2,512,20,64]{1,3,2,0:T(8,128)(2,1)} %bitcast.125, f32[2,512,20]{1,2,0:T(8,128)} %copy.153), kind=kLoop, calls=%fused_computation.12 | loop fusion | flops 7864320 | bytes 7946240 | tf_op jit(solution)/shard_map/convert_element_type | solution.py:11
  35.7 0.4 fusion.29
  36.1 0.9 add.84
  37.1 1.5 %collective-permute-start.10 = (f32[40]{0:T(128)S(1)}, f32[40]{0:T(128)S(1)}, u32[]{:S(2)}, u32[]{:S(2)}) collective-permute-start(f32[40]{0:T(128)S(1)} %add.84), channel_id=1, source_target_pairs={{8,0},{9,1},{10,2},{11,3},{12,4},{13,5},{14,6},{15,7},{24,16},{25,... | collective-permute-start | bytes 488 | tf_op jit(solution)/shard_map/ppermute | solution.py:35
  38.6 6.5 %fusion.15 = bf16[2,20,64,512]{3,2,1,0:T(8,128)(2,1)} fusion(bf16[2,512,20,64]{1,3,2,0:T(8,128)(2,1)S(1)} %bitcast.124, f32[2,20,512]{2,1,0:T(8,128)S(1)} %copy-done.13, f32[2,20,512]{2,1,0:T(8,128)S(1)} %copy-done.14, f32[2,512,512]{2,1,0:T(8,128)S(1)} %fusion.29, pred[512,512]{1,0:T(8,128)(4,1)S(1)} %iota_compare_fusion), kind=kOutput, calls=%fused_computation.26 | convolution fusion | flops 1385431040 | bytes 7766016 | tf_op jit(solution)/shard_map/chts,cthp->cshp/dot_general | solution.py:193
  45.1 1.6 %fusion.30 = f32[2,512,512]{2,1,0:T(8,128)S(1)} fusion(bf16[2,512,1280]{1,2,0:T(8,128)(2,1)S(1)} %bitcast.120, bf16[2,512,1280]{1,2,0:T(8,128)(2,1)S(1)} %bitcast.127), kind=kOutput, calls=%fused_computation.83 | convolution fusion | flops 1342177280 | bytes 7340032 | tf_op jit(solution)/shard_map/ctk,csk->cts/dot_general | solution.py:175
  46.9 1.0 fusion.17
  48.3 1.0 bitcast_add_fusion.2
  49.3 3.4 %collective-permute-start.3 = (f32[2,20,8,128]{3,2,1,0:T(8,128)S(1)}, f32[2,20,8,128]{3,2,1,0:T(8,128)S(1)}, u32[]{:S(2)}, u32[]{:S(2)}) collective-permute-start(f32[2,20,8,128]{3,2,1,0:T(8,128)S(1)} %slice_select_fusion.6), channel_id=1, source_target_pairs={{0,4},{2,6},{4,0},{6,2},{8,12},{10,14},{12,8},{14,10},{1,5},{3,7},... | collective-permute-start | bytes 491528 | tf_op jit(solution)/shard_map/ppermute | solution.py:65
  52.7 1.6 %fusion.31 = f32[2,512,512]{2,1,0:T(8,128)S(1)} fusion(bf16[2,512,1280]{1,2,0:T(8,128)(2,1)S(1)} %bitcast.121, bf16[2,512,1280]{1,2,0:T(8,128)(2,1)S(1)} %bitcast.131), kind=kOutput, calls=%fused_computation.84 | convolution fusion | flops 1342177280 | bytes 7340032 | tf_op jit(solution)/shard_map/ctk,csk->cts/dot_general | solution.py:175
  54.3 3.3 %collective-permute-done.3 = f32[2,20,8,128]{3,2,1,0:T(8,128)S(1)} collective-permute-done((f32[2,20,8,128]{3,2,1,0:T(8,128)S(1)}, f32[2,20,8,128]{3,2,1,0:T(8,128)S(1)}, u32[]{:S(2)}, u32[]{:S(2)}) %collective-permute-start.3) | collective-permute-done | bytes 163872 | tf_op jit(solution)/shard_map/ppermute | solution.py:65
  57.6 3.7 %collective-permute-start.4 = (f32[1,20,8,128]{3,2,1,0:T(8,128)S(1)}, f32[1,20,8,128]{3,2,1,0:T(8,128)S(1)}, u32[]{:S(2)}, u32[]{:S(2)}) collective-permute-start(f32[1,20,8,128]{3,2,1,0:T(8,128)S(1)} %slice_select_fusion.8), channel_id=1, source_target_pairs={{0,8},{2,10},{4,12},{6,14},{8,0},{10,2},{12,4},{14,6},{1,9},{3,11}... | collective-permute-start | bytes 245768 | tf_op jit(solution)/shard_map/ppermute | solution.py:65
  61.6 0.6 collective-permute-start.12
  62.2 1.8 %add_select_fusion = f32[2,512,512]{2,1,0:T(8,128)S(1)} fusion(f32[2,512,512]{2,1,0:T(8,128)S(1)} %fusion.30, f32[2,512,512]{2,1,0:T(8,128)S(1)} %fusion.31, bf16[2,512,1280]{1,2,0:T(8,128)(2,1)S(1)} %bitcast.126, bf16[2,512,1280]{1,2,0:T(8,128)(2,1)S(1)} %bitcast.128, pred[512,512]{1,0:T(8,128)(4,1)S(1)} %iota_compare_fusion), kind=kOutput, calls=%fused_computation.25 | convolution fusion | flops 1343750144 | bytes 11796480 | tf_op jit(solution)/shard_map/ctk,csk->cts/dot_general | solution.py:175
  64.0 1.6 %collective-permute-done.4 = f32[1,20,8,128]{3,2,1,0:T(8,128)S(1)} collective-permute-done((f32[1,20,8,128]{3,2,1,0:T(8,128)S(1)}, f32[1,20,8,128]{3,2,1,0:T(8,128)S(1)}, u32[]{:S(2)}, u32[]{:S(2)}) %collective-permute-start.4) | collective-permute-done | bytes 81952 | tf_op jit(solution)/shard_map/ppermute | solution.py:65
  65.6 1.1 collective-permute-start.5
  66.7 4.1 %collective-permute-done.12 = f32[4,20,8,128]{3,2,1,0:T(8,128)S(1)} collective-permute-done((f32[4,20,8,128]{3,2,1,0:T(8,128)S(1)}, f32[4,20,8,128]{3,2,1,0:T(8,128)S(1)}, u32[]{:S(2)}, u32[]{:S(2)}) %collective-permute-start.12) | collective-permute-done | bytes 327712 | tf_op jit(solution)/shard_map/ppermute | solution.py:65
  71.0 1.6 %collective-permute-start.13 = (f32[2,20,8,128]{3,2,1,0:T(8,128)S(1)}, f32[2,20,8,128]{3,2,1,0:T(8,128)S(1)}, u32[]{:S(2)}, u32[]{:S(2)}) collective-permute-start(f32[2,20,8,128]{3,2,1,0:T(8,128)S(1)} %slice_select_fusion.5), channel_id=1, source_target_pairs={{0,4},{2,6},{4,0},{6,2},{8,12},{10,14},{12,8},{14,10},{1,5},{3,7},... | collective-permute-start | bytes 491528 | tf_op jit(solution)/shard_map/ppermute | solution.py:65
  72.6 1.3 %fusion.33 = f32[2,512,128]{1,2,0:T(8,128)S(1)} fusion(f32[2,512,512]{2,1,0:T(8,128)S(1)} %add_select_fusion, bf16[2,512,128]{2,1,0:T(8,128)(2,1)S(1)} %copy-done.8), kind=kOutput, calls=%fused_computation.86 | convolution fusion | flops 805306368 | bytes 2883584 | tf_op jit(solution)/shard_map/cts,csn->ctn/dot_general | solution.py:185
  73.9 0.6 collective-permute-start.6
  74.4 2.8 %collective-permute-done.13 = f32[2,20,8,128]{3,2,1,0:T(8,128)S(1)} collective-permute-done((f32[2,20,8,128]{3,2,1,0:T(8,128)S(1)}, f32[2,20,8,128]{3,2,1,0:T(8,128)S(1)}, u32[]{:S(2)}, u32[]{:S(2)}) %collective-permute-start.13) | collective-permute-done | bytes 163872 | tf_op jit(solution)/shard_map/ppermute | solution.py:65
  77.3 0.4 collective-permute-start.14
  77.6 1.6 %collective-permute-done.6 = bf16[2,20,8,128]{3,2,1,0:T(8,128)(2,1)S(1)} collective-permute-done((bf16[2,20,8,128]{3,2,1,0:T(8,128)(2,1)S(1)}, bf16[2,20,8,128]{3,2,1,0:T(8,128)(2,1)S(1)}, u32[]{:S(2)}, u32[]{:S(2)}) %collective-permute-start.6) | collective-permute-done | bytes 81952 | tf_op jit(solution)/shard_map/ppermute | solution.py:76
  79.2 0.7 maximum_select_fusion.3
  79.9 0.6 collective-permute-start.7
  80.5 2.2 %collective-permute-done.14 = f32[1,20,8,128]{3,2,1,0:T(8,128)S(1)} collective-permute-done((f32[1,20,8,128]{3,2,1,0:T(8,128)S(1)}, f32[1,20,8,128]{3,2,1,0:T(8,128)S(1)}, u32[]{:S(2)}, u32[]{:S(2)}) %collective-permute-start.14) | collective-permute-done | bytes 81952 | tf_op jit(solution)/shard_map/ppermute | solution.py:65
  82.7 0.4 collective-permute-start.15
  83.2 1.7 %fusion.32 = f32[2,512,128]{1,2,0:T(8,128)} fusion(f32[2,512,512]{2,1,0:T(8,128)S(1)} %add_select_fusion, bf16[2,512,128]{2,1,0:T(8,128)(2,1)S(1)} %copy-done), kind=kOutput, calls=%fused_computation.85 | convolution fusion | flops 805306368 | bytes 2883584 | tf_op jit(solution)/shard_map/cts,ctn->csn/dot_general | solution.py:182
  84.9 4.4 %copy.179 = bf16[2,512,1280]{2,1,0:T(8,128)(2,1)} copy(bf16[2,512,1280]{1,2,0:T(8,128)(2,1)} %bitcast.130) | data formatting | bytes 5242880
  89.2 3.2 %collective-permute-start.16 = (bf16[2,20,8,128]{3,2,1,0:T(8,128)(2,1)S(1)}, bf16[2,20,8,128]{3,2,1,0:T(8,128)(2,1)S(1)}, u32[]{:S(2)}, u32[]{:S(2)}) collective-permute-start(bf16[2,20,8,128]{3,2,1,0:T(8,128)(2,1)S(1)} %maximum_select_fusion.8), channel_id=1, source_target_pairs={{0,4},{2,6},{4,0},{6,2},{8,12},{10,14},{12,8},{14,10},{1,5},{3,7},... | collective-permute-start | bytes 245768 | tf_op jit(solution)/shard_map/ppermute | solution.py:76
  92.4 1.2 %maximum_select_fusion.1 = bf16[8,20,8,128]{3,2,1,0:T(8,128)(2,1)S(1)} fusion(bf16[4,20,8,128]{3,2,1,0:T(8,128)(2,1)} %maximum_select_fusion.3, bf16[4,20,8,128]{3,2,1,0:T(8,128)(2,1)} %collective-permute-done.7, pred[]{:T(512)S(6)} %eq.35), kind=kLoop, calls=%fused_computation.38 | loop fusion | flops 491520 | bytes 655361 | tf_op jit(solution)/shard_map/jit(_where)/select_n | solution.py:78
  93.7 1.2 %collective-permute-done.16 = bf16[2,20,8,128]{3,2,1,0:T(8,128)(2,1)S(1)} collective-permute-done((bf16[2,20,8,128]{3,2,1,0:T(8,128)(2,1)S(1)}, bf16[2,20,8,128]{3,2,1,0:T(8,128)(2,1)S(1)}, u32[]{:S(2)}, u32[]{:S(2)}) %collective-permute-start.16) | collective-permute-done | bytes 81952 | tf_op jit(solution)/shard_map/ppermute | solution.py:76
  94.9 0.6 collective-permute-start.17
  95.5 0.8 copy_bitcast_fusion
  96.4 3.9 %collective-permute-done.17 = bf16[4,20,8,128]{3,2,1,0:T(8,128)(2,1)S(1)} collective-permute-done((bf16[4,20,8,128]{3,2,1,0:T(8,128)(2,1)S(1)}, bf16[4,20,8,128]{3,2,1,0:T(8,128)(2,1)S(1)}, u32[]{:S(2)}, u32[]{:S(2)}) %collective-permute-start.17) | collective-permute-done | bytes 163872 | tf_op jit(solution)/shard_map/ppermute | solution.py:76
  100.4 0.6 convolution_add_fusion
  101.4 0.7 reshape.220
  102.1 0.8 fusion.27
  103.6 0.9 select_bitcast_fusion
  104.6 2.2 %fusion.8 = f32[256,128]{0,1:T(8,128)S(1)} fusion(f32[256,40]{0,1:T(8,128)S(1)} %fusion.21, bf16[256,40,64]{0,2,1:T(8,128)(2,1)S(1)} %bitcast.135, bf16[20,64,128]{2,1,0:T(8,128)(2,1)} %collective-permute-done.8, bf16[20,64,128]{2,1,0:T(8,128)(2,1)} %copy_bitcast_fusion, pred[]{:T(512)S(6)} %eq.34), kind=kOutput, calls=%fused_computation.15 | convolution fusion | flops 171343872 | bytes 2138113 | tf_op jit(solution)/shard_map/jhp,hpn->jhn/dot_general | solution.py:215
  106.8 0.8 copy.178
  107.6 1.8 %fusion.16 = bf16[40,64,256]{2,1,0:T(8,128)(2,1)S(1)} fusion(f32[256,128]{0,1:T(8,128)S(1)} %copy-done.12, f32[256,40]{0,1:T(8,128)S(1)} %fusion.21, bf16[20,64,128]{2,1,0:T(8,128)(2,1)} %collective-permute-done.8, bf16[20,64,128]{2,1,0:T(8,128)(2,1)} %copy_bitcast_fusion, pred[]{:T(512)S(6)} %eq.34), kind=kOutput, calls=%fused_computation.27 | convolution fusion | flops 172032000 | bytes 2138113 | tf_op jit(solution)/shard_map/jhn,hpn->jhp/dot_general | solution.py:211
  109.4 1.6 %copy.177 = bf16[256,2560]{1,0:T(8,128)(2,1)} copy(bf16[256,2560]{0,1:T(8,128)(2,1)S(1)} %bitcast.136) | data formatting | bytes 2621440
  111.0 1.1 %bitcast_add_fusion = f32[2,256,256]{2,1,0:T(8,128)S(1)} fusion(f32[2,256,256]{2,1,0:T(8,128)} %collective-permute-done.18, f32[2,1,256,256]{3,2,0,1:T(8,128)S(1)} %copy.194, f32[2,1,256,256]{3,2,0,1:T(8,128)S(1)} %copy.195, pred[]{:T(512)S(6)} %eq.34), kind=kLoop, calls=%fused_computation.36 | loop fusion | flops 262144 | bytes 2097153 | tf_op jit(solution)/shard_map/add | solution.py:206
  112.2 0.8 fusion.28
  (103 shorter events, 3.7 us)
Async XLA Ops:
  0.6 17.8 %copy-start = (bf16[2,512,128]{2,1,0:T(8,128)(2,1)S(1)}, bf16[2,512,128]{2,1,0:T(8,128)(2,1)}, u32[]{:S(2)}) copy-start(bf16[2,512,128]{2,1,0:T(8,128)(2,1)} %param.14) | copy-start | bytes 786436
  0.6 9.0 %copy-start.5 = (bf16[256,2560]{1,0:T(8,128)(2,1)S(1)}, bf16[256,2560]{1,0:T(8,128)(2,1)}, u32[]{:S(2)}) copy-start(bf16[256,2560]{1,0:T(8,128)(2,1)} %param.9) | copy-start | bytes 3932164
  1.7 9.4 %copy-start.15 = (f32[40]{0:T(128)}, f32[40]{0:T(128)S(1)}, u32[]{:S(2)}) copy-start(f32[40]{0:T(128)S(1)} %get-tuple-element.29) | copy-start | bytes 484
  1.7 9.4 %copy-start.18 = (s32[2]{0:T(128)S(1)}, s32[2]{0:T(128)}, u32[]{:S(2)}) copy-start(s32[2]{0:T(128)} %param.16) | copy-start | bytes 28
  1.7 9.3 %collective-permute-start = (f32[40]{0:T(128)S(1)}, f32[40]{0:T(128)S(1)}, u32[]{:S(2)}, u32[]{:S(2)}) collective-permute-start(f32[40]{0:T(128)S(1)} %get-tuple-element.29), channel_id=1, source_target_pairs={{1,0},{2,1},{3,2},{4,3},{5,4},{6,5},{7,6},{8,7},{9,8},{10,9},{11,1... | collective-permute-start | bytes 488 | tf_op jit(solution)/shard_map/ppermute | solution.py:35
  3.8 1.3 %copy-start.9 = (f32[40,2,128]{2,0,1:T(8,128)}, f32[40,2,128]{2,0,1:T(8,128)S(1)}, u32[]{:S(2)}) copy-start(f32[40,2,128]{2,0,1:T(8,128)S(1)} %reduce-window.16) | copy-start | bytes 122884
  4.0 3.7 %copy-start.17 = (f32[40,3]{0,1:T(4,128)}, f32[40,3]{0,1:T(4,128)S(1)}, u32[]{:S(2)}) copy-start(f32[40,3]{0,1:T(4,128)S(1)} %reduce-window.19) | copy-start | bytes 1444
  11.1 9.4 %collective-permute-start.1 = (f32[40]{0:T(128)S(1)}, f32[40]{0:T(128)S(1)}, u32[]{:S(2)}, u32[]{:S(2)}) collective-permute-start(f32[40]{0:T(128)S(1)} %add.79), channel_id=1, source_target_pairs={{2,0},{3,1},{4,2},{5,3},{6,4},{7,5},{8,6},{9,7},{10,8},{11,9},{12,... | collective-permute-start | bytes 488 | tf_op jit(solution)/shard_map/ppermute | solution.py:35
  15.6 2.8 %copy-start.1 = (bf16[2,512,1280]{1,2,0:T(8,128)(2,1)}, bf16[2,512,1280]{1,2,0:T(8,128)(2,1)S(1)}, u32[]{:S(2)}) copy-start(bf16[2,512,1280]{1,2,0:T(8,128)(2,1)S(1)} %broadcast_select_fusion) | copy-start | bytes 7864324
  21.3 14.8 %collective-permute-start.9 = (f32[40]{0:T(128)}, f32[40]{0:T(128)}, u32[]{:S(2)}, u32[]{:S(2)}) collective-permute-start(f32[40]{0:T(128)} %add.80), channel_id=1, source_target_pairs={{4,0},{5,1},{6,2},{7,3},{8,4},{9,5},{10,6},{11,7},{12,8},{13,9},{1... | collective-permute-start | bytes 488 | tf_op jit(solution)/shard_map/ppermute | solution.py:35
  24.0 24.3 %collective-permute-start.2 = (f32[4,20,8,128]{3,2,1,0:T(8,128)}, f32[4,20,8,128]{3,2,1,0:T(8,128)}, u32[]{:S(2)}, u32[]{:S(2)}) collective-permute-start(f32[4,20,8,128]{3,2,1,0:T(8,128)} %bitcast.14), channel_id=1, source_target_pairs={{0,2},{2,0},{4,6},{6,4},{8,10},{10,8},{12,14},{14,12},{1,3},{3,1},... | collective-permute-start | bytes 983048 | tf_op jit(solution)/shard_map/ppermute | solution.py:65
  32.7 3.0 %copy-start.8 = (bf16[2,512,128]{2,1,0:T(8,128)(2,1)S(1)}, bf16[2,512,128]{2,1,0:T(8,128)(2,1)}, u32[]{:S(2)}) copy-start(bf16[2,512,128]{2,1,0:T(8,128)(2,1)} %param.13) | copy-start | bytes 786436
  32.7 5.9 %copy-start.13 = (f32[2,20,512]{2,1,0:T(8,128)S(1)}, f32[2,20,512]{2,1,0:T(8,128)}, u32[]{:S(2)}) copy-start(f32[2,20,512]{2,1,0:T(8,128)} %copy.158) | copy-start | bytes 245764
  32.7 5.9 %copy-start.14 = (f32[2,20,512]{2,1,0:T(8,128)S(1)}, f32[2,20,512]{2,1,0:T(8,128)}, u32[]{:S(2)}) copy-start(f32[2,20,512]{2,1,0:T(8,128)} %copy.157) | copy-start | bytes 245764
  35.7 2.9 %copy-start.2 = (bf16[2,512,1280]{1,2,0:T(8,128)(2,1)S(1)}, bf16[2,512,1280]{1,2,0:T(8,128)(2,1)}, u32[]{:S(2)}) copy-start(bf16[2,512,1280]{1,2,0:T(8,128)(2,1)} %copy-done.1) | copy-start | bytes 7864324
  37.1 9.7 %collective-permute-start.10 = (f32[40]{0:T(128)S(1)}, f32[40]{0:T(128)S(1)}, u32[]{:S(2)}, u32[]{:S(2)}) collective-permute-start(f32[40]{0:T(128)S(1)} %add.84), channel_id=1, source_target_pairs={{8,0},{9,1},{10,2},{11,3},{12,4},{13,5},{14,6},{15,7},{24,16},{25,... | collective-permute-start | bytes 488 | tf_op jit(solution)/shard_map/ppermute | solution.py:35
  45.1 1.6 %copy-start.16 = (f32[40]{0:T(128)S(1)}, f32[40]{0:T(128)}, u32[]{:S(2)}) copy-start(f32[40]{0:T(128)} %copy-done.15) | copy-start | bytes 484
  45.1 1.6 %copy-start.10 = (f32[40,2,128]{2,0,1:T(8,128)S(1)}, f32[40,2,128]{2,0,1:T(8,128)}, u32[]{:S(2)}) copy-start(f32[40,2,128]{2,0,1:T(8,128)} %copy-done.9) | copy-start | bytes 122884
  45.1 1.7 %slice-start = ((f32[40,3]{0,1:T(4,128)}), f32[40,2]{0,1:T(2,128)S(1)}, s32[]{:S(2)}) async-start(f32[40,3]{0,1:T(4,128)} %copy-done.17), calls=%async_computation | async-start | bytes 2048 | tf_op jit(solution)/shard_map/slice.3
  45.1 1.8 %copy-start.6 = (bf16[256,2560]{0,1:T(8,128)(2,1)S(1)}, bf16[256,2560]{0,1:T(8,128)(2,1)}, u32[]{:S(2)}) copy-start(bf16[256,2560]{0,1:T(8,128)(2,1)} %copy.156) | copy-start | bytes 3932164
  45.1 1.8 %copy-start.11 = (f32[256,128]{0,1:T(8,128)S(1)}, f32[256,128]{0,1:T(8,128)}, u32[]{:S(2)}) copy-start(f32[256,128]{0,1:T(8,128)} %copy.154) | copy-start | bytes 393220
  48.0 13.3 %collective-permute-start.11 = (f32[20,64,128]{2,1,0:T(8,128)S(1)}, f32[20,64,128]{2,1,0:T(8,128)S(1)}, u32[]{:S(2)}, u32[]{:S(2)}) collective-permute-start(f32[20,64,128]{2,1,0:T(8,128)S(1)} %slice_select_fusion), channel_id=1, source_target_pairs={{0,1},{1,0},{2,3},{3,2},{4,5},{5,4},{6,7},{7,6},{8,9},{9,8},{10,11... | collective-permute-start | bytes 1966088 | tf_op jit(solution)/shard_map/ppermute | solution.py:100
  49.3 8.3 %collective-permute-start.3 = (f32[2,20,8,128]{3,2,1,0:T(8,128)S(1)}, f32[2,20,8,128]{3,2,1,0:T(8,128)S(1)}, u32[]{:S(2)}, u32[]{:S(2)}) collective-permute-start(f32[2,20,8,128]{3,2,1,0:T(8,128)S(1)} %slice_select_fusion.6), channel_id=1, source_target_pairs={{0,4},{2,6},{4,0},{6,2},{8,12},{10,14},{12,8},{14,10},{1,5},{3,7},... | collective-permute-start | bytes 491528 | tf_op jit(solution)/shard_map/ppermute | solution.py:65
  57.6 4.6 %copy-start.3 = (bf16[2,512,20,64]{1,3,2,0:T(8,128)(2,1)S(1)}, bf16[2,512,20,64]{1,3,2,0:T(8,128)(2,1)}, u32[]{:S(2)}) copy-start(bf16[2,512,20,64]{1,3,2,0:T(8,128)(2,1)} %get-tuple-element.52) | copy-start | bytes 7864324
  57.6 7.9 %collective-permute-start.4 = (f32[1,20,8,128]{3,2,1,0:T(8,128)S(1)}, f32[1,20,8,128]{3,2,1,0:T(8,128)S(1)}, u32[]{:S(2)}, u32[]{:S(2)}) collective-permute-start(f32[1,20,8,128]{3,2,1,0:T(8,128)S(1)} %slice_select_fusion.8), channel_id=1, source_target_pairs={{0,8},{2,10},{4,12},{6,14},{8,0},{10,2},{12,4},{14,6},{1,9},{3,11}... | collective-permute-start | bytes 245768 | tf_op jit(solution)/shard_map/ppermute | solution.py:65
  61.6 9.3 %collective-permute-start.12 = (f32[4,20,8,128]{3,2,1,0:T(8,128)S(1)}, f32[4,20,8,128]{3,2,1,0:T(8,128)S(1)}, u32[]{:S(2)}, u32[]{:S(2)}) collective-permute-start(f32[4,20,8,128]{3,2,1,0:T(8,128)S(1)} %bitcast.143), channel_id=1, source_target_pairs={{0,2},{2,0},{4,6},{6,4},{8,10},{10,8},{12,14},{14,12},{1,3},{3,1},... | collective-permute-start | bytes 983048 | tf_op jit(solution)/shard_map/ppermute | solution.py:65
  65.6 8.3 %collective-permute-start.5 = (bf16[1,20,8,128]{3,2,1,0:T(8,128)(2,1)S(1)}, bf16[1,20,8,128]{3,2,1,0:T(8,128)(2,1)S(1)}, u32[]{:S(2)}, u32[]{:S(2)}) collective-permute-start(bf16[1,20,8,128]{3,2,1,0:T(8,128)(2,1)S(1)} %add_convert_fusion.1), channel_id=1, source_target_pairs={{0,8},{2,10},{4,12},{6,14},{8,0},{10,2},{12,4},{14,6},{1,9},{3,11}... | collective-permute-start | bytes 122888 | tf_op jit(solution)/shard_map/ppermute | solution.py:76
  71.0 6.3 %collective-permute-start.13 = (f32[2,20,8,128]{3,2,1,0:T(8,128)S(1)}, f32[2,20,8,128]{3,2,1,0:T(8,128)S(1)}, u32[]{:S(2)}, u32[]{:S(2)}) collective-permute-start(f32[2,20,8,128]{3,2,1,0:T(8,128)S(1)} %slice_select_fusion.5), channel_id=1, source_target_pairs={{0,4},{2,6},{4,0},{6,2},{8,12},{10,14},{12,8},{14,10},{1,5},{3,7},... | collective-permute-start | bytes 491528 | tf_op jit(solution)/shard_map/ppermute | solution.py:65
  73.9 5.4 %collective-permute-start.6 = (bf16[2,20,8,128]{3,2,1,0:T(8,128)(2,1)S(1)}, bf16[2,20,8,128]{3,2,1,0:T(8,128)(2,1)S(1)}, u32[]{:S(2)}, u32[]{:S(2)}) collective-permute-start(bf16[2,20,8,128]{3,2,1,0:T(8,128)(2,1)S(1)} %maximum_select_fusion.7), channel_id=1, source_target_pairs={{0,4},{2,6},{4,0},{6,2},{8,12},{10,14},{12,8},{14,10},{1,5},{3,7},... | collective-permute-start | bytes 245768 | tf_op jit(solution)/shard_map/ppermute | solution.py:76
  77.3 5.4 %collective-permute-start.14 = (f32[1,20,8,128]{3,2,1,0:T(8,128)S(1)}, f32[1,20,8,128]{3,2,1,0:T(8,128)S(1)}, u32[]{:S(2)}, u32[]{:S(2)}) collective-permute-start(f32[1,20,8,128]{3,2,1,0:T(8,128)S(1)} %slice_select_fusion.7), channel_id=1, source_target_pairs={{0,8},{2,10},{4,12},{6,14},{8,0},{10,2},{12,4},{14,6},{1,9},{3,11}... | collective-permute-start | bytes 245768 | tf_op jit(solution)/shard_map/ppermute | solution.py:65
  79.9 12.5 %collective-permute-start.7 = (bf16[4,20,8,128]{3,2,1,0:T(8,128)(2,1)}, bf16[4,20,8,128]{3,2,1,0:T(8,128)(2,1)}, u32[]{:S(2)}, u32[]{:S(2)}) collective-permute-start(bf16[4,20,8,128]{3,2,1,0:T(8,128)(2,1)} %maximum_select_fusion.3), channel_id=1, source_target_pairs={{0,2},{2,0},{4,6},{6,4},{8,10},{10,8},{12,14},{14,12},{1,3},{3,1},... | collective-permute-start | bytes 491528 | tf_op jit(solution)/shard_map/ppermute | solution.py:76
  82.7 6.5 %collective-permute-start.15 = (bf16[1,20,8,128]{3,2,1,0:T(8,128)(2,1)S(1)}, bf16[1,20,8,128]{3,2,1,0:T(8,128)(2,1)S(1)}, u32[]{:S(2)}, u32[]{:S(2)}) collective-permute-start(bf16[1,20,8,128]{3,2,1,0:T(8,128)(2,1)S(1)} %add_convert_fusion), channel_id=1, source_target_pairs={{0,8},{2,10},{4,12},{6,14},{8,0},{10,2},{12,4},{14,6},{1,9},{3,11}... | collective-permute-start | bytes 122888 | tf_op jit(solution)/shard_map/ppermute | solution.py:76
  89.2 5.6 %collective-permute-start.16 = (bf16[2,20,8,128]{3,2,1,0:T(8,128)(2,1)S(1)}, bf16[2,20,8,128]{3,2,1,0:T(8,128)(2,1)S(1)}, u32[]{:S(2)}, u32[]{:S(2)}) collective-permute-start(bf16[2,20,8,128]{3,2,1,0:T(8,128)(2,1)S(1)} %maximum_select_fusion.8), channel_id=1, source_target_pairs={{0,4},{2,6},{4,0},{6,2},{8,12},{10,14},{12,8},{14,10},{1,5},{3,7},... | collective-permute-start | bytes 245768 | tf_op jit(solution)/shard_map/ppermute | solution.py:76
  94.9 5.4 %collective-permute-start.17 = (bf16[4,20,8,128]{3,2,1,0:T(8,128)(2,1)S(1)}, bf16[4,20,8,128]{3,2,1,0:T(8,128)(2,1)S(1)}, u32[]{:S(2)}, u32[]{:S(2)}) collective-permute-start(bf16[4,20,8,128]{3,2,1,0:T(8,128)(2,1)S(1)} %maximum_select_fusion.4), channel_id=1, source_target_pairs={{0,2},{2,0},{4,6},{6,4},{8,10},{10,8},{12,14},{14,12},{1,3},{3,1},... | collective-permute-start | bytes 491528 | tf_op jit(solution)/shard_map/ppermute | solution.py:76
  96.4 8.2 %collective-permute-start.8 = (bf16[20,64,128]{2,1,0:T(8,128)(2,1)}, bf16[20,64,128]{2,1,0:T(8,128)(2,1)}, u32[]{:S(2)}, u32[]{:S(2)}) collective-permute-start(bf16[20,64,128]{2,1,0:T(8,128)(2,1)} %copy_bitcast_fusion), channel_id=1, source_target_pairs={{0,1},{1,0},{2,3},{3,2},{4,5},{5,4},{6,7},{7,6},{8,9},{9,8},{10,11... | collective-permute-start | bytes 983048 | tf_op jit(solution)/shard_map/ppermute | solution.py:100
  100.3 1.0 copy-start.4
  103.3 1.3 %copy-start.7 = (bf16[256,2560]{0,1:T(8,128)(2,1)S(1)}, bf16[256,2560]{0,1:T(8,128)(2,1)}, u32[]{:S(2)}) copy-start(bf16[256,2560]{0,1:T(8,128)(2,1)} %copy.156) | copy-start | bytes 3932164
  104.5 3.1 %copy-start.12 = (f32[256,128]{0,1:T(8,128)S(1)}, f32[256,128]{0,1:T(8,128)}, u32[]{:S(2)}) copy-start(f32[256,128]{0,1:T(8,128)} %copy.154) | copy-start | bytes 393220
  104.5 6.5 %collective-permute-start.18 = (f32[2,256,256]{2,1,0:T(8,128)}, f32[2,256,256]{2,1,0:T(8,128)}, u32[]{:S(2)}, u32[]{:S(2)}) collective-permute-start(f32[2,256,256]{2,1,0:T(8,128)} %select_bitcast_fusion), channel_id=1, source_target_pairs={{0,1},{1,0},{2,3},{3,2},{4,5},{5,4},{6,7},{7,6},{8,9},{9,8},{10,11... | collective-permute-start | bytes 1572872 | tf_op jit(solution)/shard_map/ppermute | solution.py:100

commit v10 on v9

--- a/solution.py
+++ b/solution.py
@@ -1,6 +1,7 @@
 import jax
 import jax.numpy as jnp
 from jax import lax
+from jax.experimental import pallas as pl
 from jax.sharding import PartitionSpec as P
 
 BLOCK = 256
@@ -100,6 +101,51 @@
     return lax.ppermute(value, "seq", [(at, (at + 1) % count) for at in range(count)])
 
 
+def dx_body(scores_ref, amp_ref, inv_ref, g_ref, out_ref):
+    cand_len = scores_ref.shape[1]
+    half = cand_len // 2
+    head_size = g_ref.shape[2] // 2
+    row = lax.broadcasted_iota(jnp.int32, (half, cand_len), 0)
+    col = lax.broadcasted_iota(jnp.int32, (half, cand_len), 1)
+    for j in range(2):
+        cols = slice(j * head_size, (j + 1) * head_size)
+        amp_row = amp_ref[0, 0, j:j + 1, :]
+        g_head = g_ref[0, :, cols]
+        inv_top = inv_ref[0, 0, :half, j:j + 1]
+        top = scores_ref[0, :half, :] * (amp_row * inv_top)
+        top = jnp.where(col >= row, top, 0.0).astype(jnp.bfloat16)
+        out_ref[0, :half, cols] = jnp.dot(
+            top, g_head, preferred_element_type=jnp.float32
+        ).astype(out_ref.dtype)
+        inv_low = inv_ref[0, 0, half:, j:j + 1]
+        low = scores_ref[0, half:, half:] * (amp_row[:, half:] * inv_low)
+        low = jnp.where(col[:, :half] >= row[:, :half], low, 0.0).astype(jnp.bfloat16)
+        out_ref[0, half:, cols] = jnp.dot(
+            low, g_head[half:], preferred_element_type=jnp.float32
+        ).astype(out_ref.dtype)
+
+
+def dx_kernel(scores_t, amplitude, inverse, g_flat):
+    cand_dev, cand_len, half_width = g_flat.shape
+    half_heads = amplitude.shape[2]
+    head_size = half_width // half_heads
+    pairs = half_heads // 2
+    amp_rows = jnp.transpose(amplitude.reshape(cand_dev, cand_len, pairs, 2), (0, 2, 3, 1))
+    inv_cols = jnp.transpose(inverse.reshape(cand_dev, cand_len, pairs, 2), (0, 2, 1, 3))
+    return pl.pallas_call(
+        dx_body,
+        grid=(cand_dev, pairs),
+        in_specs=[
+            pl.BlockSpec((1, cand_len, cand_len), lambda c, h: (c, 0, 0)),
+            pl.BlockSpec((1, 1, 2, cand_len), lambda c, h: (c, h, 0, 0)),
+            pl.BlockSpec((1, 1, cand_len, 2), lambda c, h: (c, h, 0, 0)),
+            pl.BlockSpec((1, cand_len, 2 * head_size), lambda c, h: (c, 0, h)),
+        ],
+        out_specs=pl.BlockSpec((1, cand_len, 2 * head_size), lambda c, h: (c, 0, h)),
+        out_shape=jax.ShapeDtypeStruct((cand_dev, cand_len, half_width), jnp.bfloat16),
+    )(scores_t, amp_rows, inv_cols, g_flat)
+
+
 def shards(x_prefix, b_prefix, code_prefix, x_cand, b_cand, c_cand, code_cand, lengths, dy_cand):
     pre_len, width = x_prefix.shape
     heads_total = code_prefix.shape[1]
@@ -129,8 +175,8 @@
     def x_work(x_cand, inverse, c_cand, b_cand):
         xc_heads = x_cand.reshape(cand_dev, cand_len, half_heads, head_size)
         x_high, x_low = split_bf16(xc_heads.astype(jnp.float32) * inverse[:, :, :, None])
-        scores = jnp.einsum("ctn,csn->cts", c_cand, b_cand, preferred_element_type=jnp.float32)
-        return x_high, x_low, scores
+        scores_t = jnp.einsum("csn,ctn->cst", b_cand, c_cand, preferred_element_type=jnp.float32)
+        return x_high, x_low, scores_t
 
     inclusive, (levels, g_parts, x_parts) = suffix_sum(
         own_total,
@@ -143,7 +189,7 @@
     )
     amplitude, inverse = levels
     g_heads, decayed_g, g_low, dstate = g_parts
-    x_high, x_low, scores = x_parts
+    x_high, x_low, scores_t = x_parts
     later_total = inclusive - own_total
     after_local = own_total[None, :] - jnp.cumsum(log_prefix, axis=0)
     weight = jnp.exp(after_local + later_total[None, :])
@@ -186,12 +232,7 @@
         "cts,csn->ctn", weight_sum, b_cand.astype(jnp.float32), precision=lax.Precision.HIGHEST
     )
 
-    amp_t = jnp.transpose(amplitude, (0, 2, 1))
-    inv_t = jnp.transpose(inverse, (0, 2, 1))
-    decay_mat = amp_t[:, :, :, None] * inv_t[:, :, None, :]
-    kernel = jnp.where(causal[None, None], scores[:, None] * decay_mat, 0.0).astype(jnp.bfloat16)
-    dx_cand = jnp.einsum("chts,cthp->cshp", kernel, g_heads, preferred_element_type=jnp.float32)
-    dx_cand = dx_cand.astype(jnp.bfloat16).reshape(flat)
+    dx_cand = dx_kernel(scores_t, amplitude, inverse, g_heads.reshape(flat))
 
     dc_state = jnp.dot(
         decayed_g.reshape(cand_dev * cand_len, half_width),

time: 114 us -> 137 us (1.20)
  Pallas kernels: 0 us -> 18 us
  local copies, waits for them, and re-layouts: 25.2 us -> 30.3 us
  starting transfers between devices: 26 us -> 22.6 us
  waiting for transfers between devices: 20.6 us -> 23.9 us
  matrix products: 21.4 us -> 18.8 us
  other arithmetic: 18.4 us -> 20.6 us
    pallas_call x0 -> x1, Pallas kernels: none -> 18 us  [dx_kernel(): pl.pallas_call(dx_body, grid=(cand_dev, pairs), in_specs=[pl.BlockSpec((1...]
    reshape x2 -> x5, local copies, waits for them, and re-layouts: 0.1 us -> 7.34 us  [the longest x1 3.91 us: dx_kernel(): inverse.reshape(cand_dev, cand_len, pairs, 2)]
    dot_general x2 -> x1, matrix products: 6.98 us -> 1.78 us  [x_work(): jnp.einsum('csn,ctn->cst', b_cand, c_cand, preferred_element_type=jnp.flo...]
    dot_general x3, matrix products: 4.95 us -> 7.56 us  [pair(): jnp.einsum('ctk,csk->cts', left.reshape(flat), right.reshape(flat), prefe...]
    ppermute x4, waiting for transfers between devices: 0.01 us -> 2.06 us  [suffix_sum(): value = value + lax.ppermute(value, axis, back)]
    ppermute x6, starting transfers between devices: 13.9 us -> 12 us  [halving_scatter(): lax.ppermute(give, axis, [(at, at ^ step) for at in range(count)])]
    select_n x1, other arithmetic: 0.18 us -> 1.92 us  [g_work(): g_cand = jnp.where(valid_rows[:, :, None], dy_cand, jnp.zeros_like(dy_cand))]
    ppermute x6, starting transfers between devices: 6.54 us -> 5.05 us  [doubling_gather(): other = lax.ppermute(value, axis, [(at, at ^ step) for at in range(count)])]
  transfers between devices with their start and end apart: 19 -> 19, of which waited for: 8 -> 9; matrix products, arithmetic and copies ran while one was open for 54% -> 47% of each run, Pallas kernels for 0% -> 13%
where the time goes in v10:
time: 137 us; the launch traced here: 135 us
  local copies, waits for them, and re-layouts  30.3 us (22%)
  waiting for transfers between devices  23.9 us (17%)
  starting transfers between devices  22.6 us (16%)
  other arithmetic  20.6 us (15%)
  matrix products  18.8 us (14%)
  Pallas kernels  18 us (13%)
    pallas_call x1, Pallas kernels, dx_kernel(): pl.pallas_call(dx_body, grid=(cand_dev, pairs), in_specs=[pl.BlockSpec((1...  18 us
    ppermute x6, waiting for transfers between devices, halving_scatter(): lax.ppermute(give, axis, [(at, at ^ step) for at in range(count)])  15.2 us
    ppermute x6, starting transfers between devices, halving_scatter(): lax.ppermute(give, axis, [(at, at ^ step) for at in range(count)])  12 us
    unnamed x47, local copies, waits for them, and re-layouts  8.16 us
    optimization_barrier x4, local copies, waits for them, and re-layouts, suffix_sum(): value, args = lax.optimization_barrier((value, pick(done)))  7.77 us
    dot_general x3, matrix products, pair(): jnp.einsum('ctk,csk->cts', left.reshape(flat), right.reshape(flat), prefe...  7.56 us
    convert_element_type x2, other arithmetic, split_bf16(): low = (value - high).astype(jnp.bfloat16)  7.02 us
    ppermute x6, waiting for transfers between devices, doubling_gather(): other = lax.ppermute(value, axis, [(at, at ^ step) for at in range(count)])  6.63 us
  transfers between devices with their start and end apart: 19, of which 9 were waited for; matrix products, arithmetic and copies ran while one was open for 47% of the time, Pallas kernels for 13%

profile of v10, /device:TPU:0, one launch (start us, length us, event | category | flops | bytes accessed | tf_op | source)
XLA Modules:
  0.0 135.4 jit_solution(6625339410453258220)
XLA Ops:
  0.6 0.9 fusion.16
  1.6 1.4 %collective-permute-start = (f32[40]{0:T(128)S(1)}, f32[40]{0:T(128)S(1)}, u32[]{:S(2)}, u32[]{:S(2)}) collective-permute-start(f32[40]{0:T(128)S(1)} %get-tuple-element.29), channel_id=1, source_target_pairs={{1,0},{2,1},{3,2},{4,3},{5,4},{6,5},{7,6},{8,7},{9,8},{10,9},{11,1... | collective-permute-start | bytes 488 | tf_op jit(solution)/shard_map/ppermute | solution.py:36
  3.1 0.8 iota_compare_fusion
  3.9 0.6 reduce-window.16
  4.7 1.0 log-plus-one_bitcast_fusion
  5.8 2.3 %reduce-window.14 = f32[2,20,4,128]{3,1,2,0:T(8,128)S(1)} reduce-window(f32[2,20,4,128]{3,1,2,0:T(8,128)S(1)} %copy.137, f32[]{:T(128)} %constant.108.clone.1), window={size=1x1x1x128 pad=0_0x0_0x0_0x127_0}, to_apply=%region_1.0 | reduce-window | flops 2600960 | bytes 163844 | tf_op jit(solution)/shard_map/reduce-window
  8.5 0.7 exp.28
  9.3 1.6 %copy.151 = f32[256,128]{0,1:T(8,128)} copy(bf16[256,128]{1,0:T(8,128)(2,1)} %param.10) | data formatting | bytes 196608 | tf_op jit(solution)/shard_map/convert_element_type | solution.py:196
  10.9 2.4 %copy.153 = bf16[256,2560]{0,1:T(8,128)(2,1)} copy(bf16[256,2560]{1,0:T(8,128)(2,1)} %param.9) | data formatting | bytes 2621440 | tf_op args[0]
  13.4 1.3 collective-permute-start.1
  14.7 0.7 copy.199
  15.4 2.6 %copy.140 = bf16[2,512,1280]{1,2,0:T(8,128)(2,1)} copy(bf16[2,512,1280]{2,1,0:T(8,128)(2,1)S(1)} %copy-done.6) | data formatting | bytes 5242880 | tf_op jit(solution)/shard_map/optimization_barrier | solution.py:35
  18.0 1.9 %broadcast_select_fusion = bf16[2,512,1280]{1,2,0:T(8,128)(2,1)S(1)} fusion(bf16[2,512,1280]{1,2,0:T(8,128)(2,1)} %copy.140, pred[2,512]{1,0:T(4,128)(4,1)S(1)} %iota_compare_fusion.1), kind=kLoop, calls=%fused_computation.17 | loop fusion | flops 1310720 | bytes 5243904 | tf_op jit(solution)/shard_map/jit(_where)/select_n | solution.py:168
  19.9 2.5 %fusion = (bf16[2,512,20,64]{1,3,2,0:T(8,128)(2,1)}, bf16[2,512,20,64]{1,3,2,0:T(8,128)(2,1)S(1)}) fusion(bf16[2,512,20,64]{1,3,2,0:T(8,128)(2,1)S(1)} %bitcast.121, f32[2,512,20]{1,2,0:T(8,128)S(1)} %copy.141), kind=kLoop, calls=%fused_computation.4 | loop fusion | flops 7864320 | bytes 7946240 | tf_op jit(solution)/shard_map/convert_element_type | solution.py:12
  22.5 1.5 %copy-done.1 = bf16[2,512,20,64]{1,3,2,0:T(8,128)(2,1)} copy-done((bf16[2,512,20,64]{1,3,2,0:T(8,128)(2,1)}, bf16[2,512,20,64]{1,3,2,0:T(8,128)(2,1)S(1)}, u32[]{:S(2)}) %copy-start.1) | copy-done | bytes 2621464
  24.0 0.8 convolution_bitcast_fusion
  24.8 3.9 %copy.155 = f32[2,512,10,2]{3,1,2,0:T(8,128)} copy(f32[2,512,10,2]{1,0,3,2:T(2,128)} %bitcast.143) | data formatting | bytes 163840 | tf_op jit(solution)/shard_map/reshape | solution.py:134
  28.9 1.3 collective-permute-start.9
  30.2 0.7 copy.150
  30.9 0.8 copy.144
  31.6 4.2 %collective-permute-start.2 = (f32[4,20,8,128]{3,2,1,0:T(8,128)}, f32[4,20,8,128]{3,2,1,0:T(8,128)}, u32[]{:S(2)}, u32[]{:S(2)}) collective-permute-start(f32[4,20,8,128]{3,2,1,0:T(8,128)} %bitcast.14), channel_id=1, source_target_pairs={{0,2},{2,0},{4,6},{6,4},{8,10},{10,8},{12,14},{14,12},{1,3},{3,1},... | collective-permute-start | bytes 983048 | tf_op jit(solution)/shard_map/ppermute | solution.py:66
  35.9 4.5 %copy.149 = bf16[2,512,1280]{1,2,0:T(8,128)(2,1)} copy(bf16[2,512,1280]{2,1,0:T(8,128)(2,1)} %param.12) | data formatting | bytes 5242880 | tf_op jit(solution)/shard_map/optimization_barrier | solution.py:35
  40.3 1.8 %fusion.21.scores_ref = f32[2,512,512]{2,1,0:T(8,128)} fusion(bf16[2,512,128]{2,1,0:T(8,128)(2,1)S(1)} %copy-done.12, bf16[2,512,128]{2,1,0:T(8,128)(2,1)S(1)} %copy-done), kind=kOutput, calls=%fused_computation.74 | convolution fusion | flops 134217728 | bytes 2621440 | tf_op jit(solution)/shard_map/csn,ctn->cst/dot_general | solution.py:178
  42.1 0.7 copy-done.3
  42.8 4.5 %fusion.1 = (bf16[2,512,20,64]{1,3,2,0:T(8,128)(2,1)}, bf16[2,512,20,64]{1,3,2,0:T(8,128)(2,1)}) fusion(bf16[2,512,20,64]{1,3,2,0:T(8,128)(2,1)S(1)} %bitcast.126, f32[2,512,20]{1,2,0:T(8,128)} %copy.150), kind=kLoop, calls=%fused_computation.5 | loop fusion | flops 7864320 | bytes 7946240 | tf_op jit(solution)/shard_map/convert_element_type | solution.py:12
  47.3 2.7 %copy.156.g_ref = bf16[2,512,1280]{2,1,0:T(8,128)(2,1)} copy(bf16[2,512,1280]{1,2,0:T(8,128)(2,1)S(1)} %broadcast_select_fusion) | data formatting | bytes 5242880 | tf_op jit(solution)/shard_map/reshape | solution.py:235
  50.0 1.5 %collective-permute-start.10 = (f32[40]{0:T(128)S(1)}, f32[40]{0:T(128)S(1)}, u32[]{:S(2)}, u32[]{:S(2)}) collective-permute-start(f32[40]{0:T(128)S(1)} %add.84), channel_id=1, source_target_pairs={{8,0},{9,1},{10,2},{11,3},{12,4},{13,5},{14,6},{15,7},{24,16},{25,... | collective-permute-start | bytes 488 | tf_op jit(solution)/shard_map/ppermute | solution.py:36
  51.5 4.2 %fusion.22 = f32[2,512,512]{2,1,0:T(8,128)S(1)} fusion(bf16[2,512,1280]{1,2,0:T(8,128)(2,1)} %bitcast.122, bf16[2,512,1280]{1,2,0:T(8,128)(2,1)} %bitcast.128), kind=kOutput, calls=%fused_computation.75 | convolution fusion | flops 1342177280 | bytes 7340032 | tf_op jit(solution)/shard_map/ctk,csk->cts/dot_general | solution.py:221
  55.7 2.0 %collective-permute-done.10 = f32[40]{0:T(128)S(1)} collective-permute-done((f32[40]{0:T(128)S(1)}, f32[40]{0:T(128)S(1)}, u32[]{:S(2)}, u32[]{:S(2)}) %collective-permute-start.10) | collective-permute-done | bytes 192 | tf_op jit(solution)/shard_map/ppermute | solution.py:36
  57.9 1.0 fusion.10
  59.1 1.1 bitcast_add_fusion.2
  60.3 2.2 %collective-permute-start.3 = (f32[2,20,8,128]{3,2,1,0:T(8,128)S(1)}, f32[2,20,8,128]{3,2,1,0:T(8,128)S(1)}, u32[]{:S(2)}, u32[]{:S(2)}) collective-permute-start(f32[2,20,8,128]{3,2,1,0:T(8,128)S(1)} %slice_select_fusion.6), channel_id=1, source_target_pairs={{0,4},{2,6},{4,0},{6,2},{8,12},{10,14},{12,8},{14,10},{1,5},{3,7},... | collective-permute-start | bytes 491528 | tf_op jit(solution)/shard_map/ppermute | solution.py:66
  62.5 1.6 %fusion.23 = f32[2,512,512]{2,1,0:T(8,128)S(1)} fusion(bf16[2,512,1280]{1,2,0:T(8,128)(2,1)S(1)} %bitcast.123, bf16[2,512,1280]{1,2,0:T(8,128)(2,1)S(1)} %bitcast.131), kind=kOutput, calls=%fused_computation.76 | convolution fusion | flops 1342177280 | bytes 7340032 | tf_op jit(solution)/shard_map/ctk,csk->cts/dot_general | solution.py:221
  64.0 3.1 %collective-permute-done.3 = f32[2,20,8,128]{3,2,1,0:T(8,128)S(1)} collective-permute-done((f32[2,20,8,128]{3,2,1,0:T(8,128)S(1)}, f32[2,20,8,128]{3,2,1,0:T(8,128)S(1)}, u32[]{:S(2)}, u32[]{:S(2)}) %collective-permute-start.3) | collective-permute-done | bytes 163872 | tf_op jit(solution)/shard_map/ppermute | solution.py:66
  67.2 3.0 %collective-permute-start.4 = (f32[1,20,8,128]{3,2,1,0:T(8,128)S(1)}, f32[1,20,8,128]{3,2,1,0:T(8,128)S(1)}, u32[]{:S(2)}, u32[]{:S(2)}) collective-permute-start(f32[1,20,8,128]{3,2,1,0:T(8,128)S(1)} %slice_select_fusion.8), channel_id=1, source_target_pairs={{0,8},{2,10},{4,12},{6,14},{8,0},{10,2},{12,4},{14,6},{1,9},{3,11}... | collective-permute-start | bytes 245768 | tf_op jit(solution)/shard_map/ppermute | solution.py:66
  70.6 0.6 collective-permute-start.12
  71.2 1.8 %add_select_fusion = f32[2,512,512]{2,1,0:T(8,128)S(1)} fusion(f32[2,512,512]{2,1,0:T(8,128)S(1)} %fusion.22, f32[2,512,512]{2,1,0:T(8,128)S(1)} %fusion.23, bf16[2,512,1280]{1,2,0:T(8,128)(2,1)S(1)} %bitcast.127, bf16[2,512,1280]{1,2,0:T(8,128)(2,1)S(1)} %bitcast.129, pred[512,512]{1,0:T(8,128)(4,1)S(1)} %copy-done.8), kind=kOutput, calls=%fused_computation.18 | convolution fusion | flops 1343750144 | bytes 11796480 | tf_op jit(solution)/shard_map/ctk,csk->cts/dot_general | solution.py:221
  73.0 1.4 %collective-permute-done.4 = f32[1,20,8,128]{3,2,1,0:T(8,128)S(1)} collective-permute-done((f32[1,20,8,128]{3,2,1,0:T(8,128)S(1)}, f32[1,20,8,128]{3,2,1,0:T(8,128)S(1)}, u32[]{:S(2)}, u32[]{:S(2)}) %collective-permute-start.4) | collective-permute-done | bytes 81952 | tf_op jit(solution)/shard_map/ppermute | solution.py:66
  74.5 1.2 collective-permute-start.5
  75.7 4.0 %collective-permute-done.12 = f32[4,20,8,128]{3,2,1,0:T(8,128)S(1)} collective-permute-done((f32[4,20,8,128]{3,2,1,0:T(8,128)S(1)}, f32[4,20,8,128]{3,2,1,0:T(8,128)S(1)}, u32[]{:S(2)}, u32[]{:S(2)}) %collective-permute-start.12) | collective-permute-done | bytes 327712 | tf_op jit(solution)/shard_map/ppermute | solution.py:66
  79.8 1.6 %collective-permute-start.13 = (f32[2,20,8,128]{3,2,1,0:T(8,128)S(1)}, f32[2,20,8,128]{3,2,1,0:T(8,128)S(1)}, u32[]{:S(2)}, u32[]{:S(2)}) collective-permute-start(f32[2,20,8,128]{3,2,1,0:T(8,128)S(1)} %slice_select_fusion.5), channel_id=1, source_target_pairs={{0,4},{2,6},{4,0},{6,2},{8,12},{10,14},{12,8},{14,10},{1,5},{3,7},... | collective-permute-start | bytes 491528 | tf_op jit(solution)/shard_map/ppermute | solution.py:66
  81.4 1.3 fusion.25
  83.3 2.8 %collective-permute-done.13 = f32[2,20,8,128]{3,2,1,0:T(8,128)S(1)} collective-permute-done((f32[2,20,8,128]{3,2,1,0:T(8,128)S(1)}, f32[2,20,8,128]{3,2,1,0:T(8,128)S(1)}, u32[]{:S(2)}, u32[]{:S(2)}) %collective-permute-start.13) | collective-permute-done | bytes 163872 | tf_op jit(solution)/shard_map/ppermute | solution.py:66
  86.5 1.4 %collective-permute-done.6 = bf16[2,20,8,128]{3,2,1,0:T(8,128)(2,1)S(1)} collective-permute-done((bf16[2,20,8,128]{3,2,1,0:T(8,128)(2,1)S(1)}, bf16[2,20,8,128]{3,2,1,0:T(8,128)(2,1)S(1)}, u32[]{:S(2)}, u32[]{:S(2)}) %collective-permute-start.6) | collective-permute-done | bytes 81952 | tf_op jit(solution)/shard_map/ppermute | solution.py:77
  87.9 0.7 maximum_select_fusion.3
  88.6 0.6 collective-permute-start.7
  89.2 3.9 %collective-permute-done.14 = f32[1,20,8,128]{3,2,1,0:T(8,128)S(1)} collective-permute-done((f32[1,20,8,128]{3,2,1,0:T(8,128)S(1)}, f32[1,20,8,128]{3,2,1,0:T(8,128)S(1)}, u32[]{:S(2)}, u32[]{:S(2)}) %collective-permute-start.14) | collective-permute-done | bytes 81952 | tf_op jit(solution)/shard_map/ppermute | solution.py:66
  93.1 1.7 %fusion.24 = f32[2,512,128]{1,2,0:T(8,128)} fusion(f32[2,512,512]{2,1,0:T(8,128)S(1)} %add_select_fusion, bf16[2,512,128]{2,1,0:T(8,128)(2,1)S(1)} %copy-done), kind=kOutput, calls=%fused_computation.77 | convolution fusion | flops 805306368 | bytes 2883584 | tf_op jit(solution)/shard_map/cts,ctn->csn/dot_general | solution.py:228
  94.8 18.0 %shard_map.128 = bf16[2,512,1280]{2,1,0:T(8,128)(2,1)} custom-call(f32[2,512,512]{2,1,0:T(8,128)} %fusion.21.scores_ref, f32[2,10,2,512]{3,2,1,0:T(2,128)} %bitcast.145, f32[2,10,512,2]{3,2,1,0:T(8,128)} %bitcast.125, bf16[2,512,1280]{2,1,0:T(8,128)(2,1)} %copy.156.g_ref), custom_call_target="tpu_custom_call" | custom-call | tf_op jit(solution)/shard_map/pallas_call | solution.py:135
  112.8 2.0 %collective-permute-start.16 = (bf16[2,20,8,128]{3,2,1,0:T(8,128)(2,1)S(1)}, bf16[2,20,8,128]{3,2,1,0:T(8,128)(2,1)S(1)}, u32[]{:S(2)}, u32[]{:S(2)}) collective-permute-start(bf16[2,20,8,128]{3,2,1,0:T(8,128)(2,1)S(1)} %maximum_select_fusion.8), channel_id=1, source_target_pairs={{0,4},{2,6},{4,0},{6,2},{8,12},{10,14},{12,8},{14,10},{1,5},{3,7},... | collective-permute-start | bytes 245768 | tf_op jit(solution)/shard_map/ppermute | solution.py:77
  114.8 1.2 maximum_select_fusion.1
  116.0 1.3 collective-permute-done.16
  117.4 0.6 collective-permute-start.17
  118.0 0.9 copy_bitcast_fusion
  118.9 3.9 %collective-permute-done.17 = bf16[4,20,8,128]{3,2,1,0:T(8,128)(2,1)S(1)} collective-permute-done((bf16[4,20,8,128]{3,2,1,0:T(8,128)(2,1)S(1)}, bf16[4,20,8,128]{3,2,1,0:T(8,128)(2,1)S(1)}, u32[]{:S(2)}, u32[]{:S(2)}) %collective-permute-start.17) | collective-permute-done | bytes 163872 | tf_op jit(solution)/shard_map/ppermute | solution.py:77
  123.9 0.7 reshape.213
  124.6 0.8 fusion.19
  126.1 0.9 select_bitcast_fusion
  127.1 2.2 %fusion.2 = f32[256,128]{0,1:T(8,128)S(1)} fusion(f32[256,40]{0,1:T(8,128)S(1)} %fusion.14, bf16[256,40,64]{0,2,1:T(8,128)(2,1)S(1)} %bitcast.135, bf16[20,64,128]{2,1,0:T(8,128)(2,1)} %collective-permute-done.8, bf16[20,64,128]{2,1,0:T(8,128)(2,1)} %copy_bitcast_fusion, pred[]{:T(512)S(6)} %eq.34), kind=kOutput, calls=%fused_computation.8 | convolution fusion | flops 171343872 | bytes 2138113 | tf_op jit(solution)/shard_map/jhp,hpn->jhn/dot_general | solution.py:256
  129.3 0.8 copy.176
  130.0 1.8 %fusion.9 = bf16[40,64,256]{2,1,0:T(8,128)(2,1)S(1)} fusion(f32[256,128]{0,1:T(8,128)S(1)} %copy-done.18, f32[256,40]{0,1:T(8,128)S(1)} %fusion.14, bf16[20,64,128]{2,1,0:T(8,128)(2,1)} %collective-permute-done.8, bf16[20,64,128]{2,1,0:T(8,128)(2,1)} %copy_bitcast_fusion, pred[]{:T(512)S(6)} %eq.34), kind=kOutput, calls=%fused_computation.19 | convolution fusion | flops 172032000 | bytes 2138113 | tf_op jit(solution)/shard_map/jhn,hpn->jhp/dot_general | solution.py:252
  131.9 1.6 %copy.175 = bf16[256,2560]{1,0:T(8,128)(2,1)} copy(bf16[256,2560]{0,1:T(8,128)(2,1)S(1)} %bitcast.136) | data formatting | bytes 2621440
  133.5 1.1 bitcast_add_fusion
  134.6 0.8 fusion.20
  (107 shorter events, 4.8 us)
Async XLA Ops:
  0.6 23.3 %copy-start = (bf16[2,512,128]{2,1,0:T(8,128)(2,1)S(1)}, bf16[2,512,128]{2,1,0:T(8,128)(2,1)}, u32[]{:S(2)}) copy-start(bf16[2,512,128]{2,1,0:T(8,128)(2,1)} %param.14) | copy-start | bytes 786436
  1.6 11.7 %copy-start.20 = (s32[2]{0:T(128)S(1)}, s32[2]{0:T(128)}, u32[]{:S(2)}) copy-start(s32[2]{0:T(128)} %param.16) | copy-start | bytes 28
  1.6 11.7 %collective-permute-start = (f32[40]{0:T(128)S(1)}, f32[40]{0:T(128)S(1)}, u32[]{:S(2)}, u32[]{:S(2)}) collective-permute-start(f32[40]{0:T(128)S(1)} %get-tuple-element.29), channel_id=1, source_target_pairs={{1,0},{2,1},{3,2},{4,3},{5,4},{6,5},{7,6},{8,7},{9,8},{10,9},{11,1... | collective-permute-start | bytes 488 | tf_op jit(solution)/shard_map/ppermute | solution.py:36
  3.9 11.5 %copy-start.6 = (bf16[2,512,1280]{2,1,0:T(8,128)(2,1)S(1)}, bf16[2,512,1280]{2,1,0:T(8,128)(2,1)}, u32[]{:S(2)}) copy-start(bf16[2,512,1280]{2,1,0:T(8,128)(2,1)} %param.17) | copy-start | bytes 7864324
  4.5 1.3 copy-start.15
  4.7 13.4 %copy-start.19 = (f32[40,3]{0,1:T(4,128)}, f32[40,3]{0,1:T(4,128)S(1)}, u32[]{:S(2)}) copy-start(f32[40,3]{0,1:T(4,128)S(1)} %reduce-window.19) | copy-start | bytes 1444
  13.4 15.3 %collective-permute-start.1 = (f32[40]{0:T(128)S(1)}, f32[40]{0:T(128)S(1)}, u32[]{:S(2)}, u32[]{:S(2)}) collective-permute-start(f32[40]{0:T(128)S(1)} %add.79), channel_id=1, source_target_pairs={{2,0},{3,1},{4,2},{5,3},{6,4},{7,5},{8,6},{9,7},{10,8},{11,9},{12,... | collective-permute-start | bytes 488 | tf_op jit(solution)/shard_map/ppermute | solution.py:36
  22.5 1.5 %copy-start.1 = (bf16[2,512,20,64]{1,3,2,0:T(8,128)(2,1)}, bf16[2,512,20,64]{1,3,2,0:T(8,128)(2,1)S(1)}, u32[]{:S(2)}) copy-start(bf16[2,512,20,64]{1,3,2,0:T(8,128)(2,1)S(1)} %get-tuple-element.49) | copy-start | bytes 7864324
  28.7 1.5 %copy-start.14 = (f32[2,20,512]{2,0,1:T(2,128)S(1)}, f32[2,20,512]{2,0,1:T(2,128)}, u32[]{:S(2)}) copy-start(f32[2,20,512]{2,0,1:T(2,128)} %exp.28) | copy-start | bytes 245764
  28.9 21.1 %collective-permute-start.9 = (f32[40]{0:T(128)S(1)}, f32[40]{0:T(128)S(1)}, u32[]{:S(2)}, u32[]{:S(2)}) collective-permute-start(f32[40]{0:T(128)S(1)} %add.80), channel_id=1, source_target_pairs={{4,0},{5,1},{6,2},{7,3},{8,4},{9,5},{10,6},{11,7},{12,8},{13,9},{1... | collective-permute-start | bytes 488 | tf_op jit(solution)/shard_map/ppermute | solution.py:36
  31.6 8.7 %copy-start.12 = (bf16[2,512,128]{2,1,0:T(8,128)(2,1)S(1)}, bf16[2,512,128]{2,1,0:T(8,128)(2,1)}, u32[]{:S(2)}) copy-start(bf16[2,512,128]{2,1,0:T(8,128)(2,1)} %param.13) | copy-start | bytes 786436
  31.6 27.5 %collective-permute-start.2 = (f32[4,20,8,128]{3,2,1,0:T(8,128)}, f32[4,20,8,128]{3,2,1,0:T(8,128)}, u32[]{:S(2)}, u32[]{:S(2)}) collective-permute-start(f32[4,20,8,128]{3,2,1,0:T(8,128)} %bitcast.14), channel_id=1, source_target_pairs={{0,2},{2,0},{4,6},{6,4},{8,10},{10,8},{12,14},{14,12},{1,3},{3,1},... | collective-permute-start | bytes 983048 | tf_op jit(solution)/shard_map/ppermute | solution.py:66
  40.3 2.5 %copy-start.3 = (bf16[2,512,1280]{1,2,0:T(8,128)(2,1)S(1)}, bf16[2,512,1280]{1,2,0:T(8,128)(2,1)}, u32[]{:S(2)}) copy-start(bf16[2,512,1280]{1,2,0:T(8,128)(2,1)} %copy.149) | copy-start | bytes 7864324
  50.0 7.8 %collective-permute-start.10 = (f32[40]{0:T(128)S(1)}, f32[40]{0:T(128)S(1)}, u32[]{:S(2)}, u32[]{:S(2)}) collective-permute-start(f32[40]{0:T(128)S(1)} %add.84), channel_id=1, source_target_pairs={{8,0},{9,1},{10,2},{11,3},{12,4},{13,5},{14,6},{15,7},{24,16},{25,... | collective-permute-start | bytes 488 | tf_op jit(solution)/shard_map/ppermute | solution.py:36
  51.5 6.3 %copy-start.16 = (f32[40,2,128]{2,0,1:T(8,128)S(1)}, f32[40,2,128]{2,0,1:T(8,128)}, u32[]{:S(2)}) copy-start(f32[40,2,128]{2,0,1:T(8,128)} %copy-done.15) | copy-start | bytes 122884
  51.5 6.3 %slice-start = ((f32[40,3]{0,1:T(4,128)}), f32[40,2]{0,1:T(2,128)S(1)}, s32[]{:S(2)}) async-start(f32[40,3]{0,1:T(4,128)} %copy-done.19), calls=%async_computation | async-start | bytes 2048 | tf_op jit(solution)/shard_map/slice.3
  51.5 6.4 %copy-start.10 = (bf16[256,2560]{0,1:T(8,128)(2,1)S(1)}, bf16[256,2560]{0,1:T(8,128)(2,1)}, u32[]{:S(2)}) copy-start(bf16[256,2560]{0,1:T(8,128)(2,1)} %copy.153) | copy-start | bytes 3932164
  51.5 6.4 %copy-start.17 = (f32[256,128]{0,1:T(8,128)S(1)}, f32[256,128]{0,1:T(8,128)}, u32[]{:S(2)}) copy-start(f32[256,128]{0,1:T(8,128)} %copy.151) | copy-start | bytes 393220
  57.9 4.6 %copy-start.7 = (bf16[2,512,20,64]{1,3,2,0:T(8,128)(2,1)S(1)}, bf16[2,512,20,64]{1,3,2,0:T(8,128)(2,1)}, u32[]{:S(2)}) copy-start(bf16[2,512,20,64]{1,3,2,0:T(8,128)(2,1)} %get-tuple-element.51) | copy-start | bytes 7864324
  58.9 3.5 %copy-start.2 = (bf16[2,512,20,64]{1,3,2,0:T(8,128)(2,1)S(1)}, bf16[2,512,20,64]{1,3,2,0:T(8,128)(2,1)}, u32[]{:S(2)}) copy-start(bf16[2,512,20,64]{1,3,2,0:T(8,128)(2,1)} %copy-done.1) | copy-start | bytes 7864324
  59.0 11.2 %collective-permute-start.11 = (f32[20,64,128]{2,1,0:T(8,128)S(1)}, f32[20,64,128]{2,1,0:T(8,128)S(1)}, u32[]{:S(2)}, u32[]{:S(2)}) collective-permute-start(f32[20,64,128]{2,1,0:T(8,128)S(1)} %slice_select_fusion), channel_id=1, source_target_pairs={{0,1},{1,0},{2,3},{3,2},{4,5},{5,4},{6,7},{7,6},{8,9},{9,8},{10,11... | collective-permute-start | bytes 1966088 | tf_op jit(solution)/shard_map/ppermute | solution.py:101
  60.3 6.9 %collective-permute-start.3 = (f32[2,20,8,128]{3,2,1,0:T(8,128)S(1)}, f32[2,20,8,128]{3,2,1,0:T(8,128)S(1)}, u32[]{:S(2)}, u32[]{:S(2)}) collective-permute-start(f32[2,20,8,128]{3,2,1,0:T(8,128)S(1)} %slice_select_fusion.6), channel_id=1, source_target_pairs={{0,4},{2,6},{4,0},{6,2},{8,12},{10,14},{12,8},{14,10},{1,5},{3,7},... | collective-permute-start | bytes 491528 | tf_op jit(solution)/shard_map/ppermute | solution.py:66
  67.2 4.0 %copy-start.4 = (bf16[2,512,20,64]{1,3,2,0:T(8,128)(2,1)S(1)}, bf16[2,512,20,64]{1,3,2,0:T(8,128)(2,1)}, u32[]{:S(2)}) copy-start(bf16[2,512,20,64]{1,3,2,0:T(8,128)(2,1)} %get-tuple-element.52) | copy-start | bytes 7864324
  67.2 4.0 %copy-start.5 = (bf16[2,512,20,64]{1,3,2,0:T(8,128)(2,1)S(1)}, bf16[2,512,20,64]{1,3,2,0:T(8,128)(2,1)}, u32[]{:S(2)}) copy-start(bf16[2,512,20,64]{1,3,2,0:T(8,128)(2,1)} %get-tuple-element.50) | copy-start | bytes 7864324
  67.2 4.0 %copy-start.8 = (pred[512,512]{1,0:T(8,128)(4,1)S(1)}, pred[512,512]{1,0:T(8,128)(4,1)}, u32[]{:S(2)}) copy-start(pred[512,512]{1,0:T(8,128)(4,1)} %iota_compare_fusion) | copy-start | bytes 786436
  67.2 7.2 %collective-permute-start.4 = (f32[1,20,8,128]{3,2,1,0:T(8,128)S(1)}, f32[1,20,8,128]{3,2,1,0:T(8,128)S(1)}, u32[]{:S(2)}, u32[]{:S(2)}) collective-permute-start(f32[1,20,8,128]{3,2,1,0:T(8,128)S(1)} %slice_select_fusion.8), channel_id=1, source_target_pairs={{0,8},{2,10},{4,12},{6,14},{8,0},{10,2},{12,4},{14,6},{1,9},{3,11}... | collective-permute-start | bytes 245768 | tf_op jit(solution)/shard_map/ppermute | solution.py:66
  70.6 9.2 %collective-permute-start.12 = (f32[4,20,8,128]{3,2,1,0:T(8,128)S(1)}, f32[4,20,8,128]{3,2,1,0:T(8,128)S(1)}, u32[]{:S(2)}, u32[]{:S(2)}) collective-permute-start(f32[4,20,8,128]{3,2,1,0:T(8,128)S(1)} %bitcast.146), channel_id=1, source_target_pairs={{0,2},{2,0},{4,6},{6,4},{8,10},{10,8},{12,14},{14,12},{1,3},{3,1},... | collective-permute-start | bytes 983048 | tf_op jit(solution)/shard_map/ppermute | solution.py:66
  71.2 10.2 %copy-start.13 = (bf16[2,512,128]{2,1,0:T(8,128)(2,1)S(1)}, bf16[2,512,128]{2,1,0:T(8,128)(2,1)}, u32[]{:S(2)}) copy-start(bf16[2,512,128]{2,1,0:T(8,128)(2,1)} %param.13) | copy-start | bytes 786436
  74.5 8.2 %collective-permute-start.5 = (bf16[1,20,8,128]{3,2,1,0:T(8,128)(2,1)S(1)}, bf16[1,20,8,128]{3,2,1,0:T(8,128)(2,1)S(1)}, u32[]{:S(2)}, u32[]{:S(2)}) collective-permute-start(bf16[1,20,8,128]{3,2,1,0:T(8,128)(2,1)S(1)} %add_convert_fusion.1), channel_id=1, source_target_pairs={{0,8},{2,10},{4,12},{6,14},{8,0},{10,2},{12,4},{14,6},{1,9},{3,11}... | collective-permute-start | bytes 122888 | tf_op jit(solution)/shard_map/ppermute | solution.py:77
  79.8 6.3 %collective-permute-start.13 = (f32[2,20,8,128]{3,2,1,0:T(8,128)S(1)}, f32[2,20,8,128]{3,2,1,0:T(8,128)S(1)}, u32[]{:S(2)}, u32[]{:S(2)}) collective-permute-start(f32[2,20,8,128]{3,2,1,0:T(8,128)S(1)} %slice_select_fusion.5), channel_id=1, source_target_pairs={{0,4},{2,6},{4,0},{6,2},{8,12},{10,14},{12,8},{14,10},{1,5},{3,7},... | collective-permute-start | bytes 491528 | tf_op jit(solution)/shard_map/ppermute | solution.py:66
  82.7 5.2 %collective-permute-start.6 = (bf16[2,20,8,128]{3,2,1,0:T(8,128)(2,1)S(1)}, bf16[2,20,8,128]{3,2,1,0:T(8,128)(2,1)S(1)}, u32[]{:S(2)}, u32[]{:S(2)}) collective-permute-start(bf16[2,20,8,128]{3,2,1,0:T(8,128)(2,1)S(1)} %maximum_select_fusion.7), channel_id=1, source_target_pairs={{0,4},{2,6},{4,0},{6,2},{8,12},{10,14},{12,8},{14,10},{1,5},{3,7},... | collective-permute-start | bytes 245768 | tf_op jit(solution)/shard_map/ppermute | solution.py:77
  86.1 6.9 %collective-permute-start.14 = (f32[1,20,8,128]{3,2,1,0:T(8,128)S(1)}, f32[1,20,8,128]{3,2,1,0:T(8,128)S(1)}, u32[]{:S(2)}, u32[]{:S(2)}) collective-permute-start(f32[1,20,8,128]{3,2,1,0:T(8,128)S(1)} %slice_select_fusion.7), channel_id=1, source_target_pairs={{0,8},{2,10},{4,12},{6,14},{8,0},{10,2},{12,4},{14,6},{1,9},{3,11}... | collective-permute-start | bytes 245768 | tf_op jit(solution)/shard_map/ppermute | solution.py:66
  88.6 26.2 %collective-permute-start.7 = (bf16[4,20,8,128]{3,2,1,0:T(8,128)(2,1)}, bf16[4,20,8,128]{3,2,1,0:T(8,128)(2,1)}, u32[]{:S(2)}, u32[]{:S(2)}) collective-permute-start(bf16[4,20,8,128]{3,2,1,0:T(8,128)(2,1)} %maximum_select_fusion.3), channel_id=1, source_target_pairs={{0,2},{2,0},{4,6},{6,4},{8,10},{10,8},{12,14},{14,12},{1,3},{3,1},... | collective-permute-start | bytes 491528 | tf_op jit(solution)/shard_map/ppermute | solution.py:77
  93.1 19.8 %collective-permute-start.15 = (bf16[1,20,8,128]{3,2,1,0:T(8,128)(2,1)S(1)}, bf16[1,20,8,128]{3,2,1,0:T(8,128)(2,1)S(1)}, u32[]{:S(2)}, u32[]{:S(2)}) collective-permute-start(bf16[1,20,8,128]{3,2,1,0:T(8,128)(2,1)S(1)} %add_convert_fusion), channel_id=1, source_target_pairs={{0,8},{2,10},{4,12},{6,14},{8,0},{10,2},{12,4},{14,6},{1,9},{3,11}... | collective-permute-start | bytes 122888 | tf_op jit(solution)/shard_map/ppermute | solution.py:77
  112.8 4.5 %collective-permute-start.16 = (bf16[2,20,8,128]{3,2,1,0:T(8,128)(2,1)S(1)}, bf16[2,20,8,128]{3,2,1,0:T(8,128)(2,1)S(1)}, u32[]{:S(2)}, u32[]{:S(2)}) collective-permute-start(bf16[2,20,8,128]{3,2,1,0:T(8,128)(2,1)S(1)} %maximum_select_fusion.8), channel_id=1, source_target_pairs={{0,4},{2,6},{4,0},{6,2},{8,12},{10,14},{12,8},{14,10},{1,5},{3,7},... | collective-permute-start | bytes 245768 | tf_op jit(solution)/shard_map/ppermute | solution.py:77
  117.4 5.4 %collective-permute-start.17 = (bf16[4,20,8,128]{3,2,1,0:T(8,128)(2,1)S(1)}, bf16[4,20,8,128]{3,2,1,0:T(8,128)(2,1)S(1)}, u32[]{:S(2)}, u32[]{:S(2)}) collective-permute-start(bf16[4,20,8,128]{3,2,1,0:T(8,128)(2,1)S(1)} %maximum_select_fusion.4), channel_id=1, source_target_pairs={{0,2},{2,0},{4,6},{6,4},{8,10},{10,8},{12,14},{14,12},{1,3},{3,1},... | collective-permute-start | bytes 491528 | tf_op jit(solution)/shard_map/ppermute | solution.py:77
  118.9 8.1 %collective-permute-start.8 = (bf16[20,64,128]{2,1,0:T(8,128)(2,1)}, bf16[20,64,128]{2,1,0:T(8,128)(2,1)}, u32[]{:S(2)}, u32[]{:S(2)}) collective-permute-start(bf16[20,64,128]{2,1,0:T(8,128)(2,1)} %copy_bitcast_fusion), channel_id=1, source_target_pairs={{0,1},{1,0},{2,3},{3,2},{4,5},{5,4},{6,7},{7,6},{8,9},{9,8},{10,11... | collective-permute-start | bytes 983048 | tf_op jit(solution)/shard_map/ppermute | solution.py:101
  122.8 1.0 copy-start.9
  125.7 1.3 copy-start.11
  127.0 3.1 %copy-start.18 = (f32[256,128]{0,1:T(8,128)S(1)}, f32[256,128]{0,1:T(8,128)}, u32[]{:S(2)}) copy-start(f32[256,128]{0,1:T(8,128)} %copy.151) | copy-start | bytes 393220
  127.0 6.5 %collective-permute-start.18 = (f32[2,256,256]{2,1,0:T(8,128)}, f32[2,256,256]{2,1,0:T(8,128)}, u32[]{:S(2)}, u32[]{:S(2)}) collective-permute-start(f32[2,256,256]{2,1,0:T(8,128)} %select_bitcast_fusion), channel_id=1, source_target_pairs={{0,1},{1,0},{2,3},{3,2},{4,5},{5,4},{6,7},{7,6},{8,9},{9,8},{10,11... | collective-permute-start | bytes 1572872 | tf_op jit(solution)/shard_map/ppermute | solution.py:101

commit v11 on v9

--- a/solution.py
+++ b/solution.py
@@ -160,6 +160,10 @@
     init_local = own_half + other_core(give_half)
 
     grad_half = cand_sum_bf16(dstate)
+    init_local, late = lax.optimization_barrier(
+        (init_local, (g_heads, decayed_g, g_low, x_high, x_low, scores))
+    )
+    g_heads, decayed_g, g_low, x_high, x_low, scores = late
     init_half = cand_sum_bf16(init_local)
     grad_other = other_core(grad_half)
     grad_state = jnp.where(

time: 114 us -> 120 us (1.053)
  waiting for transfers between devices: 20.6 us -> 31.3 us
  other arithmetic: 18.4 us -> 13.2 us
  matrix products: 21.4 us -> 23.1 us
  local copies, waits for them, and re-layouts: 25.2 us -> 23.5 us
    ppermute x4, waiting for transfers between devices: 0.01 us -> 8.38 us  [suffix_sum(): value = value + lax.ppermute(value, axis, back)]
    ppermute x6, starting transfers between devices: 6.54 us -> 10.3 us  [doubling_gather(): other = lax.ppermute(value, axis, [(at, at ^ step) for at in range(count)])]
    ppermute x6, starting transfers between devices: 13.9 us -> 11.6 us  [halving_scatter(): lax.ppermute(give, axis, [(at, at ^ step) for at in range(count)])]
    ppermute x6, waiting for transfers between devices: 6.68 us -> 8.74 us  [doubling_gather(): other = lax.ppermute(value, axis, [(at, at ^ step) for at in range(count)])]
    convert_element_type x2, other arithmetic: 5.76 us -> 4.13 us  [split_bf16(): low = (value - high).astype(jnp.bfloat16)]
    add x3, other arithmetic: 1.49 us -> 0.01 us  [suffix_sum(): value = value + lax.ppermute(value, axis, back)]
    unnamed x44 -> x46, local copies, waits for them, and re-layouts: 9.33 us -> 9.5 us
  transfers between devices with their start and end apart: 19 -> 19, of which waited for: 8 -> 11; matrix products, arithmetic and copies ran while one was open for 54% -> 41% of each run, Pallas kernels for 0% -> 0%
where the time goes in v11:
time: 120 us
  waiting for transfers between devices  31.3 us (26%)
  starting transfers between devices  27.2 us (23%)
  local copies, waits for them, and re-layouts  23.5 us (20%)
  matrix products  23.1 us (19%)
  other arithmetic  13.2 us (11%)
  between operations  1.34 us (1%)
    ppermute x6, waiting for transfers between devices, halving_scatter(): lax.ppermute(give, axis, [(at, at ^ step) for at in range(count)])  14.2 us
    ppermute x6, starting transfers between devices, halving_scatter(): lax.ppermute(give, axis, [(at, at ^ step) for at in range(count)])  11.6 us
    ppermute x6, starting transfers between devices, doubling_gather(): other = lax.ppermute(value, axis, [(at, at ^ step) for at in range(count)])  10.3 us
    unnamed x46, local copies, waits for them, and re-layouts  9.5 us
    ppermute x6, waiting for transfers between devices, doubling_gather(): other = lax.ppermute(value, axis, [(at, at ^ step) for at in range(count)])  8.74 us
    optimization_barrier x4, local copies, waits for them, and re-layouts, suffix_sum(): value, args = lax.optimization_barrier((value, pick(done)))  8.48 us
    ppermute x4, waiting for transfers between devices, suffix_sum(): value = value + lax.ppermute(value, axis, back)  8.38 us
    dot_general x1, matrix products, shards(): jnp.einsum('chts,cthp->cshp', kernel, g_heads, preferred_element_type=jnp...  7.42 us
  transfers between devices with their start and end apart: 19, of which 11 were waited for; matrix products, arithmetic and copies ran while one was open for 41% of the time, Pallas kernels for 0%

profile of v11, /device:TPU:0, one launch (start us, length us, event | category | flops | bytes accessed | tf_op | source)
XLA Modules:
  0.0 119.7 jit_solution(10462101959357948908)
XLA Ops:
  0.7 1.0 fusion.23
  1.7 1.3 %collective-permute-start = (f32[40]{0:T(128)S(1)}, f32[40]{0:T(128)S(1)}, u32[]{:S(2)}, u32[]{:S(2)}) collective-permute-start(f32[40]{0:T(128)S(1)} %get-tuple-element.36), channel_id=1, source_target_pairs={{1,0},{2,1},{3,2},{4,3},{5,4},{6,5},{7,6},{8,7},{9,8},{10,9},{11,1... | collective-permute-start | bytes 488 | tf_op jit(solution)/shard_map/ppermute | solution.py:35
  3.0 1.0 log-plus-one_bitcast_fusion
  4.2 2.3 %reduce-window.14 = f32[2,20,4,128]{3,1,2,0:T(8,128)S(1)} reduce-window(f32[2,20,4,128]{3,1,2,0:T(8,128)S(1)} %copy.140, f32[]{:T(128)} %constant.108.clone.1), window={size=1x1x1x128 pad=0_0x0_0x0_0x127_0}, to_apply=%region_1.0 | reduce-window | flops 2600960 | bytes 163844 | tf_op jit(solution)/shard_map/reduce-window
  6.5 0.2 slice_reduce_fusion
  7.0 0.7 exp.28
  7.7 0.6 reduce-window.16
  8.5 1.4 %copy.156 = bf16[256,2560]{0,1:T(8,128)(2,1)} copy(bf16[256,2560]{1,0:T(8,128)(2,1)S(1)} %copy-done.6) | data formatting | bytes 2621440 | tf_op args[0]
  9.9 0.8 copy.154
  10.7 3.0 %copy.143 = bf16[2,512,1280]{1,2,0:T(8,128)(2,1)S(1)} copy(bf16[2,512,1280]{2,1,0:T(8,128)(2,1)} %param.17) | data formatting | bytes 5242880 | tf_op jit(solution)/shard_map/optimization_barrier | solution.py:34
  13.8 1.3 %collective-permute-start.1 = (f32[40]{0:T(128)S(1)}, f32[40]{0:T(128)S(1)}, u32[]{:S(2)}, u32[]{:S(2)}) collective-permute-start(f32[40]{0:T(128)S(1)} %add.79), channel_id=1, source_target_pairs={{2,0},{3,1},{4,2},{5,3},{6,4},{7,5},{8,6},{9,7},{10,8},{11,9},{12,... | collective-permute-start | bytes 488 | tf_op jit(solution)/shard_map/ppermute | solution.py:35
  15.1 0.2 broadcast_select_fusion
  15.3 2.8 %fusion.6 = (bf16[2,512,20,64]{1,3,2,0:T(8,128)(2,1)}, bf16[2,512,20,64]{1,3,2,0:T(8,128)(2,1)S(1)}) fusion(bf16[2,512,20,64]{1,3,2,0:T(8,128)(2,1)S(1)} %bitcast.122, f32[2,512,20]{1,2,0:T(8,128)S(1)} %copy.144), kind=kLoop, calls=%fused_computation.11 | loop fusion | flops 7864320 | bytes 7946240 | tf_op jit(solution)/shard_map/convert_element_type | solution.py:11
  18.1 0.8 convolution_bitcast_fusion
  19.0 1.9 %collective-permute-done.1 = f32[40]{0:T(128)S(1)} collective-permute-done((f32[40]{0:T(128)S(1)}, f32[40]{0:T(128)S(1)}, u32[]{:S(2)}, u32[]{:S(2)}) %collective-permute-start.1) | collective-permute-done | bytes 192 | tf_op jit(solution)/shard_map/ppermute | solution.py:35
  20.8 4.4 %copy.152 = bf16[2,512,1280]{1,2,0:T(8,128)(2,1)} copy(bf16[2,512,1280]{2,1,0:T(8,128)(2,1)} %param.12) | data formatting | bytes 5242880 | tf_op jit(solution)/shard_map/optimization_barrier | solution.py:34
  25.3 1.1 copy.153
  26.3 1.3 %collective-permute-start.9 = (f32[40]{0:T(128)S(1)}, f32[40]{0:T(128)S(1)}, u32[]{:S(2)}, u32[]{:S(2)}) collective-permute-start(f32[40]{0:T(128)S(1)} %add.80), channel_id=1, source_target_pairs={{4,0},{5,1},{6,2},{7,3},{8,4},{9,5},{10,6},{11,7},{12,8},{13,9},{1... | collective-permute-start | bytes 488 | tf_op jit(solution)/shard_map/ppermute | solution.py:35
  27.7 1.4 %fusion.29 = f32[2,512,512]{2,1,0:T(8,128)S(1)} fusion(bf16[2,512,128]{2,1,0:T(8,128)(2,1)S(1)} %copy-done, bf16[2,512,128]{2,1,0:T(8,128)(2,1)} %param.13), kind=kOutput, calls=%fused_computation.82 | convolution fusion | flops 134217728 | bytes 2621440 | tf_op jit(solution)/shard_map/ctn,csn->cts/dot_general | solution.py:132
  29.1 1.4 %fusion.7 = (bf16[2,512,20,64]{1,3,2,0:T(8,128)(2,1)S(1)}, bf16[2,512,20,64]{1,3,2,0:T(8,128)(2,1)S(1)}) fusion(bf16[2,512,20,64]{1,3,2,0:T(8,128)(2,1)S(1)} %bitcast.124, f32[2,512,20]{1,2,0:T(8,128)S(1)} %copy.153), kind=kLoop, calls=%fused_computation.12 | loop fusion | flops 7864320 | bytes 7946240 | tf_op jit(solution)/shard_map/convert_element_type | solution.py:11
  30.6 3.0 %collective-permute-done.9 = f32[40]{0:T(128)S(1)} collective-permute-done((f32[40]{0:T(128)S(1)}, f32[40]{0:T(128)S(1)}, u32[]{:S(2)}, u32[]{:S(2)}) %collective-permute-start.9) | collective-permute-done | bytes 192 | tf_op jit(solution)/shard_map/ppermute | solution.py:35
  33.6 1.3 %collective-permute-start.10 = (f32[40]{0:T(128)S(1)}, f32[40]{0:T(128)S(1)}, u32[]{:S(2)}, u32[]{:S(2)}) collective-permute-start(f32[40]{0:T(128)S(1)} %add.84), channel_id=1, source_target_pairs={{8,0},{9,1},{10,2},{11,3},{12,4},{13,5},{14,6},{15,7},{24,16},{25,... | collective-permute-start | bytes 488 | tf_op jit(solution)/shard_map/ppermute | solution.py:35
  34.8 1.5 %collective-permute-start.2 = (f32[4,20,8,128]{3,2,1,0:T(8,128)S(1)}, f32[4,20,8,128]{3,2,1,0:T(8,128)S(1)}, u32[]{:S(2)}, u32[]{:S(2)}) collective-permute-start(f32[4,20,8,128]{3,2,1,0:T(8,128)S(1)} %bitcast.143), channel_id=1, source_target_pairs={{0,2},{2,0},{4,6},{6,4},{8,10},{10,8},{12,14},{14,12},{1,3},{3,1},... | collective-permute-start | bytes 983048 | tf_op jit(solution)/shard_map/ppermute | solution.py:65
  36.4 3.5 %collective-permute-done.10 = f32[40]{0:T(128)S(1)} collective-permute-done((f32[40]{0:T(128)S(1)}, f32[40]{0:T(128)S(1)}, u32[]{:S(2)}, u32[]{:S(2)}) %collective-permute-start.10) | collective-permute-done | bytes 192 | tf_op jit(solution)/shard_map/ppermute | solution.py:35
  40.0 1.0 fusion.17
  41.1 2.8 %collective-permute-done.2 = f32[4,20,8,128]{3,2,1,0:T(8,128)S(1)} collective-permute-done((f32[4,20,8,128]{3,2,1,0:T(8,128)S(1)}, f32[4,20,8,128]{3,2,1,0:T(8,128)S(1)}, u32[]{:S(2)}, u32[]{:S(2)}) %collective-permute-start.2) | collective-permute-done | bytes 327712 | tf_op jit(solution)/shard_map/ppermute | solution.py:65
  43.9 2.5 %collective-permute-start.3 = (f32[2,20,8,128]{3,2,1,0:T(8,128)S(1)}, f32[2,20,8,128]{3,2,1,0:T(8,128)S(1)}, u32[]{:S(2)}, u32[]{:S(2)}) collective-permute-start(f32[2,20,8,128]{3,2,1,0:T(8,128)S(1)} %slice_select_fusion.6), channel_id=1, source_target_pairs={{0,4},{2,6},{4,0},{6,2},{8,12},{10,14},{12,8},{14,10},{1,5},{3,7},... | collective-permute-start | bytes 491528 | tf_op jit(solution)/shard_map/ppermute | solution.py:65
  46.6 3.1 %collective-permute-done.3 = f32[2,20,8,128]{3,2,1,0:T(8,128)S(1)} collective-permute-done((f32[2,20,8,128]{3,2,1,0:T(8,128)S(1)}, f32[2,20,8,128]{3,2,1,0:T(8,128)S(1)}, u32[]{:S(2)}, u32[]{:S(2)}) %collective-permute-start.3) | collective-permute-done | bytes 163872 | tf_op jit(solution)/shard_map/ppermute | solution.py:65
  49.8 3.3 %collective-permute-start.4 = (f32[1,20,8,128]{3,2,1,0:T(8,128)S(1)}, f32[1,20,8,128]{3,2,1,0:T(8,128)S(1)}, u32[]{:S(2)}, u32[]{:S(2)}) collective-permute-start(f32[1,20,8,128]{3,2,1,0:T(8,128)S(1)} %slice_select_fusion.8), channel_id=1, source_target_pairs={{0,8},{2,10},{4,12},{6,14},{8,0},{10,2},{12,4},{14,6},{1,9},{3,11}... | collective-permute-start | bytes 245768 | tf_op jit(solution)/shard_map/ppermute | solution.py:65
  53.2 2.4 %collective-permute-done.4 = f32[1,20,8,128]{3,2,1,0:T(8,128)S(1)} collective-permute-done((f32[1,20,8,128]{3,2,1,0:T(8,128)S(1)}, f32[1,20,8,128]{3,2,1,0:T(8,128)S(1)}, u32[]{:S(2)}, u32[]{:S(2)}) %collective-permute-start.4) | collective-permute-done | bytes 81952 | tf_op jit(solution)/shard_map/ppermute | solution.py:65
  55.6 3.0 %collective-permute-start.5 = (bf16[1,20,8,128]{3,2,1,0:T(8,128)(2,1)S(1)}, bf16[1,20,8,128]{3,2,1,0:T(8,128)(2,1)S(1)}, u32[]{:S(2)}, u32[]{:S(2)}) collective-permute-start(bf16[1,20,8,128]{3,2,1,0:T(8,128)(2,1)S(1)} %add_convert_fusion.1), channel_id=1, source_target_pairs={{0,8},{2,10},{4,12},{6,14},{8,0},{10,2},{12,4},{14,6},{1,9},{3,11}... | collective-permute-start | bytes 122888 | tf_op jit(solution)/shard_map/ppermute | solution.py:76
  58.8 1.9 %collective-permute-done.5 = bf16[1,20,8,128]{3,2,1,0:T(8,128)(2,1)S(1)} collective-permute-done((bf16[1,20,8,128]{3,2,1,0:T(8,128)(2,1)S(1)}, bf16[1,20,8,128]{3,2,1,0:T(8,128)(2,1)S(1)}, u32[]{:S(2)}, u32[]{:S(2)}) %collective-permute-start.5) | collective-permute-done | bytes 40992 | tf_op jit(solution)/shard_map/ppermute | solution.py:76
  60.7 3.2 %collective-permute-start.6 = (bf16[2,20,8,128]{3,2,1,0:T(8,128)(2,1)S(1)}, bf16[2,20,8,128]{3,2,1,0:T(8,128)(2,1)S(1)}, u32[]{:S(2)}, u32[]{:S(2)}) collective-permute-start(bf16[2,20,8,128]{3,2,1,0:T(8,128)(2,1)S(1)} %maximum_select_fusion.7), channel_id=1, source_target_pairs={{0,4},{2,6},{4,0},{6,2},{8,12},{10,14},{12,8},{14,10},{1,5},{3,7},... | collective-permute-start | bytes 245768 | tf_op jit(solution)/shard_map/ppermute | solution.py:76
  64.3 0.9 collective-permute-start.12
  65.2 1.6 %fusion.31 = f32[2,512,512]{2,1,0:T(8,128)S(1)} fusion(bf16[2,512,1280]{1,2,0:T(8,128)(2,1)S(1)} %bitcast.119, bf16[2,512,1280]{1,2,0:T(8,128)(2,1)S(1)} %bitcast.129), kind=kOutput, calls=%fused_computation.84 | convolution fusion | flops 1342177280 | bytes 7340032 | tf_op jit(solution)/shard_map/ctk,csk->cts/dot_general | solution.py:179
  66.8 1.6 %fusion.30 = f32[2,512,512]{2,1,0:T(8,128)S(1)} fusion(bf16[2,512,1280]{1,2,0:T(8,128)(2,1)S(1)} %bitcast.120, bf16[2,512,1280]{1,2,0:T(8,128)(2,1)S(1)} %bitcast.126), kind=kOutput, calls=%fused_computation.83 | convolution fusion | flops 1342177280 | bytes 7340032 | tf_op jit(solution)/shard_map/ctk,csk->cts/dot_general | solution.py:179
  68.5 7.4 %fusion.15 = bf16[2,20,64,512]{3,2,1,0:T(8,128)(2,1)} fusion(bf16[2,512,20,64]{1,3,2,0:T(8,128)(2,1)S(1)} %bitcast.123, f32[2,20,512]{2,1,0:T(8,128)S(1)} %copy.159, f32[2,20,512]{2,1,0:T(8,128)S(1)} %copy.158, f32[2,512,512]{2,1,0:T(8,128)S(1)} %fusion.29, pred[512,512]{1,0:T(8,128)(4,1)S(1)} %iota_compare_fusion), kind=kOutput, calls=%fused_computation.26 | convolution fusion | flops 1385431040 | bytes 7766016 | tf_op jit(solution)/shard_map/chts,cthp->cshp/dot_general | solution.py:197
  76.0 1.8 %add_select_fusion = f32[2,512,512]{2,1,0:T(8,128)S(1)} fusion(f32[2,512,512]{2,1,0:T(8,128)S(1)} %fusion.30, f32[2,512,512]{2,1,0:T(8,128)S(1)} %fusion.31, bf16[2,512,1280]{1,2,0:T(8,128)(2,1)S(1)} %bitcast.125, bf16[2,512,1280]{1,2,0:T(8,128)(2,1)S(1)} %bitcast.127, pred[512,512]{1,0:T(8,128)(4,1)S(1)} %iota_compare_fusion), kind=kOutput, calls=%fused_computation.25 | convolution fusion | flops 1343750144 | bytes 11796480 | tf_op jit(solution)/shard_map/ctk,csk->cts/dot_general | solution.py:179
  77.9 1.3 %fusion.33 = f32[2,512,128]{1,2,0:T(8,128)S(1)} fusion(f32[2,512,512]{2,1,0:T(8,128)S(1)} %add_select_fusion, bf16[2,512,128]{2,1,0:T(8,128)(2,1)S(1)} %copy-done.9), kind=kOutput, calls=%fused_computation.86 | convolution fusion | flops 805306368 | bytes 2883584 | tf_op jit(solution)/shard_map/cts,csn->ctn/dot_general | solution.py:189
  79.2 4.2 %collective-permute-done.13 = f32[2,20,8,128]{3,2,1,0:T(8,128)S(1)} collective-permute-done((f32[2,20,8,128]{3,2,1,0:T(8,128)S(1)}, f32[2,20,8,128]{3,2,1,0:T(8,128)S(1)}, u32[]{:S(2)}, u32[]{:S(2)}) %collective-permute-start.13) | collective-permute-done | bytes 163872 | tf_op jit(solution)/shard_map/ppermute | solution.py:65
  83.5 3.2 %collective-permute-start.14 = (f32[1,20,8,128]{3,2,1,0:T(8,128)S(1)}, f32[1,20,8,128]{3,2,1,0:T(8,128)S(1)}, u32[]{:S(2)}, u32[]{:S(2)}) collective-permute-start(f32[1,20,8,128]{3,2,1,0:T(8,128)S(1)} %slice_select_fusion.7), channel_id=1, source_target_pairs={{0,8},{2,10},{4,12},{6,14},{8,0},{10,2},{12,4},{14,6},{1,9},{3,11}... | collective-permute-start | bytes 245768 | tf_op jit(solution)/shard_map/ppermute | solution.py:65
  86.7 0.7 maximum_select_fusion.3
  87.4 0.9 collective-permute-start.7
  88.2 1.7 %collective-permute-done.14 = f32[1,20,8,128]{3,2,1,0:T(8,128)S(1)} collective-permute-done((f32[1,20,8,128]{3,2,1,0:T(8,128)S(1)}, f32[1,20,8,128]{3,2,1,0:T(8,128)S(1)}, u32[]{:S(2)}, u32[]{:S(2)}) %collective-permute-start.14) | collective-permute-done | bytes 81952 | tf_op jit(solution)/shard_map/ppermute | solution.py:65
  89.9 2.2 %collective-permute-start.15 = (bf16[1,20,8,128]{3,2,1,0:T(8,128)(2,1)S(1)}, bf16[1,20,8,128]{3,2,1,0:T(8,128)(2,1)S(1)}, u32[]{:S(2)}, u32[]{:S(2)}) collective-permute-start(bf16[1,20,8,128]{3,2,1,0:T(8,128)(2,1)S(1)} %add_convert_fusion), channel_id=1, source_target_pairs={{0,8},{2,10},{4,12},{6,14},{8,0},{10,2},{12,4},{14,6},{1,9},{3,11}... | collective-permute-start | bytes 122888 | tf_op jit(solution)/shard_map/ppermute | solution.py:76
  92.1 1.7 %fusion.32 = f32[2,512,128]{1,2,0:T(8,128)} fusion(f32[2,512,512]{2,1,0:T(8,128)S(1)} %add_select_fusion, bf16[2,512,128]{2,1,0:T(8,128)(2,1)S(1)} %copy-done), kind=kOutput, calls=%fused_computation.85 | convolution fusion | flops 805306368 | bytes 2883584 | tf_op jit(solution)/shard_map/cts,ctn->csn/dot_general | solution.py:186
  93.8 4.4 %copy.179 = bf16[2,512,1280]{2,1,0:T(8,128)(2,1)} copy(bf16[2,512,1280]{1,2,0:T(8,128)(2,1)} %bitcast.130) | data formatting | bytes 5242880
  98.3 1.2 %maximum_select_fusion.1 = bf16[8,20,8,128]{3,2,1,0:T(8,128)(2,1)S(1)} fusion(bf16[4,20,8,128]{3,2,1,0:T(8,128)(2,1)} %maximum_select_fusion.3, bf16[4,20,8,128]{3,2,1,0:T(8,128)(2,1)} %collective-permute-done.7, pred[]{:T(512)S(6)} %eq.35), kind=kLoop, calls=%fused_computation.38 | loop fusion | flops 491520 | bytes 655361 | tf_op jit(solution)/shard_map/jit(_where)/select_n | solution.py:78
  99.6 3.2 %collective-permute-done.16 = bf16[2,20,8,128]{3,2,1,0:T(8,128)(2,1)S(1)} collective-permute-done((bf16[2,20,8,128]{3,2,1,0:T(8,128)(2,1)S(1)}, bf16[2,20,8,128]{3,2,1,0:T(8,128)(2,1)S(1)}, u32[]{:S(2)}, u32[]{:S(2)}) %collective-permute-start.16) | collective-permute-done | bytes 81952 | tf_op jit(solution)/shard_map/ppermute | solution.py:76
  102.7 0.9 collective-permute-start.17
  103.7 0.8 copy_bitcast_fusion
  104.5 3.6 %collective-permute-done.17 = bf16[4,20,8,128]{3,2,1,0:T(8,128)(2,1)S(1)} collective-permute-done((bf16[4,20,8,128]{3,2,1,0:T(8,128)(2,1)S(1)}, bf16[4,20,8,128]{3,2,1,0:T(8,128)(2,1)S(1)}, u32[]{:S(2)}, u32[]{:S(2)}) %collective-permute-start.17) | collective-permute-done | bytes 163872 | tf_op jit(solution)/shard_map/ppermute | solution.py:76
  108.3 0.6 convolution_add_fusion
  108.9 0.3 copy-done.5
  109.3 0.7 reshape.220
  110.0 0.8 fusion.27
  110.8 0.3 copy.194
  111.2 0.3 copy.195
  111.5 0.9 select_bitcast_fusion
  112.5 2.2 %fusion.8 = f32[256,128]{0,1:T(8,128)S(1)} fusion(f32[256,40]{0,1:T(8,128)S(1)} %fusion.21, bf16[256,40,64]{0,2,1:T(8,128)(2,1)S(1)} %bitcast.135, bf16[20,64,128]{2,1,0:T(8,128)(2,1)} %collective-permute-done.8, bf16[20,64,128]{2,1,0:T(8,128)(2,1)} %copy_bitcast_fusion, pred[]{:T(512)S(6)} %eq.34), kind=kOutput, calls=%fused_computation.15 | convolution fusion | flops 171343872 | bytes 2138113 | tf_op jit(solution)/shard_map/jhp,hpn->jhn/dot_general | solution.py:219
  114.6 0.8 copy.178
  115.4 1.8 %fusion.16 = bf16[40,64,256]{2,1,0:T(8,128)(2,1)S(1)} fusion(f32[256,128]{0,1:T(8,128)S(1)} %copy-done.16, f32[256,40]{0,1:T(8,128)S(1)} %fusion.21, bf16[20,64,128]{2,1,0:T(8,128)(2,1)} %collective-permute-done.8, bf16[20,64,128]{2,1,0:T(8,128)(2,1)} %copy_bitcast_fusion, pred[]{:T(512)S(6)} %eq.34), kind=kOutput, calls=%fused_computation.27 | convolution fusion | flops 172032000 | bytes 2138113 | tf_op jit(solution)/shard_map/jhn,hpn->jhp/dot_general | solution.py:215
  117.2 1.6 %copy.177 = bf16[256,2560]{1,0:T(8,128)(2,1)} copy(bf16[256,2560]{0,1:T(8,128)(2,1)S(1)} %bitcast.136) | data formatting | bytes 2621440
  118.9 0.8 fusion.28
  (105 shorter events, 2.5 us)
Async XLA Ops:
  0.6 17.5 %copy-start = (bf16[2,512,128]{2,1,0:T(8,128)(2,1)S(1)}, bf16[2,512,128]{2,1,0:T(8,128)(2,1)}, u32[]{:S(2)}) copy-start(bf16[2,512,128]{2,1,0:T(8,128)(2,1)} %param.14) | copy-start | bytes 786436
  0.6 7.8 %copy-start.6 = (bf16[256,2560]{1,0:T(8,128)(2,1)S(1)}, bf16[256,2560]{1,0:T(8,128)(2,1)}, u32[]{:S(2)}) copy-start(bf16[256,2560]{1,0:T(8,128)(2,1)} %param.9) | copy-start | bytes 3932164
  0.7 9.2 %copy-start.17 = (bf16[256,128]{1,0:T(8,128)(2,1)S(1)}, bf16[256,128]{1,0:T(8,128)(2,1)}, u32[]{:S(2)}) copy-start(bf16[256,128]{1,0:T(8,128)(2,1)} %param.10) | copy-start | bytes 196612
  1.7 9.0 %collective-permute-start = (f32[40]{0:T(128)S(1)}, f32[40]{0:T(128)S(1)}, u32[]{:S(2)}, u32[]{:S(2)}) collective-permute-start(f32[40]{0:T(128)S(1)} %get-tuple-element.36), channel_id=1, source_target_pairs={{1,0},{2,1},{3,2},{4,3},{5,4},{6,5},{7,6},{8,7},{9,8},{10,9},{11,1... | collective-permute-start | bytes 488 | tf_op jit(solution)/shard_map/ppermute | solution.py:35
  6.9 6.9 %copy-start.10 = (f32[2,20,512]{2,0,1:T(2,128)}, f32[2,20,512]{2,0,1:T(2,128)S(1)}, u32[]{:S(2)}) copy-start(f32[2,20,512]{2,0,1:T(2,128)S(1)} %exp.25) | copy-start | bytes 245764
  8.3 2.4 %copy-start.13 = (f32[40,2,128]{2,0,1:T(8,128)}, f32[40,2,128]{2,0,1:T(8,128)S(1)}, u32[]{:S(2)}) copy-start(f32[40,2,128]{2,0,1:T(8,128)S(1)} %reduce-window.16) | copy-start | bytes 122884
  8.5 5.3 %copy-start.18 = (f32[40,3]{0,1:T(4,128)}, f32[40,3]{0,1:T(4,128)S(1)}, u32[]{:S(2)}) copy-start(f32[40,3]{0,1:T(4,128)S(1)} %reduce-window.19) | copy-start | bytes 1444
  10.7 3.0 %copy-start.19 = (s32[2]{0:T(128)S(1)}, s32[2]{0:T(128)}, u32[]{:S(2)}) copy-start(s32[2]{0:T(128)} %param.16) | copy-start | bytes 28
  13.8 7.0 %collective-permute-start.1 = (f32[40]{0:T(128)S(1)}, f32[40]{0:T(128)S(1)}, u32[]{:S(2)}, u32[]{:S(2)}) collective-permute-start(f32[40]{0:T(128)S(1)} %add.79), channel_id=1, source_target_pairs={{2,0},{3,1},{4,2},{5,3},{6,4},{7,5},{8,6},{9,7},{10,8},{11,9},{12,... | collective-permute-start | bytes 488 | tf_op jit(solution)/shard_map/ppermute | solution.py:35
  15.3 2.8 %copy-start.1 = (bf16[2,512,1280]{1,2,0:T(8,128)(2,1)}, bf16[2,512,1280]{1,2,0:T(8,128)(2,1)S(1)}, u32[]{:S(2)}) copy-start(bf16[2,512,1280]{1,2,0:T(8,128)(2,1)S(1)} %broadcast_select_fusion) | copy-start | bytes 7864324
  25.3 3.8 %copy-start.3 = (bf16[2,512,1280]{1,2,0:T(8,128)(2,1)S(1)}, bf16[2,512,1280]{1,2,0:T(8,128)(2,1)}, u32[]{:S(2)}) copy-start(bf16[2,512,1280]{1,2,0:T(8,128)(2,1)} %copy.152) | copy-start | bytes 7864324
  26.3 7.2 %collective-permute-start.9 = (f32[40]{0:T(128)S(1)}, f32[40]{0:T(128)S(1)}, u32[]{:S(2)}, u32[]{:S(2)}) collective-permute-start(f32[40]{0:T(128)S(1)} %add.80), channel_id=1, source_target_pairs={{4,0},{5,1},{6,2},{7,3},{8,4},{9,5},{10,6},{11,7},{12,8},{13,9},{1... | collective-permute-start | bytes 488 | tf_op jit(solution)/shard_map/ppermute | solution.py:35
  30.4 9.5 %copy-start.14 = (f32[40,2,128]{2,0,1:T(8,128)S(1)}, f32[40,2,128]{2,0,1:T(8,128)}, u32[]{:S(2)}) copy-start(f32[40,2,128]{2,0,1:T(8,128)} %copy-done.13) | copy-start | bytes 122884
  30.4 9.4 %slice-start = ((f32[40,3]{0,1:T(4,128)}), f32[40,2]{0,1:T(2,128)S(1)}, s32[]{:S(2)}) async-start(f32[40,3]{0,1:T(4,128)} %copy-done.18), calls=%async_computation | async-start | bytes 2048 | tf_op jit(solution)/shard_map/slice.3
  30.4 9.5 %copy-start.7 = (bf16[256,2560]{0,1:T(8,128)(2,1)S(1)}, bf16[256,2560]{0,1:T(8,128)(2,1)}, u32[]{:S(2)}) copy-start(bf16[256,2560]{0,1:T(8,128)(2,1)} %copy.156) | copy-start | bytes 3932164
  30.5 9.5 %copy-start.15 = (f32[256,128]{0,1:T(8,128)S(1)}, f32[256,128]{0,1:T(8,128)}, u32[]{:S(2)}) copy-start(f32[256,128]{0,1:T(8,128)} %copy.154) | copy-start | bytes 393220
  33.6 6.3 %collective-permute-start.10 = (f32[40]{0:T(128)S(1)}, f32[40]{0:T(128)S(1)}, u32[]{:S(2)}, u32[]{:S(2)}) collective-permute-start(f32[40]{0:T(128)S(1)} %add.84), channel_id=1, source_target_pairs={{8,0},{9,1},{10,2},{11,3},{12,4},{13,5},{14,6},{15,7},{24,16},{25,... | collective-permute-start | bytes 488 | tf_op jit(solution)/shard_map/ppermute | solution.py:35
  34.8 9.0 %collective-permute-start.2 = (f32[4,20,8,128]{3,2,1,0:T(8,128)S(1)}, f32[4,20,8,128]{3,2,1,0:T(8,128)S(1)}, u32[]{:S(2)}, u32[]{:S(2)}) collective-permute-start(f32[4,20,8,128]{3,2,1,0:T(8,128)S(1)} %bitcast.143), channel_id=1, source_target_pairs={{0,2},{2,0},{4,6},{6,4},{8,10},{10,8},{12,14},{14,12},{1,3},{3,1},... | collective-permute-start | bytes 983048 | tf_op jit(solution)/shard_map/ppermute | solution.py:65
  41.0 17.7 %copy-start.11 = (f32[2,20,512]{2,0,1:T(2,128)S(1)}, f32[2,20,512]{2,0,1:T(2,128)}, u32[]{:S(2)}) copy-start(f32[2,20,512]{2,0,1:T(2,128)} %copy-done.10) | copy-start | bytes 245764
  41.1 17.7 %copy-start.12 = (f32[2,20,512]{2,0,1:T(2,128)S(1)}, f32[2,20,512]{2,0,1:T(2,128)}, u32[]{:S(2)}) copy-start(f32[2,20,512]{2,0,1:T(2,128)} %exp.28) | copy-start | bytes 245764
  43.9 5.8 %collective-permute-start.3 = (f32[2,20,8,128]{3,2,1,0:T(8,128)S(1)}, f32[2,20,8,128]{3,2,1,0:T(8,128)S(1)}, u32[]{:S(2)}, u32[]{:S(2)}) collective-permute-start(f32[2,20,8,128]{3,2,1,0:T(8,128)S(1)} %slice_select_fusion.6), channel_id=1, source_target_pairs={{0,4},{2,6},{4,0},{6,2},{8,12},{10,14},{12,8},{14,10},{1,5},{3,7},... | collective-permute-start | bytes 491528 | tf_op jit(solution)/shard_map/ppermute | solution.py:65
  46.6 17.4 %collective-permute-start.11 = (f32[20,64,128]{2,1,0:T(8,128)S(1)}, f32[20,64,128]{2,1,0:T(8,128)S(1)}, u32[]{:S(2)}, u32[]{:S(2)}) collective-permute-start(f32[20,64,128]{2,1,0:T(8,128)S(1)} %slice_select_fusion), channel_id=1, source_target_pairs={{0,1},{1,0},{2,3},{3,2},{4,5},{5,4},{6,7},{7,6},{8,9},{9,8},{10,11... | collective-permute-start | bytes 1966088 | tf_op jit(solution)/shard_map/ppermute | solution.py:100
  49.8 5.7 %collective-permute-start.4 = (f32[1,20,8,128]{3,2,1,0:T(8,128)S(1)}, f32[1,20,8,128]{3,2,1,0:T(8,128)S(1)}, u32[]{:S(2)}, u32[]{:S(2)}) collective-permute-start(f32[1,20,8,128]{3,2,1,0:T(8,128)S(1)} %slice_select_fusion.8), channel_id=1, source_target_pairs={{0,8},{2,10},{4,12},{6,14},{8,0},{10,2},{12,4},{14,6},{1,9},{3,11}... | collective-permute-start | bytes 245768 | tf_op jit(solution)/shard_map/ppermute | solution.py:65
  55.6 5.1 %collective-permute-start.5 = (bf16[1,20,8,128]{3,2,1,0:T(8,128)(2,1)S(1)}, bf16[1,20,8,128]{3,2,1,0:T(8,128)(2,1)S(1)}, u32[]{:S(2)}, u32[]{:S(2)}) collective-permute-start(bf16[1,20,8,128]{3,2,1,0:T(8,128)(2,1)S(1)} %add_convert_fusion.1), channel_id=1, source_target_pairs={{0,8},{2,10},{4,12},{6,14},{8,0},{10,2},{12,4},{14,6},{1,9},{3,11}... | collective-permute-start | bytes 122888 | tf_op jit(solution)/shard_map/ppermute | solution.py:76
  60.7 26.0 %collective-permute-start.6 = (bf16[2,20,8,128]{3,2,1,0:T(8,128)(2,1)S(1)}, bf16[2,20,8,128]{3,2,1,0:T(8,128)(2,1)S(1)}, u32[]{:S(2)}, u32[]{:S(2)}) collective-permute-start(bf16[2,20,8,128]{3,2,1,0:T(8,128)(2,1)S(1)} %maximum_select_fusion.7), channel_id=1, source_target_pairs={{0,4},{2,6},{4,0},{6,2},{8,12},{10,14},{12,8},{14,10},{1,5},{3,7},... | collective-permute-start | bytes 245768 | tf_op jit(solution)/shard_map/ppermute | solution.py:76
  64.3 13.5 %collective-permute-start.12 = (f32[4,20,8,128]{3,2,1,0:T(8,128)S(1)}, f32[4,20,8,128]{3,2,1,0:T(8,128)S(1)}, u32[]{:S(2)}, u32[]{:S(2)}) collective-permute-start(f32[4,20,8,128]{3,2,1,0:T(8,128)S(1)} %bitcast.144), channel_id=1, source_target_pairs={{0,2},{2,0},{4,6},{6,4},{8,10},{10,8},{12,14},{14,12},{1,3},{3,1},... | collective-permute-start | bytes 983048 | tf_op jit(solution)/shard_map/ppermute | solution.py:65
  66.8 1.7 %copy-start.2 = (bf16[2,512,1280]{1,2,0:T(8,128)(2,1)S(1)}, bf16[2,512,1280]{1,2,0:T(8,128)(2,1)}, u32[]{:S(2)}) copy-start(bf16[2,512,1280]{1,2,0:T(8,128)(2,1)} %copy-done.1) | copy-start | bytes 7864324
  68.5 7.4 %copy-start.4 = (bf16[2,512,20,64]{1,3,2,0:T(8,128)(2,1)S(1)}, bf16[2,512,20,64]{1,3,2,0:T(8,128)(2,1)}, u32[]{:S(2)}) copy-start(bf16[2,512,20,64]{1,3,2,0:T(8,128)(2,1)} %get-tuple-element.65) | copy-start | bytes 7864324
  76.0 2.0 %copy-start.9 = (bf16[2,512,128]{2,1,0:T(8,128)(2,1)S(1)}, bf16[2,512,128]{2,1,0:T(8,128)(2,1)}, u32[]{:S(2)}) copy-start(bf16[2,512,128]{2,1,0:T(8,128)(2,1)} %param.13) | copy-start | bytes 786436
  77.8 5.6 %collective-permute-start.13 = (f32[2,20,8,128]{3,2,1,0:T(8,128)S(1)}, f32[2,20,8,128]{3,2,1,0:T(8,128)S(1)}, u32[]{:S(2)}, u32[]{:S(2)}) collective-permute-start(f32[2,20,8,128]{3,2,1,0:T(8,128)S(1)} %slice_select_fusion.5), channel_id=1, source_target_pairs={{0,4},{2,6},{4,0},{6,2},{8,12},{10,14},{12,8},{14,10},{1,5},{3,7},... | collective-permute-start | bytes 491528 | tf_op jit(solution)/shard_map/ppermute | solution.py:65
  83.5 6.4 %collective-permute-start.14 = (f32[1,20,8,128]{3,2,1,0:T(8,128)S(1)}, f32[1,20,8,128]{3,2,1,0:T(8,128)S(1)}, u32[]{:S(2)}, u32[]{:S(2)}) collective-permute-start(f32[1,20,8,128]{3,2,1,0:T(8,128)S(1)} %slice_select_fusion.7), channel_id=1, source_target_pairs={{0,8},{2,10},{4,12},{6,14},{8,0},{10,2},{12,4},{14,6},{1,9},{3,11}... | collective-permute-start | bytes 245768 | tf_op jit(solution)/shard_map/ppermute | solution.py:65
  87.4 10.9 %collective-permute-start.7 = (bf16[4,20,8,128]{3,2,1,0:T(8,128)(2,1)}, bf16[4,20,8,128]{3,2,1,0:T(8,128)(2,1)}, u32[]{:S(2)}, u32[]{:S(2)}) collective-permute-start(bf16[4,20,8,128]{3,2,1,0:T(8,128)(2,1)} %maximum_select_fusion.3), channel_id=1, source_target_pairs={{0,2},{2,0},{4,6},{6,4},{8,10},{10,8},{12,14},{14,12},{1,3},{3,1},... | collective-permute-start | bytes 491528 | tf_op jit(solution)/shard_map/ppermute | solution.py:76
  89.9 8.3 %collective-permute-start.15 = (bf16[1,20,8,128]{3,2,1,0:T(8,128)(2,1)S(1)}, bf16[1,20,8,128]{3,2,1,0:T(8,128)(2,1)S(1)}, u32[]{:S(2)}, u32[]{:S(2)}) collective-permute-start(bf16[1,20,8,128]{3,2,1,0:T(8,128)(2,1)S(1)} %add_convert_fusion), channel_id=1, source_target_pairs={{0,8},{2,10},{4,12},{6,14},{8,0},{10,2},{12,4},{14,6},{1,9},{3,11}... | collective-permute-start | bytes 122888 | tf_op jit(solution)/shard_map/ppermute | solution.py:76
  98.2 4.5 %collective-permute-start.16 = (bf16[2,20,8,128]{3,2,1,0:T(8,128)(2,1)S(1)}, bf16[2,20,8,128]{3,2,1,0:T(8,128)(2,1)S(1)}, u32[]{:S(2)}, u32[]{:S(2)}) collective-permute-start(bf16[2,20,8,128]{3,2,1,0:T(8,128)(2,1)S(1)} %maximum_select_fusion.8), channel_id=1, source_target_pairs={{0,4},{2,6},{4,0},{6,2},{8,12},{10,14},{12,8},{14,10},{1,5},{3,7},... | collective-permute-start | bytes 245768 | tf_op jit(solution)/shard_map/ppermute | solution.py:76
  102.7 5.4 %collective-permute-start.17 = (bf16[4,20,8,128]{3,2,1,0:T(8,128)(2,1)S(1)}, bf16[4,20,8,128]{3,2,1,0:T(8,128)(2,1)S(1)}, u32[]{:S(2)}, u32[]{:S(2)}) collective-permute-start(bf16[4,20,8,128]{3,2,1,0:T(8,128)(2,1)S(1)} %maximum_select_fusion.4), channel_id=1, source_target_pairs={{0,2},{2,0},{4,6},{6,4},{8,10},{10,8},{12,14},{14,12},{1,3},{3,1},... | collective-permute-start | bytes 491528 | tf_op jit(solution)/shard_map/ppermute | solution.py:76
  104.5 7.9 %collective-permute-start.8 = (bf16[20,64,128]{2,1,0:T(8,128)(2,1)}, bf16[20,64,128]{2,1,0:T(8,128)(2,1)}, u32[]{:S(2)}, u32[]{:S(2)}) collective-permute-start(bf16[20,64,128]{2,1,0:T(8,128)(2,1)} %copy_bitcast_fusion), channel_id=1, source_target_pairs={{0,1},{1,0},{2,3},{3,2},{4,5},{5,4},{6,7},{7,6},{8,9},{9,8},{10,11... | collective-permute-start | bytes 983048 | tf_op jit(solution)/shard_map/ppermute | solution.py:100
  108.2 1.0 copy-start.5
  111.1 1.3 %copy-start.8 = (bf16[256,2560]{0,1:T(8,128)(2,1)S(1)}, bf16[256,2560]{0,1:T(8,128)(2,1)}, u32[]{:S(2)}) copy-start(bf16[256,2560]{0,1:T(8,128)(2,1)} %copy.156) | copy-start | bytes 3932164
  112.4 3.0 %copy-start.16 = (f32[256,128]{0,1:T(8,128)S(1)}, f32[256,128]{0,1:T(8,128)}, u32[]{:S(2)}) copy-start(f32[256,128]{0,1:T(8,128)} %copy.154) | copy-start | bytes 393220
  112.4 6.4 %collective-permute-start.18 = (f32[2,256,256]{2,1,0:T(8,128)}, f32[2,256,256]{2,1,0:T(8,128)S(1)}, u32[]{:S(2)}, u32[]{:S(2)}) collective-permute-start(f32[2,256,256]{2,1,0:T(8,128)} %select_bitcast_fusion), channel_id=1, source_target_pairs={{0,1},{1,0},{2,3},{3,2},{4,5},{5,4},{6,7},{7,6},{8,9},{9,8},{10,11... | collective-permute-start | bytes 1572872 | tf_op jit(solution)/shard_map/ppermute | solution.py:100

commit v12 on v9

--- a/solution.py
+++ b/solution.py
@@ -126,24 +126,24 @@
         dstate = jnp.einsum("cthp,ctn->hpn", decayed_g, c_cand, preferred_element_type=jnp.float32)
         return g_heads, decayed_g, g_low, dstate
 
-    def x_work(x_cand, inverse, c_cand, b_cand):
-        xc_heads = x_cand.reshape(cand_dev, cand_len, half_heads, head_size)
-        x_high, x_low = split_bf16(xc_heads.astype(jnp.float32) * inverse[:, :, :, None])
-        scores = jnp.einsum("ctn,csn->cts", c_cand, b_cand, preferred_element_type=jnp.float32)
-        return x_high, x_low, scores
-
-    inclusive, (levels, g_parts, x_parts) = suffix_sum(
+    def scores_work(c_cand, b_cand):
+        return jnp.einsum("ctn,csn->cts", c_cand, b_cand, preferred_element_type=jnp.float32)
+
+    inclusive, (levels, g_parts, scores) = suffix_sum(
         own_total,
         pre_axes,
         [
             (level_work, lambda done: (code_cand,)),
             (g_work, lambda done: (dy_cand, lengths, done[0][0], c_cand)),
-            (x_work, lambda done: (x_cand, done[0][1], c_cand, b_cand)),
+            (scores_work, lambda done: (c_cand, b_cand)),
         ],
     )
+    inclusive, late = lax.optimization_barrier((inclusive, (g_parts, levels, x_cand)))
+    g_parts, levels, x_late = late
     amplitude, inverse = levels
     g_heads, decayed_g, g_low, dstate = g_parts
-    x_high, x_low, scores = x_parts
+    xc_heads = x_late.reshape(cand_dev, cand_len, half_heads, head_size)
+    x_high, x_low = split_bf16(xc_heads.astype(jnp.float32) * inverse[:, :, :, None])
     later_total = inclusive - own_total
     after_local = own_total[None, :] - jnp.cumsum(log_prefix, axis=0)
     weight = jnp.exp(after_local + later_total[None, :])

time: 114 us -> 121 us (1.061)
  waiting for transfers between devices: 20.6 us -> 27.5 us
  starting transfers between devices: 26 us -> 21.2 us
  matrix products: 21.4 us -> 23.5 us
  other arithmetic: 18.4 us -> 20 us
    ppermute x4, waiting for transfers between devices: 0.01 us -> 7.01 us  [suffix_sum(): value = value + lax.ppermute(value, axis, back)]
    optimization_barrier x4 -> x2, local copies, waits for them, and re-layouts: 8.09 us -> 3.02 us  [suffix_sum(): value, args = lax.optimization_barrier((value, pick(done)))]
    optimization_barrier x0 -> x2, local copies, waits for them, and re-layouts: none -> 4.42 us  [shards(): lax.optimization_barrier((inclusive, (g_parts, levels, x_cand)))]
    ppermute x6, starting transfers between devices: 13.9 us -> 9.61 us  [halving_scatter(): lax.ppermute(give, axis, [(at, at ^ step) for at in range(count)])]
    unnamed x44 -> x48, local copies, waits for them, and re-layouts: 9.33 us -> 11.9 us
    add x3 -> x4, other arithmetic: 1.49 us -> 0.02 us  [suffix_sum(): value = value + lax.ppermute(value, axis, back)]
    dot_general x1, matrix products: 0.44 us -> 1.76 us  [scores_work(): jnp.einsum('ctn,csn->cts', c_cand, b_cand, preferred_element_type=jnp.flo...]
  transfers between devices with their start and end apart: 19 -> 19, of which waited for: 8 -> 10; matrix products, arithmetic and copies ran while one was open for 54% -> 53% of each run, Pallas kernels for 0% -> 0%
where the time goes in v12:
time: 121 us; the launch traced here: 120 us
  waiting for transfers between devices  27.5 us (23%)
  local copies, waits for them, and re-layouts  26.4 us (22%)
  matrix products  23.5 us (19%)
  starting transfers between devices  21.2 us (18%)
  other arithmetic  20 us (17%)
  between operations  1.32 us (1%)
    ppermute x6, waiting for transfers between devices, halving_scatter(): lax.ppermute(give, axis, [(at, at ^ step) for at in range(count)])  13.9 us
    unnamed x48, local copies, waits for them, and re-layouts  11.9 us
    ppermute x6, starting transfers between devices, halving_scatter(): lax.ppermute(give, axis, [(at, at ^ step) for at in range(count)])  9.61 us
    dot_general x1, matrix products, shards(): jnp.einsum('chts,cthp->cshp', kernel, g_heads, preferred_element_type=jnp...  7.31 us
    ppermute x4, waiting for transfers between devices, suffix_sum(): value = value + lax.ppermute(value, axis, back)  7.01 us
    ppermute x6, waiting for transfers between devices, doubling_gather(): other = lax.ppermute(value, axis, [(at, at ^ step) for at in range(count)])  6.54 us
    ppermute x6, starting transfers between devices, doubling_gather(): other = lax.ppermute(value, axis, [(at, at ^ step) for at in range(count)])  6.48 us
    convert_element_type x2, other arithmetic, split_bf16(): low = (value - high).astype(jnp.bfloat16)  5.59 us
  transfers between devices with their start and end apart: 19, of which 10 were waited for; matrix products, arithmetic and copies ran while one was open for 53% of the time, Pallas kernels for 0%

profile of v12, /device:TPU:0, one launch (start us, length us, event | category | flops | bytes accessed | tf_op | source)
XLA Modules:
  0.0 119.9 jit_solution(17976103721754545545)
XLA Ops:
  0.6 0.9 fusion.23
  1.6 1.3 %collective-permute-start = (f32[40]{0:T(128)S(1)}, f32[40]{0:T(128)S(1)}, u32[]{:S(2)}, u32[]{:S(2)}) collective-permute-start(f32[40]{0:T(128)S(1)} %get-tuple-element.33), channel_id=1, source_target_pairs={{1,0},{2,1},{3,2},{4,3},{5,4},{6,5},{7,6},{8,7},{9,8},{10,9},{11,1... | collective-permute-start | bytes 488 | tf_op jit(solution)/shard_map/ppermute | solution.py:35
  2.9 0.8 iota_compare_fusion
  3.7 0.6 reduce-window.16
  4.5 1.0 log-plus-one_bitcast_fusion
  5.7 2.3 %reduce-window.14 = f32[2,20,4,128]{3,1,2,0:T(8,128)S(1)} reduce-window(f32[2,20,4,128]{3,1,2,0:T(8,128)S(1)} %copy.140, f32[]{:T(128)} %constant.108.clone.1), window={size=1x1x1x128 pad=0_0x0_0x0_0x127_0}, to_apply=%region_1.0 | reduce-window | flops 2600960 | bytes 163844 | tf_op jit(solution)/shard_map/reduce-window
  8.4 0.7 exp.28
  9.2 0.7 broadcast_multiply_fusion
  9.9 1.3 %collective-permute-start.1 = (f32[40]{0:T(128)S(1)}, f32[40]{0:T(128)S(1)}, u32[]{:S(2)}, u32[]{:S(2)}) collective-permute-start(f32[40]{0:T(128)S(1)} %add.79), channel_id=1, source_target_pairs={{2,0},{3,1},{4,2},{5,3},{6,4},{7,5},{8,6},{9,7},{10,8},{11,9},{12,... | collective-permute-start | bytes 488 | tf_op jit(solution)/shard_map/ppermute | solution.py:35
  11.3 3.0 %copy.143 = bf16[2,512,1280]{1,2,0:T(8,128)(2,1)S(1)} copy(bf16[2,512,1280]{2,1,0:T(8,128)(2,1)} %param.17) | data formatting | bytes 5242880 | tf_op jit(solution)/shard_map/optimization_barrier | solution.py:34
  14.5 2.8 %fusion.6 = (bf16[2,512,20,64]{1,3,2,0:T(8,128)(2,1)}, bf16[2,512,20,64]{1,3,2,0:T(8,128)(2,1)S(1)}) fusion(bf16[2,512,20,64]{1,3,2,0:T(8,128)(2,1)S(1)} %bitcast.125, f32[2,512,20]{1,2,0:T(8,128)S(1)} %copy.144), kind=kLoop, calls=%fused_computation.11 | loop fusion | flops 7864320 | bytes 7946240 | tf_op jit(solution)/shard_map/convert_element_type | solution.py:11
  17.2 0.8 convolution_bitcast_fusion
  18.1 1.3 %collective-permute-start.2 = (f32[40]{0:T(128)S(1)}, f32[40]{0:T(128)S(1)}, u32[]{:S(2)}, u32[]{:S(2)}) collective-permute-start(f32[40]{0:T(128)S(1)} %add.80), channel_id=1, source_target_pairs={{4,0},{5,1},{6,2},{7,3},{8,4},{9,5},{10,6},{11,7},{12,8},{13,9},{1... | collective-permute-start | bytes 488 | tf_op jit(solution)/shard_map/ppermute | solution.py:35
  19.4 1.8 %fusion.29 = f32[2,512,512]{2,1,0:T(8,128)} fusion(bf16[2,512,128]{2,1,0:T(8,128)(2,1)S(1)} %copy-done, bf16[2,512,128]{2,1,0:T(8,128)(2,1)S(1)} %copy-done.11), kind=kOutput, calls=%fused_computation.81 | convolution fusion | flops 134217728 | bytes 2621440 | tf_op jit(solution)/shard_map/ctn,csn->cts/dot_general | solution.py:130
  21.2 6.0 %collective-permute-done.2 = f32[40]{0:T(128)S(1)} collective-permute-done((f32[40]{0:T(128)S(1)}, f32[40]{0:T(128)S(1)}, u32[]{:S(2)}, u32[]{:S(2)}) %collective-permute-start.2) | collective-permute-done | bytes 192 | tf_op jit(solution)/shard_map/ppermute | solution.py:35
  27.2 1.3 %collective-permute-start.3 = (f32[40]{0:T(128)S(1)}, f32[40]{0:T(128)S(1)}, u32[]{:S(2)}, u32[]{:S(2)}) collective-permute-start(f32[40]{0:T(128)S(1)} %add.81), channel_id=1, source_target_pairs={{8,0},{9,1},{10,2},{11,3},{12,4},{13,5},{14,6},{15,7},{24,16},{25,... | collective-permute-start | bytes 488 | tf_op jit(solution)/shard_map/ppermute | solution.py:35
  28.5 1.6 %copy.152 = f32[256,128]{0,1:T(8,128)} copy(bf16[256,128]{1,0:T(8,128)(2,1)} %param.10) | data formatting | bytes 196608 | tf_op jit(solution)/shard_map/convert_element_type | solution.py:150
  30.1 2.4 %copy.154 = bf16[256,2560]{0,1:T(8,128)(2,1)} copy(bf16[256,2560]{1,0:T(8,128)(2,1)} %param.9) | data formatting | bytes 2621440 | tf_op args[0]
  32.5 1.0 collective-permute-done.3
  33.8 0.8 copy.147
  34.5 1.5 %collective-permute-start.4 = (f32[4,20,8,128]{3,2,1,0:T(8,128)}, f32[4,20,8,128]{3,2,1,0:T(8,128)}, u32[]{:S(2)}, u32[]{:S(2)}) collective-permute-start(f32[4,20,8,128]{3,2,1,0:T(8,128)} %bitcast.14), channel_id=1, source_target_pairs={{0,2},{2,0},{4,6},{6,4},{8,10},{10,8},{12,14},{14,12},{1,3},{3,1},... | collective-permute-start | bytes 983048 | tf_op jit(solution)/shard_map/ppermute | solution.py:65
  36.1 1.0 fusion.17
  37.2 1.2 copy-done.4
  38.3 0.9 slice_select_fusion
  39.3 4.4 %copy.157 = bf16[2,512,1280]{1,2,0:T(8,128)(2,1)} copy(bf16[2,512,1280]{2,1,0:T(8,128)(2,1)} %param.12) | data formatting | bytes 5242880 | tf_op jit(solution)/shard_map/optimization_barrier | solution.py:141
  43.7 2.8 %fusion.7 = (bf16[2,512,1280]{1,2,0:T(8,128)(2,1)S(1)}, bf16[2,512,1280]{1,2,0:T(8,128)(2,1)S(1)}) fusion(bf16[2,512,1280]{1,2,0:T(8,128)(2,1)} %copy.157, f32[2,512,20]{1,2,0:T(8,128)S(1)} %copy.158), kind=kLoop, calls=%fused_computation.12 | loop fusion | flops 7864320 | bytes 7946240 | tf_op jit(solution)/shard_map/convert_element_type | solution.py:11
  46.9 7.3 %fusion.15 = bf16[2,20,64,512]{3,2,1,0:T(8,128)(2,1)} fusion(bf16[2,512,20,64]{1,3,2,0:T(8,128)(2,1)S(1)} %bitcast.126, f32[2,20,512]{2,1,0:T(8,128)S(1)} %copy.156, f32[2,20,512]{2,1,0:T(8,128)S(1)} %copy.155, f32[2,512,512]{2,1,0:T(8,128)S(1)} %copy-done.7, pred[512,512]{1,0:T(8,128)(4,1)S(1)} %copy-done.6), kind=kOutput, calls=%fused_computation.26 | convolution fusion | flops 1385431040 | bytes 7766016 | tf_op jit(solution)/shard_map/chts,cthp->cshp/dot_general | solution.py:193
  54.2 1.6 %fusion.31 = f32[2,512,512]{2,1,0:T(8,128)S(1)} fusion(bf16[2,512,1280]{1,2,0:T(8,128)(2,1)S(1)} %bitcast.122, bf16[2,512,1280]{1,2,0:T(8,128)(2,1)S(1)} %get-tuple-element.86), kind=kOutput, calls=%fused_computation.83 | convolution fusion | flops 1342177280 | bytes 7340032 | tf_op jit(solution)/shard_map/ctk,csk->cts/dot_general | solution.py:175
  55.8 1.0 bitcast_add_fusion.2
  56.8 2.1 %collective-permute-start.5 = (f32[2,20,8,128]{3,2,1,0:T(8,128)S(1)}, f32[2,20,8,128]{3,2,1,0:T(8,128)S(1)}, u32[]{:S(2)}, u32[]{:S(2)}) collective-permute-start(f32[2,20,8,128]{3,2,1,0:T(8,128)S(1)} %slice_select_fusion.6), channel_id=1, source_target_pairs={{0,4},{2,6},{4,0},{6,2},{8,12},{10,14},{12,8},{14,10},{1,5},{3,7},... | collective-permute-start | bytes 491528 | tf_op jit(solution)/shard_map/ppermute | solution.py:65
  58.9 1.6 %fusion.30 = f32[2,512,512]{2,1,0:T(8,128)S(1)} fusion(bf16[2,512,1280]{1,2,0:T(8,128)(2,1)S(1)} %bitcast.123, bf16[2,512,1280]{1,2,0:T(8,128)(2,1)S(1)} %get-tuple-element.87), kind=kOutput, calls=%fused_computation.82 | convolution fusion | flops 1342177280 | bytes 7340032 | tf_op jit(solution)/shard_map/ctk,csk->cts/dot_general | solution.py:175
  60.5 3.3 %collective-permute-done.5 = f32[2,20,8,128]{3,2,1,0:T(8,128)S(1)} collective-permute-done((f32[2,20,8,128]{3,2,1,0:T(8,128)S(1)}, f32[2,20,8,128]{3,2,1,0:T(8,128)S(1)}, u32[]{:S(2)}, u32[]{:S(2)}) %collective-permute-start.5) | collective-permute-done | bytes 163872 | tf_op jit(solution)/shard_map/ppermute | solution.py:65
  63.9 3.3 %collective-permute-start.6 = (f32[1,20,8,128]{3,2,1,0:T(8,128)S(1)}, f32[1,20,8,128]{3,2,1,0:T(8,128)S(1)}, u32[]{:S(2)}, u32[]{:S(2)}) collective-permute-start(f32[1,20,8,128]{3,2,1,0:T(8,128)S(1)} %slice_select_fusion.8), channel_id=1, source_target_pairs={{0,8},{2,10},{4,12},{6,14},{8,0},{10,2},{12,4},{14,6},{1,9},{3,11}... | collective-permute-start | bytes 245768 | tf_op jit(solution)/shard_map/ppermute | solution.py:65
  67.2 1.3 %add_bitcast_fusion = f32[20,8,8,128]{3,2,1,0:T(8,128)S(1)} fusion(f32[20,64,128]{2,1,0:T(8,128)} %collective-permute-done.11, f32[40,64,128]{2,1,0:T(8,128)S(1)} %copy-done.5, pred[]{:T(512)S(6)} %eq.34), kind=kLoop, calls=%fused_computation.34 | loop fusion | flops 327680 | bytes 2621441 | tf_op jit(solution)/shard_map/reshape | solution.py:92
  68.6 0.6 collective-permute-start.12
  69.2 1.8 %add_select_fusion = f32[2,512,512]{2,1,0:T(8,128)S(1)} fusion(f32[2,512,512]{2,1,0:T(8,128)S(1)} %fusion.30, f32[2,512,512]{2,1,0:T(8,128)S(1)} %fusion.31, bf16[2,512,1280]{1,2,0:T(8,128)(2,1)S(1)} %bitcast.127, bf16[2,512,1280]{1,2,0:T(8,128)(2,1)S(1)} %get-tuple-element.87, pred[512,512]{1,0:T(8,128)(4,1)S(1)} %copy-done.6), kind=kOutput, calls=%fused_computation.25 | convolution fusion | flops 1343750144 | bytes 11796480 | tf_op jit(solution)/shard_map/ctk,csk->cts/dot_general | solution.py:175
  71.5 1.1 collective-permute-start.7
  72.6 5.3 %collective-permute-done.12 = f32[4,20,8,128]{3,2,1,0:T(8,128)S(1)} collective-permute-done((f32[4,20,8,128]{3,2,1,0:T(8,128)S(1)}, f32[4,20,8,128]{3,2,1,0:T(8,128)S(1)}, u32[]{:S(2)}, u32[]{:S(2)}) %collective-permute-start.12) | collective-permute-done | bytes 327712 | tf_op jit(solution)/shard_map/ppermute | solution.py:65
  78.0 1.6 %collective-permute-start.13 = (f32[2,20,8,128]{3,2,1,0:T(8,128)S(1)}, f32[2,20,8,128]{3,2,1,0:T(8,128)S(1)}, u32[]{:S(2)}, u32[]{:S(2)}) collective-permute-start(f32[2,20,8,128]{3,2,1,0:T(8,128)S(1)} %slice_select_fusion.5), channel_id=1, source_target_pairs={{0,4},{2,6},{4,0},{6,2},{8,12},{10,14},{12,8},{14,10},{1,5},{3,7},... | collective-permute-start | bytes 491528 | tf_op jit(solution)/shard_map/ppermute | solution.py:65
  79.6 1.3 %fusion.33 = f32[2,512,128]{1,2,0:T(8,128)S(1)} fusion(f32[2,512,512]{2,1,0:T(8,128)S(1)} %add_select_fusion, bf16[2,512,128]{2,1,0:T(8,128)(2,1)S(1)} %copy-done.12), kind=kOutput, calls=%fused_computation.85 | convolution fusion | flops 805306368 | bytes 2883584 | tf_op jit(solution)/shard_map/cts,csn->ctn/dot_general | solution.py:185
  81.4 2.8 %collective-permute-done.13 = f32[2,20,8,128]{3,2,1,0:T(8,128)S(1)} collective-permute-done((f32[2,20,8,128]{3,2,1,0:T(8,128)S(1)}, f32[2,20,8,128]{3,2,1,0:T(8,128)S(1)}, u32[]{:S(2)}, u32[]{:S(2)}) %collective-permute-start.13) | collective-permute-done | bytes 163872 | tf_op jit(solution)/shard_map/ppermute | solution.py:65
  84.8 1.5 %collective-permute-done.8 = bf16[2,20,8,128]{3,2,1,0:T(8,128)(2,1)S(1)} collective-permute-done((bf16[2,20,8,128]{3,2,1,0:T(8,128)(2,1)S(1)}, bf16[2,20,8,128]{3,2,1,0:T(8,128)(2,1)S(1)}, u32[]{:S(2)}, u32[]{:S(2)}) %collective-permute-start.8) | collective-permute-done | bytes 81952 | tf_op jit(solution)/shard_map/ppermute | solution.py:76
  86.3 0.7 maximum_select_fusion.3
  87.0 0.6 collective-permute-start.9
  87.5 2.1 %collective-permute-done.14 = f32[1,20,8,128]{3,2,1,0:T(8,128)S(1)} collective-permute-done((f32[1,20,8,128]{3,2,1,0:T(8,128)S(1)}, f32[1,20,8,128]{3,2,1,0:T(8,128)S(1)}, u32[]{:S(2)}, u32[]{:S(2)}) %collective-permute-start.14) | collective-permute-done | bytes 81952 | tf_op jit(solution)/shard_map/ppermute | solution.py:65
  89.7 0.6 collective-permute-start.15
  90.3 1.7 %fusion.32 = f32[2,512,128]{1,2,0:T(8,128)} fusion(f32[2,512,512]{2,1,0:T(8,128)S(1)} %add_select_fusion, bf16[2,512,128]{2,1,0:T(8,128)(2,1)S(1)} %copy-done), kind=kOutput, calls=%fused_computation.84 | convolution fusion | flops 805306368 | bytes 2883584 | tf_op jit(solution)/shard_map/cts,ctn->csn/dot_general | solution.py:182
  92.0 4.4 %copy.179 = bf16[2,512,1280]{2,1,0:T(8,128)(2,1)} copy(bf16[2,512,1280]{1,2,0:T(8,128)(2,1)} %bitcast.129) | data formatting | bytes 5242880
  96.4 2.9 %collective-permute-start.16 = (bf16[2,20,8,128]{3,2,1,0:T(8,128)(2,1)S(1)}, bf16[2,20,8,128]{3,2,1,0:T(8,128)(2,1)S(1)}, u32[]{:S(2)}, u32[]{:S(2)}) collective-permute-start(bf16[2,20,8,128]{3,2,1,0:T(8,128)(2,1)S(1)} %maximum_select_fusion.8), channel_id=1, source_target_pairs={{0,4},{2,6},{4,0},{6,2},{8,12},{10,14},{12,8},{14,10},{1,5},{3,7},... | collective-permute-start | bytes 245768 | tf_op jit(solution)/shard_map/ppermute | solution.py:76
  99.4 1.2 %maximum_select_fusion.1 = bf16[8,20,8,128]{3,2,1,0:T(8,128)(2,1)S(1)} fusion(bf16[4,20,8,128]{3,2,1,0:T(8,128)(2,1)} %maximum_select_fusion.3, bf16[4,20,8,128]{3,2,1,0:T(8,128)(2,1)} %collective-permute-done.9, pred[]{:T(512)S(6)} %eq.35), kind=kLoop, calls=%fused_computation.38 | loop fusion | flops 491520 | bytes 655361 | tf_op jit(solution)/shard_map/jit(_where)/select_n | solution.py:78
  100.6 1.2 collective-permute-done.16
  101.8 0.6 collective-permute-start.17
  102.4 0.9 copy_bitcast_fusion
  103.3 3.9 %collective-permute-done.17 = bf16[4,20,8,128]{3,2,1,0:T(8,128)(2,1)S(1)} collective-permute-done((bf16[4,20,8,128]{3,2,1,0:T(8,128)(2,1)S(1)}, bf16[4,20,8,128]{3,2,1,0:T(8,128)(2,1)S(1)}, u32[]{:S(2)}, u32[]{:S(2)}) %collective-permute-start.17) | collective-permute-done | bytes 163872 | tf_op jit(solution)/shard_map/ppermute | solution.py:76
  107.4 0.6 convolution_add_fusion
  108.3 0.7 reshape.214
  109.0 0.8 fusion.27
  110.6 0.9 select_bitcast_fusion
  111.5 2.2 %fusion.8 = f32[256,128]{0,1:T(8,128)S(1)} fusion(f32[256,40]{0,1:T(8,128)S(1)} %fusion.21, bf16[256,40,64]{0,2,1:T(8,128)(2,1)S(1)} %bitcast.133, bf16[20,64,128]{2,1,0:T(8,128)(2,1)} %collective-permute-done.10, bf16[20,64,128]{2,1,0:T(8,128)(2,1)} %copy_bitcast_fusion, pred[]{:T(512)S(6)} %eq.34), kind=kOutput, calls=%fused_computation.15 | convolution fusion | flops 171343872 | bytes 2138113 | tf_op jit(solution)/shard_map/jhp,hpn->jhn/dot_general | solution.py:215
  113.7 0.8 copy.178
  114.5 1.8 %fusion.16 = bf16[40,64,256]{2,1,0:T(8,128)(2,1)S(1)} fusion(f32[256,128]{0,1:T(8,128)S(1)} %copy-done.19, f32[256,40]{0,1:T(8,128)S(1)} %fusion.21, bf16[20,64,128]{2,1,0:T(8,128)(2,1)} %collective-permute-done.10, bf16[20,64,128]{2,1,0:T(8,128)(2,1)} %copy_bitcast_fusion, pred[]{:T(512)S(6)} %eq.34), kind=kOutput, calls=%fused_computation.27 | convolution fusion | flops 172032000 | bytes 2138113 | tf_op jit(solution)/shard_map/jhn,hpn->jhp/dot_general | solution.py:211
  116.3 1.6 %copy.177 = bf16[256,2560]{1,0:T(8,128)(2,1)} copy(bf16[256,2560]{0,1:T(8,128)(2,1)S(1)} %bitcast.134) | data formatting | bytes 2621440
  117.9 1.1 bitcast_add_fusion
  119.1 0.8 fusion.28
  (108 shorter events, 5.0 us)
Async XLA Ops:
  0.6 16.6 %copy-start = (bf16[2,512,128]{2,1,0:T(8,128)(2,1)S(1)}, bf16[2,512,128]{2,1,0:T(8,128)(2,1)}, u32[]{:S(2)}) copy-start(bf16[2,512,128]{2,1,0:T(8,128)(2,1)} %param.14) | copy-start | bytes 786436
  1.6 7.6 %collective-permute-start = (f32[40]{0:T(128)S(1)}, f32[40]{0:T(128)S(1)}, u32[]{:S(2)}, u32[]{:S(2)}) collective-permute-start(f32[40]{0:T(128)S(1)} %get-tuple-element.33), channel_id=1, source_target_pairs={{1,0},{2,1},{3,2},{4,3},{5,4},{6,5},{7,6},{8,7},{9,8},{10,9},{11,1... | collective-permute-start | bytes 488 | tf_op jit(solution)/shard_map/ppermute | solution.py:35
  4.3 1.3 %copy-start.16 = (f32[40,2,128]{2,0,1:T(8,128)}, f32[40,2,128]{2,0,1:T(8,128)S(1)}, u32[]{:S(2)}) copy-start(f32[40,2,128]{2,0,1:T(8,128)S(1)} %reduce-window.16) | copy-start | bytes 122884
  4.5 9.8 %copy-start.20 = (f32[40,3]{0,1:T(4,128)}, f32[40,3]{0,1:T(4,128)S(1)}, u32[]{:S(2)}) copy-start(f32[40,3]{0,1:T(4,128)S(1)} %reduce-window.19) | copy-start | bytes 1444
  9.1 2.1 %copy-start.14 = (f32[2,20,512]{2,0,1:T(2,128)}, f32[2,20,512]{2,0,1:T(2,128)S(1)}, u32[]{:S(2)}) copy-start(f32[2,20,512]{2,0,1:T(2,128)S(1)} %exp.25) | copy-start | bytes 245764
  9.9 8.2 %collective-permute-start.1 = (f32[40]{0:T(128)S(1)}, f32[40]{0:T(128)S(1)}, u32[]{:S(2)}, u32[]{:S(2)}) collective-permute-start(f32[40]{0:T(128)S(1)} %add.79), channel_id=1, source_target_pairs={{2,0},{3,1},{4,2},{5,3},{6,4},{7,5},{8,6},{9,7},{10,8},{11,9},{12,... | collective-permute-start | bytes 488 | tf_op jit(solution)/shard_map/ppermute | solution.py:35
  14.5 2.8 %copy-start.1 = (bf16[2,512,1280]{1,2,0:T(8,128)(2,1)}, bf16[2,512,1280]{1,2,0:T(8,128)(2,1)S(1)}, u32[]{:S(2)}) copy-start(bf16[2,512,1280]{1,2,0:T(8,128)(2,1)S(1)} %broadcast_select_fusion) | copy-start | bytes 7864324
  17.2 2.2 %copy-start.11 = (bf16[2,512,128]{2,1,0:T(8,128)(2,1)S(1)}, bf16[2,512,128]{2,1,0:T(8,128)(2,1)}, u32[]{:S(2)}) copy-start(bf16[2,512,128]{2,1,0:T(8,128)(2,1)} %param.13) | copy-start | bytes 786436
  18.1 9.1 %collective-permute-start.2 = (f32[40]{0:T(128)S(1)}, f32[40]{0:T(128)S(1)}, u32[]{:S(2)}, u32[]{:S(2)}) collective-permute-start(f32[40]{0:T(128)S(1)} %add.80), channel_id=1, source_target_pairs={{4,0},{5,1},{6,2},{7,3},{8,4},{9,5},{10,6},{11,7},{12,8},{13,9},{1... | collective-permute-start | bytes 488 | tf_op jit(solution)/shard_map/ppermute | solution.py:35
  27.2 6.3 %collective-permute-start.3 = (f32[40]{0:T(128)S(1)}, f32[40]{0:T(128)S(1)}, u32[]{:S(2)}, u32[]{:S(2)}) collective-permute-start(f32[40]{0:T(128)S(1)} %add.81), channel_id=1, source_target_pairs={{8,0},{9,1},{10,2},{11,3},{12,4},{13,5},{14,6},{15,7},{24,16},{25,... | collective-permute-start | bytes 488 | tf_op jit(solution)/shard_map/ppermute | solution.py:35
  32.5 1.2 copy-start.15
  32.5 1.2 %copy-start.13 = (f32[2,20,512]{2,0,1:T(2,128)S(1)}, f32[2,20,512]{2,0,1:T(2,128)}, u32[]{:S(2)}) copy-start(f32[2,20,512]{2,0,1:T(2,128)} %exp.28) | copy-start | bytes 245764
  32.5 3.5 %copy-start.17 = (f32[40,2,128]{2,0,1:T(8,128)S(1)}, f32[40,2,128]{2,0,1:T(8,128)}, u32[]{:S(2)}) copy-start(f32[40,2,128]{2,0,1:T(8,128)} %copy-done.16) | copy-start | bytes 122884
  32.5 3.5 %slice-start = ((f32[40,3]{0,1:T(4,128)}), f32[40,2]{0,1:T(2,128)S(1)}, s32[]{:S(2)}) async-start(f32[40,3]{0,1:T(4,128)} %copy-done.20), calls=%async_computation | async-start | bytes 2048 | tf_op jit(solution)/shard_map/slice.3
  32.5 3.6 %copy-start.9 = (bf16[256,2560]{0,1:T(8,128)(2,1)S(1)}, bf16[256,2560]{0,1:T(8,128)(2,1)}, u32[]{:S(2)}) copy-start(bf16[256,2560]{0,1:T(8,128)(2,1)} %copy.154) | copy-start | bytes 3932164
  32.5 3.6 %copy-start.18 = (f32[256,128]{0,1:T(8,128)S(1)}, f32[256,128]{0,1:T(8,128)}, u32[]{:S(2)}) copy-start(f32[256,128]{0,1:T(8,128)} %copy.152) | copy-start | bytes 393220
  34.5 21.3 %collective-permute-start.4 = (f32[4,20,8,128]{3,2,1,0:T(8,128)}, f32[4,20,8,128]{3,2,1,0:T(8,128)}, u32[]{:S(2)}, u32[]{:S(2)}) collective-permute-start(f32[4,20,8,128]{3,2,1,0:T(8,128)} %bitcast.14), channel_id=1, source_target_pairs={{0,2},{2,0},{4,6},{6,4},{8,10},{10,8},{12,14},{14,12},{1,3},{3,1},... | collective-permute-start | bytes 983048 | tf_op jit(solution)/shard_map/ppermute | solution.py:65
  37.1 1.2 copy-start.4
  39.2 27.9 %collective-permute-start.11 = (f32[20,64,128]{2,1,0:T(8,128)}, f32[20,64,128]{2,1,0:T(8,128)}, u32[]{:S(2)}, u32[]{:S(2)}) collective-permute-start(f32[20,64,128]{2,1,0:T(8,128)} %slice_select_fusion), channel_id=1, source_target_pairs={{0,1},{1,0},{2,3},{3,2},{4,5},{5,4},{6,7},{7,6},{8,9},{9,8},{10,11... | collective-permute-start | bytes 1966088 | tf_op jit(solution)/shard_map/ppermute | solution.py:100
  43.7 2.8 %copy-start.2 = (bf16[2,512,1280]{1,2,0:T(8,128)(2,1)S(1)}, bf16[2,512,1280]{1,2,0:T(8,128)(2,1)}, u32[]{:S(2)}) copy-start(bf16[2,512,1280]{1,2,0:T(8,128)(2,1)} %copy-done.1) | copy-start | bytes 7864324
  43.7 2.8 %copy-start.6 = (pred[512,512]{1,0:T(8,128)(4,1)S(1)}, pred[512,512]{1,0:T(8,128)(4,1)}, u32[]{:S(2)}) copy-start(pred[512,512]{1,0:T(8,128)(4,1)} %iota_compare_fusion) | copy-start | bytes 786436
  43.7 3.2 %copy-start.7 = (f32[2,512,512]{2,1,0:T(8,128)S(1)}, f32[2,512,512]{2,1,0:T(8,128)}, u32[]{:S(2)}) copy-start(f32[2,512,512]{2,1,0:T(8,128)} %fusion.29) | copy-start | bytes 6291460
  56.8 7.0 %collective-permute-start.5 = (f32[2,20,8,128]{3,2,1,0:T(8,128)S(1)}, f32[2,20,8,128]{3,2,1,0:T(8,128)S(1)}, u32[]{:S(2)}, u32[]{:S(2)}) collective-permute-start(f32[2,20,8,128]{3,2,1,0:T(8,128)S(1)} %slice_select_fusion.6), channel_id=1, source_target_pairs={{0,4},{2,6},{4,0},{6,2},{8,12},{10,14},{12,8},{14,10},{1,5},{3,7},... | collective-permute-start | bytes 491528 | tf_op jit(solution)/shard_map/ppermute | solution.py:65
  58.9 8.2 %copy-start.5 = (f32[40,64,128]{2,1,0:T(8,128)S(1)}, f32[40,64,128]{2,1,0:T(8,128)}, u32[]{:S(2)}) copy-start(f32[40,64,128]{2,1,0:T(8,128)} %copy-done.4) | copy-start | bytes 3932164
  63.8 5.4 %copy-start.3 = (bf16[2,512,20,64]{1,3,2,0:T(8,128)(2,1)S(1)}, bf16[2,512,20,64]{1,3,2,0:T(8,128)(2,1)}, u32[]{:S(2)}) copy-start(bf16[2,512,20,64]{1,3,2,0:T(8,128)(2,1)} %get-tuple-element.60) | copy-start | bytes 7864324
  63.9 7.6 %collective-permute-start.6 = (f32[1,20,8,128]{3,2,1,0:T(8,128)S(1)}, f32[1,20,8,128]{3,2,1,0:T(8,128)S(1)}, u32[]{:S(2)}, u32[]{:S(2)}) collective-permute-start(f32[1,20,8,128]{3,2,1,0:T(8,128)S(1)} %slice_select_fusion.8), channel_id=1, source_target_pairs={{0,8},{2,10},{4,12},{6,14},{8,0},{10,2},{12,4},{14,6},{1,9},{3,11}... | collective-permute-start | bytes 245768 | tf_op jit(solution)/shard_map/ppermute | solution.py:65
  68.6 9.3 %collective-permute-start.12 = (f32[4,20,8,128]{3,2,1,0:T(8,128)S(1)}, f32[4,20,8,128]{3,2,1,0:T(8,128)S(1)}, u32[]{:S(2)}, u32[]{:S(2)}) collective-permute-start(f32[4,20,8,128]{3,2,1,0:T(8,128)S(1)} %bitcast.141), channel_id=1, source_target_pairs={{0,2},{2,0},{4,6},{6,4},{8,10},{10,8},{12,14},{14,12},{1,3},{3,1},... | collective-permute-start | bytes 983048 | tf_op jit(solution)/shard_map/ppermute | solution.py:65
  69.2 10.4 %copy-start.12 = (bf16[2,512,128]{2,1,0:T(8,128)(2,1)S(1)}, bf16[2,512,128]{2,1,0:T(8,128)(2,1)}, u32[]{:S(2)}) copy-start(bf16[2,512,128]{2,1,0:T(8,128)(2,1)} %param.13) | copy-start | bytes 786436
  71.5 9.4 %collective-permute-start.7 = (bf16[1,20,8,128]{3,2,1,0:T(8,128)(2,1)S(1)}, bf16[1,20,8,128]{3,2,1,0:T(8,128)(2,1)S(1)}, u32[]{:S(2)}, u32[]{:S(2)}) collective-permute-start(bf16[1,20,8,128]{3,2,1,0:T(8,128)(2,1)S(1)} %add_convert_fusion.1), channel_id=1, source_target_pairs={{0,8},{2,10},{4,12},{6,14},{8,0},{10,2},{12,4},{14,6},{1,9},{3,11}... | collective-permute-start | bytes 122888 | tf_op jit(solution)/shard_map/ppermute | solution.py:76
  78.0 6.3 %collective-permute-start.13 = (f32[2,20,8,128]{3,2,1,0:T(8,128)S(1)}, f32[2,20,8,128]{3,2,1,0:T(8,128)S(1)}, u32[]{:S(2)}, u32[]{:S(2)}) collective-permute-start(f32[2,20,8,128]{3,2,1,0:T(8,128)S(1)} %slice_select_fusion.5), channel_id=1, source_target_pairs={{0,4},{2,6},{4,0},{6,2},{8,12},{10,14},{12,8},{14,10},{1,5},{3,7},... | collective-permute-start | bytes 491528 | tf_op jit(solution)/shard_map/ppermute | solution.py:65
  80.9 5.4 %collective-permute-start.8 = (bf16[2,20,8,128]{3,2,1,0:T(8,128)(2,1)S(1)}, bf16[2,20,8,128]{3,2,1,0:T(8,128)(2,1)S(1)}, u32[]{:S(2)}, u32[]{:S(2)}) collective-permute-start(bf16[2,20,8,128]{3,2,1,0:T(8,128)(2,1)S(1)} %maximum_select_fusion.7), channel_id=1, source_target_pairs={{0,4},{2,6},{4,0},{6,2},{8,12},{10,14},{12,8},{14,10},{1,5},{3,7},... | collective-permute-start | bytes 245768 | tf_op jit(solution)/shard_map/ppermute | solution.py:76
  84.3 5.4 %collective-permute-start.14 = (f32[1,20,8,128]{3,2,1,0:T(8,128)S(1)}, f32[1,20,8,128]{3,2,1,0:T(8,128)S(1)}, u32[]{:S(2)}, u32[]{:S(2)}) collective-permute-start(f32[1,20,8,128]{3,2,1,0:T(8,128)S(1)} %slice_select_fusion.7), channel_id=1, source_target_pairs={{0,8},{2,10},{4,12},{6,14},{8,0},{10,2},{12,4},{14,6},{1,9},{3,11}... | collective-permute-start | bytes 245768 | tf_op jit(solution)/shard_map/ppermute | solution.py:65
  87.0 12.4 %collective-permute-start.9 = (bf16[4,20,8,128]{3,2,1,0:T(8,128)(2,1)}, bf16[4,20,8,128]{3,2,1,0:T(8,128)(2,1)}, u32[]{:S(2)}, u32[]{:S(2)}) collective-permute-start(bf16[4,20,8,128]{3,2,1,0:T(8,128)(2,1)} %maximum_select_fusion.3), channel_id=1, source_target_pairs={{0,2},{2,0},{4,6},{6,4},{8,10},{10,8},{12,14},{14,12},{1,3},{3,1},... | collective-permute-start | bytes 491528 | tf_op jit(solution)/shard_map/ppermute | solution.py:76
  89.7 6.7 %collective-permute-start.15 = (bf16[1,20,8,128]{3,2,1,0:T(8,128)(2,1)S(1)}, bf16[1,20,8,128]{3,2,1,0:T(8,128)(2,1)S(1)}, u32[]{:S(2)}, u32[]{:S(2)}) collective-permute-start(bf16[1,20,8,128]{3,2,1,0:T(8,128)(2,1)S(1)} %add_convert_fusion), channel_id=1, source_target_pairs={{0,8},{2,10},{4,12},{6,14},{8,0},{10,2},{12,4},{14,6},{1,9},{3,11}... | collective-permute-start | bytes 122888 | tf_op jit(solution)/shard_map/ppermute | solution.py:76
  96.4 5.4 %collective-permute-start.16 = (bf16[2,20,8,128]{3,2,1,0:T(8,128)(2,1)S(1)}, bf16[2,20,8,128]{3,2,1,0:T(8,128)(2,1)S(1)}, u32[]{:S(2)}, u32[]{:S(2)}) collective-permute-start(bf16[2,20,8,128]{3,2,1,0:T(8,128)(2,1)S(1)} %maximum_select_fusion.8), channel_id=1, source_target_pairs={{0,4},{2,6},{4,0},{6,2},{8,12},{10,14},{12,8},{14,10},{1,5},{3,7},... | collective-permute-start | bytes 245768 | tf_op jit(solution)/shard_map/ppermute | solution.py:76
  101.8 5.4 %collective-permute-start.17 = (bf16[4,20,8,128]{3,2,1,0:T(8,128)(2,1)S(1)}, bf16[4,20,8,128]{3,2,1,0:T(8,128)(2,1)S(1)}, u32[]{:S(2)}, u32[]{:S(2)}) collective-permute-start(bf16[4,20,8,128]{3,2,1,0:T(8,128)(2,1)S(1)} %maximum_select_fusion.4), channel_id=1, source_target_pairs={{0,2},{2,0},{4,6},{6,4},{8,10},{10,8},{12,14},{14,12},{1,3},{3,1},... | collective-permute-start | bytes 491528 | tf_op jit(solution)/shard_map/ppermute | solution.py:76
  103.3 8.1 %collective-permute-start.10 = (bf16[20,64,128]{2,1,0:T(8,128)(2,1)}, bf16[20,64,128]{2,1,0:T(8,128)(2,1)}, u32[]{:S(2)}, u32[]{:S(2)}) collective-permute-start(bf16[20,64,128]{2,1,0:T(8,128)(2,1)} %copy_bitcast_fusion), channel_id=1, source_target_pairs={{0,1},{1,0},{2,3},{3,2},{4,5},{5,4},{6,7},{7,6},{8,9},{9,8},{10,11... | collective-permute-start | bytes 983048 | tf_op jit(solution)/shard_map/ppermute | solution.py:100
  107.2 1.0 copy-start.8
  110.2 1.3 %copy-start.10 = (bf16[256,2560]{0,1:T(8,128)(2,1)S(1)}, bf16[256,2560]{0,1:T(8,128)(2,1)}, u32[]{:S(2)}) copy-start(bf16[256,2560]{0,1:T(8,128)(2,1)} %copy.154) | copy-start | bytes 3932164
  111.4 3.1 %copy-start.19 = (f32[256,128]{0,1:T(8,128)S(1)}, f32[256,128]{0,1:T(8,128)}, u32[]{:S(2)}) copy-start(f32[256,128]{0,1:T(8,128)} %copy.152) | copy-start | bytes 393220
  111.4 6.5 %collective-permute-start.18 = (f32[2,256,256]{2,1,0:T(8,128)}, f32[2,256,256]{2,1,0:T(8,128)}, u32[]{:S(2)}, u32[]{:S(2)}) collective-permute-start(f32[2,256,256]{2,1,0:T(8,128)} %select_bitcast_fusion), channel_id=1, source_target_pairs={{0,1},{1,0},{2,3},{3,2},{4,5},{5,4},{6,7},{7,6},{8,9},{9,8},{10,11... | collective-permute-start | bytes 1572872 | tf_op jit(solution)/shard_map/ppermute | solution.py:100

commit v13 on v12

--- a/solution.py
+++ b/solution.py
@@ -50,20 +50,30 @@
     return value.reshape((count,) + rest)
 
 
-def halving_scatter(blocks, axis):
+def halving_scatter(blocks, axis, works=()):
     count = lax.axis_size(axis)
     me = lax.axis_index(axis)
     rest = blocks.shape[1:]
     nbits = count.bit_length() - 1
     value = bit_order(blocks, count, list(range(nbits)))
+    done = []
     for bit in range(nbits):
         step = 1 << bit
         value = value.reshape((2, -1) + rest)
         upper = me // step % 2 == 1
         keep = jnp.where(upper, value[1], value[0])
         give = jnp.where(upper, value[0], value[1])
+        if bit < len(works):
+            fn, pick = works[bit]
+            give, args = lax.optimization_barrier((give, pick(done)))
         value = keep + lax.ppermute(give, axis, [(at, at ^ step) for at in range(count)])
-    return value[0]
+        if bit < len(works):
+            value, piece = lax.optimization_barrier((value, fn(*args)))
+            done.append(piece)
+    for bit in range(nbits, len(works)):
+        fn, pick = works[bit]
+        done.append(fn(*pick(done)))
+    return value[0], done
 
 
 def doubling_gather(piece, axis):
@@ -85,14 +95,14 @@
     return value.reshape((count,) + rest)
 
 
-def cand_sum_bf16(state):
+def cand_sum_bf16(state, works=()):
     heads, size, width = state.shape
     count = lax.axis_size("cand")
     piece = size // count
     blocks = jnp.transpose(state.reshape(heads, count, piece, width), (1, 0, 2, 3))
-    summed = halving_scatter(blocks, "cand").astype(jnp.bfloat16)
-    gathered = doubling_gather(summed, "cand")
-    return jnp.transpose(gathered, (1, 0, 2, 3)).reshape(heads, size, width)
+    summed, done = halving_scatter(blocks, "cand", works)
+    gathered = doubling_gather(summed.astype(jnp.bfloat16), "cand")
+    return jnp.transpose(gathered, (1, 0, 2, 3)).reshape(heads, size, width), done
 
 
 def other_core(value):
@@ -142,8 +152,6 @@
     g_parts, levels, x_late = late
     amplitude, inverse = levels
     g_heads, decayed_g, g_low, dstate = g_parts
-    xc_heads = x_late.reshape(cand_dev, cand_len, half_heads, head_size)
-    x_high, x_low = split_bf16(xc_heads.astype(jnp.float32) * inverse[:, :, :, None])
     later_total = inclusive - own_total
     after_local = own_total[None, :] - jnp.cumsum(log_prefix, axis=0)
     weight = jnp.exp(after_local + later_total[None, :])
@@ -159,39 +167,54 @@
     give_half = jnp.where(mine_first, state_halves[1], state_halves[0])
     init_local = own_half + other_core(give_half)
 
-    grad_half = cand_sum_bf16(dstate)
-    init_half = cand_sum_bf16(init_local)
+    causal = position[:, None] >= position[None, :]
+    flat = (cand_dev, cand_len, half_width)
+
+    def x_work(x_late, inverse):
+        xc_heads = x_late.reshape(cand_dev, cand_len, half_heads, head_size)
+        return split_bf16(xc_heads.astype(jnp.float32) * inverse[:, :, :, None])
+
+    def pair(left, right):
+        return jnp.einsum(
+            "ctk,csk->cts", left.reshape(flat), right.reshape(flat),
+            preferred_element_type=jnp.float32,
+        )
+
+    def sum_work(decayed_g, g_low, x_high, x_low, c_cand, b_cand):
+        weight_sum = pair(decayed_g, x_high) + pair(decayed_g, x_low) + pair(g_low, x_high)
+        weight_sum = jnp.where(causal[None], weight_sum, 0.0)
+        db_part = jnp.einsum(
+            "cts,ctn->csn", weight_sum, c_cand.astype(jnp.float32), precision=lax.Precision.HIGHEST
+        )
+        dc_part = jnp.einsum(
+            "cts,csn->ctn", weight_sum, b_cand.astype(jnp.float32), precision=lax.Precision.HIGHEST
+        )
+        return db_part, dc_part
+
+    def dx_work(amplitude, inverse, scores, g_heads):
+        amp_t = jnp.transpose(amplitude, (0, 2, 1))
+        inv_t = jnp.transpose(inverse, (0, 2, 1))
+        decay_mat = amp_t[:, :, :, None] * inv_t[:, :, None, :]
+        kernel = jnp.where(causal[None, None], scores[:, None] * decay_mat, 0.0).astype(jnp.bfloat16)
+        dx = jnp.einsum("chts,cthp->cshp", kernel, g_heads, preferred_element_type=jnp.float32)
+        return dx.astype(jnp.bfloat16).reshape(flat)
+
+    grad_half, _ = cand_sum_bf16(dstate)
+    init_half, (x_parts, sums, dx_cand) = cand_sum_bf16(
+        init_local,
+        [
+            (x_work, lambda done: (x_late, inverse)),
+            (sum_work, lambda done: (decayed_g, g_low) + tuple(done[0]) + (c_cand, b_cand)),
+            (dx_work, lambda done: (amplitude, inverse, scores, g_heads)),
+        ],
+    )
+    db_part, dc_part = sums
     grad_other = other_core(grad_half)
     grad_state = jnp.where(
         mine_first,
         jnp.concatenate([grad_half, grad_other], axis=0),
         jnp.concatenate([grad_other, grad_half], axis=0),
     )
-
-    causal = position[:, None] >= position[None, :]
-    flat = (cand_dev, cand_len, half_width)
-
-    def pair(left, right):
-        return jnp.einsum(
-            "ctk,csk->cts", left.reshape(flat), right.reshape(flat),
-            preferred_element_type=jnp.float32,
-        )
-
-    weight_sum = pair(decayed_g, x_high) + pair(decayed_g, x_low) + pair(g_low, x_high)
-    weight_sum = jnp.where(causal[None], weight_sum, 0.0)
-    db_part = jnp.einsum(
-        "cts,ctn->csn", weight_sum, c_cand.astype(jnp.float32), precision=lax.Precision.HIGHEST
-    )
-    dc_part = jnp.einsum(
-        "cts,csn->ctn", weight_sum, b_cand.astype(jnp.float32), precision=lax.Precision.HIGHEST
-    )
-
-    amp_t = jnp.transpose(amplitude, (0, 2, 1))
-    inv_t = jnp.transpose(inverse, (0, 2, 1))
-    decay_mat = amp_t[:, :, :, None] * inv_t[:, :, None, :]
-    kernel = jnp.where(causal[None, None], scores[:, None] * decay_mat, 0.0).astype(jnp.bfloat16)
-    dx_cand = jnp.einsum("chts,cthp->cshp", kernel, g_heads, preferred_element_type=jnp.float32)
-    dx_cand = dx_cand.astype(jnp.bfloat16).reshape(flat)
 
     dc_state = jnp.dot(
         decayed_g.reshape(cand_dev * cand_len, half_width),

time: 121 us -> 122 us (level)
  waiting for transfers between devices: 27.5 us -> 34.4 us
  other arithmetic: 20 us -> 16.3 us
  local copies, waits for them, and re-layouts: 26.4 us -> 23 us
  starting transfers between devices: 21.2 us -> 24.1 us
    ppermute x6, waiting for transfers between devices: 6.54 us -> 14.4 us  [doubling_gather(): other = lax.ppermute(value, axis, [(at, at ^ step) for at in range(count)])]
    ppermute x6, starting transfers between devices: 6.48 us -> 8.65 us  [doubling_gather(): other = lax.ppermute(value, axis, [(at, at ^ step) for at in range(count)])]
    unnamed x48 -> x42, local copies, waits for them, and re-layouts: 11.9 us -> 10.1 us
    reshape x4 -> x3, local copies, waits for them, and re-layouts: 1.63 us -> 0.2 us  [the longest x1 0.1 us: cand_sum_bf16(): jnp.transpose(gathered, (1, 0, 2, 3)).reshape(heads, size, width)]
    dot_general x1, matrix products: 2.22 us -> 0.92 us  [shards(): jnp.einsum('jhp,hpn->jhn', x_heads, grad_state, preferred_element_type=jn...]
  transfers between devices with their start and end apart: 19 -> 19, of which waited for: 10 -> 9; matrix products, arithmetic and copies ran while one was open for 53% -> 48% of each run, Pallas kernels for 0% -> 0%
where the time goes in v13:
time: 122 us
  waiting for transfers between devices  34.4 us (28%)
  starting transfers between devices  24.1 us (20%)
  local copies, waits for them, and re-layouts  23 us (19%)
  matrix products  22.6 us (19%)
  other arithmetic  16.3 us (13%)
  between operations  1.34 us (1%)
    ppermute x6, waiting for transfers between devices, doubling_gather(): other = lax.ppermute(value, axis, [(at, at ^ step) for at in range(count)])  14.4 us
    ppermute x6, waiting for transfers between devices, halving_scatter(): lax.ppermute(give, axis, [(at, at ^ step) for at in range(count)])  13.1 us
    unnamed x42, local copies, waits for them, and re-layouts  10.1 us
    ppermute x6, starting transfers between devices, halving_scatter(): lax.ppermute(give, axis, [(at, at ^ step) for at in range(count)])  9.96 us
    ppermute x6, starting transfers between devices, doubling_gather(): other = lax.ppermute(value, axis, [(at, at ^ step) for at in range(count)])  8.65 us
    dot_general x1, matrix products, dx_work(): jnp.einsum('chts,cthp->cshp', kernel, g_heads, preferred_element_type=jnp...  7.59 us
    ppermute x4, waiting for transfers between devices, suffix_sum(): value = value + lax.ppermute(value, axis, back)  6.84 us
    convert_element_type x2, other arithmetic, split_bf16(): low = (value - high).astype(jnp.bfloat16)  5.71 us
  transfers between devices with their start and end apart: 19, of which 9 were waited for; matrix products, arithmetic and copies ran while one was open for 48% of the time, Pallas kernels for 0%

profile of v13, /device:TPU:0, one launch (start us, length us, event | category | flops | bytes accessed | tf_op | source)
XLA Modules:
  0.0 121.7 jit_solution(7105519194806656701)
XLA Ops:
  0.6 0.9 fusion.23
  1.6 1.3 %collective-permute-start = (f32[40]{0:T(128)S(1)}, f32[40]{0:T(128)S(1)}, u32[]{:S(2)}, u32[]{:S(2)}) collective-permute-start(f32[40]{0:T(128)S(1)} %get-tuple-element.56), channel_id=1, source_target_pairs={{1,0},{2,1},{3,2},{4,3},{5,4},{6,5},{7,6},{8,7},{9,8},{10,9},{11,1... | collective-permute-start | bytes 488 | tf_op jit(solution)/shard_map/ppermute | solution.py:35
  3.0 0.6 reduce-window.16
  3.6 0.2 slice_reduce_fusion.1
  3.8 1.0 log-plus-one_bitcast_fusion
  4.9 2.3 %reduce-window.14 = f32[2,20,4,128]{3,1,2,0:T(8,128)S(1)} reduce-window(f32[2,20,4,128]{3,1,2,0:T(8,128)S(1)} %copy.141, f32[]{:T(128)} %constant.108.clone.1), window={size=1x1x1x128 pad=0_0x0_0x0_0x127_0}, to_apply=%region_1.0 | reduce-window | flops 2600960 | bytes 163844 | tf_op jit(solution)/shard_map/reduce-window
  7.2 0.2 slice_reduce_fusion
  7.6 0.7 exp.28
  8.4 0.7 broadcast_multiply_fusion
  9.2 1.3 %collective-permute-start.1 = (f32[40]{0:T(128)S(1)}, f32[40]{0:T(128)S(1)}, u32[]{:S(2)}, u32[]{:S(2)}) collective-permute-start(f32[40]{0:T(128)S(1)} %add.79), channel_id=1, source_target_pairs={{2,0},{3,1},{4,2},{5,3},{6,4},{7,5},{8,6},{9,7},{10,8},{11,9},{12,... | collective-permute-start | bytes 488 | tf_op jit(solution)/shard_map/ppermute | solution.py:35
  10.5 3.0 %copy.144 = bf16[2,512,1280]{1,2,0:T(8,128)(2,1)S(1)} copy(bf16[2,512,1280]{2,1,0:T(8,128)(2,1)} %param.17) | data formatting | bytes 5242880 | tf_op jit(solution)/shard_map/optimization_barrier | solution.py:34
  13.5 0.2 broadcast_select_fusion
  13.7 2.8 %fusion.6 = (bf16[2,512,20,64]{1,3,2,0:T(8,128)(2,1)}, bf16[2,512,20,64]{1,3,2,0:T(8,128)(2,1)S(1)}) fusion(bf16[2,512,20,64]{1,3,2,0:T(8,128)(2,1)S(1)} %bitcast.135, f32[2,512,20]{1,2,0:T(8,128)S(1)} %copy.145), kind=kLoop, calls=%fused_computation.11 | loop fusion | flops 7864320 | bytes 7946240 | tf_op jit(solution)/shard_map/convert_element_type | solution.py:11
  16.5 0.8 convolution_bitcast_fusion
  17.4 1.3 %collective-permute-start.2 = (f32[40]{0:T(128)S(1)}, f32[40]{0:T(128)S(1)}, u32[]{:S(2)}, u32[]{:S(2)}) collective-permute-start(f32[40]{0:T(128)S(1)} %add.80), channel_id=1, source_target_pairs={{4,0},{5,1},{6,2},{7,3},{8,4},{9,5},{10,6},{11,7},{12,8},{13,9},{1... | collective-permute-start | bytes 488 | tf_op jit(solution)/shard_map/ppermute | solution.py:35
  18.7 1.8 %fusion.28 = f32[2,512,512]{2,1,0:T(8,128)} fusion(bf16[2,512,128]{2,1,0:T(8,128)(2,1)S(1)} %copy-done, bf16[2,512,128]{2,1,0:T(8,128)(2,1)S(1)} %copy-done.7), kind=kOutput, calls=%fused_computation.81 | convolution fusion | flops 134217728 | bytes 2621440 | tf_op jit(solution)/shard_map/ctn,csn->cts/dot_general | solution.py:140
  20.5 6.0 %collective-permute-done.2 = f32[40]{0:T(128)S(1)} collective-permute-done((f32[40]{0:T(128)S(1)}, f32[40]{0:T(128)S(1)}, u32[]{:S(2)}, u32[]{:S(2)}) %collective-permute-start.2) | collective-permute-done | bytes 192 | tf_op jit(solution)/shard_map/ppermute | solution.py:35
  26.5 1.5 %collective-permute-start.3 = (f32[40]{0:T(128)S(1)}, f32[40]{0:T(128)S(1)}, u32[]{:S(2)}, u32[]{:S(2)}) collective-permute-start(f32[40]{0:T(128)S(1)} %add.81), channel_id=1, source_target_pairs={{8,0},{9,1},{10,2},{11,3},{12,4},{13,5},{14,6},{15,7},{24,16},{25,... | collective-permute-start | bytes 488 | tf_op jit(solution)/shard_map/ppermute | solution.py:35
  27.9 1.6 %copy.153 = f32[256,128]{0,1:T(8,128)} copy(bf16[256,128]{1,0:T(8,128)(2,1)} %param.10) | data formatting | bytes 196608 | tf_op jit(solution)/shard_map/convert_element_type | solution.py:158
  29.5 2.4 %copy.155 = bf16[256,2560]{0,1:T(8,128)(2,1)} copy(bf16[256,2560]{1,0:T(8,128)(2,1)} %param.9) | data formatting | bytes 2621440 | tf_op args[0]
  32.0 0.8 collective-permute-done.3
  32.9 1.5 %collective-permute-start.4 = (f32[4,20,8,128]{3,2,1,0:T(8,128)S(1)}, f32[4,20,8,128]{3,2,1,0:T(8,128)S(1)}, u32[]{:S(2)}, u32[]{:S(2)}) collective-permute-start(f32[4,20,8,128]{3,2,1,0:T(8,128)S(1)} %bitcast.157), channel_id=1, source_target_pairs={{0,2},{2,0},{4,6},{6,4},{8,10},{10,8},{12,14},{14,12},{1,3},{3,1},... | collective-permute-start | bytes 983048 | tf_op jit(solution)/shard_map/ppermute | solution.py:69
  34.6 1.0 fusion.17
  35.6 5.5 %collective-permute-done.4 = f32[4,20,8,128]{3,2,1,0:T(8,128)S(1)} collective-permute-done((f32[4,20,8,128]{3,2,1,0:T(8,128)S(1)}, f32[4,20,8,128]{3,2,1,0:T(8,128)S(1)}, u32[]{:S(2)}, u32[]{:S(2)}) %collective-permute-start.4) | collective-permute-done | bytes 327712 | tf_op jit(solution)/shard_map/ppermute | solution.py:69
  41.2 1.8 %collective-permute-start.5 = (f32[2,20,8,128]{3,2,1,0:T(8,128)S(1)}, f32[2,20,8,128]{3,2,1,0:T(8,128)S(1)}, u32[]{:S(2)}, u32[]{:S(2)}) collective-permute-start(f32[2,20,8,128]{3,2,1,0:T(8,128)S(1)} %slice_select_fusion.5), channel_id=1, source_target_pairs={{0,4},{2,6},{4,0},{6,2},{8,12},{10,14},{12,8},{14,10},{1,5},{3,7},... | collective-permute-start | bytes 491528 | tf_op jit(solution)/shard_map/ppermute | solution.py:69
  43.2 3.4 %collective-permute-done.5 = f32[2,20,8,128]{3,2,1,0:T(8,128)S(1)} collective-permute-done((f32[2,20,8,128]{3,2,1,0:T(8,128)S(1)}, f32[2,20,8,128]{3,2,1,0:T(8,128)S(1)}, u32[]{:S(2)}, u32[]{:S(2)}) %collective-permute-start.5) | collective-permute-done | bytes 163872 | tf_op jit(solution)/shard_map/ppermute | solution.py:69
  46.7 3.9 %collective-permute-start.6 = (f32[1,20,8,128]{3,2,1,0:T(8,128)S(1)}, f32[1,20,8,128]{3,2,1,0:T(8,128)S(1)}, u32[]{:S(2)}, u32[]{:S(2)}) collective-permute-start(f32[1,20,8,128]{3,2,1,0:T(8,128)S(1)} %slice_select_fusion.7), channel_id=1, source_target_pairs={{0,8},{2,10},{4,12},{6,14},{8,0},{10,2},{12,4},{14,6},{1,9},{3,11}... | collective-permute-start | bytes 245768 | tf_op jit(solution)/shard_map/ppermute | solution.py:69
  50.5 4.2 %collective-permute-done.6 = f32[1,20,8,128]{3,2,1,0:T(8,128)S(1)} collective-permute-done((f32[1,20,8,128]{3,2,1,0:T(8,128)S(1)}, f32[1,20,8,128]{3,2,1,0:T(8,128)S(1)}, u32[]{:S(2)}, u32[]{:S(2)}) %collective-permute-start.6) | collective-permute-done | bytes 81952 | tf_op jit(solution)/shard_map/ppermute | solution.py:69
  54.7 1.7 %collective-permute-start.7 = (bf16[1,20,8,128]{3,2,1,0:T(8,128)(2,1)S(1)}, bf16[1,20,8,128]{3,2,1,0:T(8,128)(2,1)S(1)}, u32[]{:S(2)}, u32[]{:S(2)}) collective-permute-start(bf16[1,20,8,128]{3,2,1,0:T(8,128)(2,1)S(1)} %add_convert_fusion), channel_id=1, source_target_pairs={{0,8},{2,10},{4,12},{6,14},{8,0},{10,2},{12,4},{14,6},{1,9},{3,11}... | collective-permute-start | bytes 122888 | tf_op jit(solution)/shard_map/ppermute | solution.py:86
  56.5 3.2 %collective-permute-done.7 = bf16[1,20,8,128]{3,2,1,0:T(8,128)(2,1)S(1)} collective-permute-done((bf16[1,20,8,128]{3,2,1,0:T(8,128)(2,1)S(1)}, bf16[1,20,8,128]{3,2,1,0:T(8,128)(2,1)S(1)}, u32[]{:S(2)}, u32[]{:S(2)}) %collective-permute-start.7) | collective-permute-done | bytes 40992 | tf_op jit(solution)/shard_map/ppermute | solution.py:86
  59.7 0.6 maximum_select_fusion.7
  60.4 1.6 %collective-permute-start.8 = (bf16[2,20,8,128]{3,2,1,0:T(8,128)(2,1)}, bf16[2,20,8,128]{3,2,1,0:T(8,128)(2,1)}, u32[]{:S(2)}, u32[]{:S(2)}) collective-permute-start(bf16[2,20,8,128]{3,2,1,0:T(8,128)(2,1)} %maximum_select_fusion.7), channel_id=1, source_target_pairs={{0,4},{2,6},{4,0},{6,2},{8,12},{10,14},{12,8},{14,10},{1,5},{3,7},... | collective-permute-start | bytes 245768 | tf_op jit(solution)/shard_map/ppermute | solution.py:86
  61.9 0.2 add_bitcast_fusion
  62.2 0.7 copy.159
  62.9 0.7 copy.161
  63.7 4.4 %copy.160 = bf16[2,512,1280]{1,2,0:T(8,128)(2,1)} copy(bf16[2,512,1280]{2,1,0:T(8,128)(2,1)} %param.12) | data formatting | bytes 5242880 | tf_op jit(solution)/shard_map/optimization_barrier | solution.py:68
  68.1 2.9 %fusion.7 = (bf16[2,512,20,64]{1,3,2,0:T(8,128)(2,1)S(1)}, bf16[2,512,20,64]{1,3,2,0:T(8,128)(2,1)S(1)}) fusion(bf16[2,512,20,64]{1,3,2,0:T(8,128)(2,1)} %bitcast.137, f32[2,512,20]{1,2,0:T(8,128)} %copy.161), kind=kLoop, calls=%fused_computation.12 | loop fusion | flops 7864320 | bytes 7946240 | tf_op jit(solution)/shard_map/convert_element_type | solution.py:11
  71.1 1.0 maximum_select_fusion.3
  72.1 2.0 %collective-permute-start.9 = (bf16[4,20,8,128]{3,2,1,0:T(8,128)(2,1)S(1)}, bf16[4,20,8,128]{3,2,1,0:T(8,128)(2,1)S(1)}, u32[]{:S(2)}, u32[]{:S(2)}) collective-permute-start(bf16[4,20,8,128]{3,2,1,0:T(8,128)(2,1)S(1)} %maximum_select_fusion.3), channel_id=1, source_target_pairs={{0,2},{2,0},{4,6},{6,4},{8,10},{10,8},{12,14},{14,12},{1,3},{3,1},... | collective-permute-start | bytes 491528 | tf_op jit(solution)/shard_map/ppermute | solution.py:86
  74.1 1.0 bitcast_add_fusion.1
  75.2 0.5 collective-permute-start.13
  75.7 1.6 %fusion.30 = f32[2,512,512]{2,1,0:T(8,128)S(1)} fusion(bf16[2,512,1280]{1,2,0:T(8,128)(2,1)S(1)} %bitcast.132, bf16[2,512,1280]{1,2,0:T(8,128)(2,1)S(1)} %bitcast.145), kind=kOutput, calls=%fused_computation.83 | convolution fusion | flops 1342177280 | bytes 7340032 | tf_op jit(solution)/shard_map/ctk,csk->cts/dot_general | solution.py:178
  77.3 1.6 %fusion.29 = f32[2,512,512]{2,1,0:T(8,128)S(1)} fusion(bf16[2,512,1280]{1,2,0:T(8,128)(2,1)S(1)} %bitcast.133, bf16[2,512,1280]{1,2,0:T(8,128)(2,1)S(1)} %bitcast.139), kind=kOutput, calls=%fused_computation.82 | convolution fusion | flops 1342177280 | bytes 7340032 | tf_op jit(solution)/shard_map/ctk,csk->cts/dot_general | solution.py:178
  78.9 0.1 copy-done.3
  79.0 1.8 %add_select_fusion = f32[2,512,512]{2,1,0:T(8,128)S(1)} fusion(f32[2,512,512]{2,1,0:T(8,128)S(1)} %fusion.29, f32[2,512,512]{2,1,0:T(8,128)S(1)} %fusion.30, bf16[2,512,1280]{1,2,0:T(8,128)(2,1)S(1)} %bitcast.138, bf16[2,512,1280]{1,2,0:T(8,128)(2,1)S(1)} %bitcast.140, pred[512,512]{1,0:T(8,128)(4,1)S(1)} %iota_compare_fusion), kind=kOutput, calls=%fused_computation.25 | convolution fusion | flops 1343750144 | bytes 11796480 | tf_op jit(solution)/shard_map/ctk,csk->cts/dot_general | solution.py:178
  80.8 1.1 fusion.32
  82.0 1.9 %fusion.31 = f32[2,512,128]{2,1,0:T(8,128)S(1)} fusion(f32[2,512,512]{2,1,0:T(8,128)S(1)} %add_select_fusion, bf16[2,512,128]{2,1,0:T(8,128)(2,1)S(1)} %copy-done), kind=kOutput, calls=%fused_computation.84 | convolution fusion | flops 805306368 | bytes 2883584 | tf_op jit(solution)/shard_map/cts,ctn->csn/dot_general | solution.py:186
  83.9 2.2 %collective-permute-start.14 = (f32[1,20,8,128]{3,2,1,0:T(8,128)S(1)}, f32[1,20,8,128]{3,2,1,0:T(8,128)S(1)}, u32[]{:S(2)}, u32[]{:S(2)}) collective-permute-start(f32[1,20,8,128]{3,2,1,0:T(8,128)S(1)} %slice_select_fusion.8), channel_id=1, source_target_pairs={{0,8},{2,10},{4,12},{6,14},{8,0},{10,2},{12,4},{14,6},{1,9},{3,11}... | collective-permute-start | bytes 245768 | tf_op jit(solution)/shard_map/ppermute | solution.py:69
  86.1 7.6 %fusion.15 = bf16[2,20,64,512]{3,2,1,0:T(8,128)(2,1)} fusion(bf16[2,512,20,64]{1,3,2,0:T(8,128)(2,1)S(1)} %bitcast.136, f32[2,20,512]{2,1,0:T(8,128)S(1)} %copy.170, f32[2,20,512]{2,1,0:T(8,128)S(1)} %copy.169, f32[2,512,512]{2,1,0:T(8,128)S(1)} %copy-done.4, pred[512,512]{1,0:T(8,128)(4,1)S(1)} %iota_compare_fusion), kind=kOutput, calls=%fused_computation.26 | convolution fusion | flops 1385431040 | bytes 7766016 | tf_op jit(solution)/shard_map/chts,cthp->cshp/dot_general | solution.py:199
  93.7 0.9 collective-permute-start.15
  94.6 4.1 %collective-permute-done.15 = bf16[1,20,8,128]{3,2,1,0:T(8,128)(2,1)S(1)} collective-permute-done((bf16[1,20,8,128]{3,2,1,0:T(8,128)(2,1)S(1)}, bf16[1,20,8,128]{3,2,1,0:T(8,128)(2,1)S(1)}, u32[]{:S(2)}, u32[]{:S(2)}) %collective-permute-start.15) | collective-permute-done | bytes 40992 | tf_op jit(solution)/shard_map/ppermute | solution.py:86
  98.7 2.1 %collective-permute-start.16 = (bf16[2,20,8,128]{3,2,1,0:T(8,128)(2,1)S(1)}, bf16[2,20,8,128]{3,2,1,0:T(8,128)(2,1)S(1)}, u32[]{:S(2)}, u32[]{:S(2)}) collective-permute-start(bf16[2,20,8,128]{3,2,1,0:T(8,128)(2,1)S(1)} %maximum_select_fusion.8), channel_id=1, source_target_pairs={{0,4},{2,6},{4,0},{6,2},{8,12},{10,14},{12,8},{14,10},{1,5},{3,7},... | collective-permute-start | bytes 245768 | tf_op jit(solution)/shard_map/ppermute | solution.py:86
  100.9 2.4 %collective-permute-done.16 = bf16[2,20,8,128]{3,2,1,0:T(8,128)(2,1)S(1)} collective-permute-done((bf16[2,20,8,128]{3,2,1,0:T(8,128)(2,1)S(1)}, bf16[2,20,8,128]{3,2,1,0:T(8,128)(2,1)S(1)}, u32[]{:S(2)}, u32[]{:S(2)}) %collective-permute-start.16) | collective-permute-done | bytes 81952 | tf_op jit(solution)/shard_map/ppermute | solution.py:86
  103.2 0.4 collective-permute-start.17
  103.8 4.8 %collective-permute-done.17 = bf16[4,20,8,128]{3,2,1,0:T(8,128)(2,1)S(1)} collective-permute-done((bf16[4,20,8,128]{3,2,1,0:T(8,128)(2,1)S(1)}, bf16[4,20,8,128]{3,2,1,0:T(8,128)(2,1)S(1)}, u32[]{:S(2)}, u32[]{:S(2)}) %collective-permute-start.17) | collective-permute-done | bytes 163872 | tf_op jit(solution)/shard_map/ppermute | solution.py:86
  108.8 0.9 fusion.33
  109.8 0.9 select_bitcast_fusion
  110.7 0.7 copy-done.18
  111.4 0.9 fusion.8
  112.4 0.8 copy.179
  113.1 1.6 %fusion.16 = bf16[40,64,256]{2,1,0:T(8,128)(2,1)S(1)} fusion(f32[256,128]{0,1:T(8,128)} %copy.153, f32[256,40]{0,1:T(8,128)S(1)} %copy-done.16, bf16[20,64,128]{2,1,0:T(8,128)(2,1)} %copy-done.18, bf16[20,64,128]{2,1,0:T(8,128)(2,1)S(1)} %copy_bitcast_fusion, pred[]{:T(512)S(6)} %eq.34), kind=kOutput, calls=%fused_computation.27 | convolution fusion | flops 172032000 | bytes 2138113 | tf_op jit(solution)/shard_map/jhn,hpn->jhp/dot_general | solution.py:234
  114.8 1.6 %copy.178 = bf16[256,2560]{1,0:T(8,128)(2,1)} copy(bf16[256,2560]{0,1:T(8,128)(2,1)S(1)} %bitcast.150) | data formatting | bytes 2621440
  116.3 4.4 %copy.180 = bf16[2,512,1280]{2,1,0:T(8,128)(2,1)} copy(bf16[2,512,1280]{1,2,0:T(8,128)(2,1)} %bitcast.144) | data formatting | bytes 5242880
  120.8 0.8 fusion.27
  (101 shorter events, 2.1 us)
Async XLA Ops:
  0.6 15.9 %copy-start = (bf16[2,512,128]{2,1,0:T(8,128)(2,1)S(1)}, bf16[2,512,128]{2,1,0:T(8,128)(2,1)}, u32[]{:S(2)}) copy-start(bf16[2,512,128]{2,1,0:T(8,128)(2,1)} %param.14) | copy-start | bytes 786436
  1.6 6.8 %collective-permute-start = (f32[40]{0:T(128)S(1)}, f32[40]{0:T(128)S(1)}, u32[]{:S(2)}, u32[]{:S(2)}) collective-permute-start(f32[40]{0:T(128)S(1)} %get-tuple-element.56), channel_id=1, source_target_pairs={{1,0},{2,1},{3,2},{4,3},{5,4},{6,5},{7,6},{8,7},{9,8},{10,9},{11,1... | collective-permute-start | bytes 488 | tf_op jit(solution)/shard_map/ppermute | solution.py:35
  3.6 1.3 %copy-start.12 = (f32[40,2,128]{2,0,1:T(8,128)}, f32[40,2,128]{2,0,1:T(8,128)S(1)}, u32[]{:S(2)}) copy-start(f32[40,2,128]{2,0,1:T(8,128)S(1)} %reduce-window.16) | copy-start | bytes 122884
  3.8 9.8 %copy-start.17 = (f32[40,3]{0,1:T(4,128)}, f32[40,3]{0,1:T(4,128)S(1)}, u32[]{:S(2)}) copy-start(f32[40,3]{0,1:T(4,128)S(1)} %reduce-window.19) | copy-start | bytes 1444
  8.4 2.1 %copy-start.10 = (f32[2,20,512]{2,0,1:T(2,128)}, f32[2,20,512]{2,0,1:T(2,128)S(1)}, u32[]{:S(2)}) copy-start(f32[2,20,512]{2,0,1:T(2,128)S(1)} %exp.25) | copy-start | bytes 245764
  9.2 8.2 %collective-permute-start.1 = (f32[40]{0:T(128)S(1)}, f32[40]{0:T(128)S(1)}, u32[]{:S(2)}, u32[]{:S(2)}) collective-permute-start(f32[40]{0:T(128)S(1)} %add.79), channel_id=1, source_target_pairs={{2,0},{3,1},{4,2},{5,3},{6,4},{7,5},{8,6},{9,7},{10,8},{11,9},{12,... | collective-permute-start | bytes 488 | tf_op jit(solution)/shard_map/ppermute | solution.py:35
  13.7 2.8 %copy-start.1 = (bf16[2,512,1280]{1,2,0:T(8,128)(2,1)}, bf16[2,512,1280]{1,2,0:T(8,128)(2,1)S(1)}, u32[]{:S(2)}) copy-start(bf16[2,512,1280]{1,2,0:T(8,128)(2,1)S(1)} %broadcast_select_fusion) | copy-start | bytes 7864324
  16.5 2.2 %copy-start.7 = (bf16[2,512,128]{2,1,0:T(8,128)(2,1)S(1)}, bf16[2,512,128]{2,1,0:T(8,128)(2,1)}, u32[]{:S(2)}) copy-start(bf16[2,512,128]{2,1,0:T(8,128)(2,1)} %param.13) | copy-start | bytes 786436
  17.4 9.1 %collective-permute-start.2 = (f32[40]{0:T(128)S(1)}, f32[40]{0:T(128)S(1)}, u32[]{:S(2)}, u32[]{:S(2)}) collective-permute-start(f32[40]{0:T(128)S(1)} %add.80), channel_id=1, source_target_pairs={{4,0},{5,1},{6,2},{7,3},{8,4},{9,5},{10,6},{11,7},{12,8},{13,9},{1... | collective-permute-start | bytes 488 | tf_op jit(solution)/shard_map/ppermute | solution.py:35
  26.5 6.3 %collective-permute-start.3 = (f32[40]{0:T(128)S(1)}, f32[40]{0:T(128)S(1)}, u32[]{:S(2)}, u32[]{:S(2)}) collective-permute-start(f32[40]{0:T(128)S(1)} %add.81), channel_id=1, source_target_pairs={{8,0},{9,1},{10,2},{11,3},{12,4},{13,5},{14,6},{15,7},{24,16},{25,... | collective-permute-start | bytes 488 | tf_op jit(solution)/shard_map/ppermute | solution.py:35
  29.5 4.9 %slice-start = ((f32[40,3]{0,1:T(4,128)}), f32[40,2]{0,1:T(2,128)S(1)}, s32[]{:S(2)}) async-start(f32[40,3]{0,1:T(4,128)} %copy-done.17), calls=%async_computation | async-start | bytes 2048 | tf_op jit(solution)/shard_map/slice.3
  32.0 2.5 %copy-start.13 = (f32[40,2,128]{2,0,1:T(8,128)S(1)}, f32[40,2,128]{2,0,1:T(8,128)}, u32[]{:S(2)}) copy-start(f32[40,2,128]{2,0,1:T(8,128)} %copy-done.12) | copy-start | bytes 122884
  32.0 2.7 %copy-start.5 = (bf16[256,2560]{0,1:T(8,128)(2,1)S(1)}, bf16[256,2560]{0,1:T(8,128)(2,1)}, u32[]{:S(2)}) copy-start(bf16[256,2560]{0,1:T(8,128)(2,1)} %copy.155) | copy-start | bytes 3932164
  32.0 2.7 %copy-start.14 = (f32[256,128]{0,1:T(8,128)S(1)}, f32[256,128]{0,1:T(8,128)}, u32[]{:S(2)}) copy-start(f32[256,128]{0,1:T(8,128)} %copy.153) | copy-start | bytes 393220
  32.9 8.2 %collective-permute-start.4 = (f32[4,20,8,128]{3,2,1,0:T(8,128)S(1)}, f32[4,20,8,128]{3,2,1,0:T(8,128)S(1)}, u32[]{:S(2)}, u32[]{:S(2)}) collective-permute-start(f32[4,20,8,128]{3,2,1,0:T(8,128)S(1)} %bitcast.157), channel_id=1, source_target_pairs={{0,2},{2,0},{4,6},{6,4},{8,10},{10,8},{12,14},{14,12},{1,3},{3,1},... | collective-permute-start | bytes 983048 | tf_op jit(solution)/shard_map/ppermute | solution.py:69
  34.6 6.6 %copy-start.15 = (f32[256,40]{0,1:T(8,128)}, f32[256,40]{0,1:T(8,128)S(1)}, u32[]{:S(2)}) copy-start(f32[256,40]{0,1:T(8,128)S(1)} %fusion.21) | copy-start | bytes 122884
  41.2 5.4 %collective-permute-start.5 = (f32[2,20,8,128]{3,2,1,0:T(8,128)S(1)}, f32[2,20,8,128]{3,2,1,0:T(8,128)S(1)}, u32[]{:S(2)}, u32[]{:S(2)}) collective-permute-start(f32[2,20,8,128]{3,2,1,0:T(8,128)S(1)} %slice_select_fusion.5), channel_id=1, source_target_pairs={{0,4},{2,6},{4,0},{6,2},{8,12},{10,14},{12,8},{14,10},{1,5},{3,7},... | collective-permute-start | bytes 491528 | tf_op jit(solution)/shard_map/ppermute | solution.py:69
  43.1 18.8 %collective-permute-start.11 = (f32[20,64,128]{2,1,0:T(8,128)S(1)}, f32[20,64,128]{2,1,0:T(8,128)S(1)}, u32[]{:S(2)}, u32[]{:S(2)}) collective-permute-start(f32[20,64,128]{2,1,0:T(8,128)S(1)} %slice_select_fusion), channel_id=1, source_target_pairs={{0,1},{1,0},{2,3},{3,2},{4,5},{5,4},{6,7},{7,6},{8,9},{9,8},{10,11... | collective-permute-start | bytes 1966088 | tf_op jit(solution)/shard_map/ppermute | solution.py:110
  46.7 8.1 %collective-permute-start.6 = (f32[1,20,8,128]{3,2,1,0:T(8,128)S(1)}, f32[1,20,8,128]{3,2,1,0:T(8,128)S(1)}, u32[]{:S(2)}, u32[]{:S(2)}) collective-permute-start(f32[1,20,8,128]{3,2,1,0:T(8,128)S(1)} %slice_select_fusion.7), channel_id=1, source_target_pairs={{0,8},{2,10},{4,12},{6,14},{8,0},{10,2},{12,4},{14,6},{1,9},{3,11}... | collective-permute-start | bytes 245768 | tf_op jit(solution)/shard_map/ppermute | solution.py:69
  54.7 5.0 %collective-permute-start.7 = (bf16[1,20,8,128]{3,2,1,0:T(8,128)(2,1)S(1)}, bf16[1,20,8,128]{3,2,1,0:T(8,128)(2,1)S(1)}, u32[]{:S(2)}, u32[]{:S(2)}) collective-permute-start(bf16[1,20,8,128]{3,2,1,0:T(8,128)(2,1)S(1)} %add_convert_fusion), channel_id=1, source_target_pairs={{0,8},{2,10},{4,12},{6,14},{8,0},{10,2},{12,4},{14,6},{1,9},{3,11}... | collective-permute-start | bytes 122888 | tf_op jit(solution)/shard_map/ppermute | solution.py:86
  60.4 2.6 %copy-start.9 = (f32[2,20,512]{2,0,1:T(2,128)S(1)}, f32[2,20,512]{2,0,1:T(2,128)}, u32[]{:S(2)}) copy-start(f32[2,20,512]{2,0,1:T(2,128)} %exp.28) | copy-start | bytes 245764
  60.4 10.7 %collective-permute-start.8 = (bf16[2,20,8,128]{3,2,1,0:T(8,128)(2,1)}, bf16[2,20,8,128]{3,2,1,0:T(8,128)(2,1)}, u32[]{:S(2)}, u32[]{:S(2)}) collective-permute-start(bf16[2,20,8,128]{3,2,1,0:T(8,128)(2,1)} %maximum_select_fusion.7), channel_id=1, source_target_pairs={{0,4},{2,6},{4,0},{6,2},{8,12},{10,14},{12,8},{14,10},{1,5},{3,7},... | collective-permute-start | bytes 245768 | tf_op jit(solution)/shard_map/ppermute | solution.py:86
  63.6 10.5 %collective-permute-start.12 = (f32[4,20,8,128]{3,2,1,0:T(8,128)}, f32[4,20,8,128]{3,2,1,0:T(8,128)}, u32[]{:S(2)}, u32[]{:S(2)}) collective-permute-start(f32[4,20,8,128]{3,2,1,0:T(8,128)} %bitcast.34), channel_id=1, source_target_pairs={{0,2},{2,0},{4,6},{6,4},{8,10},{10,8},{12,14},{14,12},{1,3},{3,1},... | collective-permute-start | bytes 983048 | tf_op jit(solution)/shard_map/ppermute | solution.py:69
  72.1 28.7 %collective-permute-start.9 = (bf16[4,20,8,128]{3,2,1,0:T(8,128)(2,1)S(1)}, bf16[4,20,8,128]{3,2,1,0:T(8,128)(2,1)S(1)}, u32[]{:S(2)}, u32[]{:S(2)}) collective-permute-start(bf16[4,20,8,128]{3,2,1,0:T(8,128)(2,1)S(1)} %maximum_select_fusion.3), channel_id=1, source_target_pairs={{0,2},{2,0},{4,6},{6,4},{8,10},{10,8},{12,14},{14,12},{1,3},{3,1},... | collective-permute-start | bytes 491528 | tf_op jit(solution)/shard_map/ppermute | solution.py:86
  75.2 8.7 %collective-permute-start.13 = (f32[2,20,8,128]{3,2,1,0:T(8,128)S(1)}, f32[2,20,8,128]{3,2,1,0:T(8,128)S(1)}, u32[]{:S(2)}, u32[]{:S(2)}) collective-permute-start(f32[2,20,8,128]{3,2,1,0:T(8,128)S(1)} %slice_select_fusion.6), channel_id=1, source_target_pairs={{0,4},{2,6},{4,0},{6,2},{8,12},{10,14},{12,8},{14,10},{1,5},{3,7},... | collective-permute-start | bytes 491528 | tf_op jit(solution)/shard_map/ppermute | solution.py:69
  77.3 1.7 %copy-start.3 = (bf16[2,512,20,64]{1,3,2,0:T(8,128)(2,1)S(1)}, bf16[2,512,20,64]{1,3,2,0:T(8,128)(2,1)}, u32[]{:S(2)}) copy-start(bf16[2,512,20,64]{1,3,2,0:T(8,128)(2,1)} %get-tuple-element.91) | copy-start | bytes 7864324
  79.0 1.8 %copy-start.8 = (bf16[2,512,128]{2,1,0:T(8,128)(2,1)S(1)}, bf16[2,512,128]{2,1,0:T(8,128)(2,1)}, u32[]{:S(2)}) copy-start(bf16[2,512,128]{2,1,0:T(8,128)(2,1)} %param.13) | copy-start | bytes 786436
  80.8 5.2 %copy-start.11 = (f32[2,20,512]{2,0,1:T(2,128)S(1)}, f32[2,20,512]{2,0,1:T(2,128)}, u32[]{:S(2)}) copy-start(f32[2,20,512]{2,0,1:T(2,128)} %copy-done.10) | copy-start | bytes 245764
  80.8 5.3 %copy-start.4 = (f32[2,512,512]{2,1,0:T(8,128)S(1)}, f32[2,512,512]{2,1,0:T(8,128)}, u32[]{:S(2)}) copy-start(f32[2,512,512]{2,1,0:T(8,128)} %fusion.28) | copy-start | bytes 6291460
  81.9 4.2 %copy-start.2 = (bf16[2,512,1280]{1,2,0:T(8,128)(2,1)S(1)}, bf16[2,512,1280]{1,2,0:T(8,128)(2,1)}, u32[]{:S(2)}) copy-start(bf16[2,512,1280]{1,2,0:T(8,128)(2,1)} %copy-done.1) | copy-start | bytes 7864324
  83.9 9.8 %collective-permute-start.14 = (f32[1,20,8,128]{3,2,1,0:T(8,128)S(1)}, f32[1,20,8,128]{3,2,1,0:T(8,128)S(1)}, u32[]{:S(2)}, u32[]{:S(2)}) collective-permute-start(f32[1,20,8,128]{3,2,1,0:T(8,128)S(1)} %slice_select_fusion.8), channel_id=1, source_target_pairs={{0,8},{2,10},{4,12},{6,14},{8,0},{10,2},{12,4},{14,6},{1,9},{3,11}... | collective-permute-start | bytes 245768 | tf_op jit(solution)/shard_map/ppermute | solution.py:69
  93.7 5.0 %collective-permute-start.15 = (bf16[1,20,8,128]{3,2,1,0:T(8,128)(2,1)S(1)}, bf16[1,20,8,128]{3,2,1,0:T(8,128)(2,1)S(1)}, u32[]{:S(2)}, u32[]{:S(2)}) collective-permute-start(bf16[1,20,8,128]{3,2,1,0:T(8,128)(2,1)S(1)} %select_add_fusion.2), channel_id=1, source_target_pairs={{0,8},{2,10},{4,12},{6,14},{8,0},{10,2},{12,4},{14,6},{1,9},{3,11}... | collective-permute-start | bytes 122888 | tf_op jit(solution)/shard_map/ppermute | solution.py:86
  98.7 4.5 %collective-permute-start.16 = (bf16[2,20,8,128]{3,2,1,0:T(8,128)(2,1)S(1)}, bf16[2,20,8,128]{3,2,1,0:T(8,128)(2,1)S(1)}, u32[]{:S(2)}, u32[]{:S(2)}) collective-permute-start(bf16[2,20,8,128]{3,2,1,0:T(8,128)(2,1)S(1)} %maximum_select_fusion.8), channel_id=1, source_target_pairs={{0,4},{2,6},{4,0},{6,2},{8,12},{10,14},{12,8},{14,10},{1,5},{3,7},... | collective-permute-start | bytes 245768 | tf_op jit(solution)/shard_map/ppermute | solution.py:86
  103.2 5.4 %collective-permute-start.17 = (bf16[4,20,8,128]{3,2,1,0:T(8,128)(2,1)S(1)}, bf16[4,20,8,128]{3,2,1,0:T(8,128)(2,1)S(1)}, u32[]{:S(2)}, u32[]{:S(2)}) collective-permute-start(bf16[4,20,8,128]{3,2,1,0:T(8,128)(2,1)S(1)} %maximum_select_fusion.4), channel_id=1, source_target_pairs={{0,2},{2,0},{4,6},{6,4},{8,10},{10,8},{12,14},{14,12},{1,3},{3,1},... | collective-permute-start | bytes 491528 | tf_op jit(solution)/shard_map/ppermute | solution.py:86
  103.8 6.9 %collective-permute-start.10 = (bf16[20,64,128]{2,1,0:T(8,128)(2,1)S(1)}, bf16[20,64,128]{2,1,0:T(8,128)(2,1)S(1)}, u32[]{:S(2)}, u32[]{:S(2)}) collective-permute-start(bf16[20,64,128]{2,1,0:T(8,128)(2,1)S(1)} %copy_bitcast_fusion), channel_id=1, source_target_pairs={{0,1},{1,0},{2,3},{3,2},{4,5},{5,4},{6,7},{7,6},{8,9},{9,8},{10,11... | collective-permute-start | bytes 983048 | tf_op jit(solution)/shard_map/ppermute | solution.py:110
  109.7 1.8 %copy-start.6 = (bf16[256,2560]{0,1:T(8,128)(2,1)S(1)}, bf16[256,2560]{0,1:T(8,128)(2,1)}, u32[]{:S(2)}) copy-start(bf16[256,2560]{0,1:T(8,128)(2,1)} %copy.155) | copy-start | bytes 3932164
  109.7 1.8 %copy-start.16 = (f32[256,40]{0,1:T(8,128)S(1)}, f32[256,40]{0,1:T(8,128)}, u32[]{:S(2)}) copy-start(f32[256,40]{0,1:T(8,128)} %copy-done.15) | copy-start | bytes 122884
  110.7 10.0 %collective-permute-start.18 = (f32[2,256,256]{2,1,0:T(8,128)}, f32[2,256,256]{2,1,0:T(8,128)S(1)}, u32[]{:S(2)}, u32[]{:S(2)}) collective-permute-start(f32[2,256,256]{2,1,0:T(8,128)} %select_bitcast_fusion), channel_id=1, source_target_pairs={{0,1},{1,0},{2,3},{3,2},{4,5},{5,4},{6,7},{7,6},{8,9},{9,8},{10,11... | collective-permute-start | bytes 1572872 | tf_op jit(solution)/shard_map/ppermute | solution.py:110
  110.7 0.7 copy-start.18

commit v14 on v9

--- a/solution.py
+++ b/solution.py
@@ -59,9 +59,9 @@
     for bit in range(nbits):
         step = 1 << bit
         value = value.reshape((2, -1) + rest)
-        upper = me // step % 2 == 1
-        keep = jnp.where(upper, value[1], value[0])
-        give = jnp.where(upper, value[0], value[1])
+        upper = me // step % 2
+        keep = lax.dynamic_index_in_dim(value, upper, 0, keepdims=False)
+        give = lax.dynamic_index_in_dim(value, 1 - upper, 0, keepdims=False)
         value = keep + lax.ppermute(give, axis, [(at, at ^ step) for at in range(count)])
     return value[0]
 
@@ -155,8 +155,8 @@
     seq_at = lax.axis_index("seq")
     state_halves = state_full.reshape(2, half_heads, head_size, nstate)
     mine_first = seq_at == 0
-    own_half = jnp.where(mine_first, state_halves[0], state_halves[1])
-    give_half = jnp.where(mine_first, state_halves[1], state_halves[0])
+    own_half = lax.dynamic_index_in_dim(state_halves, seq_at, 0, keepdims=False)
+    give_half = lax.dynamic_index_in_dim(state_halves, 1 - seq_at, 0, keepdims=False)
     init_local = own_half + other_core(give_half)
 
     grad_half = cand_sum_bf16(dstate)
@@ -201,8 +201,8 @@
     dc_total = dc_part + dc_state.reshape(cand_dev, cand_len, nstate)
     def token_half_sum(part):
         halves = part.reshape(cand_dev, 2, cand_len // 2, part.shape[2])
-        own = jnp.where(mine_first, halves[:, 0], halves[:, 1])
-        give = jnp.where(mine_first, halves[:, 1], halves[:, 0])
+        own = lax.dynamic_index_in_dim(halves, seq_at, 1, keepdims=False)
+        give = lax.dynamic_index_in_dim(halves, 1 - seq_at, 1, keepdims=False)
         return own + other_core(give)
 
     db_dc = token_half_sum(jnp.concatenate([db_part, dc_total], axis=2))

time: 114 us -> 113 us (level)
  other arithmetic: 18.4 us -> 15.3 us
  local copies, waits for them, and re-layouts: 25.2 us -> 26.8 us
    dynamic_slice x0 -> x3, local copies, waits for them, and re-layouts: none -> 2.28 us  [the longest x2 1.24 us: token_half_sum(): own = lax.dynamic_index_in_dim(halves, seq_at, 1, keepdims=False)]
    add x3, other arithmetic: 1.49 us -> 0.01 us  [suffix_sum(): value = value + lax.ppermute(value, axis, back)]
  transfers between devices with their start and end apart: 19 -> 19, of which waited for: 8 -> 8; matrix products, arithmetic and copies ran while one was open for 54% -> 55% of each run, Pallas kernels for 0% -> 0%
where the time goes in v14:
time: 113 us; the launch traced here: 112 us
  local copies, waits for them, and re-layouts  26.8 us (24%)
  starting transfers between devices  26.1 us (23%)
  matrix products  21.8 us (19%)
  waiting for transfers between devices  20.7 us (18%)
  other arithmetic  15.3 us (14%)
  between operations  1.36 us (1%)
    ppermute x6, waiting for transfers between devices, halving_scatter(): lax.ppermute(give, axis, [(at, at ^ step) for at in range(count)])  14 us
    ppermute x6, starting transfers between devices, halving_scatter(): lax.ppermute(give, axis, [(at, at ^ step) for at in range(count)])  13.9 us
    optimization_barrier x4, local copies, waits for them, and re-layouts, suffix_sum(): value, args = lax.optimization_barrier((value, pick(done)))  8.96 us
    unnamed x44, local copies, waits for them, and re-layouts  8.58 us
    ppermute x6, waiting for transfers between devices, doubling_gather(): other = lax.ppermute(value, axis, [(at, at ^ step) for at in range(count)])  6.7 us
    ppermute x6, starting transfers between devices, doubling_gather(): other = lax.ppermute(value, axis, [(at, at ^ step) for at in range(count)])  6.53 us
    dot_general x1, matrix products, shards(): jnp.einsum('chts,cthp->cshp', kernel, g_heads, preferred_element_type=jnp...  6.53 us
    convert_element_type x2, other arithmetic, split_bf16(): low = (value - high).astype(jnp.bfloat16)  5.78 us
  transfers between devices with their start and end apart: 19, of which 8 were waited for; matrix products, arithmetic and copies ran while one was open for 55% of the time, Pallas kernels for 0%

profile of v14, /device:TPU:0, one launch (start us, length us, event | category | flops | bytes accessed | tf_op | source)
XLA Modules:
  0.0 112.1 jit_solution(18115951732118472243)
XLA Ops:
  0.7 1.0 fusion.22
  1.7 1.3 %collective-permute-start = (f32[40]{0:T(128)S(1)}, f32[40]{0:T(128)S(1)}, u32[]{:S(2)}, u32[]{:S(2)}) collective-permute-start(f32[40]{0:T(128)S(1)} %get-tuple-element.29), channel_id=1, source_target_pairs={{1,0},{2,1},{3,2},{4,3},{5,4},{6,5},{7,6},{8,7},{9,8},{10,9},{11,1... | collective-permute-start | bytes 488 | tf_op jit(solution)/shard_map/ppermute | solution.py:35
  3.1 0.8 iota_compare_fusion
  3.9 0.6 reduce-window.16
  4.6 1.0 log-plus-one_bitcast_fusion
  5.8 2.3 %reduce-window.14 = f32[2,20,4,128]{3,1,2,0:T(8,128)S(1)} reduce-window(f32[2,20,4,128]{3,1,2,0:T(8,128)S(1)} %copy.135, f32[]{:T(128)} %constant.154.clone.1), window={size=1x1x1x128 pad=0_0x0_0x0_0x127_0}, to_apply=%region_1.0 | reduce-window | flops 2600960 | bytes 163844 | tf_op jit(solution)/shard_map/reduce-window
  8.7 1.6 %copy.148 = f32[256,128]{0,1:T(8,128)} copy(bf16[256,128]{1,0:T(8,128)(2,1)} %param.10) | data formatting | bytes 196608 | tf_op jit(solution)/shard_map/convert_element_type | solution.py:150
  10.3 1.4 %copy.150 = bf16[256,2560]{0,1:T(8,128)(2,1)} copy(bf16[256,2560]{1,0:T(8,128)(2,1)S(1)} %copy-done.6) | data formatting | bytes 2621440 | tf_op args[0]
  11.8 1.3 %collective-permute-start.1 = (f32[40]{0:T(128)S(1)}, f32[40]{0:T(128)S(1)}, u32[]{:S(2)}, u32[]{:S(2)}) collective-permute-start(f32[40]{0:T(128)S(1)} %add.120), channel_id=1, source_target_pairs={{2,0},{3,1},{4,2},{5,3},{6,4},{7,5},{8,6},{9,7},{10,8},{11,9},{12,... | collective-permute-start | bytes 488 | tf_op jit(solution)/shard_map/ppermute | solution.py:35
  13.1 3.0 %copy.138 = bf16[2,512,1280]{1,2,0:T(8,128)(2,1)S(1)} copy(bf16[2,512,1280]{2,1,0:T(8,128)(2,1)} %param.17) | data formatting | bytes 5242880 | tf_op jit(solution)/shard_map/optimization_barrier | solution.py:34
  16.3 2.8 %fusion.6 = (bf16[2,512,20,64]{1,3,2,0:T(8,128)(2,1)}, bf16[2,512,20,64]{1,3,2,0:T(8,128)(2,1)S(1)}) fusion(bf16[2,512,20,64]{1,3,2,0:T(8,128)(2,1)S(1)} %bitcast.141, f32[2,512,20]{1,2,0:T(8,128)S(1)} %copy.139), kind=kLoop, calls=%fused_computation.11 | loop fusion | flops 7864320 | bytes 7946240 | tf_op jit(solution)/shard_map/convert_element_type | solution.py:11
  19.1 0.8 convolution_bitcast_fusion
  19.9 0.7 copy.152
  20.6 0.6 copy.151
  21.3 1.3 %collective-permute-start.9 = (f32[40]{0:T(128)S(1)}, f32[40]{0:T(128)S(1)}, u32[]{:S(2)}, u32[]{:S(2)}) collective-permute-start(f32[40]{0:T(128)S(1)} %add.121), channel_id=1, source_target_pairs={{4,0},{5,1},{6,2},{7,3},{8,4},{9,5},{10,6},{11,7},{12,8},{13,9},{1... | collective-permute-start | bytes 488 | tf_op jit(solution)/shard_map/ppermute | solution.py:35
  22.6 1.5 %copy.147 = f32[2,512,20]{1,2,0:T(8,128)} copy(f32[2,512,20]{1,0,2:T(2,128)} %bitcast.168) | data formatting | bytes 163840 | tf_op jit(solution)/shard_map/optimization_barrier | solution.py:34
  24.1 0.8 dynamic-slice_bitcast_fusion.2
  24.9 4.2 %collective-permute-start.2 = (f32[4,20,8,128]{3,2,1,0:T(8,128)}, f32[4,20,8,128]{3,2,1,0:T(8,128)}, u32[]{:S(2)}, u32[]{:S(2)}) collective-permute-start(f32[4,20,8,128]{3,2,1,0:T(8,128)} %dynamic-slice_bitcast_fusion.2), channel_id=1, source_target_pairs={{0,2},{2,0},{4,6},{6,4},{8,10},{10,8},{12,14},{14,12},{1,3},{3,1},... | collective-permute-start | bytes 983048 | tf_op jit(solution)/shard_map/ppermute | solution.py:65
  29.1 4.4 %copy.146 = bf16[2,512,1280]{1,2,0:T(8,128)(2,1)} copy(bf16[2,512,1280]{2,1,0:T(8,128)(2,1)} %param.12) | data formatting | bytes 5242880 | tf_op jit(solution)/shard_map/optimization_barrier | solution.py:34
  33.5 3.0 %fusion.7 = (bf16[2,512,20,64]{1,3,2,0:T(8,128)(2,1)S(1)}, bf16[2,512,20,64]{1,3,2,0:T(8,128)(2,1)S(1)}) fusion(bf16[2,512,20,64]{1,3,2,0:T(8,128)(2,1)} %bitcast.143, f32[2,512,20]{1,2,0:T(8,128)} %copy.147), kind=kLoop, calls=%fused_computation.12 | loop fusion | flops 7864320 | bytes 7946240 | tf_op jit(solution)/shard_map/convert_element_type | solution.py:11
  36.6 0.4 fusion.27
  37.0 1.6 %collective-permute-start.10 = (f32[40]{0:T(128)S(1)}, f32[40]{0:T(128)S(1)}, u32[]{:S(2)}, u32[]{:S(2)}) collective-permute-start(f32[40]{0:T(128)S(1)} %add.131), channel_id=1, source_target_pairs={{8,0},{9,1},{10,2},{11,3},{12,4},{13,5},{14,6},{15,7},{24,16},{25,... | collective-permute-start | bytes 488 | tf_op jit(solution)/shard_map/ppermute | solution.py:35
  38.7 6.5 %fusion.15 = bf16[2,20,64,512]{3,2,1,0:T(8,128)(2,1)} fusion(bf16[2,512,20,64]{1,3,2,0:T(8,128)(2,1)S(1)} %bitcast.142, f32[2,20,512]{2,1,0:T(8,128)S(1)} %copy-done.14, f32[2,20,512]{2,1,0:T(8,128)S(1)} %copy-done.15, f32[2,512,512]{2,1,0:T(8,128)S(1)} %fusion.27, pred[512,512]{1,0:T(8,128)(4,1)S(1)} %copy-done.4), kind=kOutput, calls=%fused_computation.26 | convolution fusion | flops 1385431040 | bytes 7766016 | tf_op jit(solution)/shard_map/chts,cthp->cshp/dot_general | solution.py:193
  45.2 1.6 %fusion.28 = f32[2,512,512]{2,1,0:T(8,128)S(1)} fusion(bf16[2,512,1280]{1,2,0:T(8,128)(2,1)S(1)} %bitcast.138, bf16[2,512,1280]{1,2,0:T(8,128)(2,1)S(1)} %bitcast.145), kind=kOutput, calls=%fused_computation.80 | convolution fusion | flops 1342177280 | bytes 7340032 | tf_op jit(solution)/shard_map/ctk,csk->cts/dot_general | solution.py:175
  47.0 1.0 fusion.9
  48.4 1.0 bitcast_add_fusion.3
  49.4 3.4 %collective-permute-start.3 = (f32[2,20,8,128]{3,2,1,0:T(8,128)S(1)}, f32[2,20,8,128]{3,2,1,0:T(8,128)S(1)}, u32[]{:S(2)}, u32[]{:S(2)}) collective-permute-start(f32[2,20,8,128]{3,2,1,0:T(8,128)S(1)} %dynamic-slice_bitcast_fusion.4), channel_id=1, source_target_pairs={{0,4},{2,6},{4,0},{6,2},{8,12},{10,14},{12,8},{14,10},{1,5},{3,7},... | collective-permute-start | bytes 491528 | tf_op jit(solution)/shard_map/ppermute | solution.py:65
  52.8 1.6 %fusion.29 = f32[2,512,512]{2,1,0:T(8,128)S(1)} fusion(bf16[2,512,1280]{1,2,0:T(8,128)(2,1)S(1)} %bitcast.139, bf16[2,512,1280]{1,2,0:T(8,128)(2,1)S(1)} %bitcast.149), kind=kOutput, calls=%fused_computation.81 | convolution fusion | flops 1342177280 | bytes 7340032 | tf_op jit(solution)/shard_map/ctk,csk->cts/dot_general | solution.py:175
  54.4 3.2 %collective-permute-done.3 = f32[2,20,8,128]{3,2,1,0:T(8,128)S(1)} collective-permute-done((f32[2,20,8,128]{3,2,1,0:T(8,128)S(1)}, f32[2,20,8,128]{3,2,1,0:T(8,128)S(1)}, u32[]{:S(2)}, u32[]{:S(2)}) %collective-permute-start.3) | collective-permute-done | bytes 163872 | tf_op jit(solution)/shard_map/ppermute | solution.py:65
  57.7 3.6 %collective-permute-start.4 = (f32[1,20,8,128]{3,2,1,0:T(8,128)S(1)}, f32[1,20,8,128]{3,2,1,0:T(8,128)S(1)}, u32[]{:S(2)}, u32[]{:S(2)}) collective-permute-start(f32[1,20,8,128]{3,2,1,0:T(8,128)S(1)} %constant_dynamic-slice_fusion.3), channel_id=1, source_target_pairs={{0,8},{2,10},{4,12},{6,14},{8,0},{10,2},{12,4},{14,6},{1,9},{3,11}... | collective-permute-start | bytes 245768 | tf_op jit(solution)/shard_map/ppermute | solution.py:65
  61.5 0.6 collective-permute-start.12
  62.1 1.8 %add_select_fusion = f32[2,512,512]{2,1,0:T(8,128)S(1)} fusion(f32[2,512,512]{2,1,0:T(8,128)S(1)} %fusion.28, f32[2,512,512]{2,1,0:T(8,128)S(1)} %fusion.29, bf16[2,512,1280]{1,2,0:T(8,128)(2,1)S(1)} %bitcast.144, bf16[2,512,1280]{1,2,0:T(8,128)(2,1)S(1)} %bitcast.146, pred[512,512]{1,0:T(8,128)(4,1)S(1)} %copy-done.4), kind=kOutput, calls=%fused_computation.25 | convolution fusion | flops 1343750144 | bytes 11796480 | tf_op jit(solution)/shard_map/ctk,csk->cts/dot_general | solution.py:175
  63.9 1.7 %collective-permute-done.4 = f32[1,20,8,128]{3,2,1,0:T(8,128)S(1)} collective-permute-done((f32[1,20,8,128]{3,2,1,0:T(8,128)S(1)}, f32[1,20,8,128]{3,2,1,0:T(8,128)S(1)}, u32[]{:S(2)}, u32[]{:S(2)}) %collective-permute-start.4) | collective-permute-done | bytes 81952 | tf_op jit(solution)/shard_map/ppermute | solution.py:65
  65.6 1.1 %collective-permute-start.5 = (bf16[1,20,8,128]{3,2,1,0:T(8,128)(2,1)S(1)}, bf16[1,20,8,128]{3,2,1,0:T(8,128)(2,1)S(1)}, u32[]{:S(2)}, u32[]{:S(2)}) collective-permute-start(bf16[1,20,8,128]{3,2,1,0:T(8,128)(2,1)S(1)} %add_convert_fusion.1), channel_id=1, source_target_pairs={{0,8},{2,10},{4,12},{6,14},{8,0},{10,2},{12,4},{14,6},{1,9},{3,11}... | collective-permute-start | bytes 122888 | tf_op jit(solution)/shard_map/ppermute | solution.py:76
  66.7 4.1 %collective-permute-done.12 = f32[4,20,8,128]{3,2,1,0:T(8,128)S(1)} collective-permute-done((f32[4,20,8,128]{3,2,1,0:T(8,128)S(1)}, f32[4,20,8,128]{3,2,1,0:T(8,128)S(1)}, u32[]{:S(2)}, u32[]{:S(2)}) %collective-permute-start.12) | collective-permute-done | bytes 327712 | tf_op jit(solution)/shard_map/ppermute | solution.py:65
  70.9 1.6 %collective-permute-start.13 = (f32[2,20,8,128]{3,2,1,0:T(8,128)S(1)}, f32[2,20,8,128]{3,2,1,0:T(8,128)S(1)}, u32[]{:S(2)}, u32[]{:S(2)}) collective-permute-start(f32[2,20,8,128]{3,2,1,0:T(8,128)S(1)} %dynamic-slice_bitcast_fusion.3), channel_id=1, source_target_pairs={{0,4},{2,6},{4,0},{6,2},{8,12},{10,14},{12,8},{14,10},{1,5},{3,7},... | collective-permute-start | bytes 491528 | tf_op jit(solution)/shard_map/ppermute | solution.py:65
  72.5 1.3 %fusion.31 = f32[2,512,128]{1,2,0:T(8,128)S(1)} fusion(f32[2,512,512]{2,1,0:T(8,128)S(1)} %add_select_fusion, bf16[2,512,128]{2,1,0:T(8,128)(2,1)S(1)} %copy-done.8), kind=kOutput, calls=%fused_computation.83 | convolution fusion | flops 805306368 | bytes 2883584 | tf_op jit(solution)/shard_map/cts,csn->ctn/dot_general | solution.py:185
  73.8 0.6 collective-permute-start.6
  74.4 2.8 %collective-permute-done.13 = f32[2,20,8,128]{3,2,1,0:T(8,128)S(1)} collective-permute-done((f32[2,20,8,128]{3,2,1,0:T(8,128)S(1)}, f32[2,20,8,128]{3,2,1,0:T(8,128)S(1)}, u32[]{:S(2)}, u32[]{:S(2)}) %collective-permute-start.13) | collective-permute-done | bytes 163872 | tf_op jit(solution)/shard_map/ppermute | solution.py:65
  77.2 0.4 collective-permute-start.14
  77.6 1.6 %collective-permute-done.6 = bf16[2,20,8,128]{3,2,1,0:T(8,128)(2,1)S(1)} collective-permute-done((bf16[2,20,8,128]{3,2,1,0:T(8,128)(2,1)S(1)}, bf16[2,20,8,128]{3,2,1,0:T(8,128)(2,1)S(1)}, u32[]{:S(2)}, u32[]{:S(2)}) %collective-permute-start.6) | collective-permute-done | bytes 81952 | tf_op jit(solution)/shard_map/ppermute | solution.py:76
  79.2 0.7 maximum_select_fusion.3
  79.8 0.6 collective-permute-start.7
  80.4 2.2 %collective-permute-done.14 = f32[1,20,8,128]{3,2,1,0:T(8,128)S(1)} collective-permute-done((f32[1,20,8,128]{3,2,1,0:T(8,128)S(1)}, f32[1,20,8,128]{3,2,1,0:T(8,128)S(1)}, u32[]{:S(2)}, u32[]{:S(2)}) %collective-permute-start.14) | collective-permute-done | bytes 81952 | tf_op jit(solution)/shard_map/ppermute | solution.py:65
  82.6 0.4 collective-permute-start.15
  83.1 1.7 %fusion.30 = f32[2,512,128]{1,2,0:T(8,128)} fusion(f32[2,512,512]{2,1,0:T(8,128)S(1)} %add_select_fusion, bf16[2,512,128]{2,1,0:T(8,128)(2,1)S(1)} %copy-done), kind=kOutput, calls=%fused_computation.82 | convolution fusion | flops 805306368 | bytes 2883584 | tf_op jit(solution)/shard_map/cts,ctn->csn/dot_general | solution.py:182
  84.8 4.4 %copy.172 = bf16[2,512,1280]{2,1,0:T(8,128)(2,1)} copy(bf16[2,512,1280]{1,2,0:T(8,128)(2,1)} %bitcast.148) | data formatting | bytes 5242880
  89.1 3.2 %collective-permute-start.16 = (bf16[2,20,8,128]{3,2,1,0:T(8,128)(2,1)S(1)}, bf16[2,20,8,128]{3,2,1,0:T(8,128)(2,1)S(1)}, u32[]{:S(2)}, u32[]{:S(2)}) collective-permute-start(bf16[2,20,8,128]{3,2,1,0:T(8,128)(2,1)S(1)} %maximum_select_fusion.8), channel_id=1, source_target_pairs={{0,4},{2,6},{4,0},{6,2},{8,12},{10,14},{12,8},{14,10},{1,5},{3,7},... | collective-permute-start | bytes 245768 | tf_op jit(solution)/shard_map/ppermute | solution.py:76
  92.4 1.2 %maximum_select_fusion.1 = bf16[8,20,8,128]{3,2,1,0:T(8,128)(2,1)S(1)} fusion(bf16[4,20,8,128]{3,2,1,0:T(8,128)(2,1)} %maximum_select_fusion.3, bf16[4,20,8,128]{3,2,1,0:T(8,128)(2,1)} %collective-permute-done.7, pred[]{:T(512)S(6)} %eq.29), kind=kLoop, calls=%fused_computation.36 | loop fusion | flops 491520 | bytes 655361 | tf_op jit(solution)/shard_map/jit(_where)/select_n | solution.py:78
  93.6 1.2 %collective-permute-done.16 = bf16[2,20,8,128]{3,2,1,0:T(8,128)(2,1)S(1)} collective-permute-done((bf16[2,20,8,128]{3,2,1,0:T(8,128)(2,1)S(1)}, bf16[2,20,8,128]{3,2,1,0:T(8,128)(2,1)S(1)}, u32[]{:S(2)}, u32[]{:S(2)}) %collective-permute-start.16) | collective-permute-done | bytes 81952 | tf_op jit(solution)/shard_map/ppermute | solution.py:76
  94.8 0.6 collective-permute-start.17
  95.4 0.8 copy_bitcast_fusion
  96.3 3.9 %collective-permute-done.17 = bf16[4,20,8,128]{3,2,1,0:T(8,128)(2,1)S(1)} collective-permute-done((bf16[4,20,8,128]{3,2,1,0:T(8,128)(2,1)S(1)}, bf16[4,20,8,128]{3,2,1,0:T(8,128)(2,1)S(1)}, u32[]{:S(2)}, u32[]{:S(2)}) %collective-permute-start.17) | collective-permute-done | bytes 163872 | tf_op jit(solution)/shard_map/ppermute | solution.py:76
  100.3 0.6 convolution_add_fusion
  100.9 0.3 copy-done.5
  101.3 0.7 reshape.197
  102.0 0.9 constant_dynamic-slice_fusion.1
  102.9 1.0 copy.169
  104.0 2.7 %fusion.8 = f32[256,128]{0,1:T(8,128)S(1)} fusion(f32[256,40]{0,1:T(8,128)S(1)} %copy-done.17, bf16[256,40,64]{0,2,1:T(8,128)(2,1)} %bitcast.159, bf16[20,64,128]{2,1,0:T(8,128)(2,1)} %collective-permute-done.8, bf16[20,64,128]{2,1,0:T(8,128)(2,1)} %copy_bitcast_fusion, pred[]{:T(512)S(6)} %eq.28), kind=kOutput, calls=%fused_computation.15 | convolution fusion | flops 171343872 | bytes 2138113 | tf_op jit(solution)/shard_map/jhp,hpn->jhn/dot_general | solution.py:215
  106.7 0.8 copy.171
  107.4 1.8 %fusion.16 = bf16[40,64,256]{2,1,0:T(8,128)(2,1)S(1)} fusion(f32[256,128]{0,1:T(8,128)S(1)} %copy-done.13, f32[256,40]{0,1:T(8,128)S(1)} %copy-done.17, bf16[20,64,128]{2,1,0:T(8,128)(2,1)} %collective-permute-done.8, bf16[20,64,128]{2,1,0:T(8,128)(2,1)} %copy_bitcast_fusion, pred[]{:T(512)S(6)} %eq.28), kind=kOutput, calls=%fused_computation.27 | convolution fusion | flops 172032000 | bytes 2138113 | tf_op jit(solution)/shard_map/jhn,hpn->jhp/dot_general | solution.py:211
  109.2 1.6 %copy.170 = bf16[256,2560]{1,0:T(8,128)(2,1)} copy(bf16[256,2560]{0,1:T(8,128)(2,1)S(1)} %bitcast.163) | data formatting | bytes 2621440
  110.8 0.3 copy.168
  111.2 0.8 fusion.26
  (100 shorter events, 2.4 us)
Async XLA Ops:
  0.6 18.5 %copy-start = (bf16[2,512,128]{2,1,0:T(8,128)(2,1)S(1)}, bf16[2,512,128]{2,1,0:T(8,128)(2,1)}, u32[]{:S(2)}) copy-start(bf16[2,512,128]{2,1,0:T(8,128)(2,1)} %param.14) | copy-start | bytes 786436
  0.6 9.6 %copy-start.6 = (bf16[256,2560]{1,0:T(8,128)(2,1)S(1)}, bf16[256,2560]{1,0:T(8,128)(2,1)}, u32[]{:S(2)}) copy-start(bf16[256,2560]{1,0:T(8,128)(2,1)} %param.9) | copy-start | bytes 3932164
  1.7 10.0 %collective-permute-start = (f32[40]{0:T(128)S(1)}, f32[40]{0:T(128)S(1)}, u32[]{:S(2)}, u32[]{:S(2)}) collective-permute-start(f32[40]{0:T(128)S(1)} %get-tuple-element.29), channel_id=1, source_target_pairs={{1,0},{2,1},{3,2},{4,3},{5,4},{6,5},{7,6},{8,7},{9,8},{10,9},{11,1... | collective-permute-start | bytes 488 | tf_op jit(solution)/shard_map/ppermute | solution.py:35
  3.0 8.7 %copy-start.19 = (s32[2]{0:T(128)S(1)}, s32[2]{0:T(128)}, u32[]{:S(2)}) copy-start(s32[2]{0:T(128)} %param.16) | copy-start | bytes 28
  4.4 1.3 %copy-start.10 = (f32[40,2,128]{2,0,1:T(8,128)}, f32[40,2,128]{2,0,1:T(8,128)S(1)}, u32[]{:S(2)}) copy-start(f32[40,2,128]{2,0,1:T(8,128)S(1)} %reduce-window.16) | copy-start | bytes 122884
  4.6 11.5 %copy-start.18 = (f32[40,3]{0,1:T(4,128)}, f32[40,3]{0,1:T(4,128)S(1)}, u32[]{:S(2)}) copy-start(f32[40,3]{0,1:T(4,128)S(1)} %reduce-window.19) | copy-start | bytes 1444
  8.5 11.4 %copy-start.9 = (f32[2,20,512]{2,0,1:T(2,128)}, f32[2,20,512]{2,0,1:T(2,128)S(1)}, u32[]{:S(2)}) copy-start(f32[2,20,512]{2,0,1:T(2,128)S(1)} %exp.28) | copy-start | bytes 245764
  11.8 9.5 %collective-permute-start.1 = (f32[40]{0:T(128)S(1)}, f32[40]{0:T(128)S(1)}, u32[]{:S(2)}, u32[]{:S(2)}) collective-permute-start(f32[40]{0:T(128)S(1)} %add.120), channel_id=1, source_target_pairs={{2,0},{3,1},{4,2},{5,3},{6,4},{7,5},{8,6},{9,7},{10,8},{11,9},{12,... | collective-permute-start | bytes 488 | tf_op jit(solution)/shard_map/ppermute | solution.py:35
  16.3 2.8 %copy-start.1 = (bf16[2,512,1280]{1,2,0:T(8,128)(2,1)}, bf16[2,512,1280]{1,2,0:T(8,128)(2,1)S(1)}, u32[]{:S(2)}) copy-start(bf16[2,512,1280]{1,2,0:T(8,128)(2,1)S(1)} %broadcast_select_fusion) | copy-start | bytes 7864324
  21.3 15.7 %collective-permute-start.9 = (f32[40]{0:T(128)S(1)}, f32[40]{0:T(128)S(1)}, u32[]{:S(2)}, u32[]{:S(2)}) collective-permute-start(f32[40]{0:T(128)S(1)} %add.121), channel_id=1, source_target_pairs={{4,0},{5,1},{6,2},{7,3},{8,4},{9,5},{10,6},{11,7},{12,8},{13,9},{1... | collective-permute-start | bytes 488 | tf_op jit(solution)/shard_map/ppermute | solution.py:35
  24.9 23.5 %collective-permute-start.2 = (f32[4,20,8,128]{3,2,1,0:T(8,128)}, f32[4,20,8,128]{3,2,1,0:T(8,128)}, u32[]{:S(2)}, u32[]{:S(2)}) collective-permute-start(f32[4,20,8,128]{3,2,1,0:T(8,128)} %dynamic-slice_bitcast_fusion.2), channel_id=1, source_target_pairs={{0,2},{2,0},{4,6},{6,4},{8,10},{10,8},{12,14},{14,12},{1,3},{3,1},... | collective-permute-start | bytes 983048 | tf_op jit(solution)/shard_map/ppermute | solution.py:65
  33.5 3.0 %copy-start.8 = (bf16[2,512,128]{2,1,0:T(8,128)(2,1)S(1)}, bf16[2,512,128]{2,1,0:T(8,128)(2,1)}, u32[]{:S(2)}) copy-start(bf16[2,512,128]{2,1,0:T(8,128)(2,1)} %param.13) | copy-start | bytes 786436
  33.5 5.1 %copy-start.4 = (pred[512,512]{1,0:T(8,128)(4,1)S(1)}, pred[512,512]{1,0:T(8,128)(4,1)}, u32[]{:S(2)}) copy-start(pred[512,512]{1,0:T(8,128)(4,1)} %iota_compare_fusion) | copy-start | bytes 786436
  33.5 5.1 %copy-start.14 = (f32[2,20,512]{2,1,0:T(8,128)S(1)}, f32[2,20,512]{2,1,0:T(8,128)}, u32[]{:S(2)}) copy-start(f32[2,20,512]{2,1,0:T(8,128)} %copy.152) | copy-start | bytes 245764
  33.5 5.1 %copy-start.15 = (f32[2,20,512]{2,1,0:T(8,128)S(1)}, f32[2,20,512]{2,1,0:T(8,128)}, u32[]{:S(2)}) copy-start(f32[2,20,512]{2,1,0:T(8,128)} %copy.151) | copy-start | bytes 245764
  36.6 2.1 %copy-start.2 = (bf16[2,512,1280]{1,2,0:T(8,128)(2,1)S(1)}, bf16[2,512,1280]{1,2,0:T(8,128)(2,1)}, u32[]{:S(2)}) copy-start(bf16[2,512,1280]{1,2,0:T(8,128)(2,1)} %copy-done.1) | copy-start | bytes 7864324
  37.0 9.8 %collective-permute-start.10 = (f32[40]{0:T(128)S(1)}, f32[40]{0:T(128)S(1)}, u32[]{:S(2)}, u32[]{:S(2)}) collective-permute-start(f32[40]{0:T(128)S(1)} %add.131), channel_id=1, source_target_pairs={{8,0},{9,1},{10,2},{11,3},{12,4},{13,5},{14,6},{15,7},{24,16},{25,... | collective-permute-start | bytes 488 | tf_op jit(solution)/shard_map/ppermute | solution.py:35
  45.2 1.6 %copy-start.11 = (f32[40,2,128]{2,0,1:T(8,128)S(1)}, f32[40,2,128]{2,0,1:T(8,128)}, u32[]{:S(2)}) copy-start(f32[40,2,128]{2,0,1:T(8,128)} %copy-done.10) | copy-start | bytes 122884
  45.2 1.6 %slice-start = ((f32[40,3]{0,1:T(4,128)}), f32[40,2]{0,1:T(2,128)S(1)}, s32[]{:S(2)}) async-start(f32[40,3]{0,1:T(4,128)} %copy-done.18), calls=%async_computation | async-start | bytes 2048 | tf_op jit(solution)/shard_map/slice.5
  45.2 1.8 %copy-start.7 = (bf16[256,2560]{0,1:T(8,128)(2,1)S(1)}, bf16[256,2560]{0,1:T(8,128)(2,1)}, u32[]{:S(2)}) copy-start(bf16[256,2560]{0,1:T(8,128)(2,1)} %copy.150) | copy-start | bytes 3932164
  45.2 1.8 %copy-start.12 = (f32[256,128]{0,1:T(8,128)S(1)}, f32[256,128]{0,1:T(8,128)}, u32[]{:S(2)}) copy-start(f32[256,128]{0,1:T(8,128)} %copy.148) | copy-start | bytes 393220
  47.0 2.4 %copy-start.16 = (f32[256,40]{0,1:T(8,128)}, f32[256,40]{0,1:T(8,128)S(1)}, u32[]{:S(2)}) copy-start(f32[256,40]{0,1:T(8,128)S(1)} %fusion.20) | copy-start | bytes 122884
  48.1 13.2 %collective-permute-start.11 = (f32[20,64,128]{2,1,0:T(8,128)S(1)}, f32[20,64,128]{2,1,0:T(8,128)S(1)}, u32[]{:S(2)}, u32[]{:S(2)}) collective-permute-start(f32[20,64,128]{2,1,0:T(8,128)S(1)} %dynamic-slice_bitcast_fusion), channel_id=1, source_target_pairs={{0,1},{1,0},{2,3},{3,2},{4,5},{5,4},{6,7},{7,6},{8,9},{9,8},{10,11... | collective-permute-start | bytes 1966088 | tf_op jit(solution)/shard_map/ppermute | solution.py:100
  49.4 8.3 %collective-permute-start.3 = (f32[2,20,8,128]{3,2,1,0:T(8,128)S(1)}, f32[2,20,8,128]{3,2,1,0:T(8,128)S(1)}, u32[]{:S(2)}, u32[]{:S(2)}) collective-permute-start(f32[2,20,8,128]{3,2,1,0:T(8,128)S(1)} %dynamic-slice_bitcast_fusion.4), channel_id=1, source_target_pairs={{0,4},{2,6},{4,0},{6,2},{8,12},{10,14},{12,8},{14,10},{1,5},{3,7},... | collective-permute-start | bytes 491528 | tf_op jit(solution)/shard_map/ppermute | solution.py:65
  54.4 7.7 %copy-start.3 = (bf16[2,512,20,64]{1,3,2,0:T(8,128)(2,1)S(1)}, bf16[2,512,20,64]{1,3,2,0:T(8,128)(2,1)}, u32[]{:S(2)}) copy-start(bf16[2,512,20,64]{1,3,2,0:T(8,128)(2,1)} %get-tuple-element.52) | copy-start | bytes 7864324
  57.7 7.9 %collective-permute-start.4 = (f32[1,20,8,128]{3,2,1,0:T(8,128)S(1)}, f32[1,20,8,128]{3,2,1,0:T(8,128)S(1)}, u32[]{:S(2)}, u32[]{:S(2)}) collective-permute-start(f32[1,20,8,128]{3,2,1,0:T(8,128)S(1)} %constant_dynamic-slice_fusion.3), channel_id=1, source_target_pairs={{0,8},{2,10},{4,12},{6,14},{8,0},{10,2},{12,4},{14,6},{1,9},{3,11}... | collective-permute-start | bytes 245768 | tf_op jit(solution)/shard_map/ppermute | solution.py:65
  61.5 9.3 %collective-permute-start.12 = (f32[4,20,8,128]{3,2,1,0:T(8,128)S(1)}, f32[4,20,8,128]{3,2,1,0:T(8,128)S(1)}, u32[]{:S(2)}, u32[]{:S(2)}) collective-permute-start(f32[4,20,8,128]{3,2,1,0:T(8,128)S(1)} %dynamic-slice_bitcast_fusion.1), channel_id=1, source_target_pairs={{0,2},{2,0},{4,6},{6,4},{8,10},{10,8},{12,14},{14,12},{1,3},{3,1},... | collective-permute-start | bytes 983048 | tf_op jit(solution)/shard_map/ppermute | solution.py:65
  65.6 8.2 %collective-permute-start.5 = (bf16[1,20,8,128]{3,2,1,0:T(8,128)(2,1)S(1)}, bf16[1,20,8,128]{3,2,1,0:T(8,128)(2,1)S(1)}, u32[]{:S(2)}, u32[]{:S(2)}) collective-permute-start(bf16[1,20,8,128]{3,2,1,0:T(8,128)(2,1)S(1)} %add_convert_fusion.1), channel_id=1, source_target_pairs={{0,8},{2,10},{4,12},{6,14},{8,0},{10,2},{12,4},{14,6},{1,9},{3,11}... | collective-permute-start | bytes 122888 | tf_op jit(solution)/shard_map/ppermute | solution.py:76
  70.9 6.3 %collective-permute-start.13 = (f32[2,20,8,128]{3,2,1,0:T(8,128)S(1)}, f32[2,20,8,128]{3,2,1,0:T(8,128)S(1)}, u32[]{:S(2)}, u32[]{:S(2)}) collective-permute-start(f32[2,20,8,128]{3,2,1,0:T(8,128)S(1)} %dynamic-slice_bitcast_fusion.3), channel_id=1, source_target_pairs={{0,4},{2,6},{4,0},{6,2},{8,12},{10,14},{12,8},{14,10},{1,5},{3,7},... | collective-permute-start | bytes 491528 | tf_op jit(solution)/shard_map/ppermute | solution.py:65
  73.8 5.4 %collective-permute-start.6 = (bf16[2,20,8,128]{3,2,1,0:T(8,128)(2,1)S(1)}, bf16[2,20,8,128]{3,2,1,0:T(8,128)(2,1)S(1)}, u32[]{:S(2)}, u32[]{:S(2)}) collective-permute-start(bf16[2,20,8,128]{3,2,1,0:T(8,128)(2,1)S(1)} %maximum_select_fusion.7), channel_id=1, source_target_pairs={{0,4},{2,6},{4,0},{6,2},{8,12},{10,14},{12,8},{14,10},{1,5},{3,7},... | collective-permute-start | bytes 245768 | tf_op jit(solution)/shard_map/ppermute | solution.py:76
  77.2 5.4 %collective-permute-start.14 = (f32[1,20,8,128]{3,2,1,0:T(8,128)S(1)}, f32[1,20,8,128]{3,2,1,0:T(8,128)S(1)}, u32[]{:S(2)}, u32[]{:S(2)}) collective-permute-start(f32[1,20,8,128]{3,2,1,0:T(8,128)S(1)} %constant_dynamic-slice_fusion.2), channel_id=1, source_target_pairs={{0,8},{2,10},{4,12},{6,14},{8,0},{10,2},{12,4},{14,6},{1,9},{3,11}... | collective-permute-start | bytes 245768 | tf_op jit(solution)/shard_map/ppermute | solution.py:65
  79.8 12.5 %collective-permute-start.7 = (bf16[4,20,8,128]{3,2,1,0:T(8,128)(2,1)}, bf16[4,20,8,128]{3,2,1,0:T(8,128)(2,1)}, u32[]{:S(2)}, u32[]{:S(2)}) collective-permute-start(bf16[4,20,8,128]{3,2,1,0:T(8,128)(2,1)} %maximum_select_fusion.3), channel_id=1, source_target_pairs={{0,2},{2,0},{4,6},{6,4},{8,10},{10,8},{12,14},{14,12},{1,3},{3,1},... | collective-permute-start | bytes 491528 | tf_op jit(solution)/shard_map/ppermute | solution.py:76
  82.6 6.5 %collective-permute-start.15 = (bf16[1,20,8,128]{3,2,1,0:T(8,128)(2,1)S(1)}, bf16[1,20,8,128]{3,2,1,0:T(8,128)(2,1)S(1)}, u32[]{:S(2)}, u32[]{:S(2)}) collective-permute-start(bf16[1,20,8,128]{3,2,1,0:T(8,128)(2,1)S(1)} %add_convert_fusion), channel_id=1, source_target_pairs={{0,8},{2,10},{4,12},{6,14},{8,0},{10,2},{12,4},{14,6},{1,9},{3,11}... | collective-permute-start | bytes 122888 | tf_op jit(solution)/shard_map/ppermute | solution.py:76
  89.1 5.6 %collective-permute-start.16 = (bf16[2,20,8,128]{3,2,1,0:T(8,128)(2,1)S(1)}, bf16[2,20,8,128]{3,2,1,0:T(8,128)(2,1)S(1)}, u32[]{:S(2)}, u32[]{:S(2)}) collective-permute-start(bf16[2,20,8,128]{3,2,1,0:T(8,128)(2,1)S(1)} %maximum_select_fusion.8), channel_id=1, source_target_pairs={{0,4},{2,6},{4,0},{6,2},{8,12},{10,14},{12,8},{14,10},{1,5},{3,7},... | collective-permute-start | bytes 245768 | tf_op jit(solution)/shard_map/ppermute | solution.py:76
  94.8 5.4 %collective-permute-start.17 = (bf16[4,20,8,128]{3,2,1,0:T(8,128)(2,1)S(1)}, bf16[4,20,8,128]{3,2,1,0:T(8,128)(2,1)S(1)}, u32[]{:S(2)}, u32[]{:S(2)}) collective-permute-start(bf16[4,20,8,128]{3,2,1,0:T(8,128)(2,1)S(1)} %maximum_select_fusion.4), channel_id=1, source_target_pairs={{0,2},{2,0},{4,6},{6,4},{8,10},{10,8},{12,14},{14,12},{1,3},{3,1},... | collective-permute-start | bytes 491528 | tf_op jit(solution)/shard_map/ppermute | solution.py:76
  96.3 7.7 %collective-permute-start.8 = (bf16[20,64,128]{2,1,0:T(8,128)(2,1)}, bf16[20,64,128]{2,1,0:T(8,128)(2,1)}, u32[]{:S(2)}, u32[]{:S(2)}) collective-permute-start(bf16[20,64,128]{2,1,0:T(8,128)(2,1)} %copy_bitcast_fusion), channel_id=1, source_target_pairs={{0,1},{1,0},{2,3},{3,2},{4,5},{5,4},{6,7},{7,6},{8,9},{9,8},{10,11... | collective-permute-start | bytes 983048 | tf_op jit(solution)/shard_map/ppermute | solution.py:100
  100.2 1.0 copy-start.5
  101.3 2.7 %copy-start.17 = (f32[256,40]{0,1:T(8,128)S(1)}, f32[256,40]{0,1:T(8,128)}, u32[]{:S(2)}) copy-start(f32[256,40]{0,1:T(8,128)} %copy-done.16) | copy-start | bytes 122884
  104.0 3.4 %copy-start.13 = (f32[256,128]{0,1:T(8,128)S(1)}, f32[256,128]{0,1:T(8,128)}, u32[]{:S(2)}) copy-start(f32[256,128]{0,1:T(8,128)} %copy.148) | copy-start | bytes 393220
  104.0 7.2 %collective-permute-start.18 = (f32[2,256,256]{2,1,0:T(8,128)}, f32[2,256,256]{2,1,0:T(8,128)S(1)}, u32[]{:S(2)}, u32[]{:S(2)}) collective-permute-start(f32[2,256,256]{2,1,0:T(8,128)} %bitcast.64), channel_id=1, source_target_pairs={{0,1},{1,0},{2,3},{3,2},{4,5},{5,4},{6,7},{7,6},{8,9},{9,8},{10,11... | collective-permute-start | bytes 1572872 | tf_op jit(solution)/shard_map/ppermute | solution.py:100

commit v15 on v14

--- a/solution.py
+++ b/solution.py
@@ -114,7 +114,9 @@
     position = jnp.arange(cand_len, dtype=jnp.int32)
 
     def level_work(code_cand):
-        level_all = jnp.cumsum(jnp.log1p(-code_cand.astype(jnp.float32) * 1e-06), axis=1)
+        rates = jnp.log1p(-code_cand.astype(jnp.float32) * 1e-06)
+        lower = (position[:, None] >= position[None, :]).astype(jnp.float32)
+        level_all = jnp.einsum("ts,csh->cth", lower, rates, precision=lax.Precision.HIGHEST)
         return jnp.exp(level_all), jnp.exp(-level_all)
 
     def g_work(dy_cand, lengths, amplitude, c_cand):

time: 113 us -> 109 us (0.965)
  other arithmetic: 15.3 us -> 12.8 us
  local copies, waits for them, and re-layouts: 26.8 us -> 24.5 us
    another operation x4 -> x2, other arithmetic: 2.96 us -> 0.62 us
    optimization_barrier x4 -> x2, local copies, waits for them, and re-layouts: 8.96 us -> 7.39 us  [suffix_sum(): value, args = lax.optimization_barrier((value, pick(done)))]
    transpose x2 -> x0, local copies, waits for them, and re-layouts: 1.3 us -> none  [the longest x1 0.66 us: shards(): inv_t = jnp.transpose(inverse, (0, 2, 1))]
    dot_general x0 -> x1, matrix products: none -> 1.13 us  [level_work(): jnp.einsum('ts,csh->cth', lower, rates, precision=lax.Precision.HIGHEST)]
    unnamed x44 -> x42, local copies, waits for them, and re-layouts: 8.58 us -> 9.56 us
  transfers between devices with their start and end apart: 19 -> 19, of which waited for: 8 -> 8; matrix products, arithmetic and copies ran while one was open for 55% -> 53% of each run, Pallas kernels for 0% -> 0%
where the time goes in v15:
time: 109 us; the launch traced here: 108 us
  starting transfers between devices  26.1 us (24%)
  local copies, waits for them, and re-layouts  24.5 us (22%)
  matrix products  22.9 us (21%)
  waiting for transfers between devices  20.7 us (19%)
  other arithmetic  12.8 us (12%)
  between operations  1.29 us (1%)
    ppermute x6, waiting for transfers between devices, halving_scatter(): lax.ppermute(give, axis, [(at, at ^ step) for at in range(count)])  14 us
    ppermute x6, starting transfers between devices, halving_scatter(): lax.ppermute(give, axis, [(at, at ^ step) for at in range(count)])  13.8 us
    unnamed x42, local copies, waits for them, and re-layouts  9.56 us
    optimization_barrier x2, local copies, waits for them, and re-layouts, suffix_sum(): value, args = lax.optimization_barrier((value, pick(done)))  7.39 us
    ppermute x6, waiting for transfers between devices, doubling_gather(): other = lax.ppermute(value, axis, [(at, at ^ step) for at in range(count)])  6.69 us
    dot_general x1, matrix products, shards(): jnp.einsum('chts,cthp->cshp', kernel, g_heads, preferred_element_type=jnp...  6.54 us
    ppermute x6, starting transfers between devices, doubling_gather(): other = lax.ppermute(value, axis, [(at, at ^ step) for at in range(count)])  6.51 us
    convert_element_type x2, other arithmetic, split_bf16(): low = (value - high).astype(jnp.bfloat16)  5.78 us
  transfers between devices with their start and end apart: 19, of which 8 were waited for; matrix products, arithmetic and copies ran while one was open for 53% of the time, Pallas kernels for 0%

profile of v15, /device:TPU:0, one launch (start us, length us, event | category | flops | bytes accessed | tf_op | source)
XLA Modules:
  0.0 108.3 jit_solution(7155438205659498710)
XLA Ops:
  0.7 1.0 fusion.25
  1.6 1.3 %collective-permute-start = (f32[40]{0:T(128)S(1)}, f32[40]{0:T(128)S(1)}, u32[]{:S(2)}, u32[]{:S(2)}) collective-permute-start(f32[40]{0:T(128)S(1)} %get-tuple-element.29), channel_id=1, source_target_pairs={{1,0},{2,1},{3,2},{4,3},{5,4},{6,5},{7,6},{8,7},{9,8},{10,9},{11,1... | collective-permute-start | bytes 488 | tf_op jit(solution)/shard_map/ppermute | solution.py:35
  3.0 0.8 iota_compare_fusion
  3.8 0.6 reduce-window.6
  4.4 0.2 slice_reduce_fusion
  4.6 1.0 multiply_log-plus-one_fusion
  5.6 1.1 %exponential_bitcast_fusion = (f32[2,512,20]{1,2,0:T(8,128)}, f32[2,512,20]{1,2,0:T(8,128)S(1)}) fusion(f32[2,512,20]{1,0,2:T(2,128)S(1)} %multiply_log-plus-one_fusion), kind=kOutput, calls=%fused_computation.53 | convolution fusion | flops 126111744 | bytes 245760 | tf_op jit(solution)/shard_map/ts,csh->cth/dot_general | solution.py:119
  6.7 1.6 %copy.126 = f32[256,128]{0,1:T(8,128)} copy(bf16[256,128]{1,0:T(8,128)(2,1)} %param.10) | data formatting | bytes 196608 | tf_op jit(solution)/shard_map/convert_element_type | solution.py:152
  8.3 2.4 %copy.128 = bf16[256,2560]{0,1:T(8,128)(2,1)} copy(bf16[256,2560]{1,0:T(8,128)(2,1)} %param.9) | data formatting | bytes 2621440 | tf_op args[0]
  10.9 1.3 %collective-permute-start.1 = (f32[40]{0:T(128)S(1)}, f32[40]{0:T(128)S(1)}, u32[]{:S(2)}, u32[]{:S(2)}) collective-permute-start(f32[40]{0:T(128)S(1)} %add.120), channel_id=1, source_target_pairs={{2,0},{3,1},{4,2},{5,3},{6,4},{7,5},{8,6},{9,7},{10,8},{11,9},{12,... | collective-permute-start | bytes 488 | tf_op jit(solution)/shard_map/ppermute | solution.py:35
  12.2 3.0 %copy.118 = bf16[2,512,1280]{1,2,0:T(8,128)(2,1)S(1)} copy(bf16[2,512,1280]{2,1,0:T(8,128)(2,1)} %param.17) | data formatting | bytes 5242880 | tf_op jit(solution)/shard_map/optimization_barrier | solution.py:34
  15.2 0.2 broadcast_select_fusion
  15.4 2.8 %fusion.6 = (bf16[2,512,20,64]{1,3,2,0:T(8,128)(2,1)}, bf16[2,512,20,64]{1,3,2,0:T(8,128)(2,1)S(1)}) fusion(bf16[2,512,20,64]{1,3,2,0:T(8,128)(2,1)S(1)} %bitcast.140, f32[2,512,20]{1,2,0:T(8,128)S(1)} %get-tuple-element.36), kind=kLoop, calls=%fused_computation.11 | loop fusion | flops 7864320 | bytes 7946240 | tf_op jit(solution)/shard_map/convert_element_type | solution.py:11
  18.1 0.8 convolution_bitcast_fusion
  19.1 1.3 %collective-permute-start.9 = (f32[40]{0:T(128)S(1)}, f32[40]{0:T(128)S(1)}, u32[]{:S(2)}, u32[]{:S(2)}) collective-permute-start(f32[40]{0:T(128)S(1)} %add.121), channel_id=1, source_target_pairs={{4,0},{5,1},{6,2},{7,3},{8,4},{9,5},{10,6},{11,7},{12,8},{13,9},{1... | collective-permute-start | bytes 488 | tf_op jit(solution)/shard_map/ppermute | solution.py:35
  20.4 0.8 dynamic-slice_bitcast_fusion.2
  21.1 4.2 %collective-permute-start.2 = (f32[4,20,8,128]{3,2,1,0:T(8,128)}, f32[4,20,8,128]{3,2,1,0:T(8,128)}, u32[]{:S(2)}, u32[]{:S(2)}) collective-permute-start(f32[4,20,8,128]{3,2,1,0:T(8,128)} %dynamic-slice_bitcast_fusion.2), channel_id=1, source_target_pairs={{0,2},{2,0},{4,6},{6,4},{8,10},{10,8},{12,14},{14,12},{1,3},{3,1},... | collective-permute-start | bytes 983048 | tf_op jit(solution)/shard_map/ppermute | solution.py:65
  25.4 4.4 %copy.125 = bf16[2,512,1280]{1,2,0:T(8,128)(2,1)} copy(bf16[2,512,1280]{2,1,0:T(8,128)(2,1)} %param.12) | data formatting | bytes 5242880 | tf_op jit(solution)/shard_map/optimization_barrier | solution.py:34
  29.8 3.0 %fusion.7 = (bf16[2,512,20,64]{1,3,2,0:T(8,128)(2,1)S(1)}, bf16[2,512,20,64]{1,3,2,0:T(8,128)(2,1)S(1)}) fusion(bf16[2,512,20,64]{1,3,2,0:T(8,128)(2,1)} %bitcast.142, f32[2,512,20]{1,2,0:T(8,128)} %get-tuple-element.43), kind=kLoop, calls=%fused_computation.12 | loop fusion | flops 7864320 | bytes 7946240 | tf_op jit(solution)/shard_map/convert_element_type | solution.py:11
  32.8 0.4 fusion.34
  33.3 1.6 %collective-permute-start.10 = (f32[40]{0:T(128)S(1)}, f32[40]{0:T(128)S(1)}, u32[]{:S(2)}, u32[]{:S(2)}) collective-permute-start(f32[40]{0:T(128)S(1)} %add.131), channel_id=1, source_target_pairs={{8,0},{9,1},{10,2},{11,3},{12,4},{13,5},{14,6},{15,7},{24,16},{25,... | collective-permute-start | bytes 488 | tf_op jit(solution)/shard_map/ppermute | solution.py:35
  34.9 6.5 %fusion.15 = bf16[2,20,64,512]{3,2,1,0:T(8,128)(2,1)} fusion(bf16[2,512,20,64]{1,3,2,0:T(8,128)(2,1)S(1)} %bitcast.141, f32[2,20,512]{2,1,0:T(8,128)S(1)} %bitcast.168, f32[2,20,512]{2,1,0:T(8,128)S(1)} %bitcast.169, f32[2,512,512]{2,1,0:T(8,128)S(1)} %fusion.34, pred[512,512]{1,0:T(8,128)(4,1)S(1)} %copy-done.4), kind=kOutput, calls=%fused_computation.26 | convolution fusion | flops 1385431040 | bytes 7766016 | tf_op jit(solution)/shard_map/chts,cthp->cshp/dot_general | solution.py:195
  41.5 1.6 %fusion.35 = f32[2,512,512]{2,1,0:T(8,128)S(1)} fusion(bf16[2,512,1280]{1,2,0:T(8,128)(2,1)S(1)} %bitcast.137, bf16[2,512,1280]{1,2,0:T(8,128)(2,1)S(1)} %bitcast.144), kind=kOutput, calls=%fused_computation.82 | convolution fusion | flops 1342177280 | bytes 7340032 | tf_op jit(solution)/shard_map/ctk,csk->cts/dot_general | solution.py:177
  43.2 1.0 fusion.9
  44.3 0.3 collective-permute-start.11
  44.6 1.0 bitcast_add_fusion.3
  45.7 3.4 %collective-permute-start.3 = (f32[2,20,8,128]{3,2,1,0:T(8,128)S(1)}, f32[2,20,8,128]{3,2,1,0:T(8,128)S(1)}, u32[]{:S(2)}, u32[]{:S(2)}) collective-permute-start(f32[2,20,8,128]{3,2,1,0:T(8,128)S(1)} %dynamic-slice_bitcast_fusion.4), channel_id=1, source_target_pairs={{0,4},{2,6},{4,0},{6,2},{8,12},{10,14},{12,8},{14,10},{1,5},{3,7},... | collective-permute-start | bytes 491528 | tf_op jit(solution)/shard_map/ppermute | solution.py:65
  49.1 1.6 %fusion.36 = f32[2,512,512]{2,1,0:T(8,128)S(1)} fusion(bf16[2,512,1280]{1,2,0:T(8,128)(2,1)S(1)} %bitcast.138, bf16[2,512,1280]{1,2,0:T(8,128)(2,1)S(1)} %bitcast.148), kind=kOutput, calls=%fused_computation.83 | convolution fusion | flops 1342177280 | bytes 7340032 | tf_op jit(solution)/shard_map/ctk,csk->cts/dot_general | solution.py:177
  50.7 3.3 %collective-permute-done.3 = f32[2,20,8,128]{3,2,1,0:T(8,128)S(1)} collective-permute-done((f32[2,20,8,128]{3,2,1,0:T(8,128)S(1)}, f32[2,20,8,128]{3,2,1,0:T(8,128)S(1)}, u32[]{:S(2)}, u32[]{:S(2)}) %collective-permute-start.3) | collective-permute-done | bytes 163872 | tf_op jit(solution)/shard_map/ppermute | solution.py:65
  54.0 3.6 %collective-permute-start.4 = (f32[1,20,8,128]{3,2,1,0:T(8,128)S(1)}, f32[1,20,8,128]{3,2,1,0:T(8,128)S(1)}, u32[]{:S(2)}, u32[]{:S(2)}) collective-permute-start(f32[1,20,8,128]{3,2,1,0:T(8,128)S(1)} %constant_dynamic-slice_fusion.3), channel_id=1, source_target_pairs={{0,8},{2,10},{4,12},{6,14},{8,0},{10,2},{12,4},{14,6},{1,9},{3,11}... | collective-permute-start | bytes 245768 | tf_op jit(solution)/shard_map/ppermute | solution.py:65
  57.8 0.6 collective-permute-start.12
  58.4 1.8 %add_select_fusion = f32[2,512,512]{2,1,0:T(8,128)S(1)} fusion(f32[2,512,512]{2,1,0:T(8,128)S(1)} %fusion.35, f32[2,512,512]{2,1,0:T(8,128)S(1)} %fusion.36, bf16[2,512,1280]{1,2,0:T(8,128)(2,1)S(1)} %bitcast.143, bf16[2,512,1280]{1,2,0:T(8,128)(2,1)S(1)} %bitcast.145, pred[512,512]{1,0:T(8,128)(4,1)S(1)} %copy-done.4), kind=kOutput, calls=%fused_computation.25 | convolution fusion | flops 1343750144 | bytes 11796480 | tf_op jit(solution)/shard_map/ctk,csk->cts/dot_general | solution.py:177
  60.2 1.7 %collective-permute-done.4 = f32[1,20,8,128]{3,2,1,0:T(8,128)S(1)} collective-permute-done((f32[1,20,8,128]{3,2,1,0:T(8,128)S(1)}, f32[1,20,8,128]{3,2,1,0:T(8,128)S(1)}, u32[]{:S(2)}, u32[]{:S(2)}) %collective-permute-start.4) | collective-permute-done | bytes 81952 | tf_op jit(solution)/shard_map/ppermute | solution.py:65
  61.9 1.1 %collective-permute-start.5 = (bf16[1,20,8,128]{3,2,1,0:T(8,128)(2,1)S(1)}, bf16[1,20,8,128]{3,2,1,0:T(8,128)(2,1)S(1)}, u32[]{:S(2)}, u32[]{:S(2)}) collective-permute-start(bf16[1,20,8,128]{3,2,1,0:T(8,128)(2,1)S(1)} %add_convert_fusion.1), channel_id=1, source_target_pairs={{0,8},{2,10},{4,12},{6,14},{8,0},{10,2},{12,4},{14,6},{1,9},{3,11}... | collective-permute-start | bytes 122888 | tf_op jit(solution)/shard_map/ppermute | solution.py:76
  63.0 4.1 %collective-permute-done.12 = f32[4,20,8,128]{3,2,1,0:T(8,128)S(1)} collective-permute-done((f32[4,20,8,128]{3,2,1,0:T(8,128)S(1)}, f32[4,20,8,128]{3,2,1,0:T(8,128)S(1)}, u32[]{:S(2)}, u32[]{:S(2)}) %collective-permute-start.12) | collective-permute-done | bytes 327712 | tf_op jit(solution)/shard_map/ppermute | solution.py:65
  67.1 1.6 %collective-permute-start.13 = (f32[2,20,8,128]{3,2,1,0:T(8,128)S(1)}, f32[2,20,8,128]{3,2,1,0:T(8,128)S(1)}, u32[]{:S(2)}, u32[]{:S(2)}) collective-permute-start(f32[2,20,8,128]{3,2,1,0:T(8,128)S(1)} %dynamic-slice_bitcast_fusion.3), channel_id=1, source_target_pairs={{0,4},{2,6},{4,0},{6,2},{8,12},{10,14},{12,8},{14,10},{1,5},{3,7},... | collective-permute-start | bytes 491528 | tf_op jit(solution)/shard_map/ppermute | solution.py:65
  68.7 1.3 %fusion.38 = f32[2,512,128]{1,2,0:T(8,128)S(1)} fusion(f32[2,512,512]{2,1,0:T(8,128)S(1)} %add_select_fusion, bf16[2,512,128]{2,1,0:T(8,128)(2,1)S(1)} %copy-done.7), kind=kOutput, calls=%fused_computation.85 | convolution fusion | flops 805306368 | bytes 2883584 | tf_op jit(solution)/shard_map/cts,csn->ctn/dot_general | solution.py:187
  70.1 0.6 collective-permute-start.6
  70.6 2.8 %collective-permute-done.13 = f32[2,20,8,128]{3,2,1,0:T(8,128)S(1)} collective-permute-done((f32[2,20,8,128]{3,2,1,0:T(8,128)S(1)}, f32[2,20,8,128]{3,2,1,0:T(8,128)S(1)}, u32[]{:S(2)}, u32[]{:S(2)}) %collective-permute-start.13) | collective-permute-done | bytes 163872 | tf_op jit(solution)/shard_map/ppermute | solution.py:65
  73.4 0.4 collective-permute-start.14
  73.8 1.6 %collective-permute-done.6 = bf16[2,20,8,128]{3,2,1,0:T(8,128)(2,1)S(1)} collective-permute-done((bf16[2,20,8,128]{3,2,1,0:T(8,128)(2,1)S(1)}, bf16[2,20,8,128]{3,2,1,0:T(8,128)(2,1)S(1)}, u32[]{:S(2)}, u32[]{:S(2)}) %collective-permute-start.6) | collective-permute-done | bytes 81952 | tf_op jit(solution)/shard_map/ppermute | solution.py:76
  75.4 0.7 maximum_select_fusion.3
  76.1 0.6 collective-permute-start.7
  76.7 2.2 %collective-permute-done.14 = f32[1,20,8,128]{3,2,1,0:T(8,128)S(1)} collective-permute-done((f32[1,20,8,128]{3,2,1,0:T(8,128)S(1)}, f32[1,20,8,128]{3,2,1,0:T(8,128)S(1)}, u32[]{:S(2)}, u32[]{:S(2)}) %collective-permute-start.14) | collective-permute-done | bytes 81952 | tf_op jit(solution)/shard_map/ppermute | solution.py:65
  78.9 0.4 collective-permute-start.15
  79.3 1.7 %fusion.37 = f32[2,512,128]{1,2,0:T(8,128)} fusion(f32[2,512,512]{2,1,0:T(8,128)S(1)} %add_select_fusion, bf16[2,512,128]{2,1,0:T(8,128)(2,1)S(1)} %copy-done), kind=kOutput, calls=%fused_computation.84 | convolution fusion | flops 805306368 | bytes 2883584 | tf_op jit(solution)/shard_map/cts,ctn->csn/dot_general | solution.py:184
  81.0 4.4 %copy.148 = bf16[2,512,1280]{2,1,0:T(8,128)(2,1)} copy(bf16[2,512,1280]{1,2,0:T(8,128)(2,1)} %bitcast.147) | data formatting | bytes 5242880
  85.4 3.2 %collective-permute-start.16 = (bf16[2,20,8,128]{3,2,1,0:T(8,128)(2,1)S(1)}, bf16[2,20,8,128]{3,2,1,0:T(8,128)(2,1)S(1)}, u32[]{:S(2)}, u32[]{:S(2)}) collective-permute-start(bf16[2,20,8,128]{3,2,1,0:T(8,128)(2,1)S(1)} %maximum_select_fusion.8), channel_id=1, source_target_pairs={{0,4},{2,6},{4,0},{6,2},{8,12},{10,14},{12,8},{14,10},{1,5},{3,7},... | collective-permute-start | bytes 245768 | tf_op jit(solution)/shard_map/ppermute | solution.py:76
  88.6 1.2 %maximum_select_fusion.1 = bf16[8,20,8,128]{3,2,1,0:T(8,128)(2,1)S(1)} fusion(bf16[4,20,8,128]{3,2,1,0:T(8,128)(2,1)} %maximum_select_fusion.3, bf16[4,20,8,128]{3,2,1,0:T(8,128)(2,1)} %collective-permute-done.7, pred[]{:T(512)S(6)} %eq.29), kind=kLoop, calls=%fused_computation.38 | loop fusion | flops 491520 | bytes 655361 | tf_op jit(solution)/shard_map/jit(_where)/select_n | solution.py:78
  89.8 1.2 %collective-permute-done.16 = bf16[2,20,8,128]{3,2,1,0:T(8,128)(2,1)S(1)} collective-permute-done((bf16[2,20,8,128]{3,2,1,0:T(8,128)(2,1)S(1)}, bf16[2,20,8,128]{3,2,1,0:T(8,128)(2,1)S(1)}, u32[]{:S(2)}, u32[]{:S(2)}) %collective-permute-start.16) | collective-permute-done | bytes 81952 | tf_op jit(solution)/shard_map/ppermute | solution.py:76
  91.0 0.6 collective-permute-start.17
  91.7 0.8 copy_bitcast_fusion
  92.5 3.9 %collective-permute-done.17 = bf16[4,20,8,128]{3,2,1,0:T(8,128)(2,1)S(1)} collective-permute-done((bf16[4,20,8,128]{3,2,1,0:T(8,128)(2,1)S(1)}, bf16[4,20,8,128]{3,2,1,0:T(8,128)(2,1)S(1)}, u32[]{:S(2)}, u32[]{:S(2)}) %collective-permute-start.17) | collective-permute-done | bytes 163872 | tf_op jit(solution)/shard_map/ppermute | solution.py:76
  96.6 0.6 convolution_add_fusion
  97.2 0.3 copy-done.5
  97.6 0.7 reshape.182
  98.3 0.9 constant_dynamic-slice_fusion.1
  99.2 1.0 copy.145
  100.3 2.7 %fusion.8 = f32[256,128]{0,1:T(8,128)S(1)} fusion(f32[256,40]{0,1:T(8,128)S(1)} %copy-done.16, bf16[256,40,64]{0,2,1:T(8,128)(2,1)} %bitcast.158, bf16[20,64,128]{2,1,0:T(8,128)(2,1)} %collective-permute-done.8, bf16[20,64,128]{2,1,0:T(8,128)(2,1)} %copy_bitcast_fusion, pred[]{:T(512)S(6)} %eq.28), kind=kOutput, calls=%fused_computation.15 | convolution fusion | flops 171343872 | bytes 2138113 | tf_op jit(solution)/shard_map/jhp,hpn->jhn/dot_general | solution.py:217
  102.9 0.8 copy.147
  103.7 1.8 %fusion.16 = bf16[40,64,256]{2,1,0:T(8,128)(2,1)S(1)} fusion(f32[256,128]{0,1:T(8,128)S(1)} %copy-done.11, f32[256,40]{0,1:T(8,128)S(1)} %copy-done.16, bf16[20,64,128]{2,1,0:T(8,128)(2,1)} %collective-permute-done.8, bf16[20,64,128]{2,1,0:T(8,128)(2,1)} %copy_bitcast_fusion, pred[]{:T(512)S(6)} %eq.28), kind=kOutput, calls=%fused_computation.27 | convolution fusion | flops 172032000 | bytes 2138113 | tf_op jit(solution)/shard_map/jhn,hpn->jhp/dot_general | solution.py:213
  105.5 1.6 %copy.146 = bf16[256,2560]{1,0:T(8,128)(2,1)} copy(bf16[256,2560]{0,1:T(8,128)(2,1)S(1)} %bitcast.162) | data formatting | bytes 2621440
  107.1 0.3 copy.144
  107.5 0.8 fusion.29
  (84 shorter events, 1.1 us)
Async XLA Ops:
  0.6 17.5 %copy-start = (bf16[2,512,128]{2,1,0:T(8,128)(2,1)S(1)}, bf16[2,512,128]{2,1,0:T(8,128)(2,1)}, u32[]{:S(2)}) copy-start(bf16[2,512,128]{2,1,0:T(8,128)(2,1)} %param.14) | copy-start | bytes 786436
  0.6 10.1 %copy-start.18 = (s32[2]{0:T(128)S(1)}, s32[2]{0:T(128)}, u32[]{:S(2)}) copy-start(s32[2]{0:T(128)} %param.16) | copy-start | bytes 28
  1.6 9.2 %collective-permute-start = (f32[40]{0:T(128)S(1)}, f32[40]{0:T(128)S(1)}, u32[]{:S(2)}, u32[]{:S(2)}) collective-permute-start(f32[40]{0:T(128)S(1)} %get-tuple-element.29), channel_id=1, source_target_pairs={{1,0},{2,1},{3,2},{4,3},{5,4},{6,5},{7,6},{8,7},{9,8},{10,9},{11,1... | collective-permute-start | bytes 488 | tf_op jit(solution)/shard_map/ppermute | solution.py:35
  4.4 6.5 %copy-start.8 = (f32[40,2,128]{2,0,1:T(8,128)}, f32[40,2,128]{2,0,1:T(8,128)S(1)}, u32[]{:S(2)}) copy-start(f32[40,2,128]{2,0,1:T(8,128)S(1)} %reduce-window.6) | copy-start | bytes 122884
  4.6 10.6 %copy-start.17 = (f32[40,3]{0,1:T(4,128)}, f32[40,3]{0,1:T(4,128)S(1)}, u32[]{:S(2)}) copy-start(f32[40,3]{0,1:T(4,128)S(1)} %reduce-window.9) | copy-start | bytes 1444
  6.7 8.7 %copy-start.13 = (f32[2,512,20]{1,2,0:T(8,128)}, f32[2,512,20]{1,2,0:T(8,128)S(1)}, u32[]{:S(2)}) copy-start(f32[2,512,20]{1,2,0:T(8,128)S(1)} %get-tuple-element.36) | copy-start | bytes 245764
  10.9 8.1 %collective-permute-start.1 = (f32[40]{0:T(128)S(1)}, f32[40]{0:T(128)S(1)}, u32[]{:S(2)}, u32[]{:S(2)}) collective-permute-start(f32[40]{0:T(128)S(1)} %add.120), channel_id=1, source_target_pairs={{2,0},{3,1},{4,2},{5,3},{6,4},{7,5},{8,6},{9,7},{10,8},{11,9},{12,... | collective-permute-start | bytes 488 | tf_op jit(solution)/shard_map/ppermute | solution.py:35
  15.4 2.8 %copy-start.1 = (bf16[2,512,1280]{1,2,0:T(8,128)(2,1)}, bf16[2,512,1280]{1,2,0:T(8,128)(2,1)S(1)}, u32[]{:S(2)}) copy-start(bf16[2,512,1280]{1,2,0:T(8,128)(2,1)S(1)} %broadcast_select_fusion) | copy-start | bytes 7864324
  19.1 14.2 %collective-permute-start.9 = (f32[40]{0:T(128)S(1)}, f32[40]{0:T(128)S(1)}, u32[]{:S(2)}, u32[]{:S(2)}) collective-permute-start(f32[40]{0:T(128)S(1)} %add.121), channel_id=1, source_target_pairs={{4,0},{5,1},{6,2},{7,3},{8,4},{9,5},{10,6},{11,7},{12,8},{13,9},{1... | collective-permute-start | bytes 488 | tf_op jit(solution)/shard_map/ppermute | solution.py:35
  21.1 23.5 %collective-permute-start.2 = (f32[4,20,8,128]{3,2,1,0:T(8,128)}, f32[4,20,8,128]{3,2,1,0:T(8,128)}, u32[]{:S(2)}, u32[]{:S(2)}) collective-permute-start(f32[4,20,8,128]{3,2,1,0:T(8,128)} %dynamic-slice_bitcast_fusion.2), channel_id=1, source_target_pairs={{0,2},{2,0},{4,6},{6,4},{8,10},{10,8},{12,14},{14,12},{1,3},{3,1},... | collective-permute-start | bytes 983048 | tf_op jit(solution)/shard_map/ppermute | solution.py:65
  29.8 3.0 %copy-start.7 = (bf16[2,512,128]{2,1,0:T(8,128)(2,1)S(1)}, bf16[2,512,128]{2,1,0:T(8,128)(2,1)}, u32[]{:S(2)}) copy-start(bf16[2,512,128]{2,1,0:T(8,128)(2,1)} %param.13) | copy-start | bytes 786436
  29.8 5.1 %copy-start.4 = (pred[512,512]{1,0:T(8,128)(4,1)S(1)}, pred[512,512]{1,0:T(8,128)(4,1)}, u32[]{:S(2)}) copy-start(pred[512,512]{1,0:T(8,128)(4,1)} %iota_compare_fusion) | copy-start | bytes 786436
  29.8 5.1 %copy-start.12 = (f32[2,512,20]{1,2,0:T(8,128)S(1)}, f32[2,512,20]{1,2,0:T(8,128)}, u32[]{:S(2)}) copy-start(f32[2,512,20]{1,2,0:T(8,128)} %get-tuple-element.43) | copy-start | bytes 245764
  29.8 5.1 %copy-start.14 = (f32[2,512,20]{1,2,0:T(8,128)S(1)}, f32[2,512,20]{1,2,0:T(8,128)}, u32[]{:S(2)}) copy-start(f32[2,512,20]{1,2,0:T(8,128)} %copy-done.13) | copy-start | bytes 245764
  32.8 2.1 %copy-start.2 = (bf16[2,512,1280]{1,2,0:T(8,128)(2,1)S(1)}, bf16[2,512,1280]{1,2,0:T(8,128)(2,1)}, u32[]{:S(2)}) copy-start(bf16[2,512,1280]{1,2,0:T(8,128)(2,1)} %copy-done.1) | copy-start | bytes 7864324
  33.3 9.8 %collective-permute-start.10 = (f32[40]{0:T(128)S(1)}, f32[40]{0:T(128)S(1)}, u32[]{:S(2)}, u32[]{:S(2)}) collective-permute-start(f32[40]{0:T(128)S(1)} %add.131), channel_id=1, source_target_pairs={{8,0},{9,1},{10,2},{11,3},{12,4},{13,5},{14,6},{15,7},{24,16},{25,... | collective-permute-start | bytes 488 | tf_op jit(solution)/shard_map/ppermute | solution.py:35
  41.5 1.6 %copy-start.9 = (f32[40,2,128]{2,0,1:T(8,128)S(1)}, f32[40,2,128]{2,0,1:T(8,128)}, u32[]{:S(2)}) copy-start(f32[40,2,128]{2,0,1:T(8,128)} %copy-done.8) | copy-start | bytes 122884
  41.5 1.6 %slice-start = ((f32[40,3]{0,1:T(4,128)}), f32[40,2]{0,1:T(2,128)S(1)}, s32[]{:S(2)}) async-start(f32[40,3]{0,1:T(4,128)} %copy-done.17), calls=%async_computation | async-start | bytes 2048 | tf_op jit(solution)/shard_map/slice.1
  41.5 1.8 %copy-start.6 = (bf16[256,2560]{0,1:T(8,128)(2,1)S(1)}, bf16[256,2560]{0,1:T(8,128)(2,1)}, u32[]{:S(2)}) copy-start(bf16[256,2560]{0,1:T(8,128)(2,1)} %copy.128) | copy-start | bytes 3932164
  41.5 1.8 %copy-start.10 = (f32[256,128]{0,1:T(8,128)S(1)}, f32[256,128]{0,1:T(8,128)}, u32[]{:S(2)}) copy-start(f32[256,128]{0,1:T(8,128)} %copy.126) | copy-start | bytes 393220
  43.2 2.4 %copy-start.15 = (f32[256,40]{0,1:T(8,128)}, f32[256,40]{0,1:T(8,128)S(1)}, u32[]{:S(2)}) copy-start(f32[256,40]{0,1:T(8,128)S(1)} %fusion.23) | copy-start | bytes 122884
  44.3 13.2 %collective-permute-start.11 = (f32[20,64,128]{2,1,0:T(8,128)S(1)}, f32[20,64,128]{2,1,0:T(8,128)S(1)}, u32[]{:S(2)}, u32[]{:S(2)}) collective-permute-start(f32[20,64,128]{2,1,0:T(8,128)S(1)} %dynamic-slice_bitcast_fusion), channel_id=1, source_target_pairs={{0,1},{1,0},{2,3},{3,2},{4,5},{5,4},{6,7},{7,6},{8,9},{9,8},{10,11... | collective-permute-start | bytes 1966088 | tf_op jit(solution)/shard_map/ppermute | solution.py:100
  45.7 8.3 %collective-permute-start.3 = (f32[2,20,8,128]{3,2,1,0:T(8,128)S(1)}, f32[2,20,8,128]{3,2,1,0:T(8,128)S(1)}, u32[]{:S(2)}, u32[]{:S(2)}) collective-permute-start(f32[2,20,8,128]{3,2,1,0:T(8,128)S(1)} %dynamic-slice_bitcast_fusion.4), channel_id=1, source_target_pairs={{0,4},{2,6},{4,0},{6,2},{8,12},{10,14},{12,8},{14,10},{1,5},{3,7},... | collective-permute-start | bytes 491528 | tf_op jit(solution)/shard_map/ppermute | solution.py:65
  50.7 7.7 %copy-start.3 = (bf16[2,512,20,64]{1,3,2,0:T(8,128)(2,1)S(1)}, bf16[2,512,20,64]{1,3,2,0:T(8,128)(2,1)}, u32[]{:S(2)}) copy-start(bf16[2,512,20,64]{1,3,2,0:T(8,128)(2,1)} %get-tuple-element.52) | copy-start | bytes 7864324
  54.0 7.9 %collective-permute-start.4 = (f32[1,20,8,128]{3,2,1,0:T(8,128)S(1)}, f32[1,20,8,128]{3,2,1,0:T(8,128)S(1)}, u32[]{:S(2)}, u32[]{:S(2)}) collective-permute-start(f32[1,20,8,128]{3,2,1,0:T(8,128)S(1)} %constant_dynamic-slice_fusion.3), channel_id=1, source_target_pairs={{0,8},{2,10},{4,12},{6,14},{8,0},{10,2},{12,4},{14,6},{1,9},{3,11}... | collective-permute-start | bytes 245768 | tf_op jit(solution)/shard_map/ppermute | solution.py:65
  57.8 9.3 %collective-permute-start.12 = (f32[4,20,8,128]{3,2,1,0:T(8,128)S(1)}, f32[4,20,8,128]{3,2,1,0:T(8,128)S(1)}, u32[]{:S(2)}, u32[]{:S(2)}) collective-permute-start(f32[4,20,8,128]{3,2,1,0:T(8,128)S(1)} %dynamic-slice_bitcast_fusion.1), channel_id=1, source_target_pairs={{0,2},{2,0},{4,6},{6,4},{8,10},{10,8},{12,14},{14,12},{1,3},{3,1},... | collective-permute-start | bytes 983048 | tf_op jit(solution)/shard_map/ppermute | solution.py:65
  61.9 8.2 %collective-permute-start.5 = (bf16[1,20,8,128]{3,2,1,0:T(8,128)(2,1)S(1)}, bf16[1,20,8,128]{3,2,1,0:T(8,128)(2,1)S(1)}, u32[]{:S(2)}, u32[]{:S(2)}) collective-permute-start(bf16[1,20,8,128]{3,2,1,0:T(8,128)(2,1)S(1)} %add_convert_fusion.1), channel_id=1, source_target_pairs={{0,8},{2,10},{4,12},{6,14},{8,0},{10,2},{12,4},{14,6},{1,9},{3,11}... | collective-permute-start | bytes 122888 | tf_op jit(solution)/shard_map/ppermute | solution.py:76
  67.1 6.3 %collective-permute-start.13 = (f32[2,20,8,128]{3,2,1,0:T(8,128)S(1)}, f32[2,20,8,128]{3,2,1,0:T(8,128)S(1)}, u32[]{:S(2)}, u32[]{:S(2)}) collective-permute-start(f32[2,20,8,128]{3,2,1,0:T(8,128)S(1)} %dynamic-slice_bitcast_fusion.3), channel_id=1, source_target_pairs={{0,4},{2,6},{4,0},{6,2},{8,12},{10,14},{12,8},{14,10},{1,5},{3,7},... | collective-permute-start | bytes 491528 | tf_op jit(solution)/shard_map/ppermute | solution.py:65
  70.1 5.4 %collective-permute-start.6 = (bf16[2,20,8,128]{3,2,1,0:T(8,128)(2,1)S(1)}, bf16[2,20,8,128]{3,2,1,0:T(8,128)(2,1)S(1)}, u32[]{:S(2)}, u32[]{:S(2)}) collective-permute-start(bf16[2,20,8,128]{3,2,1,0:T(8,128)(2,1)S(1)} %maximum_select_fusion.7), channel_id=1, source_target_pairs={{0,4},{2,6},{4,0},{6,2},{8,12},{10,14},{12,8},{14,10},{1,5},{3,7},... | collective-permute-start | bytes 245768 | tf_op jit(solution)/shard_map/ppermute | solution.py:76
  73.4 5.4 %collective-permute-start.14 = (f32[1,20,8,128]{3,2,1,0:T(8,128)S(1)}, f32[1,20,8,128]{3,2,1,0:T(8,128)S(1)}, u32[]{:S(2)}, u32[]{:S(2)}) collective-permute-start(f32[1,20,8,128]{3,2,1,0:T(8,128)S(1)} %constant_dynamic-slice_fusion.2), channel_id=1, source_target_pairs={{0,8},{2,10},{4,12},{6,14},{8,0},{10,2},{12,4},{14,6},{1,9},{3,11}... | collective-permute-start | bytes 245768 | tf_op jit(solution)/shard_map/ppermute | solution.py:65
  76.1 12.5 %collective-permute-start.7 = (bf16[4,20,8,128]{3,2,1,0:T(8,128)(2,1)}, bf16[4,20,8,128]{3,2,1,0:T(8,128)(2,1)}, u32[]{:S(2)}, u32[]{:S(2)}) collective-permute-start(bf16[4,20,8,128]{3,2,1,0:T(8,128)(2,1)} %maximum_select_fusion.3), channel_id=1, source_target_pairs={{0,2},{2,0},{4,6},{6,4},{8,10},{10,8},{12,14},{14,12},{1,3},{3,1},... | collective-permute-start | bytes 491528 | tf_op jit(solution)/shard_map/ppermute | solution.py:76
  78.9 6.5 %collective-permute-start.15 = (bf16[1,20,8,128]{3,2,1,0:T(8,128)(2,1)S(1)}, bf16[1,20,8,128]{3,2,1,0:T(8,128)(2,1)S(1)}, u32[]{:S(2)}, u32[]{:S(2)}) collective-permute-start(bf16[1,20,8,128]{3,2,1,0:T(8,128)(2,1)S(1)} %add_convert_fusion), channel_id=1, source_target_pairs={{0,8},{2,10},{4,12},{6,14},{8,0},{10,2},{12,4},{14,6},{1,9},{3,11}... | collective-permute-start | bytes 122888 | tf_op jit(solution)/shard_map/ppermute | solution.py:76
  85.4 5.6 %collective-permute-start.16 = (bf16[2,20,8,128]{3,2,1,0:T(8,128)(2,1)S(1)}, bf16[2,20,8,128]{3,2,1,0:T(8,128)(2,1)S(1)}, u32[]{:S(2)}, u32[]{:S(2)}) collective-permute-start(bf16[2,20,8,128]{3,2,1,0:T(8,128)(2,1)S(1)} %maximum_select_fusion.8), channel_id=1, source_target_pairs={{0,4},{2,6},{4,0},{6,2},{8,12},{10,14},{12,8},{14,10},{1,5},{3,7},... | collective-permute-start | bytes 245768 | tf_op jit(solution)/shard_map/ppermute | solution.py:76
  91.0 5.4 %collective-permute-start.17 = (bf16[4,20,8,128]{3,2,1,0:T(8,128)(2,1)S(1)}, bf16[4,20,8,128]{3,2,1,0:T(8,128)(2,1)S(1)}, u32[]{:S(2)}, u32[]{:S(2)}) collective-permute-start(bf16[4,20,8,128]{3,2,1,0:T(8,128)(2,1)S(1)} %maximum_select_fusion.4), channel_id=1, source_target_pairs={{0,2},{2,0},{4,6},{6,4},{8,10},{10,8},{12,14},{14,12},{1,3},{3,1},... | collective-permute-start | bytes 491528 | tf_op jit(solution)/shard_map/ppermute | solution.py:76
  92.5 7.7 %collective-permute-start.8 = (bf16[20,64,128]{2,1,0:T(8,128)(2,1)}, bf16[20,64,128]{2,1,0:T(8,128)(2,1)}, u32[]{:S(2)}, u32[]{:S(2)}) collective-permute-start(bf16[20,64,128]{2,1,0:T(8,128)(2,1)} %copy_bitcast_fusion), channel_id=1, source_target_pairs={{0,1},{1,0},{2,3},{3,2},{4,5},{5,4},{6,7},{7,6},{8,9},{9,8},{10,11... | collective-permute-start | bytes 983048 | tf_op jit(solution)/shard_map/ppermute | solution.py:100
  96.5 1.0 copy-start.5
  97.6 2.7 %copy-start.16 = (f32[256,40]{0,1:T(8,128)S(1)}, f32[256,40]{0,1:T(8,128)}, u32[]{:S(2)}) copy-start(f32[256,40]{0,1:T(8,128)} %copy-done.15) | copy-start | bytes 122884
  100.2 3.4 %copy-start.11 = (f32[256,128]{0,1:T(8,128)S(1)}, f32[256,128]{0,1:T(8,128)}, u32[]{:S(2)}) copy-start(f32[256,128]{0,1:T(8,128)} %copy.126) | copy-start | bytes 393220
  100.2 7.2 %collective-permute-start.18 = (f32[2,256,256]{2,1,0:T(8,128)}, f32[2,256,256]{2,1,0:T(8,128)S(1)}, u32[]{:S(2)}, u32[]{:S(2)}) collective-permute-start(f32[2,256,256]{2,1,0:T(8,128)} %bitcast.64), channel_id=1, source_target_pairs={{0,1},{1,0},{2,3},{3,2},{4,5},{5,4},{6,7},{7,6},{8,9},{9,8},{10,11... | collective-permute-start | bytes 1572872 | tf_op jit(solution)/shard_map/ppermute | solution.py:100

commit v16 on v15

--- a/solution.py
+++ b/solution.py
@@ -147,7 +147,9 @@
     g_heads, decayed_g, g_low, dstate = g_parts
     x_high, x_low, scores = x_parts
     later_total = inclusive - own_total
-    after_local = own_total[None, :] - jnp.cumsum(log_prefix, axis=0)
+    token_at = jnp.arange(pre_len, dtype=jnp.int32)
+    later_rows = (token_at[None, :] > token_at[:, None]).astype(jnp.float32)
+    after_local = jnp.dot(later_rows, log_prefix, precision=lax.Precision.HIGHEST)
     weight = jnp.exp(after_local + later_total[None, :])
     weighted_b = (weight[:, :, None] * b_prefix[:, None, :].astype(jnp.float32)).astype(
         jnp.bfloat16

time: 109 us -> 108 us (level)
    unnamed x42 -> x38, local copies, waits for them, and re-layouts: 9.56 us -> 9.55 us
where the time goes in v16:
time: 108 us
  starting transfers between devices  26.1 us (24%)
  local copies, waits for them, and re-layouts  24.3 us (22%)
  matrix products  23.2 us (21%)
  waiting for transfers between devices  20.7 us (19%)
  other arithmetic  12.1 us (11%)
  between operations  1.26 us (1%)
    ppermute x6, waiting for transfers between devices, halving_scatter(): lax.ppermute(give, axis, [(at, at ^ step) for at in range(count)])  14 us
    ppermute x6, starting transfers between devices, halving_scatter(): lax.ppermute(give, axis, [(at, at ^ step) for at in range(count)])  13.8 us
    unnamed x38, local copies, waits for them, and re-layouts  9.55 us
    optimization_barrier x2, local copies, waits for them, and re-layouts, suffix_sum(): value, args = lax.optimization_barrier((value, pick(done)))  7.43 us
    ppermute x6, waiting for transfers between devices, doubling_gather(): other = lax.ppermute(value, axis, [(at, at ^ step) for at in range(count)])  6.71 us
    dot_general x1, matrix products, shards(): jnp.einsum('chts,cthp->cshp', kernel, g_heads, preferred_element_type=jnp...  6.55 us
    ppermute x6, starting transfers between devices, doubling_gather(): other = lax.ppermute(value, axis, [(at, at ^ step) for at in range(count)])  6.51 us
    convert_element_type x2, other arithmetic, split_bf16(): low = (value - high).astype(jnp.bfloat16)  5.78 us
  transfers between devices with their start and end apart: 19, of which 8 were waited for; matrix products, arithmetic and copies ran while one was open for 53% of the time, Pallas kernels for 0%

profile of v16, /device:TPU:0, one launch (start us, length us, event | category | flops | bytes accessed | tf_op | source)
XLA Modules:
  0.0 107.7 jit_solution(16791354557530626856)
XLA Ops:
  0.7 0.9 fusion.22
  1.6 1.3 %collective-permute-start = (f32[40]{0:T(128)S(1)}, f32[40]{0:T(128)S(1)}, u32[]{:S(2)}, u32[]{:S(2)}) collective-permute-start(f32[40]{0:T(128)S(1)} %fusion.22), channel_id=1, source_target_pairs={{1,0},{2,1},{3,2},{4,3},{5,4},{6,5},{7,6},{8,7},{9,8},{10,9},{11,1... | collective-permute-start | bytes 488 | tf_op jit(solution)/shard_map/ppermute | solution.py:35
  3.0 0.8 iota_compare_fusion
  3.8 1.0 multiply_log-plus-one_fusion
  4.8 1.1 %exponential_bitcast_fusion = (f32[2,512,20]{1,2,0:T(8,128)}, f32[2,512,20]{1,2,0:T(8,128)S(1)}) fusion(f32[2,512,20]{1,0,2:T(2,128)S(1)} %multiply_log-plus-one_fusion), kind=kOutput, calls=%fused_computation.55 | convolution fusion | flops 126111744 | bytes 245760 | tf_op jit(solution)/shard_map/ts,csh->cth/dot_general | solution.py:119
  5.9 1.6 %copy.117 = f32[256,128]{0,1:T(8,128)} copy(bf16[256,128]{1,0:T(8,128)(2,1)} %param.10) | data formatting | bytes 196608 | tf_op jit(solution)/shard_map/convert_element_type | solution.py:154
  7.5 2.4 %copy.119 = bf16[256,2560]{0,1:T(8,128)(2,1)} copy(bf16[256,2560]{1,0:T(8,128)(2,1)} %param.9) | data formatting | bytes 2621440 | tf_op args[0]
  10.1 1.3 %collective-permute-start.1 = (f32[40]{0:T(128)S(1)}, f32[40]{0:T(128)S(1)}, u32[]{:S(2)}, u32[]{:S(2)}) collective-permute-start(f32[40]{0:T(128)S(1)} %add.119), channel_id=1, source_target_pairs={{2,0},{3,1},{4,2},{5,3},{6,4},{7,5},{8,6},{9,7},{10,8},{11,9},{12,... | collective-permute-start | bytes 488 | tf_op jit(solution)/shard_map/ppermute | solution.py:35
  11.3 3.0 %copy.111 = bf16[2,512,1280]{1,2,0:T(8,128)(2,1)S(1)} copy(bf16[2,512,1280]{2,1,0:T(8,128)(2,1)} %param.17) | data formatting | bytes 5242880 | tf_op jit(solution)/shard_map/optimization_barrier | solution.py:34
  14.4 0.2 broadcast_select_fusion
  14.6 2.8 %fusion.6 = (bf16[2,512,20,64]{1,3,2,0:T(8,128)(2,1)}, bf16[2,512,20,64]{1,3,2,0:T(8,128)(2,1)S(1)}) fusion(bf16[2,512,20,64]{1,3,2,0:T(8,128)(2,1)S(1)} %bitcast.121, f32[2,512,20]{1,2,0:T(8,128)S(1)} %get-tuple-element.36), kind=kLoop, calls=%fused_computation.11 | loop fusion | flops 7864320 | bytes 7946240 | tf_op jit(solution)/shard_map/convert_element_type | solution.py:11
  17.3 0.8 convolution_bitcast_fusion
  18.3 1.3 %collective-permute-start.9 = (f32[40]{0:T(128)S(1)}, f32[40]{0:T(128)S(1)}, u32[]{:S(2)}, u32[]{:S(2)}) collective-permute-start(f32[40]{0:T(128)S(1)} %add.120), channel_id=1, source_target_pairs={{4,0},{5,1},{6,2},{7,3},{8,4},{9,5},{10,6},{11,7},{12,8},{13,9},{1... | collective-permute-start | bytes 488 | tf_op jit(solution)/shard_map/ppermute | solution.py:35
  19.6 0.8 dynamic-slice_bitcast_fusion.2
  20.3 4.2 %collective-permute-start.2 = (f32[4,20,8,128]{3,2,1,0:T(8,128)}, f32[4,20,8,128]{3,2,1,0:T(8,128)}, u32[]{:S(2)}, u32[]{:S(2)}) collective-permute-start(f32[4,20,8,128]{3,2,1,0:T(8,128)} %dynamic-slice_bitcast_fusion.2), channel_id=1, source_target_pairs={{0,2},{2,0},{4,6},{6,4},{8,10},{10,8},{12,14},{14,12},{1,3},{3,1},... | collective-permute-start | bytes 983048 | tf_op jit(solution)/shard_map/ppermute | solution.py:65
  24.5 4.4 %copy.116 = bf16[2,512,1280]{1,2,0:T(8,128)(2,1)} copy(bf16[2,512,1280]{2,1,0:T(8,128)(2,1)} %param.12) | data formatting | bytes 5242880 | tf_op jit(solution)/shard_map/optimization_barrier | solution.py:34
  29.0 3.0 %fusion.7 = (bf16[2,512,20,64]{1,3,2,0:T(8,128)(2,1)S(1)}, bf16[2,512,20,64]{1,3,2,0:T(8,128)(2,1)S(1)}) fusion(bf16[2,512,20,64]{1,3,2,0:T(8,128)(2,1)} %bitcast.123, f32[2,512,20]{1,2,0:T(8,128)} %get-tuple-element.43), kind=kLoop, calls=%fused_computation.12 | loop fusion | flops 7864320 | bytes 7946240 | tf_op jit(solution)/shard_map/convert_element_type | solution.py:11
  32.0 0.4 fusion.33
  32.5 1.6 %collective-permute-start.10 = (f32[40]{0:T(128)S(1)}, f32[40]{0:T(128)S(1)}, u32[]{:S(2)}, u32[]{:S(2)}) collective-permute-start(f32[40]{0:T(128)S(1)} %add.130), channel_id=1, source_target_pairs={{8,0},{9,1},{10,2},{11,3},{12,4},{13,5},{14,6},{15,7},{24,16},{25,... | collective-permute-start | bytes 488 | tf_op jit(solution)/shard_map/ppermute | solution.py:35
  34.1 6.6 %fusion.15 = bf16[2,20,64,512]{3,2,1,0:T(8,128)(2,1)} fusion(bf16[2,512,20,64]{1,3,2,0:T(8,128)(2,1)S(1)} %bitcast.122, f32[2,20,512]{2,1,0:T(8,128)S(1)} %bitcast.148, f32[2,20,512]{2,1,0:T(8,128)S(1)} %bitcast.149, f32[2,512,512]{2,1,0:T(8,128)S(1)} %fusion.33, pred[512,512]{1,0:T(8,128)(4,1)S(1)} %copy-done.4), kind=kOutput, calls=%fused_computation.26 | convolution fusion | flops 1385431040 | bytes 7766016 | tf_op jit(solution)/shard_map/chts,cthp->cshp/dot_general | solution.py:197
  40.7 1.6 %fusion.34 = f32[2,512,512]{2,1,0:T(8,128)S(1)} fusion(bf16[2,512,1280]{1,2,0:T(8,128)(2,1)S(1)} %bitcast.118, bf16[2,512,1280]{1,2,0:T(8,128)(2,1)S(1)} %bitcast.125), kind=kOutput, calls=%fused_computation.79 | convolution fusion | flops 1342177280 | bytes 7340032 | tf_op jit(solution)/shard_map/ctk,csk->cts/dot_general | solution.py:179
  42.3 0.3 add_exponential_fusion
  42.6 1.0 fusion.9
  43.7 0.3 collective-permute-start.11
  44.0 1.0 bitcast_add_fusion.3
  45.1 3.4 %collective-permute-start.3 = (f32[2,20,8,128]{3,2,1,0:T(8,128)S(1)}, f32[2,20,8,128]{3,2,1,0:T(8,128)S(1)}, u32[]{:S(2)}, u32[]{:S(2)}) collective-permute-start(f32[2,20,8,128]{3,2,1,0:T(8,128)S(1)} %dynamic-slice_bitcast_fusion.4), channel_id=1, source_target_pairs={{0,4},{2,6},{4,0},{6,2},{8,12},{10,14},{12,8},{14,10},{1,5},{3,7},... | collective-permute-start | bytes 491528 | tf_op jit(solution)/shard_map/ppermute | solution.py:65
  48.5 1.6 %fusion.35 = f32[2,512,512]{2,1,0:T(8,128)S(1)} fusion(bf16[2,512,1280]{1,2,0:T(8,128)(2,1)S(1)} %bitcast.119, bf16[2,512,1280]{1,2,0:T(8,128)(2,1)S(1)} %bitcast.129), kind=kOutput, calls=%fused_computation.80 | convolution fusion | flops 1342177280 | bytes 7340032 | tf_op jit(solution)/shard_map/ctk,csk->cts/dot_general | solution.py:179
  50.1 3.3 %collective-permute-done.3 = f32[2,20,8,128]{3,2,1,0:T(8,128)S(1)} collective-permute-done((f32[2,20,8,128]{3,2,1,0:T(8,128)S(1)}, f32[2,20,8,128]{3,2,1,0:T(8,128)S(1)}, u32[]{:S(2)}, u32[]{:S(2)}) %collective-permute-start.3) | collective-permute-done | bytes 163872 | tf_op jit(solution)/shard_map/ppermute | solution.py:65
  53.4 3.6 %collective-permute-start.4 = (f32[1,20,8,128]{3,2,1,0:T(8,128)S(1)}, f32[1,20,8,128]{3,2,1,0:T(8,128)S(1)}, u32[]{:S(2)}, u32[]{:S(2)}) collective-permute-start(f32[1,20,8,128]{3,2,1,0:T(8,128)S(1)} %constant_dynamic-slice_fusion.3), channel_id=1, source_target_pairs={{0,8},{2,10},{4,12},{6,14},{8,0},{10,2},{12,4},{14,6},{1,9},{3,11}... | collective-permute-start | bytes 245768 | tf_op jit(solution)/shard_map/ppermute | solution.py:65
  57.0 0.1 bitcast_add_fusion
  57.1 0.6 collective-permute-start.12
  57.8 1.8 %add_select_fusion = f32[2,512,512]{2,1,0:T(8,128)S(1)} fusion(f32[2,512,512]{2,1,0:T(8,128)S(1)} %fusion.34, f32[2,512,512]{2,1,0:T(8,128)S(1)} %fusion.35, bf16[2,512,1280]{1,2,0:T(8,128)(2,1)S(1)} %bitcast.124, bf16[2,512,1280]{1,2,0:T(8,128)(2,1)S(1)} %bitcast.126, pred[512,512]{1,0:T(8,128)(4,1)S(1)} %copy-done.4), kind=kOutput, calls=%fused_computation.25 | convolution fusion | flops 1343750144 | bytes 11796480 | tf_op jit(solution)/shard_map/ctk,csk->cts/dot_general | solution.py:179
  59.6 1.7 %collective-permute-done.4 = f32[1,20,8,128]{3,2,1,0:T(8,128)S(1)} collective-permute-done((f32[1,20,8,128]{3,2,1,0:T(8,128)S(1)}, f32[1,20,8,128]{3,2,1,0:T(8,128)S(1)}, u32[]{:S(2)}, u32[]{:S(2)}) %collective-permute-start.4) | collective-permute-done | bytes 81952 | tf_op jit(solution)/shard_map/ppermute | solution.py:65
  61.3 1.1 %collective-permute-start.5 = (bf16[1,20,8,128]{3,2,1,0:T(8,128)(2,1)S(1)}, bf16[1,20,8,128]{3,2,1,0:T(8,128)(2,1)S(1)}, u32[]{:S(2)}, u32[]{:S(2)}) collective-permute-start(bf16[1,20,8,128]{3,2,1,0:T(8,128)(2,1)S(1)} %add_convert_fusion.1), channel_id=1, source_target_pairs={{0,8},{2,10},{4,12},{6,14},{8,0},{10,2},{12,4},{14,6},{1,9},{3,11}... | collective-permute-start | bytes 122888 | tf_op jit(solution)/shard_map/ppermute | solution.py:76
  62.4 4.1 %collective-permute-done.12 = f32[4,20,8,128]{3,2,1,0:T(8,128)S(1)} collective-permute-done((f32[4,20,8,128]{3,2,1,0:T(8,128)S(1)}, f32[4,20,8,128]{3,2,1,0:T(8,128)S(1)}, u32[]{:S(2)}, u32[]{:S(2)}) %collective-permute-start.12) | collective-permute-done | bytes 327712 | tf_op jit(solution)/shard_map/ppermute | solution.py:65
  66.5 1.6 %collective-permute-start.13 = (f32[2,20,8,128]{3,2,1,0:T(8,128)S(1)}, f32[2,20,8,128]{3,2,1,0:T(8,128)S(1)}, u32[]{:S(2)}, u32[]{:S(2)}) collective-permute-start(f32[2,20,8,128]{3,2,1,0:T(8,128)S(1)} %dynamic-slice_bitcast_fusion.3), channel_id=1, source_target_pairs={{0,4},{2,6},{4,0},{6,2},{8,12},{10,14},{12,8},{14,10},{1,5},{3,7},... | collective-permute-start | bytes 491528 | tf_op jit(solution)/shard_map/ppermute | solution.py:65
  68.1 1.3 %fusion.37 = f32[2,512,128]{1,2,0:T(8,128)S(1)} fusion(f32[2,512,512]{2,1,0:T(8,128)S(1)} %add_select_fusion, bf16[2,512,128]{2,1,0:T(8,128)(2,1)S(1)} %copy-done.7), kind=kOutput, calls=%fused_computation.82 | convolution fusion | flops 805306368 | bytes 2883584 | tf_op jit(solution)/shard_map/cts,csn->ctn/dot_general | solution.py:189
  69.5 0.6 collective-permute-start.6
  70.0 2.8 %collective-permute-done.13 = f32[2,20,8,128]{3,2,1,0:T(8,128)S(1)} collective-permute-done((f32[2,20,8,128]{3,2,1,0:T(8,128)S(1)}, f32[2,20,8,128]{3,2,1,0:T(8,128)S(1)}, u32[]{:S(2)}, u32[]{:S(2)}) %collective-permute-start.13) | collective-permute-done | bytes 163872 | tf_op jit(solution)/shard_map/ppermute | solution.py:65
  72.8 0.4 collective-permute-start.14
  73.2 1.6 %collective-permute-done.6 = bf16[2,20,8,128]{3,2,1,0:T(8,128)(2,1)S(1)} collective-permute-done((bf16[2,20,8,128]{3,2,1,0:T(8,128)(2,1)S(1)}, bf16[2,20,8,128]{3,2,1,0:T(8,128)(2,1)S(1)}, u32[]{:S(2)}, u32[]{:S(2)}) %collective-permute-start.6) | collective-permute-done | bytes 81952 | tf_op jit(solution)/shard_map/ppermute | solution.py:76
  74.8 0.7 maximum_select_fusion.3
  75.5 0.6 collective-permute-start.7
  76.1 2.2 %collective-permute-done.14 = f32[1,20,8,128]{3,2,1,0:T(8,128)S(1)} collective-permute-done((f32[1,20,8,128]{3,2,1,0:T(8,128)S(1)}, f32[1,20,8,128]{3,2,1,0:T(8,128)S(1)}, u32[]{:S(2)}, u32[]{:S(2)}) %collective-permute-start.14) | collective-permute-done | bytes 81952 | tf_op jit(solution)/shard_map/ppermute | solution.py:65
  78.3 0.4 collective-permute-start.15
  78.7 1.7 %fusion.36 = f32[2,512,128]{1,2,0:T(8,128)} fusion(f32[2,512,512]{2,1,0:T(8,128)S(1)} %add_select_fusion, bf16[2,512,128]{2,1,0:T(8,128)(2,1)S(1)} %copy-done), kind=kOutput, calls=%fused_computation.81 | convolution fusion | flops 805306368 | bytes 2883584 | tf_op jit(solution)/shard_map/cts,ctn->csn/dot_general | solution.py:186
  80.4 4.4 %copy.139 = bf16[2,512,1280]{2,1,0:T(8,128)(2,1)} copy(bf16[2,512,1280]{1,2,0:T(8,128)(2,1)} %bitcast.128) | data formatting | bytes 5242880
  84.8 3.2 %collective-permute-start.16 = (bf16[2,20,8,128]{3,2,1,0:T(8,128)(2,1)S(1)}, bf16[2,20,8,128]{3,2,1,0:T(8,128)(2,1)S(1)}, u32[]{:S(2)}, u32[]{:S(2)}) collective-permute-start(bf16[2,20,8,128]{3,2,1,0:T(8,128)(2,1)S(1)} %maximum_select_fusion.8), channel_id=1, source_target_pairs={{0,4},{2,6},{4,0},{6,2},{8,12},{10,14},{12,8},{14,10},{1,5},{3,7},... | collective-permute-start | bytes 245768 | tf_op jit(solution)/shard_map/ppermute | solution.py:76
  88.0 1.2 %maximum_select_fusion.1 = bf16[8,20,8,128]{3,2,1,0:T(8,128)(2,1)S(1)} fusion(bf16[4,20,8,128]{3,2,1,0:T(8,128)(2,1)} %maximum_select_fusion.3, bf16[4,20,8,128]{3,2,1,0:T(8,128)(2,1)} %collective-permute-done.7, pred[]{:T(512)S(6)} %eq.29), kind=kLoop, calls=%fused_computation.38 | loop fusion | flops 491520 | bytes 655361 | tf_op jit(solution)/shard_map/jit(_where)/select_n | solution.py:78
  89.2 1.2 %collective-permute-done.16 = bf16[2,20,8,128]{3,2,1,0:T(8,128)(2,1)S(1)} collective-permute-done((bf16[2,20,8,128]{3,2,1,0:T(8,128)(2,1)S(1)}, bf16[2,20,8,128]{3,2,1,0:T(8,128)(2,1)S(1)}, u32[]{:S(2)}, u32[]{:S(2)}) %collective-permute-start.16) | collective-permute-done | bytes 81952 | tf_op jit(solution)/shard_map/ppermute | solution.py:76
  90.4 0.6 collective-permute-start.17
  91.1 0.8 copy_bitcast_fusion
  91.9 3.9 %collective-permute-done.17 = bf16[4,20,8,128]{3,2,1,0:T(8,128)(2,1)S(1)} collective-permute-done((bf16[4,20,8,128]{3,2,1,0:T(8,128)(2,1)S(1)}, bf16[4,20,8,128]{3,2,1,0:T(8,128)(2,1)S(1)}, u32[]{:S(2)}, u32[]{:S(2)}) %collective-permute-start.17) | collective-permute-done | bytes 163872 | tf_op jit(solution)/shard_map/ppermute | solution.py:76
  96.0 0.6 convolution_add_fusion
  96.6 0.3 copy-done.5
  97.0 0.7 reshape.169
  97.7 0.9 constant_dynamic-slice_fusion.1
  98.6 1.0 copy.136
  99.6 2.7 %fusion.8 = f32[256,128]{0,1:T(8,128)S(1)} fusion(f32[256,40]{0,1:T(8,128)S(1)} %copy-done.16, bf16[256,40,64]{0,2,1:T(8,128)(2,1)} %bitcast.139, bf16[20,64,128]{2,1,0:T(8,128)(2,1)} %collective-permute-done.8, bf16[20,64,128]{2,1,0:T(8,128)(2,1)} %copy_bitcast_fusion, pred[]{:T(512)S(6)} %eq.28), kind=kOutput, calls=%fused_computation.15 | convolution fusion | flops 171343872 | bytes 2138113 | tf_op jit(solution)/shard_map/jhp,hpn->jhn/dot_general | solution.py:219
  102.3 0.8 copy.138
  103.1 1.8 %fusion.16 = bf16[40,64,256]{2,1,0:T(8,128)(2,1)S(1)} fusion(f32[256,128]{0,1:T(8,128)S(1)} %copy-done.9, f32[256,40]{0,1:T(8,128)S(1)} %copy-done.16, bf16[20,64,128]{2,1,0:T(8,128)(2,1)} %collective-permute-done.8, bf16[20,64,128]{2,1,0:T(8,128)(2,1)} %copy_bitcast_fusion, pred[]{:T(512)S(6)} %eq.28), kind=kOutput, calls=%fused_computation.27 | convolution fusion | flops 172032000 | bytes 2138113 | tf_op jit(solution)/shard_map/jhn,hpn->jhp/dot_general | solution.py:215
  104.9 1.6 %copy.137 = bf16[256,2560]{1,0:T(8,128)(2,1)} copy(bf16[256,2560]{0,1:T(8,128)(2,1)S(1)} %bitcast.143) | data formatting | bytes 2621440
  106.4 0.3 copy.135
  106.9 0.8 fusion.28
  (74 shorter events, 0.9 us)
Async XLA Ops:
  0.6 16.7 %copy-start = (bf16[2,512,128]{2,1,0:T(8,128)(2,1)S(1)}, bf16[2,512,128]{2,1,0:T(8,128)(2,1)}, u32[]{:S(2)}) copy-start(bf16[2,512,128]{2,1,0:T(8,128)(2,1)} %param.14) | copy-start | bytes 786436
  0.6 9.3 %copy-start.14 = (s32[2]{0:T(128)S(1)}, s32[2]{0:T(128)}, u32[]{:S(2)}) copy-start(s32[2]{0:T(128)} %param.16) | copy-start | bytes 28
  1.6 8.4 %collective-permute-start = (f32[40]{0:T(128)S(1)}, f32[40]{0:T(128)S(1)}, u32[]{:S(2)}, u32[]{:S(2)}) collective-permute-start(f32[40]{0:T(128)S(1)} %fusion.22), channel_id=1, source_target_pairs={{1,0},{2,1},{3,2},{4,3},{5,4},{6,5},{7,6},{8,7},{9,8},{10,9},{11,1... | collective-permute-start | bytes 488 | tf_op jit(solution)/shard_map/ppermute | solution.py:35
  5.9 8.6 %copy-start.11 = (f32[2,512,20]{1,2,0:T(8,128)}, f32[2,512,20]{1,2,0:T(8,128)S(1)}, u32[]{:S(2)}) copy-start(f32[2,512,20]{1,2,0:T(8,128)S(1)} %get-tuple-element.36) | copy-start | bytes 245764
  10.1 8.1 %collective-permute-start.1 = (f32[40]{0:T(128)S(1)}, f32[40]{0:T(128)S(1)}, u32[]{:S(2)}, u32[]{:S(2)}) collective-permute-start(f32[40]{0:T(128)S(1)} %add.119), channel_id=1, source_target_pairs={{2,0},{3,1},{4,2},{5,3},{6,4},{7,5},{8,6},{9,7},{10,8},{11,9},{12,... | collective-permute-start | bytes 488 | tf_op jit(solution)/shard_map/ppermute | solution.py:35
  14.5 2.8 %copy-start.1 = (bf16[2,512,1280]{1,2,0:T(8,128)(2,1)}, bf16[2,512,1280]{1,2,0:T(8,128)(2,1)S(1)}, u32[]{:S(2)}) copy-start(bf16[2,512,1280]{1,2,0:T(8,128)(2,1)S(1)} %broadcast_select_fusion) | copy-start | bytes 7864324
  18.3 14.2 %collective-permute-start.9 = (f32[40]{0:T(128)S(1)}, f32[40]{0:T(128)S(1)}, u32[]{:S(2)}, u32[]{:S(2)}) collective-permute-start(f32[40]{0:T(128)S(1)} %add.120), channel_id=1, source_target_pairs={{4,0},{5,1},{6,2},{7,3},{8,4},{9,5},{10,6},{11,7},{12,8},{13,9},{1... | collective-permute-start | bytes 488 | tf_op jit(solution)/shard_map/ppermute | solution.py:35
  20.3 23.7 %collective-permute-start.2 = (f32[4,20,8,128]{3,2,1,0:T(8,128)}, f32[4,20,8,128]{3,2,1,0:T(8,128)}, u32[]{:S(2)}, u32[]{:S(2)}) collective-permute-start(f32[4,20,8,128]{3,2,1,0:T(8,128)} %dynamic-slice_bitcast_fusion.2), channel_id=1, source_target_pairs={{0,2},{2,0},{4,6},{6,4},{8,10},{10,8},{12,14},{14,12},{1,3},{3,1},... | collective-permute-start | bytes 983048 | tf_op jit(solution)/shard_map/ppermute | solution.py:65
  29.0 3.0 %copy-start.7 = (bf16[2,512,128]{2,1,0:T(8,128)(2,1)S(1)}, bf16[2,512,128]{2,1,0:T(8,128)(2,1)}, u32[]{:S(2)}) copy-start(bf16[2,512,128]{2,1,0:T(8,128)(2,1)} %param.13) | copy-start | bytes 786436
  29.0 5.1 %copy-start.4 = (pred[512,512]{1,0:T(8,128)(4,1)S(1)}, pred[512,512]{1,0:T(8,128)(4,1)}, u32[]{:S(2)}) copy-start(pred[512,512]{1,0:T(8,128)(4,1)} %iota_compare_fusion) | copy-start | bytes 786436
  29.0 5.1 %copy-start.10 = (f32[2,512,20]{1,2,0:T(8,128)S(1)}, f32[2,512,20]{1,2,0:T(8,128)}, u32[]{:S(2)}) copy-start(f32[2,512,20]{1,2,0:T(8,128)} %get-tuple-element.43) | copy-start | bytes 245764
  29.0 5.1 %copy-start.12 = (f32[2,512,20]{1,2,0:T(8,128)S(1)}, f32[2,512,20]{1,2,0:T(8,128)}, u32[]{:S(2)}) copy-start(f32[2,512,20]{1,2,0:T(8,128)} %copy-done.11) | copy-start | bytes 245764
  32.0 2.1 %copy-start.2 = (bf16[2,512,1280]{1,2,0:T(8,128)(2,1)S(1)}, bf16[2,512,1280]{1,2,0:T(8,128)(2,1)}, u32[]{:S(2)}) copy-start(bf16[2,512,1280]{1,2,0:T(8,128)(2,1)} %copy-done.1) | copy-start | bytes 7864324
  32.5 9.8 %collective-permute-start.10 = (f32[40]{0:T(128)S(1)}, f32[40]{0:T(128)S(1)}, u32[]{:S(2)}, u32[]{:S(2)}) collective-permute-start(f32[40]{0:T(128)S(1)} %add.130), channel_id=1, source_target_pairs={{8,0},{9,1},{10,2},{11,3},{12,4},{13,5},{14,6},{15,7},{24,16},{25,... | collective-permute-start | bytes 488 | tf_op jit(solution)/shard_map/ppermute | solution.py:35
  40.7 1.6 %copy-start.13 = (s32[256,40]{0,1:T(8,128)S(1)}, s32[256,40]{0,1:T(8,128)}, u32[]{:S(2)}) copy-start(s32[256,40]{0,1:T(8,128)} %param.11) | copy-start | bytes 122884
  40.7 1.9 %copy-start.6 = (bf16[256,2560]{0,1:T(8,128)(2,1)S(1)}, bf16[256,2560]{0,1:T(8,128)(2,1)}, u32[]{:S(2)}) copy-start(bf16[256,2560]{0,1:T(8,128)(2,1)} %copy.119) | copy-start | bytes 3932164
  40.7 1.9 %copy-start.8 = (f32[256,128]{0,1:T(8,128)S(1)}, f32[256,128]{0,1:T(8,128)}, u32[]{:S(2)}) copy-start(f32[256,128]{0,1:T(8,128)} %copy.117) | copy-start | bytes 393220
  42.6 2.4 %copy-start.15 = (f32[256,40]{0,1:T(8,128)}, f32[256,40]{0,1:T(8,128)S(1)}, u32[]{:S(2)}) copy-start(f32[256,40]{0,1:T(8,128)S(1)} %add_exponential_fusion) | copy-start | bytes 122884
  43.7 13.2 %collective-permute-start.11 = (f32[20,64,128]{2,1,0:T(8,128)S(1)}, f32[20,64,128]{2,1,0:T(8,128)S(1)}, u32[]{:S(2)}, u32[]{:S(2)}) collective-permute-start(f32[20,64,128]{2,1,0:T(8,128)S(1)} %dynamic-slice_bitcast_fusion), channel_id=1, source_target_pairs={{0,1},{1,0},{2,3},{3,2},{4,5},{5,4},{6,7},{7,6},{8,9},{9,8},{10,11... | collective-permute-start | bytes 1966088 | tf_op jit(solution)/shard_map/ppermute | solution.py:100
  45.1 8.2 %collective-permute-start.3 = (f32[2,20,8,128]{3,2,1,0:T(8,128)S(1)}, f32[2,20,8,128]{3,2,1,0:T(8,128)S(1)}, u32[]{:S(2)}, u32[]{:S(2)}) collective-permute-start(f32[2,20,8,128]{3,2,1,0:T(8,128)S(1)} %dynamic-slice_bitcast_fusion.4), channel_id=1, source_target_pairs={{0,4},{2,6},{4,0},{6,2},{8,12},{10,14},{12,8},{14,10},{1,5},{3,7},... | collective-permute-start | bytes 491528 | tf_op jit(solution)/shard_map/ppermute | solution.py:65
  50.0 7.7 %copy-start.3 = (bf16[2,512,20,64]{1,3,2,0:T(8,128)(2,1)S(1)}, bf16[2,512,20,64]{1,3,2,0:T(8,128)(2,1)}, u32[]{:S(2)}) copy-start(bf16[2,512,20,64]{1,3,2,0:T(8,128)(2,1)} %get-tuple-element.52) | copy-start | bytes 7864324
  53.4 7.9 %collective-permute-start.4 = (f32[1,20,8,128]{3,2,1,0:T(8,128)S(1)}, f32[1,20,8,128]{3,2,1,0:T(8,128)S(1)}, u32[]{:S(2)}, u32[]{:S(2)}) collective-permute-start(f32[1,20,8,128]{3,2,1,0:T(8,128)S(1)} %constant_dynamic-slice_fusion.3), channel_id=1, source_target_pairs={{0,8},{2,10},{4,12},{6,14},{8,0},{10,2},{12,4},{14,6},{1,9},{3,11}... | collective-permute-start | bytes 245768 | tf_op jit(solution)/shard_map/ppermute | solution.py:65
  57.1 9.3 %collective-permute-start.12 = (f32[4,20,8,128]{3,2,1,0:T(8,128)S(1)}, f32[4,20,8,128]{3,2,1,0:T(8,128)S(1)}, u32[]{:S(2)}, u32[]{:S(2)}) collective-permute-start(f32[4,20,8,128]{3,2,1,0:T(8,128)S(1)} %dynamic-slice_bitcast_fusion.1), channel_id=1, source_target_pairs={{0,2},{2,0},{4,6},{6,4},{8,10},{10,8},{12,14},{14,12},{1,3},{3,1},... | collective-permute-start | bytes 983048 | tf_op jit(solution)/shard_map/ppermute | solution.py:65
  61.3 8.2 %collective-permute-start.5 = (bf16[1,20,8,128]{3,2,1,0:T(8,128)(2,1)S(1)}, bf16[1,20,8,128]{3,2,1,0:T(8,128)(2,1)S(1)}, u32[]{:S(2)}, u32[]{:S(2)}) collective-permute-start(bf16[1,20,8,128]{3,2,1,0:T(8,128)(2,1)S(1)} %add_convert_fusion.1), channel_id=1, source_target_pairs={{0,8},{2,10},{4,12},{6,14},{8,0},{10,2},{12,4},{14,6},{1,9},{3,11}... | collective-permute-start | bytes 122888 | tf_op jit(solution)/shard_map/ppermute | solution.py:76
  66.5 6.3 %collective-permute-start.13 = (f32[2,20,8,128]{3,2,1,0:T(8,128)S(1)}, f32[2,20,8,128]{3,2,1,0:T(8,128)S(1)}, u32[]{:S(2)}, u32[]{:S(2)}) collective-permute-start(f32[2,20,8,128]{3,2,1,0:T(8,128)S(1)} %dynamic-slice_bitcast_fusion.3), channel_id=1, source_target_pairs={{0,4},{2,6},{4,0},{6,2},{8,12},{10,14},{12,8},{14,10},{1,5},{3,7},... | collective-permute-start | bytes 491528 | tf_op jit(solution)/shard_map/ppermute | solution.py:65
  69.5 5.4 %collective-permute-start.6 = (bf16[2,20,8,128]{3,2,1,0:T(8,128)(2,1)S(1)}, bf16[2,20,8,128]{3,2,1,0:T(8,128)(2,1)S(1)}, u32[]{:S(2)}, u32[]{:S(2)}) collective-permute-start(bf16[2,20,8,128]{3,2,1,0:T(8,128)(2,1)S(1)} %maximum_select_fusion.7), channel_id=1, source_target_pairs={{0,4},{2,6},{4,0},{6,2},{8,12},{10,14},{12,8},{14,10},{1,5},{3,7},... | collective-permute-start | bytes 245768 | tf_op jit(solution)/shard_map/ppermute | solution.py:76
  72.8 5.4 %collective-permute-start.14 = (f32[1,20,8,128]{3,2,1,0:T(8,128)S(1)}, f32[1,20,8,128]{3,2,1,0:T(8,128)S(1)}, u32[]{:S(2)}, u32[]{:S(2)}) collective-permute-start(f32[1,20,8,128]{3,2,1,0:T(8,128)S(1)} %constant_dynamic-slice_fusion.2), channel_id=1, source_target_pairs={{0,8},{2,10},{4,12},{6,14},{8,0},{10,2},{12,4},{14,6},{1,9},{3,11}... | collective-permute-start | bytes 245768 | tf_op jit(solution)/shard_map/ppermute | solution.py:65
  75.5 12.5 %collective-permute-start.7 = (bf16[4,20,8,128]{3,2,1,0:T(8,128)(2,1)}, bf16[4,20,8,128]{3,2,1,0:T(8,128)(2,1)}, u32[]{:S(2)}, u32[]{:S(2)}) collective-permute-start(bf16[4,20,8,128]{3,2,1,0:T(8,128)(2,1)} %maximum_select_fusion.3), channel_id=1, source_target_pairs={{0,2},{2,0},{4,6},{6,4},{8,10},{10,8},{12,14},{14,12},{1,3},{3,1},... | collective-permute-start | bytes 491528 | tf_op jit(solution)/shard_map/ppermute | solution.py:76
  78.3 6.5 %collective-permute-start.15 = (bf16[1,20,8,128]{3,2,1,0:T(8,128)(2,1)S(1)}, bf16[1,20,8,128]{3,2,1,0:T(8,128)(2,1)S(1)}, u32[]{:S(2)}, u32[]{:S(2)}) collective-permute-start(bf16[1,20,8,128]{3,2,1,0:T(8,128)(2,1)S(1)} %add_convert_fusion), channel_id=1, source_target_pairs={{0,8},{2,10},{4,12},{6,14},{8,0},{10,2},{12,4},{14,6},{1,9},{3,11}... | collective-permute-start | bytes 122888 | tf_op jit(solution)/shard_map/ppermute | solution.py:76
  84.8 5.6 %collective-permute-start.16 = (bf16[2,20,8,128]{3,2,1,0:T(8,128)(2,1)S(1)}, bf16[2,20,8,128]{3,2,1,0:T(8,128)(2,1)S(1)}, u32[]{:S(2)}, u32[]{:S(2)}) collective-permute-start(bf16[2,20,8,128]{3,2,1,0:T(8,128)(2,1)S(1)} %maximum_select_fusion.8), channel_id=1, source_target_pairs={{0,4},{2,6},{4,0},{6,2},{8,12},{10,14},{12,8},{14,10},{1,5},{3,7},... | collective-permute-start | bytes 245768 | tf_op jit(solution)/shard_map/ppermute | solution.py:76
  90.4 5.4 %collective-permute-start.17 = (bf16[4,20,8,128]{3,2,1,0:T(8,128)(2,1)S(1)}, bf16[4,20,8,128]{3,2,1,0:T(8,128)(2,1)S(1)}, u32[]{:S(2)}, u32[]{:S(2)}) collective-permute-start(bf16[4,20,8,128]{3,2,1,0:T(8,128)(2,1)S(1)} %maximum_select_fusion.4), channel_id=1, source_target_pairs={{0,2},{2,0},{4,6},{6,4},{8,10},{10,8},{12,14},{14,12},{1,3},{3,1},... | collective-permute-start | bytes 491528 | tf_op jit(solution)/shard_map/ppermute | solution.py:76
  91.9 7.7 %collective-permute-start.8 = (bf16[20,64,128]{2,1,0:T(8,128)(2,1)}, bf16[20,64,128]{2,1,0:T(8,128)(2,1)}, u32[]{:S(2)}, u32[]{:S(2)}) collective-permute-start(bf16[20,64,128]{2,1,0:T(8,128)(2,1)} %copy_bitcast_fusion), channel_id=1, source_target_pairs={{0,1},{1,0},{2,3},{3,2},{4,5},{5,4},{6,7},{7,6},{8,9},{9,8},{10,11... | collective-permute-start | bytes 983048 | tf_op jit(solution)/shard_map/ppermute | solution.py:100
  95.9 1.0 copy-start.5
  97.0 2.7 %copy-start.16 = (f32[256,40]{0,1:T(8,128)S(1)}, f32[256,40]{0,1:T(8,128)}, u32[]{:S(2)}) copy-start(f32[256,40]{0,1:T(8,128)} %copy-done.15) | copy-start | bytes 122884
  99.6 3.5 %copy-start.9 = (f32[256,128]{0,1:T(8,128)S(1)}, f32[256,128]{0,1:T(8,128)}, u32[]{:S(2)}) copy-start(f32[256,128]{0,1:T(8,128)} %copy.117) | copy-start | bytes 393220
  99.6 7.2 %collective-permute-start.18 = (f32[2,256,256]{2,1,0:T(8,128)}, f32[2,256,256]{2,1,0:T(8,128)S(1)}, u32[]{:S(2)}, u32[]{:S(2)}) collective-permute-start(f32[2,256,256]{2,1,0:T(8,128)} %bitcast.62), channel_id=1, source_target_pairs={{0,1},{1,0},{2,3},{3,2},{4,5},{5,4},{6,7},{7,6},{8,9},{9,8},{10,11... | collective-permute-start | bytes 1572872 | tf_op jit(solution)/shard_map/ppermute | solution.py:100

commit v17 on v16

--- a/solution.py
+++ b/solution.py
@@ -74,10 +74,12 @@
     for bit in reversed(range(nbits)):
         step = 1 << bit
         other = lax.ppermute(value, axis, [(at, at ^ step) for at in range(count)])
-        upper = me // step % 2 == 1
-        value = jnp.where(
-            upper, jnp.concatenate([other, value]), jnp.concatenate([value, other])
-        )
+        upper = me // step % 2
+        both = jnp.stack([value, other])
+        value = jnp.concatenate([
+            lax.dynamic_index_in_dim(both, upper, 0, keepdims=False),
+            lax.dynamic_index_in_dim(both, 1 - upper, 0, keepdims=False),
+        ])
     rest = piece.shape
     value = value.reshape((2,) * nbits + rest)
     axes = list(reversed(range(nbits)))

time: 108 us -> 115 us (1.065)
  starting transfers between devices: 26.1 us -> 29.6 us
  local copies, waits for them, and re-layouts: 24.3 us -> 25.9 us
  other arithmetic: 12.1 us -> 13.3 us
    ppermute x6, waiting for transfers between devices: 14 us -> 8.61 us  [halving_scatter(): lax.ppermute(give, axis, [(at, at ^ step) for at in range(count)])]
    ppermute x6, waiting for transfers between devices: 6.71 us -> 11.7 us  [doubling_gather(): other = lax.ppermute(value, axis, [(at, at ^ step) for at in range(count)])]
    ppermute x6, starting transfers between devices: 6.51 us -> 9.19 us  [doubling_gather(): other = lax.ppermute(value, axis, [(at, at ^ step) for at in range(count)])]
    select_n x6 -> x0, other arithmetic: 1.96 us -> none  [doubling_gather(): jnp.where(upper, jnp.concatenate([other, value]), jnp.concatenate([value,...]
    squeeze x0 -> x6, other arithmetic: none -> 1.37 us  [doubling_gather(): lax.dynamic_index_in_dim(both, upper, 0, keepdims=False)]
    ppermute x6, starting transfers between devices: 13.8 us -> 15 us  [halving_scatter(): lax.ppermute(give, axis, [(at, at ^ step) for at in range(count)])]
    unnamed x38 -> x40, local copies, waits for them, and re-layouts: 9.55 us -> 10.4 us
  transfers between devices with their start and end apart: 19 -> 19, of which waited for: 8 -> 7; matrix products, arithmetic and copies ran while one was open for 53% -> 50% of each run, Pallas kernels for 0% -> 0%
where the time goes in v17:
time: 115 us
  starting transfers between devices  29.6 us (26%)
  local copies, waits for them, and re-layouts  25.9 us (23%)
  matrix products  24.1 us (21%)
  waiting for transfers between devices  20.3 us (18%)
  other arithmetic  13.3 us (12%)
  between operations  1.31 us (1%)
    ppermute x6, starting transfers between devices, halving_scatter(): lax.ppermute(give, axis, [(at, at ^ step) for at in range(count)])  15 us
    ppermute x6, waiting for transfers between devices, doubling_gather(): other = lax.ppermute(value, axis, [(at, at ^ step) for at in range(count)])  11.7 us
    unnamed x40, local copies, waits for them, and re-layouts  10.4 us
    ppermute x6, starting transfers between devices, doubling_gather(): other = lax.ppermute(value, axis, [(at, at ^ step) for at in range(count)])  9.19 us
    ppermute x6, waiting for transfers between devices, halving_scatter(): lax.ppermute(give, axis, [(at, at ^ step) for at in range(count)])  8.61 us
    optimization_barrier x2, local copies, waits for them, and re-layouts, suffix_sum(): value, args = lax.optimization_barrier((value, pick(done)))  7.43 us
    dot_general x1, matrix products, shards(): jnp.einsum('chts,cthp->cshp', kernel, g_heads, preferred_element_type=jnp...  7.35 us
    convert_element_type x2, other arithmetic, split_bf16(): low = (value - high).astype(jnp.bfloat16)  5.75 us
  transfers between devices with their start and end apart: 19, of which 7 were waited for; matrix products, arithmetic and copies ran while one was open for 50% of the time, Pallas kernels for 0%

profile of v17, /device:TPU:0, one launch (start us, length us, event | category | flops | bytes accessed | tf_op | source)
XLA Modules:
  0.0 114.5 jit_solution(6602768091624949210)
XLA Ops:
  0.7 0.9 fusion.46
  1.6 1.3 %collective-permute-start = (f32[40]{0:T(128)S(1)}, f32[40]{0:T(128)S(1)}, u32[]{:S(2)}, u32[]{:S(2)}) collective-permute-start(f32[40]{0:T(128)S(1)} %fusion.46), channel_id=1, source_target_pairs={{1,0},{2,1},{3,2},{4,3},{5,4},{6,5},{7,6},{8,7},{9,8},{10,9},{11,1... | collective-permute-start | bytes 488 | tf_op jit(solution)/shard_map/ppermute | solution.py:35
  3.0 0.8 iota_compare_fusion
  3.8 1.0 multiply_log-plus-one_fusion
  4.8 1.1 exponential_bitcast_fusion
  5.9 1.6 %copy.117 = f32[256,128]{0,1:T(8,128)} copy(bf16[256,128]{1,0:T(8,128)(2,1)} %param.10) | data formatting | bytes 196608 | tf_op jit(solution)/shard_map/convert_element_type | solution.py:156
  7.5 2.4 %copy.119 = bf16[256,2560]{0,1:T(8,128)(2,1)} copy(bf16[256,2560]{1,0:T(8,128)(2,1)} %param.9) | data formatting | bytes 2621440 | tf_op args[0]
  10.1 1.3 %collective-permute-start.1 = (f32[40]{0:T(128)S(1)}, f32[40]{0:T(128)S(1)}, u32[]{:S(2)}, u32[]{:S(2)}) collective-permute-start(f32[40]{0:T(128)S(1)} %add.131), channel_id=1, source_target_pairs={{2,0},{3,1},{4,2},{5,3},{6,4},{7,5},{8,6},{9,7},{10,8},{11,9},{12,... | collective-permute-start | bytes 488 | tf_op jit(solution)/shard_map/ppermute | solution.py:35
  11.3 3.0 %copy.111 = bf16[2,512,1280]{1,2,0:T(8,128)(2,1)S(1)} copy(bf16[2,512,1280]{2,1,0:T(8,128)(2,1)} %param.17) | data formatting | bytes 5242880 | tf_op jit(solution)/shard_map/optimization_barrier | solution.py:34
  14.3 0.2 broadcast_select_fusion
  14.6 2.8 %fusion.6 = (bf16[2,512,20,64]{1,3,2,0:T(8,128)(2,1)}, bf16[2,512,20,64]{1,3,2,0:T(8,128)(2,1)S(1)}) fusion(bf16[2,512,20,64]{1,3,2,0:T(8,128)(2,1)S(1)} %bitcast.161, f32[2,512,20]{1,2,0:T(8,128)S(1)} %get-tuple-element.36), kind=kLoop, calls=%fused_computation.11 | loop fusion | flops 7864320 | bytes 7946240 | tf_op jit(solution)/shard_map/convert_element_type | solution.py:11
  17.3 0.8 convolution_bitcast_fusion
  18.2 1.3 %collective-permute-start.9 = (f32[40]{0:T(128)S(1)}, f32[40]{0:T(128)S(1)}, u32[]{:S(2)}, u32[]{:S(2)}) collective-permute-start(f32[40]{0:T(128)S(1)} %add.132), channel_id=1, source_target_pairs={{4,0},{5,1},{6,2},{7,3},{8,4},{9,5},{10,6},{11,7},{12,8},{13,9},{1... | collective-permute-start | bytes 488 | tf_op jit(solution)/shard_map/ppermute | solution.py:35
  19.5 0.8 dynamic-slice_bitcast_fusion.2
  20.3 4.2 %collective-permute-start.2 = (f32[4,20,8,128]{3,2,1,0:T(8,128)}, f32[4,20,8,128]{3,2,1,0:T(8,128)}, u32[]{:S(2)}, u32[]{:S(2)}) collective-permute-start(f32[4,20,8,128]{3,2,1,0:T(8,128)} %dynamic-slice_bitcast_fusion.2), channel_id=1, source_target_pairs={{0,2},{2,0},{4,6},{6,4},{8,10},{10,8},{12,14},{14,12},{1,3},{3,1},... | collective-permute-start | bytes 983048 | tf_op jit(solution)/shard_map/ppermute | solution.py:65
  24.5 4.4 %copy.116 = bf16[2,512,1280]{1,2,0:T(8,128)(2,1)} copy(bf16[2,512,1280]{2,1,0:T(8,128)(2,1)} %param.12) | data formatting | bytes 5242880 | tf_op jit(solution)/shard_map/optimization_barrier | solution.py:34
  29.0 3.0 %fusion.7 = (bf16[2,512,20,64]{1,3,2,0:T(8,128)(2,1)S(1)}, bf16[2,512,20,64]{1,3,2,0:T(8,128)(2,1)S(1)}) fusion(bf16[2,512,20,64]{1,3,2,0:T(8,128)(2,1)} %bitcast.163, f32[2,512,20]{1,2,0:T(8,128)} %get-tuple-element.43), kind=kLoop, calls=%fused_computation.12 | loop fusion | flops 7864320 | bytes 7946240 | tf_op jit(solution)/shard_map/convert_element_type | solution.py:11
  32.0 0.4 fusion.61
  32.4 1.5 %collective-permute-start.10 = (f32[40]{0:T(128)S(1)}, f32[40]{0:T(128)S(1)}, u32[]{:S(2)}, u32[]{:S(2)}) collective-permute-start(f32[40]{0:T(128)S(1)} %add.145), channel_id=1, source_target_pairs={{8,0},{9,1},{10,2},{11,3},{12,4},{13,5},{14,6},{15,7},{24,16},{25,... | collective-permute-start | bytes 488 | tf_op jit(solution)/shard_map/ppermute | solution.py:35
  34.0 1.6 %fusion.62 = f32[2,512,512]{2,1,0:T(8,128)S(1)} fusion(bf16[2,512,1280]{1,2,0:T(8,128)(2,1)S(1)} %bitcast.158, bf16[2,512,1280]{1,2,0:T(8,128)(2,1)S(1)} %bitcast.165), kind=kOutput, calls=%fused_computation.131 | convolution fusion | flops 1342177280 | bytes 7340032 | tf_op jit(solution)/shard_map/ctk,csk->cts/dot_general | solution.py:181
  35.5 0.1 copy-done.2
  35.7 7.4 %fusion.15 = bf16[2,20,64,512]{3,2,1,0:T(8,128)(2,1)} fusion(bf16[2,512,20,64]{1,3,2,0:T(8,128)(2,1)S(1)} %bitcast.162, f32[2,20,512]{2,1,0:T(8,128)S(1)} %bitcast.192, f32[2,20,512]{2,1,0:T(8,128)S(1)} %bitcast.193, f32[2,512,512]{2,1,0:T(8,128)S(1)} %fusion.61, pred[512,512]{1,0:T(8,128)(4,1)S(1)} %copy-done.4), kind=kOutput, calls=%fused_computation.26 | convolution fusion | flops 1385431040 | bytes 7766016 | tf_op jit(solution)/shard_map/chts,cthp->cshp/dot_general | solution.py:199
  43.1 1.6 %fusion.63 = f32[2,512,512]{2,1,0:T(8,128)S(1)} fusion(bf16[2,512,1280]{1,2,0:T(8,128)(2,1)S(1)} %bitcast.159, bf16[2,512,1280]{1,2,0:T(8,128)(2,1)S(1)} %bitcast.169), kind=kOutput, calls=%fused_computation.132 | convolution fusion | flops 1342177280 | bytes 7340032 | tf_op jit(solution)/shard_map/ctk,csk->cts/dot_general | solution.py:181
  44.7 0.3 add_exponential_fusion
  45.0 1.0 bitcast_add_fusion.3
  46.0 3.6 %collective-permute-start.3 = (f32[2,20,8,128]{3,2,1,0:T(8,128)S(1)}, f32[2,20,8,128]{3,2,1,0:T(8,128)S(1)}, u32[]{:S(2)}, u32[]{:S(2)}) collective-permute-start(f32[2,20,8,128]{3,2,1,0:T(8,128)S(1)} %dynamic-slice_bitcast_fusion.4), channel_id=1, source_target_pairs={{0,4},{2,6},{4,0},{6,2},{8,12},{10,14},{12,8},{14,10},{1,5},{3,7},... | collective-permute-start | bytes 491528 | tf_op jit(solution)/shard_map/ppermute | solution.py:65
  49.6 1.0 fusion.9
  50.8 2.3 %collective-permute-done.3 = f32[2,20,8,128]{3,2,1,0:T(8,128)S(1)} collective-permute-done((f32[2,20,8,128]{3,2,1,0:T(8,128)S(1)}, f32[2,20,8,128]{3,2,1,0:T(8,128)S(1)}, u32[]{:S(2)}, u32[]{:S(2)}) %collective-permute-start.3) | collective-permute-done | bytes 163872 | tf_op jit(solution)/shard_map/ppermute | solution.py:65
  53.1 3.4 %collective-permute-start.4 = (f32[1,20,8,128]{3,2,1,0:T(8,128)S(1)}, f32[1,20,8,128]{3,2,1,0:T(8,128)S(1)}, u32[]{:S(2)}, u32[]{:S(2)}) collective-permute-start(f32[1,20,8,128]{3,2,1,0:T(8,128)S(1)} %constant_dynamic-slice_fusion.3), channel_id=1, source_target_pairs={{0,8},{2,10},{4,12},{6,14},{8,0},{10,2},{12,4},{14,6},{1,9},{3,11}... | collective-permute-start | bytes 245768 | tf_op jit(solution)/shard_map/ppermute | solution.py:65
  56.6 1.8 %add_select_fusion = f32[2,512,512]{2,1,0:T(8,128)S(1)} fusion(f32[2,512,512]{2,1,0:T(8,128)S(1)} %fusion.62, f32[2,512,512]{2,1,0:T(8,128)S(1)} %fusion.63, bf16[2,512,1280]{1,2,0:T(8,128)(2,1)S(1)} %bitcast.164, bf16[2,512,1280]{1,2,0:T(8,128)(2,1)S(1)} %bitcast.166, pred[512,512]{1,0:T(8,128)(4,1)S(1)} %copy-done.4), kind=kOutput, calls=%fused_computation.25 | convolution fusion | flops 1343750144 | bytes 11796480 | tf_op jit(solution)/shard_map/ctk,csk->cts/dot_general | solution.py:181
  58.4 0.6 collective-permute-done.4
  59.0 3.0 %collective-permute-start.5 = (bf16[1,20,8,128]{3,2,1,0:T(8,128)(2,1)S(1)}, bf16[1,20,8,128]{3,2,1,0:T(8,128)(2,1)S(1)}, u32[]{:S(2)}, u32[]{:S(2)}) collective-permute-start(bf16[1,20,8,128]{3,2,1,0:T(8,128)(2,1)S(1)} %add_convert_fusion.1), channel_id=1, source_target_pairs={{0,8},{2,10},{4,12},{6,14},{8,0},{10,2},{12,4},{14,6},{1,9},{3,11}... | collective-permute-start | bytes 122888 | tf_op jit(solution)/shard_map/ppermute | solution.py:76
  62.2 1.4 %collective-permute-start.12 = (f32[4,20,8,128]{3,2,1,0:T(8,128)S(1)}, f32[4,20,8,128]{3,2,1,0:T(8,128)S(1)}, u32[]{:S(2)}, u32[]{:S(2)}) collective-permute-start(f32[4,20,8,128]{3,2,1,0:T(8,128)S(1)} %dynamic-slice_bitcast_fusion.1), channel_id=1, source_target_pairs={{0,2},{2,0},{4,6},{6,4},{8,10},{10,8},{12,14},{14,12},{1,3},{3,1},... | collective-permute-start | bytes 983048 | tf_op jit(solution)/shard_map/ppermute | solution.py:65
  63.6 1.3 %fusion.65 = f32[2,512,128]{1,2,0:T(8,128)S(1)} fusion(f32[2,512,512]{2,1,0:T(8,128)S(1)} %add_select_fusion, bf16[2,512,128]{2,1,0:T(8,128)(2,1)S(1)} %copy-done.8), kind=kOutput, calls=%fused_computation.134 | convolution fusion | flops 805306368 | bytes 2883584 | tf_op jit(solution)/shard_map/cts,csn->ctn/dot_general | solution.py:191
  65.0 0.6 pad_maximum_fusion.5
  65.6 2.3 %collective-permute-start.6 = (bf16[2,20,8,128]{3,2,1,0:T(8,128)(2,1)}, bf16[2,20,8,128]{3,2,1,0:T(8,128)(2,1)}, u32[]{:S(2)}, u32[]{:S(2)}) collective-permute-start(bf16[2,20,8,128]{3,2,1,0:T(8,128)(2,1)} %get-tuple-element.104), channel_id=1, source_target_pairs={{0,4},{2,6},{4,0},{6,2},{8,12},{10,14},{12,8},{14,10},{1,5},{3,7},... | collective-permute-start | bytes 245768 | tf_op jit(solution)/shard_map/ppermute | solution.py:76
  67.9 1.4 %collective-permute-done.12 = f32[4,20,8,128]{3,2,1,0:T(8,128)S(1)} collective-permute-done((f32[4,20,8,128]{3,2,1,0:T(8,128)S(1)}, f32[4,20,8,128]{3,2,1,0:T(8,128)S(1)}, u32[]{:S(2)}, u32[]{:S(2)}) %collective-permute-start.12) | collective-permute-done | bytes 327712 | tf_op jit(solution)/shard_map/ppermute | solution.py:65
  69.4 0.7 copy-done.6
  70.1 0.7 dynamic-slice_bitcast_fusion.3
  70.8 2.3 %collective-permute-start.13 = (f32[2,20,8,128]{3,2,1,0:T(8,128)}, f32[2,20,8,128]{3,2,1,0:T(8,128)}, u32[]{:S(2)}, u32[]{:S(2)}) collective-permute-start(f32[2,20,8,128]{3,2,1,0:T(8,128)} %dynamic-slice_bitcast_fusion.3), channel_id=1, source_target_pairs={{0,4},{2,6},{4,0},{6,2},{8,12},{10,14},{12,8},{14,10},{1,5},{3,7},... | collective-permute-start | bytes 491528 | tf_op jit(solution)/shard_map/ppermute | solution.py:65
  73.1 1.7 %fusion.64 = f32[2,512,128]{1,2,0:T(8,128)} fusion(f32[2,512,512]{2,1,0:T(8,128)S(1)} %add_select_fusion, bf16[2,512,128]{2,1,0:T(8,128)(2,1)S(1)} %copy-done), kind=kOutput, calls=%fused_computation.133 | convolution fusion | flops 805306368 | bytes 2883584 | tf_op jit(solution)/shard_map/cts,ctn->csn/dot_general | solution.py:188
  74.8 4.4 %copy.139 = bf16[2,512,1280]{2,1,0:T(8,128)(2,1)} copy(bf16[2,512,1280]{1,2,0:T(8,128)(2,1)} %bitcast.168) | data formatting | bytes 5242880
  79.2 1.0 fusion.37
  80.2 1.0 bitcast_add_fusion.4
  81.3 1.8 %collective-permute-start.7 = (bf16[4,20,8,128]{3,2,1,0:T(8,128)(2,1)S(1)}, bf16[4,20,8,128]{3,2,1,0:T(8,128)(2,1)S(1)}, u32[]{:S(2)}, u32[]{:S(2)}) collective-permute-start(bf16[4,20,8,128]{3,2,1,0:T(8,128)(2,1)S(1)} %get-tuple-element.94), channel_id=1, source_target_pairs={{0,2},{2,0},{4,6},{6,4},{8,10},{10,8},{12,14},{14,12},{1,3},{3,1},... | collective-permute-start | bytes 491528 | tf_op jit(solution)/shard_map/ppermute | solution.py:76
  83.1 4.3 %collective-permute-done.14 = f32[1,20,8,128]{3,2,1,0:T(8,128)S(1)} collective-permute-done((f32[1,20,8,128]{3,2,1,0:T(8,128)S(1)}, f32[1,20,8,128]{3,2,1,0:T(8,128)S(1)}, u32[]{:S(2)}, u32[]{:S(2)}) %collective-permute-start.14) | collective-permute-done | bytes 81952 | tf_op jit(solution)/shard_map/ppermute | solution.py:65
  87.5 0.1 fusion.28
  87.6 4.7 %collective-permute-done.15 = bf16[1,20,8,128]{3,2,1,0:T(8,128)(2,1)S(1)} collective-permute-done((bf16[1,20,8,128]{3,2,1,0:T(8,128)(2,1)S(1)}, bf16[1,20,8,128]{3,2,1,0:T(8,128)(2,1)S(1)}, u32[]{:S(2)}, u32[]{:S(2)}) %collective-permute-start.15) | collective-permute-done | bytes 40992 | tf_op jit(solution)/shard_map/ppermute | solution.py:76
  92.6 4.4 %collective-permute-done.16 = bf16[2,20,8,128]{3,2,1,0:T(8,128)(2,1)S(1)} collective-permute-done((bf16[2,20,8,128]{3,2,1,0:T(8,128)(2,1)S(1)}, bf16[2,20,8,128]{3,2,1,0:T(8,128)(2,1)S(1)}, u32[]{:S(2)}, u32[]{:S(2)}) %collective-permute-start.16) | collective-permute-done | bytes 81952 | tf_op jit(solution)/shard_map/ppermute | solution.py:76
  97.0 2.0 %collective-permute-start.17 = (bf16[4,20,8,128]{3,2,1,0:T(8,128)(2,1)S(1)}, bf16[4,20,8,128]{3,2,1,0:T(8,128)(2,1)S(1)}, u32[]{:S(2)}, u32[]{:S(2)}) collective-permute-start(bf16[4,20,8,128]{3,2,1,0:T(8,128)(2,1)S(1)} %get-tuple-element.90), channel_id=1, source_target_pairs={{0,2},{2,0},{4,6},{6,4},{8,10},{10,8},{12,14},{14,12},{1,3},{3,1},... | collective-permute-start | bytes 491528 | tf_op jit(solution)/shard_map/ppermute | solution.py:76
  99.0 0.8 copy_bitcast_fusion
  99.9 2.6 %collective-permute-done.17 = bf16[4,20,8,128]{3,2,1,0:T(8,128)(2,1)S(1)} collective-permute-done((bf16[4,20,8,128]{3,2,1,0:T(8,128)(2,1)S(1)}, bf16[4,20,8,128]{3,2,1,0:T(8,128)(2,1)S(1)}, u32[]{:S(2)}, u32[]{:S(2)}) %collective-permute-start.17) | collective-permute-done | bytes 163872 | tf_op jit(solution)/shard_map/ppermute | solution.py:76
  102.4 0.1 fusion.24
  102.7 0.6 convolution_add_fusion
  103.3 0.3 copy-done.5
  103.7 0.7 reshape.189
  104.4 0.9 constant_dynamic-slice_fusion.1
  105.3 1.1 copy.136
  106.4 2.7 %fusion.8 = f32[256,128]{0,1:T(8,128)S(1)} fusion(f32[256,40]{0,1:T(8,128)S(1)} %copy-done.17, bf16[256,40,64]{0,2,1:T(8,128)(2,1)} %bitcast.179, bf16[20,64,128]{2,1,0:T(8,128)(2,1)} %collective-permute-done.8, bf16[20,64,128]{2,1,0:T(8,128)(2,1)} %copy_bitcast_fusion, pred[]{:T(512)S(6)} %eq.16), kind=kOutput, calls=%fused_computation.15 | convolution fusion | flops 171343872 | bytes 2138113 | tf_op jit(solution)/shard_map/jhp,hpn->jhn/dot_general | solution.py:221
  109.1 0.8 copy.138
  109.8 1.8 %fusion.16 = bf16[40,64,256]{2,1,0:T(8,128)(2,1)S(1)} fusion(f32[256,128]{0,1:T(8,128)S(1)} %copy-done.10, f32[256,40]{0,1:T(8,128)S(1)} %copy-done.17, bf16[20,64,128]{2,1,0:T(8,128)(2,1)} %collective-permute-done.8, bf16[20,64,128]{2,1,0:T(8,128)(2,1)} %copy_bitcast_fusion, pred[]{:T(512)S(6)} %eq.16), kind=kOutput, calls=%fused_computation.27 | convolution fusion | flops 172032000 | bytes 2138113 | tf_op jit(solution)/shard_map/jhn,hpn->jhp/dot_general | solution.py:217
  111.7 1.6 %copy.137 = bf16[256,2560]{1,0:T(8,128)(2,1)} copy(bf16[256,2560]{0,1:T(8,128)(2,1)S(1)} %bitcast.183) | data formatting | bytes 2621440
  113.3 0.3 copy.135
  113.7 0.8 fusion.56
  (82 shorter events, 1.5 us)
Async XLA Ops:
  0.6 16.7 %copy-start = (bf16[2,512,128]{2,1,0:T(8,128)(2,1)S(1)}, bf16[2,512,128]{2,1,0:T(8,128)(2,1)}, u32[]{:S(2)}) copy-start(bf16[2,512,128]{2,1,0:T(8,128)(2,1)} %param.14) | copy-start | bytes 786436
  0.6 9.3 %copy-start.15 = (s32[2]{0:T(128)S(1)}, s32[2]{0:T(128)}, u32[]{:S(2)}) copy-start(s32[2]{0:T(128)} %param.16) | copy-start | bytes 28
  1.6 8.4 %collective-permute-start = (f32[40]{0:T(128)S(1)}, f32[40]{0:T(128)S(1)}, u32[]{:S(2)}, u32[]{:S(2)}) collective-permute-start(f32[40]{0:T(128)S(1)} %fusion.46), channel_id=1, source_target_pairs={{1,0},{2,1},{3,2},{4,3},{5,4},{6,5},{7,6},{8,7},{9,8},{10,9},{11,1... | collective-permute-start | bytes 488 | tf_op jit(solution)/shard_map/ppermute | solution.py:35
  5.9 8.6 %copy-start.12 = (f32[2,512,20]{1,2,0:T(8,128)}, f32[2,512,20]{1,2,0:T(8,128)S(1)}, u32[]{:S(2)}) copy-start(f32[2,512,20]{1,2,0:T(8,128)S(1)} %get-tuple-element.36) | copy-start | bytes 245764
  10.1 8.1 %collective-permute-start.1 = (f32[40]{0:T(128)S(1)}, f32[40]{0:T(128)S(1)}, u32[]{:S(2)}, u32[]{:S(2)}) collective-permute-start(f32[40]{0:T(128)S(1)} %add.131), channel_id=1, source_target_pairs={{2,0},{3,1},{4,2},{5,3},{6,4},{7,5},{8,6},{9,7},{10,8},{11,9},{12,... | collective-permute-start | bytes 488 | tf_op jit(solution)/shard_map/ppermute | solution.py:35
  14.5 2.8 %copy-start.1 = (bf16[2,512,1280]{1,2,0:T(8,128)(2,1)}, bf16[2,512,1280]{1,2,0:T(8,128)(2,1)S(1)}, u32[]{:S(2)}) copy-start(bf16[2,512,1280]{1,2,0:T(8,128)(2,1)S(1)} %broadcast_select_fusion) | copy-start | bytes 7864324
  18.2 14.2 %collective-permute-start.9 = (f32[40]{0:T(128)S(1)}, f32[40]{0:T(128)S(1)}, u32[]{:S(2)}, u32[]{:S(2)}) collective-permute-start(f32[40]{0:T(128)S(1)} %add.132), channel_id=1, source_target_pairs={{4,0},{5,1},{6,2},{7,3},{8,4},{9,5},{10,6},{11,7},{12,8},{13,9},{1... | collective-permute-start | bytes 488 | tf_op jit(solution)/shard_map/ppermute | solution.py:35
  20.3 24.7 %collective-permute-start.2 = (f32[4,20,8,128]{3,2,1,0:T(8,128)}, f32[4,20,8,128]{3,2,1,0:T(8,128)}, u32[]{:S(2)}, u32[]{:S(2)}) collective-permute-start(f32[4,20,8,128]{3,2,1,0:T(8,128)} %dynamic-slice_bitcast_fusion.2), channel_id=1, source_target_pairs={{0,2},{2,0},{4,6},{6,4},{8,10},{10,8},{12,14},{14,12},{1,3},{3,1},... | collective-permute-start | bytes 983048 | tf_op jit(solution)/shard_map/ppermute | solution.py:65
  29.0 3.0 %copy-start.8 = (bf16[2,512,128]{2,1,0:T(8,128)(2,1)S(1)}, bf16[2,512,128]{2,1,0:T(8,128)(2,1)}, u32[]{:S(2)}) copy-start(bf16[2,512,128]{2,1,0:T(8,128)(2,1)} %param.13) | copy-start | bytes 786436
  32.4 12.2 %collective-permute-start.10 = (f32[40]{0:T(128)S(1)}, f32[40]{0:T(128)S(1)}, u32[]{:S(2)}, u32[]{:S(2)}) collective-permute-start(f32[40]{0:T(128)S(1)} %add.145), channel_id=1, source_target_pairs={{8,0},{9,1},{10,2},{11,3},{12,4},{13,5},{14,6},{15,7},{24,16},{25,... | collective-permute-start | bytes 488 | tf_op jit(solution)/shard_map/ppermute | solution.py:35
  33.9 1.7 %copy-start.2 = (bf16[2,512,1280]{1,2,0:T(8,128)(2,1)S(1)}, bf16[2,512,1280]{1,2,0:T(8,128)(2,1)}, u32[]{:S(2)}) copy-start(bf16[2,512,1280]{1,2,0:T(8,128)(2,1)} %copy-done.1) | copy-start | bytes 7864324
  33.9 1.7 %copy-start.4 = (pred[512,512]{1,0:T(8,128)(4,1)S(1)}, pred[512,512]{1,0:T(8,128)(4,1)}, u32[]{:S(2)}) copy-start(pred[512,512]{1,0:T(8,128)(4,1)} %iota_compare_fusion) | copy-start | bytes 786436
  33.9 1.7 %copy-start.11 = (f32[2,512,20]{1,2,0:T(8,128)S(1)}, f32[2,512,20]{1,2,0:T(8,128)}, u32[]{:S(2)}) copy-start(f32[2,512,20]{1,2,0:T(8,128)} %get-tuple-element.43) | copy-start | bytes 245764
  33.9 1.8 %copy-start.13 = (f32[2,512,20]{1,2,0:T(8,128)S(1)}, f32[2,512,20]{1,2,0:T(8,128)}, u32[]{:S(2)}) copy-start(f32[2,512,20]{1,2,0:T(8,128)} %copy-done.12) | copy-start | bytes 245764
  43.1 1.6 %copy-start.14 = (s32[256,40]{0,1:T(8,128)S(1)}, s32[256,40]{0,1:T(8,128)}, u32[]{:S(2)}) copy-start(s32[256,40]{0,1:T(8,128)} %param.11) | copy-start | bytes 122884
  43.1 6.6 %copy-start.7 = (bf16[256,2560]{0,1:T(8,128)(2,1)S(1)}, bf16[256,2560]{0,1:T(8,128)(2,1)}, u32[]{:S(2)}) copy-start(bf16[256,2560]{0,1:T(8,128)(2,1)} %copy.119) | copy-start | bytes 3932164
  43.1 6.6 %copy-start.9 = (f32[256,128]{0,1:T(8,128)S(1)}, f32[256,128]{0,1:T(8,128)}, u32[]{:S(2)}) copy-start(f32[256,128]{0,1:T(8,128)} %copy.117) | copy-start | bytes 393220
  45.0 5.8 %copy-start.16 = (f32[256,40]{0,1:T(8,128)}, f32[256,40]{0,1:T(8,128)S(1)}, u32[]{:S(2)}) copy-start(f32[256,40]{0,1:T(8,128)S(1)} %add_exponential_fusion) | copy-start | bytes 122884
  46.0 7.1 %collective-permute-start.3 = (f32[2,20,8,128]{3,2,1,0:T(8,128)S(1)}, f32[2,20,8,128]{3,2,1,0:T(8,128)S(1)}, u32[]{:S(2)}, u32[]{:S(2)}) collective-permute-start(f32[2,20,8,128]{3,2,1,0:T(8,128)S(1)} %dynamic-slice_bitcast_fusion.4), channel_id=1, source_target_pairs={{0,4},{2,6},{4,0},{6,2},{8,12},{10,14},{12,8},{14,10},{1,5},{3,7},... | collective-permute-start | bytes 491528 | tf_op jit(solution)/shard_map/ppermute | solution.py:65
  49.6 6.9 %copy-start.3 = (bf16[2,512,20,64]{1,3,2,0:T(8,128)(2,1)S(1)}, bf16[2,512,20,64]{1,3,2,0:T(8,128)(2,1)}, u32[]{:S(2)}) copy-start(bf16[2,512,20,64]{1,3,2,0:T(8,128)(2,1)} %get-tuple-element.52) | copy-start | bytes 7864324
  50.7 11.3 %collective-permute-start.11 = (f32[20,64,128]{2,1,0:T(8,128)S(1)}, f32[20,64,128]{2,1,0:T(8,128)S(1)}, u32[]{:S(2)}, u32[]{:S(2)}) collective-permute-start(f32[20,64,128]{2,1,0:T(8,128)S(1)} %dynamic-slice_bitcast_fusion), channel_id=1, source_target_pairs={{0,1},{1,0},{2,3},{3,2},{4,5},{5,4},{6,7},{7,6},{8,9},{9,8},{10,11... | collective-permute-start | bytes 1966088 | tf_op jit(solution)/shard_map/ppermute | solution.py:102
  53.1 5.8 %collective-permute-start.4 = (f32[1,20,8,128]{3,2,1,0:T(8,128)S(1)}, f32[1,20,8,128]{3,2,1,0:T(8,128)S(1)}, u32[]{:S(2)}, u32[]{:S(2)}) collective-permute-start(f32[1,20,8,128]{3,2,1,0:T(8,128)S(1)} %constant_dynamic-slice_fusion.3), channel_id=1, source_target_pairs={{0,8},{2,10},{4,12},{6,14},{8,0},{10,2},{12,4},{14,6},{1,9},{3,11}... | collective-permute-start | bytes 245768 | tf_op jit(solution)/shard_map/ppermute | solution.py:65
  59.0 5.9 %collective-permute-start.5 = (bf16[1,20,8,128]{3,2,1,0:T(8,128)(2,1)S(1)}, bf16[1,20,8,128]{3,2,1,0:T(8,128)(2,1)S(1)}, u32[]{:S(2)}, u32[]{:S(2)}) collective-permute-start(bf16[1,20,8,128]{3,2,1,0:T(8,128)(2,1)S(1)} %add_convert_fusion.1), channel_id=1, source_target_pairs={{0,8},{2,10},{4,12},{6,14},{8,0},{10,2},{12,4},{14,6},{1,9},{3,11}... | collective-permute-start | bytes 122888 | tf_op jit(solution)/shard_map/ppermute | solution.py:76
  62.2 7.1 %collective-permute-start.12 = (f32[4,20,8,128]{3,2,1,0:T(8,128)S(1)}, f32[4,20,8,128]{3,2,1,0:T(8,128)S(1)}, u32[]{:S(2)}, u32[]{:S(2)}) collective-permute-start(f32[4,20,8,128]{3,2,1,0:T(8,128)S(1)} %dynamic-slice_bitcast_fusion.1), channel_id=1, source_target_pairs={{0,2},{2,0},{4,6},{6,4},{8,10},{10,8},{12,14},{14,12},{1,3},{3,1},... | collective-permute-start | bytes 983048 | tf_op jit(solution)/shard_map/ppermute | solution.py:65
  65.6 13.6 %collective-permute-start.6 = (bf16[2,20,8,128]{3,2,1,0:T(8,128)(2,1)}, bf16[2,20,8,128]{3,2,1,0:T(8,128)(2,1)}, u32[]{:S(2)}, u32[]{:S(2)}) collective-permute-start(bf16[2,20,8,128]{3,2,1,0:T(8,128)(2,1)} %get-tuple-element.104), channel_id=1, source_target_pairs={{0,4},{2,6},{4,0},{6,2},{8,12},{10,14},{12,8},{14,10},{1,5},{3,7},... | collective-permute-start | bytes 245768 | tf_op jit(solution)/shard_map/ppermute | solution.py:76
  69.4 0.7 copy-start.6
  70.8 9.4 %collective-permute-start.13 = (f32[2,20,8,128]{3,2,1,0:T(8,128)}, f32[2,20,8,128]{3,2,1,0:T(8,128)}, u32[]{:S(2)}, u32[]{:S(2)}) collective-permute-start(f32[2,20,8,128]{3,2,1,0:T(8,128)} %dynamic-slice_bitcast_fusion.3), channel_id=1, source_target_pairs={{0,4},{2,6},{4,0},{6,2},{8,12},{10,14},{12,8},{14,10},{1,5},{3,7},... | collective-permute-start | bytes 491528 | tf_op jit(solution)/shard_map/ppermute | solution.py:65
  81.2 6.2 %collective-permute-start.14 = (f32[1,20,8,128]{3,2,1,0:T(8,128)S(1)}, f32[1,20,8,128]{3,2,1,0:T(8,128)S(1)}, u32[]{:S(2)}, u32[]{:S(2)}) collective-permute-start(f32[1,20,8,128]{3,2,1,0:T(8,128)S(1)} %constant_dynamic-slice_fusion.2), channel_id=1, source_target_pairs={{0,8},{2,10},{4,12},{6,14},{8,0},{10,2},{12,4},{14,6},{1,9},{3,11}... | collective-permute-start | bytes 245768 | tf_op jit(solution)/shard_map/ppermute | solution.py:65
  81.3 6.1 %collective-permute-start.7 = (bf16[4,20,8,128]{3,2,1,0:T(8,128)(2,1)S(1)}, bf16[4,20,8,128]{3,2,1,0:T(8,128)(2,1)S(1)}, u32[]{:S(2)}, u32[]{:S(2)}) collective-permute-start(bf16[4,20,8,128]{3,2,1,0:T(8,128)(2,1)S(1)} %get-tuple-element.94), channel_id=1, source_target_pairs={{0,2},{2,0},{4,6},{6,4},{8,10},{10,8},{12,14},{14,12},{1,3},{3,1},... | collective-permute-start | bytes 491528 | tf_op jit(solution)/shard_map/ppermute | solution.py:76
  87.4 5.0 %collective-permute-start.15 = (bf16[1,20,8,128]{3,2,1,0:T(8,128)(2,1)S(1)}, bf16[1,20,8,128]{3,2,1,0:T(8,128)(2,1)S(1)}, u32[]{:S(2)}, u32[]{:S(2)}) collective-permute-start(bf16[1,20,8,128]{3,2,1,0:T(8,128)(2,1)S(1)} %add_convert_fusion), channel_id=1, source_target_pairs={{0,8},{2,10},{4,12},{6,14},{8,0},{10,2},{12,4},{14,6},{1,9},{3,11}... | collective-permute-start | bytes 122888 | tf_op jit(solution)/shard_map/ppermute | solution.py:76
  92.4 4.5 %collective-permute-start.16 = (bf16[2,20,8,128]{3,2,1,0:T(8,128)(2,1)S(1)}, bf16[2,20,8,128]{3,2,1,0:T(8,128)(2,1)S(1)}, u32[]{:S(2)}, u32[]{:S(2)}) collective-permute-start(bf16[2,20,8,128]{3,2,1,0:T(8,128)(2,1)S(1)} %get-tuple-element.100), channel_id=1, source_target_pairs={{0,4},{2,6},{4,0},{6,2},{8,12},{10,14},{12,8},{14,10},{1,5},{3,7},... | collective-permute-start | bytes 245768 | tf_op jit(solution)/shard_map/ppermute | solution.py:76
  97.0 5.4 %collective-permute-start.17 = (bf16[4,20,8,128]{3,2,1,0:T(8,128)(2,1)S(1)}, bf16[4,20,8,128]{3,2,1,0:T(8,128)(2,1)S(1)}, u32[]{:S(2)}, u32[]{:S(2)}) collective-permute-start(bf16[4,20,8,128]{3,2,1,0:T(8,128)(2,1)S(1)} %get-tuple-element.90), channel_id=1, source_target_pairs={{0,2},{2,0},{4,6},{6,4},{8,10},{10,8},{12,14},{14,12},{1,3},{3,1},... | collective-permute-start | bytes 491528 | tf_op jit(solution)/shard_map/ppermute | solution.py:76
  99.8 6.5 %collective-permute-start.8 = (bf16[20,64,128]{2,1,0:T(8,128)(2,1)}, bf16[20,64,128]{2,1,0:T(8,128)(2,1)}, u32[]{:S(2)}, u32[]{:S(2)}) collective-permute-start(bf16[20,64,128]{2,1,0:T(8,128)(2,1)} %copy_bitcast_fusion), channel_id=1, source_target_pairs={{0,1},{1,0},{2,3},{3,2},{4,5},{5,4},{6,7},{7,6},{8,9},{9,8},{10,11... | collective-permute-start | bytes 983048 | tf_op jit(solution)/shard_map/ppermute | solution.py:102
  102.6 1.0 copy-start.5
  103.7 2.7 %copy-start.17 = (f32[256,40]{0,1:T(8,128)S(1)}, f32[256,40]{0,1:T(8,128)}, u32[]{:S(2)}) copy-start(f32[256,40]{0,1:T(8,128)} %copy-done.16) | copy-start | bytes 122884
  106.4 3.4 %copy-start.10 = (f32[256,128]{0,1:T(8,128)S(1)}, f32[256,128]{0,1:T(8,128)}, u32[]{:S(2)}) copy-start(f32[256,128]{0,1:T(8,128)} %copy.117) | copy-start | bytes 393220
  106.4 7.2 %collective-permute-start.18 = (f32[2,256,256]{2,1,0:T(8,128)}, f32[2,256,256]{2,1,0:T(8,128)S(1)}, u32[]{:S(2)}, u32[]{:S(2)}) collective-permute-start(f32[2,256,256]{2,1,0:T(8,128)} %bitcast.86), channel_id=1, source_target_pairs={{0,1},{1,0},{2,3},{3,2},{4,5},{5,4},{6,7},{7,6},{8,9},{9,8},{10,11... | collective-permute-start | bytes 1572872 | tf_op jit(solution)/shard_map/ppermute | solution.py:102

commit v18 on v16

--- a/solution.py
+++ b/solution.py
@@ -183,12 +183,15 @@
 
     weight_sum = pair(decayed_g, x_high) + pair(decayed_g, x_low) + pair(g_low, x_high)
     weight_sum = jnp.where(causal[None], weight_sum, 0.0)
-    db_part = jnp.einsum(
-        "cts,ctn->csn", weight_sum, c_cand.astype(jnp.float32), precision=lax.Precision.HIGHEST
-    )
-    dc_part = jnp.einsum(
-        "cts,csn->ctn", weight_sum, b_cand.astype(jnp.float32), precision=lax.Precision.HIGHEST
-    )
+    sum_high, sum_low = split_bf16(weight_sum)
+
+    def two_pass(spec, other):
+        return jnp.einsum(spec, sum_high, other, preferred_element_type=jnp.float32) + jnp.einsum(
+            spec, sum_low, other, preferred_element_type=jnp.float32
+        )
+
+    db_part = two_pass("cts,ctn->csn", c_cand)
+    dc_part = two_pass("cts,csn->ctn", b_cand)
 
     amp_t = jnp.transpose(amplitude, (0, 2, 1))
     inv_t = jnp.transpose(inverse, (0, 2, 1))

time: 108 us -> 107 us (level)
  waiting for transfers between devices: 20.7 us -> 26.4 us
  other arithmetic: 12.1 us -> 9.28 us
  starting transfers between devices: 26.1 us -> 24.1 us
  local copies, waits for them, and re-layouts: 24.3 us -> 22.4 us
    ppermute x6, waiting for transfers between devices: 14 us -> 16.1 us  [halving_scatter(): lax.ppermute(give, axis, [(at, at ^ step) for at in range(count)])]
    ppermute x4, waiting for transfers between devices: 0.01 us -> 1.9 us  [suffix_sum(): value = value + lax.ppermute(value, axis, back)]
    select_n x6, other arithmetic: 1.96 us -> 0.12 us  [doubling_gather(): jnp.where(upper, jnp.concatenate([other, value]), jnp.concatenate([value,...]
    ppermute x6, waiting for transfers between devices: 6.71 us -> 8.36 us  [doubling_gather(): other = lax.ppermute(value, axis, [(at, at ^ step) for at in range(count)])]
    ppermute x6, starting transfers between devices: 13.8 us -> 12.2 us  [halving_scatter(): lax.ppermute(give, axis, [(at, at ^ step) for at in range(count)])]
    dot_general x2 -> x4, matrix products: 2.98 us -> 2.48 us  [the longest x2 1.66 us: two_pass(): jnp.einsum(spec, sum_low, other, preferred_element_type=jnp.float32)]
    unnamed x38 -> x44, local copies, waits for them, and re-layouts: 9.55 us -> 9.94 us
  transfers between devices with their start and end apart: 19 -> 19, of which waited for: 8 -> 9; matrix products, arithmetic and copies ran while one was open for 53% -> 42% of each run, Pallas kernels for 0% -> 0%
where the time goes in v18:
time: 107 us; the launch traced here: 106 us
  waiting for transfers between devices  26.4 us (25%)
  starting transfers between devices  24.1 us (23%)
  matrix products  22.5 us (21%)
  local copies, waits for them, and re-layouts  22.4 us (21%)
  other arithmetic  9.28 us (9%)
  between operations  1.23 us (1%)
    ppermute x6, waiting for transfers between devices, halving_scatter(): lax.ppermute(give, axis, [(at, at ^ step) for at in range(count)])  16.1 us
    ppermute x6, starting transfers between devices, halving_scatter(): lax.ppermute(give, axis, [(at, at ^ step) for at in range(count)])  12.2 us
    unnamed x44, local copies, waits for them, and re-layouts  9.94 us
    ppermute x6, waiting for transfers between devices, doubling_gather(): other = lax.ppermute(value, axis, [(at, at ^ step) for at in range(count)])  8.36 us
    optimization_barrier x2, local copies, waits for them, and re-layouts, suffix_sum(): value, args = lax.optimization_barrier((value, pick(done)))  7.45 us
    dot_general x1, matrix products, shards(): jnp.einsum('chts,cthp->cshp', kernel, g_heads, preferred_element_type=jnp...  6.71 us
    ppermute x6, starting transfers between devices, doubling_gather(): other = lax.ppermute(value, axis, [(at, at ^ step) for at in range(count)])  6.6 us
    convert_element_type x2, other arithmetic, split_bf16(): low = (value - high).astype(jnp.bfloat16)  5.75 us
  transfers between devices with their start and end apart: 19, of which 9 were waited for; matrix products, arithmetic and copies ran while one was open for 42% of the time, Pallas kernels for 0%

profile of v18, /device:TPU:0, one launch (start us, length us, event | category | flops | bytes accessed | tf_op | source)
XLA Modules:
  0.0 105.9 jit_solution(14650967731624150705)
XLA Ops:
  0.7 1.0 fusion.28
  1.6 1.3 %collective-permute-start = (f32[40]{0:T(128)S(1)}, f32[40]{0:T(128)S(1)}, u32[]{:S(2)}, u32[]{:S(2)}) collective-permute-start(f32[40]{0:T(128)S(1)} %fusion.28), channel_id=1, source_target_pairs={{1,0},{2,1},{3,2},{4,3},{5,4},{6,5},{7,6},{8,7},{9,8},{10,9},{11,1... | collective-permute-start | bytes 488 | tf_op jit(solution)/shard_map/ppermute | solution.py:35
  2.9 0.8 iota_compare_fusion
  3.7 1.0 multiply_log-plus-one_fusion
  4.7 1.1 %exponential_bitcast_fusion = (f32[2,512,20]{1,2,0:T(8,128)}, f32[2,512,20]{1,2,0:T(8,128)S(1)}) fusion(f32[2,512,20]{1,0,2:T(2,128)S(1)} %multiply_log-plus-one_fusion), kind=kOutput, calls=%fused_computation.62 | convolution fusion | flops 126111744 | bytes 245760 | tf_op jit(solution)/shard_map/ts,csh->cth/dot_general | solution.py:119
  5.8 2.5 %copy.127 = bf16[256,2560]{0,1:T(8,128)(2,1)} copy(bf16[256,2560]{1,0:T(8,128)(2,1)} %param.9) | data formatting | bytes 2621440 | tf_op args[0]
  8.3 0.8 copy.125
  9.1 3.0 %copy.119 = bf16[2,512,1280]{1,2,0:T(8,128)(2,1)S(1)} copy(bf16[2,512,1280]{2,1,0:T(8,128)(2,1)} %param.17) | data formatting | bytes 5242880 | tf_op jit(solution)/shard_map/optimization_barrier | solution.py:34
  12.2 1.3 %collective-permute-start.1 = (f32[40]{0:T(128)S(1)}, f32[40]{0:T(128)S(1)}, u32[]{:S(2)}, u32[]{:S(2)}) collective-permute-start(f32[40]{0:T(128)S(1)} %add.125), channel_id=1, source_target_pairs={{2,0},{3,1},{4,2},{5,3},{6,4},{7,5},{8,6},{9,7},{10,8},{11,9},{12,... | collective-permute-start | bytes 488 | tf_op jit(solution)/shard_map/ppermute | solution.py:35
  13.5 0.2 broadcast_select_fusion
  13.7 2.8 %fusion.6 = (bf16[2,512,20,64]{1,3,2,0:T(8,128)(2,1)}, bf16[2,512,20,64]{1,3,2,0:T(8,128)(2,1)S(1)}) fusion(bf16[2,512,20,64]{1,3,2,0:T(8,128)(2,1)S(1)} %bitcast.121, f32[2,512,20]{1,2,0:T(8,128)S(1)} %get-tuple-element.36), kind=kLoop, calls=%fused_computation.11 | loop fusion | flops 7864320 | bytes 7946240 | tf_op jit(solution)/shard_map/convert_element_type | solution.py:11
  16.5 0.8 convolution_bitcast_fusion
  17.3 1.9 %collective-permute-done.1 = f32[40]{0:T(128)S(1)} collective-permute-done((f32[40]{0:T(128)S(1)}, f32[40]{0:T(128)S(1)}, u32[]{:S(2)}, u32[]{:S(2)}) %collective-permute-start.1) | collective-permute-done | bytes 192 | tf_op jit(solution)/shard_map/ppermute | solution.py:35
  19.2 4.4 %copy.124 = bf16[2,512,1280]{1,2,0:T(8,128)(2,1)} copy(bf16[2,512,1280]{2,1,0:T(8,128)(2,1)} %param.12) | data formatting | bytes 5242880 | tf_op jit(solution)/shard_map/optimization_barrier | solution.py:34
  23.6 1.3 %collective-permute-start.9 = (f32[40]{0:T(128)S(1)}, f32[40]{0:T(128)S(1)}, u32[]{:S(2)}, u32[]{:S(2)}) collective-permute-start(f32[40]{0:T(128)S(1)} %add.126), channel_id=1, source_target_pairs={{4,0},{5,1},{6,2},{7,3},{8,4},{9,5},{10,6},{11,7},{12,8},{13,9},{1... | collective-permute-start | bytes 488 | tf_op jit(solution)/shard_map/ppermute | solution.py:35
  25.0 3.0 %collective-permute-start.2 = (f32[4,20,8,128]{3,2,1,0:T(8,128)S(1)}, f32[4,20,8,128]{3,2,1,0:T(8,128)S(1)}, u32[]{:S(2)}, u32[]{:S(2)}) collective-permute-start(f32[4,20,8,128]{3,2,1,0:T(8,128)S(1)} %dynamic-slice_bitcast_fusion.2), channel_id=1, source_target_pairs={{0,2},{2,0},{4,6},{6,4},{8,10},{10,8},{12,14},{14,12},{1,3},{3,1},... | collective-permute-start | bytes 983048 | tf_op jit(solution)/shard_map/ppermute | solution.py:65
  28.0 3.0 %fusion.7 = (bf16[2,512,20,64]{1,3,2,0:T(8,128)(2,1)S(1)}, bf16[2,512,20,64]{1,3,2,0:T(8,128)(2,1)S(1)}) fusion(bf16[2,512,20,64]{1,3,2,0:T(8,128)(2,1)} %bitcast.123, f32[2,512,20]{1,2,0:T(8,128)} %get-tuple-element.43), kind=kLoop, calls=%fused_computation.12 | loop fusion | flops 7864320 | bytes 7946240 | tf_op jit(solution)/shard_map/convert_element_type | solution.py:11
  31.0 0.4 fusion.39
  31.5 1.3 %collective-permute-start.10 = (f32[40]{0:T(128)S(1)}, f32[40]{0:T(128)S(1)}, u32[]{:S(2)}, u32[]{:S(2)}) collective-permute-start(f32[40]{0:T(128)S(1)} %add.136), channel_id=1, source_target_pairs={{8,0},{9,1},{10,2},{11,3},{12,4},{13,5},{14,6},{15,7},{24,16},{25,... | collective-permute-start | bytes 488 | tf_op jit(solution)/shard_map/ppermute | solution.py:35
  32.8 1.6 %fusion.40 = f32[2,512,512]{2,1,0:T(8,128)S(1)} fusion(bf16[2,512,1280]{1,2,0:T(8,128)(2,1)S(1)} %bitcast.118, bf16[2,512,1280]{1,2,0:T(8,128)(2,1)S(1)} %bitcast.125), kind=kOutput, calls=%fused_computation.86 | convolution fusion | flops 1342177280 | bytes 7340032 | tf_op jit(solution)/shard_map/ctk,csk->cts/dot_general | solution.py:179
  34.4 0.1 copy-done.4
  34.6 6.7 %fusion.16 = bf16[2,20,64,512]{3,2,1,0:T(8,128)(2,1)} fusion(bf16[2,512,20,64]{1,3,2,0:T(8,128)(2,1)S(1)} %bitcast.122, f32[2,20,512]{2,1,0:T(8,128)S(1)} %bitcast.148, f32[2,20,512]{2,1,0:T(8,128)S(1)} %bitcast.149, f32[2,512,512]{2,1,0:T(8,128)S(1)} %fusion.39, pred[512,512]{1,0:T(8,128)(4,1)S(1)} %copy-done.6), kind=kOutput, calls=%fused_computation.29 | convolution fusion | flops 1385431040 | bytes 7766016 | tf_op jit(solution)/shard_map/chts,cthp->cshp/dot_general | solution.py:200
  41.3 1.6 %fusion.41 = f32[2,512,512]{2,1,0:T(8,128)S(1)} fusion(bf16[2,512,1280]{1,2,0:T(8,128)(2,1)S(1)} %bitcast.119, bf16[2,512,1280]{1,2,0:T(8,128)(2,1)S(1)} %bitcast.129), kind=kOutput, calls=%fused_computation.87 | convolution fusion | flops 1342177280 | bytes 7340032 | tf_op jit(solution)/shard_map/ctk,csk->cts/dot_general | solution.py:179
  42.9 0.3 add_exponential_fusion
  43.2 1.0 fusion.9
  44.5 3.0 %collective-permute-start.3 = (f32[2,20,8,128]{3,2,1,0:T(8,128)S(1)}, f32[2,20,8,128]{3,2,1,0:T(8,128)S(1)}, u32[]{:S(2)}, u32[]{:S(2)}) collective-permute-start(f32[2,20,8,128]{3,2,1,0:T(8,128)S(1)} %dynamic-slice_bitcast_fusion.4), channel_id=1, source_target_pairs={{0,4},{2,6},{4,0},{6,2},{8,12},{10,14},{12,8},{14,10},{1,5},{3,7},... | collective-permute-start | bytes 491528 | tf_op jit(solution)/shard_map/ppermute | solution.py:65
  47.6 1.8 %add_select_fusion = f32[2,512,512]{2,1,0:T(8,128)S(1)} fusion(f32[2,512,512]{2,1,0:T(8,128)S(1)} %fusion.40, f32[2,512,512]{2,1,0:T(8,128)S(1)} %fusion.41, bf16[2,512,1280]{1,2,0:T(8,128)(2,1)S(1)} %bitcast.124, bf16[2,512,1280]{1,2,0:T(8,128)(2,1)S(1)} %bitcast.126, pred[512,512]{1,0:T(8,128)(4,1)S(1)} %copy-done.6), kind=kOutput, calls=%fused_computation.28 | convolution fusion | flops 1343750144 | bytes 11796480 | tf_op jit(solution)/shard_map/ctk,csk->cts/dot_general | solution.py:179
  49.3 3.1 %collective-permute-done.3 = f32[2,20,8,128]{3,2,1,0:T(8,128)S(1)} collective-permute-done((f32[2,20,8,128]{3,2,1,0:T(8,128)S(1)}, f32[2,20,8,128]{3,2,1,0:T(8,128)S(1)}, u32[]{:S(2)}, u32[]{:S(2)}) %collective-permute-start.3) | collective-permute-done | bytes 163872 | tf_op jit(solution)/shard_map/ppermute | solution.py:65
  52.5 3.6 %collective-permute-start.4 = (f32[1,20,8,128]{3,2,1,0:T(8,128)S(1)}, f32[1,20,8,128]{3,2,1,0:T(8,128)S(1)}, u32[]{:S(2)}, u32[]{:S(2)}) collective-permute-start(f32[1,20,8,128]{3,2,1,0:T(8,128)S(1)} %constant_dynamic-slice_fusion.3), channel_id=1, source_target_pairs={{0,8},{2,10},{4,12},{6,14},{8,0},{10,2},{12,4},{14,6},{1,9},{3,11}... | collective-permute-start | bytes 245768 | tf_op jit(solution)/shard_map/ppermute | solution.py:65
  56.1 0.1 bitcast_add_fusion
  56.2 0.6 collective-permute-start.12
  56.9 0.3 fusion.22
  57.2 3.1 %collective-permute-done.4 = f32[1,20,8,128]{3,2,1,0:T(8,128)S(1)} collective-permute-done((f32[1,20,8,128]{3,2,1,0:T(8,128)S(1)}, f32[1,20,8,128]{3,2,1,0:T(8,128)S(1)}, u32[]{:S(2)}, u32[]{:S(2)}) %collective-permute-start.4) | collective-permute-done | bytes 81952 | tf_op jit(solution)/shard_map/ppermute | solution.py:65
  60.3 1.1 %collective-permute-start.5 = (bf16[1,20,8,128]{3,2,1,0:T(8,128)(2,1)S(1)}, bf16[1,20,8,128]{3,2,1,0:T(8,128)(2,1)S(1)}, u32[]{:S(2)}, u32[]{:S(2)}) collective-permute-start(bf16[1,20,8,128]{3,2,1,0:T(8,128)(2,1)S(1)} %add_convert_fusion.1), channel_id=1, source_target_pairs={{0,8},{2,10},{4,12},{6,14},{8,0},{10,2},{12,4},{14,6},{1,9},{3,11}... | collective-permute-start | bytes 122888 | tf_op jit(solution)/shard_map/ppermute | solution.py:76
  61.5 4.1 %collective-permute-done.12 = f32[4,20,8,128]{3,2,1,0:T(8,128)S(1)} collective-permute-done((f32[4,20,8,128]{3,2,1,0:T(8,128)S(1)}, f32[4,20,8,128]{3,2,1,0:T(8,128)S(1)}, u32[]{:S(2)}, u32[]{:S(2)}) %collective-permute-start.12) | collective-permute-done | bytes 327712 | tf_op jit(solution)/shard_map/ppermute | solution.py:65
  65.6 1.6 %collective-permute-start.13 = (f32[2,20,8,128]{3,2,1,0:T(8,128)S(1)}, f32[2,20,8,128]{3,2,1,0:T(8,128)S(1)}, u32[]{:S(2)}, u32[]{:S(2)}) collective-permute-start(f32[2,20,8,128]{3,2,1,0:T(8,128)S(1)} %dynamic-slice_bitcast_fusion.3), channel_id=1, source_target_pairs={{0,4},{2,6},{4,0},{6,2},{8,12},{10,14},{12,8},{14,10},{1,5},{3,7},... | collective-permute-start | bytes 491528 | tf_op jit(solution)/shard_map/ppermute | solution.py:65
  67.2 1.2 %convolution_add_fusion.1 = f32[2,512,128]{1,2,0:T(8,128)} fusion(f32[2,512,128]{1,2,0:T(8,128)S(1)} %fusion.22, bf16[2,512,128]{2,1,0:T(8,128)(2,1)S(1)} %copy-done, f32[2,512,512]{2,1,0:T(8,128)S(1)} %add_select_fusion), kind=kOutput, calls=%fused_computation.33 | convolution fusion | flops 135921664 | bytes 3407872 | tf_op jit(solution)/shard_map/cts,ctn->csn/dot_general | solution.py:189
  68.4 0.6 collective-permute-start.6
  69.0 2.9 %collective-permute-done.13 = f32[2,20,8,128]{3,2,1,0:T(8,128)S(1)} collective-permute-done((f32[2,20,8,128]{3,2,1,0:T(8,128)S(1)}, f32[2,20,8,128]{3,2,1,0:T(8,128)S(1)}, u32[]{:S(2)}, u32[]{:S(2)}) %collective-permute-start.13) | collective-permute-done | bytes 163872 | tf_op jit(solution)/shard_map/ppermute | solution.py:65
  71.9 0.4 collective-permute-start.14
  72.3 1.5 %collective-permute-done.6 = bf16[2,20,8,128]{3,2,1,0:T(8,128)(2,1)S(1)} collective-permute-done((bf16[2,20,8,128]{3,2,1,0:T(8,128)(2,1)S(1)}, bf16[2,20,8,128]{3,2,1,0:T(8,128)(2,1)S(1)}, u32[]{:S(2)}, u32[]{:S(2)}) %collective-permute-start.6) | collective-permute-done | bytes 81952 | tf_op jit(solution)/shard_map/ppermute | solution.py:76
  73.8 0.6 collective-permute-start.7
  74.4 3.0 %collective-permute-done.14 = f32[1,20,8,128]{3,2,1,0:T(8,128)S(1)} collective-permute-done((f32[1,20,8,128]{3,2,1,0:T(8,128)S(1)}, f32[1,20,8,128]{3,2,1,0:T(8,128)S(1)}, u32[]{:S(2)}, u32[]{:S(2)}) %collective-permute-start.14) | collective-permute-done | bytes 81952 | tf_op jit(solution)/shard_map/ppermute | solution.py:65
  77.4 0.4 collective-permute-start.15
  77.8 0.5 fusion.21
  78.3 4.4 %copy.149 = bf16[2,512,1280]{2,1,0:T(8,128)(2,1)} copy(bf16[2,512,1280]{1,2,0:T(8,128)(2,1)} %bitcast.128) | data formatting | bytes 5242880
  82.7 3.2 %collective-permute-start.16 = (bf16[2,20,8,128]{3,2,1,0:T(8,128)(2,1)S(1)}, bf16[2,20,8,128]{3,2,1,0:T(8,128)(2,1)S(1)}, u32[]{:S(2)}, u32[]{:S(2)}) collective-permute-start(bf16[2,20,8,128]{3,2,1,0:T(8,128)(2,1)S(1)} %maximum_select_fusion.8), channel_id=1, source_target_pairs={{0,4},{2,6},{4,0},{6,2},{8,12},{10,14},{12,8},{14,10},{1,5},{3,7},... | collective-permute-start | bytes 245768 | tf_op jit(solution)/shard_map/ppermute | solution.py:76
  86.0 2.3 %collective-permute-done.16 = bf16[2,20,8,128]{3,2,1,0:T(8,128)(2,1)S(1)} collective-permute-done((bf16[2,20,8,128]{3,2,1,0:T(8,128)(2,1)S(1)}, bf16[2,20,8,128]{3,2,1,0:T(8,128)(2,1)S(1)}, u32[]{:S(2)}, u32[]{:S(2)}) %collective-permute-start.16) | collective-permute-done | bytes 81952 | tf_op jit(solution)/shard_map/ppermute | solution.py:76
  88.3 0.6 collective-permute-start.17
  89.0 0.1 copy_bitcast_fusion
  89.2 4.6 %collective-permute-done.17 = bf16[4,20,8,128]{3,2,1,0:T(8,128)(2,1)S(1)} collective-permute-done((bf16[4,20,8,128]{3,2,1,0:T(8,128)(2,1)S(1)}, bf16[4,20,8,128]{3,2,1,0:T(8,128)(2,1)S(1)}, u32[]{:S(2)}, u32[]{:S(2)}) %collective-permute-start.17) | collective-permute-done | bytes 163872 | tf_op jit(solution)/shard_map/ppermute | solution.py:76
  93.8 0.1 copy.142
  93.9 0.6 fusion.42
  94.5 0.5 fusion.18
  95.0 0.5 copy-done.8
  95.6 0.7 reshape.169
  96.3 0.9 constant_dynamic-slice_fusion.1
  97.2 1.0 copy.146
  98.2 2.5 %fusion.8 = f32[256,128]{0,1:T(8,128)S(1)} fusion(f32[256,40]{0,1:T(8,128)S(1)} %copy-done.19, bf16[256,40,64]{0,2,1:T(8,128)(2,1)} %bitcast.139, bf16[20,64,128]{2,1,0:T(8,128)(2,1)} %collective-permute-done.8, bf16[20,64,128]{2,1,0:T(8,128)(2,1)S(1)} %copy_bitcast_fusion, pred[]{:T(512)S(6)} %eq.28), kind=kOutput, calls=%fused_computation.15 | convolution fusion | flops 171343872 | bytes 2138113 | tf_op jit(solution)/shard_map/jhp,hpn->jhn/dot_general | solution.py:222
  100.7 0.8 copy.148
  101.5 1.6 %fusion.17 = bf16[40,64,256]{2,1,0:T(8,128)(2,1)S(1)} fusion(f32[256,128]{0,1:T(8,128)S(1)} %copy-done.11, f32[256,40]{0,1:T(8,128)S(1)} %copy-done.19, bf16[20,64,128]{2,1,0:T(8,128)(2,1)} %collective-permute-done.8, bf16[20,64,128]{2,1,0:T(8,128)(2,1)S(1)} %copy_bitcast_fusion, pred[]{:T(512)S(6)} %eq.28), kind=kOutput, calls=%fused_computation.30 | convolution fusion | flops 172032000 | bytes 2138113 | tf_op jit(solution)/shard_map/jhn,hpn->jhp/dot_general | solution.py:218
  103.1 1.6 %copy.147 = bf16[256,2560]{1,0:T(8,128)(2,1)} copy(bf16[256,2560]{0,1:T(8,128)(2,1)S(1)} %bitcast.143) | data formatting | bytes 2621440
  104.6 0.3 copy.145
  105.1 0.8 fusion.34
  (82 shorter events, 1.1 us)
Async XLA Ops:
  0.6 15.8 %copy-start = (bf16[2,512,128]{2,1,0:T(8,128)(2,1)S(1)}, bf16[2,512,128]{2,1,0:T(8,128)(2,1)}, u32[]{:S(2)}) copy-start(bf16[2,512,128]{2,1,0:T(8,128)(2,1)} %param.14) | copy-start | bytes 786436
  0.6 7.7 %copy-start.15 = (bf16[256,128]{1,0:T(8,128)(2,1)S(1)}, bf16[256,128]{1,0:T(8,128)(2,1)}, u32[]{:S(2)}) copy-start(bf16[256,128]{1,0:T(8,128)(2,1)} %param.10) | copy-start | bytes 196612
  1.6 7.5 %collective-permute-start = (f32[40]{0:T(128)S(1)}, f32[40]{0:T(128)S(1)}, u32[]{:S(2)}, u32[]{:S(2)}) collective-permute-start(f32[40]{0:T(128)S(1)} %fusion.28), channel_id=1, source_target_pairs={{1,0},{2,1},{3,2},{4,3},{5,4},{6,5},{7,6},{8,7},{9,8},{10,9},{11,1... | collective-permute-start | bytes 488 | tf_op jit(solution)/shard_map/ppermute | solution.py:35
  5.8 7.8 %copy-start.13 = (f32[2,512,20]{1,2,0:T(8,128)}, f32[2,512,20]{1,2,0:T(8,128)S(1)}, u32[]{:S(2)}) copy-start(f32[2,512,20]{1,2,0:T(8,128)S(1)} %get-tuple-element.36) | copy-start | bytes 245764
  9.1 3.0 %copy-start.17 = (s32[2]{0:T(128)S(1)}, s32[2]{0:T(128)}, u32[]{:S(2)}) copy-start(s32[2]{0:T(128)} %param.16) | copy-start | bytes 28
  12.2 7.0 %collective-permute-start.1 = (f32[40]{0:T(128)S(1)}, f32[40]{0:T(128)S(1)}, u32[]{:S(2)}, u32[]{:S(2)}) collective-permute-start(f32[40]{0:T(128)S(1)} %add.125), channel_id=1, source_target_pairs={{2,0},{3,1},{4,2},{5,3},{6,4},{7,5},{8,6},{9,7},{10,8},{11,9},{12,... | collective-permute-start | bytes 488 | tf_op jit(solution)/shard_map/ppermute | solution.py:35
  13.7 2.8 %copy-start.3 = (bf16[2,512,1280]{1,2,0:T(8,128)(2,1)}, bf16[2,512,1280]{1,2,0:T(8,128)(2,1)S(1)}, u32[]{:S(2)}) copy-start(bf16[2,512,1280]{1,2,0:T(8,128)(2,1)S(1)} %broadcast_select_fusion) | copy-start | bytes 7864324
  16.5 24.8 %copy-start.1 = (bf16[2,512,20,64]{1,3,2,0:T(8,128)(2,1)}, bf16[2,512,20,64]{1,3,2,0:T(8,128)(2,1)S(1)}, u32[]{:S(2)}) copy-start(bf16[2,512,20,64]{1,3,2,0:T(8,128)(2,1)S(1)} %get-tuple-element.49) | copy-start | bytes 7864324
  23.6 7.8 %collective-permute-start.9 = (f32[40]{0:T(128)S(1)}, f32[40]{0:T(128)S(1)}, u32[]{:S(2)}, u32[]{:S(2)}) collective-permute-start(f32[40]{0:T(128)S(1)} %add.126), channel_id=1, source_target_pairs={{4,0},{5,1},{6,2},{7,3},{8,4},{9,5},{10,6},{11,7},{12,8},{13,9},{1... | collective-permute-start | bytes 488 | tf_op jit(solution)/shard_map/ppermute | solution.py:35
  25.0 19.4 %collective-permute-start.2 = (f32[4,20,8,128]{3,2,1,0:T(8,128)S(1)}, f32[4,20,8,128]{3,2,1,0:T(8,128)S(1)}, u32[]{:S(2)}, u32[]{:S(2)}) collective-permute-start(f32[4,20,8,128]{3,2,1,0:T(8,128)S(1)} %dynamic-slice_bitcast_fusion.2), channel_id=1, source_target_pairs={{0,2},{2,0},{4,6},{6,4},{8,10},{10,8},{12,14},{14,12},{1,3},{3,1},... | collective-permute-start | bytes 983048 | tf_op jit(solution)/shard_map/ppermute | solution.py:65
  28.0 3.0 %copy-start.7 = (bf16[2,512,128]{2,1,0:T(8,128)(2,1)S(1)}, bf16[2,512,128]{2,1,0:T(8,128)(2,1)}, u32[]{:S(2)}) copy-start(bf16[2,512,128]{2,1,0:T(8,128)(2,1)} %param.13) | copy-start | bytes 786436
  31.5 11.4 %collective-permute-start.10 = (f32[40]{0:T(128)S(1)}, f32[40]{0:T(128)S(1)}, u32[]{:S(2)}, u32[]{:S(2)}) collective-permute-start(f32[40]{0:T(128)S(1)} %add.136), channel_id=1, source_target_pairs={{8,0},{9,1},{10,2},{11,3},{12,4},{13,5},{14,6},{15,7},{24,16},{25,... | collective-permute-start | bytes 488 | tf_op jit(solution)/shard_map/ppermute | solution.py:35
  32.8 1.7 %copy-start.4 = (bf16[2,512,1280]{1,2,0:T(8,128)(2,1)S(1)}, bf16[2,512,1280]{1,2,0:T(8,128)(2,1)}, u32[]{:S(2)}) copy-start(bf16[2,512,1280]{1,2,0:T(8,128)(2,1)} %copy-done.3) | copy-start | bytes 7864324
  32.8 1.7 %copy-start.6 = (pred[512,512]{1,0:T(8,128)(4,1)S(1)}, pred[512,512]{1,0:T(8,128)(4,1)}, u32[]{:S(2)}) copy-start(pred[512,512]{1,0:T(8,128)(4,1)} %iota_compare_fusion) | copy-start | bytes 786436
  32.8 1.7 %copy-start.12 = (f32[2,512,20]{1,2,0:T(8,128)S(1)}, f32[2,512,20]{1,2,0:T(8,128)}, u32[]{:S(2)}) copy-start(f32[2,512,20]{1,2,0:T(8,128)} %get-tuple-element.43) | copy-start | bytes 245764
  32.8 1.8 %copy-start.14 = (f32[2,512,20]{1,2,0:T(8,128)S(1)}, f32[2,512,20]{1,2,0:T(8,128)}, u32[]{:S(2)}) copy-start(f32[2,512,20]{1,2,0:T(8,128)} %copy-done.13) | copy-start | bytes 245764
  41.3 1.6 %copy-start.16 = (s32[256,40]{0,1:T(8,128)S(1)}, s32[256,40]{0,1:T(8,128)}, u32[]{:S(2)}) copy-start(s32[256,40]{0,1:T(8,128)} %param.11) | copy-start | bytes 122884
  41.3 1.9 %copy-start.9 = (bf16[256,2560]{0,1:T(8,128)(2,1)S(1)}, bf16[256,2560]{0,1:T(8,128)(2,1)}, u32[]{:S(2)}) copy-start(bf16[256,2560]{0,1:T(8,128)(2,1)} %copy.127) | copy-start | bytes 3932164
  41.3 1.9 %copy-start.10 = (f32[256,128]{0,1:T(8,128)S(1)}, f32[256,128]{0,1:T(8,128)}, u32[]{:S(2)}) copy-start(f32[256,128]{0,1:T(8,128)} %copy.125) | copy-start | bytes 393220
  43.2 1.1 %copy-start.18 = (f32[256,40]{0,1:T(8,128)}, f32[256,40]{0,1:T(8,128)S(1)}, u32[]{:S(2)}) copy-start(f32[256,40]{0,1:T(8,128)S(1)} %add_exponential_fusion) | copy-start | bytes 122884
  43.2 4.3 %copy-start.5 = (bf16[2,512,20,64]{1,3,2,0:T(8,128)(2,1)S(1)}, bf16[2,512,20,64]{1,3,2,0:T(8,128)(2,1)}, u32[]{:S(2)}) copy-start(bf16[2,512,20,64]{1,3,2,0:T(8,128)(2,1)} %get-tuple-element.52) | copy-start | bytes 7864324
  44.4 11.7 %collective-permute-start.11 = (f32[20,64,128]{2,1,0:T(8,128)S(1)}, f32[20,64,128]{2,1,0:T(8,128)S(1)}, u32[]{:S(2)}, u32[]{:S(2)}) collective-permute-start(f32[20,64,128]{2,1,0:T(8,128)S(1)} %dynamic-slice_bitcast_fusion), channel_id=1, source_target_pairs={{0,1},{1,0},{2,3},{3,2},{4,5},{5,4},{6,7},{7,6},{8,9},{9,8},{10,11... | collective-permute-start | bytes 1966088 | tf_op jit(solution)/shard_map/ppermute | solution.py:100
  44.5 7.9 %collective-permute-start.3 = (f32[2,20,8,128]{3,2,1,0:T(8,128)S(1)}, f32[2,20,8,128]{3,2,1,0:T(8,128)S(1)}, u32[]{:S(2)}, u32[]{:S(2)}) collective-permute-start(f32[2,20,8,128]{3,2,1,0:T(8,128)S(1)} %dynamic-slice_bitcast_fusion.4), channel_id=1, source_target_pairs={{0,4},{2,6},{4,0},{6,2},{8,12},{10,14},{12,8},{14,10},{1,5},{3,7},... | collective-permute-start | bytes 491528 | tf_op jit(solution)/shard_map/ppermute | solution.py:65
  52.5 7.9 %collective-permute-start.4 = (f32[1,20,8,128]{3,2,1,0:T(8,128)S(1)}, f32[1,20,8,128]{3,2,1,0:T(8,128)S(1)}, u32[]{:S(2)}, u32[]{:S(2)}) collective-permute-start(f32[1,20,8,128]{3,2,1,0:T(8,128)S(1)} %constant_dynamic-slice_fusion.3), channel_id=1, source_target_pairs={{0,8},{2,10},{4,12},{6,14},{8,0},{10,2},{12,4},{14,6},{1,9},{3,11}... | collective-permute-start | bytes 245768 | tf_op jit(solution)/shard_map/ppermute | solution.py:65
  56.2 9.3 %collective-permute-start.12 = (f32[4,20,8,128]{3,2,1,0:T(8,128)S(1)}, f32[4,20,8,128]{3,2,1,0:T(8,128)S(1)}, u32[]{:S(2)}, u32[]{:S(2)}) collective-permute-start(f32[4,20,8,128]{3,2,1,0:T(8,128)S(1)} %dynamic-slice_bitcast_fusion.1), channel_id=1, source_target_pairs={{0,2},{2,0},{4,6},{6,4},{8,10},{10,8},{12,14},{14,12},{1,3},{3,1},... | collective-permute-start | bytes 983048 | tf_op jit(solution)/shard_map/ppermute | solution.py:65
  60.3 8.1 %collective-permute-start.5 = (bf16[1,20,8,128]{3,2,1,0:T(8,128)(2,1)S(1)}, bf16[1,20,8,128]{3,2,1,0:T(8,128)(2,1)S(1)}, u32[]{:S(2)}, u32[]{:S(2)}) collective-permute-start(bf16[1,20,8,128]{3,2,1,0:T(8,128)(2,1)S(1)} %add_convert_fusion.1), channel_id=1, source_target_pairs={{0,8},{2,10},{4,12},{6,14},{8,0},{10,2},{12,4},{14,6},{1,9},{3,11}... | collective-permute-start | bytes 122888 | tf_op jit(solution)/shard_map/ppermute | solution.py:76
  65.6 6.3 %collective-permute-start.13 = (f32[2,20,8,128]{3,2,1,0:T(8,128)S(1)}, f32[2,20,8,128]{3,2,1,0:T(8,128)S(1)}, u32[]{:S(2)}, u32[]{:S(2)}) collective-permute-start(f32[2,20,8,128]{3,2,1,0:T(8,128)S(1)} %dynamic-slice_bitcast_fusion.3), channel_id=1, source_target_pairs={{0,4},{2,6},{4,0},{6,2},{8,12},{10,14},{12,8},{14,10},{1,5},{3,7},... | collective-permute-start | bytes 491528 | tf_op jit(solution)/shard_map/ppermute | solution.py:65
  68.4 5.3 %collective-permute-start.6 = (bf16[2,20,8,128]{3,2,1,0:T(8,128)(2,1)S(1)}, bf16[2,20,8,128]{3,2,1,0:T(8,128)(2,1)S(1)}, u32[]{:S(2)}, u32[]{:S(2)}) collective-permute-start(bf16[2,20,8,128]{3,2,1,0:T(8,128)(2,1)S(1)} %maximum_select_fusion.7), channel_id=1, source_target_pairs={{0,4},{2,6},{4,0},{6,2},{8,12},{10,14},{12,8},{14,10},{1,5},{3,7},... | collective-permute-start | bytes 245768 | tf_op jit(solution)/shard_map/ppermute | solution.py:76
  71.9 5.4 %collective-permute-start.14 = (f32[1,20,8,128]{3,2,1,0:T(8,128)S(1)}, f32[1,20,8,128]{3,2,1,0:T(8,128)S(1)}, u32[]{:S(2)}, u32[]{:S(2)}) collective-permute-start(f32[1,20,8,128]{3,2,1,0:T(8,128)S(1)} %constant_dynamic-slice_fusion.2), channel_id=1, source_target_pairs={{0,8},{2,10},{4,12},{6,14},{8,0},{10,2},{12,4},{14,6},{1,9},{3,11}... | collective-permute-start | bytes 245768 | tf_op jit(solution)/shard_map/ppermute | solution.py:65
  73.8 12.1 %collective-permute-start.7 = (bf16[4,20,8,128]{3,2,1,0:T(8,128)(2,1)S(1)}, bf16[4,20,8,128]{3,2,1,0:T(8,128)(2,1)S(1)}, u32[]{:S(2)}, u32[]{:S(2)}) collective-permute-start(bf16[4,20,8,128]{3,2,1,0:T(8,128)(2,1)S(1)} %maximum_select_fusion.3), channel_id=1, source_target_pairs={{0,2},{2,0},{4,6},{6,4},{8,10},{10,8},{12,14},{14,12},{1,3},{3,1},... | collective-permute-start | bytes 491528 | tf_op jit(solution)/shard_map/ppermute | solution.py:76
  77.4 5.3 %collective-permute-start.15 = (bf16[1,20,8,128]{3,2,1,0:T(8,128)(2,1)S(1)}, bf16[1,20,8,128]{3,2,1,0:T(8,128)(2,1)S(1)}, u32[]{:S(2)}, u32[]{:S(2)}) collective-permute-start(bf16[1,20,8,128]{3,2,1,0:T(8,128)(2,1)S(1)} %add_convert_fusion), channel_id=1, source_target_pairs={{0,8},{2,10},{4,12},{6,14},{8,0},{10,2},{12,4},{14,6},{1,9},{3,11}... | collective-permute-start | bytes 122888 | tf_op jit(solution)/shard_map/ppermute | solution.py:76
  82.7 11.2 %copy-start.2 = (bf16[2,512,20,64]{1,3,2,0:T(8,128)(2,1)S(1)}, bf16[2,512,20,64]{1,3,2,0:T(8,128)(2,1)}, u32[]{:S(2)}) copy-start(bf16[2,512,20,64]{1,3,2,0:T(8,128)(2,1)} %copy-done.1) | copy-start | bytes 7864324
  82.7 5.6 %collective-permute-start.16 = (bf16[2,20,8,128]{3,2,1,0:T(8,128)(2,1)S(1)}, bf16[2,20,8,128]{3,2,1,0:T(8,128)(2,1)S(1)}, u32[]{:S(2)}, u32[]{:S(2)}) collective-permute-start(bf16[2,20,8,128]{3,2,1,0:T(8,128)(2,1)S(1)} %maximum_select_fusion.8), channel_id=1, source_target_pairs={{0,4},{2,6},{4,0},{6,2},{8,12},{10,14},{12,8},{14,10},{1,5},{3,7},... | collective-permute-start | bytes 245768 | tf_op jit(solution)/shard_map/ppermute | solution.py:76
  88.3 5.4 %collective-permute-start.17 = (bf16[4,20,8,128]{3,2,1,0:T(8,128)(2,1)S(1)}, bf16[4,20,8,128]{3,2,1,0:T(8,128)(2,1)S(1)}, u32[]{:S(2)}, u32[]{:S(2)}) collective-permute-start(bf16[4,20,8,128]{3,2,1,0:T(8,128)(2,1)S(1)} %maximum_select_fusion.4), channel_id=1, source_target_pairs={{0,2},{2,0},{4,6},{6,4},{8,10},{10,8},{12,14},{14,12},{1,3},{3,1},... | collective-permute-start | bytes 491528 | tf_op jit(solution)/shard_map/ppermute | solution.py:76
  89.1 9.1 %collective-permute-start.8 = (bf16[20,64,128]{2,1,0:T(8,128)(2,1)S(1)}, bf16[20,64,128]{2,1,0:T(8,128)(2,1)}, u32[]{:S(2)}, u32[]{:S(2)}) collective-permute-start(bf16[20,64,128]{2,1,0:T(8,128)(2,1)S(1)} %copy_bitcast_fusion), channel_id=1, source_target_pairs={{0,1},{1,0},{2,3},{3,2},{4,5},{5,4},{6,7},{7,6},{8,9},{9,8},{10,11... | collective-permute-start | bytes 983048 | tf_op jit(solution)/shard_map/ppermute | solution.py:100
  94.4 1.0 copy-start.8
  95.6 2.7 %copy-start.19 = (f32[256,40]{0,1:T(8,128)S(1)}, f32[256,40]{0,1:T(8,128)}, u32[]{:S(2)}) copy-start(f32[256,40]{0,1:T(8,128)} %copy-done.18) | copy-start | bytes 122884
  98.2 3.3 %copy-start.11 = (f32[256,128]{0,1:T(8,128)S(1)}, f32[256,128]{0,1:T(8,128)}, u32[]{:S(2)}) copy-start(f32[256,128]{0,1:T(8,128)} %copy.125) | copy-start | bytes 393220
  98.2 6.8 %collective-permute-start.18 = (f32[2,256,256]{2,1,0:T(8,128)}, f32[2,256,256]{2,1,0:T(8,128)S(1)}, u32[]{:S(2)}, u32[]{:S(2)}) collective-permute-start(f32[2,256,256]{2,1,0:T(8,128)} %bitcast.62), channel_id=1, source_target_pairs={{0,1},{1,0},{2,3},{3,2},{4,5},{5,4},{6,7},{7,6},{8,9},{9,8},{10,11... | collective-permute-start | bytes 1572872 | tf_op jit(solution)/shard_map/ppermute | solution.py:100

commit v19 on v18

--- a/solution.py
+++ b/solution.py
@@ -10,6 +10,16 @@
     high = lax.reduce_precision(value, exponent_bits=8, mantissa_bits=7)
     low = (value - high).astype(jnp.bfloat16)
     return high.astype(jnp.bfloat16), low
+
+
+def exact_sum_dot(ones, value, spec):
+    high = lax.reduce_precision(value, exponent_bits=8, mantissa_bits=7)
+    rest = value - high
+    mid = lax.reduce_precision(rest, exponent_bits=8, mantissa_bits=7)
+    low = rest - mid
+    total = jnp.einsum(spec, ones, high.astype(jnp.bfloat16), preferred_element_type=jnp.float32)
+    total = total + jnp.einsum(spec, ones, mid.astype(jnp.bfloat16), preferred_element_type=jnp.float32)
+    return total + jnp.einsum(spec, ones, low.astype(jnp.bfloat16), preferred_element_type=jnp.float32)
 
 
 def butterfly_sum(value, axis):
@@ -115,8 +125,8 @@
 
     def level_work(code_cand):
         rates = jnp.log1p(-code_cand.astype(jnp.float32) * 1e-06)
-        lower = (position[:, None] >= position[None, :]).astype(jnp.float32)
-        level_all = jnp.einsum("ts,csh->cth", lower, rates, precision=lax.Precision.HIGHEST)
+        lower = (position[:, None] >= position[None, :]).astype(jnp.bfloat16)
+        level_all = exact_sum_dot(lower, rates, "ts,csh->cth")
         return jnp.exp(level_all), jnp.exp(-level_all)
 
     def g_work(dy_cand, lengths, amplitude, c_cand):
@@ -148,8 +158,8 @@
     x_high, x_low, scores = x_parts
     later_total = inclusive - own_total
     token_at = jnp.arange(pre_len, dtype=jnp.int32)
-    later_rows = (token_at[None, :] > token_at[:, None]).astype(jnp.float32)
-    after_local = jnp.dot(later_rows, log_prefix, precision=lax.Precision.HIGHEST)
+    later_rows = (token_at[None, :] > token_at[:, None]).astype(jnp.bfloat16)
+    after_local = exact_sum_dot(later_rows, log_prefix, "ji,ih->jh")
     weight = jnp.exp(after_local + later_total[None, :])
     weighted_b = (weight[:, :, None] * b_prefix[:, None, :].astype(jnp.float32)).astype(
         jnp.bfloat16

time: 107 us -> 110 us (1.028)
  matrix products: 22.5 us -> 25.3 us
    dot_general x2 -> x6, matrix products: 1.41 us -> 4.21 us  [the longest x2 1.89 us: exact_sum_dot(): jnp.einsum(spec, ones, mid.astype(jnp.bfloat16), preferred_element_type=j...]
    convert_element_type x0 -> x1, other arithmetic: none -> 1.11 us  [exact_sum_dot(): low.astype(jnp.bfloat16)]
    unnamed x44 -> x46, local copies, waits for them, and re-layouts: 9.94 us -> 9.91 us
  transfers between devices with their start and end apart: 19 -> 19, of which waited for: 9 -> 9; matrix products, arithmetic and copies ran while one was open for 42% -> 43% of each run, Pallas kernels for 0% -> 0%
where the time goes in v19:
time: 110 us; the launch traced here: 109 us
  waiting for transfers between devices  26.4 us (24%)
  matrix products  25.3 us (23%)
  starting transfers between devices  24.1 us (22%)
  local copies, waits for them, and re-layouts  22.5 us (20%)
  other arithmetic  9.38 us (9%)
  between operations  1.26 us (1%)
    ppermute x6, waiting for transfers between devices, halving_scatter(): lax.ppermute(give, axis, [(at, at ^ step) for at in range(count)])  16.1 us
    ppermute x6, starting transfers between devices, halving_scatter(): lax.ppermute(give, axis, [(at, at ^ step) for at in range(count)])  12.2 us
    unnamed x46, local copies, waits for them, and re-layouts  9.91 us
    ppermute x6, waiting for transfers between devices, doubling_gather(): other = lax.ppermute(value, axis, [(at, at ^ step) for at in range(count)])  8.35 us
    optimization_barrier x2, local copies, waits for them, and re-layouts, suffix_sum(): value, args = lax.optimization_barrier((value, pick(done)))  7.5 us
    dot_general x1, matrix products, shards(): jnp.einsum('chts,cthp->cshp', kernel, g_heads, preferred_element_type=jnp...  6.7 us
    ppermute x6, starting transfers between devices, doubling_gather(): other = lax.ppermute(value, axis, [(at, at ^ step) for at in range(count)])  6.59 us
    convert_element_type x2, other arithmetic, split_bf16(): low = (value - high).astype(jnp.bfloat16)  5.75 us
  transfers between devices with their start and end apart: 19, of which 9 were waited for; matrix products, arithmetic and copies ran while one was open for 43% of the time, Pallas kernels for 0%

profile of v19, /device:TPU:0, one launch (start us, length us, event | category | flops | bytes accessed | tf_op | source)
XLA Modules:
  0.0 108.8 jit_solution(8102335493608256417)
XLA Ops:
  0.7 1.0 fusion.35
  1.6 1.3 %collective-permute-start = (f32[40]{0:T(128)S(1)}, f32[40]{0:T(128)S(1)}, u32[]{:S(2)}, u32[]{:S(2)}) collective-permute-start(f32[40]{0:T(128)S(1)} %fusion.35), channel_id=1, source_target_pairs={{1,0},{2,1},{3,2},{4,3},{5,4},{6,5},{7,6},{8,7},{9,8},{10,9},{11,1... | collective-permute-start | bytes 488 | tf_op jit(solution)/shard_map/ppermute | solution.py:45
  2.9 0.8 iota_compare_fusion
  3.7 1.0 fusion.28
  4.7 1.1 %fusion.29 = (bf16[2,512,20]{1,0,2:T(2,128)(2,1)S(1)}, bf16[2,512,20]{1,0,2:T(2,128)(2,1)S(1)}, bf16[2,512,20]{1,0,2:T(2,128)(2,1)S(1)}) fusion(s32[2,512,20]{1,0,2:T(2,128)} %param.15), kind=kLoop, calls=%fused_computation.73 | loop fusion | flops 204800 | bytes 204800 | tf_op jit(solution)/shard_map/convert_element_type | solution.py:22
  5.8 0.2 fusion.21
  6.0 1.6 %convolution_add_fusion.5 = f32[256,40]{0,1:T(8,128)} fusion(f32[256,40]{0,1:T(8,128)S(1)} %fusion.28, s32[256,40]{0,1:T(8,128)} %param.11), kind=kOutput, calls=%fused_computation.38 | convolution fusion | flops 5390336 | bytes 122880 | tf_op jit(solution)/shard_map/ji,ih->jh/dot_general | solution.py:21
  7.6 2.4 %copy.137 = bf16[256,2560]{0,1:T(8,128)(2,1)} copy(bf16[256,2560]{1,0:T(8,128)(2,1)} %param.9) | data formatting | bytes 2621440 | tf_op args[0]
  10.0 0.8 copy.135
  10.8 0.3 convolution_add_fusion.3
  11.1 0.9 exponential_bitcast_fusion
  12.0 3.0 %copy.129 = bf16[2,512,1280]{1,2,0:T(8,128)(2,1)S(1)} copy(bf16[2,512,1280]{2,1,0:T(8,128)(2,1)} %param.17) | data formatting | bytes 5242880 | tf_op jit(solution)/shard_map/optimization_barrier | solution.py:44
  15.2 1.3 %collective-permute-start.1 = (f32[40]{0:T(128)S(1)}, f32[40]{0:T(128)S(1)}, u32[]{:S(2)}, u32[]{:S(2)}) collective-permute-start(f32[40]{0:T(128)S(1)} %add.139), channel_id=1, source_target_pairs={{2,0},{3,1},{4,2},{5,3},{6,4},{7,5},{8,6},{9,7},{10,8},{11,9},{12,... | collective-permute-start | bytes 488 | tf_op jit(solution)/shard_map/ppermute | solution.py:45
  16.5 0.2 broadcast_select_fusion
  16.7 2.8 %fusion.6 = (bf16[2,512,20,64]{1,3,2,0:T(8,128)(2,1)}, bf16[2,512,20,64]{1,3,2,0:T(8,128)(2,1)S(1)}) fusion(bf16[2,512,20,64]{1,3,2,0:T(8,128)(2,1)S(1)} %bitcast.125, f32[2,512,20]{1,2,0:T(8,128)S(1)} %get-tuple-element.36), kind=kLoop, calls=%fused_computation.11 | loop fusion | flops 7864320 | bytes 7946240 | tf_op jit(solution)/shard_map/convert_element_type | solution.py:11
  19.4 0.8 convolution_bitcast_fusion
  20.3 1.9 %collective-permute-done.1 = f32[40]{0:T(128)S(1)} collective-permute-done((f32[40]{0:T(128)S(1)}, f32[40]{0:T(128)S(1)}, u32[]{:S(2)}, u32[]{:S(2)}) %collective-permute-start.1) | collective-permute-done | bytes 192 | tf_op jit(solution)/shard_map/ppermute | solution.py:45
  22.2 4.5 %copy.134 = bf16[2,512,1280]{1,2,0:T(8,128)(2,1)} copy(bf16[2,512,1280]{2,1,0:T(8,128)(2,1)} %param.12) | data formatting | bytes 5242880 | tf_op jit(solution)/shard_map/optimization_barrier | solution.py:44
  26.6 1.3 %collective-permute-start.9 = (f32[40]{0:T(128)S(1)}, f32[40]{0:T(128)S(1)}, u32[]{:S(2)}, u32[]{:S(2)}) collective-permute-start(f32[40]{0:T(128)S(1)} %add.142), channel_id=1, source_target_pairs={{4,0},{5,1},{6,2},{7,3},{8,4},{9,5},{10,6},{11,7},{12,8},{13,9},{1... | collective-permute-start | bytes 488 | tf_op jit(solution)/shard_map/ppermute | solution.py:45
  28.0 3.0 %collective-permute-start.2 = (f32[4,20,8,128]{3,2,1,0:T(8,128)S(1)}, f32[4,20,8,128]{3,2,1,0:T(8,128)S(1)}, u32[]{:S(2)}, u32[]{:S(2)}) collective-permute-start(f32[4,20,8,128]{3,2,1,0:T(8,128)S(1)} %dynamic-slice_bitcast_fusion.2), channel_id=1, source_target_pairs={{0,2},{2,0},{4,6},{6,4},{8,10},{10,8},{12,14},{14,12},{1,3},{3,1},... | collective-permute-start | bytes 983048 | tf_op jit(solution)/shard_map/ppermute | solution.py:75
  31.0 3.0 %fusion.7 = (bf16[2,512,20,64]{1,3,2,0:T(8,128)(2,1)S(1)}, bf16[2,512,20,64]{1,3,2,0:T(8,128)(2,1)S(1)}) fusion(bf16[2,512,20,64]{1,3,2,0:T(8,128)(2,1)} %bitcast.127, f32[2,512,20]{1,2,0:T(8,128)} %get-tuple-element.43), kind=kLoop, calls=%fused_computation.12 | loop fusion | flops 7864320 | bytes 7946240 | tf_op jit(solution)/shard_map/convert_element_type | solution.py:11
  34.0 0.4 fusion.49
  34.5 1.3 %collective-permute-start.10 = (f32[40]{0:T(128)S(1)}, f32[40]{0:T(128)S(1)}, u32[]{:S(2)}, u32[]{:S(2)}) collective-permute-start(f32[40]{0:T(128)S(1)} %add.154), channel_id=1, source_target_pairs={{8,0},{9,1},{10,2},{11,3},{12,4},{13,5},{14,6},{15,7},{24,16},{25,... | collective-permute-start | bytes 488 | tf_op jit(solution)/shard_map/ppermute | solution.py:45
  35.8 1.6 %fusion.50 = f32[2,512,512]{2,1,0:T(8,128)S(1)} fusion(bf16[2,512,1280]{1,2,0:T(8,128)(2,1)S(1)} %bitcast.122, bf16[2,512,1280]{1,2,0:T(8,128)(2,1)S(1)} %bitcast.129), kind=kOutput, calls=%fused_computation.105 | convolution fusion | flops 1342177280 | bytes 7340032 | tf_op jit(solution)/shard_map/ctk,csk->cts/dot_general | solution.py:189
  37.6 6.7 %fusion.16 = bf16[2,20,64,512]{3,2,1,0:T(8,128)(2,1)} fusion(bf16[2,512,20,64]{1,3,2,0:T(8,128)(2,1)S(1)} %bitcast.126, f32[2,20,512]{2,1,0:T(8,128)S(1)} %bitcast.152, f32[2,20,512]{2,1,0:T(8,128)S(1)} %bitcast.153, f32[2,512,512]{2,1,0:T(8,128)S(1)} %fusion.49, pred[512,512]{1,0:T(8,128)(4,1)S(1)} %copy-done.6), kind=kOutput, calls=%fused_computation.29 | convolution fusion | flops 1385431040 | bytes 7766016 | tf_op jit(solution)/shard_map/chts,cthp->cshp/dot_general | solution.py:210
  44.3 1.6 %fusion.51 = f32[2,512,512]{2,1,0:T(8,128)S(1)} fusion(bf16[2,512,1280]{1,2,0:T(8,128)(2,1)S(1)} %bitcast.123, bf16[2,512,1280]{1,2,0:T(8,128)(2,1)S(1)} %bitcast.133), kind=kOutput, calls=%fused_computation.106 | convolution fusion | flops 1342177280 | bytes 7340032 | tf_op jit(solution)/shard_map/ctk,csk->cts/dot_general | solution.py:189
  45.9 0.2 add_exponential_fusion
  46.2 1.0 fusion.9
  47.5 3.0 %collective-permute-start.3 = (f32[2,20,8,128]{3,2,1,0:T(8,128)S(1)}, f32[2,20,8,128]{3,2,1,0:T(8,128)S(1)}, u32[]{:S(2)}, u32[]{:S(2)}) collective-permute-start(f32[2,20,8,128]{3,2,1,0:T(8,128)S(1)} %dynamic-slice_bitcast_fusion.4), channel_id=1, source_target_pairs={{0,4},{2,6},{4,0},{6,2},{8,12},{10,14},{12,8},{14,10},{1,5},{3,7},... | collective-permute-start | bytes 491528 | tf_op jit(solution)/shard_map/ppermute | solution.py:75
  50.5 1.8 %add_select_fusion = f32[2,512,512]{2,1,0:T(8,128)S(1)} fusion(f32[2,512,512]{2,1,0:T(8,128)S(1)} %fusion.50, f32[2,512,512]{2,1,0:T(8,128)S(1)} %fusion.51, bf16[2,512,1280]{1,2,0:T(8,128)(2,1)S(1)} %bitcast.128, bf16[2,512,1280]{1,2,0:T(8,128)(2,1)S(1)} %bitcast.130, pred[512,512]{1,0:T(8,128)(4,1)S(1)} %copy-done.6), kind=kOutput, calls=%fused_computation.28 | convolution fusion | flops 1343750144 | bytes 11796480 | tf_op jit(solution)/shard_map/ctk,csk->cts/dot_general | solution.py:189
  52.3 3.1 %collective-permute-done.3 = f32[2,20,8,128]{3,2,1,0:T(8,128)S(1)} collective-permute-done((f32[2,20,8,128]{3,2,1,0:T(8,128)S(1)}, f32[2,20,8,128]{3,2,1,0:T(8,128)S(1)}, u32[]{:S(2)}, u32[]{:S(2)}) %collective-permute-start.3) | collective-permute-done | bytes 163872 | tf_op jit(solution)/shard_map/ppermute | solution.py:75
  55.4 3.6 %collective-permute-start.4 = (f32[1,20,8,128]{3,2,1,0:T(8,128)S(1)}, f32[1,20,8,128]{3,2,1,0:T(8,128)S(1)}, u32[]{:S(2)}, u32[]{:S(2)}) collective-permute-start(f32[1,20,8,128]{3,2,1,0:T(8,128)S(1)} %constant_dynamic-slice_fusion.3), channel_id=1, source_target_pairs={{0,8},{2,10},{4,12},{6,14},{8,0},{10,2},{12,4},{14,6},{1,9},{3,11}... | collective-permute-start | bytes 245768 | tf_op jit(solution)/shard_map/ppermute | solution.py:75
  59.2 0.6 collective-permute-start.12
  59.8 0.3 fusion.24
  60.2 3.1 %collective-permute-done.4 = f32[1,20,8,128]{3,2,1,0:T(8,128)S(1)} collective-permute-done((f32[1,20,8,128]{3,2,1,0:T(8,128)S(1)}, f32[1,20,8,128]{3,2,1,0:T(8,128)S(1)}, u32[]{:S(2)}, u32[]{:S(2)}) %collective-permute-start.4) | collective-permute-done | bytes 81952 | tf_op jit(solution)/shard_map/ppermute | solution.py:75
  63.3 1.1 %collective-permute-start.5 = (bf16[1,20,8,128]{3,2,1,0:T(8,128)(2,1)S(1)}, bf16[1,20,8,128]{3,2,1,0:T(8,128)(2,1)S(1)}, u32[]{:S(2)}, u32[]{:S(2)}) collective-permute-start(bf16[1,20,8,128]{3,2,1,0:T(8,128)(2,1)S(1)} %add_convert_fusion.1), channel_id=1, source_target_pairs={{0,8},{2,10},{4,12},{6,14},{8,0},{10,2},{12,4},{14,6},{1,9},{3,11}... | collective-permute-start | bytes 122888 | tf_op jit(solution)/shard_map/ppermute | solution.py:86
  64.4 4.1 %collective-permute-done.12 = f32[4,20,8,128]{3,2,1,0:T(8,128)S(1)} collective-permute-done((f32[4,20,8,128]{3,2,1,0:T(8,128)S(1)}, f32[4,20,8,128]{3,2,1,0:T(8,128)S(1)}, u32[]{:S(2)}, u32[]{:S(2)}) %collective-permute-start.12) | collective-permute-done | bytes 327712 | tf_op jit(solution)/shard_map/ppermute | solution.py:75
  68.6 1.6 %collective-permute-start.13 = (f32[2,20,8,128]{3,2,1,0:T(8,128)S(1)}, f32[2,20,8,128]{3,2,1,0:T(8,128)S(1)}, u32[]{:S(2)}, u32[]{:S(2)}) collective-permute-start(f32[2,20,8,128]{3,2,1,0:T(8,128)S(1)} %dynamic-slice_bitcast_fusion.3), channel_id=1, source_target_pairs={{0,4},{2,6},{4,0},{6,2},{8,12},{10,14},{12,8},{14,10},{1,5},{3,7},... | collective-permute-start | bytes 491528 | tf_op jit(solution)/shard_map/ppermute | solution.py:75
  70.2 1.2 %convolution_add_fusion.1 = f32[2,512,128]{1,2,0:T(8,128)} fusion(f32[2,512,128]{1,2,0:T(8,128)S(1)} %fusion.24, bf16[2,512,128]{2,1,0:T(8,128)(2,1)S(1)} %copy-done, f32[2,512,512]{2,1,0:T(8,128)S(1)} %add_select_fusion), kind=kOutput, calls=%fused_computation.33 | convolution fusion | flops 135921664 | bytes 3407872 | tf_op jit(solution)/shard_map/cts,ctn->csn/dot_general | solution.py:199
  71.3 0.6 collective-permute-start.6
  71.9 2.9 %collective-permute-done.13 = f32[2,20,8,128]{3,2,1,0:T(8,128)S(1)} collective-permute-done((f32[2,20,8,128]{3,2,1,0:T(8,128)S(1)}, f32[2,20,8,128]{3,2,1,0:T(8,128)S(1)}, u32[]{:S(2)}, u32[]{:S(2)}) %collective-permute-start.13) | collective-permute-done | bytes 163872 | tf_op jit(solution)/shard_map/ppermute | solution.py:75
  74.9 0.4 collective-permute-start.14
  75.2 1.4 %collective-permute-done.6 = bf16[2,20,8,128]{3,2,1,0:T(8,128)(2,1)S(1)} collective-permute-done((bf16[2,20,8,128]{3,2,1,0:T(8,128)(2,1)S(1)}, bf16[2,20,8,128]{3,2,1,0:T(8,128)(2,1)S(1)}, u32[]{:S(2)}, u32[]{:S(2)}) %collective-permute-start.6) | collective-permute-done | bytes 81952 | tf_op jit(solution)/shard_map/ppermute | solution.py:86
  76.7 0.6 collective-permute-start.7
  77.3 3.0 %collective-permute-done.14 = f32[1,20,8,128]{3,2,1,0:T(8,128)S(1)} collective-permute-done((f32[1,20,8,128]{3,2,1,0:T(8,128)S(1)}, f32[1,20,8,128]{3,2,1,0:T(8,128)S(1)}, u32[]{:S(2)}, u32[]{:S(2)}) %collective-permute-start.14) | collective-permute-done | bytes 81952 | tf_op jit(solution)/shard_map/ppermute | solution.py:75
  80.3 0.4 collective-permute-start.15
  80.7 0.5 fusion.23
  81.2 4.4 %copy.159 = bf16[2,512,1280]{2,1,0:T(8,128)(2,1)} copy(bf16[2,512,1280]{1,2,0:T(8,128)(2,1)} %bitcast.132) | data formatting | bytes 5242880
  85.6 3.2 %collective-permute-start.16 = (bf16[2,20,8,128]{3,2,1,0:T(8,128)(2,1)S(1)}, bf16[2,20,8,128]{3,2,1,0:T(8,128)(2,1)S(1)}, u32[]{:S(2)}, u32[]{:S(2)}) collective-permute-start(bf16[2,20,8,128]{3,2,1,0:T(8,128)(2,1)S(1)} %maximum_select_fusion.8), channel_id=1, source_target_pairs={{0,4},{2,6},{4,0},{6,2},{8,12},{10,14},{12,8},{14,10},{1,5},{3,7},... | collective-permute-start | bytes 245768 | tf_op jit(solution)/shard_map/ppermute | solution.py:86
  88.9 2.3 %collective-permute-done.16 = bf16[2,20,8,128]{3,2,1,0:T(8,128)(2,1)S(1)} collective-permute-done((bf16[2,20,8,128]{3,2,1,0:T(8,128)(2,1)S(1)}, bf16[2,20,8,128]{3,2,1,0:T(8,128)(2,1)S(1)}, u32[]{:S(2)}, u32[]{:S(2)}) %collective-permute-start.16) | collective-permute-done | bytes 81952 | tf_op jit(solution)/shard_map/ppermute | solution.py:86
  91.3 0.6 collective-permute-start.17
  92.1 4.6 %collective-permute-done.17 = bf16[4,20,8,128]{3,2,1,0:T(8,128)(2,1)S(1)} collective-permute-done((bf16[4,20,8,128]{3,2,1,0:T(8,128)(2,1)S(1)}, bf16[4,20,8,128]{3,2,1,0:T(8,128)(2,1)S(1)}, u32[]{:S(2)}, u32[]{:S(2)}) %collective-permute-start.17) | collective-permute-done | bytes 163872 | tf_op jit(solution)/shard_map/ppermute | solution.py:86
  96.8 0.6 fusion.52
  97.4 0.5 fusion.18
  97.9 0.5 copy-done.8
  98.5 0.7 reshape.169
  99.2 0.9 constant_dynamic-slice_fusion.1
  100.1 1.0 copy.156
  101.2 2.5 %fusion.8 = f32[256,128]{0,1:T(8,128)S(1)} fusion(f32[256,40]{0,1:T(8,128)S(1)} %copy-done.20, bf16[256,40,64]{0,2,1:T(8,128)(2,1)} %bitcast.143, bf16[20,64,128]{2,1,0:T(8,128)(2,1)} %collective-permute-done.8, bf16[20,64,128]{2,1,0:T(8,128)(2,1)S(1)} %copy_bitcast_fusion, pred[]{:T(512)S(6)} %eq.28), kind=kOutput, calls=%fused_computation.15 | convolution fusion | flops 171343872 | bytes 2138113 | tf_op jit(solution)/shard_map/jhp,hpn->jhn/dot_general | solution.py:232
  103.6 0.8 copy.158
  104.4 1.6 %fusion.17 = bf16[40,64,256]{2,1,0:T(8,128)(2,1)S(1)} fusion(f32[256,128]{0,1:T(8,128)S(1)} %copy-done.11, f32[256,40]{0,1:T(8,128)S(1)} %copy-done.20, bf16[20,64,128]{2,1,0:T(8,128)(2,1)} %collective-permute-done.8, bf16[20,64,128]{2,1,0:T(8,128)(2,1)S(1)} %copy_bitcast_fusion, pred[]{:T(512)S(6)} %eq.28), kind=kOutput, calls=%fused_computation.30 | convolution fusion | flops 172032000 | bytes 2138113 | tf_op jit(solution)/shard_map/jhn,hpn->jhp/dot_general | solution.py:228
  106.0 1.6 %copy.157 = bf16[256,2560]{1,0:T(8,128)(2,1)} copy(bf16[256,2560]{0,1:T(8,128)(2,1)S(1)} %bitcast.147) | data formatting | bytes 2621440
  107.6 0.3 copy.155
  108.0 0.8 fusion.44
  (88 shorter events, 1.5 us)
Async XLA Ops:
  0.6 18.8 %copy-start = (bf16[2,512,128]{2,1,0:T(8,128)(2,1)S(1)}, bf16[2,512,128]{2,1,0:T(8,128)(2,1)}, u32[]{:S(2)}) copy-start(bf16[2,512,128]{2,1,0:T(8,128)(2,1)} %param.14) | copy-start | bytes 786436
  0.6 9.4 %copy-start.15 = (bf16[256,128]{1,0:T(8,128)(2,1)S(1)}, bf16[256,128]{1,0:T(8,128)(2,1)}, u32[]{:S(2)}) copy-start(bf16[256,128]{1,0:T(8,128)(2,1)} %param.10) | copy-start | bytes 196612
  1.6 10.4 %collective-permute-start = (f32[40]{0:T(128)S(1)}, f32[40]{0:T(128)S(1)}, u32[]{:S(2)}, u32[]{:S(2)}) collective-permute-start(f32[40]{0:T(128)S(1)} %fusion.35), channel_id=1, source_target_pairs={{1,0},{2,1},{3,2},{4,3},{5,4},{6,5},{7,6},{8,7},{9,8},{10,9},{11,1... | collective-permute-start | bytes 488 | tf_op jit(solution)/shard_map/ppermute | solution.py:45
  12.0 4.6 %copy-start.13 = (f32[2,512,20]{1,2,0:T(8,128)}, f32[2,512,20]{1,2,0:T(8,128)S(1)}, u32[]{:S(2)}) copy-start(f32[2,512,20]{1,2,0:T(8,128)S(1)} %get-tuple-element.36) | copy-start | bytes 245764
  12.0 3.1 %copy-start.17 = (s32[2]{0:T(128)S(1)}, s32[2]{0:T(128)}, u32[]{:S(2)}) copy-start(s32[2]{0:T(128)} %param.16) | copy-start | bytes 28
  15.2 7.0 %collective-permute-start.1 = (f32[40]{0:T(128)S(1)}, f32[40]{0:T(128)S(1)}, u32[]{:S(2)}, u32[]{:S(2)}) collective-permute-start(f32[40]{0:T(128)S(1)} %add.139), channel_id=1, source_target_pairs={{2,0},{3,1},{4,2},{5,3},{6,4},{7,5},{8,6},{9,7},{10,8},{11,9},{12,... | collective-permute-start | bytes 488 | tf_op jit(solution)/shard_map/ppermute | solution.py:45
  16.6 2.8 %copy-start.3 = (bf16[2,512,1280]{1,2,0:T(8,128)(2,1)}, bf16[2,512,1280]{1,2,0:T(8,128)(2,1)S(1)}, u32[]{:S(2)}) copy-start(bf16[2,512,1280]{1,2,0:T(8,128)(2,1)S(1)} %broadcast_select_fusion) | copy-start | bytes 7864324
  19.4 24.8 %copy-start.1 = (bf16[2,512,20,64]{1,3,2,0:T(8,128)(2,1)}, bf16[2,512,20,64]{1,3,2,0:T(8,128)(2,1)S(1)}, u32[]{:S(2)}) copy-start(bf16[2,512,20,64]{1,3,2,0:T(8,128)(2,1)S(1)} %get-tuple-element.49) | copy-start | bytes 7864324
  26.6 7.8 %collective-permute-start.9 = (f32[40]{0:T(128)S(1)}, f32[40]{0:T(128)S(1)}, u32[]{:S(2)}, u32[]{:S(2)}) collective-permute-start(f32[40]{0:T(128)S(1)} %add.142), channel_id=1, source_target_pairs={{4,0},{5,1},{6,2},{7,3},{8,4},{9,5},{10,6},{11,7},{12,8},{13,9},{1... | collective-permute-start | bytes 488 | tf_op jit(solution)/shard_map/ppermute | solution.py:45
  28.0 19.3 %collective-permute-start.2 = (f32[4,20,8,128]{3,2,1,0:T(8,128)S(1)}, f32[4,20,8,128]{3,2,1,0:T(8,128)S(1)}, u32[]{:S(2)}, u32[]{:S(2)}) collective-permute-start(f32[4,20,8,128]{3,2,1,0:T(8,128)S(1)} %dynamic-slice_bitcast_fusion.2), channel_id=1, source_target_pairs={{0,2},{2,0},{4,6},{6,4},{8,10},{10,8},{12,14},{14,12},{1,3},{3,1},... | collective-permute-start | bytes 983048 | tf_op jit(solution)/shard_map/ppermute | solution.py:75
  31.0 3.0 %copy-start.7 = (bf16[2,512,128]{2,1,0:T(8,128)(2,1)S(1)}, bf16[2,512,128]{2,1,0:T(8,128)(2,1)}, u32[]{:S(2)}) copy-start(bf16[2,512,128]{2,1,0:T(8,128)(2,1)} %param.13) | copy-start | bytes 786436
  34.5 11.4 %collective-permute-start.10 = (f32[40]{0:T(128)S(1)}, f32[40]{0:T(128)S(1)}, u32[]{:S(2)}, u32[]{:S(2)}) collective-permute-start(f32[40]{0:T(128)S(1)} %add.154), channel_id=1, source_target_pairs={{8,0},{9,1},{10,2},{11,3},{12,4},{13,5},{14,6},{15,7},{24,16},{25,... | collective-permute-start | bytes 488 | tf_op jit(solution)/shard_map/ppermute | solution.py:45
  35.8 1.7 %copy-start.4 = (bf16[2,512,1280]{1,2,0:T(8,128)(2,1)S(1)}, bf16[2,512,1280]{1,2,0:T(8,128)(2,1)}, u32[]{:S(2)}) copy-start(bf16[2,512,1280]{1,2,0:T(8,128)(2,1)} %copy-done.3) | copy-start | bytes 7864324
  35.8 1.7 %copy-start.6 = (pred[512,512]{1,0:T(8,128)(4,1)S(1)}, pred[512,512]{1,0:T(8,128)(4,1)}, u32[]{:S(2)}) copy-start(pred[512,512]{1,0:T(8,128)(4,1)} %iota_compare_fusion) | copy-start | bytes 786436
  35.8 1.7 %copy-start.12 = (f32[2,512,20]{1,2,0:T(8,128)S(1)}, f32[2,512,20]{1,2,0:T(8,128)}, u32[]{:S(2)}) copy-start(f32[2,512,20]{1,2,0:T(8,128)} %get-tuple-element.43) | copy-start | bytes 245764
  35.8 1.8 %copy-start.14 = (f32[2,512,20]{1,2,0:T(8,128)S(1)}, f32[2,512,20]{1,2,0:T(8,128)}, u32[]{:S(2)}) copy-start(f32[2,512,20]{1,2,0:T(8,128)} %copy-done.13) | copy-start | bytes 245764
  44.3 1.6 %copy-start.16 = (s32[256,40]{0,1:T(8,128)S(1)}, s32[256,40]{0,1:T(8,128)}, u32[]{:S(2)}) copy-start(s32[256,40]{0,1:T(8,128)} %param.11) | copy-start | bytes 122884
  44.3 1.6 %copy-start.18 = (f32[256,40]{0,1:T(8,128)S(1)}, f32[256,40]{0,1:T(8,128)}, u32[]{:S(2)}) copy-start(f32[256,40]{0,1:T(8,128)} %convolution_add_fusion.5) | copy-start | bytes 122884
  44.3 1.9 %copy-start.9 = (bf16[256,2560]{0,1:T(8,128)(2,1)S(1)}, bf16[256,2560]{0,1:T(8,128)(2,1)}, u32[]{:S(2)}) copy-start(bf16[256,2560]{0,1:T(8,128)(2,1)} %copy.137) | copy-start | bytes 3932164
  44.3 1.9 %copy-start.10 = (f32[256,128]{0,1:T(8,128)S(1)}, f32[256,128]{0,1:T(8,128)}, u32[]{:S(2)}) copy-start(f32[256,128]{0,1:T(8,128)} %copy.135) | copy-start | bytes 393220
  46.1 1.1 copy-start.19
  46.2 4.3 %copy-start.5 = (bf16[2,512,20,64]{1,3,2,0:T(8,128)(2,1)S(1)}, bf16[2,512,20,64]{1,3,2,0:T(8,128)(2,1)}, u32[]{:S(2)}) copy-start(bf16[2,512,20,64]{1,3,2,0:T(8,128)(2,1)} %get-tuple-element.52) | copy-start | bytes 7864324
  47.3 11.7 %collective-permute-start.11 = (f32[20,64,128]{2,1,0:T(8,128)S(1)}, f32[20,64,128]{2,1,0:T(8,128)S(1)}, u32[]{:S(2)}, u32[]{:S(2)}) collective-permute-start(f32[20,64,128]{2,1,0:T(8,128)S(1)} %dynamic-slice_bitcast_fusion), channel_id=1, source_target_pairs={{0,1},{1,0},{2,3},{3,2},{4,5},{5,4},{6,7},{7,6},{8,9},{9,8},{10,11... | collective-permute-start | bytes 1966088 | tf_op jit(solution)/shard_map/ppermute | solution.py:110
  47.5 7.9 %collective-permute-start.3 = (f32[2,20,8,128]{3,2,1,0:T(8,128)S(1)}, f32[2,20,8,128]{3,2,1,0:T(8,128)S(1)}, u32[]{:S(2)}, u32[]{:S(2)}) collective-permute-start(f32[2,20,8,128]{3,2,1,0:T(8,128)S(1)} %dynamic-slice_bitcast_fusion.4), channel_id=1, source_target_pairs={{0,4},{2,6},{4,0},{6,2},{8,12},{10,14},{12,8},{14,10},{1,5},{3,7},... | collective-permute-start | bytes 491528 | tf_op jit(solution)/shard_map/ppermute | solution.py:75
  55.4 7.9 %collective-permute-start.4 = (f32[1,20,8,128]{3,2,1,0:T(8,128)S(1)}, f32[1,20,8,128]{3,2,1,0:T(8,128)S(1)}, u32[]{:S(2)}, u32[]{:S(2)}) collective-permute-start(f32[1,20,8,128]{3,2,1,0:T(8,128)S(1)} %constant_dynamic-slice_fusion.3), channel_id=1, source_target_pairs={{0,8},{2,10},{4,12},{6,14},{8,0},{10,2},{12,4},{14,6},{1,9},{3,11}... | collective-permute-start | bytes 245768 | tf_op jit(solution)/shard_map/ppermute | solution.py:75
  59.2 9.3 %collective-permute-start.12 = (f32[4,20,8,128]{3,2,1,0:T(8,128)S(1)}, f32[4,20,8,128]{3,2,1,0:T(8,128)S(1)}, u32[]{:S(2)}, u32[]{:S(2)}) collective-permute-start(f32[4,20,8,128]{3,2,1,0:T(8,128)S(1)} %dynamic-slice_bitcast_fusion.1), channel_id=1, source_target_pairs={{0,2},{2,0},{4,6},{6,4},{8,10},{10,8},{12,14},{14,12},{1,3},{3,1},... | collective-permute-start | bytes 983048 | tf_op jit(solution)/shard_map/ppermute | solution.py:75
  63.3 8.0 %collective-permute-start.5 = (bf16[1,20,8,128]{3,2,1,0:T(8,128)(2,1)S(1)}, bf16[1,20,8,128]{3,2,1,0:T(8,128)(2,1)S(1)}, u32[]{:S(2)}, u32[]{:S(2)}) collective-permute-start(bf16[1,20,8,128]{3,2,1,0:T(8,128)(2,1)S(1)} %add_convert_fusion.1), channel_id=1, source_target_pairs={{0,8},{2,10},{4,12},{6,14},{8,0},{10,2},{12,4},{14,6},{1,9},{3,11}... | collective-permute-start | bytes 122888 | tf_op jit(solution)/shard_map/ppermute | solution.py:86
  68.6 6.3 %collective-permute-start.13 = (f32[2,20,8,128]{3,2,1,0:T(8,128)S(1)}, f32[2,20,8,128]{3,2,1,0:T(8,128)S(1)}, u32[]{:S(2)}, u32[]{:S(2)}) collective-permute-start(f32[2,20,8,128]{3,2,1,0:T(8,128)S(1)} %dynamic-slice_bitcast_fusion.3), channel_id=1, source_target_pairs={{0,4},{2,6},{4,0},{6,2},{8,12},{10,14},{12,8},{14,10},{1,5},{3,7},... | collective-permute-start | bytes 491528 | tf_op jit(solution)/shard_map/ppermute | solution.py:75
  71.3 5.3 %collective-permute-start.6 = (bf16[2,20,8,128]{3,2,1,0:T(8,128)(2,1)S(1)}, bf16[2,20,8,128]{3,2,1,0:T(8,128)(2,1)S(1)}, u32[]{:S(2)}, u32[]{:S(2)}) collective-permute-start(bf16[2,20,8,128]{3,2,1,0:T(8,128)(2,1)S(1)} %maximum_select_fusion.7), channel_id=1, source_target_pairs={{0,4},{2,6},{4,0},{6,2},{8,12},{10,14},{12,8},{14,10},{1,5},{3,7},... | collective-permute-start | bytes 245768 | tf_op jit(solution)/shard_map/ppermute | solution.py:86
  74.9 5.4 %collective-permute-start.14 = (f32[1,20,8,128]{3,2,1,0:T(8,128)S(1)}, f32[1,20,8,128]{3,2,1,0:T(8,128)S(1)}, u32[]{:S(2)}, u32[]{:S(2)}) collective-permute-start(f32[1,20,8,128]{3,2,1,0:T(8,128)S(1)} %constant_dynamic-slice_fusion.2), channel_id=1, source_target_pairs={{0,8},{2,10},{4,12},{6,14},{8,0},{10,2},{12,4},{14,6},{1,9},{3,11}... | collective-permute-start | bytes 245768 | tf_op jit(solution)/shard_map/ppermute | solution.py:75
  76.7 12.1 %collective-permute-start.7 = (bf16[4,20,8,128]{3,2,1,0:T(8,128)(2,1)S(1)}, bf16[4,20,8,128]{3,2,1,0:T(8,128)(2,1)S(1)}, u32[]{:S(2)}, u32[]{:S(2)}) collective-permute-start(bf16[4,20,8,128]{3,2,1,0:T(8,128)(2,1)S(1)} %maximum_select_fusion.3), channel_id=1, source_target_pairs={{0,2},{2,0},{4,6},{6,4},{8,10},{10,8},{12,14},{14,12},{1,3},{3,1},... | collective-permute-start | bytes 491528 | tf_op jit(solution)/shard_map/ppermute | solution.py:86
  80.3 5.3 %collective-permute-start.15 = (bf16[1,20,8,128]{3,2,1,0:T(8,128)(2,1)S(1)}, bf16[1,20,8,128]{3,2,1,0:T(8,128)(2,1)S(1)}, u32[]{:S(2)}, u32[]{:S(2)}) collective-permute-start(bf16[1,20,8,128]{3,2,1,0:T(8,128)(2,1)S(1)} %add_convert_fusion), channel_id=1, source_target_pairs={{0,8},{2,10},{4,12},{6,14},{8,0},{10,2},{12,4},{14,6},{1,9},{3,11}... | collective-permute-start | bytes 122888 | tf_op jit(solution)/shard_map/ppermute | solution.py:86
  85.6 11.2 %copy-start.2 = (bf16[2,512,20,64]{1,3,2,0:T(8,128)(2,1)S(1)}, bf16[2,512,20,64]{1,3,2,0:T(8,128)(2,1)}, u32[]{:S(2)}) copy-start(bf16[2,512,20,64]{1,3,2,0:T(8,128)(2,1)} %copy-done.1) | copy-start | bytes 7864324
  85.6 5.6 %collective-permute-start.16 = (bf16[2,20,8,128]{3,2,1,0:T(8,128)(2,1)S(1)}, bf16[2,20,8,128]{3,2,1,0:T(8,128)(2,1)S(1)}, u32[]{:S(2)}, u32[]{:S(2)}) collective-permute-start(bf16[2,20,8,128]{3,2,1,0:T(8,128)(2,1)S(1)} %maximum_select_fusion.8), channel_id=1, source_target_pairs={{0,4},{2,6},{4,0},{6,2},{8,12},{10,14},{12,8},{14,10},{1,5},{3,7},... | collective-permute-start | bytes 245768 | tf_op jit(solution)/shard_map/ppermute | solution.py:86
  91.3 5.4 %collective-permute-start.17 = (bf16[4,20,8,128]{3,2,1,0:T(8,128)(2,1)S(1)}, bf16[4,20,8,128]{3,2,1,0:T(8,128)(2,1)S(1)}, u32[]{:S(2)}, u32[]{:S(2)}) collective-permute-start(bf16[4,20,8,128]{3,2,1,0:T(8,128)(2,1)S(1)} %maximum_select_fusion.4), channel_id=1, source_target_pairs={{0,2},{2,0},{4,6},{6,4},{8,10},{10,8},{12,14},{14,12},{1,3},{3,1},... | collective-permute-start | bytes 491528 | tf_op jit(solution)/shard_map/ppermute | solution.py:86
  92.0 9.1 %collective-permute-start.8 = (bf16[20,64,128]{2,1,0:T(8,128)(2,1)S(1)}, bf16[20,64,128]{2,1,0:T(8,128)(2,1)}, u32[]{:S(2)}, u32[]{:S(2)}) collective-permute-start(bf16[20,64,128]{2,1,0:T(8,128)(2,1)S(1)} %copy_bitcast_fusion), channel_id=1, source_target_pairs={{0,1},{1,0},{2,3},{3,2},{4,5},{5,4},{6,7},{7,6},{8,9},{9,8},{10,11... | collective-permute-start | bytes 983048 | tf_op jit(solution)/shard_map/ppermute | solution.py:110
  97.4 1.0 copy-start.8
  98.5 2.7 %copy-start.20 = (f32[256,40]{0,1:T(8,128)S(1)}, f32[256,40]{0,1:T(8,128)}, u32[]{:S(2)}) copy-start(f32[256,40]{0,1:T(8,128)} %copy-done.19) | copy-start | bytes 122884
  101.2 3.3 %copy-start.11 = (f32[256,128]{0,1:T(8,128)S(1)}, f32[256,128]{0,1:T(8,128)}, u32[]{:S(2)}) copy-start(f32[256,128]{0,1:T(8,128)} %copy.135) | copy-start | bytes 393220
  101.2 6.8 %collective-permute-start.18 = (f32[2,256,256]{2,1,0:T(8,128)}, f32[2,256,256]{2,1,0:T(8,128)S(1)}, u32[]{:S(2)}, u32[]{:S(2)}) collective-permute-start(f32[2,256,256]{2,1,0:T(8,128)} %bitcast.62), channel_id=1, source_target_pairs={{0,1},{1,0},{2,3},{3,2},{4,5},{5,4},{6,7},{7,6},{8,9},{9,8},{10,11... | collective-permute-start | bytes 1572872 | tf_op jit(solution)/shard_map/ppermute | solution.py:110

commit v20 on v18

--- a/solution.py
+++ b/solution.py
@@ -181,7 +181,10 @@
             preferred_element_type=jnp.float32,
         )
 
-    weight_sum = pair(decayed_g, x_high) + pair(decayed_g, x_low) + pair(g_low, x_high)
+    cross_left = jnp.concatenate([decayed_g.reshape(flat), g_low.reshape(flat)], axis=2)
+    cross_right = jnp.concatenate([x_low.reshape(flat), x_high.reshape(flat)], axis=2)
+    cross = jnp.einsum("ctk,csk->cts", cross_left, cross_right, preferred_element_type=jnp.float32)
+    weight_sum = pair(decayed_g, x_high) + cross
     weight_sum = jnp.where(causal[None], weight_sum, 0.0)
     sum_high, sum_low = split_bf16(weight_sum)
 

time: 107 us -> 135 us (1.26)
  local copies, waits for them, and re-layouts: 22.4 us -> 39.6 us
  matrix products: 22.5 us -> 30.9 us
  other arithmetic: 9.28 us -> 11.7 us
  starting transfers between devices: 24.1 us -> 26.1 us
  waiting for transfers between devices: 26.4 us -> 24.5 us
    reshape x0 -> x4, local copies, waits for them, and re-layouts: none -> 15.8 us  [the longest x1 4.41 us: shards(): g_low.reshape(flat)]
    dot_general x0 -> x1, matrix products: none -> 4.1 us  [shards(): jnp.einsum('ctk,csk->cts', cross_left, cross_right, preferred_element_typ...]
    dot_general x3 -> x1, matrix products: 4.94 us -> 1.72 us  [pair(): jnp.einsum('ctk,csk->cts', left.reshape(flat), right.reshape(flat), prefe...]
    dot_general x1, matrix products: 6.71 us -> 9.53 us  [shards(): jnp.einsum('chts,cthp->cshp', kernel, g_heads, preferred_element_type=jnp...]
    dot_general x1, matrix products: 0.43 us -> 2.86 us  [x_work(): jnp.einsum('ctn,csn->cts', c_cand, b_cand, preferred_element_type=jnp.flo...]
    ppermute x4, waiting for transfers between devices: 1.9 us -> 0.01 us  [suffix_sum(): value = value + lax.ppermute(value, axis, back)]
    ppermute x6, starting transfers between devices: 12.2 us -> 13.9 us  [halving_scatter(): lax.ppermute(give, axis, [(at, at ^ step) for at in range(count)])]
    convert_element_type x2, other arithmetic: 5.75 us -> 7.27 us  [split_bf16(): low = (value - high).astype(jnp.bfloat16)]
  transfers between devices with their start and end apart: 19 -> 19, of which waited for: 9 -> 8; matrix products, arithmetic and copies ran while one was open for 42% -> 59% of each run, Pallas kernels for 0% -> 0%
where the time goes in v20:
time: 135 us; the launch traced here: 134 us
  local copies, waits for them, and re-layouts  39.6 us (29%)
  matrix products  30.9 us (23%)
  starting transfers between devices  26.1 us (19%)
  waiting for transfers between devices  24.5 us (18%)
  other arithmetic  11.7 us (9%)
    ppermute x6, waiting for transfers between devices, halving_scatter(): lax.ppermute(give, axis, [(at, at ^ step) for at in range(count)])  16.1 us
    ppermute x6, starting transfers between devices, halving_scatter(): lax.ppermute(give, axis, [(at, at ^ step) for at in range(count)])  13.9 us
    unnamed x48, local copies, waits for them, and re-layouts  9.77 us
    dot_general x1, matrix products, shards(): jnp.einsum('chts,cthp->cshp', kernel, g_heads, preferred_element_type=jnp...  9.53 us
    ppermute x6, waiting for transfers between devices, doubling_gather(): other = lax.ppermute(value, axis, [(at, at ^ step) for at in range(count)])  8.36 us
    optimization_barrier x2, local copies, waits for them, and re-layouts, suffix_sum(): value, args = lax.optimization_barrier((value, pick(done)))  7.41 us
    convert_element_type x2, other arithmetic, split_bf16(): low = (value - high).astype(jnp.bfloat16)  7.27 us
    ppermute x6, starting transfers between devices, doubling_gather(): other = lax.ppermute(value, axis, [(at, at ^ step) for at in range(count)])  6.58 us
  transfers between devices with their start and end apart: 19, of which 8 were waited for; matrix products, arithmetic and copies ran while one was open for 59% of the time, Pallas kernels for 0%

profile of v20, /device:TPU:0, one launch (start us, length us, event | category | flops | bytes accessed | tf_op | source)
XLA Modules:
  0.0 134.1 jit_solution(3499230476413230532)
XLA Ops:
  0.7 0.9 fusion.35
  1.6 1.3 collective-permute-start
  3.0 0.8 iota_compare_fusion
  3.8 1.0 multiply_log-plus-one_fusion
  4.8 1.1 exponential_bitcast_fusion
  5.9 1.6 %copy.125 = f32[256,128]{0,1:T(8,128)} copy(bf16[256,128]{1,0:T(8,128)(2,1)} %param.10) | data formatting | bytes 196608 | tf_op jit(solution)/shard_map/convert_element_type | solution.py:154
  7.5 2.4 %copy.127 = bf16[256,2560]{0,1:T(8,128)(2,1)} copy(bf16[256,2560]{1,0:T(8,128)(2,1)} %param.9) | data formatting | bytes 2621440 | tf_op args[0]
  10.1 1.3 collective-permute-start.1
  11.3 3.0 %copy.119 = bf16[2,512,1280]{1,2,0:T(8,128)(2,1)S(1)} copy(bf16[2,512,1280]{2,1,0:T(8,128)(2,1)} %param.17) | data formatting | bytes 5242880 | tf_op jit(solution)/shard_map/optimization_barrier | solution.py:34
  14.6 2.8 %fusion.6 = (bf16[2,512,20,64]{1,3,2,0:T(8,128)(2,1)}, bf16[2,512,20,64]{1,3,2,0:T(8,128)(2,1)S(1)}) fusion(bf16[2,512,20,64]{1,3,2,0:T(8,128)(2,1)S(1)} %bitcast.119, f32[2,512,20]{1,2,0:T(8,128)S(1)} %get-tuple-element.36), kind=kLoop, calls=%fused_computation.11 | loop fusion | flops 7864320 | bytes 7946240 | tf_op jit(solution)/shard_map/convert_element_type | solution.py:11
  17.3 0.8 convolution_bitcast_fusion
  18.3 1.3 collective-permute-start.9
  19.6 0.8 dynamic-slice_bitcast_fusion.2
  20.3 4.2 %collective-permute-start.2 = (f32[4,20,8,128]{3,2,1,0:T(8,128)}, f32[4,20,8,128]{3,2,1,0:T(8,128)}, u32[]{:S(2)}, u32[]{:S(2)}) collective-permute-start(f32[4,20,8,128]{3,2,1,0:T(8,128)} %dynamic-slice_bitcast_fusion.2), channel_id=1, source_target_pairs={{0,2},{2,0},{4,6},{6,4},{8,10},{10,8},{12,14},{14,12},{1,3},{3,1},... | collective-permute-start | bytes 983048 | tf_op jit(solution)/shard_map/ppermute | solution.py:65
  24.5 4.4 %copy.124 = bf16[2,512,1280]{1,2,0:T(8,128)(2,1)} copy(bf16[2,512,1280]{2,1,0:T(8,128)(2,1)} %param.12) | data formatting | bytes 5242880 | tf_op jit(solution)/shard_map/optimization_barrier | solution.py:34
  29.0 2.6 %copy.130 = bf16[2,512,1280]{2,1,0:T(8,128)(2,1)} copy(bf16[2,512,1280]{1,2,0:T(8,128)(2,1)S(1)} %bitcast.114) | data formatting | bytes 5242880 | tf_op jit(solution)/shard_map/reshape | solution.py:180
  31.6 2.9 %fusion.47 = f32[2,512,512]{2,1,0:T(8,128)} fusion(bf16[2,512,128]{2,1,0:T(8,128)(2,1)S(1)} %copy-done, bf16[2,512,128]{2,1,0:T(8,128)(2,1)} %param.13), kind=kOutput, calls=%fused_computation.93 | convolution fusion | flops 134217728 | bytes 2621440 | tf_op jit(solution)/shard_map/ctn,csn->cts/dot_general | solution.py:134
  34.4 4.5 %fusion.7 = (bf16[2,512,20,64]{1,3,2,0:T(8,128)(2,1)}, bf16[2,512,20,64]{1,3,2,0:T(8,128)(2,1)}) fusion(bf16[2,512,20,64]{1,3,2,0:T(8,128)(2,1)S(1)} %bitcast.123, f32[2,512,20]{1,2,0:T(8,128)} %get-tuple-element.43), kind=kLoop, calls=%fused_computation.12 | loop fusion | flops 7864320 | bytes 7946240 | tf_op jit(solution)/shard_map/convert_element_type | solution.py:11
  38.9 4.4 %copy.131 = bf16[2,512,1280]{2,1,0:T(8,128)(2,1)} copy(bf16[2,512,1280]{1,2,0:T(8,128)(2,1)} %bitcast.121) | data formatting | bytes 5242880 | tf_op jit(solution)/shard_map/reshape | solution.py:184
  43.4 1.5 %collective-permute-start.10 = (f32[40]{0:T(128)S(1)}, f32[40]{0:T(128)S(1)}, u32[]{:S(2)}, u32[]{:S(2)}) collective-permute-start(f32[40]{0:T(128)S(1)} %add.133), channel_id=1, source_target_pairs={{8,0},{9,1},{10,2},{11,3},{12,4},{13,5},{14,6},{15,7},{24,16},{25,... | collective-permute-start | bytes 488 | tf_op jit(solution)/shard_map/ppermute | solution.py:35
  44.8 4.4 %copy.133 = bf16[2,512,1280]{2,1,0:T(8,128)(2,1)} copy(bf16[2,512,1280]{1,2,0:T(8,128)(2,1)} %bitcast.117) | data formatting | bytes 5242880 | tf_op jit(solution)/shard_map/reshape | solution.py:180
  49.2 4.4 %copy.132 = bf16[2,512,1280]{2,1,0:T(8,128)(2,1)} copy(bf16[2,512,1280]{1,2,0:T(8,128)(2,1)} %bitcast.122) | data formatting | bytes 5242880 | tf_op jit(solution)/shard_map/reshape | solution.py:185
  53.6 9.5 %fusion.23 = bf16[2,20,64,512]{3,2,1,0:T(8,128)(2,1)} fusion(bf16[2,512,20,64]{1,3,2,0:T(8,128)(2,1)} %bitcast.120, f32[2,20,512]{2,1,0:T(8,128)} %bitcast.144, f32[2,20,512]{2,1,0:T(8,128)} %bitcast.145, f32[2,512,512]{2,1,0:T(8,128)} %fusion.47, pred[512,512]{1,0:T(8,128)(4,1)} %iota_compare_fusion), kind=kOutput, calls=%fused_computation.36 | convolution fusion | flops 1385431040 | bytes 7766016 | tf_op jit(solution)/shard_map/chts,cthp->cshp/dot_general | solution.py:203
  63.2 4.1 %fusion.8 = f32[2,512,512]{2,1,0:T(8,128)} fusion(bf16[2,512,1280]{2,1,0:T(8,128)(2,1)S(1)} %copy-done.7, bf16[2,512,1280]{2,1,0:T(8,128)(2,1)S(1)} %copy-done.6, bf16[2,512,1280]{2,1,0:T(8,128)(2,1)S(1)} %copy-done.8, bf16[2,512,1280]{2,1,0:T(8,128)(2,1)S(1)} %copy-done.9), kind=kOutput, calls=%fused_computation.13 | convolution fusion | flops 2705326080 | bytes 12582912 | tf_op jit(solution)/shard_map/ctk,csk->cts/dot_general | solution.py:186
  67.3 0.3 add_exponential_fusion
  67.6 2.5 %fusion.16 = f32[40,128,64]{1,2,0:T(8,128)S(1)} fusion(bf16[256,40,64]{0,2,1:T(8,128)(2,1)} %bitcast.135, f32[256,128]{0,1:T(8,128)S(1)} %copy-done.14, f32[256,40]{0,1:T(8,128)S(1)} %add_exponential_fusion), kind=kOutput, calls=%fused_computation.25 | convolution fusion | flops 170393600 | bytes 2793472 | tf_op jit(solution)/shard_map/jhp,jhn->hpn/dot_general | solution.py:158
  70.2 0.3 collective-permute-start.11
  70.5 1.0 bitcast_add_fusion.3
  71.5 3.4 %collective-permute-start.3 = (f32[2,20,8,128]{3,2,1,0:T(8,128)S(1)}, f32[2,20,8,128]{3,2,1,0:T(8,128)S(1)}, u32[]{:S(2)}, u32[]{:S(2)}) collective-permute-start(f32[2,20,8,128]{3,2,1,0:T(8,128)S(1)} %dynamic-slice_bitcast_fusion.4), channel_id=1, source_target_pairs={{0,4},{2,6},{4,0},{6,2},{8,12},{10,14},{12,8},{14,10},{1,5},{3,7},... | collective-permute-start | bytes 491528 | tf_op jit(solution)/shard_map/ppermute | solution.py:65
  74.9 1.7 %add_select_fusion = f32[2,512,512]{2,1,0:T(8,128)S(1)} fusion(f32[2,512,512]{2,1,0:T(8,128)S(1)} %copy-done.21, bf16[2,512,1280]{1,2,0:T(8,128)(2,1)S(1)} %bitcast.115, bf16[2,512,1280]{1,2,0:T(8,128)(2,1)S(1)} %bitcast.118, pred[512,512]{1,0:T(8,128)(4,1)S(1)} %copy-done.13), kind=kOutput, calls=%fused_computation.35 | convolution fusion | flops 1343225856 | bytes 9699328 | tf_op jit(solution)/shard_map/ctk,csk->cts/dot_general | solution.py:179
  76.7 3.1 %collective-permute-done.3 = f32[2,20,8,128]{3,2,1,0:T(8,128)S(1)} collective-permute-done((f32[2,20,8,128]{3,2,1,0:T(8,128)S(1)}, f32[2,20,8,128]{3,2,1,0:T(8,128)S(1)}, u32[]{:S(2)}, u32[]{:S(2)}) %collective-permute-start.3) | collective-permute-done | bytes 163872 | tf_op jit(solution)/shard_map/ppermute | solution.py:65
  79.8 3.6 %collective-permute-start.4 = (f32[1,20,8,128]{3,2,1,0:T(8,128)S(1)}, f32[1,20,8,128]{3,2,1,0:T(8,128)S(1)}, u32[]{:S(2)}, u32[]{:S(2)}) collective-permute-start(f32[1,20,8,128]{3,2,1,0:T(8,128)S(1)} %constant_dynamic-slice_fusion.3), channel_id=1, source_target_pairs={{0,8},{2,10},{4,12},{6,14},{8,0},{10,2},{12,4},{14,6},{1,9},{3,11}... | collective-permute-start | bytes 245768 | tf_op jit(solution)/shard_map/ppermute | solution.py:65
  83.6 0.6 collective-permute-start.12
  84.3 0.4 fusion.29
  84.6 3.1 %collective-permute-done.4 = f32[1,20,8,128]{3,2,1,0:T(8,128)S(1)} collective-permute-done((f32[1,20,8,128]{3,2,1,0:T(8,128)S(1)}, f32[1,20,8,128]{3,2,1,0:T(8,128)S(1)}, u32[]{:S(2)}, u32[]{:S(2)}) %collective-permute-start.4) | collective-permute-done | bytes 81952 | tf_op jit(solution)/shard_map/ppermute | solution.py:65
  87.7 1.1 collective-permute-start.5
  88.9 4.1 %collective-permute-done.12 = f32[4,20,8,128]{3,2,1,0:T(8,128)S(1)} collective-permute-done((f32[4,20,8,128]{3,2,1,0:T(8,128)S(1)}, f32[4,20,8,128]{3,2,1,0:T(8,128)S(1)}, u32[]{:S(2)}, u32[]{:S(2)}) %collective-permute-start.12) | collective-permute-done | bytes 327712 | tf_op jit(solution)/shard_map/ppermute | solution.py:65
  93.0 1.6 %collective-permute-start.13 = (f32[2,20,8,128]{3,2,1,0:T(8,128)S(1)}, f32[2,20,8,128]{3,2,1,0:T(8,128)S(1)}, u32[]{:S(2)}, u32[]{:S(2)}) collective-permute-start(f32[2,20,8,128]{3,2,1,0:T(8,128)S(1)} %dynamic-slice_bitcast_fusion.3), channel_id=1, source_target_pairs={{0,4},{2,6},{4,0},{6,2},{8,12},{10,14},{12,8},{14,10},{1,5},{3,7},... | collective-permute-start | bytes 491528 | tf_op jit(solution)/shard_map/ppermute | solution.py:65
  94.6 1.2 convolution_add_fusion.1
  95.8 0.6 collective-permute-start.6
  96.4 2.9 %collective-permute-done.13 = f32[2,20,8,128]{3,2,1,0:T(8,128)S(1)} collective-permute-done((f32[2,20,8,128]{3,2,1,0:T(8,128)S(1)}, f32[2,20,8,128]{3,2,1,0:T(8,128)S(1)}, u32[]{:S(2)}, u32[]{:S(2)}) %collective-permute-start.13) | collective-permute-done | bytes 163872 | tf_op jit(solution)/shard_map/ppermute | solution.py:65
  99.3 0.4 collective-permute-start.14
  99.7 1.5 %collective-permute-done.6 = bf16[2,20,8,128]{3,2,1,0:T(8,128)(2,1)S(1)} collective-permute-done((bf16[2,20,8,128]{3,2,1,0:T(8,128)(2,1)S(1)}, bf16[2,20,8,128]{3,2,1,0:T(8,128)(2,1)S(1)}, u32[]{:S(2)}, u32[]{:S(2)}) %collective-permute-start.6) | collective-permute-done | bytes 81952 | tf_op jit(solution)/shard_map/ppermute | solution.py:76
  101.2 0.6 collective-permute-start.7
  101.8 3.0 %collective-permute-done.14 = f32[1,20,8,128]{3,2,1,0:T(8,128)S(1)} collective-permute-done((f32[1,20,8,128]{3,2,1,0:T(8,128)S(1)}, f32[1,20,8,128]{3,2,1,0:T(8,128)S(1)}, u32[]{:S(2)}, u32[]{:S(2)}) %collective-permute-start.14) | collective-permute-done | bytes 81952 | tf_op jit(solution)/shard_map/ppermute | solution.py:65
  104.8 0.4 collective-permute-start.15
  105.2 1.3 fusion.28
  106.5 4.4 %copy.149 = bf16[2,512,1280]{2,1,0:T(8,128)(2,1)} copy(bf16[2,512,1280]{1,2,0:T(8,128)(2,1)} %bitcast.125) | data formatting | bytes 5242880
  110.9 3.2 %collective-permute-start.16 = (bf16[2,20,8,128]{3,2,1,0:T(8,128)(2,1)S(1)}, bf16[2,20,8,128]{3,2,1,0:T(8,128)(2,1)S(1)}, u32[]{:S(2)}, u32[]{:S(2)}) collective-permute-start(bf16[2,20,8,128]{3,2,1,0:T(8,128)(2,1)S(1)} %maximum_select_fusion.8), channel_id=1, source_target_pairs={{0,4},{2,6},{4,0},{6,2},{8,12},{10,14},{12,8},{14,10},{1,5},{3,7},... | collective-permute-start | bytes 245768 | tf_op jit(solution)/shard_map/ppermute | solution.py:76
  114.1 2.3 %collective-permute-done.16 = bf16[2,20,8,128]{3,2,1,0:T(8,128)(2,1)S(1)} collective-permute-done((bf16[2,20,8,128]{3,2,1,0:T(8,128)(2,1)S(1)}, bf16[2,20,8,128]{3,2,1,0:T(8,128)(2,1)S(1)}, u32[]{:S(2)}, u32[]{:S(2)}) %collective-permute-start.16) | collective-permute-done | bytes 81952 | tf_op jit(solution)/shard_map/ppermute | solution.py:76
  116.5 0.6 collective-permute-start.17
  117.3 4.5 %collective-permute-done.17 = bf16[4,20,8,128]{3,2,1,0:T(8,128)(2,1)S(1)} collective-permute-done((bf16[4,20,8,128]{3,2,1,0:T(8,128)(2,1)S(1)}, bf16[4,20,8,128]{3,2,1,0:T(8,128)(2,1)S(1)}, u32[]{:S(2)}, u32[]{:S(2)}) %collective-permute-start.17) | collective-permute-done | bytes 163872 | tf_op jit(solution)/shard_map/ppermute | solution.py:76
  122.0 0.6 fusion.48
  122.6 0.5 fusion.25
  123.1 0.5 copy-done.12
  123.8 0.7 reshape.169
  124.4 0.9 constant_dynamic-slice_fusion.1
  125.4 1.0 copy.146
  126.4 2.5 %fusion.15 = f32[256,128]{0,1:T(8,128)S(1)} fusion(f32[256,40]{0,1:T(8,128)S(1)} %copy-done.20, bf16[256,40,64]{0,2,1:T(8,128)(2,1)} %bitcast.136, bf16[20,64,128]{2,1,0:T(8,128)(2,1)} %collective-permute-done.8, bf16[20,64,128]{2,1,0:T(8,128)(2,1)S(1)} %copy_bitcast_fusion, pred[]{:T(512)S(6)} %eq.28), kind=kOutput, calls=%fused_computation.22 | convolution fusion | flops 171343872 | bytes 2138113 | tf_op jit(solution)/shard_map/jhp,hpn->jhn/dot_general | solution.py:225
  128.9 0.8 copy.148
  129.7 1.6 %fusion.24 = bf16[40,64,256]{2,1,0:T(8,128)(2,1)S(1)} fusion(f32[256,128]{0,1:T(8,128)S(1)} %copy-done.15, f32[256,40]{0,1:T(8,128)S(1)} %copy-done.20, bf16[20,64,128]{2,1,0:T(8,128)(2,1)} %collective-permute-done.8, bf16[20,64,128]{2,1,0:T(8,128)(2,1)S(1)} %copy_bitcast_fusion, pred[]{:T(512)S(6)} %eq.28), kind=kOutput, calls=%fused_computation.37 | convolution fusion | flops 172032000 | bytes 2138113 | tf_op jit(solution)/shard_map/jhn,hpn->jhp/dot_general | solution.py:221
  131.3 1.6 %copy.147 = bf16[256,2560]{1,0:T(8,128)(2,1)} copy(bf16[256,2560]{0,1:T(8,128)(2,1)S(1)} %bitcast.139) | data formatting | bytes 2621440
  132.8 0.3 copy.145
  133.3 0.8 fusion.42
  (89 shorter events, 1.4 us)
Async XLA Ops:
  0.6 16.7 %copy-start = (bf16[2,512,128]{2,1,0:T(8,128)(2,1)S(1)}, bf16[2,512,128]{2,1,0:T(8,128)(2,1)}, u32[]{:S(2)}) copy-start(bf16[2,512,128]{2,1,0:T(8,128)(2,1)} %param.14) | copy-start | bytes 786436
  0.6 9.3 %copy-start.18 = (s32[2]{0:T(128)S(1)}, s32[2]{0:T(128)}, u32[]{:S(2)}) copy-start(s32[2]{0:T(128)} %param.16) | copy-start | bytes 28
  1.6 8.4 %collective-permute-start = (f32[40]{0:T(128)S(1)}, f32[40]{0:T(128)S(1)}, u32[]{:S(2)}, u32[]{:S(2)}) collective-permute-start(f32[40]{0:T(128)S(1)} %fusion.35), channel_id=1, source_target_pairs={{1,0},{2,1},{3,2},{4,3},{5,4},{6,5},{7,6},{8,7},{9,8},{10,9},{11,1... | collective-permute-start | bytes 488 | tf_op jit(solution)/shard_map/ppermute | solution.py:35
  5.9 8.6 %copy-start.16 = (f32[2,512,20]{1,2,0:T(8,128)}, f32[2,512,20]{1,2,0:T(8,128)S(1)}, u32[]{:S(2)}) copy-start(f32[2,512,20]{1,2,0:T(8,128)S(1)} %get-tuple-element.36) | copy-start | bytes 245764
  10.1 8.1 %collective-permute-start.1 = (f32[40]{0:T(128)S(1)}, f32[40]{0:T(128)S(1)}, u32[]{:S(2)}, u32[]{:S(2)}) collective-permute-start(f32[40]{0:T(128)S(1)} %add.122), channel_id=1, source_target_pairs={{2,0},{3,1},{4,2},{5,3},{6,4},{7,5},{8,6},{9,7},{10,8},{11,9},{12,... | collective-permute-start | bytes 488 | tf_op jit(solution)/shard_map/ppermute | solution.py:35
  14.5 2.8 %copy-start.4 = (bf16[2,512,1280]{1,2,0:T(8,128)(2,1)}, bf16[2,512,1280]{1,2,0:T(8,128)(2,1)S(1)}, u32[]{:S(2)}) copy-start(bf16[2,512,1280]{1,2,0:T(8,128)(2,1)S(1)} %broadcast_select_fusion) | copy-start | bytes 7864324
  18.3 25.1 %collective-permute-start.9 = (f32[40]{0:T(128)S(1)}, f32[40]{0:T(128)S(1)}, u32[]{:S(2)}, u32[]{:S(2)}) collective-permute-start(f32[40]{0:T(128)S(1)} %add.123), channel_id=1, source_target_pairs={{4,0},{5,1},{6,2},{7,3},{8,4},{9,5},{10,6},{11,7},{12,8},{13,9},{1... | collective-permute-start | bytes 488 | tf_op jit(solution)/shard_map/ppermute | solution.py:35
  20.3 50.2 %collective-permute-start.2 = (f32[4,20,8,128]{3,2,1,0:T(8,128)}, f32[4,20,8,128]{3,2,1,0:T(8,128)}, u32[]{:S(2)}, u32[]{:S(2)}) collective-permute-start(f32[4,20,8,128]{3,2,1,0:T(8,128)} %dynamic-slice_bitcast_fusion.2), channel_id=1, source_target_pairs={{0,2},{2,0},{4,6},{6,4},{8,10},{10,8},{12,14},{14,12},{1,3},{3,1},... | collective-permute-start | bytes 983048 | tf_op jit(solution)/shard_map/ppermute | solution.py:65
  31.6 2.9 %copy-start.5 = (bf16[2,512,1280]{1,2,0:T(8,128)(2,1)S(1)}, bf16[2,512,1280]{1,2,0:T(8,128)(2,1)}, u32[]{:S(2)}) copy-start(bf16[2,512,1280]{1,2,0:T(8,128)(2,1)} %copy.124) | copy-start | bytes 7864324
  43.4 23.9 %collective-permute-start.10 = (f32[40]{0:T(128)S(1)}, f32[40]{0:T(128)S(1)}, u32[]{:S(2)}, u32[]{:S(2)}) collective-permute-start(f32[40]{0:T(128)S(1)} %add.133), channel_id=1, source_target_pairs={{8,0},{9,1},{10,2},{11,3},{12,4},{13,5},{14,6},{15,7},{24,16},{25,... | collective-permute-start | bytes 488 | tf_op jit(solution)/shard_map/ppermute | solution.py:35
  53.6 9.5 %copy-start.6 = (bf16[2,512,1280]{2,1,0:T(8,128)(2,1)S(1)}, bf16[2,512,1280]{2,1,0:T(8,128)(2,1)}, u32[]{:S(2)}) copy-start(bf16[2,512,1280]{2,1,0:T(8,128)(2,1)} %copy.130) | copy-start | bytes 7864324
  53.6 9.5 %copy-start.7 = (bf16[2,512,1280]{2,1,0:T(8,128)(2,1)S(1)}, bf16[2,512,1280]{2,1,0:T(8,128)(2,1)}, u32[]{:S(2)}) copy-start(bf16[2,512,1280]{2,1,0:T(8,128)(2,1)} %copy.131) | copy-start | bytes 7864324
  53.6 9.5 %copy-start.8 = (bf16[2,512,1280]{2,1,0:T(8,128)(2,1)S(1)}, bf16[2,512,1280]{2,1,0:T(8,128)(2,1)}, u32[]{:S(2)}) copy-start(bf16[2,512,1280]{2,1,0:T(8,128)(2,1)} %copy.133) | copy-start | bytes 7864324
  53.6 9.6 %copy-start.9 = (bf16[2,512,1280]{2,1,0:T(8,128)(2,1)S(1)}, bf16[2,512,1280]{2,1,0:T(8,128)(2,1)}, u32[]{:S(2)}) copy-start(bf16[2,512,1280]{2,1,0:T(8,128)(2,1)} %copy.132) | copy-start | bytes 7864324
  63.2 4.1 %copy-start.17 = (s32[256,40]{0,1:T(8,128)S(1)}, s32[256,40]{0,1:T(8,128)}, u32[]{:S(2)}) copy-start(s32[256,40]{0,1:T(8,128)} %param.11) | copy-start | bytes 122884
  63.2 4.4 %copy-start.14 = (f32[256,128]{0,1:T(8,128)S(1)}, f32[256,128]{0,1:T(8,128)}, u32[]{:S(2)}) copy-start(f32[256,128]{0,1:T(8,128)} %copy.125) | copy-start | bytes 393220
  67.6 2.9 %copy-start.19 = (f32[256,40]{0,1:T(8,128)}, f32[256,40]{0,1:T(8,128)S(1)}, u32[]{:S(2)}) copy-start(f32[256,40]{0,1:T(8,128)S(1)} %add_exponential_fusion) | copy-start | bytes 122884
  67.6 7.3 %copy-start.3 = (bf16[2,512,20,64]{1,3,2,0:T(8,128)(2,1)S(1)}, bf16[2,512,20,64]{1,3,2,0:T(8,128)(2,1)}, u32[]{:S(2)}) copy-start(bf16[2,512,20,64]{1,3,2,0:T(8,128)(2,1)} %get-tuple-element.50) | copy-start | bytes 7864324
  67.6 7.3 %copy-start.13 = (pred[512,512]{1,0:T(8,128)(4,1)S(1)}, pred[512,512]{1,0:T(8,128)(4,1)}, u32[]{:S(2)}) copy-start(pred[512,512]{1,0:T(8,128)(4,1)} %iota_compare_fusion) | copy-start | bytes 786436
  67.6 7.3 %copy-start.21 = (f32[2,512,512]{2,1,0:T(8,128)S(1)}, f32[2,512,512]{2,1,0:T(8,128)}, u32[]{:S(2)}) copy-start(f32[2,512,512]{2,1,0:T(8,128)} %fusion.8) | copy-start | bytes 6291460
  70.2 13.2 %collective-permute-start.11 = (f32[20,64,128]{2,1,0:T(8,128)S(1)}, f32[20,64,128]{2,1,0:T(8,128)S(1)}, u32[]{:S(2)}, u32[]{:S(2)}) collective-permute-start(f32[20,64,128]{2,1,0:T(8,128)S(1)} %dynamic-slice_bitcast_fusion), channel_id=1, source_target_pairs={{0,1},{1,0},{2,3},{3,2},{4,5},{5,4},{6,7},{7,6},{8,9},{9,8},{10,11... | collective-permute-start | bytes 1966088 | tf_op jit(solution)/shard_map/ppermute | solution.py:100
  71.5 8.3 %collective-permute-start.3 = (f32[2,20,8,128]{3,2,1,0:T(8,128)S(1)}, f32[2,20,8,128]{3,2,1,0:T(8,128)S(1)}, u32[]{:S(2)}, u32[]{:S(2)}) collective-permute-start(f32[2,20,8,128]{3,2,1,0:T(8,128)S(1)} %dynamic-slice_bitcast_fusion.4), channel_id=1, source_target_pairs={{0,4},{2,6},{4,0},{6,2},{8,12},{10,14},{12,8},{14,10},{1,5},{3,7},... | collective-permute-start | bytes 491528 | tf_op jit(solution)/shard_map/ppermute | solution.py:65
  76.7 28.5 %copy-start.1 = (f32[2,512,512]{2,1,0:T(8,128)}, f32[2,512,512]{2,1,0:T(8,128)S(1)}, u32[]{:S(2)}) copy-start(f32[2,512,512]{2,1,0:T(8,128)S(1)} %add_select_fusion) | copy-start | bytes 6291460
  79.8 7.9 %collective-permute-start.4 = (f32[1,20,8,128]{3,2,1,0:T(8,128)S(1)}, f32[1,20,8,128]{3,2,1,0:T(8,128)S(1)}, u32[]{:S(2)}, u32[]{:S(2)}) collective-permute-start(f32[1,20,8,128]{3,2,1,0:T(8,128)S(1)} %constant_dynamic-slice_fusion.3), channel_id=1, source_target_pairs={{0,8},{2,10},{4,12},{6,14},{8,0},{10,2},{12,4},{14,6},{1,9},{3,11}... | collective-permute-start | bytes 245768 | tf_op jit(solution)/shard_map/ppermute | solution.py:65
  83.6 9.3 %collective-permute-start.12 = (f32[4,20,8,128]{3,2,1,0:T(8,128)S(1)}, f32[4,20,8,128]{3,2,1,0:T(8,128)S(1)}, u32[]{:S(2)}, u32[]{:S(2)}) collective-permute-start(f32[4,20,8,128]{3,2,1,0:T(8,128)S(1)} %dynamic-slice_bitcast_fusion.1), channel_id=1, source_target_pairs={{0,2},{2,0},{4,6},{6,4},{8,10},{10,8},{12,14},{14,12},{1,3},{3,1},... | collective-permute-start | bytes 983048 | tf_op jit(solution)/shard_map/ppermute | solution.py:65
  87.7 8.1 %collective-permute-start.5 = (bf16[1,20,8,128]{3,2,1,0:T(8,128)(2,1)S(1)}, bf16[1,20,8,128]{3,2,1,0:T(8,128)(2,1)S(1)}, u32[]{:S(2)}, u32[]{:S(2)}) collective-permute-start(bf16[1,20,8,128]{3,2,1,0:T(8,128)(2,1)S(1)} %add_convert_fusion.1), channel_id=1, source_target_pairs={{0,8},{2,10},{4,12},{6,14},{8,0},{10,2},{12,4},{14,6},{1,9},{3,11}... | collective-permute-start | bytes 122888 | tf_op jit(solution)/shard_map/ppermute | solution.py:76
  93.0 12.2 %copy-start.10 = (bf16[2,512,128]{2,1,0:T(8,128)(2,1)S(1)}, bf16[2,512,128]{2,1,0:T(8,128)(2,1)}, u32[]{:S(2)}) copy-start(bf16[2,512,128]{2,1,0:T(8,128)(2,1)} %param.13) | copy-start | bytes 786436
  93.0 6.3 %collective-permute-start.13 = (f32[2,20,8,128]{3,2,1,0:T(8,128)S(1)}, f32[2,20,8,128]{3,2,1,0:T(8,128)S(1)}, u32[]{:S(2)}, u32[]{:S(2)}) collective-permute-start(f32[2,20,8,128]{3,2,1,0:T(8,128)S(1)} %dynamic-slice_bitcast_fusion.3), channel_id=1, source_target_pairs={{0,4},{2,6},{4,0},{6,2},{8,12},{10,14},{12,8},{14,10},{1,5},{3,7},... | collective-permute-start | bytes 491528 | tf_op jit(solution)/shard_map/ppermute | solution.py:65
  95.8 5.3 %collective-permute-start.6 = (bf16[2,20,8,128]{3,2,1,0:T(8,128)(2,1)S(1)}, bf16[2,20,8,128]{3,2,1,0:T(8,128)(2,1)S(1)}, u32[]{:S(2)}, u32[]{:S(2)}) collective-permute-start(bf16[2,20,8,128]{3,2,1,0:T(8,128)(2,1)S(1)} %maximum_select_fusion.7), channel_id=1, source_target_pairs={{0,4},{2,6},{4,0},{6,2},{8,12},{10,14},{12,8},{14,10},{1,5},{3,7},... | collective-permute-start | bytes 245768 | tf_op jit(solution)/shard_map/ppermute | solution.py:76
  99.3 5.4 %collective-permute-start.14 = (f32[1,20,8,128]{3,2,1,0:T(8,128)S(1)}, f32[1,20,8,128]{3,2,1,0:T(8,128)S(1)}, u32[]{:S(2)}, u32[]{:S(2)}) collective-permute-start(f32[1,20,8,128]{3,2,1,0:T(8,128)S(1)} %constant_dynamic-slice_fusion.2), channel_id=1, source_target_pairs={{0,8},{2,10},{4,12},{6,14},{8,0},{10,2},{12,4},{14,6},{1,9},{3,11}... | collective-permute-start | bytes 245768 | tf_op jit(solution)/shard_map/ppermute | solution.py:65
  101.2 12.9 %collective-permute-start.7 = (bf16[4,20,8,128]{3,2,1,0:T(8,128)(2,1)S(1)}, bf16[4,20,8,128]{3,2,1,0:T(8,128)(2,1)S(1)}, u32[]{:S(2)}, u32[]{:S(2)}) collective-permute-start(bf16[4,20,8,128]{3,2,1,0:T(8,128)(2,1)S(1)} %maximum_select_fusion.3), channel_id=1, source_target_pairs={{0,2},{2,0},{4,6},{6,4},{8,10},{10,8},{12,14},{14,12},{1,3},{3,1},... | collective-permute-start | bytes 491528 | tf_op jit(solution)/shard_map/ppermute | solution.py:76
  104.8 6.1 %collective-permute-start.15 = (bf16[1,20,8,128]{3,2,1,0:T(8,128)(2,1)S(1)}, bf16[1,20,8,128]{3,2,1,0:T(8,128)(2,1)S(1)}, u32[]{:S(2)}, u32[]{:S(2)}) collective-permute-start(bf16[1,20,8,128]{3,2,1,0:T(8,128)(2,1)S(1)} %add_convert_fusion), channel_id=1, source_target_pairs={{0,8},{2,10},{4,12},{6,14},{8,0},{10,2},{12,4},{14,6},{1,9},{3,11}... | collective-permute-start | bytes 122888 | tf_op jit(solution)/shard_map/ppermute | solution.py:76
  110.9 5.6 %collective-permute-start.16 = (bf16[2,20,8,128]{3,2,1,0:T(8,128)(2,1)S(1)}, bf16[2,20,8,128]{3,2,1,0:T(8,128)(2,1)S(1)}, u32[]{:S(2)}, u32[]{:S(2)}) collective-permute-start(bf16[2,20,8,128]{3,2,1,0:T(8,128)(2,1)S(1)} %maximum_select_fusion.8), channel_id=1, source_target_pairs={{0,4},{2,6},{4,0},{6,2},{8,12},{10,14},{12,8},{14,10},{1,5},{3,7},... | collective-permute-start | bytes 245768 | tf_op jit(solution)/shard_map/ppermute | solution.py:76
  116.5 5.4 %collective-permute-start.17 = (bf16[4,20,8,128]{3,2,1,0:T(8,128)(2,1)S(1)}, bf16[4,20,8,128]{3,2,1,0:T(8,128)(2,1)S(1)}, u32[]{:S(2)}, u32[]{:S(2)}) collective-permute-start(bf16[4,20,8,128]{3,2,1,0:T(8,128)(2,1)S(1)} %maximum_select_fusion.4), channel_id=1, source_target_pairs={{0,2},{2,0},{4,6},{6,4},{8,10},{10,8},{12,14},{14,12},{1,3},{3,1},... | collective-permute-start | bytes 491528 | tf_op jit(solution)/shard_map/ppermute | solution.py:76
  117.2 5.4 %copy-start.2 = (f32[2,512,512]{2,1,0:T(8,128)S(1)}, f32[2,512,512]{2,1,0:T(8,128)}, u32[]{:S(2)}) copy-start(f32[2,512,512]{2,1,0:T(8,128)} %copy-done.1) | copy-start | bytes 6291460
  117.3 5.4 %copy-start.11 = (f32[2,512,128]{1,2,0:T(8,128)S(1)}, f32[2,512,128]{1,2,0:T(8,128)}, u32[]{:S(2)}) copy-start(f32[2,512,128]{1,2,0:T(8,128)} %fusion.28) | copy-start | bytes 1572868
  117.3 9.1 %collective-permute-start.8 = (bf16[20,64,128]{2,1,0:T(8,128)(2,1)S(1)}, bf16[20,64,128]{2,1,0:T(8,128)(2,1)}, u32[]{:S(2)}, u32[]{:S(2)}) collective-permute-start(bf16[20,64,128]{2,1,0:T(8,128)(2,1)S(1)} %copy_bitcast_fusion), channel_id=1, source_target_pairs={{0,1},{1,0},{2,3},{3,2},{4,5},{5,4},{6,7},{7,6},{8,9},{9,8},{10,11... | collective-permute-start | bytes 983048 | tf_op jit(solution)/shard_map/ppermute | solution.py:100
  122.6 1.0 copy-start.12
  123.7 2.7 %copy-start.20 = (f32[256,40]{0,1:T(8,128)S(1)}, f32[256,40]{0,1:T(8,128)}, u32[]{:S(2)}) copy-start(f32[256,40]{0,1:T(8,128)} %copy-done.19) | copy-start | bytes 122884
  126.4 3.3 %copy-start.15 = (f32[256,128]{0,1:T(8,128)S(1)}, f32[256,128]{0,1:T(8,128)}, u32[]{:S(2)}) copy-start(f32[256,128]{0,1:T(8,128)} %copy.125) | copy-start | bytes 393220
  126.4 6.8 %collective-permute-start.18 = (f32[2,256,256]{2,1,0:T(8,128)}, f32[2,256,256]{2,1,0:T(8,128)S(1)}, u32[]{:S(2)}, u32[]{:S(2)}) collective-permute-start(f32[2,256,256]{2,1,0:T(8,128)} %bitcast.62), channel_id=1, source_target_pairs={{0,1},{1,0},{2,3},{3,2},{4,5},{5,4},{6,7},{7,6},{8,9},{9,8},{10,11... | collective-permute-start | bytes 1572872 | tf_op jit(solution)/shard_map/ppermute | solution.py:100
